TPU v7x, 32 devices: a whole 2x2x4 slice. The times are simulated.
32 devices in a mesh: real: 2 (over y), slab: 4 (over z), pencil: 2 (over x), sub: 2 (over core).
Axes of the slice: x: 2, y: 2, z: 4, core: 2. Of those that a mesh axis runs over, the one named last changes fastest.
Arguments:
- permeability: float32 [128, 64, 256], P(('real', 'slab'), ('pencil', 'sub')), parts along dimension 0, may hold values from 0.1 to 10
- source: float32 [128, 64, 256], P(('real', 'slab'), ('pencil', 'sub')), parts along dimension 0, may hold values from -24 to 24
- pressure: float32 [128, 64, 256], P(('real', 'slab'), ('pencil', 'sub')), parts along dimension 0, may hold values from -24 to 24
- aggregate: int32 [128], P('real'), parts along dimension 0, may hold values from 0 to 31, as said below
Outputs:
- pressure_out: float32 [128, 64, 256], P(('real', 'slab'), ('pencil', 'sub')), parts along dimension 0
There are 2 independent parts, one for each index of `real`. A program takes and returns all parts, laid end to end along the dimension named above; each array names one. Nothing has to cross between parts.
Inputs may be any that keep to these rules, and one draw needn't show every extreme that they name: `aggregate`: never falls along its dimension; each value covers 1 to 4 consecutive positions, some value exactly 4; positions k * 16 - 1 and k * 16 always hold the same value.
All inputs are finite; a program needn't handle non-finite values.
Results may differ from a plain program's by a relative error of at most 0.000068.
Values sent between devices are 32-bit elements; how exact they have to be, the bound alone decides.
No kernel may reach another device: no remote copies, remote signals or barrier semaphores. Data moves between devices by JAX's collectives and lax.ppermute only.
A program may use at most 64 MiB of HBM per device.

v0:
```python
import jax
import jax.numpy as jnp
from jax import lax
from jax.sharding import PartitionSpec as P

NU = 2
NCS = 4


OMEGA = 0.8


def padded(array, sides, width):
    for axis, dim in sides:
        count, length = (lax.axis_size(axis), array.shape[dim])
        up = [(i, (i + 1) % count) for i in range(count - 1)]
        down = [(j, i) for i, j in up]
        last = lax.slice_in_dim(array, length - width, length, axis=dim)
        leading = lax.slice_in_dim(array, 0, width, axis=dim)
        before = lax.ppermute(last, axis, up)
        after = lax.ppermute(leading, axis, down)
        array = jnp.concatenate([before, array, after], axis=dim)
    return array


def passed_along(array, axis, by):
    count = lax.axis_size(axis)
    pairs = [(i, i + by) for i in range(count) if 0 <= i + by < count]
    return lax.ppermute(array, axis, pairs)


def harmonic(lower_k, upper_k, inside):
    denom_sum = jnp.where(inside, lower_k + upper_k, 1.0)
    return jnp.where(inside, 2.0 * lower_k * upper_k / denom_sum, 0.0)


def geometry(perm_ext, glob_x, glob_y, inside_x, inside_y, total_x, total_y):
    count_z = perm_ext.shape[2]
    both_x = (inside_x[:-1] & inside_x[1:])[:, None, None] & inside_y[None, :, None]
    both_y = (inside_y[:-1] & inside_y[1:])[None, :, None] & inside_x[:, None, None]
    plane_in = inside_x[:, None, None] & inside_y[None, :, None]
    face_x = harmonic(perm_ext[:-1], perm_ext[1:], both_x)
    face_y = harmonic(perm_ext[:, :-1], perm_ext[:, 1:], both_y)
    face_z = harmonic(perm_ext[:, :, :-1], perm_ext[:, :, 1:], plane_in)
    cell_perm = perm_ext[1:-1, 1:-1]
    face_west = face_x[:-1, 1:-1]
    face_east = face_x[1:, 1:-1]
    face_south = face_y[1:-1, :-1]
    face_north = face_y[1:-1, 1:]
    zero_plane = jnp.zeros_like(cell_perm[:, :, :1])
    face_below = jnp.concatenate([zero_plane, face_z[1:-1, 1:-1]], axis=2)
    face_above = jnp.concatenate([face_z[1:-1, 1:-1], zero_plane], axis=2)
    cell_x = glob_x[1:-1]
    cell_y = glob_y[1:-1]
    index_z = jnp.arange(count_z)
    ends_x = (cell_x == 0).astype(jnp.float32) + (cell_x == total_x - 1).astype(jnp.float32)
    ends_y = (cell_y == 0).astype(jnp.float32) + (cell_y == total_y - 1).astype(jnp.float32)
    ends_z = (index_z == 0).astype(jnp.float32) + (index_z == count_z - 1).astype(jnp.float32)
    edges = ends_x[:, None, None] + ends_y[None, :, None] + ends_z[None, None, :]
    boundary = 2.0 * cell_perm * edges
    diagonal = face_west + face_east + face_south + face_north + face_below + face_above + boundary
    cell_in = plane_in[1:-1, 1:-1]
    safe_diag = jnp.where(cell_in, diagonal, 1.0)
    return (
        face_west,
        face_east,
        face_south,
        face_north,
        face_below,
        face_above,
        boundary,
        safe_diag,
    )


def apply_fine(ext_field, faces_now):
    face_west, face_east, face_south, face_north, face_below, face_above, boundary, safe_diag = (
        faces_now
    )
    center = ext_field[1:-1, 1:-1]
    zero_plane = jnp.zeros_like(center[:, :, :1])
    below_vals = jnp.concatenate([zero_plane, center[:, :, :-1]], axis=2)
    above_vals = jnp.concatenate([center[:, :, 1:], zero_plane], axis=2)
    beside_all = face_west * ext_field[:-2, 1:-1] + face_east * ext_field[2:, 1:-1]
    beside_all = beside_all + face_south * ext_field[1:-1, :-2] + face_north * ext_field[1:-1, 2:]
    beside_all = beside_all + face_below * below_vals + face_above * above_vals
    return (center, safe_diag * center - beside_all)


def fine_halo(field_in):
    return padded(field_in, (("slab", 0), (("pencil", "sub"), 1)), 1)


def body(permeability, source, pressure, aggregate):
    width_x, width_y, depth_cells = permeability.shape
    slab_index = lax.axis_index("slab")
    slab_count = lax.axis_size("slab")
    row_index = lax.axis_index(("pencil", "sub"))
    row_count = lax.axis_size(("pencil", "sub"))
    total_x = width_x * slab_count
    total_y = width_y * row_count
    fine_rim = 1
    perm_ext = padded(permeability, (("slab", 0), (("pencil", "sub"), 1)), fine_rim)
    glob_x = slab_index * width_x - fine_rim + jnp.arange(width_x + 2 * fine_rim)
    glob_y = row_index * width_y - fine_rim + jnp.arange(width_y + 2 * fine_rim)
    inside_x = (glob_x >= 0) & (glob_x < total_x)
    inside_y = (glob_y >= 0) & (glob_y < total_y)
    faces_full = geometry(perm_ext, glob_x, glob_y, inside_x, inside_y, total_x, total_y)
    faces_zero = tuple((member for member in faces_full))

    def smooth(field_in):
        for sweep_index in range(NU):
            center, product = apply_fine(fine_halo(field_in), faces_zero)
            field_in = center + OMEGA * (source - product) / faces_zero[7]
        return field_in

    pressure = smooth(pressure)
    center, product = apply_fine(fine_halo(pressure), faces_zero)
    residual = source - product
    half_y = width_y // 2
    half_z = depth_cells // 2

    def pair_sum(block_in):
        return block_in.reshape(width_x, half_y, 2, half_z, 2).sum(axis=(2, 4))

    padded_ids = jnp.concatenate([aggregate[:1], aggregate, aggregate[-1:]])
    ext_ids = lax.dynamic_slice_in_dim(padded_ids, slab_index * width_x, width_x + 2)
    local_ids = ext_ids[1:-1]
    straddles = (slab_index > 0) & (ext_ids[0] == local_ids[0])
    first_id = local_ids[0] + straddles.astype(jnp.int32)
    count_live = local_ids[-1] - first_id + 1
    slot_ids = local_ids - first_id
    crossing = (local_ids != ext_ids[2:]).astype(jnp.float32)
    face_east = faces_zero[1]
    face_north = faces_zero[3]
    face_above = faces_zero[5]
    boundary = faces_zero[6]
    east_part = pair_sum(face_east * crossing[:, None, None])
    north_part = face_north[:, 1::2].reshape(width_x, half_y, half_z, 2).sum(axis=3)
    above_part = face_above[:, :, 1::2].reshape(width_x, half_y, 2, half_z).sum(axis=2)
    stacked = jnp.stack([pair_sum(residual), east_part, north_part, above_part, pair_sum(boundary)])
    slot_range = jnp.arange(width_x)
    owner_map = (slot_ids[:, None] == slot_range[None, :]).astype(jnp.float32)
    spill_map = (slot_ids == -1).astype(jnp.float32)
    coarse = jnp.einsum("qxjk,xs->qsjk", stacked, owner_map, precision=lax.Precision.HIGHEST)
    edge_sums = jnp.einsum("qxjk,x->qjk", stacked, spill_map, precision=lax.Precision.HIGHEST)
    arriving = passed_along(edge_sums, "slab", -1)
    last_slot = (slot_range == count_live - 1).astype(jnp.float32)
    coarse = coarse + arriving[:, None] * last_slot[None, :, None, None]

    def coarse_extend(coarse_block, rim_width):
        tail_planes = lax.dynamic_slice_in_dim(
            coarse_block, count_live - rim_width, rim_width, axis=1
        )
        sent_block = jnp.concatenate([coarse_block, tail_planes], axis=1)
        wide_block = padded(sent_block, (("slab", 1), (("pencil", "sub"), 2)), rim_width)
        ahead_planes = wide_block[:, width_x + 2 * rim_width :]
        base_block = wide_block[:, : width_x + 2 * rim_width]
        return lax.dynamic_update_slice_in_dim(
            base_block, ahead_planes, rim_width + count_live, axis=1
        )

    coarse_rim = NCS
    coef_ext = coarse_extend(coarse, coarse_rim)
    coarse_corr = jnp.zeros((width_x + 2 * NCS, half_y + 2 * NCS, half_z), jnp.float32)
    for sweep_index in range(NCS):
        out_rim = NCS - 1 - sweep_index
        start_at = coarse_rim - out_rim
        size_x = width_x + 2 * out_rim
        size_y = half_y + 2 * out_rim

        def region(offset_x, offset_y):
            return coef_ext[
                :,
                start_at + offset_x : start_at + offset_x + size_x,
                start_at + offset_y : start_at + offset_y + size_y,
            ]

        here_coef = region(0, 0)
        coarse_rhs = here_coef[0]
        coarse_east = here_coef[1]
        coarse_north = here_coef[2]
        coarse_above = here_coef[3]
        coarse_bound = here_coef[4]
        coarse_west = region(-1, 0)[1]
        coarse_south = region(0, -1)[2]
        zero_plane = jnp.zeros_like(coarse_above[:, :, :1])
        coarse_below = jnp.concatenate([zero_plane, coarse_above[:, :, :-1]], axis=2)
        diag_coarse = (
            coarse_east
            + coarse_west
            + coarse_north
            + coarse_south
            + coarse_above
            + coarse_below
            + coarse_bound
        )
        safe_coarse = jnp.where(diag_coarse > 0, diag_coarse, 1.0)
        coarse_center = coarse_corr[1:-1, 1:-1]
        above_vals = jnp.concatenate([coarse_center[:, :, 1:], zero_plane], axis=2)
        below_vals = jnp.concatenate([zero_plane, coarse_center[:, :, :-1]], axis=2)
        beside_all = coarse_east * coarse_corr[2:, 1:-1] + coarse_west * coarse_corr[:-2, 1:-1]
        beside_all = (
            beside_all
            + coarse_north * coarse_corr[1:-1, 2:]
            + coarse_south * coarse_corr[1:-1, :-2]
        )
        beside_all = beside_all + coarse_above * above_vals + coarse_below * below_vals
        coarse_corr = (
            coarse_center
            + OMEGA * (coarse_rhs - (diag_coarse * coarse_center - beside_all)) / safe_coarse
        )
    corr_wide = coarse_extend(coarse_corr[None], 1)[0][:, 1:-1]
    pick_map = ((slot_ids + 1)[:, None] == jnp.arange(width_x + 2)[None, :]).astype(jnp.float32)
    correction = jnp.einsum("xs,sjk->xjk", pick_map, corr_wide, precision=lax.Precision.HIGHEST)
    correction = jnp.repeat(jnp.repeat(correction, 2, axis=1), 2, axis=2)
    pressure = pressure + correction
    return smooth(pressure)


def solution(mesh):
    in_specs = (
        P(("real", "slab"), ("pencil", "sub"), None),
        P(("real", "slab"), ("pencil", "sub"), None),
        P(("real", "slab"), ("pencil", "sub"), None),
        P("real"),
    )
    out_specs = P(("real", "slab"), ("pencil", "sub"), None)
    return jax.shard_map(body, mesh=mesh, in_specs=in_specs, out_specs=out_specs, check_vma=False)
```

profile of v0, /device:TPU:1, one launch (start us, length us, event | category | flops | bytes accessed | tf_op | source)
XLA Modules:
  0.0 181.4 jit_solution(6753484500826297644)
XLA Ops:
  0.8 1.3 collective-permute-start.5
  2.1 4.7 %collective-permute-start.4 = (f32[1,16,256]{2,0,1:T(1,128)S(1)}, f32[1,16,256]{2,0,1:T(1,128)S(1)}, u32[]{:S(2)}, u32[]{:S(2)}) collective-permute-start(f32[1,16,256]{2,0,1:T(1,128)S(1)} %copy.61), channel_id=1, source_target_pairs={{0,4},{4,8},{8,12},{1,5},{5,9},{9,13},{2,6},{6,10},{10,14},{3,7},{... | collective-permute-start | bytes 49160 | tf_op jit(solution)/shard_map/ppermute | solution.py:20
  7.6 1.3 collective-permute-start.1
  8.9 4.0 %collective-permute-start = (f32[1,16,256]{2,0,1:T(1,128)S(1)}, f32[1,16,256]{2,0,1:T(1,128)S(1)}, u32[]{:S(2)}, u32[]{:S(2)}) collective-permute-start(f32[1,16,256]{2,0,1:T(1,128)S(1)} %copy.56), channel_id=1, source_target_pairs={{0,4},{4,8},{8,12},{1,5},{5,9},{9,13},{2,6},{6,10},{10,14},{3,7},{... | collective-permute-start | bytes 49160 | tf_op jit(solution)/shard_map/ppermute | solution.py:20
  13.2 1.3 fusion.142
  14.6 2.0 %pad_add_fusion = s32[66]{0:T(128)S(1)} fusion(s32[1]{0:T(128)} %get-tuple-element.61, s32[64]{0:T(128)} %param.7, s32[1]{0:T(128)} %get-tuple-element.60), kind=kLoop, calls=%fused_computation.270 | loop fusion | flops 132 | bytes 528 | tf_op jit(solution)/shard_map/concatenate | solution.py:126
  17.4 1.1 copy.69
  22.0 5.0 %collective-permute-start.2 = (f32[18,1,256]{2,0,1:T(8,128)S(1)}, f32[18,1,256]{2,0,1:T(8,128)S(1)}, u32[]{:S(2)}, u32[]{:S(2)}) collective-permute-start(f32[18,1,256]{2,0,1:T(8,128)S(1)} %get-tuple-element.23), channel_id=1, source_target_pairs={{0,1},{1,2},{2,3},{4,5},{5,6},{6,7},{8,9},{9,10},{10,11},{12,13},{... | collective-permute-start | bytes 55304 | tf_op jit(solution)/shard_map/ppermute | solution.py:20
  27.0 1.9 %collective-permute-start.3 = (f32[18,1,256]{2,0,1:T(8,128)S(1)}, f32[18,1,256]{2,0,1:T(8,128)S(1)}, u32[]{:S(2)}, u32[]{:S(2)}) collective-permute-start(f32[18,1,256]{2,0,1:T(8,128)S(1)} %get-tuple-element.24), channel_id=1, source_target_pairs={{1,0},{2,1},{3,2},{5,4},{6,5},{7,6},{9,8},{10,9},{11,10},{13,12},{... | collective-permute-start | bytes 55304 | tf_op jit(solution)/shard_map/ppermute | solution.py:21
  29.0 3.6 %collective-permute-start.6 = (f32[18,1,256]{2,0,1:T(8,128)S(1)}, f32[18,1,256]{2,0,1:T(8,128)S(1)}, u32[]{:S(2)}, u32[]{:S(2)}) collective-permute-start(f32[18,1,256]{2,0,1:T(8,128)S(1)} %get-tuple-element.25), channel_id=1, source_target_pairs={{0,1},{1,2},{2,3},{4,5},{5,6},{6,7},{8,9},{9,10},{10,11},{12,13},{... | collective-permute-start | bytes 55304 | tf_op jit(solution)/shard_map/ppermute | solution.py:20
  32.6 1.9 %collective-permute-start.7 = (f32[18,1,256]{2,0,1:T(8,128)S(1)}, f32[18,1,256]{2,0,1:T(8,128)S(1)}, u32[]{:S(2)}, u32[]{:S(2)}) collective-permute-start(f32[18,1,256]{2,0,1:T(8,128)S(1)} %get-tuple-element.26), channel_id=1, source_target_pairs={{1,0},{2,1},{3,2},{5,4},{6,5},{7,6},{9,8},{10,9},{11,10},{13,12},{... | collective-permute-start | bytes 55304 | tf_op jit(solution)/shard_map/ppermute | solution.py:21
  35.3 2.4 %collective-permute-done.7 = f32[18,1,256]{2,0,1:T(8,128)S(1)} collective-permute-done((f32[18,1,256]{2,0,1:T(8,128)S(1)}, f32[18,1,256]{2,0,1:T(8,128)S(1)}, u32[]{:S(2)}, u32[]{:S(2)}) %collective-permute-start.7) | collective-permute-done | bytes 18464 | tf_op jit(solution)/shard_map/ppermute | solution.py:21
  38.6 0.9 fusion.133
  39.4 3.2 %collective-permute-start.8 = (f32[1,16,256]{2,0,1:T(1,128)S(1)}, f32[1,16,256]{2,0,1:T(1,128)S(1)}, u32[]{:S(2)}, u32[]{:S(2)}) collective-permute-start(f32[1,16,256]{2,0,1:T(1,128)S(1)} %get-tuple-element.41), channel_id=1, source_target_pairs={{0,4},{4,8},{8,12},{1,5},{5,9},{9,13},{2,6},{6,10},{10,14},{3,7},{... | collective-permute-start | bytes 49160 | tf_op jit(solution)/shard_map/ppermute | solution.py:20
  42.6 1.3 collective-permute-start.9
  44.5 2.6 %collective-permute-done.9 = f32[1,16,256]{2,0,1:T(1,128)S(1)} collective-permute-done((f32[1,16,256]{2,0,1:T(1,128)S(1)}, f32[1,16,256]{2,0,1:T(1,128)S(1)}, u32[]{:S(2)}, u32[]{:S(2)}) %collective-permute-start.9) | collective-permute-done | bytes 16416 | tf_op jit(solution)/shard_map/ppermute | solution.py:21
  47.8 3.3 %collective-permute-start.10 = (f32[18,1,256]{2,0,1:T(8,128)}, f32[18,1,256]{2,0,1:T(8,128)S(1)}, u32[]{:S(2)}, u32[]{:S(2)}) collective-permute-start(f32[18,1,256]{2,0,1:T(8,128)} %get-tuple-element.21), channel_id=1, source_target_pairs={{0,1},{1,2},{2,3},{4,5},{5,6},{6,7},{8,9},{9,10},{10,11},{12,13},{... | collective-permute-start | bytes 55304 | tf_op jit(solution)/shard_map/ppermute | solution.py:20
  51.1 1.9 %collective-permute-start.11 = (f32[18,1,256]{2,0,1:T(8,128)}, f32[18,1,256]{2,0,1:T(8,128)}, u32[]{:S(2)}, u32[]{:S(2)}) collective-permute-start(f32[18,1,256]{2,0,1:T(8,128)} %get-tuple-element.22), channel_id=1, source_target_pairs={{1,0},{2,1},{3,2},{5,4},{6,5},{7,6},{9,8},{10,9},{11,10},{13,12},{... | collective-permute-start | bytes 55304 | tf_op jit(solution)/shard_map/ppermute | solution.py:21
  53.0 0.9 bitcast_reduce_fusion
  54.0 4.5 %slice.560 = f32[16,16,128]{2,0,1:T(8,128)S(1)} slice(f32[16,16,256]{2,0,1:T(8,128)S(1)} %concatenate.178), slice={[0:16:1], [0:16:1], [1:256:2]} | slice | bytes 262144 | tf_op jit(solution)/shard_map/slice | solution.py:140
  58.5 1.7 fusion.47
  60.2 3.3 %collective-permute-start.12 = (f32[1,16,256]{2,0,1:T(1,128)S(1)}, f32[1,16,256]{2,0,1:T(1,128)S(1)}, u32[]{:S(2)}, u32[]{:S(2)}) collective-permute-start(f32[1,16,256]{2,0,1:T(1,128)S(1)} %get-tuple-element.37), channel_id=1, source_target_pairs={{0,4},{4,8},{8,12},{1,5},{5,9},{9,13},{2,6},{6,10},{10,14},{3,7},{... | collective-permute-start | bytes 49160 | tf_op jit(solution)/shard_map/ppermute | solution.py:20
  63.5 1.3 collective-permute-start.13
  64.9 1.9 %copy.78 = f32[16,16,256]{0,2,1:T(8,128)} copy(f32[16,16,256]{2,0,1:T(8,128)S(1)} %get-tuple-element.8) | data formatting | bytes 524288 | tf_op jit(solution)/shard_map/mul | solution.py:60
  67.0 2.0 %copy.74 = f32[16,16,256]{0,2,1:T(8,128)} copy(f32[16,16,256]{2,0,1:T(8,128)S(1)} %slice_multiply_fusion) | data formatting | bytes 524288 | tf_op jit(solution)/shard_map/mul | solution.py:138
  69.0 3.4 %reduce_sum.46 = f32[16,8,128]{0,2,1:T(8,128)S(1)} reduce(f32[16,8,2,128,2]{0,4,3,2,1:T(2,128)} %bitcast.185, f32[]{:T(128)} %constant.31.clone.1), dimensions={2,4}, to_apply=%region_1.2 | reduce | flops 49152 | bytes 327684 | tf_op jit(solution)/shard_map/reduce_sum | solution.py:124
  72.6 3.5 %reduce_sum.49 = f32[16,8,128]{0,2,1:T(8,128)S(1)} reduce(f32[16,8,2,128,2]{0,4,3,2,1:T(2,128)} %bitcast.183, f32[]{:T(128)} %constant.31.clone.1), dimensions={2,4}, to_apply=%region_4.5 | reduce | flops 49152 | bytes 327684 | tf_op jit(solution)/shard_map/reduce_sum | solution.py:124
  76.3 3.9 %collective-permute-start.14 = (f32[18,1,256]{2,0,1:T(8,128)S(1)}, f32[18,1,256]{2,0,1:T(8,128)S(1)}, u32[]{:S(2)}, u32[]{:S(2)}) collective-permute-start(f32[18,1,256]{2,0,1:T(8,128)S(1)} %get-tuple-element.19), channel_id=1, source_target_pairs={{0,1},{1,2},{2,3},{4,5},{5,6},{6,7},{8,9},{9,10},{10,11},{12,13},{... | collective-permute-start | bytes 55304 | tf_op jit(solution)/shard_map/ppermute | solution.py:20
  80.2 2.1 %collective-permute-start.15 = (f32[18,1,256]{2,0,1:T(8,128)S(1)}, f32[18,1,256]{2,0,1:T(8,128)S(1)}, u32[]{:S(2)}, u32[]{:S(2)}) collective-permute-start(f32[18,1,256]{2,0,1:T(8,128)S(1)} %get-tuple-element.20), channel_id=1, source_target_pairs={{1,0},{2,1},{3,2},{5,4},{6,5},{7,6},{9,8},{10,9},{11,10},{13,12},{... | collective-permute-start | bytes 55304 | tf_op jit(solution)/shard_map/ppermute | solution.py:21
  82.5 2.9 %collective-permute-done.15 = f32[18,1,256]{2,0,1:T(8,128)S(1)} collective-permute-done((f32[18,1,256]{2,0,1:T(8,128)S(1)}, f32[18,1,256]{2,0,1:T(8,128)S(1)}, u32[]{:S(2)}, u32[]{:S(2)}) %collective-permute-start.15) | collective-permute-done | bytes 18464 | tf_op jit(solution)/shard_map/ppermute | solution.py:21
  85.9 1.9 %copy.72 = f32[16,16,256]{0,2,1:T(8,128)} copy(f32[16,16,256]{2,0,1:T(8,128)S(1)} %fusion.33) | data formatting | bytes 524288 | tf_op jit(solution)/shard_map/sub | solution.py:119
  87.9 3.4 %reduce_sum.45 = f32[16,8,128]{0,2,1:T(8,128)S(1)} reduce(f32[16,8,2,128,2]{0,4,3,2,1:T(2,128)} %bitcast.184, f32[]{:T(128)} %constant.31.clone.1), dimensions={2,4}, to_apply=%region_0.1 | reduce | flops 49152 | bytes 327684 | tf_op jit(solution)/shard_map/reduce_sum | solution.py:124
  91.8 1.3 collective-permute-start.16
  93.1 4.1 %collective-permute-done.16 = f32[5,8,128]{2,1,0:T(8,128)S(1)} collective-permute-done((f32[5,8,128]{2,1,0:T(8,128)S(1)}, f32[5,8,128]{2,1,0:T(8,128)S(1)}, u32[]{:S(2)}, u32[]{:S(2)}) %collective-permute-start.16) | collective-permute-done | bytes 20512 | tf_op jit(solution)/shard_map/ppermute | solution.py:29
  97.6 1.3 collective-permute-start.18
  98.9 4.0 %collective-permute-start.17 = (f32[5,4,8,128]{3,1,2,0:T(4,128)S(1)}, f32[5,4,8,128]{3,1,2,0:T(4,128)S(1)}, u32[]{:S(2)}, u32[]{:S(2)}) collective-permute-start(f32[5,4,8,128]{3,1,2,0:T(4,128)S(1)} %get-tuple-element.13), channel_id=1, source_target_pairs={{0,4},{4,8},{8,12},{1,5},{5,9},{9,13},{2,6},{6,10},{10,14},{3,7},{... | collective-permute-start | bytes 245768 | tf_op jit(solution)/shard_map/ppermute | solution.py:20
  102.9 1.8 collective-permute-done.17
  104.8 0.8 fusion.125
  105.6 3.6 %collective-permute-start.19 = (f32[5,28,4,128]{3,1,2,0:T(8,128)}, f32[5,28,4,128]{3,1,2,0:T(8,128)S(1)}, u32[]{:S(2)}, u32[]{:S(2)}) collective-permute-start(f32[5,28,4,128]{3,1,2,0:T(8,128)} %get-tuple-element.9), channel_id=1, source_target_pairs={{0,1},{1,2},{2,3},{4,5},{5,6},{6,7},{8,9},{9,10},{10,11},{12,13},{... | collective-permute-start | bytes 860168 | tf_op jit(solution)/shard_map/ppermute | solution.py:20
  109.2 1.9 %collective-permute-start.20 = (f32[5,28,4,128]{3,1,2,0:T(8,128)S(1)}, f32[5,28,4,128]{3,1,2,0:T(8,128)S(1)}, u32[]{:S(2)}, u32[]{:S(2)}) collective-permute-start(f32[5,28,4,128]{3,1,2,0:T(8,128)S(1)} %get-tuple-element.10), channel_id=1, source_target_pairs={{1,0},{2,1},{3,2},{5,4},{6,5},{7,6},{9,8},{10,9},{11,10},{13,12},{... | collective-permute-start | bytes 860168 | tf_op jit(solution)/shard_map/ppermute | solution.py:21
  111.1 2.4 %collective-permute-done.19 = f32[5,28,4,128]{3,1,2,0:T(8,128)S(1)} collective-permute-done((f32[5,28,4,128]{3,1,2,0:T(8,128)}, f32[5,28,4,128]{3,1,2,0:T(8,128)S(1)}, u32[]{:S(2)}, u32[]{:S(2)}) %collective-permute-start.19) | collective-permute-done | bytes 286752 | tf_op jit(solution)/shard_map/ppermute | solution.py:20
  113.5 4.1 %collective-permute-done.20 = f32[5,28,4,128]{3,1,2,0:T(8,128)S(1)} collective-permute-done((f32[5,28,4,128]{3,1,2,0:T(8,128)S(1)}, f32[5,28,4,128]{3,1,2,0:T(8,128)S(1)}, u32[]{:S(2)}, u32[]{:S(2)}) %collective-permute-start.20) | collective-permute-done | bytes 286752 | tf_op jit(solution)/shard_map/ppermute | solution.py:21
  118.6 0.9 copy-done.3
  120.3 4.8 %dynamic_update_slice.7 = f32[5,24,16,128]{3,1,2,0:T(8,128)S(1)} dynamic-update-slice(f32[5,24,16,128]{3,1,2,0:T(8,128)S(1)} %slice.672, f32[5,4,16,128]{3,1,2,0:T(4,128)} %pad_maximum_fusion.44, s32[]{:T(128)} %constant.25.clone.1, s32[]{:T(128)S(6)} %select_n.65, s32[]{:T(128)} %constant.25.clone.1, s32[]{:T(128)} %constant.25.clone.1) | dynamic-update-slice | bytes 327684 | tf_op jit(solution)/shard_map/dynamic_update_slice | solution.py:159
  126.4 1.3 collective-permute-start.22
  127.7 4.6 %collective-permute-start.21 = (f32[1,1,8,128]{3,1,2,0:T(1,128)S(1)}, f32[1,1,8,128]{3,1,2,0:T(1,128)S(1)}, u32[]{:S(2)}, u32[]{:S(2)}) collective-permute-start(f32[1,1,8,128]{3,1,2,0:T(1,128)S(1)} %dynamic-slice_bitcast_fusion), channel_id=1, source_target_pairs={{0,4},{4,8},{8,12},{1,5},{5,9},{9,13},{2,6},{6,10},{10,14},{3,7},{... | collective-permute-start | bytes 12296 | tf_op jit(solution)/shard_map/ppermute | solution.py:20
  133.0 2.6 %collective-permute-start.23 = (f32[1,19,1,128]{3,1,2,0:T(8,128)S(1)}, f32[1,19,1,128]{3,1,2,0:T(8,128)S(1)}, u32[]{:S(2)}, u32[]{:S(2)}) collective-permute-start(f32[1,19,1,128]{3,1,2,0:T(8,128)S(1)} %get-tuple-element.55), channel_id=1, source_target_pairs={{0,1},{1,2},{2,3},{4,5},{5,6},{6,7},{8,9},{9,10},{10,11},{12,13},{... | collective-permute-start | bytes 29192 | tf_op jit(solution)/shard_map/ppermute | solution.py:20
  135.6 1.9 %collective-permute-start.24 = (f32[1,19,1,128]{3,1,2,0:T(8,128)S(1)}, f32[1,19,1,128]{3,1,2,0:T(8,128)S(1)}, u32[]{:S(2)}, u32[]{:S(2)}) collective-permute-start(f32[1,19,1,128]{3,1,2,0:T(8,128)S(1)} %get-tuple-element.56), channel_id=1, source_target_pairs={{1,0},{2,1},{3,2},{5,4},{6,5},{7,6},{9,8},{10,9},{11,10},{13,12},{... | collective-permute-start | bytes 29192 | tf_op jit(solution)/shard_map/ppermute | solution.py:21
  137.6 3.1 %collective-permute-done.24 = f32[1,19,1,128]{3,1,2,0:T(8,128)S(1)} collective-permute-done((f32[1,19,1,128]{3,1,2,0:T(8,128)S(1)}, f32[1,19,1,128]{3,1,2,0:T(8,128)S(1)}, u32[]{:S(2)}, u32[]{:S(2)}) %collective-permute-start.24) | collective-permute-done | bytes 9760 | tf_op jit(solution)/shard_map/ppermute | solution.py:21
  141.5 1.5 broadcast_in_dim.131
  143.0 2.6 %copy.81 = f32[16,16,256]{2,0,1:T(8,128)S(1)} copy(f32[16,16,256]{1,0,2:T(8,128)} %bitcast.182) | data formatting | bytes 524288 | tf_op jit(solution)/shard_map/reshape | solution.py:216
  145.7 3.9 %collective-permute-start.25 = (f32[1,16,256]{2,0,1:T(1,128)S(1)}, f32[1,16,256]{2,0,1:T(1,128)S(1)}, u32[]{:S(2)}, u32[]{:S(2)}) collective-permute-start(f32[1,16,256]{2,0,1:T(1,128)S(1)} %get-tuple-element.33), channel_id=1, source_target_pairs={{0,4},{4,8},{8,12},{1,5},{5,9},{9,13},{2,6},{6,10},{10,14},{3,7},{... | collective-permute-start | bytes 49160 | tf_op jit(solution)/shard_map/ppermute | solution.py:20
  149.6 1.3 collective-permute-start.26
  150.9 3.5 %collective-permute-done.26 = f32[1,16,256]{2,0,1:T(1,128)S(1)} collective-permute-done((f32[1,16,256]{2,0,1:T(1,128)S(1)}, f32[1,16,256]{2,0,1:T(1,128)S(1)}, u32[]{:S(2)}, u32[]{:S(2)}) %collective-permute-start.26) | collective-permute-done | bytes 16416 | tf_op jit(solution)/shard_map/ppermute | solution.py:21
  154.4 3.1 %collective-permute-start.27 = (f32[18,1,256]{2,0,1:T(8,128)S(1)}, f32[18,1,256]{2,0,1:T(8,128)S(1)}, u32[]{:S(2)}, u32[]{:S(2)}) collective-permute-start(f32[18,1,256]{2,0,1:T(8,128)S(1)} %get-tuple-element.17), channel_id=1, source_target_pairs={{0,1},{1,2},{2,3},{4,5},{5,6},{6,7},{8,9},{9,10},{10,11},{12,13},{... | collective-permute-start | bytes 55304 | tf_op jit(solution)/shard_map/ppermute | solution.py:20
  157.5 1.9 %collective-permute-start.28 = (f32[18,1,256]{2,0,1:T(8,128)S(1)}, f32[18,1,256]{2,0,1:T(8,128)S(1)}, u32[]{:S(2)}, u32[]{:S(2)}) collective-permute-start(f32[18,1,256]{2,0,1:T(8,128)S(1)} %get-tuple-element.18), channel_id=1, source_target_pairs={{1,0},{2,1},{3,2},{5,4},{6,5},{7,6},{9,8},{10,9},{11,10},{13,12},{... | collective-permute-start | bytes 55304 | tf_op jit(solution)/shard_map/ppermute | solution.py:21
  159.6 3.1 %collective-permute-done.28 = f32[18,1,256]{2,0,1:T(8,128)S(1)} collective-permute-done((f32[18,1,256]{2,0,1:T(8,128)S(1)}, f32[18,1,256]{2,0,1:T(8,128)S(1)}, u32[]{:S(2)}, u32[]{:S(2)}) %collective-permute-start.28) | collective-permute-done | bytes 18464 | tf_op jit(solution)/shard_map/ppermute | solution.py:21
  163.3 3.6 %collective-permute-start.29 = (f32[1,16,256]{2,0,1:T(1,128)S(1)}, f32[1,16,256]{2,0,1:T(1,128)S(1)}, u32[]{:S(2)}, u32[]{:S(2)}) collective-permute-start(f32[1,16,256]{2,0,1:T(1,128)S(1)} %get-tuple-element.29), channel_id=1, source_target_pairs={{0,4},{4,8},{8,12},{1,5},{5,9},{9,13},{2,6},{6,10},{10,14},{3,7},{... | collective-permute-start | bytes 49160 | tf_op jit(solution)/shard_map/ppermute | solution.py:20
  166.9 1.3 collective-permute-start.30
  168.2 3.5 %collective-permute-done.30 = f32[1,16,256]{2,0,1:T(1,128)S(1)} collective-permute-done((f32[1,16,256]{2,0,1:T(1,128)S(1)}, f32[1,16,256]{2,0,1:T(1,128)S(1)}, u32[]{:S(2)}, u32[]{:S(2)}) %collective-permute-start.30) | collective-permute-done | bytes 16416 | tf_op jit(solution)/shard_map/ppermute | solution.py:21
  171.7 3.1 %collective-permute-start.31 = (f32[18,1,256]{2,0,1:T(8,128)S(1)}, f32[18,1,256]{2,0,1:T(8,128)S(1)}, u32[]{:S(2)}, u32[]{:S(2)}) collective-permute-start(f32[18,1,256]{2,0,1:T(8,128)S(1)} %get-tuple-element.15), channel_id=1, source_target_pairs={{0,1},{1,2},{2,3},{4,5},{5,6},{6,7},{8,9},{9,10},{10,11},{12,13},{... | collective-permute-start | bytes 55304 | tf_op jit(solution)/shard_map/ppermute | solution.py:20
  174.8 1.9 %collective-permute-start.32 = (f32[18,1,256]{2,0,1:T(8,128)S(1)}, f32[18,1,256]{2,0,1:T(8,128)S(1)}, u32[]{:S(2)}, u32[]{:S(2)}) collective-permute-start(f32[18,1,256]{2,0,1:T(8,128)S(1)} %get-tuple-element.16), channel_id=1, source_target_pairs={{1,0},{2,1},{3,2},{5,4},{6,5},{7,6},{9,8},{10,9},{11,10},{13,12},{... | collective-permute-start | bytes 55304 | tf_op jit(solution)/shard_map/ppermute | solution.py:21
  176.9 3.1 %collective-permute-done.32 = f32[18,1,256]{2,0,1:T(8,128)S(1)} collective-permute-done((f32[18,1,256]{2,0,1:T(8,128)S(1)}, f32[18,1,256]{2,0,1:T(8,128)S(1)}, u32[]{:S(2)}, u32[]{:S(2)}) %collective-permute-start.32) | collective-permute-done | bytes 18464 | tf_op jit(solution)/shard_map/ppermute | solution.py:21
  180.5 0.9 copy.84
  (128 shorter events, 14.8 us)
Async XLA Ops:
  0.0 21.2 %copy-start.6 = (f32[16,16,256]{2,1,0:T(8,128)S(1)}, f32[16,16,256]{2,1,0:T(8,128)}, u32[]{:S(2)}) copy-start(f32[16,16,256]{2,1,0:T(8,128)} %param.4) | copy-start | bytes 786436
  0.8 28.1 %collective-permute-start.5 = (f32[1,16,256]{2,0,1:T(1,128)S(1)}, f32[1,16,256]{2,0,1:T(1,128)S(1)}, u32[]{:S(2)}, u32[]{:S(2)}) collective-permute-start(f32[1,16,256]{2,0,1:T(1,128)S(1)} %copy.63), channel_id=1, source_target_pairs={{4,0},{8,4},{12,8},{5,1},{9,5},{13,9},{6,2},{10,6},{14,10},{7,3},{... | collective-permute-start | bytes 49160 | tf_op jit(solution)/shard_map/ppermute | solution.py:21
  2.1 26.8 %collective-permute-start.4 = (f32[1,16,256]{2,0,1:T(1,128)S(1)}, f32[1,16,256]{2,0,1:T(1,128)S(1)}, u32[]{:S(2)}, u32[]{:S(2)}) collective-permute-start(f32[1,16,256]{2,0,1:T(1,128)S(1)} %copy.61), channel_id=1, source_target_pairs={{0,4},{4,8},{8,12},{1,5},{5,9},{9,13},{2,6},{6,10},{10,14},{3,7},{... | collective-permute-start | bytes 49160 | tf_op jit(solution)/shard_map/ppermute | solution.py:20
  7.6 14.4 %collective-permute-start.1 = (f32[1,16,256]{2,0,1:T(1,128)S(1)}, f32[1,16,256]{2,0,1:T(1,128)S(1)}, u32[]{:S(2)}, u32[]{:S(2)}) collective-permute-start(f32[1,16,256]{2,0,1:T(1,128)S(1)} %copy.57), channel_id=1, source_target_pairs={{4,0},{8,4},{12,8},{5,1},{9,5},{13,9},{6,2},{10,6},{14,10},{7,3},{... | collective-permute-start | bytes 49160 | tf_op jit(solution)/shard_map/ppermute | solution.py:21
  8.9 13.1 %collective-permute-start = (f32[1,16,256]{2,0,1:T(1,128)S(1)}, f32[1,16,256]{2,0,1:T(1,128)S(1)}, u32[]{:S(2)}, u32[]{:S(2)}) collective-permute-start(f32[1,16,256]{2,0,1:T(1,128)S(1)} %copy.56), channel_id=1, source_target_pairs={{0,4},{4,8},{8,12},{1,5},{5,9},{9,13},{2,6},{6,10},{10,14},{3,7},{... | collective-permute-start | bytes 49160 | tf_op jit(solution)/shard_map/ppermute | solution.py:20
  22.0 12.5 %collective-permute-start.2 = (f32[18,1,256]{2,0,1:T(8,128)S(1)}, f32[18,1,256]{2,0,1:T(8,128)S(1)}, u32[]{:S(2)}, u32[]{:S(2)}) collective-permute-start(f32[18,1,256]{2,0,1:T(8,128)S(1)} %get-tuple-element.23), channel_id=1, source_target_pairs={{0,1},{1,2},{2,3},{4,5},{5,6},{6,7},{8,9},{9,10},{10,11},{12,13},{... | collective-permute-start | bytes 55304 | tf_op jit(solution)/shard_map/ppermute | solution.py:20
  27.0 7.6 %collective-permute-start.3 = (f32[18,1,256]{2,0,1:T(8,128)S(1)}, f32[18,1,256]{2,0,1:T(8,128)S(1)}, u32[]{:S(2)}, u32[]{:S(2)}) collective-permute-start(f32[18,1,256]{2,0,1:T(8,128)S(1)} %get-tuple-element.24), channel_id=1, source_target_pairs={{1,0},{2,1},{3,2},{5,4},{6,5},{7,6},{9,8},{10,9},{11,10},{13,12},{... | collective-permute-start | bytes 55304 | tf_op jit(solution)/shard_map/ppermute | solution.py:21
  29.0 6.3 %collective-permute-start.6 = (f32[18,1,256]{2,0,1:T(8,128)S(1)}, f32[18,1,256]{2,0,1:T(8,128)S(1)}, u32[]{:S(2)}, u32[]{:S(2)}) collective-permute-start(f32[18,1,256]{2,0,1:T(8,128)S(1)} %get-tuple-element.25), channel_id=1, source_target_pairs={{0,1},{1,2},{2,3},{4,5},{5,6},{6,7},{8,9},{9,10},{10,11},{12,13},{... | collective-permute-start | bytes 55304 | tf_op jit(solution)/shard_map/ppermute | solution.py:20
  32.6 5.1 %collective-permute-start.7 = (f32[18,1,256]{2,0,1:T(8,128)S(1)}, f32[18,1,256]{2,0,1:T(8,128)S(1)}, u32[]{:S(2)}, u32[]{:S(2)}) collective-permute-start(f32[18,1,256]{2,0,1:T(8,128)S(1)} %get-tuple-element.26), channel_id=1, source_target_pairs={{1,0},{2,1},{3,2},{5,4},{6,5},{7,6},{9,8},{10,9},{11,10},{13,12},{... | collective-permute-start | bytes 55304 | tf_op jit(solution)/shard_map/ppermute | solution.py:21
  34.8 2.9 %copy-start = (f32[16,16,256]{2,1,0:T(8,128)S(1)}, f32[16,16,256]{2,1,0:T(8,128)}, u32[]{:S(2)}) copy-start(f32[16,16,256]{2,1,0:T(8,128)} %param.5) | copy-start | bytes 786436
  39.4 5.1 %collective-permute-start.8 = (f32[1,16,256]{2,0,1:T(1,128)S(1)}, f32[1,16,256]{2,0,1:T(1,128)S(1)}, u32[]{:S(2)}, u32[]{:S(2)}) collective-permute-start(f32[1,16,256]{2,0,1:T(1,128)S(1)} %get-tuple-element.41), channel_id=1, source_target_pairs={{0,4},{4,8},{8,12},{1,5},{5,9},{9,13},{2,6},{6,10},{10,14},{3,7},{... | collective-permute-start | bytes 49160 | tf_op jit(solution)/shard_map/ppermute | solution.py:20
  42.6 4.5 %collective-permute-start.9 = (f32[1,16,256]{2,0,1:T(1,128)S(1)}, f32[1,16,256]{2,0,1:T(1,128)S(1)}, u32[]{:S(2)}, u32[]{:S(2)}) collective-permute-start(f32[1,16,256]{2,0,1:T(1,128)S(1)} %get-tuple-element.42), channel_id=1, source_target_pairs={{4,0},{8,4},{12,8},{5,1},{9,5},{13,9},{6,2},{10,6},{14,10},{7,3},{... | collective-permute-start | bytes 49160 | tf_op jit(solution)/shard_map/ppermute | solution.py:21
  47.8 10.7 %collective-permute-start.10 = (f32[18,1,256]{2,0,1:T(8,128)}, f32[18,1,256]{2,0,1:T(8,128)S(1)}, u32[]{:S(2)}, u32[]{:S(2)}) collective-permute-start(f32[18,1,256]{2,0,1:T(8,128)} %get-tuple-element.21), channel_id=1, source_target_pairs={{0,1},{1,2},{2,3},{4,5},{5,6},{6,7},{8,9},{9,10},{10,11},{12,13},{... | collective-permute-start | bytes 55304 | tf_op jit(solution)/shard_map/ppermute | solution.py:20
  51.1 7.4 %collective-permute-start.11 = (f32[18,1,256]{2,0,1:T(8,128)}, f32[18,1,256]{2,0,1:T(8,128)}, u32[]{:S(2)}, u32[]{:S(2)}) collective-permute-start(f32[18,1,256]{2,0,1:T(8,128)} %get-tuple-element.22), channel_id=1, source_target_pairs={{1,0},{2,1},{3,2},{5,4},{6,5},{7,6},{9,8},{10,9},{11,10},{13,12},{... | collective-permute-start | bytes 55304 | tf_op jit(solution)/shard_map/ppermute | solution.py:21
  60.2 6.7 %copy-start.1 = (f32[16,8,128]{0,1,2:T(8,128)S(1)}, f32[16,8,128]{0,1,2:T(8,128)}, u32[]{:S(2)}) copy-start(f32[16,8,128]{0,1,2:T(8,128)} %bitcast_reduce_fusion) | copy-start | bytes 196612
  60.2 16.0 %collective-permute-start.12 = (f32[1,16,256]{2,0,1:T(1,128)S(1)}, f32[1,16,256]{2,0,1:T(1,128)S(1)}, u32[]{:S(2)}, u32[]{:S(2)}) collective-permute-start(f32[1,16,256]{2,0,1:T(1,128)S(1)} %get-tuple-element.37), channel_id=1, source_target_pairs={{0,4},{4,8},{8,12},{1,5},{5,9},{9,13},{2,6},{6,10},{10,14},{3,7},{... | collective-permute-start | bytes 49160 | tf_op jit(solution)/shard_map/ppermute | solution.py:20
  63.5 12.7 %collective-permute-start.13 = (f32[1,16,256]{2,0,1:T(1,128)S(1)}, f32[1,16,256]{2,0,1:T(1,128)S(1)}, u32[]{:S(2)}, u32[]{:S(2)}) collective-permute-start(f32[1,16,256]{2,0,1:T(1,128)S(1)} %get-tuple-element.38), channel_id=1, source_target_pairs={{4,0},{8,4},{12,8},{5,1},{9,5},{13,9},{6,2},{10,6},{14,10},{7,3},{... | collective-permute-start | bytes 49160 | tf_op jit(solution)/shard_map/ppermute | solution.py:21
  76.3 6.2 %collective-permute-start.14 = (f32[18,1,256]{2,0,1:T(8,128)S(1)}, f32[18,1,256]{2,0,1:T(8,128)S(1)}, u32[]{:S(2)}, u32[]{:S(2)}) collective-permute-start(f32[18,1,256]{2,0,1:T(8,128)S(1)} %get-tuple-element.19), channel_id=1, source_target_pairs={{0,1},{1,2},{2,3},{4,5},{5,6},{6,7},{8,9},{9,10},{10,11},{12,13},{... | collective-permute-start | bytes 55304 | tf_op jit(solution)/shard_map/ppermute | solution.py:20
  80.2 5.1 %collective-permute-start.15 = (f32[18,1,256]{2,0,1:T(8,128)S(1)}, f32[18,1,256]{2,0,1:T(8,128)S(1)}, u32[]{:S(2)}, u32[]{:S(2)}) collective-permute-start(f32[18,1,256]{2,0,1:T(8,128)S(1)} %get-tuple-element.20), channel_id=1, source_target_pairs={{1,0},{2,1},{3,2},{5,4},{6,5},{7,6},{9,8},{10,9},{11,10},{13,12},{... | collective-permute-start | bytes 55304 | tf_op jit(solution)/shard_map/ppermute | solution.py:21
  91.8 5.4 %collective-permute-start.16 = (f32[5,8,128]{2,1,0:T(8,128)S(1)}, f32[5,8,128]{2,1,0:T(8,128)S(1)}, u32[]{:S(2)}, u32[]{:S(2)}) collective-permute-start(f32[5,8,128]{2,1,0:T(8,128)S(1)} %bitcast.195), channel_id=1, source_target_pairs={{4,0},{8,4},{12,8},{5,1},{9,5},{13,9},{6,2},{10,6},{14,10},{7,3},{... | collective-permute-start | bytes 61448 | tf_op jit(solution)/shard_map/ppermute | solution.py:29
  97.6 5.4 %collective-permute-start.18 = (f32[5,4,8,128]{3,1,2,0:T(4,128)S(1)}, f32[5,4,8,128]{3,1,2,0:T(4,128)S(1)}, u32[]{:S(2)}, u32[]{:S(2)}) collective-permute-start(f32[5,4,8,128]{3,1,2,0:T(4,128)S(1)} %get-tuple-element.14), channel_id=1, source_target_pairs={{4,0},{8,4},{12,8},{5,1},{9,5},{13,9},{6,2},{10,6},{14,10},{7,3},{... | collective-permute-start | bytes 245768 | tf_op jit(solution)/shard_map/ppermute | solution.py:21
  98.9 5.8 %collective-permute-start.17 = (f32[5,4,8,128]{3,1,2,0:T(4,128)S(1)}, f32[5,4,8,128]{3,1,2,0:T(4,128)S(1)}, u32[]{:S(2)}, u32[]{:S(2)}) collective-permute-start(f32[5,4,8,128]{3,1,2,0:T(4,128)S(1)} %get-tuple-element.13), channel_id=1, source_target_pairs={{0,4},{4,8},{8,12},{1,5},{5,9},{9,13},{2,6},{6,10},{10,14},{3,7},{... | collective-permute-start | bytes 245768 | tf_op jit(solution)/shard_map/ppermute | solution.py:20
  105.6 7.9 %collective-permute-start.19 = (f32[5,28,4,128]{3,1,2,0:T(8,128)}, f32[5,28,4,128]{3,1,2,0:T(8,128)S(1)}, u32[]{:S(2)}, u32[]{:S(2)}) collective-permute-start(f32[5,28,4,128]{3,1,2,0:T(8,128)} %get-tuple-element.9), channel_id=1, source_target_pairs={{0,1},{1,2},{2,3},{4,5},{5,6},{6,7},{8,9},{9,10},{10,11},{12,13},{... | collective-permute-start | bytes 860168 | tf_op jit(solution)/shard_map/ppermute | solution.py:20
  109.2 8.4 %collective-permute-start.20 = (f32[5,28,4,128]{3,1,2,0:T(8,128)S(1)}, f32[5,28,4,128]{3,1,2,0:T(8,128)S(1)}, u32[]{:S(2)}, u32[]{:S(2)}) collective-permute-start(f32[5,28,4,128]{3,1,2,0:T(8,128)S(1)} %get-tuple-element.10), channel_id=1, source_target_pairs={{1,0},{2,1},{3,2},{5,4},{6,5},{7,6},{9,8},{10,9},{11,10},{13,12},{... | collective-permute-start | bytes 860168 | tf_op jit(solution)/shard_map/ppermute | solution.py:21
  113.5 4.1 %copy-start.2 = (f32[5,28,4,128]{3,1,2,0:T(8,128)}, f32[5,28,4,128]{3,1,2,0:T(8,128)S(1)}, u32[]{:S(2)}) copy-start(f32[5,28,4,128]{3,1,2,0:T(8,128)S(1)} %collective-permute-done.19) | copy-start | bytes 860164
  117.6 0.7 copy-start.4
  118.5 1.0 copy-start.3
  118.5 1.1 copy-start.5
  126.4 5.9 %collective-permute-start.22 = (f32[1,1,8,128]{3,1,2,0:T(1,128)S(1)}, f32[1,1,8,128]{3,1,2,0:T(1,128)S(1)}, u32[]{:S(2)}, u32[]{:S(2)}) collective-permute-start(f32[1,1,8,128]{3,1,2,0:T(1,128)S(1)} %slice.726), channel_id=1, source_target_pairs={{4,0},{8,4},{12,8},{5,1},{9,5},{13,9},{6,2},{10,6},{14,10},{7,3},{... | collective-permute-start | bytes 12296 | tf_op jit(solution)/shard_map/ppermute | solution.py:21
  127.7 5.4 %collective-permute-start.21 = (f32[1,1,8,128]{3,1,2,0:T(1,128)S(1)}, f32[1,1,8,128]{3,1,2,0:T(1,128)S(1)}, u32[]{:S(2)}, u32[]{:S(2)}) collective-permute-start(f32[1,1,8,128]{3,1,2,0:T(1,128)S(1)} %dynamic-slice_bitcast_fusion), channel_id=1, source_target_pairs={{0,4},{4,8},{8,12},{1,5},{5,9},{9,13},{2,6},{6,10},{10,14},{3,7},{... | collective-permute-start | bytes 12296 | tf_op jit(solution)/shard_map/ppermute | solution.py:20
  133.0 4.5 %collective-permute-start.23 = (f32[1,19,1,128]{3,1,2,0:T(8,128)S(1)}, f32[1,19,1,128]{3,1,2,0:T(8,128)S(1)}, u32[]{:S(2)}, u32[]{:S(2)}) collective-permute-start(f32[1,19,1,128]{3,1,2,0:T(8,128)S(1)} %get-tuple-element.55), channel_id=1, source_target_pairs={{0,1},{1,2},{2,3},{4,5},{5,6},{6,7},{8,9},{9,10},{10,11},{12,13},{... | collective-permute-start | bytes 29192 | tf_op jit(solution)/shard_map/ppermute | solution.py:20
  135.6 5.0 %collective-permute-start.24 = (f32[1,19,1,128]{3,1,2,0:T(8,128)S(1)}, f32[1,19,1,128]{3,1,2,0:T(8,128)S(1)}, u32[]{:S(2)}, u32[]{:S(2)}) collective-permute-start(f32[1,19,1,128]{3,1,2,0:T(8,128)S(1)} %get-tuple-element.56), channel_id=1, source_target_pairs={{1,0},{2,1},{3,2},{5,4},{6,5},{7,6},{9,8},{10,9},{11,10},{13,12},{... | collective-permute-start | bytes 29192 | tf_op jit(solution)/shard_map/ppermute | solution.py:21
  145.7 5.2 %collective-permute-start.25 = (f32[1,16,256]{2,0,1:T(1,128)S(1)}, f32[1,16,256]{2,0,1:T(1,128)S(1)}, u32[]{:S(2)}, u32[]{:S(2)}) collective-permute-start(f32[1,16,256]{2,0,1:T(1,128)S(1)} %get-tuple-element.33), channel_id=1, source_target_pairs={{0,4},{4,8},{8,12},{1,5},{5,9},{9,13},{2,6},{6,10},{10,14},{3,7},{... | collective-permute-start | bytes 49160 | tf_op jit(solution)/shard_map/ppermute | solution.py:20
  149.6 4.8 %collective-permute-start.26 = (f32[1,16,256]{2,0,1:T(1,128)S(1)}, f32[1,16,256]{2,0,1:T(1,128)S(1)}, u32[]{:S(2)}, u32[]{:S(2)}) collective-permute-start(f32[1,16,256]{2,0,1:T(1,128)S(1)} %get-tuple-element.34), channel_id=1, source_target_pairs={{4,0},{8,4},{12,8},{5,1},{9,5},{13,9},{6,2},{10,6},{14,10},{7,3},{... | collective-permute-start | bytes 49160 | tf_op jit(solution)/shard_map/ppermute | solution.py:21
  154.4 5.2 %collective-permute-start.27 = (f32[18,1,256]{2,0,1:T(8,128)S(1)}, f32[18,1,256]{2,0,1:T(8,128)S(1)}, u32[]{:S(2)}, u32[]{:S(2)}) collective-permute-start(f32[18,1,256]{2,0,1:T(8,128)S(1)} %get-tuple-element.17), channel_id=1, source_target_pairs={{0,1},{1,2},{2,3},{4,5},{5,6},{6,7},{8,9},{9,10},{10,11},{12,13},{... | collective-permute-start | bytes 55304 | tf_op jit(solution)/shard_map/ppermute | solution.py:20
  157.5 5.1 %collective-permute-start.28 = (f32[18,1,256]{2,0,1:T(8,128)S(1)}, f32[18,1,256]{2,0,1:T(8,128)S(1)}, u32[]{:S(2)}, u32[]{:S(2)}) collective-permute-start(f32[18,1,256]{2,0,1:T(8,128)S(1)} %get-tuple-element.18), channel_id=1, source_target_pairs={{1,0},{2,1},{3,2},{5,4},{6,5},{7,6},{9,8},{10,9},{11,10},{13,12},{... | collective-permute-start | bytes 55304 | tf_op jit(solution)/shard_map/ppermute | solution.py:21
  163.3 4.9 %collective-permute-start.29 = (f32[1,16,256]{2,0,1:T(1,128)S(1)}, f32[1,16,256]{2,0,1:T(1,128)S(1)}, u32[]{:S(2)}, u32[]{:S(2)}) collective-permute-start(f32[1,16,256]{2,0,1:T(1,128)S(1)} %get-tuple-element.29), channel_id=1, source_target_pairs={{0,4},{4,8},{8,12},{1,5},{5,9},{9,13},{2,6},{6,10},{10,14},{3,7},{... | collective-permute-start | bytes 49160 | tf_op jit(solution)/shard_map/ppermute | solution.py:20
  166.9 4.8 %collective-permute-start.30 = (f32[1,16,256]{2,0,1:T(1,128)S(1)}, f32[1,16,256]{2,0,1:T(1,128)S(1)}, u32[]{:S(2)}, u32[]{:S(2)}) collective-permute-start(f32[1,16,256]{2,0,1:T(1,128)S(1)} %get-tuple-element.30), channel_id=1, source_target_pairs={{4,0},{8,4},{12,8},{5,1},{9,5},{13,9},{6,2},{10,6},{14,10},{7,3},{... | collective-permute-start | bytes 49160 | tf_op jit(solution)/shard_map/ppermute | solution.py:21
  171.7 5.2 %collective-permute-start.31 = (f32[18,1,256]{2,0,1:T(8,128)S(1)}, f32[18,1,256]{2,0,1:T(8,128)S(1)}, u32[]{:S(2)}, u32[]{:S(2)}) collective-permute-start(f32[18,1,256]{2,0,1:T(8,128)S(1)} %get-tuple-element.15), channel_id=1, source_target_pairs={{0,1},{1,2},{2,3},{4,5},{5,6},{6,7},{8,9},{9,10},{10,11},{12,13},{... | collective-permute-start | bytes 55304 | tf_op jit(solution)/shard_map/ppermute | solution.py:20
  174.8 5.1 %collective-permute-start.32 = (f32[18,1,256]{2,0,1:T(8,128)S(1)}, f32[18,1,256]{2,0,1:T(8,128)S(1)}, u32[]{:S(2)}, u32[]{:S(2)}) collective-permute-start(f32[18,1,256]{2,0,1:T(8,128)S(1)} %get-tuple-element.16), channel_id=1, source_target_pairs={{1,0},{2,1},{3,2},{5,4},{6,5},{7,6},{9,8},{10,9},{11,10},{13,12},{... | collective-permute-start | bytes 55304 | tf_op jit(solution)/shard_map/ppermute | solution.py:21
where the time goes:
time: 183 us; the launch traced here: 181 us
  starting transfers between devices  86.7 us (47%)
  waiting for transfers between devices  37.2 us (20%)
  local copies, waits for them, and re-layouts  31.6 us (17%)
  other arithmetic  21.6 us (12%)
  between operations  3.57 us (2%)
    ppermute x16, starting transfers between devices, padded(): before = lax.ppermute(last, axis, up)  59.5 us
    ppermute x16, waiting for transfers between devices, padded(): after = lax.ppermute(leading, axis, down)  28.2 us
    ppermute x16, starting transfers between devices, padded(): after = lax.ppermute(leading, axis, down)  25.9 us
    reduce_sum x3, other arithmetic, pair_sum(): return block_in.reshape(width_x, half_y, 2, half_z, 2).sum(axis=(2, 4))  10.4 us
    ppermute x16, waiting for transfers between devices, padded(): before = lax.ppermute(last, axis, up)  4.89 us
    dynamic_update_slice x2, local copies, waits for them, and re-layouts, coarse_extend(): lax.dynamic_update_slice_in_dim(base_block, ahead_planes, rim_width + cou...  4.83 us
    slice x1, local copies, waits for them, and re-layouts, body(): face_above[:, :, 1::2].reshape(width_x, half_y, 2, half_z).sum(axis=2)  4.49 us
    ppermute x1, waiting for transfers between devices, passed_along(): return lax.ppermute(array, axis, pairs)  4.12 us
  transfers between devices with their start and end apart: 33, of which 14 were waited for; matrix products, arithmetic and copies ran while one was open for 14% of the time, Pallas kernels for 0%

commit v1 on v0

--- a/solution.py
+++ b/solution.py
@@ -87,8 +87,23 @@
     return (center, safe_diag * center - beside_all)
 
 
-def fine_halo(field_in):
-    return padded(field_in, (("slab", 0), (("pencil", "sub"), 1)), 1)
+def crop(array, rim):
+    if rim == 0:
+        return array
+    return array[rim : array.shape[0] - rim, rim : array.shape[1] - rim]
+
+
+def sweeps(field_ext, source_ext, faces_ext, count, width):
+    def rim_of(array):
+        return (array.shape[0] - width) // 2
+
+    for sweep_index in range(count):
+        out_rim = rim_of(field_ext) - 1
+        faces_now = tuple(crop(member, rim_of(member) - out_rim) for member in faces_ext)
+        center, product = apply_fine(field_ext, faces_now)
+        source_now = crop(source_ext, rim_of(source_ext) - out_rim)
+        field_ext = center + OMEGA * (source_now - product) / faces_now[7]
+    return field_ext
 
 
 def body(permeability, source, pressure, aggregate):
@@ -99,23 +114,21 @@
     row_count = lax.axis_size(("pencil", "sub"))
     total_x = width_x * slab_count
     total_y = width_y * row_count
-    fine_rim = 1
-    perm_ext = padded(permeability, (("slab", 0), (("pencil", "sub"), 1)), fine_rim)
+    sides = (("slab", 0), (("pencil", "sub"), 1))
+    stacked_sides = (("slab", 1), (("pencil", "sub"), 2))
+    fine_rim = NU + 1
+    ext_all = padded(jnp.stack([permeability, source, pressure]), stacked_sides, fine_rim)
+    perm_ext = ext_all[0]
+    source_ext = crop(ext_all[1], 1)
     glob_x = slab_index * width_x - fine_rim + jnp.arange(width_x + 2 * fine_rim)
     glob_y = row_index * width_y - fine_rim + jnp.arange(width_y + 2 * fine_rim)
     inside_x = (glob_x >= 0) & (glob_x < total_x)
     inside_y = (glob_y >= 0) & (glob_y < total_y)
-    faces_full = geometry(perm_ext, glob_x, glob_y, inside_x, inside_y, total_x, total_y)
-    faces_zero = tuple((member for member in faces_full))
-
-    def smooth(field_in):
-        for sweep_index in range(NU):
-            center, product = apply_fine(fine_halo(field_in), faces_zero)
-            field_in = center + OMEGA * (source - product) / faces_zero[7]
-        return field_in
-
-    pressure = smooth(pressure)
-    center, product = apply_fine(fine_halo(pressure), faces_zero)
+    faces_ext = geometry(perm_ext, glob_x, glob_y, inside_x, inside_y, total_x, total_y)
+    smooth_ext = sweeps(ext_all[2], source_ext, faces_ext, NU, width_x)
+    faces_zero = tuple(crop(member, fine_rim - 1) for member in faces_ext)
+    pressure = crop(smooth_ext, 1)
+    center, product = apply_fine(smooth_ext, faces_zero)
     residual = source - product
     half_y = width_y // 2
     half_z = depth_cells // 2
@@ -210,12 +223,14 @@
             coarse_center
             + OMEGA * (coarse_rhs - (diag_coarse * coarse_center - beside_all)) / safe_coarse
         )
-    corr_wide = coarse_extend(coarse_corr[None], 1)[0][:, 1:-1]
-    pick_map = ((slot_ids + 1)[:, None] == jnp.arange(width_x + 2)[None, :]).astype(jnp.float32)
+    last_corr = lax.dynamic_index_in_dim(coarse_corr, count_live - 1, axis=0, keepdims=False)
+    corr_wide = jnp.concatenate([passed_along(last_corr, "slab", 1)[None], coarse_corr], axis=0)
+    pick_map = ((slot_ids + 1)[:, None] == jnp.arange(width_x + 1)[None, :]).astype(jnp.float32)
     correction = jnp.einsum("xs,sjk->xjk", pick_map, corr_wide, precision=lax.Precision.HIGHEST)
     correction = jnp.repeat(jnp.repeat(correction, 2, axis=1), 2, axis=2)
     pressure = pressure + correction
-    return smooth(pressure)
+    post_ext = padded(pressure, sides, NU)
+    return sweeps(post_ext, source_ext, faces_ext, NU, width_x)
 
 
 def solution(mesh):

time: 183 us -> 129 us (0.70)
  starting transfers between devices: 86.7 us -> 39.9 us
  waiting for transfers between devices: 37.2 us -> 24.3 us
  local copies, waits for them, and re-layouts: 31.6 us -> 36.9 us
    ppermute x16 -> x6, starting transfers between devices: 59.5 us -> 25 us  [padded(): before = lax.ppermute(last, axis, up)]
    ppermute x16 -> x6, starting transfers between devices: 25.9 us -> 9.64 us  [padded(): after = lax.ppermute(leading, axis, down)]
    ppermute x16 -> x6, waiting for transfers between devices: 28.2 us -> 15.7 us  [padded(): after = lax.ppermute(leading, axis, down)]
    ppermute x1 -> x2, starting transfers between devices: 1.29 us -> 5.3 us  [passed_along(): return lax.ppermute(array, axis, pairs)]
    slice x4 -> x2, local copies, waits for them, and re-layouts: 0.07 us -> 3.74 us  [crop(): return array[rim:array.shape[0] - rim, rim:array.shape[1] - rim]]
    mul x1 -> x0, local copies, waits for them, and re-layouts: 1.95 us -> none  [geometry(): boundary = 2.0 * cell_perm * edges]
    ppermute x16 -> x6, waiting for transfers between devices: 4.89 us -> 4.67 us  [padded(): before = lax.ppermute(last, axis, up)]
    ppermute x1 -> x2, waiting for transfers between devices: 4.12 us -> 3.94 us  [passed_along(): return lax.ppermute(array, axis, pairs)]
  transfers between devices with their start and end apart: 33 -> 14, of which waited for: 14 -> 10; matrix products, arithmetic and copies ran while one was open for 14% -> 3% of each run, Pallas kernels for 0% -> 0%
where the time goes in v1:
time: 129 us; the launch traced here: 128 us
  starting transfers between devices  39.9 us (31%)
  local copies, waits for them, and re-layouts  36.9 us (29%)
  waiting for transfers between devices  24.3 us (19%)
  other arithmetic  22.9 us (18%)
  between operations  3.17 us (2%)
    ppermute x6, starting transfers between devices, padded(): before = lax.ppermute(last, axis, up)  25 us
    ppermute x6, waiting for transfers between devices, padded(): after = lax.ppermute(leading, axis, down)  15.7 us
    reduce_sum x3, other arithmetic, pair_sum(): return block_in.reshape(width_x, half_y, 2, half_z, 2).sum(axis=(2, 4))  10.3 us
    ppermute x6, starting transfers between devices, padded(): after = lax.ppermute(leading, axis, down)  9.64 us
    slice x1, local copies, waits for them, and re-layouts, body(): face_above[:, :, 1::2].reshape(width_x, half_y, 2, half_z).sum(axis=2)  5.54 us
    ppermute x2, starting transfers between devices, passed_along(): return lax.ppermute(array, axis, pairs)  5.3 us
    dynamic_update_slice x1, local copies, waits for them, and re-layouts, coarse_extend(): lax.dynamic_update_slice_in_dim(base_block, ahead_planes, rim_width + cou...  4.79 us
    ppermute x6, waiting for transfers between devices, padded(): before = lax.ppermute(last, axis, up)  4.67 us
  transfers between devices with their start and end apart: 14, of which 10 were waited for; matrix products, arithmetic and copies ran while one was open for 3% of the time, Pallas kernels for 0%

profile of v1, /device:TPU:1, one launch (start us, length us, event | category | flops | bytes accessed | tf_op | source)
XLA Modules:
  0.0 127.9 jit_solution(11421761808661950937)
XLA Ops:
  0.0 1.1 copy.49
  1.1 1.3 %copy_bitcast_fusion = (f32[1,16,16,256]{3,1,2,0:T(8,128)S(1)}, f32[1,16,16,256]{3,1,2,0:T(8,128)S(1)}) fusion(f32[16,16,256]{2,1,0:T(8,128)} %param.6, f32[16,16,256]{2,1,0:T(8,128)} %param.4), kind=kLoop, calls=%fused_computation.96 | loop fusion | bytes 1048576 | tf_op jit(solution)/shard_map/stack | solution.py:120
  2.5 4.0 %collective-permute-start = (f32[3,3,16,256]{3,1,2,0:T(4,128)S(1)}, f32[3,3,16,256]{3,1,2,0:T(4,128)S(1)}, u32[]{:S(2)}, u32[]{:S(2)}) collective-permute-start(f32[3,3,16,256]{3,1,2,0:T(4,128)S(1)} %get-tuple-element.15), channel_id=1, source_target_pairs={{0,4},{4,8},{8,12},{1,5},{5,9},{9,13},{2,6},{6,10},{10,14},{3,7},{... | collective-permute-start | bytes 442376 | tf_op jit(solution)/shard_map/ppermute | solution.py:20
  6.6 1.3 %collective-permute-start.1 = (f32[3,3,16,256]{3,1,2,0:T(4,128)S(1)}, f32[3,3,16,256]{3,1,2,0:T(4,128)S(1)}, u32[]{:S(2)}, u32[]{:S(2)}) collective-permute-start(f32[3,3,16,256]{3,1,2,0:T(4,128)S(1)} %get-tuple-element.16), channel_id=1, source_target_pairs={{4,0},{8,4},{12,8},{5,1},{9,5},{13,9},{6,2},{10,6},{14,10},{7,3},{... | collective-permute-start | bytes 442376 | tf_op jit(solution)/shard_map/ppermute | solution.py:21
  8.3 0.6 fusion.124
  8.9 1.3 %pad_add_fusion = s32[66]{0:T(128)S(1)} fusion(s32[1]{0:T(128)} %get-tuple-element.51, s32[64]{0:T(128)S(1)} %copy-done.14, s32[1]{0:T(128)} %get-tuple-element.50), kind=kLoop, calls=%fused_computation.234 | loop fusion | flops 132 | bytes 528 | tf_op jit(solution)/shard_map/concatenate | solution.py:139
  10.3 0.6 fusion.123
  14.0 4.9 %collective-permute-start.2 = (f32[3,22,3,256]{3,1,2,0:T(8,128)S(1)}, f32[3,22,3,256]{3,1,2,0:T(8,128)S(1)}, u32[]{:S(2)}, u32[]{:S(2)}) collective-permute-start(f32[3,22,3,256]{3,1,2,0:T(8,128)S(1)} %get-tuple-element.13), channel_id=1, source_target_pairs={{0,1},{1,2},{2,3},{4,5},{5,6},{6,7},{8,9},{9,10},{10,11},{12,13},{... | collective-permute-start | bytes 608264 | tf_op jit(solution)/shard_map/ppermute | solution.py:20
  18.9 1.9 %collective-permute-start.3 = (f32[3,22,3,256]{3,1,2,0:T(8,128)S(1)}, f32[3,22,3,256]{3,1,2,0:T(8,128)S(1)}, u32[]{:S(2)}, u32[]{:S(2)}) collective-permute-start(f32[3,22,3,256]{3,1,2,0:T(8,128)S(1)} %get-tuple-element.14), channel_id=1, source_target_pairs={{1,0},{2,1},{3,2},{5,4},{6,5},{7,6},{9,8},{10,9},{11,10},{13,12},{... | collective-permute-start | bytes 608264 | tf_op jit(solution)/shard_map/ppermute | solution.py:21
  20.9 0.9 collective-permute-done.2
  21.7 4.4 %collective-permute-done.3 = f32[3,22,3,256]{3,1,2,0:T(8,128)S(1)} collective-permute-done((f32[3,22,3,256]{3,1,2,0:T(8,128)S(1)}, f32[3,22,3,256]{3,1,2,0:T(8,128)S(1)}, u32[]{:S(2)}, u32[]{:S(2)}) %collective-permute-start.3) | collective-permute-done | bytes 202784 | tf_op jit(solution)/shard_map/ppermute | solution.py:21
  26.1 0.2 pad_maximum_fusion
  26.5 0.2 divide_select_fusion
  26.7 0.2 fusion.113
  27.1 0.2 fusion.114
  27.3 0.2 divide_select_fusion.2
  27.5 1.0 fusion.7
  28.5 0.8 slice.750
  29.5 0.7 fusion.30
  30.4 1.3 %slice_multiply_fusion.19 = (f32[16,16,256]{2,0,1:T(8,128)}, f32[16,16,256]{2,0,1:T(8,128)S(1)}, f32[16,16,256]{2,0,1:T(8,128)S(1)}, f32[16,16,256]{2,0,1:T(8,128)}) fusion(f32[21,22,256]{2,0,1:T(8,128)S(1)} %divide_select_fusion, f32[16]{0:T(128)S(1)} %compare_convert_fusion.1, f32[16,16,255]{2,0,1:T(8,128)S(1)} %get-tuple-element.34, ...), kind=kLoop, calls=%fused_computation.100 | loop fusion | flops 983040 | bytes 4862464 | tf_op jit(solution)/shard_map/mul | solution.py:151
  31.8 5.5 %slice.618 = f32[16,16,128]{2,0,1:T(8,128)S(1)} slice(f32[16,16,256]{2,0,1:T(8,128)} %get-tuple-element.26), slice={[0:16:1], [0:16:1], [1:256:2]} | slice | bytes 262144 | tf_op jit(solution)/shard_map/slice | solution.py:153
  37.4 1.3 %copy.35 = f32[16,8,256]{0,1,2:T(8,128)} copy(f32[16,8,256]{2,0,1:T(8,128)S(1)} %slice.617) | data formatting | bytes 262144 | tf_op jit(solution)/shard_map/slice | solution.py:152
  38.7 1.4 %bitcast_reduce_fusion = f32[16,8,128]{0,1,2:T(8,128)S(1)} fusion(f32[16,8,256]{0,1,2:T(8,128)} %copy.35), kind=kLoop, calls=%fused_computation.3 | loop fusion | flops 16384 | bytes 196608 | tf_op jit(solution)/shard_map/reduce_sum | solution.py:152
  40.3 2.9 %copy.33 = f32[16,16,256]{0,2,1:T(8,128)} copy(f32[16,16,256]{2,0,1:T(8,128)} %get-tuple-element.19) | data formatting | bytes 524288 | tf_op jit(solution)/shard_map/mul | solution.py:151
  43.2 3.5 %reduce_sum.46 = f32[16,8,128]{0,2,1:T(8,128)S(1)} reduce(f32[16,8,2,128,2]{0,4,3,2,1:T(2,128)} %bitcast.200, f32[]{:T(128)} %constant.30.clone.1), dimensions={2,4}, to_apply=%region_1.2 | reduce | flops 49152 | bytes 327684 | tf_op jit(solution)/shard_map/reduce_sum | solution.py:137
  46.7 0.8 copy.34
  47.5 2.9 %copy.37 = f32[16,16,256]{0,2,1:T(8,128)} copy(f32[16,16,256]{2,0,1:T(8,128)} %slice.750) | data formatting | bytes 524288 | tf_op jit(solution)/shard_map/slice | solution.py:93
  50.4 3.5 %reduce_sum.49 = f32[16,8,128]{0,2,1:T(8,128)S(1)} reduce(f32[16,8,2,128,2]{0,4,3,2,1:T(2,128)} %bitcast.201, f32[]{:T(128)} %constant.30.clone.1), dimensions={2,4}, to_apply=%region_4.5 | reduce | flops 49152 | bytes 327684 | tf_op jit(solution)/shard_map/reduce_sum | solution.py:137
  54.0 2.0 %copy.31 = f32[16,16,256]{0,2,1:T(8,128)} copy(f32[16,16,256]{2,0,1:T(8,128)S(1)} %get-tuple-element.20) | data formatting | bytes 524288 | tf_op jit(solution)/shard_map/sub | solution.py:132
  56.0 3.5 %reduce_sum.45 = f32[16,8,128]{0,2,1:T(8,128)S(1)} reduce(f32[16,8,2,128,2]{0,4,3,2,1:T(2,128)} %bitcast.199, f32[]{:T(128)} %constant.30.clone.1), dimensions={2,4}, to_apply=%region_0.1 | reduce | flops 49152 | bytes 327684 | tf_op jit(solution)/shard_map/reduce_sum | solution.py:137
  59.7 0.2 fusion.102
  59.9 1.3 %collective-permute-start.4 = (f32[5,8,128]{2,1,0:T(8,128)S(1)}, f32[5,8,128]{2,1,0:T(8,128)S(1)}, u32[]{:S(2)}, u32[]{:S(2)}) collective-permute-start(f32[5,8,128]{2,1,0:T(8,128)S(1)} %bitcast.210), channel_id=1, source_target_pairs={{4,0},{8,4},{12,8},{5,1},{9,5},{13,9},{6,2},{10,6},{14,10},{7,3},{... | collective-permute-start | bytes 61448 | tf_op jit(solution)/shard_map/ppermute | solution.py:29
  61.3 3.2 %collective-permute-done.4 = f32[5,8,128]{2,1,0:T(8,128)S(1)} collective-permute-done((f32[5,8,128]{2,1,0:T(8,128)S(1)}, f32[5,8,128]{2,1,0:T(8,128)S(1)}, u32[]{:S(2)}, u32[]{:S(2)}) %collective-permute-start.4) | collective-permute-done | bytes 20512 | tf_op jit(solution)/shard_map/ppermute | solution.py:29
  64.5 0.3 multiply_add_fusion
  64.8 1.3 %collective-permute-start.6 = (f32[5,4,8,128]{3,1,2,0:T(4,128)S(1)}, f32[5,4,8,128]{3,1,2,0:T(4,128)S(1)}, u32[]{:S(2)}, u32[]{:S(2)}) collective-permute-start(f32[5,4,8,128]{3,1,2,0:T(4,128)S(1)} %get-tuple-element.38), channel_id=1, source_target_pairs={{4,0},{8,4},{12,8},{5,1},{9,5},{13,9},{6,2},{10,6},{14,10},{7,3},{... | collective-permute-start | bytes 245768 | tf_op jit(solution)/shard_map/ppermute | solution.py:21
  66.1 4.0 %collective-permute-start.5 = (f32[5,4,8,128]{3,1,2,0:T(4,128)S(1)}, f32[5,4,8,128]{3,1,2,0:T(4,128)S(1)}, u32[]{:S(2)}, u32[]{:S(2)}) collective-permute-start(f32[5,4,8,128]{3,1,2,0:T(4,128)S(1)} %get-tuple-element.37), channel_id=1, source_target_pairs={{0,4},{4,8},{8,12},{1,5},{5,9},{9,13},{2,6},{6,10},{10,14},{3,7},{... | collective-permute-start | bytes 245768 | tf_op jit(solution)/shard_map/ppermute | solution.py:20
  70.1 1.4 %collective-permute-done.5 = f32[5,4,8,128]{3,1,2,0:T(4,128)S(1)} collective-permute-done((f32[5,4,8,128]{3,1,2,0:T(4,128)S(1)}, f32[5,4,8,128]{3,1,2,0:T(4,128)S(1)}, u32[]{:S(2)}, u32[]{:S(2)}) %collective-permute-start.5) | collective-permute-done | bytes 81952 | tf_op jit(solution)/shard_map/ppermute | solution.py:20
  71.7 0.9 fusion.112
  72.6 4.0 %collective-permute-start.7 = (f32[5,28,4,128]{3,1,2,0:T(8,128)}, f32[5,28,4,128]{3,1,2,0:T(8,128)S(1)}, u32[]{:S(2)}, u32[]{:S(2)}) collective-permute-start(f32[5,28,4,128]{3,1,2,0:T(8,128)} %get-tuple-element.17), channel_id=1, source_target_pairs={{0,1},{1,2},{2,3},{4,5},{5,6},{6,7},{8,9},{9,10},{10,11},{12,13},{... | collective-permute-start | bytes 860168 | tf_op jit(solution)/shard_map/ppermute | solution.py:20
  76.7 1.9 %collective-permute-start.8 = (f32[5,28,4,128]{3,1,2,0:T(8,128)}, f32[5,28,4,128]{3,1,2,0:T(8,128)}, u32[]{:S(2)}, u32[]{:S(2)}) collective-permute-start(f32[5,28,4,128]{3,1,2,0:T(8,128)} %get-tuple-element.18), channel_id=1, source_target_pairs={{1,0},{2,1},{3,2},{5,4},{6,5},{7,6},{9,8},{10,9},{11,10},{13,12},{... | collective-permute-start | bytes 860168 | tf_op jit(solution)/shard_map/ppermute | solution.py:21
  78.6 2.4 %collective-permute-done.7 = f32[5,28,4,128]{3,1,2,0:T(8,128)S(1)} collective-permute-done((f32[5,28,4,128]{3,1,2,0:T(8,128)}, f32[5,28,4,128]{3,1,2,0:T(8,128)S(1)}, u32[]{:S(2)}, u32[]{:S(2)}) %collective-permute-start.7) | collective-permute-done | bytes 286752 | tf_op jit(solution)/shard_map/ppermute | solution.py:20
  81.0 4.4 %collective-permute-done.8 = f32[5,28,4,128]{3,1,2,0:T(8,128)} collective-permute-done((f32[5,28,4,128]{3,1,2,0:T(8,128)}, f32[5,28,4,128]{3,1,2,0:T(8,128)}, u32[]{:S(2)}, u32[]{:S(2)}) %collective-permute-start.8) | collective-permute-done | bytes 286752 | tf_op jit(solution)/shard_map/ppermute | solution.py:21
  85.4 1.2 pad_maximum_fusion.1
  86.7 0.8 copy-done.3
  87.7 1.6 %pad_maximum_fusion.18 = f32[5,4,16,128]{3,1,2,0:T(4,128)} fusion(f32[5,28,4,128]{3,1,2,0:T(8,128)} %collective-permute-done.8, f32[5,28,4,128]{3,1,2,0:T(8,128)S(1)} %copy-done.7, f32[5,4,8,128]{3,1,2,0:T(4,128)S(1)} %copy-done.10, f32[5,4,8,128]{3,1,2,0:T(4,128)S(1)} %copy-done.5, f32[5,16,8,128]{3,1,2,0:T(8,128)S(1)} %copy-done.3, ...), kind=kLoop, calls=%fused_computation.125 | loop fusion | flops 204800 | bytes 1310720 | tf_op jit(solution)/shard_map/slice | solution.py:170
  89.3 4.8 %dynamic_update_slice.3 = f32[5,24,16,128]{3,1,2,0:T(8,128)S(1)} dynamic-update-slice(f32[5,24,16,128]{3,1,2,0:T(8,128)S(1)} %slice.754, f32[5,4,16,128]{3,1,2,0:T(4,128)} %pad_maximum_fusion.18, s32[]{:T(128)} %constant.24.clone.1, s32[]{:T(128)S(6)} %select_n.63, s32[]{:T(128)} %constant.24.clone.1, s32[]{:T(128)} %constant.24.clone.1) | dynamic-update-slice | bytes 327684 | tf_op jit(solution)/shard_map/dynamic_update_slice | solution.py:172
  94.2 0.2 fusion.50
  94.5 0.3 fusion.58
  94.9 0.2 fusion.69
  95.4 4.0 %collective-permute-start.9 = (f32[8,128]{1,0:T(8,128)S(1)}, f32[8,128]{1,0:T(8,128)S(1)}, u32[]{:S(2)}, u32[]{:S(2)}) collective-permute-start(f32[8,128]{1,0:T(8,128)S(1)} %bitcast.212), channel_id=1, source_target_pairs={{0,4},{4,8},{8,12},{1,5},{5,9},{9,13},{2,6},{6,10},{10,14},{3,7},{... | collective-permute-start | bytes 12296 | tf_op jit(solution)/shard_map/ppermute | solution.py:29
  99.4 0.7 collective-permute-done.9
  100.2 0.2 fusion.79
  100.4 1.4 %copy.39 = f32[16,16,128]{1,0,2:T(8,128)} copy(f32[16,16,128]{2,0,1:T(8,128)S(1)} %bitcast.207) | data formatting | bytes 262144 | tf_op jit(solution)/shard_map/reshape | solution.py:230
  101.8 2.8 %broadcast_in_dim.131 = f32[16,16,128,2]{1,0,3,2:T(8,128)} broadcast(f32[16,16,128]{1,0,2:T(8,128)} %copy.39), dimensions={0,1,2} | broadcast | bytes 393216 | tf_op jit(solution)/shard_map/broadcast_in_dim | solution.py:230
  104.6 2.6 %copy.40 = f32[16,16,256]{2,0,1:T(8,128)S(1)} copy(f32[16,16,256]{1,0,2:T(8,128)} %bitcast.198) | data formatting | bytes 524288 | tf_op jit(solution)/shard_map/reshape | solution.py:230
  107.2 3.7 %collective-permute-start.10 = (f32[2,16,256]{2,0,1:T(2,128)S(1)}, f32[2,16,256]{2,0,1:T(2,128)S(1)}, u32[]{:S(2)}, u32[]{:S(2)}) collective-permute-start(f32[2,16,256]{2,0,1:T(2,128)S(1)} %get-tuple-element.39), channel_id=1, source_target_pairs={{0,4},{4,8},{8,12},{1,5},{5,9},{9,13},{2,6},{6,10},{10,14},{3,7},{... | collective-permute-start | bytes 98312 | tf_op jit(solution)/shard_map/ppermute | solution.py:20
  111.0 1.3 %collective-permute-start.11 = (f32[2,16,256]{2,0,1:T(2,128)S(1)}, f32[2,16,256]{2,0,1:T(2,128)S(1)}, u32[]{:S(2)}, u32[]{:S(2)}) collective-permute-start(f32[2,16,256]{2,0,1:T(2,128)S(1)} %get-tuple-element.40), channel_id=1, source_target_pairs={{4,0},{8,4},{12,8},{5,1},{9,5},{13,9},{6,2},{10,6},{14,10},{7,3},{... | collective-permute-start | bytes 98312 | tf_op jit(solution)/shard_map/ppermute | solution.py:21
  112.3 3.3 %collective-permute-done.11 = f32[2,16,256]{2,0,1:T(2,128)S(1)} collective-permute-done((f32[2,16,256]{2,0,1:T(2,128)S(1)}, f32[2,16,256]{2,0,1:T(2,128)S(1)}, u32[]{:S(2)}, u32[]{:S(2)}) %collective-permute-start.11) | collective-permute-done | bytes 32800 | tf_op jit(solution)/shard_map/ppermute | solution.py:21
  115.7 4.3 %collective-permute-start.12 = (f32[20,2,256]{2,0,1:T(8,128)S(1)}, f32[20,2,256]{2,0,1:T(8,128)S(1)}, u32[]{:S(2)}, u32[]{:S(2)}) collective-permute-start(f32[20,2,256]{2,0,1:T(8,128)S(1)} %get-tuple-element.35), channel_id=1, source_target_pairs={{0,1},{1,2},{2,3},{4,5},{5,6},{6,7},{8,9},{9,10},{10,11},{12,13},{... | collective-permute-start | bytes 122888 | tf_op jit(solution)/shard_map/ppermute | solution.py:20
  120.0 1.9 %collective-permute-start.13 = (f32[20,2,256]{2,0,1:T(8,128)S(1)}, f32[20,2,256]{2,0,1:T(8,128)S(1)}, u32[]{:S(2)}, u32[]{:S(2)}) collective-permute-start(f32[20,2,256]{2,0,1:T(8,128)S(1)} %get-tuple-element.36), channel_id=1, source_target_pairs={{1,0},{2,1},{3,2},{5,4},{6,5},{7,6},{9,8},{10,9},{11,10},{13,12},{... | collective-permute-start | bytes 122888 | tf_op jit(solution)/shard_map/ppermute | solution.py:21
  121.9 3.5 %collective-permute-done.13 = f32[20,2,256]{2,0,1:T(8,128)S(1)} collective-permute-done((f32[20,2,256]{2,0,1:T(8,128)S(1)}, f32[20,2,256]{2,0,1:T(8,128)S(1)}, u32[]{:S(2)}, u32[]{:S(2)}) %collective-permute-start.13) | collective-permute-done | bytes 40992 | tf_op jit(solution)/shard_map/ppermute | solution.py:21
  125.7 0.8 fusion.19
  126.6 0.4 fusion.40
  127.1 0.9 copy.41
  (88 shorter events, 3.9 us)
Async XLA Ops:
  0.0 8.3 %copy-start.14 = (s32[64]{0:T(128)S(1)}, s32[64]{0:T(128)}, u32[]{:S(2)}) copy-start(s32[64]{0:T(128)} %param.7) | copy-start | bytes 772
  2.5 11.3 %collective-permute-start = (f32[3,3,16,256]{3,1,2,0:T(4,128)S(1)}, f32[3,3,16,256]{3,1,2,0:T(4,128)S(1)}, u32[]{:S(2)}, u32[]{:S(2)}) collective-permute-start(f32[3,3,16,256]{3,1,2,0:T(4,128)S(1)} %get-tuple-element.15), channel_id=1, source_target_pairs={{0,4},{4,8},{8,12},{1,5},{5,9},{9,13},{2,6},{6,10},{10,14},{3,7},{... | collective-permute-start | bytes 442376 | tf_op jit(solution)/shard_map/ppermute | solution.py:20
  6.6 7.3 %collective-permute-start.1 = (f32[3,3,16,256]{3,1,2,0:T(4,128)S(1)}, f32[3,3,16,256]{3,1,2,0:T(4,128)S(1)}, u32[]{:S(2)}, u32[]{:S(2)}) collective-permute-start(f32[3,3,16,256]{3,1,2,0:T(4,128)S(1)} %get-tuple-element.16), channel_id=1, source_target_pairs={{4,0},{8,4},{12,8},{5,1},{9,5},{13,9},{6,2},{10,6},{14,10},{7,3},{... | collective-permute-start | bytes 442376 | tf_op jit(solution)/shard_map/ppermute | solution.py:21
  14.0 7.7 %collective-permute-start.2 = (f32[3,22,3,256]{3,1,2,0:T(8,128)S(1)}, f32[3,22,3,256]{3,1,2,0:T(8,128)S(1)}, u32[]{:S(2)}, u32[]{:S(2)}) collective-permute-start(f32[3,22,3,256]{3,1,2,0:T(8,128)S(1)} %get-tuple-element.13), channel_id=1, source_target_pairs={{0,1},{1,2},{2,3},{4,5},{5,6},{6,7},{8,9},{9,10},{10,11},{12,13},{... | collective-permute-start | bytes 608264 | tf_op jit(solution)/shard_map/ppermute | solution.py:20
  18.9 7.3 %collective-permute-start.3 = (f32[3,22,3,256]{3,1,2,0:T(8,128)S(1)}, f32[3,22,3,256]{3,1,2,0:T(8,128)S(1)}, u32[]{:S(2)}, u32[]{:S(2)}) collective-permute-start(f32[3,22,3,256]{3,1,2,0:T(8,128)S(1)} %get-tuple-element.14), channel_id=1, source_target_pairs={{1,0},{2,1},{3,2},{5,4},{6,5},{7,6},{9,8},{10,9},{11,10},{13,12},{... | collective-permute-start | bytes 608264 | tf_op jit(solution)/shard_map/ppermute | solution.py:21
  28.5 1.9 %copy-start = (f32[20,20,256]{2,0,1:T(8,128)}, f32[20,20,256]{2,0,1:T(8,128)S(1)}, u32[]{:S(2)}) copy-start(f32[20,20,256]{2,0,1:T(8,128)S(1)} %get-tuple-element.8) | copy-start | bytes 1228804
  29.5 1.0 copy-start.8
  56.0 3.6 %copy-start.13 = (f32[16,8,128]{2,0,1:T(8,128)S(1)}, f32[16,8,128]{2,0,1:T(8,128)}, u32[]{:S(2)}) copy-start(f32[16,8,128]{2,0,1:T(8,128)} %copy.34) | copy-start | bytes 196612
  59.9 4.5 %collective-permute-start.4 = (f32[5,8,128]{2,1,0:T(8,128)S(1)}, f32[5,8,128]{2,1,0:T(8,128)S(1)}, u32[]{:S(2)}, u32[]{:S(2)}) collective-permute-start(f32[5,8,128]{2,1,0:T(8,128)S(1)} %bitcast.210), channel_id=1, source_target_pairs={{4,0},{8,4},{12,8},{5,1},{9,5},{13,9},{6,2},{10,6},{14,10},{7,3},{... | collective-permute-start | bytes 61448 | tf_op jit(solution)/shard_map/ppermute | solution.py:29
  64.8 20.6 %copy-start.2 = (f32[5,16,8,128]{3,1,2,0:T(8,128)}, f32[5,16,8,128]{3,1,2,0:T(8,128)S(1)}, u32[]{:S(2)}) copy-start(f32[5,16,8,128]{3,1,2,0:T(8,128)S(1)} %multiply_add_fusion) | copy-start | bytes 983044
  64.8 20.5 %copy-start.4 = (f32[5,4,8,128]{3,1,2,0:T(4,128)}, f32[5,4,8,128]{3,1,2,0:T(4,128)S(1)}, u32[]{:S(2)}) copy-start(f32[5,4,8,128]{3,1,2,0:T(4,128)S(1)} %get-tuple-element.37) | copy-start | bytes 245764
  64.8 5.3 %collective-permute-start.6 = (f32[5,4,8,128]{3,1,2,0:T(4,128)S(1)}, f32[5,4,8,128]{3,1,2,0:T(4,128)S(1)}, u32[]{:S(2)}, u32[]{:S(2)}) collective-permute-start(f32[5,4,8,128]{3,1,2,0:T(4,128)S(1)} %get-tuple-element.38), channel_id=1, source_target_pairs={{4,0},{8,4},{12,8},{5,1},{9,5},{13,9},{6,2},{10,6},{14,10},{7,3},{... | collective-permute-start | bytes 245768 | tf_op jit(solution)/shard_map/ppermute | solution.py:21
  66.1 5.5 %collective-permute-start.5 = (f32[5,4,8,128]{3,1,2,0:T(4,128)S(1)}, f32[5,4,8,128]{3,1,2,0:T(4,128)S(1)}, u32[]{:S(2)}, u32[]{:S(2)}) collective-permute-start(f32[5,4,8,128]{3,1,2,0:T(4,128)S(1)} %get-tuple-element.37), channel_id=1, source_target_pairs={{0,4},{4,8},{8,12},{1,5},{5,9},{9,13},{2,6},{6,10},{10,14},{3,7},{... | collective-permute-start | bytes 245768 | tf_op jit(solution)/shard_map/ppermute | solution.py:20
  70.1 15.2 %copy-start.9 = (f32[5,4,8,128]{3,1,2,0:T(4,128)}, f32[5,4,8,128]{3,1,2,0:T(4,128)S(1)}, u32[]{:S(2)}) copy-start(f32[5,4,8,128]{3,1,2,0:T(4,128)S(1)} %collective-permute-done.6) | copy-start | bytes 245764
  71.6 13.8 %copy-start.11 = (f32[5,4,8,128]{3,1,2,0:T(4,128)}, f32[5,4,8,128]{3,1,2,0:T(4,128)S(1)}, u32[]{:S(2)}) copy-start(f32[5,4,8,128]{3,1,2,0:T(4,128)S(1)} %collective-permute-done.5) | copy-start | bytes 245764
  72.6 8.3 %collective-permute-start.7 = (f32[5,28,4,128]{3,1,2,0:T(8,128)}, f32[5,28,4,128]{3,1,2,0:T(8,128)S(1)}, u32[]{:S(2)}, u32[]{:S(2)}) collective-permute-start(f32[5,28,4,128]{3,1,2,0:T(8,128)} %get-tuple-element.17), channel_id=1, source_target_pairs={{0,1},{1,2},{2,3},{4,5},{5,6},{6,7},{8,9},{9,10},{10,11},{12,13},{... | collective-permute-start | bytes 860168 | tf_op jit(solution)/shard_map/ppermute | solution.py:20
  76.7 8.7 %collective-permute-start.8 = (f32[5,28,4,128]{3,1,2,0:T(8,128)}, f32[5,28,4,128]{3,1,2,0:T(8,128)}, u32[]{:S(2)}, u32[]{:S(2)}) collective-permute-start(f32[5,28,4,128]{3,1,2,0:T(8,128)} %get-tuple-element.18), channel_id=1, source_target_pairs={{1,0},{2,1},{3,2},{5,4},{6,5},{7,6},{9,8},{10,9},{11,10},{13,12},{... | collective-permute-start | bytes 860168 | tf_op jit(solution)/shard_map/ppermute | solution.py:21
  81.0 4.4 %copy-start.6 = (f32[5,28,4,128]{3,1,2,0:T(8,128)}, f32[5,28,4,128]{3,1,2,0:T(8,128)S(1)}, u32[]{:S(2)}) copy-start(f32[5,28,4,128]{3,1,2,0:T(8,128)S(1)} %collective-permute-done.7) | copy-start | bytes 860164
  86.6 1.0 copy-start.3
  86.6 1.0 copy-start.5
  86.6 1.1 copy-start.7
  86.6 1.1 copy-start.10
  86.6 1.1 copy-start.12
  95.4 4.8 %collective-permute-start.9 = (f32[8,128]{1,0:T(8,128)S(1)}, f32[8,128]{1,0:T(8,128)S(1)}, u32[]{:S(2)}, u32[]{:S(2)}) collective-permute-start(f32[8,128]{1,0:T(8,128)S(1)} %bitcast.212), channel_id=1, source_target_pairs={{0,4},{4,8},{8,12},{1,5},{5,9},{9,13},{2,6},{6,10},{10,14},{3,7},{... | collective-permute-start | bytes 12296 | tf_op jit(solution)/shard_map/ppermute | solution.py:29
  107.2 18.5 %copy-start.1 = (f32[20,20,256]{2,0,1:T(8,128)S(1)}, f32[20,20,256]{2,0,1:T(8,128)}, u32[]{:S(2)}) copy-start(f32[20,20,256]{2,0,1:T(8,128)} %copy-done) | copy-start | bytes 1228804
  107.2 5.1 %collective-permute-start.10 = (f32[2,16,256]{2,0,1:T(2,128)S(1)}, f32[2,16,256]{2,0,1:T(2,128)S(1)}, u32[]{:S(2)}, u32[]{:S(2)}) collective-permute-start(f32[2,16,256]{2,0,1:T(2,128)S(1)} %get-tuple-element.39), channel_id=1, source_target_pairs={{0,4},{4,8},{8,12},{1,5},{5,9},{9,13},{2,6},{6,10},{10,14},{3,7},{... | collective-permute-start | bytes 98312 | tf_op jit(solution)/shard_map/ppermute | solution.py:20
  111.0 4.7 %collective-permute-start.11 = (f32[2,16,256]{2,0,1:T(2,128)S(1)}, f32[2,16,256]{2,0,1:T(2,128)S(1)}, u32[]{:S(2)}, u32[]{:S(2)}) collective-permute-start(f32[2,16,256]{2,0,1:T(2,128)S(1)} %get-tuple-element.40), channel_id=1, source_target_pairs={{4,0},{8,4},{12,8},{5,1},{9,5},{13,9},{6,2},{10,6},{14,10},{7,3},{... | collective-permute-start | bytes 98312 | tf_op jit(solution)/shard_map/ppermute | solution.py:21
  115.7 6.3 %collective-permute-start.12 = (f32[20,2,256]{2,0,1:T(8,128)S(1)}, f32[20,2,256]{2,0,1:T(8,128)S(1)}, u32[]{:S(2)}, u32[]{:S(2)}) collective-permute-start(f32[20,2,256]{2,0,1:T(8,128)S(1)} %get-tuple-element.35), channel_id=1, source_target_pairs={{0,1},{1,2},{2,3},{4,5},{5,6},{6,7},{8,9},{9,10},{10,11},{12,13},{... | collective-permute-start | bytes 122888 | tf_op jit(solution)/shard_map/ppermute | solution.py:20
  120.0 5.4 %collective-permute-start.13 = (f32[20,2,256]{2,0,1:T(8,128)S(1)}, f32[20,2,256]{2,0,1:T(8,128)S(1)}, u32[]{:S(2)}, u32[]{:S(2)}) collective-permute-start(f32[20,2,256]{2,0,1:T(8,128)S(1)} %get-tuple-element.36), channel_id=1, source_target_pairs={{1,0},{2,1},{3,2},{5,4},{6,5},{7,6},{9,8},{10,9},{11,10},{13,12},{... | collective-permute-start | bytes 122888 | tf_op jit(solution)/shard_map/ppermute | solution.py:21

commit v2 on v1

--- a/solution.py
+++ b/solution.py
@@ -133,9 +133,6 @@
     half_y = width_y // 2
     half_z = depth_cells // 2
 
-    def pair_sum(block_in):
-        return block_in.reshape(width_x, half_y, 2, half_z, 2).sum(axis=(2, 4))
-
     padded_ids = jnp.concatenate([aggregate[:1], aggregate, aggregate[-1:]])
     ext_ids = lax.dynamic_slice_in_dim(padded_ids, slab_index * width_x, width_x + 2)
     local_ids = ext_ids[1:-1]
@@ -148,16 +145,45 @@
     face_north = faces_zero[3]
     face_above = faces_zero[5]
     boundary = faces_zero[6]
-    east_part = pair_sum(face_east * crossing[:, None, None])
-    north_part = face_north[:, 1::2].reshape(width_x, half_y, half_z, 2).sum(axis=3)
-    above_part = face_above[:, :, 1::2].reshape(width_x, half_y, 2, half_z).sum(axis=2)
-    stacked = jnp.stack([pair_sum(residual), east_part, north_part, above_part, pair_sum(boundary)])
+    index_z = jnp.arange(depth_cells)[:, None]
+    coarse_z = jnp.arange(half_z)[None, :]
+    pair_z = (index_z // 2 == coarse_z).astype(jnp.float32)
+    odd_z = (index_z == 2 * coarse_z + 1).astype(jnp.float32)
+    cells = width_x * width_y
+
+    def z_sum(block_in, pick_z):
+        flat = block_in.reshape(cells, depth_cells)
+        return jnp.dot(flat, pick_z, precision=lax.Precision.HIGHEST)
+
+    z_parts = jnp.stack(
+        [
+            z_sum(residual, pair_z),
+            z_sum(face_east * crossing[:, None, None], pair_z),
+            z_sum(face_north, pair_z),
+            z_sum(face_above, odd_z),
+            z_sum(boundary, pair_z),
+        ]
+    )
+    slot_wide = jnp.arange(width_x + 1)
+    owner_wide = ((slot_ids + 1)[:, None] == slot_wide[None, :]).astype(jnp.float32)
+    index_y = jnp.arange(width_y)[:, None]
+    coarse_y = jnp.arange(half_y)[None, :]
+    pair_y = (index_y // 2 == coarse_y).astype(jnp.float32)
+    odd_y = (index_y == 2 * coarse_y + 1).astype(jnp.float32)
+
+    def xy_map(pick_y):
+        joint = owner_wide[:, None, :, None] * pick_y[None, :, None, :]
+        return joint.reshape(cells, (width_x + 1) * half_y)
+
+    spread_map = xy_map(pair_y)
+    north_map = xy_map(odd_y)
+    maps = jnp.stack([spread_map, spread_map, north_map, spread_map, spread_map])
+    slot_sums = jnp.einsum("qnm,qnl->qml", maps, z_parts, precision=lax.Precision.HIGHEST)
+    slot_sums = slot_sums.reshape(5, width_x + 1, half_y, half_z)
+    coarse = slot_sums[:, 1:]
+    edge_sums = slot_sums[:, 0]
+    arriving = passed_along(edge_sums, "slab", -1)
     slot_range = jnp.arange(width_x)
-    owner_map = (slot_ids[:, None] == slot_range[None, :]).astype(jnp.float32)
-    spill_map = (slot_ids == -1).astype(jnp.float32)
-    coarse = jnp.einsum("qxjk,xs->qsjk", stacked, owner_map, precision=lax.Precision.HIGHEST)
-    edge_sums = jnp.einsum("qxjk,x->qjk", stacked, spill_map, precision=lax.Precision.HIGHEST)
-    arriving = passed_along(edge_sums, "slab", -1)
     last_slot = (slot_range == count_live - 1).astype(jnp.float32)
     coarse = coarse + arriving[:, None] * last_slot[None, :, None, None]
 
@@ -225,9 +251,11 @@
         )
     last_corr = lax.dynamic_index_in_dim(coarse_corr, count_live - 1, axis=0, keepdims=False)
     corr_wide = jnp.concatenate([passed_along(last_corr, "slab", 1)[None], coarse_corr], axis=0)
-    pick_map = ((slot_ids + 1)[:, None] == jnp.arange(width_x + 1)[None, :]).astype(jnp.float32)
-    correction = jnp.einsum("xs,sjk->xjk", pick_map, corr_wide, precision=lax.Precision.HIGHEST)
-    correction = jnp.repeat(jnp.repeat(correction, 2, axis=1), 2, axis=2)
+    corr_z = jnp.dot(
+        corr_wide.reshape((width_x + 1) * half_y, half_z), pair_z.T, precision=lax.Precision.HIGHEST
+    )
+    correction = jnp.dot(spread_map, corr_z, precision=lax.Precision.HIGHEST)
+    correction = correction.reshape(width_x, width_y, depth_cells)
     pressure = pressure + correction
     post_ext = padded(pressure, sides, NU)
     return sweeps(post_ext, source_ext, faces_ext, NU, width_x)

time: 129 us -> 90.7 us (0.70)
  local copies, waits for them, and re-layouts: 36.9 us -> 7.4 us
  other arithmetic: 22.9 us -> 13.3 us
  matrix products: 0.73 us -> 3.1 us
  starting transfers between devices: 39.9 us -> 38.4 us
    reduce_sum x5 -> x0, other arithmetic: 11.8 us -> none  [the longest x3 10.3 us: pair_sum(): return block_in.reshape(width_x, half_y, 2, half_z, 2).sum(axis=(2, 4))]
    slice x4 -> x1, local copies, waits for them, and re-layouts: 7.46 us -> 0.65 us  [body(): count_live = local_ids[-1] - first_id + 1]
    dynamic_update_slice x1 -> x0, local copies, waits for them, and re-layouts: 4.79 us -> none  [coarse_extend(): lax.dynamic_update_slice_in_dim(base_block, ahead_planes, rim_width + cou...]
    reshape x2 -> x0, local copies, waits for them, and re-layouts: 3.96 us -> none  [body(): correction = jnp.repeat(jnp.repeat(correction, 2, axis=1), 2, axis=2)]
    slice x2 -> x1, local copies, waits for them, and re-layouts: 3.74 us -> 0.03 us  [crop(): return array[rim:array.shape[0] - rim, rim:array.shape[1] - rim]]
    broadcast_in_dim x2 -> x0, local copies, waits for them, and re-layouts: 2.78 us -> none  [body(): correction = jnp.repeat(jnp.repeat(correction, 2, axis=1), 2, axis=2)]
    dot_general x3 -> x8, matrix products: 0.73 us -> 3.1 us  [the longest x5 1.66 us: z_sum(): return jnp.dot(flat, pick_z, precision=lax.Precision.HIGHEST)]
    sub x1 -> x0, local copies, waits for them, and re-layouts: 1.99 us -> none  [body(): residual = source - product]
  transfers between devices with their start and end apart: 14 -> 14, of which waited for: 10 -> 9; matrix products, arithmetic and copies ran while one was open for 3% -> 6% of each run, Pallas kernels for 0% -> 0%
where the time goes in v2:
time: 90.7 us; the launch traced here: 90 us
  starting transfers between devices  38.4 us (42%)
  waiting for transfers between devices  24.6 us (27%)
  other arithmetic  13.3 us (15%)
  local copies, waits for them, and re-layouts  7.4 us (8%)
  between operations  3.15 us (3%)
  matrix products  3.1 us (3%)
    ppermute x6, starting transfers between devices, padded(): before = lax.ppermute(last, axis, up)  23.4 us
    ppermute x6, waiting for transfers between devices, padded(): after = lax.ppermute(leading, axis, down)  15.8 us
    ppermute x6, starting transfers between devices, padded(): after = lax.ppermute(leading, axis, down)  9.64 us
    ppermute x2, starting transfers between devices, passed_along(): return lax.ppermute(array, axis, pairs)  5.29 us
    ppermute x2, waiting for transfers between devices, passed_along(): return lax.ppermute(array, axis, pairs)  4.69 us
    ppermute x6, waiting for transfers between devices, padded(): before = lax.ppermute(last, axis, up)  4.15 us
    add x4, other arithmetic, sweeps(): field_ext = center + OMEGA * (source_now - product) / faces_now[7]  3.74 us
  transfers between devices with their start and end apart: 14, of which 9 were waited for; matrix products, arithmetic and copies ran while one was open for 6% of the time, Pallas kernels for 0%

profile of v2, /device:TPU:1, one launch (start us, length us, event | category | flops | bytes accessed | tf_op | source)
XLA Modules:
  0.0 90.0 jit_solution(11831700469936109639)
XLA Ops:
  0.0 1.6 %pad_maximum_fusion.17 = (f32[3,3,16,256]{3,2,1,0:T(8,128)}, f32[3,3,16,256]{3,2,1,0:T(8,128)S(1)}) fusion(f32[1,16,16,256]{3,2,1,0:T(8,128)} %bitcast.210, f32[1,16,16,256]{3,2,1,0:T(8,128)} %bitcast.207, f32[1,16,16,256]{3,2,1,0:T(8,128)} %bitcast.213), kind=kLoop, calls=%fused_computation.179 | loop fusion | flops 147456 | bytes 1081344 | tf_op jit(solution)/shard_map/slice | solution.py:18
  1.6 4.0 %collective-permute-start = (f32[3,3,16,256]{3,2,1,0:T(8,128)}, f32[3,3,16,256]{3,2,1,0:T(8,128)S(1)}, u32[]{:S(2)}, u32[]{:S(2)}) collective-permute-start(f32[3,3,16,256]{3,2,1,0:T(8,128)} %get-tuple-element.13), channel_id=1, source_target_pairs={{0,4},{4,8},{8,12},{1,5},{5,9},{9,13},{2,6},{6,10},{10,14},{3,7},{... | collective-permute-start | bytes 442376 | tf_op jit(solution)/shard_map/ppermute | solution.py:20
  5.6 1.3 %collective-permute-start.1 = (f32[3,3,16,256]{3,2,1,0:T(8,128)S(1)}, f32[3,3,16,256]{3,2,1,0:T(8,128)S(1)}, u32[]{:S(2)}, u32[]{:S(2)}) collective-permute-start(f32[3,3,16,256]{3,2,1,0:T(8,128)S(1)} %get-tuple-element.14), channel_id=1, source_target_pairs={{4,0},{8,4},{12,8},{5,1},{9,5},{13,9},{6,2},{10,6},{14,10},{7,3},{... | collective-permute-start | bytes 442376 | tf_op jit(solution)/shard_map/ppermute | solution.py:21
  7.4 0.6 fusion.127
  8.0 1.3 %pad_add_fusion = s32[66]{0:T(128)S(1)} fusion(s32[1]{0:T(128)} %get-tuple-element.51, s32[64]{0:T(128)S(1)} %copy-done.9, s32[1]{0:T(128)} %get-tuple-element.50), kind=kLoop, calls=%fused_computation.262 | loop fusion | flops 132 | bytes 528 | tf_op jit(solution)/shard_map/concatenate | solution.py:136
  9.3 0.7 fusion.126
  12.1 0.2 broadcast_multiply_fusion
  12.3 0.5 mul.427
  12.8 0.5 mul.423
  14.5 4.0 %collective-permute-start.2 = (f32[3,22,3,256]{3,2,1,0:T(4,128)S(1)}, f32[3,22,3,256]{3,2,1,0:T(4,128)S(1)}, u32[]{:S(2)}, u32[]{:S(2)}) collective-permute-start(f32[3,22,3,256]{3,2,1,0:T(4,128)S(1)} %get-tuple-element.11), channel_id=1, source_target_pairs={{0,1},{1,2},{2,3},{4,5},{5,6},{6,7},{8,9},{9,10},{10,11},{12,13},{... | collective-permute-start | bytes 608264 | tf_op jit(solution)/shard_map/ppermute | solution.py:20
  18.4 1.9 %collective-permute-start.3 = (f32[3,22,3,256]{3,2,1,0:T(4,128)S(1)}, f32[3,22,3,256]{3,2,1,0:T(4,128)S(1)}, u32[]{:S(2)}, u32[]{:S(2)}) collective-permute-start(f32[3,22,3,256]{3,2,1,0:T(4,128)S(1)} %get-tuple-element.12), channel_id=1, source_target_pairs={{1,0},{2,1},{3,2},{5,4},{6,5},{7,6},{9,8},{10,9},{11,10},{13,12},{... | collective-permute-start | bytes 608264 | tf_op jit(solution)/shard_map/ppermute | solution.py:21
  20.4 1.4 %collective-permute-done.2 = f32[3,22,3,256]{3,2,1,0:T(4,128)S(1)} collective-permute-done((f32[3,22,3,256]{3,2,1,0:T(4,128)S(1)}, f32[3,22,3,256]{3,2,1,0:T(4,128)S(1)}, u32[]{:S(2)}, u32[]{:S(2)}) %collective-permute-start.2) | collective-permute-done | bytes 202784 | tf_op jit(solution)/shard_map/ppermute | solution.py:20
  21.8 4.4 %collective-permute-done.3 = f32[3,22,3,256]{3,2,1,0:T(4,128)S(1)} collective-permute-done((f32[3,22,3,256]{3,2,1,0:T(4,128)S(1)}, f32[3,22,3,256]{3,2,1,0:T(4,128)S(1)}, u32[]{:S(2)}, u32[]{:S(2)}) %collective-permute-start.3) | collective-permute-done | bytes 202784 | tf_op jit(solution)/shard_map/ppermute | solution.py:21
  26.2 0.3 pad_maximum_fusion
  26.6 0.2 divide_select_fusion.1
  26.8 0.2 fusion.116
  27.0 0.2 divide_select_fusion
  27.2 0.2 fusion.117
  27.4 0.2 divide_select_fusion.2
  27.6 1.0 %fusion.12 = (f32[20,20,256]{2,1,0:T(8,128)S(1)}, f32[20,20,256]{2,1,0:T(8,128)S(1)}, f32[20,20,256]{2,1,0:T(8,128)S(1)}) fusion(f32[22,22,256]{2,1,0:T(8,128)S(1)} %get-tuple-element.10, f32[22,22,256]{2,1,0:T(8,128)S(1)} %get-tuple-element.9, f32[20,20,255]{2,1,0:T(8,128)S(1)} %get-tuple-element.22, f32[20,20,255]{2,1,0:T(8,128)S(1)} %get-tuple-element.21, ...), kind=kLoop, calls=%fused_computation.34 | loop fusion | flops 2764800 | bytes 6961424 | tf_op jit(solution)/shard_map/add | solution.py:105
  28.7 0.2 fusion.119
  28.9 0.8 fusion.35
  29.6 0.1 fusion.121
  29.8 0.5 fusion.115
  30.3 0.3 fusion.4
  30.6 0.3 fusion.3
  31.0 0.3 fusion.2
  31.3 0.3 fusion.1
  31.6 0.3 fusion
  32.0 0.8 convolution_bitcast_fusion
  32.8 0.7 copy-done.3
  33.5 1.3 %collective-permute-start.4 = (f32[5,8,128]{2,1,0:T(8,128)S(1)}, f32[5,8,128]{2,1,0:T(8,128)S(1)}, u32[]{:S(2)}, u32[]{:S(2)}) collective-permute-start(f32[5,8,128]{2,1,0:T(8,128)S(1)} %slice_bitcast_fusion.29), channel_id=1, source_target_pairs={{4,0},{8,4},{12,8},{5,1},{9,5},{13,9},{6,2},{10,6},{14,10},{7,3},{... | collective-permute-start | bytes 61448 | tf_op jit(solution)/shard_map/ppermute | solution.py:29
  34.8 4.1 %collective-permute-done.4 = f32[5,8,128]{2,1,0:T(8,128)S(1)} collective-permute-done((f32[5,8,128]{2,1,0:T(8,128)S(1)}, f32[5,8,128]{2,1,0:T(8,128)S(1)}, u32[]{:S(2)}, u32[]{:S(2)}) %collective-permute-start.4) | collective-permute-done | bytes 20512 | tf_op jit(solution)/shard_map/ppermute | solution.py:29
  38.9 1.1 %slice_add_fusion = f32[5,16,8,128]{3,2,1,0:T(8,128)S(1)} fusion(f32[5,17,8,128]{3,2,1,0:T(8,128)} %copy-done.3, f32[16]{0:T(128)S(1)} %compare_convert_fusion, f32[5,8,128]{2,1,0:T(8,128)S(1)} %collective-permute-done.4), kind=kLoop, calls=%fused_computation.83 | loop fusion | flops 163840 | bytes 675904 | tf_op jit(solution)/shard_map/add | solution.py:188
  40.0 1.3 %collective-permute-start.6 = (f32[5,4,8,128]{3,2,1,0:T(8,128)S(1)}, f32[5,4,8,128]{3,2,1,0:T(8,128)S(1)}, u32[]{:S(2)}, u32[]{:S(2)}) collective-permute-start(f32[5,4,8,128]{3,2,1,0:T(8,128)S(1)} %get-tuple-element.36), channel_id=1, source_target_pairs={{4,0},{8,4},{12,8},{5,1},{9,5},{13,9},{6,2},{10,6},{14,10},{7,3},{... | collective-permute-start | bytes 245768 | tf_op jit(solution)/shard_map/ppermute | solution.py:21
  41.3 4.0 %collective-permute-start.5 = (f32[5,4,8,128]{3,2,1,0:T(8,128)S(1)}, f32[5,4,8,128]{3,2,1,0:T(8,128)S(1)}, u32[]{:S(2)}, u32[]{:S(2)}) collective-permute-start(f32[5,4,8,128]{3,2,1,0:T(8,128)S(1)} %get-tuple-element.35), channel_id=1, source_target_pairs={{0,4},{4,8},{8,12},{1,5},{5,9},{9,13},{2,6},{6,10},{10,14},{3,7},{... | collective-permute-start | bytes 245768 | tf_op jit(solution)/shard_map/ppermute | solution.py:20
  45.3 1.5 %collective-permute-done.5 = f32[5,4,8,128]{3,2,1,0:T(8,128)S(1)} collective-permute-done((f32[5,4,8,128]{3,2,1,0:T(8,128)S(1)}, f32[5,4,8,128]{3,2,1,0:T(8,128)S(1)}, u32[]{:S(2)}, u32[]{:S(2)}) %collective-permute-start.5) | collective-permute-done | bytes 81952 | tf_op jit(solution)/shard_map/ppermute | solution.py:20
  46.8 0.9 fusion.114
  47.7 3.7 %collective-permute-start.7 = (f32[5,28,4,128]{3,2,1,0:T(4,128)}, f32[5,28,4,128]{3,2,1,0:T(4,128)}, u32[]{:S(2)}, u32[]{:S(2)}) collective-permute-start(f32[5,28,4,128]{3,2,1,0:T(4,128)} %get-tuple-element.15), channel_id=1, source_target_pairs={{0,1},{1,2},{2,3},{4,5},{5,6},{6,7},{8,9},{9,10},{10,11},{12,13},{... | collective-permute-start | bytes 860168 | tf_op jit(solution)/shard_map/ppermute | solution.py:20
  51.5 1.9 %collective-permute-start.8 = (f32[5,28,4,128]{3,2,1,0:T(4,128)}, f32[5,28,4,128]{3,2,1,0:T(4,128)}, u32[]{:S(2)}, u32[]{:S(2)}) collective-permute-start(f32[5,28,4,128]{3,2,1,0:T(4,128)} %get-tuple-element.16), channel_id=1, source_target_pairs={{1,0},{2,1},{3,2},{5,4},{6,5},{7,6},{9,8},{10,9},{11,10},{13,12},{... | collective-permute-start | bytes 860168 | tf_op jit(solution)/shard_map/ppermute | solution.py:21
  53.4 0.6 broadcast_bitcast_fusion.1
  54.0 1.3 %collective-permute-done.7 = f32[5,28,4,128]{3,2,1,0:T(4,128)} collective-permute-done((f32[5,28,4,128]{3,2,1,0:T(4,128)}, f32[5,28,4,128]{3,2,1,0:T(4,128)}, u32[]{:S(2)}, u32[]{:S(2)}) %collective-permute-start.7) | collective-permute-done | bytes 286752 | tf_op jit(solution)/shard_map/ppermute | solution.py:20
  55.3 4.4 %collective-permute-done.8 = f32[5,28,4,128]{3,2,1,0:T(4,128)} collective-permute-done((f32[5,28,4,128]{3,2,1,0:T(4,128)}, f32[5,28,4,128]{3,2,1,0:T(4,128)}, u32[]{:S(2)}, u32[]{:S(2)}) %collective-permute-start.8) | collective-permute-done | bytes 286752 | tf_op jit(solution)/shard_map/ppermute | solution.py:21
  59.7 1.3 %pad_maximum_fusion.1 = f32[5,28,16,128]{3,2,1,0:T(8,128)S(1)} fusion(f32[5,28,4,128]{3,2,1,0:T(4,128)} %collective-permute-done.8, f32[5,4,8,128]{3,2,1,0:T(8,128)S(1)} %collective-permute-done.6, f32[5,4,8,128]{3,2,1,0:T(8,128)S(1)} %get-tuple-element.35, f32[5,16,8,128]{3,2,1,0:T(8,128)S(1)} %slice_add_fusion, f32[5,4,8,128]{3,2,1,0:T(8,128)} %copy-done.6, ...), kind=kLoop, calls=%fused_computation.3 | loop fusion | flops 1433600 | bytes 2293760 | tf_op jit(solution)/shard_map/concatenate | solution.py:22
  61.1 0.8 copy-done.7
  61.9 0.8 maximum_dynamic-update-slice_fusion
  62.9 0.2 fusion.56
  63.2 0.3 fusion.64
  63.6 0.3 fusion.75
  64.0 0.1 fusion.90
  64.1 4.0 %collective-permute-start.9 = (f32[8,128]{1,0:T(8,128)S(1)}, f32[8,128]{1,0:T(8,128)S(1)}, u32[]{:S(2)}, u32[]{:S(2)}) collective-permute-start(f32[8,128]{1,0:T(8,128)S(1)} %dynamic-slice_bitcast_fusion), channel_id=1, source_target_pairs={{0,4},{4,8},{8,12},{1,5},{5,9},{9,13},{2,6},{6,10},{10,14},{3,7},{... | collective-permute-start | bytes 12296 | tf_op jit(solution)/shard_map/ppermute | solution.py:29
  68.3 0.6 collective-permute-done.9
  68.9 0.3 convolution_bitcast_fusion.1
  69.2 0.4 convolution_add_fusion
  69.6 3.6 %collective-permute-start.10 = (f32[2,16,256]{2,1,0:T(8,128)S(1)}, f32[2,16,256]{2,1,0:T(8,128)S(1)}, u32[]{:S(2)}, u32[]{:S(2)}) collective-permute-start(f32[2,16,256]{2,1,0:T(8,128)S(1)} %get-tuple-element.37), channel_id=1, source_target_pairs={{0,4},{4,8},{8,12},{1,5},{5,9},{9,13},{2,6},{6,10},{10,14},{3,7},{... | collective-permute-start | bytes 98312 | tf_op jit(solution)/shard_map/ppermute | solution.py:20
  73.2 1.3 %collective-permute-start.11 = (f32[2,16,256]{2,1,0:T(8,128)S(1)}, f32[2,16,256]{2,1,0:T(8,128)S(1)}, u32[]{:S(2)}, u32[]{:S(2)}) collective-permute-start(f32[2,16,256]{2,1,0:T(8,128)S(1)} %get-tuple-element.38), channel_id=1, source_target_pairs={{4,0},{8,4},{12,8},{5,1},{9,5},{13,9},{6,2},{10,6},{14,10},{7,3},{... | collective-permute-start | bytes 98312 | tf_op jit(solution)/shard_map/ppermute | solution.py:21
  74.5 3.6 %collective-permute-done.11 = f32[2,16,256]{2,1,0:T(8,128)S(1)} collective-permute-done((f32[2,16,256]{2,1,0:T(8,128)S(1)}, f32[2,16,256]{2,1,0:T(8,128)S(1)}, u32[]{:S(2)}, u32[]{:S(2)}) %collective-permute-start.11) | collective-permute-done | bytes 32800 | tf_op jit(solution)/shard_map/ppermute | solution.py:21
  78.1 4.1 %collective-permute-start.12 = (f32[20,2,256]{2,1,0:T(2,128)S(1)}, f32[20,2,256]{2,1,0:T(2,128)S(1)}, u32[]{:S(2)}, u32[]{:S(2)}) collective-permute-start(f32[20,2,256]{2,1,0:T(2,128)S(1)} %get-tuple-element.33), channel_id=1, source_target_pairs={{0,1},{1,2},{2,3},{4,5},{5,6},{6,7},{8,9},{9,10},{10,11},{12,13},{... | collective-permute-start | bytes 122888 | tf_op jit(solution)/shard_map/ppermute | solution.py:20
  82.2 1.9 %collective-permute-start.13 = (f32[20,2,256]{2,1,0:T(2,128)S(1)}, f32[20,2,256]{2,1,0:T(2,128)S(1)}, u32[]{:S(2)}, u32[]{:S(2)}) collective-permute-start(f32[20,2,256]{2,1,0:T(2,128)S(1)} %get-tuple-element.34), channel_id=1, source_target_pairs={{1,0},{2,1},{3,2},{5,4},{6,5},{7,6},{9,8},{10,9},{11,10},{13,12},{... | collective-permute-start | bytes 122888 | tf_op jit(solution)/shard_map/ppermute | solution.py:21
  84.2 3.4 %collective-permute-done.13 = f32[20,2,256]{2,1,0:T(2,128)S(1)} collective-permute-done((f32[20,2,256]{2,1,0:T(2,128)S(1)}, f32[20,2,256]{2,1,0:T(2,128)S(1)}, u32[]{:S(2)}, u32[]{:S(2)}) %collective-permute-start.13) | collective-permute-done | bytes 40992 | tf_op jit(solution)/shard_map/ppermute | solution.py:21
  87.6 0.2 fusion.118
  87.8 0.8 fusion.24
  88.7 0.1 fusion.120
  88.8 1.2 %fusion.45 = f32[16,16,256]{2,1,0:T(8,128)} fusion(f32[18,18,256]{2,1,0:T(8,128)S(1)} %fusion.24, f32[22,22,256]{2,1,0:T(8,128)S(1)} %get-tuple-element.9, f32[16,16,255]{2,1,0:T(8,128)S(1)} %get-tuple-element.30, f32[16,16,255]{2,1,0:T(8,128)S(1)} %get-tuple-element.29, f32[22,21,256]{2,1,0:T(8,128)S(1)} %divide_select_fusion, ...), kind=kLoop, calls=%fused_computation.97 | loop fusion | flops 1114112 | bytes 4075968 | tf_op jit(solution)/shard_map/add | solution.py:105
  (74 shorter events, 2.2 us)
Async XLA Ops:
  0.0 7.4 %copy-start.9 = (s32[64]{0:T(128)S(1)}, s32[64]{0:T(128)}, u32[]{:S(2)}) copy-start(s32[64]{0:T(128)} %param.7) | copy-start | bytes 772
  1.6 12.7 %collective-permute-start = (f32[3,3,16,256]{3,2,1,0:T(8,128)}, f32[3,3,16,256]{3,2,1,0:T(8,128)S(1)}, u32[]{:S(2)}, u32[]{:S(2)}) collective-permute-start(f32[3,3,16,256]{3,2,1,0:T(8,128)} %get-tuple-element.13), channel_id=1, source_target_pairs={{0,4},{4,8},{8,12},{1,5},{5,9},{9,13},{2,6},{6,10},{10,14},{3,7},{... | collective-permute-start | bytes 442376 | tf_op jit(solution)/shard_map/ppermute | solution.py:20
  5.6 8.7 %collective-permute-start.1 = (f32[3,3,16,256]{3,2,1,0:T(8,128)S(1)}, f32[3,3,16,256]{3,2,1,0:T(8,128)S(1)}, u32[]{:S(2)}, u32[]{:S(2)}) collective-permute-start(f32[3,3,16,256]{3,2,1,0:T(8,128)S(1)} %get-tuple-element.14), channel_id=1, source_target_pairs={{4,0},{8,4},{12,8},{5,1},{9,5},{13,9},{6,2},{10,6},{14,10},{7,3},{... | collective-permute-start | bytes 442376 | tf_op jit(solution)/shard_map/ppermute | solution.py:21
  12.8 1.6 %copy-start = (f32[16,16,256]{2,1,0:T(8,128)S(1)}, f32[16,16,256]{2,1,0:T(8,128)}, u32[]{:S(2)}) copy-start(f32[16,16,256]{2,1,0:T(8,128)} %param.5) | copy-start | bytes 786436
  12.8 1.6 %copy-start.1 = (f32[16,16,256]{2,1,0:T(8,128)S(1)}, f32[16,16,256]{2,1,0:T(8,128)}, u32[]{:S(2)}) copy-start(f32[16,16,256]{2,1,0:T(8,128)} %param.6) | copy-start | bytes 786436
  12.8 1.6 %copy-start.2 = (f32[16,16,256]{2,1,0:T(8,128)S(1)}, f32[16,16,256]{2,1,0:T(8,128)}, u32[]{:S(2)}) copy-start(f32[16,16,256]{2,1,0:T(8,128)} %param.4) | copy-start | bytes 786436
  14.3 7.5 %copy-start.4 = (f32[5,256,136]{1,2,0:T(8,128)}, f32[5,256,136]{1,2,0:T(8,128)S(1)}, u32[]{:S(2)}) copy-start(f32[5,256,136]{1,2,0:T(8,128)S(1)} %constant_dynamic-update-slice_fusion) | copy-start | bytes 2088964
  14.5 7.4 %collective-permute-start.2 = (f32[3,22,3,256]{3,2,1,0:T(4,128)S(1)}, f32[3,22,3,256]{3,2,1,0:T(4,128)S(1)}, u32[]{:S(2)}, u32[]{:S(2)}) collective-permute-start(f32[3,22,3,256]{3,2,1,0:T(4,128)S(1)} %get-tuple-element.11), channel_id=1, source_target_pairs={{0,1},{1,2},{2,3},{4,5},{5,6},{6,7},{8,9},{9,10},{10,11},{12,13},{... | collective-permute-start | bytes 608264 | tf_op jit(solution)/shard_map/ppermute | solution.py:20
  18.4 7.8 %collective-permute-start.3 = (f32[3,22,3,256]{3,2,1,0:T(4,128)S(1)}, f32[3,22,3,256]{3,2,1,0:T(4,128)S(1)}, u32[]{:S(2)}, u32[]{:S(2)}) collective-permute-start(f32[3,22,3,256]{3,2,1,0:T(4,128)S(1)} %get-tuple-element.12), channel_id=1, source_target_pairs={{1,0},{2,1},{3,2},{5,4},{6,5},{7,6},{9,8},{10,9},{11,10},{13,12},{... | collective-permute-start | bytes 608264 | tf_op jit(solution)/shard_map/ppermute | solution.py:21
  30.3 1.7 %copy-start.5 = (f32[5,256,136]{1,2,0:T(8,128)S(1)}, f32[5,256,136]{1,2,0:T(8,128)}, u32[]{:S(2)}) copy-start(f32[5,256,136]{1,2,0:T(8,128)} %copy-done.4) | copy-start | bytes 2088964
  32.8 0.7 copy-start.3
  33.5 5.4 %collective-permute-start.4 = (f32[5,8,128]{2,1,0:T(8,128)S(1)}, f32[5,8,128]{2,1,0:T(8,128)S(1)}, u32[]{:S(2)}, u32[]{:S(2)}) collective-permute-start(f32[5,8,128]{2,1,0:T(8,128)S(1)} %slice_bitcast_fusion.29), channel_id=1, source_target_pairs={{4,0},{8,4},{12,8},{5,1},{9,5},{13,9},{6,2},{10,6},{14,10},{7,3},{... | collective-permute-start | bytes 61448 | tf_op jit(solution)/shard_map/ppermute | solution.py:29
  40.0 5.3 %collective-permute-start.6 = (f32[5,4,8,128]{3,2,1,0:T(8,128)S(1)}, f32[5,4,8,128]{3,2,1,0:T(8,128)S(1)}, u32[]{:S(2)}, u32[]{:S(2)}) collective-permute-start(f32[5,4,8,128]{3,2,1,0:T(8,128)S(1)} %get-tuple-element.36), channel_id=1, source_target_pairs={{4,0},{8,4},{12,8},{5,1},{9,5},{13,9},{6,2},{10,6},{14,10},{7,3},{... | collective-permute-start | bytes 245768 | tf_op jit(solution)/shard_map/ppermute | solution.py:21
  41.3 5.5 %collective-permute-start.5 = (f32[5,4,8,128]{3,2,1,0:T(8,128)S(1)}, f32[5,4,8,128]{3,2,1,0:T(8,128)S(1)}, u32[]{:S(2)}, u32[]{:S(2)}) collective-permute-start(f32[5,4,8,128]{3,2,1,0:T(8,128)S(1)} %get-tuple-element.35), channel_id=1, source_target_pairs={{0,4},{4,8},{8,12},{1,5},{5,9},{9,13},{2,6},{6,10},{10,14},{3,7},{... | collective-permute-start | bytes 245768 | tf_op jit(solution)/shard_map/ppermute | solution.py:20
  46.8 0.9 %copy-start.6 = (f32[5,4,8,128]{3,2,1,0:T(8,128)}, f32[5,4,8,128]{3,2,1,0:T(8,128)S(1)}, u32[]{:S(2)}) copy-start(f32[5,4,8,128]{3,2,1,0:T(8,128)S(1)} %collective-permute-done.5) | copy-start | bytes 245764
  47.7 7.6 %collective-permute-start.7 = (f32[5,28,4,128]{3,2,1,0:T(4,128)}, f32[5,28,4,128]{3,2,1,0:T(4,128)}, u32[]{:S(2)}, u32[]{:S(2)}) collective-permute-start(f32[5,28,4,128]{3,2,1,0:T(4,128)} %get-tuple-element.15), channel_id=1, source_target_pairs={{0,1},{1,2},{2,3},{4,5},{5,6},{6,7},{8,9},{9,10},{10,11},{12,13},{... | collective-permute-start | bytes 860168 | tf_op jit(solution)/shard_map/ppermute | solution.py:20
  51.5 8.3 %collective-permute-start.8 = (f32[5,28,4,128]{3,2,1,0:T(4,128)}, f32[5,28,4,128]{3,2,1,0:T(4,128)}, u32[]{:S(2)}, u32[]{:S(2)}) collective-permute-start(f32[5,28,4,128]{3,2,1,0:T(4,128)} %get-tuple-element.16), channel_id=1, source_target_pairs={{1,0},{2,1},{3,2},{5,4},{6,5},{7,6},{9,8},{10,9},{11,10},{13,12},{... | collective-permute-start | bytes 860168 | tf_op jit(solution)/shard_map/ppermute | solution.py:21
  61.1 0.9 copy-start.7
  63.9 4.3 %copy-start.8 = (f32[16,136]{0,1:T(8,128)S(1)}, f32[16,136]{0,1:T(8,128)}, u32[]{:S(2)}) copy-start(f32[16,136]{0,1:T(8,128)} %broadcast_bitcast_fusion.1) | copy-start | bytes 26116
  64.1 4.8 %collective-permute-start.9 = (f32[8,128]{1,0:T(8,128)S(1)}, f32[8,128]{1,0:T(8,128)S(1)}, u32[]{:S(2)}, u32[]{:S(2)}) collective-permute-start(f32[8,128]{1,0:T(8,128)S(1)} %dynamic-slice_bitcast_fusion), channel_id=1, source_target_pairs={{0,4},{4,8},{8,12},{1,5},{5,9},{9,13},{2,6},{6,10},{10,14},{3,7},{... | collective-permute-start | bytes 12296 | tf_op jit(solution)/shard_map/ppermute | solution.py:29
  69.6 5.0 %collective-permute-start.10 = (f32[2,16,256]{2,1,0:T(8,128)S(1)}, f32[2,16,256]{2,1,0:T(8,128)S(1)}, u32[]{:S(2)}, u32[]{:S(2)}) collective-permute-start(f32[2,16,256]{2,1,0:T(8,128)S(1)} %get-tuple-element.37), channel_id=1, source_target_pairs={{0,4},{4,8},{8,12},{1,5},{5,9},{9,13},{2,6},{6,10},{10,14},{3,7},{... | collective-permute-start | bytes 98312 | tf_op jit(solution)/shard_map/ppermute | solution.py:20
  73.2 4.9 %collective-permute-start.11 = (f32[2,16,256]{2,1,0:T(8,128)S(1)}, f32[2,16,256]{2,1,0:T(8,128)S(1)}, u32[]{:S(2)}, u32[]{:S(2)}) collective-permute-start(f32[2,16,256]{2,1,0:T(8,128)S(1)} %get-tuple-element.38), channel_id=1, source_target_pairs={{4,0},{8,4},{12,8},{5,1},{9,5},{13,9},{6,2},{10,6},{14,10},{7,3},{... | collective-permute-start | bytes 98312 | tf_op jit(solution)/shard_map/ppermute | solution.py:21
  78.1 6.0 %collective-permute-start.12 = (f32[20,2,256]{2,1,0:T(2,128)S(1)}, f32[20,2,256]{2,1,0:T(2,128)S(1)}, u32[]{:S(2)}, u32[]{:S(2)}) collective-permute-start(f32[20,2,256]{2,1,0:T(2,128)S(1)} %get-tuple-element.33), channel_id=1, source_target_pairs={{0,1},{1,2},{2,3},{4,5},{5,6},{6,7},{8,9},{9,10},{10,11},{12,13},{... | collective-permute-start | bytes 122888 | tf_op jit(solution)/shard_map/ppermute | solution.py:20
  82.2 5.3 %collective-permute-start.13 = (f32[20,2,256]{2,1,0:T(2,128)S(1)}, f32[20,2,256]{2,1,0:T(2,128)S(1)}, u32[]{:S(2)}, u32[]{:S(2)}) collective-permute-start(f32[20,2,256]{2,1,0:T(2,128)S(1)} %get-tuple-element.34), channel_id=1, source_target_pairs={{1,0},{2,1},{3,2},{5,4},{6,5},{7,6},{9,8},{10,9},{11,10},{13,12},{... | collective-permute-start | bytes 122888 | tf_op jit(solution)/shard_map/ppermute | solution.py:21

commit v3 on v2

--- a/solution.py
+++ b/solution.py
@@ -182,25 +182,19 @@
     slot_sums = slot_sums.reshape(5, width_x + 1, half_y, half_z)
     coarse = slot_sums[:, 1:]
     edge_sums = slot_sums[:, 0]
-    arriving = passed_along(edge_sums, "slab", -1)
     slot_range = jnp.arange(width_x)
     last_slot = (slot_range == count_live - 1).astype(jnp.float32)
-    coarse = coarse + arriving[:, None] * last_slot[None, :, None, None]
-
-    def coarse_extend(coarse_block, rim_width):
-        tail_planes = lax.dynamic_slice_in_dim(
-            coarse_block, count_live - rim_width, rim_width, axis=1
-        )
-        sent_block = jnp.concatenate([coarse_block, tail_planes], axis=1)
-        wide_block = padded(sent_block, (("slab", 1), (("pencil", "sub"), 2)), rim_width)
-        ahead_planes = wide_block[:, width_x + 2 * rim_width :]
-        base_block = wide_block[:, : width_x + 2 * rim_width]
-        return lax.dynamic_update_slice_in_dim(
-            base_block, ahead_planes, rim_width + count_live, axis=1
-        )
-
+    tail_planes = lax.dynamic_slice_in_dim(coarse, count_live - NCS, NCS, axis=1)
+    head_planes = jnp.concatenate([coarse[:, :NCS], edge_sums[:, None]], axis=1)
+    from_prev = passed_along(tail_planes, "slab", 1)
+    from_next = passed_along(head_planes, "slab", -1)
+    coarse = coarse + from_next[:, NCS][:, None] * last_slot[None, :, None, None]
+    prev_last = (jnp.arange(NCS) == NCS - 1).astype(jnp.float32)
+    from_prev = from_prev + edge_sums[:, None] * prev_last[None, :, None, None]
+    x_ext = jnp.concatenate([from_prev, coarse, jnp.zeros_like(tail_planes)], axis=1)
+    x_ext = lax.dynamic_update_slice_in_dim(x_ext, from_next[:, :NCS], NCS + count_live, axis=1)
     coarse_rim = NCS
-    coef_ext = coarse_extend(coarse, coarse_rim)
+    coef_ext = padded(x_ext, ((("pencil", "sub"), 2),), coarse_rim)
     coarse_corr = jnp.zeros((width_x + 2 * NCS, half_y + 2 * NCS, half_z), jnp.float32)
     for sweep_index in range(NCS):
         out_rim = NCS - 1 - sweep_index
@@ -250,14 +244,25 @@
             + OMEGA * (coarse_rhs - (diag_coarse * coarse_center - beside_all)) / safe_coarse
         )
     last_corr = lax.dynamic_index_in_dim(coarse_corr, count_live - 1, axis=0, keepdims=False)
-    corr_wide = jnp.concatenate([passed_along(last_corr, "slab", 1)[None], coarse_corr], axis=0)
+    corr_wide = jnp.concatenate([jnp.zeros_like(last_corr)[None], coarse_corr], axis=0)
     corr_z = jnp.dot(
         corr_wide.reshape((width_x + 1) * half_y, half_z), pair_z.T, precision=lax.Precision.HIGHEST
     )
     correction = jnp.dot(spread_map, corr_z, precision=lax.Precision.HIGHEST)
-    correction = correction.reshape(width_x, width_y, depth_cells)
-    pressure = pressure + correction
-    post_ext = padded(pressure, sides, NU)
+    base = pressure + correction.reshape(width_x, width_y, depth_cells)
+    last_z = jnp.dot(last_corr, pair_z.T, precision=lax.Precision.HIGHEST)
+    last_fine = jnp.dot(pair_y, last_z, precision=lax.Precision.HIGHEST)
+    up_block = jnp.concatenate([base[width_x - NU :], last_fine[None]], axis=0)
+    below_prev = passed_along(up_block, "slab", 1)
+    above_next = passed_along(base[:NU], "slab", -1)
+    from_owner = (slot_ids == -1).astype(jnp.float32)
+    own = base + from_owner[:, None, None] * below_prev[NU][None]
+    tail_ids = jnp.concatenate([aggregate, jnp.full((NU,), -1, aggregate.dtype)])
+    next_ids = lax.dynamic_slice_in_dim(tail_ids, (slab_index + 1) * width_x, NU)
+    to_owner = (next_ids == local_ids[-1]).astype(jnp.float32)
+    high_halo = above_next + to_owner[:, None, None] * last_fine[None]
+    post_x = jnp.concatenate([below_prev[:NU], own, high_halo], axis=0)
+    post_ext = padded(post_x, ((("pencil", "sub"), 1),), NU)
     return sweeps(post_ext, source_ext, faces_ext, NU, width_x)
 
 

time: 90.7 us -> 83.6 us (0.922)
  starting transfers between devices: 38.4 us -> 32 us
  waiting for transfers between devices: 24.6 us -> 19.4 us
  other arithmetic: 13.3 us -> 15.2 us
  local copies, waits for them, and re-layouts: 7.4 us -> 9.06 us
    ppermute x6 -> x4, starting transfers between devices: 23.4 us -> 14.3 us  [padded(): before = lax.ppermute(last, axis, up)]
    ppermute x2 -> x4, starting transfers between devices: 5.29 us -> 10.6 us  [passed_along(): return lax.ppermute(array, axis, pairs)]
    ppermute x6 -> x4, waiting for transfers between devices: 15.8 us -> 10.5 us  [padded(): after = lax.ppermute(leading, axis, down)]
    ppermute x2 -> x4, waiting for transfers between devices: 4.69 us -> 7.52 us  [passed_along(): return lax.ppermute(array, axis, pairs)]
    ppermute x6 -> x4, waiting for transfers between devices: 4.15 us -> 1.39 us  [padded(): before = lax.ppermute(last, axis, up)]
    ppermute x6 -> x4, starting transfers between devices: 9.64 us -> 7.05 us  [padded(): after = lax.ppermute(leading, axis, down)]
    mul x6, local copies, waits for them, and re-layouts: 1.69 us -> 4.07 us  [xy_map(): joint = owner_wide[:, None, :, None] * pick_y[None, :, None, :]]
    add x3, other arithmetic: 0.68 us -> 2.22 us  [body(): coarse_center + OMEGA * (coarse_rhs - (diag_coarse * coarse_center - besi...]
  transfers between devices with their start and end apart: 14 -> 12, of which waited for: 9 -> 7; matrix products, arithmetic and copies ran while one was open for 6% -> 13% of each run, Pallas kernels for 0% -> 0%
where the time goes in v3:
time: 83.6 us; the launch traced here: 82.4 us
  starting transfers between devices  32 us (38%)
  waiting for transfers between devices  19.4 us (23%)
  other arithmetic  15.2 us (18%)
  local copies, waits for them, and re-layouts  9.06 us (11%)
  matrix products  3.55 us (4%)
  between operations  3.17 us (4%)
    ppermute x4, starting transfers between devices, padded(): before = lax.ppermute(last, axis, up)  14.3 us
    ppermute x4, starting transfers between devices, passed_along(): return lax.ppermute(array, axis, pairs)  10.6 us
    ppermute x4, waiting for transfers between devices, padded(): after = lax.ppermute(leading, axis, down)  10.5 us
    ppermute x4, waiting for transfers between devices, passed_along(): return lax.ppermute(array, axis, pairs)  7.52 us
    ppermute x4, starting transfers between devices, padded(): after = lax.ppermute(leading, axis, down)  7.05 us
    mul x6, local copies, waits for them, and re-layouts, xy_map(): joint = owner_wide[:, None, :, None] * pick_y[None, :, None, :]  4.07 us
    add x4, other arithmetic, sweeps(): field_ext = center + OMEGA * (source_now - product) / faces_now[7]  3.75 us
    add x3, other arithmetic, body(): coarse_center + OMEGA * (coarse_rhs - (diag_coarse * coarse_center - besi...  2.22 us
  transfers between devices with their start and end apart: 12, of which 7 were waited for; matrix products, arithmetic and copies ran while one was open for 13% of the time, Pallas kernels for 0%

profile of v3, /device:TPU:1, one launch (start us, length us, event | category | flops | bytes accessed | tf_op | source)
XLA Modules:
  0.0 82.4 jit_solution(133805848099917981)
XLA Ops:
  0.0 1.6 %pad_maximum_fusion.16 = (f32[3,3,16,256]{3,2,1,0:T(8,128)}, f32[3,3,16,256]{3,2,1,0:T(8,128)S(1)}) fusion(f32[1,16,16,256]{3,2,1,0:T(8,128)} %bitcast.216, f32[1,16,16,256]{3,2,1,0:T(8,128)} %bitcast.213, f32[1,16,16,256]{3,2,1,0:T(8,128)} %bitcast.219), kind=kLoop, calls=%fused_computation.179 | loop fusion | flops 147456 | bytes 1081344 | tf_op jit(solution)/shard_map/slice | solution.py:18
  1.6 4.0 %collective-permute-start = (f32[3,3,16,256]{3,2,1,0:T(8,128)}, f32[3,3,16,256]{3,2,1,0:T(8,128)S(1)}, u32[]{:S(2)}, u32[]{:S(2)}) collective-permute-start(f32[3,3,16,256]{3,2,1,0:T(8,128)} %get-tuple-element.13), channel_id=1, source_target_pairs={{0,4},{4,8},{8,12},{1,5},{5,9},{9,13},{2,6},{6,10},{10,14},{3,7},{... | collective-permute-start | bytes 442376 | tf_op jit(solution)/shard_map/ppermute | solution.py:20
  5.6 1.3 %collective-permute-start.1 = (f32[3,3,16,256]{3,2,1,0:T(8,128)S(1)}, f32[3,3,16,256]{3,2,1,0:T(8,128)S(1)}, u32[]{:S(2)}, u32[]{:S(2)}) collective-permute-start(f32[3,3,16,256]{3,2,1,0:T(8,128)S(1)} %get-tuple-element.14), channel_id=1, source_target_pairs={{4,0},{8,4},{12,8},{5,1},{9,5},{13,9},{6,2},{10,6},{14,10},{7,3},{... | collective-permute-start | bytes 442376 | tf_op jit(solution)/shard_map/ppermute | solution.py:21
  7.4 1.4 %fusion.136 = (s32[1]{0:T(128)}, s32[1]{0:T(128)}) fusion(s32[64]{0:T(128)} %param.7), kind=kLoop, calls=%fused_computation.299 | loop fusion | bytes 16 | tf_op jit(solution)/shard_map/slice | solution.py:136
  8.8 1.9 %pad_add_fusion = s32[66]{0:T(128)S(1)} fusion(s32[1]{0:T(128)} %get-tuple-element.55, s32[64]{0:T(128)} %param.7, s32[1]{0:T(128)} %get-tuple-element.54), kind=kLoop, calls=%fused_computation.277 | loop fusion | flops 132 | bytes 528 | tf_op jit(solution)/shard_map/concatenate | solution.py:136
  10.8 0.7 fusion.135
  13.5 0.6 broadcast_bitcast_fusion.1
  14.2 0.6 broadcast_bitcast_fusion
  14.8 0.2 broadcast_multiply_fusion
  15.0 0.5 mul.475
  15.5 0.5 mul.471
  17.3 4.0 %collective-permute-start.2 = (f32[3,22,3,256]{3,2,1,0:T(4,128)S(1)}, f32[3,22,3,256]{3,2,1,0:T(4,128)S(1)}, u32[]{:S(2)}, u32[]{:S(2)}) collective-permute-start(f32[3,22,3,256]{3,2,1,0:T(4,128)S(1)} %get-tuple-element.11), channel_id=1, source_target_pairs={{0,1},{1,2},{2,3},{4,5},{5,6},{6,7},{8,9},{9,10},{10,11},{12,13},{... | collective-permute-start | bytes 608264 | tf_op jit(solution)/shard_map/ppermute | solution.py:20
  21.2 1.9 %collective-permute-start.3 = (f32[3,22,3,256]{3,2,1,0:T(4,128)S(1)}, f32[3,22,3,256]{3,2,1,0:T(4,128)S(1)}, u32[]{:S(2)}, u32[]{:S(2)}) collective-permute-start(f32[3,22,3,256]{3,2,1,0:T(4,128)S(1)} %get-tuple-element.12), channel_id=1, source_target_pairs={{1,0},{2,1},{3,2},{5,4},{6,5},{7,6},{9,8},{10,9},{11,10},{13,12},{... | collective-permute-start | bytes 608264 | tf_op jit(solution)/shard_map/ppermute | solution.py:21
  23.2 1.4 %collective-permute-done.2 = f32[3,22,3,256]{3,2,1,0:T(4,128)S(1)} collective-permute-done((f32[3,22,3,256]{3,2,1,0:T(4,128)S(1)}, f32[3,22,3,256]{3,2,1,0:T(4,128)S(1)}, u32[]{:S(2)}, u32[]{:S(2)}) %collective-permute-start.2) | collective-permute-done | bytes 202784 | tf_op jit(solution)/shard_map/ppermute | solution.py:20
  24.6 4.4 %collective-permute-done.3 = f32[3,22,3,256]{3,2,1,0:T(4,128)S(1)} collective-permute-done((f32[3,22,3,256]{3,2,1,0:T(4,128)S(1)}, f32[3,22,3,256]{3,2,1,0:T(4,128)S(1)}, u32[]{:S(2)}, u32[]{:S(2)}) %collective-permute-start.3) | collective-permute-done | bytes 202784 | tf_op jit(solution)/shard_map/ppermute | solution.py:21
  29.0 0.3 pad_maximum_fusion
  29.3 0.1 slice_bitcast_fusion
  29.4 0.2 divide_select_fusion.1
  29.6 0.2 fusion.123
  29.8 0.2 divide_select_fusion
  30.0 0.2 fusion.124
  30.2 0.2 divide_select_fusion.2
  30.4 1.0 %fusion.12 = (f32[20,20,256]{2,1,0:T(8,128)S(1)}, f32[20,20,256]{2,1,0:T(8,128)S(1)}, f32[20,20,256]{2,1,0:T(8,128)S(1)}) fusion(f32[22,22,256]{2,1,0:T(8,128)S(1)} %get-tuple-element.10, f32[22,22,256]{2,1,0:T(8,128)S(1)} %get-tuple-element.9, f32[20,20,255]{2,1,0:T(8,128)S(1)} %get-tuple-element.20, f32[20,20,255]{2,1,0:T(8,128)S(1)} %get-tuple-element.19, ...), kind=kLoop, calls=%fused_computation.33 | loop fusion | flops 2764800 | bytes 6961424 | tf_op jit(solution)/shard_map/add | solution.py:105
  31.5 0.2 fusion.127
  31.7 0.8 fusion.35
  32.4 0.1 fusion.129
  32.6 0.5 fusion.122
  33.1 0.3 fusion.4
  33.4 0.3 fusion.3
  33.8 0.3 fusion.2
  34.1 0.3 fusion.1
  34.4 0.3 fusion
  34.8 0.8 convolution_bitcast_fusion
  35.6 1.3 %collective-permute-start.5 = (f32[5,5,8,128]{3,2,1,0:T(8,128)S(1)}, f32[5,5,8,128]{3,2,1,0:T(8,128)S(1)}, u32[]{:S(2)}, u32[]{:S(2)}) collective-permute-start(f32[5,5,8,128]{3,2,1,0:T(8,128)S(1)} %pad_maximum_fusion.17), channel_id=1, source_target_pairs={{4,0},{8,4},{12,8},{5,1},{9,5},{13,9},{6,2},{10,6},{14,10},{7,3},{... | collective-permute-start | bytes 307208 | tf_op jit(solution)/shard_map/ppermute | solution.py:29
  36.9 5.0 %collective-permute-done.5 = f32[5,5,8,128]{3,2,1,0:T(8,128)S(1)} collective-permute-done((f32[5,5,8,128]{3,2,1,0:T(8,128)S(1)}, f32[5,5,8,128]{3,2,1,0:T(8,128)S(1)}, u32[]{:S(2)}, u32[]{:S(2)}) %collective-permute-start.5) | collective-permute-done | bytes 102432 | tf_op jit(solution)/shard_map/ppermute | solution.py:29
  42.1 3.4 %collective-permute-start.4 = (f32[5,4,8,128]{3,2,1,0:T(8,128)S(1)}, f32[5,4,8,128]{3,2,1,0:T(8,128)S(1)}, u32[]{:S(2)}, u32[]{:S(2)}) collective-permute-start(f32[5,4,8,128]{3,2,1,0:T(8,128)S(1)} %constant_dynamic-slice_fusion), channel_id=1, source_target_pairs={{0,4},{4,8},{8,12},{1,5},{5,9},{9,13},{2,6},{6,10},{10,14},{3,7},{... | collective-permute-start | bytes 245768 | tf_op jit(solution)/shard_map/ppermute | solution.py:29
  45.4 1.5 %collective-permute-done.4 = f32[5,4,8,128]{3,2,1,0:T(8,128)S(1)} collective-permute-done((f32[5,4,8,128]{3,2,1,0:T(8,128)S(1)}, f32[5,4,8,128]{3,2,1,0:T(8,128)S(1)}, u32[]{:S(2)}, u32[]{:S(2)}) %collective-permute-start.4) | collective-permute-done | bytes 81952 | tf_op jit(solution)/shard_map/ppermute | solution.py:29
  47.1 0.9 %fusion.126 = (f32[5,24,4,128]{3,2,1,0:T(4,128)}, f32[5,24,4,128]{3,2,1,0:T(4,128)}) fusion(f32[5,24,8,128]{3,2,1,0:T(8,128)S(1)} %slice_dynamic-update-slice_fusion), kind=kLoop, calls=%fused_computation.289 | loop fusion | bytes 983040 | tf_op jit(solution)/shard_map/slice | solution.py:18
  48.0 3.7 %collective-permute-start.6 = (f32[5,24,4,128]{3,2,1,0:T(4,128)}, f32[5,24,4,128]{3,2,1,0:T(4,128)}, u32[]{:S(2)}, u32[]{:S(2)}) collective-permute-start(f32[5,24,4,128]{3,2,1,0:T(4,128)} %get-tuple-element.25), channel_id=1, source_target_pairs={{0,1},{1,2},{2,3},{4,5},{5,6},{6,7},{8,9},{9,10},{10,11},{12,13},{... | collective-permute-start | bytes 737288 | tf_op jit(solution)/shard_map/ppermute | solution.py:20
  51.7 1.9 %collective-permute-start.7 = (f32[5,24,4,128]{3,2,1,0:T(4,128)}, f32[5,24,4,128]{3,2,1,0:T(4,128)}, u32[]{:S(2)}, u32[]{:S(2)}) collective-permute-start(f32[5,24,4,128]{3,2,1,0:T(4,128)} %get-tuple-element.26), channel_id=1, source_target_pairs={{1,0},{2,1},{3,2},{5,4},{6,5},{7,6},{9,8},{10,9},{11,10},{13,12},{... | collective-permute-start | bytes 737288 | tf_op jit(solution)/shard_map/ppermute | solution.py:21
  53.6 1.2 %compare_convert_fusion = f32[2]{0:T(128)} fusion(s32[]{:T(128)S(6)} %select_n.108, s32[64]{0:T(128)S(1)} %copy-done.5, s32[]{:T(128)} %bitcast.24), kind=kLoop, calls=%fused_computation.252 | loop fusion | flops 4 | bytes 272 | tf_op jit(solution)/shard_map/convert_element_type | solution.py:262
  54.9 0.9 %copy.7 = f32[16,136]{1,0:T(8,128)S(1)} copy(f32[16,136]{0,1:T(8,128)} %broadcast_bitcast_fusion.1) | data formatting | bytes 17408 | tf_op jit(solution)/shard_map/mul | solution.py:175
  55.8 1.0 %copy.8 = f32[16,136]{1,0:T(8,128)S(1)} copy(f32[16,136]{0,1:T(8,128)} %broadcast_bitcast_fusion) | data formatting | bytes 17408 | tf_op jit(solution)/shard_map/mul | solution.py:175
  56.8 2.7 %collective-permute-done.7 = f32[5,24,4,128]{3,2,1,0:T(4,128)} collective-permute-done((f32[5,24,4,128]{3,2,1,0:T(4,128)}, f32[5,24,4,128]{3,2,1,0:T(4,128)}, u32[]{:S(2)}, u32[]{:S(2)}) %collective-permute-start.7) | collective-permute-done | bytes 245792 | tf_op jit(solution)/shard_map/ppermute | solution.py:21
  59.5 1.3 %pad_maximum_fusion.1 = f32[5,24,16,128]{3,2,1,0:T(8,128)S(1)} fusion(f32[5,24,4,128]{3,2,1,0:T(4,128)} %collective-permute-done.7, f32[5,24,8,128]{3,2,1,0:T(8,128)S(1)} %slice_dynamic-update-slice_fusion, f32[5,24,4,128]{3,2,1,0:T(4,128)} %collective-permute-done.6), kind=kLoop, calls=%fused_computation.14 | loop fusion | flops 491520 | bytes 1966080 | tf_op jit(solution)/shard_map/concatenate | solution.py:22
  60.9 0.2 fusion.56
  61.1 0.1 fusion.132
  61.2 0.3 fusion.64
  61.6 1.0 %fusion.75 = f32[18,10,128]{2,1,0:T(8,128)S(1)} fusion(f32[20,12,128]{2,1,0:T(8,128)S(1)} %fusion.64, f32[5,24,16,128]{3,2,1,0:T(8,128)S(1)} %pad_maximum_fusion.1, f32[18,10,127]{2,1,0:T(8,128)S(1)} %get-tuple-element.44, f32[18,10,127]{2,1,0:T(8,128)S(1)} %get-tuple-element.43, f32[18,10,127]{2,1,0:T(8,128)S(1)} %bitcast.229, ...), kind=kLoop, calls=%fused_computation.156 | loop fusion | flops 599040 | bytes 2117520 | tf_op jit(solution)/shard_map/add | solution.py:243
  62.8 0.9 %fusion.91 = f32[16,8,128]{2,1,0:T(8,128)S(1)} fusion(f32[18,10,128]{2,1,0:T(8,128)S(1)} %fusion.75, f32[5,24,8,128]{3,2,1,0:T(8,128)S(1)} %slice_dynamic-update-slice_fusion, f32[16,8,127]{2,1,0:T(8,128)S(1)} %get-tuple-element.46, f32[16,8,127]{2,1,0:T(8,128)S(1)} %get-tuple-element.45, f32[16,8,127]{2,1,0:T(8,128)S(1)} %bitcast.230, ...), kind=kLoop, calls=%fused_computation.191 | loop fusion | flops 425984 | bytes 1720320 | tf_op jit(solution)/shard_map/add | solution.py:243
  63.6 0.3 convolution_bitcast_fusion.1
  63.9 0.2 fusion.85
  64.1 0.3 fusion.112
  64.4 0.4 convolution_add_fusion
  64.8 1.3 %collective-permute-start.9 = (f32[2,16,256]{2,1,0:T(8,128)S(1)}, f32[2,16,256]{2,1,0:T(8,128)S(1)}, u32[]{:S(2)}, u32[]{:S(2)}) collective-permute-start(f32[2,16,256]{2,1,0:T(8,128)S(1)} %get-tuple-element.40), channel_id=1, source_target_pairs={{4,0},{8,4},{12,8},{5,1},{9,5},{13,9},{6,2},{10,6},{14,10},{7,3},{... | collective-permute-start | bytes 98312 | tf_op jit(solution)/shard_map/ppermute | solution.py:29
  66.1 4.6 %collective-permute-start.8 = (f32[3,16,256]{2,1,0:T(8,128)S(1)}, f32[3,16,256]{2,1,0:T(8,128)S(1)}, u32[]{:S(2)}, u32[]{:S(2)}) collective-permute-start(f32[3,16,256]{2,1,0:T(8,128)S(1)} %pad_maximum_fusion.19), channel_id=1, source_target_pairs={{0,4},{4,8},{8,12},{1,5},{5,9},{9,13},{2,6},{6,10},{10,14},{3,7},{... | collective-permute-start | bytes 147464 | tf_op jit(solution)/shard_map/ppermute | solution.py:29
  70.8 1.1 %collective-permute-done.8 = f32[3,16,256]{2,1,0:T(8,128)S(1)} collective-permute-done((f32[3,16,256]{2,1,0:T(8,128)S(1)}, f32[3,16,256]{2,1,0:T(8,128)S(1)}, u32[]{:S(2)}, u32[]{:S(2)}) %collective-permute-start.8) | collective-permute-done | bytes 49184 | tf_op jit(solution)/shard_map/ppermute | solution.py:29
  72.1 2.6 %collective-permute-start.10 = (f32[20,2,256]{2,1,0:T(2,128)S(1)}, f32[20,2,256]{2,1,0:T(2,128)S(1)}, u32[]{:S(2)}, u32[]{:S(2)}) collective-permute-start(f32[20,2,256]{2,1,0:T(2,128)S(1)} %get-tuple-element.37), channel_id=1, source_target_pairs={{0,1},{1,2},{2,3},{4,5},{5,6},{6,7},{8,9},{9,10},{10,11},{12,13},{... | collective-permute-start | bytes 122888 | tf_op jit(solution)/shard_map/ppermute | solution.py:20
  74.7 1.9 %collective-permute-start.11 = (f32[20,2,256]{2,1,0:T(2,128)S(1)}, f32[20,2,256]{2,1,0:T(2,128)S(1)}, u32[]{:S(2)}, u32[]{:S(2)}) collective-permute-start(f32[20,2,256]{2,1,0:T(2,128)S(1)} %get-tuple-element.38), channel_id=1, source_target_pairs={{1,0},{2,1},{3,2},{5,4},{6,5},{7,6},{9,8},{10,9},{11,10},{13,12},{... | collective-permute-start | bytes 122888 | tf_op jit(solution)/shard_map/ppermute | solution.py:21
  76.6 3.4 %collective-permute-done.11 = f32[20,2,256]{2,1,0:T(2,128)S(1)} collective-permute-done((f32[20,2,256]{2,1,0:T(2,128)S(1)}, f32[20,2,256]{2,1,0:T(2,128)S(1)}, u32[]{:S(2)}, u32[]{:S(2)}) %collective-permute-start.11) | collective-permute-done | bytes 40992 | tf_op jit(solution)/shard_map/ppermute | solution.py:21
  80.1 0.2 fusion.125
  80.3 0.8 %fusion.24 = f32[18,18,256]{2,1,0:T(8,128)S(1)} fusion(f32[20,2,256]{2,1,0:T(2,128)S(1)} %collective-permute-done.11, f32[2,16,256]{2,1,0:T(8,128)S(1)} %multiply_add_fusion.3, f32[16,16,256]{2,1,0:T(8,128)S(1)} %multiply_add_fusion.1, f32[2,16,256]{2,1,0:T(8,128)S(1)} %slice.822, f32[20,2,256]{2,1,0:T(2,128)S(1)} %collective-permute-done.10, ...), kind=kLoop, calls=%fused_computation.55 | loop fusion | flops 1907712 | bytes 4796320 | tf_op jit(solution)/shard_map/add | solution.py:105
  81.1 0.1 fusion.128
  81.2 1.2 %fusion.45 = f32[16,16,256]{2,1,0:T(8,128)} fusion(f32[18,18,256]{2,1,0:T(8,128)S(1)} %fusion.24, f32[22,22,256]{2,1,0:T(8,128)S(1)} %get-tuple-element.9, f32[16,16,255]{2,1,0:T(8,128)S(1)} %get-tuple-element.30, f32[16,16,255]{2,1,0:T(8,128)S(1)} %get-tuple-element.29, f32[22,21,256]{2,1,0:T(8,128)S(1)} %divide_select_fusion, ...), kind=kLoop, calls=%fused_computation.97 | loop fusion | flops 1114112 | bytes 4075968 | tf_op jit(solution)/shard_map/add | solution.py:105
  (81 shorter events, 2.3 us)
Async XLA Ops:
  1.6 15.5 %collective-permute-start = (f32[3,3,16,256]{3,2,1,0:T(8,128)}, f32[3,3,16,256]{3,2,1,0:T(8,128)S(1)}, u32[]{:S(2)}, u32[]{:S(2)}) collective-permute-start(f32[3,3,16,256]{3,2,1,0:T(8,128)} %get-tuple-element.13), channel_id=1, source_target_pairs={{0,4},{4,8},{8,12},{1,5},{5,9},{9,13},{2,6},{6,10},{10,14},{3,7},{... | collective-permute-start | bytes 442376 | tf_op jit(solution)/shard_map/ppermute | solution.py:20
  5.6 11.5 %collective-permute-start.1 = (f32[3,3,16,256]{3,2,1,0:T(8,128)S(1)}, f32[3,3,16,256]{3,2,1,0:T(8,128)S(1)}, u32[]{:S(2)}, u32[]{:S(2)}) collective-permute-start(f32[3,3,16,256]{3,2,1,0:T(8,128)S(1)} %get-tuple-element.14), channel_id=1, source_target_pairs={{4,0},{8,4},{12,8},{5,1},{9,5},{13,9},{6,2},{10,6},{14,10},{7,3},{... | collective-permute-start | bytes 442376 | tf_op jit(solution)/shard_map/ppermute | solution.py:21
  6.9 8.5 %copy-start.7 = (s32[16]{0:T(128)}, s32[16]{0:T(128)S(1)}, u32[]{:S(2)}) copy-start(s32[16]{0:T(128)S(1)} %and_select_fusion.1) | copy-start | bytes 196
  15.5 1.7 %copy-start = (f32[16,16,256]{2,1,0:T(8,128)S(1)}, f32[16,16,256]{2,1,0:T(8,128)}, u32[]{:S(2)}) copy-start(f32[16,16,256]{2,1,0:T(8,128)} %param.5) | copy-start | bytes 786436
  15.5 1.7 %copy-start.1 = (f32[16,16,256]{2,1,0:T(8,128)S(1)}, f32[16,16,256]{2,1,0:T(8,128)}, u32[]{:S(2)}) copy-start(f32[16,16,256]{2,1,0:T(8,128)} %param.6) | copy-start | bytes 786436
  15.5 1.6 %copy-start.2 = (f32[16,16,256]{2,1,0:T(8,128)S(1)}, f32[16,16,256]{2,1,0:T(8,128)}, u32[]{:S(2)}) copy-start(f32[16,16,256]{2,1,0:T(8,128)} %param.4) | copy-start | bytes 786436
  17.1 12.2 %copy-start.3 = (f32[5,256,136]{1,2,0:T(8,128)}, f32[5,256,136]{1,2,0:T(8,128)S(1)}, u32[]{:S(2)}) copy-start(f32[5,256,136]{1,2,0:T(8,128)S(1)} %constant_dynamic-update-slice_fusion) | copy-start | bytes 2088964
  17.3 7.4 %collective-permute-start.2 = (f32[3,22,3,256]{3,2,1,0:T(4,128)S(1)}, f32[3,22,3,256]{3,2,1,0:T(4,128)S(1)}, u32[]{:S(2)}, u32[]{:S(2)}) collective-permute-start(f32[3,22,3,256]{3,2,1,0:T(4,128)S(1)} %get-tuple-element.11), channel_id=1, source_target_pairs={{0,1},{1,2},{2,3},{4,5},{5,6},{6,7},{8,9},{9,10},{10,11},{12,13},{... | collective-permute-start | bytes 608264 | tf_op jit(solution)/shard_map/ppermute | solution.py:20
  21.2 7.8 %collective-permute-start.3 = (f32[3,22,3,256]{3,2,1,0:T(4,128)S(1)}, f32[3,22,3,256]{3,2,1,0:T(4,128)S(1)}, u32[]{:S(2)}, u32[]{:S(2)}) collective-permute-start(f32[3,22,3,256]{3,2,1,0:T(4,128)S(1)} %get-tuple-element.12), channel_id=1, source_target_pairs={{1,0},{2,1},{3,2},{5,4},{6,5},{7,6},{9,8},{10,9},{11,10},{13,12},{... | collective-permute-start | bytes 608264 | tf_op jit(solution)/shard_map/ppermute | solution.py:21
  33.1 1.7 %copy-start.4 = (f32[5,256,136]{1,2,0:T(8,128)S(1)}, f32[5,256,136]{1,2,0:T(8,128)}, u32[]{:S(2)}) copy-start(f32[5,256,136]{1,2,0:T(8,128)} %copy-done.3) | copy-start | bytes 2088964
  35.6 6.3 %collective-permute-start.5 = (f32[5,5,8,128]{3,2,1,0:T(8,128)S(1)}, f32[5,5,8,128]{3,2,1,0:T(8,128)S(1)}, u32[]{:S(2)}, u32[]{:S(2)}) collective-permute-start(f32[5,5,8,128]{3,2,1,0:T(8,128)S(1)} %pad_maximum_fusion.17), channel_id=1, source_target_pairs={{4,0},{8,4},{12,8},{5,1},{9,5},{13,9},{6,2},{10,6},{14,10},{7,3},{... | collective-permute-start | bytes 307208 | tf_op jit(solution)/shard_map/ppermute | solution.py:29
  41.9 11.7 %copy-start.5 = (s32[64]{0:T(128)S(1)}, s32[64]{0:T(128)}, u32[]{:S(2)}) copy-start(s32[64]{0:T(128)} %param.7) | copy-start | bytes 772
  42.1 4.8 %collective-permute-start.4 = (f32[5,4,8,128]{3,2,1,0:T(8,128)S(1)}, f32[5,4,8,128]{3,2,1,0:T(8,128)S(1)}, u32[]{:S(2)}, u32[]{:S(2)}) collective-permute-start(f32[5,4,8,128]{3,2,1,0:T(8,128)S(1)} %constant_dynamic-slice_fusion), channel_id=1, source_target_pairs={{0,4},{4,8},{8,12},{1,5},{5,9},{9,13},{2,6},{6,10},{10,14},{3,7},{... | collective-permute-start | bytes 245768 | tf_op jit(solution)/shard_map/ppermute | solution.py:29
  48.0 8.8 %collective-permute-start.6 = (f32[5,24,4,128]{3,2,1,0:T(4,128)}, f32[5,24,4,128]{3,2,1,0:T(4,128)}, u32[]{:S(2)}, u32[]{:S(2)}) collective-permute-start(f32[5,24,4,128]{3,2,1,0:T(4,128)} %get-tuple-element.25), channel_id=1, source_target_pairs={{0,1},{1,2},{2,3},{4,5},{5,6},{6,7},{8,9},{9,10},{10,11},{12,13},{... | collective-permute-start | bytes 737288 | tf_op jit(solution)/shard_map/ppermute | solution.py:20
  51.7 7.8 %collective-permute-start.7 = (f32[5,24,4,128]{3,2,1,0:T(4,128)}, f32[5,24,4,128]{3,2,1,0:T(4,128)}, u32[]{:S(2)}, u32[]{:S(2)}) collective-permute-start(f32[5,24,4,128]{3,2,1,0:T(4,128)} %get-tuple-element.26), channel_id=1, source_target_pairs={{1,0},{2,1},{3,2},{5,4},{6,5},{7,6},{9,8},{10,9},{11,10},{13,12},{... | collective-permute-start | bytes 737288 | tf_op jit(solution)/shard_map/ppermute | solution.py:21
  62.6 1.5 %copy-start.8 = (s32[16]{0:T(128)S(1)}, s32[16]{0:T(128)}, u32[]{:S(2)}) copy-start(s32[16]{0:T(128)} %copy-done.7) | copy-start | bytes 196
  62.7 8.1 %copy-start.6 = (f32[2]{0:T(128)S(1)}, f32[2]{0:T(128)}, u32[]{:S(2)}) copy-start(f32[2]{0:T(128)} %compare_convert_fusion) | copy-start | bytes 28
  64.8 6.0 %collective-permute-start.9 = (f32[2,16,256]{2,1,0:T(8,128)S(1)}, f32[2,16,256]{2,1,0:T(8,128)S(1)}, u32[]{:S(2)}, u32[]{:S(2)}) collective-permute-start(f32[2,16,256]{2,1,0:T(8,128)S(1)} %get-tuple-element.40), channel_id=1, source_target_pairs={{4,0},{8,4},{12,8},{5,1},{9,5},{13,9},{6,2},{10,6},{14,10},{7,3},{... | collective-permute-start | bytes 98312 | tf_op jit(solution)/shard_map/ppermute | solution.py:29
  66.1 5.8 %collective-permute-start.8 = (f32[3,16,256]{2,1,0:T(8,128)S(1)}, f32[3,16,256]{2,1,0:T(8,128)S(1)}, u32[]{:S(2)}, u32[]{:S(2)}) collective-permute-start(f32[3,16,256]{2,1,0:T(8,128)S(1)} %pad_maximum_fusion.19), channel_id=1, source_target_pairs={{0,4},{4,8},{8,12},{1,5},{5,9},{9,13},{2,6},{6,10},{10,14},{3,7},{... | collective-permute-start | bytes 147464 | tf_op jit(solution)/shard_map/ppermute | solution.py:29
  72.1 4.5 %collective-permute-start.10 = (f32[20,2,256]{2,1,0:T(2,128)S(1)}, f32[20,2,256]{2,1,0:T(2,128)S(1)}, u32[]{:S(2)}, u32[]{:S(2)}) collective-permute-start(f32[20,2,256]{2,1,0:T(2,128)S(1)} %get-tuple-element.37), channel_id=1, source_target_pairs={{0,1},{1,2},{2,3},{4,5},{5,6},{6,7},{8,9},{9,10},{10,11},{12,13},{... | collective-permute-start | bytes 122888 | tf_op jit(solution)/shard_map/ppermute | solution.py:20
  74.7 5.3 %collective-permute-start.11 = (f32[20,2,256]{2,1,0:T(2,128)S(1)}, f32[20,2,256]{2,1,0:T(2,128)S(1)}, u32[]{:S(2)}, u32[]{:S(2)}) collective-permute-start(f32[20,2,256]{2,1,0:T(2,128)S(1)} %get-tuple-element.38), channel_id=1, source_target_pairs={{1,0},{2,1},{3,2},{5,4},{6,5},{7,6},{9,8},{10,9},{11,10},{13,12},{... | collective-permute-start | bytes 122888 | tf_op jit(solution)/shard_map/ppermute | solution.py:21

commit v4 on v3

--- a/solution.py
+++ b/solution.py
@@ -186,6 +186,7 @@
     last_slot = (slot_range == count_live - 1).astype(jnp.float32)
     tail_planes = lax.dynamic_slice_in_dim(coarse, count_live - NCS, NCS, axis=1)
     head_planes = jnp.concatenate([coarse[:, :NCS], edge_sums[:, None]], axis=1)
+    tail_planes, head_planes = lax.optimization_barrier((tail_planes, head_planes))
     from_prev = passed_along(tail_planes, "slab", 1)
     from_next = passed_along(head_planes, "slab", -1)
     coarse = coarse + from_next[:, NCS][:, None] * last_slot[None, :, None, None]

time: 83.6 us -> 80.6 us (0.964)
  waiting for transfers between devices: 19.4 us -> 17 us
    ppermute x4, waiting for transfers between devices: 7.52 us -> 5.09 us  [passed_along(): return lax.ppermute(array, axis, pairs)]
  transfers between devices with their start and end apart: 12 -> 12, of which waited for: 7 -> 7; matrix products, arithmetic and copies ran while one was open for 13% -> 14% of each run, Pallas kernels for 0% -> 0%
where the time goes in v4:
time: 80.6 us; the launch traced here: 79.9 us
  starting transfers between devices  31.9 us (40%)
  waiting for transfers between devices  17 us (21%)
  other arithmetic  15.3 us (19%)
  local copies, waits for them, and re-layouts  8.96 us (11%)
  matrix products  3.57 us (4%)
  between operations  3.13 us (4%)
    ppermute x4, starting transfers between devices, padded(): before = lax.ppermute(last, axis, up)  14 us
    ppermute x4, starting transfers between devices, passed_along(): return lax.ppermute(array, axis, pairs)  10.8 us
    ppermute x4, waiting for transfers between devices, padded(): after = lax.ppermute(leading, axis, down)  10.5 us
    ppermute x4, starting transfers between devices, padded(): after = lax.ppermute(leading, axis, down)  7.05 us
    ppermute x4, waiting for transfers between devices, passed_along(): return lax.ppermute(array, axis, pairs)  5.09 us
    mul x6, local copies, waits for them, and re-layouts, xy_map(): joint = owner_wide[:, None, :, None] * pick_y[None, :, None, :]  4.09 us
    add x4, other arithmetic, sweeps(): field_ext = center + OMEGA * (source_now - product) / faces_now[7]  3.75 us
    add x3, other arithmetic, body(): coarse_center + OMEGA * (coarse_rhs - (diag_coarse * coarse_center - besi...  2.22 us
  transfers between devices with their start and end apart: 12, of which 7 were waited for; matrix products, arithmetic and copies ran while one was open for 14% of the time, Pallas kernels for 0%

profile of v4, /device:TPU:1, one launch (start us, length us, event | category | flops | bytes accessed | tf_op | source)
XLA Modules:
  0.0 79.9 jit_solution(792185171468297678)
XLA Ops:
  0.0 1.6 %pad_maximum_fusion.16 = (f32[3,3,16,256]{3,2,1,0:T(8,128)}, f32[3,3,16,256]{3,2,1,0:T(8,128)S(1)}) fusion(f32[1,16,16,256]{3,2,1,0:T(8,128)} %bitcast.216, f32[1,16,16,256]{3,2,1,0:T(8,128)} %bitcast.213, f32[1,16,16,256]{3,2,1,0:T(8,128)} %bitcast.219), kind=kLoop, calls=%fused_computation.179 | loop fusion | flops 147456 | bytes 1081344 | tf_op jit(solution)/shard_map/slice | solution.py:18
  1.6 4.0 %collective-permute-start = (f32[3,3,16,256]{3,2,1,0:T(8,128)}, f32[3,3,16,256]{3,2,1,0:T(8,128)S(1)}, u32[]{:S(2)}, u32[]{:S(2)}) collective-permute-start(f32[3,3,16,256]{3,2,1,0:T(8,128)} %get-tuple-element.17), channel_id=1, source_target_pairs={{0,4},{4,8},{8,12},{1,5},{5,9},{9,13},{2,6},{6,10},{10,14},{3,7},{... | collective-permute-start | bytes 442376 | tf_op jit(solution)/shard_map/ppermute | solution.py:20
  5.6 1.3 %collective-permute-start.1 = (f32[3,3,16,256]{3,2,1,0:T(8,128)S(1)}, f32[3,3,16,256]{3,2,1,0:T(8,128)S(1)}, u32[]{:S(2)}, u32[]{:S(2)}) collective-permute-start(f32[3,3,16,256]{3,2,1,0:T(8,128)S(1)} %get-tuple-element.18), channel_id=1, source_target_pairs={{4,0},{8,4},{12,8},{5,1},{9,5},{13,9},{6,2},{10,6},{14,10},{7,3},{... | collective-permute-start | bytes 442376 | tf_op jit(solution)/shard_map/ppermute | solution.py:21
  7.4 1.3 %fusion.135 = (s32[1]{0:T(128)}, s32[1]{0:T(128)}) fusion(s32[64]{0:T(128)} %param.7), kind=kLoop, calls=%fused_computation.298 | loop fusion | bytes 16 | tf_op jit(solution)/shard_map/slice | solution.py:136
  8.7 1.9 %pad_add_fusion = s32[66]{0:T(128)S(1)} fusion(s32[1]{0:T(128)} %get-tuple-element.57, s32[64]{0:T(128)} %param.7, s32[1]{0:T(128)} %get-tuple-element.56), kind=kLoop, calls=%fused_computation.277 | loop fusion | flops 132 | bytes 528 | tf_op jit(solution)/shard_map/concatenate | solution.py:136
  10.7 0.6 fusion.134
  13.4 0.6 broadcast_bitcast_fusion.1
  14.1 0.6 broadcast_bitcast_fusion
  14.7 0.2 broadcast_multiply_fusion
  14.9 0.5 mul.475
  15.4 0.5 mul.471
  17.2 4.0 %collective-permute-start.2 = (f32[3,22,3,256]{3,2,1,0:T(4,128)S(1)}, f32[3,22,3,256]{3,2,1,0:T(4,128)S(1)}, u32[]{:S(2)}, u32[]{:S(2)}) collective-permute-start(f32[3,22,3,256]{3,2,1,0:T(4,128)S(1)} %get-tuple-element.15), channel_id=1, source_target_pairs={{0,1},{1,2},{2,3},{4,5},{5,6},{6,7},{8,9},{9,10},{10,11},{12,13},{... | collective-permute-start | bytes 608264 | tf_op jit(solution)/shard_map/ppermute | solution.py:20
  21.1 1.9 %collective-permute-start.3 = (f32[3,22,3,256]{3,2,1,0:T(4,128)S(1)}, f32[3,22,3,256]{3,2,1,0:T(4,128)S(1)}, u32[]{:S(2)}, u32[]{:S(2)}) collective-permute-start(f32[3,22,3,256]{3,2,1,0:T(4,128)S(1)} %get-tuple-element.16), channel_id=1, source_target_pairs={{1,0},{2,1},{3,2},{5,4},{6,5},{7,6},{9,8},{10,9},{11,10},{13,12},{... | collective-permute-start | bytes 608264 | tf_op jit(solution)/shard_map/ppermute | solution.py:21
  23.1 1.4 %collective-permute-done.2 = f32[3,22,3,256]{3,2,1,0:T(4,128)S(1)} collective-permute-done((f32[3,22,3,256]{3,2,1,0:T(4,128)S(1)}, f32[3,22,3,256]{3,2,1,0:T(4,128)S(1)}, u32[]{:S(2)}, u32[]{:S(2)}) %collective-permute-start.2) | collective-permute-done | bytes 202784 | tf_op jit(solution)/shard_map/ppermute | solution.py:20
  24.5 4.4 %collective-permute-done.3 = f32[3,22,3,256]{3,2,1,0:T(4,128)S(1)} collective-permute-done((f32[3,22,3,256]{3,2,1,0:T(4,128)S(1)}, f32[3,22,3,256]{3,2,1,0:T(4,128)S(1)}, u32[]{:S(2)}, u32[]{:S(2)}) %collective-permute-start.3) | collective-permute-done | bytes 202784 | tf_op jit(solution)/shard_map/ppermute | solution.py:21
  28.9 0.3 pad_maximum_fusion
  29.2 0.1 slice_bitcast_fusion
  29.3 0.2 divide_select_fusion.1
  29.5 0.2 fusion.123
  29.7 0.2 divide_select_fusion
  29.9 0.2 fusion.124
  30.1 0.2 divide_select_fusion.2
  30.3 1.0 %fusion.12 = (f32[20,20,256]{2,1,0:T(8,128)S(1)}, f32[20,20,256]{2,1,0:T(8,128)S(1)}, f32[20,20,256]{2,1,0:T(8,128)S(1)}) fusion(f32[22,22,256]{2,1,0:T(8,128)S(1)} %get-tuple-element.14, f32[22,22,256]{2,1,0:T(8,128)S(1)} %get-tuple-element.13, f32[20,20,255]{2,1,0:T(8,128)S(1)} %get-tuple-element.24, f32[20,20,255]{2,1,0:T(8,128)S(1)} %get-tuple-element.23, ...), kind=kLoop, calls=%fused_computation.33 | loop fusion | flops 2764800 | bytes 6961424 | tf_op jit(solution)/shard_map/add | solution.py:105
  31.4 0.2 fusion.127
  31.5 0.8 fusion.35
  32.3 0.1 fusion.129
  32.5 0.5 fusion.122
  33.0 0.3 fusion.4
  33.3 0.3 fusion.3
  33.7 0.3 fusion.2
  34.0 0.3 fusion.1
  34.3 0.3 fusion
  34.7 0.8 convolution_bitcast_fusion
  35.6 4.3 %collective-permute-start.4 = (f32[5,4,8,128]{3,2,1,0:T(8,128)S(1)}, f32[5,4,8,128]{3,2,1,0:T(8,128)S(1)}, u32[]{:S(2)}, u32[]{:S(2)}) collective-permute-start(f32[5,4,8,128]{3,2,1,0:T(8,128)S(1)} %constant_dynamic-slice_fusion), channel_id=1, source_target_pairs={{0,4},{4,8},{8,12},{1,5},{5,9},{9,13},{2,6},{6,10},{10,14},{3,7},{... | collective-permute-start | bytes 245768 | tf_op jit(solution)/shard_map/ppermute | solution.py:29
  39.9 1.3 %collective-permute-start.5 = (f32[5,5,8,128]{3,2,1,0:T(8,128)S(1)}, f32[5,5,8,128]{3,2,1,0:T(8,128)S(1)}, u32[]{:S(2)}, u32[]{:S(2)}) collective-permute-start(f32[5,5,8,128]{3,2,1,0:T(8,128)S(1)} %pad_maximum_fusion.17), channel_id=1, source_target_pairs={{4,0},{8,4},{12,8},{5,1},{9,5},{13,9},{6,2},{10,6},{14,10},{7,3},{... | collective-permute-start | bytes 307208 | tf_op jit(solution)/shard_map/ppermute | solution.py:29
  41.2 0.2 collective-permute-done.4
  41.4 3.9 %collective-permute-done.5 = f32[5,5,8,128]{3,2,1,0:T(8,128)S(1)} collective-permute-done((f32[5,5,8,128]{3,2,1,0:T(8,128)S(1)}, f32[5,5,8,128]{3,2,1,0:T(8,128)S(1)}, u32[]{:S(2)}, u32[]{:S(2)}) %collective-permute-start.5) | collective-permute-done | bytes 102432 | tf_op jit(solution)/shard_map/ppermute | solution.py:29
  45.5 0.9 %fusion.126 = (f32[5,24,4,128]{3,2,1,0:T(4,128)}, f32[5,24,4,128]{3,2,1,0:T(4,128)}) fusion(f32[5,24,8,128]{3,2,1,0:T(8,128)S(1)} %slice_dynamic-update-slice_fusion), kind=kLoop, calls=%fused_computation.289 | loop fusion | bytes 983040 | tf_op jit(solution)/shard_map/slice | solution.py:18
  46.4 3.2 %collective-permute-start.6 = (f32[5,24,4,128]{3,2,1,0:T(4,128)}, f32[5,24,4,128]{3,2,1,0:T(4,128)}, u32[]{:S(2)}, u32[]{:S(2)}) collective-permute-start(f32[5,24,4,128]{3,2,1,0:T(4,128)} %get-tuple-element.29), channel_id=1, source_target_pairs={{0,1},{1,2},{2,3},{4,5},{5,6},{6,7},{8,9},{9,10},{10,11},{12,13},{... | collective-permute-start | bytes 737288 | tf_op jit(solution)/shard_map/ppermute | solution.py:20
  49.5 1.9 %collective-permute-start.7 = (f32[5,24,4,128]{3,2,1,0:T(4,128)}, f32[5,24,4,128]{3,2,1,0:T(4,128)}, u32[]{:S(2)}, u32[]{:S(2)}) collective-permute-start(f32[5,24,4,128]{3,2,1,0:T(4,128)} %get-tuple-element.30), channel_id=1, source_target_pairs={{1,0},{2,1},{3,2},{5,4},{6,5},{7,6},{9,8},{10,9},{11,10},{13,12},{... | collective-permute-start | bytes 737288 | tf_op jit(solution)/shard_map/ppermute | solution.py:21
  51.5 1.3 %compare_convert_fusion = f32[2]{0:T(128)} fusion(s32[]{:T(128)S(6)} %select_n.108, s32[64]{0:T(128)S(1)} %copy-done.5, s32[]{:T(128)} %bitcast.24), kind=kLoop, calls=%fused_computation.252 | loop fusion | flops 4 | bytes 272 | tf_op jit(solution)/shard_map/convert_element_type | solution.py:263
  52.7 0.9 %copy.7 = f32[16,136]{1,0:T(8,128)S(1)} copy(f32[16,136]{0,1:T(8,128)} %broadcast_bitcast_fusion.1) | data formatting | bytes 17408 | tf_op jit(solution)/shard_map/mul | solution.py:175
  53.7 1.0 %copy.8 = f32[16,136]{1,0:T(8,128)S(1)} copy(f32[16,136]{0,1:T(8,128)} %broadcast_bitcast_fusion) | data formatting | bytes 17408 | tf_op jit(solution)/shard_map/mul | solution.py:175
  54.7 2.7 %collective-permute-done.7 = f32[5,24,4,128]{3,2,1,0:T(4,128)} collective-permute-done((f32[5,24,4,128]{3,2,1,0:T(4,128)}, f32[5,24,4,128]{3,2,1,0:T(4,128)}, u32[]{:S(2)}, u32[]{:S(2)}) %collective-permute-start.7) | collective-permute-done | bytes 245792 | tf_op jit(solution)/shard_map/ppermute | solution.py:21
  57.4 1.3 %pad_maximum_fusion.1 = f32[5,24,16,128]{3,2,1,0:T(8,128)S(1)} fusion(f32[5,24,4,128]{3,2,1,0:T(4,128)} %collective-permute-done.7, f32[5,24,8,128]{3,2,1,0:T(8,128)S(1)} %slice_dynamic-update-slice_fusion, f32[5,24,4,128]{3,2,1,0:T(4,128)} %collective-permute-done.6), kind=kLoop, calls=%fused_computation.14 | loop fusion | flops 491520 | bytes 1966080 | tf_op jit(solution)/shard_map/concatenate | solution.py:22
  58.7 0.2 fusion.56
  58.9 0.1 fusion.131
  59.0 0.3 fusion.64
  59.4 1.0 %fusion.75 = f32[18,10,128]{2,1,0:T(8,128)S(1)} fusion(f32[20,12,128]{2,1,0:T(8,128)S(1)} %fusion.64, f32[5,24,16,128]{3,2,1,0:T(8,128)S(1)} %pad_maximum_fusion.1, f32[18,10,127]{2,1,0:T(8,128)S(1)} %get-tuple-element.46, f32[18,10,127]{2,1,0:T(8,128)S(1)} %get-tuple-element.45, f32[18,10,127]{2,1,0:T(8,128)S(1)} %bitcast.229, ...), kind=kLoop, calls=%fused_computation.156 | loop fusion | flops 599040 | bytes 2117520 | tf_op jit(solution)/shard_map/add | solution.py:244
  60.6 0.9 %fusion.91 = f32[16,8,128]{2,1,0:T(8,128)S(1)} fusion(f32[18,10,128]{2,1,0:T(8,128)S(1)} %fusion.75, f32[5,24,8,128]{3,2,1,0:T(8,128)S(1)} %slice_dynamic-update-slice_fusion, f32[16,8,127]{2,1,0:T(8,128)S(1)} %get-tuple-element.48, f32[16,8,127]{2,1,0:T(8,128)S(1)} %get-tuple-element.47, f32[16,8,127]{2,1,0:T(8,128)S(1)} %bitcast.230, ...), kind=kLoop, calls=%fused_computation.191 | loop fusion | flops 425984 | bytes 1720320 | tf_op jit(solution)/shard_map/add | solution.py:244
  61.5 0.3 convolution_bitcast_fusion.1
  61.8 0.2 fusion.85
  62.0 0.3 fusion.112
  62.2 0.4 convolution_add_fusion
  62.6 1.3 %collective-permute-start.9 = (f32[2,16,256]{2,1,0:T(8,128)S(1)}, f32[2,16,256]{2,1,0:T(8,128)S(1)}, u32[]{:S(2)}, u32[]{:S(2)}) collective-permute-start(f32[2,16,256]{2,1,0:T(8,128)S(1)} %get-tuple-element.42), channel_id=1, source_target_pairs={{4,0},{8,4},{12,8},{5,1},{9,5},{13,9},{6,2},{10,6},{14,10},{7,3},{... | collective-permute-start | bytes 98312 | tf_op jit(solution)/shard_map/ppermute | solution.py:29
  63.9 4.0 %collective-permute-start.8 = (f32[3,16,256]{2,1,0:T(8,128)S(1)}, f32[3,16,256]{2,1,0:T(8,128)S(1)}, u32[]{:S(2)}, u32[]{:S(2)}) collective-permute-start(f32[3,16,256]{2,1,0:T(8,128)S(1)} %pad_maximum_fusion.19), channel_id=1, source_target_pairs={{0,4},{4,8},{8,12},{1,5},{5,9},{9,13},{2,6},{6,10},{10,14},{3,7},{... | collective-permute-start | bytes 147464 | tf_op jit(solution)/shard_map/ppermute | solution.py:29
  68.0 1.1 %collective-permute-done.8 = f32[3,16,256]{2,1,0:T(8,128)S(1)} collective-permute-done((f32[3,16,256]{2,1,0:T(8,128)S(1)}, f32[3,16,256]{2,1,0:T(8,128)S(1)}, u32[]{:S(2)}, u32[]{:S(2)}) %collective-permute-start.8) | collective-permute-done | bytes 49184 | tf_op jit(solution)/shard_map/ppermute | solution.py:29
  69.2 2.9 %collective-permute-start.10 = (f32[20,2,256]{2,1,0:T(2,128)S(1)}, f32[20,2,256]{2,1,0:T(2,128)S(1)}, u32[]{:S(2)}, u32[]{:S(2)}) collective-permute-start(f32[20,2,256]{2,1,0:T(2,128)S(1)} %get-tuple-element.39), channel_id=1, source_target_pairs={{0,1},{1,2},{2,3},{4,5},{5,6},{6,7},{8,9},{9,10},{10,11},{12,13},{... | collective-permute-start | bytes 122888 | tf_op jit(solution)/shard_map/ppermute | solution.py:20
  72.1 1.9 %collective-permute-start.11 = (f32[20,2,256]{2,1,0:T(2,128)S(1)}, f32[20,2,256]{2,1,0:T(2,128)S(1)}, u32[]{:S(2)}, u32[]{:S(2)}) collective-permute-start(f32[20,2,256]{2,1,0:T(2,128)S(1)} %get-tuple-element.40), channel_id=1, source_target_pairs={{1,0},{2,1},{3,2},{5,4},{6,5},{7,6},{9,8},{10,9},{11,10},{13,12},{... | collective-permute-start | bytes 122888 | tf_op jit(solution)/shard_map/ppermute | solution.py:21
  74.1 3.4 %collective-permute-done.11 = f32[20,2,256]{2,1,0:T(2,128)S(1)} collective-permute-done((f32[20,2,256]{2,1,0:T(2,128)S(1)}, f32[20,2,256]{2,1,0:T(2,128)S(1)}, u32[]{:S(2)}, u32[]{:S(2)}) %collective-permute-start.11) | collective-permute-done | bytes 40992 | tf_op jit(solution)/shard_map/ppermute | solution.py:21
  77.5 0.2 fusion.125
  77.7 0.8 %fusion.24 = f32[18,18,256]{2,1,0:T(8,128)S(1)} fusion(f32[20,2,256]{2,1,0:T(2,128)S(1)} %collective-permute-done.11, f32[2,16,256]{2,1,0:T(8,128)S(1)} %multiply_add_fusion.3, f32[16,16,256]{2,1,0:T(8,128)S(1)} %multiply_add_fusion.1, f32[2,16,256]{2,1,0:T(8,128)S(1)} %slice.822, f32[20,2,256]{2,1,0:T(2,128)S(1)} %collective-permute-done.10, ...), kind=kLoop, calls=%fused_computation.55 | loop fusion | flops 1907712 | bytes 4796320 | tf_op jit(solution)/shard_map/add | solution.py:105
  78.6 0.1 fusion.128
  78.7 1.2 %fusion.45 = f32[16,16,256]{2,1,0:T(8,128)} fusion(f32[18,18,256]{2,1,0:T(8,128)S(1)} %fusion.24, f32[22,22,256]{2,1,0:T(8,128)S(1)} %get-tuple-element.13, f32[16,16,255]{2,1,0:T(8,128)S(1)} %get-tuple-element.34, f32[16,16,255]{2,1,0:T(8,128)S(1)} %get-tuple-element.33, f32[22,21,256]{2,1,0:T(8,128)S(1)} %divide_select_fusion, ...), kind=kLoop, calls=%fused_computation.97 | loop fusion | flops 1114112 | bytes 4075968 | tf_op jit(solution)/shard_map/add | solution.py:105
  (82 shorter events, 2.4 us)
Async XLA Ops:
  1.6 15.4 %collective-permute-start = (f32[3,3,16,256]{3,2,1,0:T(8,128)}, f32[3,3,16,256]{3,2,1,0:T(8,128)S(1)}, u32[]{:S(2)}, u32[]{:S(2)}) collective-permute-start(f32[3,3,16,256]{3,2,1,0:T(8,128)} %get-tuple-element.17), channel_id=1, source_target_pairs={{0,4},{4,8},{8,12},{1,5},{5,9},{9,13},{2,6},{6,10},{10,14},{3,7},{... | collective-permute-start | bytes 442376 | tf_op jit(solution)/shard_map/ppermute | solution.py:20
  5.6 11.4 %collective-permute-start.1 = (f32[3,3,16,256]{3,2,1,0:T(8,128)S(1)}, f32[3,3,16,256]{3,2,1,0:T(8,128)S(1)}, u32[]{:S(2)}, u32[]{:S(2)}) collective-permute-start(f32[3,3,16,256]{3,2,1,0:T(8,128)S(1)} %get-tuple-element.18), channel_id=1, source_target_pairs={{4,0},{8,4},{12,8},{5,1},{9,5},{13,9},{6,2},{10,6},{14,10},{7,3},{... | collective-permute-start | bytes 442376 | tf_op jit(solution)/shard_map/ppermute | solution.py:21
  6.9 8.4 %copy-start.7 = (s32[16]{0:T(128)}, s32[16]{0:T(128)S(1)}, u32[]{:S(2)}) copy-start(s32[16]{0:T(128)S(1)} %and_select_fusion.1) | copy-start | bytes 196
  15.4 1.6 %copy-start = (f32[16,16,256]{2,1,0:T(8,128)S(1)}, f32[16,16,256]{2,1,0:T(8,128)}, u32[]{:S(2)}) copy-start(f32[16,16,256]{2,1,0:T(8,128)} %param.5) | copy-start | bytes 786436
  15.4 1.6 %copy-start.1 = (f32[16,16,256]{2,1,0:T(8,128)S(1)}, f32[16,16,256]{2,1,0:T(8,128)}, u32[]{:S(2)}) copy-start(f32[16,16,256]{2,1,0:T(8,128)} %param.6) | copy-start | bytes 786436
  15.4 1.6 %copy-start.2 = (f32[16,16,256]{2,1,0:T(8,128)S(1)}, f32[16,16,256]{2,1,0:T(8,128)}, u32[]{:S(2)}) copy-start(f32[16,16,256]{2,1,0:T(8,128)} %param.4) | copy-start | bytes 786436
  17.0 12.2 %copy-start.3 = (f32[5,256,136]{1,2,0:T(8,128)}, f32[5,256,136]{1,2,0:T(8,128)S(1)}, u32[]{:S(2)}) copy-start(f32[5,256,136]{1,2,0:T(8,128)S(1)} %constant_dynamic-update-slice_fusion) | copy-start | bytes 2088964
  17.2 7.4 %collective-permute-start.2 = (f32[3,22,3,256]{3,2,1,0:T(4,128)S(1)}, f32[3,22,3,256]{3,2,1,0:T(4,128)S(1)}, u32[]{:S(2)}, u32[]{:S(2)}) collective-permute-start(f32[3,22,3,256]{3,2,1,0:T(4,128)S(1)} %get-tuple-element.15), channel_id=1, source_target_pairs={{0,1},{1,2},{2,3},{4,5},{5,6},{6,7},{8,9},{9,10},{10,11},{12,13},{... | collective-permute-start | bytes 608264 | tf_op jit(solution)/shard_map/ppermute | solution.py:20
  21.1 7.8 %collective-permute-start.3 = (f32[3,22,3,256]{3,2,1,0:T(4,128)S(1)}, f32[3,22,3,256]{3,2,1,0:T(4,128)S(1)}, u32[]{:S(2)}, u32[]{:S(2)}) collective-permute-start(f32[3,22,3,256]{3,2,1,0:T(4,128)S(1)} %get-tuple-element.16), channel_id=1, source_target_pairs={{1,0},{2,1},{3,2},{5,4},{6,5},{7,6},{9,8},{10,9},{11,10},{13,12},{... | collective-permute-start | bytes 608264 | tf_op jit(solution)/shard_map/ppermute | solution.py:21
  33.0 1.7 %copy-start.4 = (f32[5,256,136]{1,2,0:T(8,128)S(1)}, f32[5,256,136]{1,2,0:T(8,128)}, u32[]{:S(2)}) copy-start(f32[5,256,136]{1,2,0:T(8,128)} %copy-done.3) | copy-start | bytes 2088964
  35.5 15.9 %copy-start.5 = (s32[64]{0:T(128)S(1)}, s32[64]{0:T(128)}, u32[]{:S(2)}) copy-start(s32[64]{0:T(128)} %param.7) | copy-start | bytes 772
  35.6 5.7 %collective-permute-start.4 = (f32[5,4,8,128]{3,2,1,0:T(8,128)S(1)}, f32[5,4,8,128]{3,2,1,0:T(8,128)S(1)}, u32[]{:S(2)}, u32[]{:S(2)}) collective-permute-start(f32[5,4,8,128]{3,2,1,0:T(8,128)S(1)} %constant_dynamic-slice_fusion), channel_id=1, source_target_pairs={{0,4},{4,8},{8,12},{1,5},{5,9},{9,13},{2,6},{6,10},{10,14},{3,7},{... | collective-permute-start | bytes 245768 | tf_op jit(solution)/shard_map/ppermute | solution.py:29
  39.9 5.4 %collective-permute-start.5 = (f32[5,5,8,128]{3,2,1,0:T(8,128)S(1)}, f32[5,5,8,128]{3,2,1,0:T(8,128)S(1)}, u32[]{:S(2)}, u32[]{:S(2)}) collective-permute-start(f32[5,5,8,128]{3,2,1,0:T(8,128)S(1)} %pad_maximum_fusion.17), channel_id=1, source_target_pairs={{4,0},{8,4},{12,8},{5,1},{9,5},{13,9},{6,2},{10,6},{14,10},{7,3},{... | collective-permute-start | bytes 307208 | tf_op jit(solution)/shard_map/ppermute | solution.py:29
  46.4 8.3 %collective-permute-start.6 = (f32[5,24,4,128]{3,2,1,0:T(4,128)}, f32[5,24,4,128]{3,2,1,0:T(4,128)}, u32[]{:S(2)}, u32[]{:S(2)}) collective-permute-start(f32[5,24,4,128]{3,2,1,0:T(4,128)} %get-tuple-element.29), channel_id=1, source_target_pairs={{0,1},{1,2},{2,3},{4,5},{5,6},{6,7},{8,9},{9,10},{10,11},{12,13},{... | collective-permute-start | bytes 737288 | tf_op jit(solution)/shard_map/ppermute | solution.py:20
  49.5 7.8 %collective-permute-start.7 = (f32[5,24,4,128]{3,2,1,0:T(4,128)}, f32[5,24,4,128]{3,2,1,0:T(4,128)}, u32[]{:S(2)}, u32[]{:S(2)}) collective-permute-start(f32[5,24,4,128]{3,2,1,0:T(4,128)} %get-tuple-element.30), channel_id=1, source_target_pairs={{1,0},{2,1},{3,2},{5,4},{6,5},{7,6},{9,8},{10,9},{11,10},{13,12},{... | collective-permute-start | bytes 737288 | tf_op jit(solution)/shard_map/ppermute | solution.py:21
  60.5 1.5 %copy-start.8 = (s32[16]{0:T(128)S(1)}, s32[16]{0:T(128)}, u32[]{:S(2)}) copy-start(s32[16]{0:T(128)} %copy-done.7) | copy-start | bytes 196
  60.5 7.5 %copy-start.6 = (f32[2]{0:T(128)S(1)}, f32[2]{0:T(128)}, u32[]{:S(2)}) copy-start(f32[2]{0:T(128)} %compare_convert_fusion) | copy-start | bytes 28
  62.6 5.3 %collective-permute-start.9 = (f32[2,16,256]{2,1,0:T(8,128)S(1)}, f32[2,16,256]{2,1,0:T(8,128)S(1)}, u32[]{:S(2)}, u32[]{:S(2)}) collective-permute-start(f32[2,16,256]{2,1,0:T(8,128)S(1)} %get-tuple-element.42), channel_id=1, source_target_pairs={{4,0},{8,4},{12,8},{5,1},{9,5},{13,9},{6,2},{10,6},{14,10},{7,3},{... | collective-permute-start | bytes 98312 | tf_op jit(solution)/shard_map/ppermute | solution.py:29
  63.9 5.2 %collective-permute-start.8 = (f32[3,16,256]{2,1,0:T(8,128)S(1)}, f32[3,16,256]{2,1,0:T(8,128)S(1)}, u32[]{:S(2)}, u32[]{:S(2)}) collective-permute-start(f32[3,16,256]{2,1,0:T(8,128)S(1)} %pad_maximum_fusion.19), channel_id=1, source_target_pairs={{0,4},{4,8},{8,12},{1,5},{5,9},{9,13},{2,6},{6,10},{10,14},{3,7},{... | collective-permute-start | bytes 147464 | tf_op jit(solution)/shard_map/ppermute | solution.py:29
  69.2 4.8 %collective-permute-start.10 = (f32[20,2,256]{2,1,0:T(2,128)S(1)}, f32[20,2,256]{2,1,0:T(2,128)S(1)}, u32[]{:S(2)}, u32[]{:S(2)}) collective-permute-start(f32[20,2,256]{2,1,0:T(2,128)S(1)} %get-tuple-element.39), channel_id=1, source_target_pairs={{0,1},{1,2},{2,3},{4,5},{5,6},{6,7},{8,9},{9,10},{10,11},{12,13},{... | collective-permute-start | bytes 122888 | tf_op jit(solution)/shard_map/ppermute | solution.py:20
  72.1 5.3 %collective-permute-start.11 = (f32[20,2,256]{2,1,0:T(2,128)S(1)}, f32[20,2,256]{2,1,0:T(2,128)S(1)}, u32[]{:S(2)}, u32[]{:S(2)}) collective-permute-start(f32[20,2,256]{2,1,0:T(2,128)S(1)} %get-tuple-element.40), channel_id=1, source_target_pairs={{1,0},{2,1},{3,2},{5,4},{6,5},{7,6},{9,8},{10,9},{11,10},{13,12},{... | collective-permute-start | bytes 122888 | tf_op jit(solution)/shard_map/ppermute | solution.py:21

commit v5 on v4

--- a/solution.py
+++ b/solution.py
@@ -21,6 +21,40 @@
         after = lax.ppermute(leading, axis, down)
         array = jnp.concatenate([before, array, after], axis=dim)
     return array
+
+
+def halo_round(array, dim_x, dim_y, width):
+    count_x = lax.axis_size("slab")
+    count_y = lax.axis_size(("pencil", "sub"))
+    size_x, size_y = array.shape[dim_x], array.shape[dim_y]
+
+    def part(lo_x, hi_x, lo_y, hi_y):
+        block = lax.slice_in_dim(array, lo_x, hi_x, axis=dim_x)
+        return lax.slice_in_dim(block, lo_y, hi_y, axis=dim_y)
+
+    def moved(block, step_x, step_y):
+        pairs = [
+            (i * count_y + j, (i + step_x) * count_y + j + step_y)
+            for i in range(count_x)
+            for j in range(count_y)
+            if 0 <= i + step_x < count_x and 0 <= j + step_y < count_y
+        ]
+        return lax.ppermute(block, ("slab", "pencil", "sub"), pairs)
+
+    spans_x = {-1: (0, width), 0: (0, size_x), 1: (size_x - width, size_x)}
+    spans_y = {-1: (0, width), 0: (0, size_y), 1: (size_y - width, size_y)}
+    rows = []
+    for from_x in (-1, 0, 1):
+        row = []
+        for from_y in (-1, 0, 1):
+            if from_x == 0 and from_y == 0:
+                row.append(array)
+                continue
+            lo_x, hi_x = spans_x[-from_x]
+            lo_y, hi_y = spans_y[-from_y]
+            row.append(moved(part(lo_x, hi_x, lo_y, hi_y), -from_x, -from_y))
+        rows.append(jnp.concatenate(row, axis=dim_y))
+    return jnp.concatenate(rows, axis=dim_x)
 
 
 def passed_along(array, axis, by):
@@ -117,7 +151,7 @@
     sides = (("slab", 0), (("pencil", "sub"), 1))
     stacked_sides = (("slab", 1), (("pencil", "sub"), 2))
     fine_rim = NU + 1
-    ext_all = padded(jnp.stack([permeability, source, pressure]), stacked_sides, fine_rim)
+    ext_all = halo_round(jnp.stack([permeability, source, pressure]), 1, 2, fine_rim)
     perm_ext = ext_all[0]
     source_ext = crop(ext_all[1], 1)
     glob_x = slab_index * width_x - fine_rim + jnp.arange(width_x + 2 * fine_rim)

time: 80.6 us -> 95.9 us (1.19)
  starting transfers between devices: 31.9 us -> 46.2 us
  waiting for transfers between devices: 17 us -> 12.1 us
  other arithmetic: 15.3 us -> 19.3 us
  local copies, waits for them, and re-layouts: 8.96 us -> 10.5 us
    ppermute x0 -> x8, starting transfers between devices: none -> 23.5 us  [moved(): return lax.ppermute(block, ('slab', 'pencil', 'sub'), pairs)]
    ppermute x4 -> x2, starting transfers between devices: 14 us -> 7.02 us  [padded(): before = lax.ppermute(last, axis, up)]
    ppermute x4 -> x2, waiting for transfers between devices: 10.5 us -> 6.19 us  [padded(): after = lax.ppermute(leading, axis, down)]
    ppermute x4 -> x2, starting transfers between devices: 7.05 us -> 3.84 us  [padded(): after = lax.ppermute(leading, axis, down)]
    slice x0 -> x2, other arithmetic: none -> 3.14 us  [the longest x1 1.62 us: part(): return lax.slice_in_dim(block, lo_y, hi_y, axis=dim_y)]
    slice x3 -> x1, other arithmetic: 1.73 us -> 0.03 us  [padded(): last = lax.slice_in_dim(array, length - width, length, axis=dim)]
    slice x0 -> x2, local copies, waits for them, and re-layouts: none -> 1.43 us  [the longest x1 0.75 us: part(): return lax.slice_in_dim(block, lo_y, hi_y, axis=dim_y)]
    ppermute x4 -> x2, waiting for transfers between devices: 1.39 us -> 0.01 us  [padded(): before = lax.ppermute(last, axis, up)]
  transfers between devices with their start and end apart: 12 -> 16, of which waited for: 7 -> 6; matrix products, arithmetic and copies ran while one was open for 14% -> 16% of each run, Pallas kernels for 0% -> 0%
where the time goes in v5:
time: 95.9 us; the launch traced here: 95 us
  starting transfers between devices  46.2 us (48%)
  other arithmetic  19.3 us (20%)
  waiting for transfers between devices  12.1 us (13%)
  local copies, waits for them, and re-layouts  10.5 us (11%)
  matrix products  3.56 us (4%)
  between operations  3.24 us (3%)
    ppermute x8, starting transfers between devices, moved(): return lax.ppermute(block, ('slab', 'pencil', 'sub'), pairs)  23.5 us
    ppermute x4, starting transfers between devices, passed_along(): return lax.ppermute(array, axis, pairs)  11.9 us
    ppermute x2, starting transfers between devices, padded(): before = lax.ppermute(last, axis, up)  7.02 us
    ppermute x2, waiting for transfers between devices, padded(): after = lax.ppermute(leading, axis, down)  6.19 us
    ppermute x4, waiting for transfers between devices, passed_along(): return lax.ppermute(array, axis, pairs)  5.11 us
    mul x6, local copies, waits for them, and re-layouts, xy_map(): joint = owner_wide[:, None, :, None] * pick_y[None, :, None, :]  4.09 us
    ppermute x2, starting transfers between devices, padded(): after = lax.ppermute(leading, axis, down)  3.84 us
    add x4, other arithmetic, sweeps(): field_ext = center + OMEGA * (source_now - product) / faces_now[7]  3.73 us
  transfers between devices with their start and end apart: 16, of which 6 were waited for; matrix products, arithmetic and copies ran while one was open for 16% of the time, Pallas kernels for 0%

profile of v5, /device:TPU:1, one launch (start us, length us, event | category | flops | bytes accessed | tf_op | source)
XLA Modules:
  0.0 95.0 jit_solution(10118986125929322781)
XLA Ops:
  0.0 1.6 %pad_maximum_fusion.19 = (f32[3,3,3,256]{3,2,1,0:T(4,128)}, f32[3,3,3,256]{3,2,1,0:T(4,128)}, f32[3,3,3,256]{3,2,1,0:T(4,128)}, f32[3,3,3,256]{3,2,1,0:T(4,128)}) fusion(f32[1,16,16,256]{3,2,1,0:T(8,128)} %bitcast.217, f32[1,16,16,256]{3,2,1,0:T(8,128)} %bitcast.213, f32[1,16,16,256]{3,2,1,0:T(8,128)} %bitcast.221), kind=kLoop, calls=%fused_computation.221 | loop fusion | flops 55296 | bytes 897024 | tf_op jit(solution)/shard_map/slice | solution.py:33
  1.6 6.3 %collective-permute-start = (f32[3,3,3,256]{3,2,1,0:T(4,128)}, f32[3,3,3,256]{3,2,1,0:T(4,128)}, u32[]{:S(2)}, u32[]{:S(2)}) collective-permute-start(f32[3,3,3,256]{3,2,1,0:T(4,128)} %get-tuple-element.15), channel_id=1, source_target_pairs={{0,5},{1,6},{2,7},{4,9},{5,10},{6,11},{8,13},{9,14},{10,15},{16,21... | collective-permute-start | bytes 82952 | tf_op jit(solution)/shard_map/ppermute | solution.py:42
  7.9 1.3 %collective-permute-start.7 = (f32[3,3,3,256]{3,2,1,0:T(4,128)}, f32[3,3,3,256]{3,2,1,0:T(4,128)}, u32[]{:S(2)}, u32[]{:S(2)}) collective-permute-start(f32[3,3,3,256]{3,2,1,0:T(4,128)} %get-tuple-element.16), channel_id=1, source_target_pairs={{5,0},{6,1},{7,2},{9,4},{10,5},{11,6},{13,8},{14,9},{15,10},{21,16... | collective-permute-start | bytes 82952 | tf_op jit(solution)/shard_map/ppermute | solution.py:42
  9.2 1.3 %collective-permute-start.5 = (f32[3,3,3,256]{3,2,1,0:T(4,128)}, f32[3,3,3,256]{3,2,1,0:T(4,128)}, u32[]{:S(2)}, u32[]{:S(2)}) collective-permute-start(f32[3,3,3,256]{3,2,1,0:T(4,128)} %get-tuple-element.17), channel_id=1, source_target_pairs={{4,1},{5,2},{6,3},{8,5},{9,6},{10,7},{12,9},{13,10},{14,11},{20,17... | collective-permute-start | bytes 82952 | tf_op jit(solution)/shard_map/ppermute | solution.py:42
  10.5 1.5 %pad_maximum_fusion.9 = f32[3,3,16,256]{3,2,1,0:T(8,128)} fusion(f32[1,16,16,256]{3,2,1,0:T(8,128)} %bitcast.218, f32[1,16,16,256]{3,2,1,0:T(8,128)} %bitcast.214, f32[1,16,16,256]{3,2,1,0:T(8,128)} %bitcast.222), kind=kLoop, calls=%fused_computation.173 | loop fusion | flops 73728 | bytes 933888 | tf_op jit(solution)/shard_map/slice | solution.py:32
  12.0 1.3 %collective-permute-start.6 = (f32[3,3,16,256]{3,2,1,0:T(8,128)}, f32[3,3,16,256]{3,2,1,0:T(8,128)}, u32[]{:S(2)}, u32[]{:S(2)}) collective-permute-start(f32[3,3,16,256]{3,2,1,0:T(8,128)} %pad_maximum_fusion.9), channel_id=1, source_target_pairs={{4,0},{5,1},{6,2},{7,3},{8,4},{9,5},{10,6},{11,7},{12,8},{13,9},{1... | collective-permute-start | bytes 442376 | tf_op jit(solution)/shard_map/ppermute | solution.py:42
  13.4 0.7 slice.734
  14.1 5.2 %collective-permute-start.1 = (f32[3,3,16,256]{3,2,1,0:T(8,128)}, f32[3,3,16,256]{3,2,1,0:T(8,128)}, u32[]{:S(2)}, u32[]{:S(2)}) collective-permute-start(f32[3,3,16,256]{3,2,1,0:T(8,128)} %slice.734), channel_id=1, source_target_pairs={{0,4},{1,5},{2,6},{3,7},{4,8},{5,9},{6,10},{7,11},{8,12},{9,13},{1... | collective-permute-start | bytes 442376 | tf_op jit(solution)/shard_map/ppermute | solution.py:42
  19.6 0.6 fusion.136
  20.2 1.4 %pad_add_fusion = s32[66]{0:T(128)S(1)} fusion(s32[1]{0:T(128)} %get-tuple-element.59, s32[64]{0:T(128)S(1)} %copy-done.5, s32[1]{0:T(128)} %get-tuple-element.58), kind=kLoop, calls=%fused_computation.275 | loop fusion | flops 132 | bytes 528 | tf_op jit(solution)/shard_map/concatenate | solution.py:170
  21.6 0.7 fusion.135
  24.3 0.7 compare_convert_fusion.1
  25.0 0.7 fusion.122
  25.9 0.6 broadcast_bitcast_fusion.1
  26.6 0.6 broadcast_bitcast_fusion
  27.3 0.2 broadcast_multiply_fusion
  27.5 0.5 mul.475
  28.0 0.5 mul.471
  28.7 0.6 fusion.116
  29.4 4.4 %collective-permute-start.3 = (f32[3,16,3,256]{3,2,1,0:T(4,128)}, f32[3,16,3,256]{3,2,1,0:T(4,128)S(1)}, u32[]{:S(2)}, u32[]{:S(2)}) collective-permute-start(f32[3,16,3,256]{3,2,1,0:T(4,128)} %get-tuple-element.19), channel_id=1, source_target_pairs={{0,1},{1,2},{2,3},{4,5},{5,6},{6,7},{8,9},{9,10},{10,11},{12,13},{... | collective-permute-start | bytes 442376 | tf_op jit(solution)/shard_map/ppermute | solution.py:42
  33.8 1.9 %collective-permute-start.4 = (f32[3,16,3,256]{3,2,1,0:T(4,128)S(1)}, f32[3,16,3,256]{3,2,1,0:T(4,128)S(1)}, u32[]{:S(2)}, u32[]{:S(2)}) collective-permute-start(f32[3,16,3,256]{3,2,1,0:T(4,128)S(1)} %get-tuple-element.20), channel_id=1, source_target_pairs={{1,0},{2,1},{3,2},{5,4},{6,5},{7,6},{9,8},{10,9},{11,10},{13,12},{... | collective-permute-start | bytes 442376 | tf_op jit(solution)/shard_map/ppermute | solution.py:42
  35.7 0.5 multiply_add_fusion.4
  36.2 1.9 %collective-permute-start.2 = (f32[3,3,3,256]{3,2,1,0:T(4,128)}, f32[3,3,3,256]{3,2,1,0:T(4,128)S(1)}, u32[]{:S(2)}, u32[]{:S(2)}) collective-permute-start(f32[3,3,3,256]{3,2,1,0:T(4,128)} %get-tuple-element.18), channel_id=1, source_target_pairs={{1,4},{2,5},{3,6},{5,8},{6,9},{7,10},{9,12},{10,13},{11,14},{17,20... | collective-permute-start | bytes 82952 | tf_op jit(solution)/shard_map/ppermute | solution.py:42
  38.2 0.5 compare_convert_fusion.3
  39.4 0.6 pad.49.clone
  40.0 0.8 collective-permute-done.4
  40.8 1.3 %maximum_maximum_fusion = f32[3,22,22,256]{3,2,1,0:T(8,128)S(1)} fusion(f32[3,3,3,256]{3,2,1,0:T(4,128)} %collective-permute-done.7, f32[3,3,16,256]{3,2,1,0:T(8,128)} %collective-permute-done.6, f32[3,3,3,256]{3,2,1,0:T(4,128)} %collective-permute-done.5, f32[3,16,3,256]{3,2,1,0:T(4,128)S(1)} %collective-permute-done.4, f32[1,16,16,256]{3,2,1,0:T(8,128)S(1)} %bitcast.220, ...), kind=kLoop, calls=%fused_computation | loop fusion | flops 3717120 | bytes 2973696 | tf_op jit(solution)/shard_map/concatenate | solution.py:57
  42.3 0.2 fusion.124
  43.0 0.2 divide_select_fusion.2
  43.2 0.2 copy-done.11
  43.4 1.0 %fusion.12 = (f32[20,20,256]{2,1,0:T(8,128)S(1)}, f32[20,20,256]{2,1,0:T(8,128)S(1)}, f32[20,20,256]{2,1,0:T(8,128)S(1)}) fusion(f32[22,22,256]{2,1,0:T(8,128)S(1)} %get-tuple-element.14, f32[22,22,256]{2,1,0:T(8,128)S(1)} %get-tuple-element.13, f32[20,20,255]{2,1,0:T(8,128)S(1)} %get-tuple-element.26, f32[20,20,255]{2,1,0:T(8,128)S(1)} %get-tuple-element.25, ...), kind=kLoop, calls=%fused_computation.34 | loop fusion | flops 2764800 | bytes 6961424 | tf_op jit(solution)/shard_map/add | solution.py:139
  44.7 0.8 fusion.35
  45.6 0.5 fusion.123
  46.1 0.3 fusion.4
  46.4 0.3 fusion.3
  46.8 0.3 fusion.2
  47.1 0.3 fusion.1
  47.4 0.3 fusion
  47.8 0.8 convolution_bitcast_fusion
  48.7 5.3 %collective-permute-start.8 = (f32[5,4,8,128]{3,2,1,0:T(8,128)S(1)}, f32[5,4,8,128]{3,2,1,0:T(8,128)S(1)}, u32[]{:S(2)}, u32[]{:S(2)}) collective-permute-start(f32[5,4,8,128]{3,2,1,0:T(8,128)S(1)} %constant_dynamic-slice_fusion), channel_id=1, source_target_pairs={{0,4},{4,8},{8,12},{1,5},{5,9},{9,13},{2,6},{6,10},{10,14},{3,7},{... | collective-permute-start | bytes 245768 | tf_op jit(solution)/shard_map/ppermute | solution.py:63
  54.0 1.3 %collective-permute-start.9 = (f32[5,5,8,128]{3,2,1,0:T(8,128)S(1)}, f32[5,5,8,128]{3,2,1,0:T(8,128)S(1)}, u32[]{:S(2)}, u32[]{:S(2)}) collective-permute-start(f32[5,5,8,128]{3,2,1,0:T(8,128)S(1)} %pad_maximum_fusion.10), channel_id=1, source_target_pairs={{4,0},{8,4},{12,8},{5,1},{9,5},{13,9},{6,2},{10,6},{14,10},{7,3},{... | collective-permute-start | bytes 307208 | tf_op jit(solution)/shard_map/ppermute | solution.py:63
  55.6 3.9 %collective-permute-done.9 = f32[5,5,8,128]{3,2,1,0:T(8,128)S(1)} collective-permute-done((f32[5,5,8,128]{3,2,1,0:T(8,128)S(1)}, f32[5,5,8,128]{3,2,1,0:T(8,128)S(1)}, u32[]{:S(2)}, u32[]{:S(2)}) %collective-permute-start.9) | collective-permute-done | bytes 102432 | tf_op jit(solution)/shard_map/ppermute | solution.py:63
  59.7 0.9 fusion.127
  60.5 4.1 %collective-permute-start.10 = (f32[5,24,4,128]{3,2,1,0:T(4,128)}, f32[5,24,4,128]{3,2,1,0:T(4,128)}, u32[]{:S(2)}, u32[]{:S(2)}) collective-permute-start(f32[5,24,4,128]{3,2,1,0:T(4,128)} %get-tuple-element.31), channel_id=1, source_target_pairs={{0,1},{1,2},{2,3},{4,5},{5,6},{6,7},{8,9},{9,10},{10,11},{12,13},{... | collective-permute-start | bytes 737288 | tf_op jit(solution)/shard_map/ppermute | solution.py:20
  64.7 1.9 %collective-permute-start.11 = (f32[5,24,4,128]{3,2,1,0:T(4,128)}, f32[5,24,4,128]{3,2,1,0:T(4,128)}, u32[]{:S(2)}, u32[]{:S(2)}) collective-permute-start(f32[5,24,4,128]{3,2,1,0:T(4,128)} %get-tuple-element.32), channel_id=1, source_target_pairs={{1,0},{2,1},{3,2},{5,4},{6,5},{7,6},{9,8},{10,9},{11,10},{13,12},{... | collective-permute-start | bytes 737288 | tf_op jit(solution)/shard_map/ppermute | solution.py:21
  66.6 1.2 %compare_convert_fusion = f32[2]{0:T(128)} fusion(s32[]{:T(128)S(6)} %select_n.108, s32[64]{0:T(128)S(1)} %copy-done.5, s32[]{:T(128)} %bitcast.24), kind=kLoop, calls=%fused_computation.250 | loop fusion | flops 4 | bytes 272 | tf_op jit(solution)/shard_map/convert_element_type | solution.py:297
  67.8 0.9 copy.7
  68.7 1.0 %copy.8 = f32[16,136]{1,0:T(8,128)S(1)} copy(f32[16,136]{0,1:T(8,128)} %broadcast_bitcast_fusion) | data formatting | bytes 17408 | tf_op jit(solution)/shard_map/mul | solution.py:209
  69.7 2.8 %collective-permute-done.11 = f32[5,24,4,128]{3,2,1,0:T(4,128)} collective-permute-done((f32[5,24,4,128]{3,2,1,0:T(4,128)}, f32[5,24,4,128]{3,2,1,0:T(4,128)}, u32[]{:S(2)}, u32[]{:S(2)}) %collective-permute-start.11) | collective-permute-done | bytes 245792 | tf_op jit(solution)/shard_map/ppermute | solution.py:21
  72.5 1.3 %pad_maximum_fusion = f32[5,24,16,128]{3,2,1,0:T(8,128)S(1)} fusion(f32[5,24,4,128]{3,2,1,0:T(4,128)} %collective-permute-done.11, f32[5,24,8,128]{3,2,1,0:T(8,128)S(1)} %slice_dynamic-update-slice_fusion, f32[5,24,4,128]{3,2,1,0:T(4,128)} %collective-permute-done.10), kind=kLoop, calls=%fused_computation.14 | loop fusion | flops 491520 | bytes 1966080 | tf_op jit(solution)/shard_map/concatenate | solution.py:22
  74.2 0.3 fusion.64
  74.6 1.0 %fusion.75 = f32[18,10,128]{2,1,0:T(8,128)S(1)} fusion(f32[20,12,128]{2,1,0:T(8,128)S(1)} %fusion.64, f32[5,24,16,128]{3,2,1,0:T(8,128)S(1)} %pad_maximum_fusion, f32[18,10,127]{2,1,0:T(8,128)S(1)} %get-tuple-element.48, f32[18,10,127]{2,1,0:T(8,128)S(1)} %get-tuple-element.47, f32[18,10,127]{2,1,0:T(8,128)S(1)} %bitcast.232, ...), kind=kLoop, calls=%fused_computation.152 | loop fusion | flops 599040 | bytes 2117520 | tf_op jit(solution)/shard_map/add | solution.py:278
  75.7 0.9 fusion.91
  76.6 0.3 convolution_bitcast_fusion.1
  77.1 0.3 fusion.112
  77.4 0.4 convolution_add_fusion
  77.8 1.3 %collective-permute-start.13 = (f32[2,16,256]{2,1,0:T(8,128)S(1)}, f32[2,16,256]{2,1,0:T(8,128)S(1)}, u32[]{:S(2)}, u32[]{:S(2)}) collective-permute-start(f32[2,16,256]{2,1,0:T(8,128)S(1)} %get-tuple-element.44), channel_id=1, source_target_pairs={{4,0},{8,4},{12,8},{5,1},{9,5},{13,9},{6,2},{10,6},{14,10},{7,3},{... | collective-permute-start | bytes 98312 | tf_op jit(solution)/shard_map/ppermute | solution.py:63
  79.1 4.0 %collective-permute-start.12 = (f32[3,16,256]{2,1,0:T(8,128)S(1)}, f32[3,16,256]{2,1,0:T(8,128)S(1)}, u32[]{:S(2)}, u32[]{:S(2)}) collective-permute-start(f32[3,16,256]{2,1,0:T(8,128)S(1)} %pad_maximum_fusion.12), channel_id=1, source_target_pairs={{0,4},{4,8},{8,12},{1,5},{5,9},{9,13},{2,6},{6,10},{10,14},{3,7},{... | collective-permute-start | bytes 147464 | tf_op jit(solution)/shard_map/ppermute | solution.py:63
  83.2 1.1 %collective-permute-done.12 = f32[3,16,256]{2,1,0:T(8,128)S(1)} collective-permute-done((f32[3,16,256]{2,1,0:T(8,128)S(1)}, f32[3,16,256]{2,1,0:T(8,128)S(1)}, u32[]{:S(2)}, u32[]{:S(2)}) %collective-permute-start.12) | collective-permute-done | bytes 49184 | tf_op jit(solution)/shard_map/ppermute | solution.py:63
  84.4 2.9 %collective-permute-start.14 = (f32[20,2,256]{2,1,0:T(2,128)S(1)}, f32[20,2,256]{2,1,0:T(2,128)S(1)}, u32[]{:S(2)}, u32[]{:S(2)}) collective-permute-start(f32[20,2,256]{2,1,0:T(2,128)S(1)} %get-tuple-element.41), channel_id=1, source_target_pairs={{0,1},{1,2},{2,3},{4,5},{5,6},{6,7},{8,9},{9,10},{10,11},{12,13},{... | collective-permute-start | bytes 122888 | tf_op jit(solution)/shard_map/ppermute | solution.py:20
  87.3 1.9 %collective-permute-start.15 = (f32[20,2,256]{2,1,0:T(2,128)S(1)}, f32[20,2,256]{2,1,0:T(2,128)S(1)}, u32[]{:S(2)}, u32[]{:S(2)}) collective-permute-start(f32[20,2,256]{2,1,0:T(2,128)S(1)} %get-tuple-element.42), channel_id=1, source_target_pairs={{1,0},{2,1},{3,2},{5,4},{6,5},{7,6},{9,8},{10,9},{11,10},{13,12},{... | collective-permute-start | bytes 122888 | tf_op jit(solution)/shard_map/ppermute | solution.py:21
  89.2 3.4 %collective-permute-done.15 = f32[20,2,256]{2,1,0:T(2,128)S(1)} collective-permute-done((f32[20,2,256]{2,1,0:T(2,128)S(1)}, f32[20,2,256]{2,1,0:T(2,128)S(1)}, u32[]{:S(2)}, u32[]{:S(2)}) %collective-permute-start.15) | collective-permute-done | bytes 40992 | tf_op jit(solution)/shard_map/ppermute | solution.py:21
  92.9 0.8 fusion.24
  93.9 1.2 %fusion.45 = f32[16,16,256]{2,1,0:T(8,128)} fusion(f32[18,18,256]{2,1,0:T(8,128)S(1)} %fusion.24, f32[22,22,256]{2,1,0:T(8,128)S(1)} %get-tuple-element.13, f32[16,16,255]{2,1,0:T(8,128)S(1)} %get-tuple-element.36, f32[16,16,255]{2,1,0:T(8,128)S(1)} %get-tuple-element.35, f32[22,21,256]{2,1,0:T(8,128)S(1)} %divide_select_fusion, ...), kind=kLoop, calls=%fused_computation.93 | loop fusion | flops 1114112 | bytes 4075968 | tf_op jit(solution)/shard_map/add | solution.py:139
  (105 shorter events, 4.1 us)
Async XLA Ops:
  0.0 13.3 %copy-start = (f32[16,16,256]{2,1,0:T(8,128)S(1)}, f32[16,16,256]{2,1,0:T(8,128)}, u32[]{:S(2)}) copy-start(f32[16,16,256]{2,1,0:T(8,128)} %param.5) | copy-start | bytes 786436
  0.0 13.3 %copy-start.1 = (f32[16,16,256]{2,1,0:T(8,128)S(1)}, f32[16,16,256]{2,1,0:T(8,128)}, u32[]{:S(2)}) copy-start(f32[16,16,256]{2,1,0:T(8,128)} %param.6) | copy-start | bytes 786436
  0.0 13.3 %copy-start.2 = (f32[16,16,256]{2,1,0:T(8,128)S(1)}, f32[16,16,256]{2,1,0:T(8,128)}, u32[]{:S(2)}) copy-start(f32[16,16,256]{2,1,0:T(8,128)} %param.4) | copy-start | bytes 786436
  1.6 17.9 %copy-start.5 = (s32[64]{0:T(128)S(1)}, s32[64]{0:T(128)}, u32[]{:S(2)}) copy-start(s32[64]{0:T(128)} %param.7) | copy-start | bytes 772
  1.6 27.7 %collective-permute-start = (f32[3,3,3,256]{3,2,1,0:T(4,128)}, f32[3,3,3,256]{3,2,1,0:T(4,128)}, u32[]{:S(2)}, u32[]{:S(2)}) collective-permute-start(f32[3,3,3,256]{3,2,1,0:T(4,128)} %get-tuple-element.15), channel_id=1, source_target_pairs={{0,5},{1,6},{2,7},{4,9},{5,10},{6,11},{8,13},{9,14},{10,15},{16,21... | collective-permute-start | bytes 82952 | tf_op jit(solution)/shard_map/ppermute | solution.py:42
  7.9 25.9 %collective-permute-start.7 = (f32[3,3,3,256]{3,2,1,0:T(4,128)}, f32[3,3,3,256]{3,2,1,0:T(4,128)}, u32[]{:S(2)}, u32[]{:S(2)}) collective-permute-start(f32[3,3,3,256]{3,2,1,0:T(4,128)} %get-tuple-element.16), channel_id=1, source_target_pairs={{5,0},{6,1},{7,2},{9,4},{10,5},{11,6},{13,8},{14,9},{15,10},{21,16... | collective-permute-start | bytes 82952 | tf_op jit(solution)/shard_map/ppermute | solution.py:42
  9.2 27.1 %collective-permute-start.5 = (f32[3,3,3,256]{3,2,1,0:T(4,128)}, f32[3,3,3,256]{3,2,1,0:T(4,128)}, u32[]{:S(2)}, u32[]{:S(2)}) collective-permute-start(f32[3,3,3,256]{3,2,1,0:T(4,128)} %get-tuple-element.17), channel_id=1, source_target_pairs={{4,1},{5,2},{6,3},{8,5},{9,6},{10,7},{12,9},{13,10},{14,11},{20,17... | collective-permute-start | bytes 82952 | tf_op jit(solution)/shard_map/ppermute | solution.py:42
  12.0 28.0 %collective-permute-start.6 = (f32[3,3,16,256]{3,2,1,0:T(8,128)}, f32[3,3,16,256]{3,2,1,0:T(8,128)}, u32[]{:S(2)}, u32[]{:S(2)}) collective-permute-start(f32[3,3,16,256]{3,2,1,0:T(8,128)} %pad_maximum_fusion.9), channel_id=1, source_target_pairs={{4,0},{5,1},{6,2},{7,3},{8,4},{9,5},{10,6},{11,7},{12,8},{13,9},{1... | collective-permute-start | bytes 442376 | tf_op jit(solution)/shard_map/ppermute | solution.py:42
  14.1 25.9 %collective-permute-start.1 = (f32[3,3,16,256]{3,2,1,0:T(8,128)}, f32[3,3,16,256]{3,2,1,0:T(8,128)}, u32[]{:S(2)}, u32[]{:S(2)}) collective-permute-start(f32[3,3,16,256]{3,2,1,0:T(8,128)} %slice.734), channel_id=1, source_target_pairs={{0,4},{1,5},{2,6},{3,7},{4,8},{5,9},{6,10},{7,11},{8,12},{9,13},{1... | collective-permute-start | bytes 442376 | tf_op jit(solution)/shard_map/ppermute | solution.py:42
  19.2 8.3 %copy-start.9 = (s32[16]{0:T(128)}, s32[16]{0:T(128)S(1)}, u32[]{:S(2)}) copy-start(s32[16]{0:T(128)S(1)} %and_select_fusion.1) | copy-start | bytes 196
  28.5 12.3 %copy-start.3 = (f32[5,256,136]{1,2,0:T(8,128)}, f32[5,256,136]{1,2,0:T(8,128)S(1)}, u32[]{:S(2)}) copy-start(f32[5,256,136]{1,2,0:T(8,128)S(1)} %constant_dynamic-update-slice_fusion) | copy-start | bytes 2088964
  29.4 10.6 %collective-permute-start.3 = (f32[3,16,3,256]{3,2,1,0:T(4,128)}, f32[3,16,3,256]{3,2,1,0:T(4,128)S(1)}, u32[]{:S(2)}, u32[]{:S(2)}) collective-permute-start(f32[3,16,3,256]{3,2,1,0:T(4,128)} %get-tuple-element.19), channel_id=1, source_target_pairs={{0,1},{1,2},{2,3},{4,5},{5,6},{6,7},{8,9},{9,10},{10,11},{12,13},{... | collective-permute-start | bytes 442376 | tf_op jit(solution)/shard_map/ppermute | solution.py:42
  33.8 7.0 %collective-permute-start.4 = (f32[3,16,3,256]{3,2,1,0:T(4,128)S(1)}, f32[3,16,3,256]{3,2,1,0:T(4,128)S(1)}, u32[]{:S(2)}, u32[]{:S(2)}) collective-permute-start(f32[3,16,3,256]{3,2,1,0:T(4,128)S(1)} %get-tuple-element.20), channel_id=1, source_target_pairs={{1,0},{2,1},{3,2},{5,4},{6,5},{7,6},{9,8},{10,9},{11,10},{13,12},{... | collective-permute-start | bytes 442376 | tf_op jit(solution)/shard_map/ppermute | solution.py:42
  36.2 3.7 %collective-permute-start.2 = (f32[3,3,3,256]{3,2,1,0:T(4,128)}, f32[3,3,3,256]{3,2,1,0:T(4,128)S(1)}, u32[]{:S(2)}, u32[]{:S(2)}) collective-permute-start(f32[3,3,3,256]{3,2,1,0:T(4,128)} %get-tuple-element.18), channel_id=1, source_target_pairs={{1,4},{2,5},{3,6},{5,8},{6,9},{7,10},{9,12},{10,13},{11,14},{17,20... | collective-permute-start | bytes 82952 | tf_op jit(solution)/shard_map/ppermute | solution.py:42
  42.7 0.7 copy-start.11
  44.7 0.9 copy-start.7
  45.6 1.5 %copy-start.14 = (s32[128]{0:T(128)S(1)}, s32[128]{0:T(128)}, u32[]{:S(2)}) copy-start(s32[128]{0:T(128)} %multiply_add_fusion.4) | copy-start | bytes 1540
  46.1 1.7 %copy-start.4 = (f32[5,256,136]{1,2,0:T(8,128)S(1)}, f32[5,256,136]{1,2,0:T(8,128)}, u32[]{:S(2)}) copy-start(f32[5,256,136]{1,2,0:T(8,128)} %copy-done.3) | copy-start | bytes 2088964
  47.4 8.0 %copy-start.12 = (f32[4]{0:T(128)S(1)}, f32[4]{0:T(128)}, u32[]{:S(2)}) copy-start(f32[4]{0:T(128)} %compare_convert_fusion.3) | copy-start | bytes 52
  47.8 11.8 %copy-start.13 = (f32[24]{0:T(128)S(1)}, f32[24]{0:T(128)}, u32[]{:S(2)}) copy-start(f32[24]{0:T(128)} %pad.49.clone) | copy-start | bytes 292
  48.7 6.8 %collective-permute-start.8 = (f32[5,4,8,128]{3,2,1,0:T(8,128)S(1)}, f32[5,4,8,128]{3,2,1,0:T(8,128)S(1)}, u32[]{:S(2)}, u32[]{:S(2)}) collective-permute-start(f32[5,4,8,128]{3,2,1,0:T(8,128)S(1)} %constant_dynamic-slice_fusion), channel_id=1, source_target_pairs={{0,4},{4,8},{8,12},{1,5},{5,9},{9,13},{2,6},{6,10},{10,14},{3,7},{... | collective-permute-start | bytes 245768 | tf_op jit(solution)/shard_map/ppermute | solution.py:63
  54.0 5.4 %collective-permute-start.9 = (f32[5,5,8,128]{3,2,1,0:T(8,128)S(1)}, f32[5,5,8,128]{3,2,1,0:T(8,128)S(1)}, u32[]{:S(2)}, u32[]{:S(2)}) collective-permute-start(f32[5,5,8,128]{3,2,1,0:T(8,128)S(1)} %pad_maximum_fusion.10), channel_id=1, source_target_pairs={{4,0},{8,4},{12,8},{5,1},{9,5},{13,9},{6,2},{10,6},{14,10},{7,3},{... | collective-permute-start | bytes 307208 | tf_op jit(solution)/shard_map/ppermute | solution.py:63
  60.5 9.2 %collective-permute-start.10 = (f32[5,24,4,128]{3,2,1,0:T(4,128)}, f32[5,24,4,128]{3,2,1,0:T(4,128)}, u32[]{:S(2)}, u32[]{:S(2)}) collective-permute-start(f32[5,24,4,128]{3,2,1,0:T(4,128)} %get-tuple-element.31), channel_id=1, source_target_pairs={{0,1},{1,2},{2,3},{4,5},{5,6},{6,7},{8,9},{9,10},{10,11},{12,13},{... | collective-permute-start | bytes 737288 | tf_op jit(solution)/shard_map/ppermute | solution.py:20
  64.7 7.8 %collective-permute-start.11 = (f32[5,24,4,128]{3,2,1,0:T(4,128)}, f32[5,24,4,128]{3,2,1,0:T(4,128)}, u32[]{:S(2)}, u32[]{:S(2)}) collective-permute-start(f32[5,24,4,128]{3,2,1,0:T(4,128)} %get-tuple-element.32), channel_id=1, source_target_pairs={{1,0},{2,1},{3,2},{5,4},{6,5},{7,6},{9,8},{10,9},{11,10},{13,12},{... | collective-permute-start | bytes 737288 | tf_op jit(solution)/shard_map/ppermute | solution.py:21
  75.6 1.5 %copy-start.10 = (s32[16]{0:T(128)S(1)}, s32[16]{0:T(128)}, u32[]{:S(2)}) copy-start(s32[16]{0:T(128)} %copy-done.9) | copy-start | bytes 196
  75.6 7.5 %copy-start.8 = (f32[2]{0:T(128)S(1)}, f32[2]{0:T(128)}, u32[]{:S(2)}) copy-start(f32[2]{0:T(128)} %compare_convert_fusion) | copy-start | bytes 28
  75.7 8.6 %copy-start.6 = (f32[16]{0:T(128)S(1)}, f32[16]{0:T(128)}, u32[]{:S(2)}) copy-start(f32[16]{0:T(128)} %get-tuple-element.53) | copy-start | bytes 196
  77.8 5.3 %collective-permute-start.13 = (f32[2,16,256]{2,1,0:T(8,128)S(1)}, f32[2,16,256]{2,1,0:T(8,128)S(1)}, u32[]{:S(2)}, u32[]{:S(2)}) collective-permute-start(f32[2,16,256]{2,1,0:T(8,128)S(1)} %get-tuple-element.44), channel_id=1, source_target_pairs={{4,0},{8,4},{12,8},{5,1},{9,5},{13,9},{6,2},{10,6},{14,10},{7,3},{... | collective-permute-start | bytes 98312 | tf_op jit(solution)/shard_map/ppermute | solution.py:63
  79.1 5.2 %collective-permute-start.12 = (f32[3,16,256]{2,1,0:T(8,128)S(1)}, f32[3,16,256]{2,1,0:T(8,128)S(1)}, u32[]{:S(2)}, u32[]{:S(2)}) collective-permute-start(f32[3,16,256]{2,1,0:T(8,128)S(1)} %pad_maximum_fusion.12), channel_id=1, source_target_pairs={{0,4},{4,8},{8,12},{1,5},{5,9},{9,13},{2,6},{6,10},{10,14},{3,7},{... | collective-permute-start | bytes 147464 | tf_op jit(solution)/shard_map/ppermute | solution.py:63
  84.4 4.8 %collective-permute-start.14 = (f32[20,2,256]{2,1,0:T(2,128)S(1)}, f32[20,2,256]{2,1,0:T(2,128)S(1)}, u32[]{:S(2)}, u32[]{:S(2)}) collective-permute-start(f32[20,2,256]{2,1,0:T(2,128)S(1)} %get-tuple-element.41), channel_id=1, source_target_pairs={{0,1},{1,2},{2,3},{4,5},{5,6},{6,7},{8,9},{9,10},{10,11},{12,13},{... | collective-permute-start | bytes 122888 | tf_op jit(solution)/shard_map/ppermute | solution.py:20
  87.3 5.3 %collective-permute-start.15 = (f32[20,2,256]{2,1,0:T(2,128)S(1)}, f32[20,2,256]{2,1,0:T(2,128)S(1)}, u32[]{:S(2)}, u32[]{:S(2)}) collective-permute-start(f32[20,2,256]{2,1,0:T(2,128)S(1)} %get-tuple-element.42), channel_id=1, source_target_pairs={{1,0},{2,1},{3,2},{5,4},{6,5},{7,6},{9,8},{10,9},{11,10},{13,12},{... | collective-permute-start | bytes 122888 | tf_op jit(solution)/shard_map/ppermute | solution.py:21

commit v6 on v4

--- a/solution.py
+++ b/solution.py
@@ -133,14 +133,17 @@
     half_y = width_y // 2
     half_z = depth_cells // 2
 
-    padded_ids = jnp.concatenate([aggregate[:1], aggregate, aggregate[-1:]])
-    ext_ids = lax.dynamic_slice_in_dim(padded_ids, slab_index * width_x, width_x + 2)
-    local_ids = ext_ids[1:-1]
+    plane_count = aggregate.shape[0]
+    ext_pos = slab_index * width_x - 1 + jnp.arange(width_x + 1 + NU)
+    pick_ids = ext_pos[:, None] == jnp.arange(plane_count)[None, :]
+    ext_ids = jnp.sum(jnp.where(pick_ids, aggregate.astype(jnp.float32)[None, :], 0.0), axis=1)
+    local_ids = ext_ids[1 : width_x + 1]
     straddles = (slab_index > 0) & (ext_ids[0] == local_ids[0])
-    first_id = local_ids[0] + straddles.astype(jnp.int32)
+    first_id = local_ids[0] + straddles.astype(jnp.float32)
     count_live = local_ids[-1] - first_id + 1
     slot_ids = local_ids - first_id
-    crossing = (local_ids != ext_ids[2:]).astype(jnp.float32)
+    has_next = ext_pos[2 : width_x + 2] < plane_count
+    crossing = ((local_ids != ext_ids[2 : width_x + 2]) & has_next).astype(jnp.float32)
     face_east = faces_zero[1]
     face_north = faces_zero[3]
     face_above = faces_zero[5]
@@ -184,7 +187,8 @@
     edge_sums = slot_sums[:, 0]
     slot_range = jnp.arange(width_x)
     last_slot = (slot_range == count_live - 1).astype(jnp.float32)
-    tail_planes = lax.dynamic_slice_in_dim(coarse, count_live - NCS, NCS, axis=1)
+    tail_pick = (slot_range[None, :] == count_live - NCS + jnp.arange(NCS)[:, None]).astype(jnp.float32)
+    tail_planes = jnp.einsum("ks,qsjl->qkjl", tail_pick, coarse, precision=lax.Precision.HIGHEST)
     head_planes = jnp.concatenate([coarse[:, :NCS], edge_sums[:, None]], axis=1)
     tail_planes, head_planes = lax.optimization_barrier((tail_planes, head_planes))
     from_prev = passed_along(tail_planes, "slab", 1)
@@ -193,7 +197,9 @@
     prev_last = (jnp.arange(NCS) == NCS - 1).astype(jnp.float32)
     from_prev = from_prev + edge_sums[:, None] * prev_last[None, :, None, None]
     x_ext = jnp.concatenate([from_prev, coarse, jnp.zeros_like(tail_planes)], axis=1)
-    x_ext = lax.dynamic_update_slice_in_dim(x_ext, from_next[:, :NCS], NCS + count_live, axis=1)
+    wide_range = jnp.arange(width_x + 2 * NCS)[:, None]
+    place = (wide_range == NCS + count_live + jnp.arange(NCS)[None, :]).astype(jnp.float32)
+    x_ext = x_ext + jnp.einsum("tk,qkjl->qtjl", place, from_next[:, :NCS], precision=lax.Precision.HIGHEST)
     coarse_rim = NCS
     coef_ext = padded(x_ext, ((("pencil", "sub"), 2),), coarse_rim)
     coarse_corr = jnp.zeros((width_x + 2 * NCS, half_y + 2 * NCS, half_z), jnp.float32)
@@ -244,7 +250,7 @@
             coarse_center
             + OMEGA * (coarse_rhs - (diag_coarse * coarse_center - beside_all)) / safe_coarse
         )
-    last_corr = lax.dynamic_index_in_dim(coarse_corr, count_live - 1, axis=0, keepdims=False)
+    last_corr = jnp.sum(last_slot[:, None, None] * coarse_corr, axis=0)
     corr_wide = jnp.concatenate([jnp.zeros_like(last_corr)[None], coarse_corr], axis=0)
     corr_z = jnp.dot(
         corr_wide.reshape((width_x + 1) * half_y, half_z), pair_z.T, precision=lax.Precision.HIGHEST
@@ -258,9 +264,9 @@
     above_next = passed_along(base[:NU], "slab", -1)
     from_owner = (slot_ids == -1).astype(jnp.float32)
     own = base + from_owner[:, None, None] * below_prev[NU][None]
-    tail_ids = jnp.concatenate([aggregate, jnp.full((NU,), -1, aggregate.dtype)])
-    next_ids = lax.dynamic_slice_in_dim(tail_ids, (slab_index + 1) * width_x, NU)
-    to_owner = (next_ids == local_ids[-1]).astype(jnp.float32)
+    next_ids = ext_ids[width_x + 1 :]
+    next_in = ext_pos[width_x + 1 :] < plane_count
+    to_owner = ((next_ids == local_ids[-1]) & next_in).astype(jnp.float32)
     high_halo = above_next + to_owner[:, None, None] * last_fine[None]
     post_x = jnp.concatenate([below_prev[:NU], own, high_halo], axis=0)
     post_ext = padded(post_x, ((("pencil", "sub"), 1),), NU)

time: 80.6 us -> 80 us (level)
  local copies, waits for them, and re-layouts: 8.96 us -> 7.72 us
    concatenate x2 -> x0, other arithmetic: 2.05 us -> none  [the longest x1 1.95 us: body(): padded_ids = jnp.concatenate([aggregate[:1], aggregate, aggregate[-1:]])]
    slice x1, local copies, waits for them, and re-layouts: 1.31 us -> 0.02 us  [body(): from_next[:, NCS][:, None] * last_slot[None, :, None, None]]
    convert_element_type x1 -> x5, other arithmetic: 1.27 us -> 2.43 us  [the longest x1 1.19 us: body(): to_owner = ((next_ids == local_ids[-1]) & next_in).astype(jnp.float32)]
    reduce_sum x0 -> x2, other arithmetic: none -> 1.03 us  [the longest x1 0.85 us: body(): last_corr = jnp.sum(last_slot[:, None, None] * coarse_corr, axis=0)]
    add x3 -> x2, other arithmetic: 2.22 us -> 1.29 us  [body(): coarse_center + OMEGA * (coarse_rhs - (diag_coarse * coarse_center - besi...]
  transfers between devices with their start and end apart: 12 -> 12, of which waited for: 7 -> 7; matrix products, arithmetic and copies ran while one was open for 14% -> 12% of each run, Pallas kernels for 0% -> 0%
where the time goes in v6:
time: 80 us; the launch traced here: 79.3 us
  starting transfers between devices  31.9 us (40%)
  waiting for transfers between devices  17.2 us (22%)
  other arithmetic  15.1 us (19%)
  local copies, waits for them, and re-layouts  7.72 us (10%)
  matrix products  4.32 us (5%)
  between operations  3.09 us (4%)
    ppermute x4, starting transfers between devices, padded(): before = lax.ppermute(last, axis, up)  14 us
    ppermute x4, starting transfers between devices, passed_along(): return lax.ppermute(array, axis, pairs)  10.8 us
    ppermute x4, waiting for transfers between devices, padded(): after = lax.ppermute(leading, axis, down)  10.6 us
    ppermute x4, starting transfers between devices, padded(): after = lax.ppermute(leading, axis, down)  7.05 us
    ppermute x4, waiting for transfers between devices, passed_along(): return lax.ppermute(array, axis, pairs)  5.74 us
    mul x6, local copies, waits for them, and re-layouts, xy_map(): joint = owner_wide[:, None, :, None] * pick_y[None, :, None, :]  4.08 us
    add x4, other arithmetic, sweeps(): field_ext = center + OMEGA * (source_now - product) / faces_now[7]  3.76 us
    slice x3, other arithmetic, padded(): last = lax.slice_in_dim(array, length - width, length, axis=dim)  1.73 us
  transfers between devices with their start and end apart: 12, of which 7 were waited for; matrix products, arithmetic and copies ran while one was open for 12% of the time, Pallas kernels for 0%

profile of v6, /device:TPU:1, one launch (start us, length us, event | category | flops | bytes accessed | tf_op | source)
XLA Modules:
  0.0 79.3 jit_solution(5796490359080472387)
XLA Ops:
  0.0 1.6 %pad_maximum_fusion.17 = (f32[3,3,16,256]{3,2,1,0:T(8,128)}, f32[3,3,16,256]{3,2,1,0:T(8,128)S(1)}) fusion(f32[1,16,16,256]{3,2,1,0:T(8,128)} %bitcast.238, f32[1,16,16,256]{3,2,1,0:T(8,128)} %bitcast.235, f32[1,16,16,256]{3,2,1,0:T(8,128)} %bitcast.241), kind=kLoop, calls=%fused_computation.161 | loop fusion | flops 147456 | bytes 1081344 | tf_op jit(solution)/shard_map/slice | solution.py:18
  1.6 4.0 %collective-permute-start = (f32[3,3,16,256]{3,2,1,0:T(8,128)}, f32[3,3,16,256]{3,2,1,0:T(8,128)S(1)}, u32[]{:S(2)}, u32[]{:S(2)}) collective-permute-start(f32[3,3,16,256]{3,2,1,0:T(8,128)} %get-tuple-element.19), channel_id=1, source_target_pairs={{0,4},{4,8},{8,12},{1,5},{5,9},{9,13},{2,6},{6,10},{10,14},{3,7},{... | collective-permute-start | bytes 442376 | tf_op jit(solution)/shard_map/ppermute | solution.py:20
  5.6 1.3 %collective-permute-start.1 = (f32[3,3,16,256]{3,2,1,0:T(8,128)S(1)}, f32[3,3,16,256]{3,2,1,0:T(8,128)S(1)}, u32[]{:S(2)}, u32[]{:S(2)}) collective-permute-start(f32[3,3,16,256]{3,2,1,0:T(8,128)S(1)} %get-tuple-element.20), channel_id=1, source_target_pairs={{4,0},{8,4},{12,8},{5,1},{9,5},{13,9},{6,2},{10,6},{14,10},{7,3},{... | collective-permute-start | bytes 442376 | tf_op jit(solution)/shard_map/ppermute | solution.py:21
  7.3 0.6 iota_convert_fusion
  8.0 0.7 convert_element_type.143
  8.7 0.2 select_reduce_fusion
  8.8 0.7 fusion.141
  12.2 0.6 broadcast_bitcast_fusion.1
  12.9 0.6 broadcast_bitcast_fusion
  13.5 0.2 broadcast_multiply_fusion
  13.7 0.5 mul.480
  14.2 0.5 mul.476
  15.4 4.0 %collective-permute-start.2 = (f32[3,22,3,256]{3,2,1,0:T(4,128)S(1)}, f32[3,22,3,256]{3,2,1,0:T(4,128)S(1)}, u32[]{:S(2)}, u32[]{:S(2)}) collective-permute-start(f32[3,22,3,256]{3,2,1,0:T(4,128)S(1)} %get-tuple-element.17), channel_id=1, source_target_pairs={{0,1},{1,2},{2,3},{4,5},{5,6},{6,7},{8,9},{9,10},{10,11},{12,13},{... | collective-permute-start | bytes 608264 | tf_op jit(solution)/shard_map/ppermute | solution.py:20
  19.4 1.9 %collective-permute-start.3 = (f32[3,22,3,256]{3,2,1,0:T(4,128)S(1)}, f32[3,22,3,256]{3,2,1,0:T(4,128)S(1)}, u32[]{:S(2)}, u32[]{:S(2)}) collective-permute-start(f32[3,22,3,256]{3,2,1,0:T(4,128)S(1)} %get-tuple-element.18), channel_id=1, source_target_pairs={{1,0},{2,1},{3,2},{5,4},{6,5},{7,6},{9,8},{10,9},{11,10},{13,12},{... | collective-permute-start | bytes 608264 | tf_op jit(solution)/shard_map/ppermute | solution.py:21
  21.3 0.6 compare_convert_fusion.1
  21.9 0.8 %collective-permute-done.2 = f32[3,22,3,256]{3,2,1,0:T(4,128)S(1)} collective-permute-done((f32[3,22,3,256]{3,2,1,0:T(4,128)S(1)}, f32[3,22,3,256]{3,2,1,0:T(4,128)S(1)}, u32[]{:S(2)}, u32[]{:S(2)}) %collective-permute-start.2) | collective-permute-done | bytes 202784 | tf_op jit(solution)/shard_map/ppermute | solution.py:20
  22.8 4.4 %collective-permute-done.3 = f32[3,22,3,256]{3,2,1,0:T(4,128)S(1)} collective-permute-done((f32[3,22,3,256]{3,2,1,0:T(4,128)S(1)}, f32[3,22,3,256]{3,2,1,0:T(4,128)S(1)}, u32[]{:S(2)}, u32[]{:S(2)}) %collective-permute-start.3) | collective-permute-done | bytes 202784 | tf_op jit(solution)/shard_map/ppermute | solution.py:21
  27.2 0.3 pad_maximum_fusion
  27.6 0.2 divide_select_fusion.1
  27.7 0.2 fusion.130
  27.9 0.2 divide_select_fusion
  28.1 0.2 fusion.131
  28.3 0.2 divide_select_fusion.2
  28.6 1.0 %fusion.12 = (f32[20,20,256]{2,1,0:T(8,128)S(1)}, f32[20,20,256]{2,1,0:T(8,128)S(1)}, f32[20,20,256]{2,1,0:T(8,128)S(1)}) fusion(f32[22,22,256]{2,1,0:T(8,128)S(1)} %get-tuple-element.16, f32[22,22,256]{2,1,0:T(8,128)S(1)} %get-tuple-element.15, f32[20,20,255]{2,1,0:T(8,128)S(1)} %get-tuple-element.26, f32[20,20,255]{2,1,0:T(8,128)S(1)} %get-tuple-element.25, ...), kind=kLoop, calls=%fused_computation.35 | loop fusion | flops 2764800 | bytes 6961424 | tf_op jit(solution)/shard_map/add | solution.py:105
  29.6 0.2 fusion.134
  29.8 0.8 fusion.35
  30.7 0.5 fusion.129
  31.2 0.3 fusion.4
  31.6 0.3 fusion.3
  31.9 0.3 fusion.2
  32.2 0.3 fusion.1
  32.5 0.3 fusion
  32.9 0.8 convolution_bitcast_fusion.1
  33.8 0.3 convolution_bitcast_fusion.8
  34.1 4.3 %collective-permute-start.4 = (f32[5,4,8,128]{3,1,2,0:T(4,128)S(1)}, f32[5,4,8,128]{3,1,2,0:T(4,128)S(1)}, u32[]{:S(2)}, u32[]{:S(2)}) collective-permute-start(f32[5,4,8,128]{3,1,2,0:T(4,128)S(1)} %convolution_bitcast_fusion.8), channel_id=1, source_target_pairs={{0,4},{4,8},{8,12},{1,5},{5,9},{9,13},{2,6},{6,10},{10,14},{3,7},{... | collective-permute-start | bytes 245768 | tf_op jit(solution)/shard_map/ppermute | solution.py:29
  38.4 1.3 %collective-permute-start.5 = (f32[5,5,8,128]{3,1,2,0:T(8,128)S(1)}, f32[5,5,8,128]{3,1,2,0:T(8,128)S(1)}, u32[]{:S(2)}, u32[]{:S(2)}) collective-permute-start(f32[5,5,8,128]{3,1,2,0:T(8,128)S(1)} %pad_maximum_fusion.14), channel_id=1, source_target_pairs={{4,0},{8,4},{12,8},{5,1},{9,5},{13,9},{6,2},{10,6},{14,10},{7,3},{... | collective-permute-start | bytes 307208 | tf_op jit(solution)/shard_map/ppermute | solution.py:29
  39.7 0.1 collective-permute-done.4
  39.9 4.5 %collective-permute-done.5 = f32[5,5,8,128]{3,1,2,0:T(8,128)S(1)} collective-permute-done((f32[5,5,8,128]{3,1,2,0:T(8,128)S(1)}, f32[5,5,8,128]{3,1,2,0:T(8,128)S(1)}, u32[]{:S(2)}, u32[]{:S(2)}) %collective-permute-start.5) | collective-permute-done | bytes 102432 | tf_op jit(solution)/shard_map/ppermute | solution.py:29
  44.6 0.5 maximum_add_fusion
  45.2 0.8 %fusion.133 = (f32[5,24,4,128]{3,1,2,0:T(8,128)}, f32[5,24,4,128]{3,1,2,0:T(8,128)}) fusion(f32[5,24,8,128]{3,1,2,0:T(8,128)S(1)} %maximum_add_fusion), kind=kLoop, calls=%fused_computation.301 | loop fusion | bytes 983040 | tf_op jit(solution)/shard_map/slice | solution.py:18
  46.0 3.2 %collective-permute-start.6 = (f32[5,24,4,128]{3,1,2,0:T(8,128)}, f32[5,24,4,128]{3,1,2,0:T(8,128)}, u32[]{:S(2)}, u32[]{:S(2)}) collective-permute-start(f32[5,24,4,128]{3,1,2,0:T(8,128)} %get-tuple-element.31), channel_id=1, source_target_pairs={{0,1},{1,2},{2,3},{4,5},{5,6},{6,7},{8,9},{9,10},{10,11},{12,13},{... | collective-permute-start | bytes 737288 | tf_op jit(solution)/shard_map/ppermute | solution.py:20
  49.1 1.9 %collective-permute-start.7 = (f32[5,24,4,128]{3,1,2,0:T(8,128)}, f32[5,24,4,128]{3,1,2,0:T(8,128)}, u32[]{:S(2)}, u32[]{:S(2)}) collective-permute-start(f32[5,24,4,128]{3,1,2,0:T(8,128)} %get-tuple-element.32), channel_id=1, source_target_pairs={{1,0},{2,1},{3,2},{5,4},{6,5},{7,6},{9,8},{10,9},{11,10},{13,12},{... | collective-permute-start | bytes 737288 | tf_op jit(solution)/shard_map/ppermute | solution.py:21
  51.1 1.2 %and_convert_fusion = f32[2]{0:T(128)} fusion(s32[19]{0:T(128)S(1)} %iota_add_fusion, f32[19]{0:T(128)S(1)} %select_reduce_fusion, f32[]{:T(128)} %bitcast.24), kind=kLoop, calls=%fused_computation.255 | loop fusion | flops 8 | bytes 28 | tf_op jit(solution)/shard_map/convert_element_type | solution.py:269
  52.2 0.9 %copy.16 = f32[16,136]{1,0:T(8,128)S(1)} copy(f32[16,136]{0,1:T(8,128)} %broadcast_bitcast_fusion.1) | data formatting | bytes 17408 | tf_op jit(solution)/shard_map/mul | solution.py:178
  53.2 1.0 %copy.17 = f32[16,136]{1,0:T(8,128)S(1)} copy(f32[16,136]{0,1:T(8,128)} %broadcast_bitcast_fusion) | data formatting | bytes 17408 | tf_op jit(solution)/shard_map/mul | solution.py:178
  54.2 2.8 %collective-permute-done.7 = f32[5,24,4,128]{3,1,2,0:T(8,128)} collective-permute-done((f32[5,24,4,128]{3,1,2,0:T(8,128)}, f32[5,24,4,128]{3,1,2,0:T(8,128)}, u32[]{:S(2)}, u32[]{:S(2)}) %collective-permute-start.7) | collective-permute-done | bytes 245792 | tf_op jit(solution)/shard_map/ppermute | solution.py:21
  57.0 1.1 %pad_maximum_fusion.1 = f32[5,24,16,128]{3,1,2,0:T(8,128)S(1)} fusion(f32[5,24,4,128]{3,1,2,0:T(8,128)} %collective-permute-done.7, f32[5,24,8,128]{3,1,2,0:T(8,128)S(1)} %maximum_add_fusion, f32[5,24,4,128]{3,1,2,0:T(8,128)} %collective-permute-done.6), kind=kLoop, calls=%fused_computation.16 | loop fusion | flops 491520 | bytes 1966080 | tf_op jit(solution)/shard_map/concatenate | solution.py:22
  58.2 0.2 fusion.57
  58.5 0.3 fusion.65
  58.9 1.0 %fusion.79 = f32[18,10,128]{2,0,1:T(8,128)S(1)} fusion(f32[20,12,128]{2,0,1:T(8,128)S(1)} %fusion.65, f32[5,24,16,128]{3,1,2,0:T(8,128)S(1)} %pad_maximum_fusion.1, f32[18,10,127]{2,0,1:T(8,128)S(1)} %get-tuple-element.48, f32[18,10,127]{2,0,1:T(8,128)S(1)} %get-tuple-element.47, f32[18,10,127]{2,0,1:T(8,128)S(1)} %bitcast.251, ...), kind=kLoop, calls=%fused_computation.168 | loop fusion | flops 599040 | bytes 2117520 | tf_op jit(solution)/shard_map/add | solution.py:250
  60.0 0.9 %multiply_reduce_fusion = (f32[8,128]{1,0:T(8,128)S(1)}, f32[16,8,128]{2,0,1:T(8,128)S(1)}) fusion(f32[16]{0:T(128)S(1)} %compare_convert_fusion.2, f32[16,8,127]{2,0,1:T(8,128)S(1)} %get-tuple-element.50, f32[16,8,127]{2,0,1:T(8,128)S(1)} %get-tuple-element.49, f32[18,10,128]{2,0,1:T(8,128)S(1)} %fusion.79, f32[5,24,8,128]{3,1,2,0:T(8,128)S(1)} %maximum_add_fusion, ...), kind=kLoop, calls=%fused_computation.215 | loop fusion | flops 457728 | bytes 1724928 | tf_op jit(solution)/shard_map/reduce_sum | solution.py:253
  60.9 0.2 fusion.75
  61.0 0.3 fusion.111
  61.3 0.3 convolution_bitcast_fusion.2
  61.6 0.4 convolution_add_fusion
  62.0 1.3 %collective-permute-start.9 = (f32[2,16,256]{2,1,0:T(8,128)S(1)}, f32[2,16,256]{2,1,0:T(8,128)S(1)}, u32[]{:S(2)}, u32[]{:S(2)}) collective-permute-start(f32[2,16,256]{2,1,0:T(8,128)S(1)} %get-tuple-element.44), channel_id=1, source_target_pairs={{4,0},{8,4},{12,8},{5,1},{9,5},{13,9},{6,2},{10,6},{14,10},{7,3},{... | collective-permute-start | bytes 98312 | tf_op jit(solution)/shard_map/ppermute | solution.py:29
  63.3 4.0 %collective-permute-start.8 = (f32[3,16,256]{2,1,0:T(8,128)S(1)}, f32[3,16,256]{2,1,0:T(8,128)S(1)}, u32[]{:S(2)}, u32[]{:S(2)}) collective-permute-start(f32[3,16,256]{2,1,0:T(8,128)S(1)} %pad_maximum_fusion.19), channel_id=1, source_target_pairs={{0,4},{4,8},{8,12},{1,5},{5,9},{9,13},{2,6},{6,10},{10,14},{3,7},{... | collective-permute-start | bytes 147464 | tf_op jit(solution)/shard_map/ppermute | solution.py:29
  67.4 1.1 %collective-permute-done.8 = f32[3,16,256]{2,1,0:T(8,128)S(1)} collective-permute-done((f32[3,16,256]{2,1,0:T(8,128)S(1)}, f32[3,16,256]{2,1,0:T(8,128)S(1)}, u32[]{:S(2)}, u32[]{:S(2)}) %collective-permute-start.8) | collective-permute-done | bytes 49184 | tf_op jit(solution)/shard_map/ppermute | solution.py:29
  68.7 2.9 %collective-permute-start.10 = (f32[20,2,256]{2,1,0:T(2,128)S(1)}, f32[20,2,256]{2,1,0:T(2,128)S(1)}, u32[]{:S(2)}, u32[]{:S(2)}) collective-permute-start(f32[20,2,256]{2,1,0:T(2,128)S(1)} %get-tuple-element.41), channel_id=1, source_target_pairs={{0,1},{1,2},{2,3},{4,5},{5,6},{6,7},{8,9},{9,10},{10,11},{12,13},{... | collective-permute-start | bytes 122888 | tf_op jit(solution)/shard_map/ppermute | solution.py:20
  71.5 1.9 %collective-permute-start.11 = (f32[20,2,256]{2,1,0:T(2,128)S(1)}, f32[20,2,256]{2,1,0:T(2,128)S(1)}, u32[]{:S(2)}, u32[]{:S(2)}) collective-permute-start(f32[20,2,256]{2,1,0:T(2,128)S(1)} %get-tuple-element.42), channel_id=1, source_target_pairs={{1,0},{2,1},{3,2},{5,4},{6,5},{7,6},{9,8},{10,9},{11,10},{13,12},{... | collective-permute-start | bytes 122888 | tf_op jit(solution)/shard_map/ppermute | solution.py:21
  73.5 3.4 %collective-permute-done.11 = f32[20,2,256]{2,1,0:T(2,128)S(1)} collective-permute-done((f32[20,2,256]{2,1,0:T(2,128)S(1)}, f32[20,2,256]{2,1,0:T(2,128)S(1)}, u32[]{:S(2)}, u32[]{:S(2)}) %collective-permute-start.11) | collective-permute-done | bytes 40992 | tf_op jit(solution)/shard_map/ppermute | solution.py:21
  76.9 0.2 fusion.132
  77.1 0.8 %fusion.24 = f32[18,18,256]{2,1,0:T(8,128)S(1)} fusion(f32[20,2,256]{2,1,0:T(2,128)S(1)} %collective-permute-done.11, f32[2,16,256]{2,1,0:T(8,128)S(1)} %multiply_add_fusion.3, f32[16,16,256]{2,1,0:T(8,128)S(1)} %multiply_add_fusion.1, f32[2,16,256]{2,1,0:T(8,128)S(1)} %slice.826, f32[20,2,256]{2,1,0:T(2,128)S(1)} %collective-permute-done.10, ...), kind=kLoop, calls=%fused_computation.56 | loop fusion | flops 1907712 | bytes 4796320 | tf_op jit(solution)/shard_map/add | solution.py:105
  78.1 1.2 %fusion.46 = f32[16,16,256]{2,1,0:T(8,128)} fusion(f32[18,18,256]{2,1,0:T(8,128)S(1)} %fusion.24, f32[22,22,256]{2,1,0:T(8,128)S(1)} %get-tuple-element.15, f32[16,16,255]{2,1,0:T(8,128)S(1)} %get-tuple-element.36, f32[16,16,255]{2,1,0:T(8,128)S(1)} %get-tuple-element.35, f32[22,21,256]{2,1,0:T(8,128)S(1)} %divide_select_fusion, ...), kind=kLoop, calls=%fused_computation.100 | loop fusion | flops 1114112 | bytes 4075968 | tf_op jit(solution)/shard_map/add | solution.py:105
  (90 shorter events, 2.9 us)
Async XLA Ops:
  1.6 13.6 %collective-permute-start = (f32[3,3,16,256]{3,2,1,0:T(8,128)}, f32[3,3,16,256]{3,2,1,0:T(8,128)S(1)}, u32[]{:S(2)}, u32[]{:S(2)}) collective-permute-start(f32[3,3,16,256]{3,2,1,0:T(8,128)} %get-tuple-element.19), channel_id=1, source_target_pairs={{0,4},{4,8},{8,12},{1,5},{5,9},{9,13},{2,6},{6,10},{10,14},{3,7},{... | collective-permute-start | bytes 442376 | tf_op jit(solution)/shard_map/ppermute | solution.py:20
  5.6 9.6 %collective-permute-start.1 = (f32[3,3,16,256]{3,2,1,0:T(8,128)S(1)}, f32[3,3,16,256]{3,2,1,0:T(8,128)S(1)}, u32[]{:S(2)}, u32[]{:S(2)}) collective-permute-start(f32[3,3,16,256]{3,2,1,0:T(8,128)S(1)} %get-tuple-element.20), channel_id=1, source_target_pairs={{4,0},{8,4},{12,8},{5,1},{9,5},{13,9},{6,2},{10,6},{14,10},{7,3},{... | collective-permute-start | bytes 442376 | tf_op jit(solution)/shard_map/ppermute | solution.py:21
  6.9 7.2 %copy-start.7 = (s32[16]{0:T(128)}, s32[16]{0:T(128)S(1)}, u32[]{:S(2)}) copy-start(s32[16]{0:T(128)S(1)} %and_select_fusion.1) | copy-start | bytes 196
  14.2 1.0 %copy-start = (f32[16,16,256]{2,1,0:T(8,128)S(1)}, f32[16,16,256]{2,1,0:T(8,128)}, u32[]{:S(2)}) copy-start(f32[16,16,256]{2,1,0:T(8,128)} %param.5) | copy-start | bytes 786436
  14.2 1.0 %copy-start.1 = (f32[16,16,256]{2,1,0:T(8,128)S(1)}, f32[16,16,256]{2,1,0:T(8,128)}, u32[]{:S(2)}) copy-start(f32[16,16,256]{2,1,0:T(8,128)} %param.6) | copy-start | bytes 786436
  14.2 1.1 %copy-start.2 = (f32[16,16,256]{2,1,0:T(8,128)S(1)}, f32[16,16,256]{2,1,0:T(8,128)}, u32[]{:S(2)}) copy-start(f32[16,16,256]{2,1,0:T(8,128)} %param.4) | copy-start | bytes 786436
  15.2 12.3 %copy-start.3 = (f32[5,256,136]{1,2,0:T(8,128)}, f32[5,256,136]{1,2,0:T(8,128)S(1)}, u32[]{:S(2)}) copy-start(f32[5,256,136]{1,2,0:T(8,128)S(1)} %constant_dynamic-update-slice_fusion) | copy-start | bytes 2088964
  15.4 7.4 %collective-permute-start.2 = (f32[3,22,3,256]{3,2,1,0:T(4,128)S(1)}, f32[3,22,3,256]{3,2,1,0:T(4,128)S(1)}, u32[]{:S(2)}, u32[]{:S(2)}) collective-permute-start(f32[3,22,3,256]{3,2,1,0:T(4,128)S(1)} %get-tuple-element.17), channel_id=1, source_target_pairs={{0,1},{1,2},{2,3},{4,5},{5,6},{6,7},{8,9},{9,10},{10,11},{12,13},{... | collective-permute-start | bytes 608264 | tf_op jit(solution)/shard_map/ppermute | solution.py:20
  19.4 7.8 %collective-permute-start.3 = (f32[3,22,3,256]{3,2,1,0:T(4,128)S(1)}, f32[3,22,3,256]{3,2,1,0:T(4,128)S(1)}, u32[]{:S(2)}, u32[]{:S(2)}) collective-permute-start(f32[3,22,3,256]{3,2,1,0:T(4,128)S(1)} %get-tuple-element.18), channel_id=1, source_target_pairs={{1,0},{2,1},{3,2},{5,4},{6,5},{7,6},{9,8},{10,9},{11,10},{13,12},{... | collective-permute-start | bytes 608264 | tf_op jit(solution)/shard_map/ppermute | solution.py:21
  31.2 1.7 %copy-start.4 = (f32[5,256,136]{1,2,0:T(8,128)S(1)}, f32[5,256,136]{1,2,0:T(8,128)}, u32[]{:S(2)}) copy-start(f32[5,256,136]{1,2,0:T(8,128)} %copy-done.3) | copy-start | bytes 2088964
  33.7 10.9 %copy-start.9 = (f32[24]{0:T(128)S(1)}, f32[24]{0:T(128)}, u32[]{:S(2)}) copy-start(f32[24]{0:T(128)} %iota_convert_fusion) | copy-start | bytes 292
  34.1 5.7 %collective-permute-start.4 = (f32[5,4,8,128]{3,1,2,0:T(4,128)S(1)}, f32[5,4,8,128]{3,1,2,0:T(4,128)S(1)}, u32[]{:S(2)}, u32[]{:S(2)}) collective-permute-start(f32[5,4,8,128]{3,1,2,0:T(4,128)S(1)} %convolution_bitcast_fusion.8), channel_id=1, source_target_pairs={{0,4},{4,8},{8,12},{1,5},{5,9},{9,13},{2,6},{6,10},{10,14},{3,7},{... | collective-permute-start | bytes 245768 | tf_op jit(solution)/shard_map/ppermute | solution.py:29
  38.4 6.1 %collective-permute-start.5 = (f32[5,5,8,128]{3,1,2,0:T(8,128)S(1)}, f32[5,5,8,128]{3,1,2,0:T(8,128)S(1)}, u32[]{:S(2)}, u32[]{:S(2)}) collective-permute-start(f32[5,5,8,128]{3,1,2,0:T(8,128)S(1)} %pad_maximum_fusion.14), channel_id=1, source_target_pairs={{4,0},{8,4},{12,8},{5,1},{9,5},{13,9},{6,2},{10,6},{14,10},{7,3},{... | collective-permute-start | bytes 307208 | tf_op jit(solution)/shard_map/ppermute | solution.py:29
  46.0 8.2 %collective-permute-start.6 = (f32[5,24,4,128]{3,1,2,0:T(8,128)}, f32[5,24,4,128]{3,1,2,0:T(8,128)}, u32[]{:S(2)}, u32[]{:S(2)}) collective-permute-start(f32[5,24,4,128]{3,1,2,0:T(8,128)} %get-tuple-element.31), channel_id=1, source_target_pairs={{0,1},{1,2},{2,3},{4,5},{5,6},{6,7},{8,9},{9,10},{10,11},{12,13},{... | collective-permute-start | bytes 737288 | tf_op jit(solution)/shard_map/ppermute | solution.py:20
  49.1 7.8 %collective-permute-start.7 = (f32[5,24,4,128]{3,1,2,0:T(8,128)}, f32[5,24,4,128]{3,1,2,0:T(8,128)}, u32[]{:S(2)}, u32[]{:S(2)}) collective-permute-start(f32[5,24,4,128]{3,1,2,0:T(8,128)} %get-tuple-element.32), channel_id=1, source_target_pairs={{1,0},{2,1},{3,2},{5,4},{6,5},{7,6},{9,8},{10,9},{11,10},{13,12},{... | collective-permute-start | bytes 737288 | tf_op jit(solution)/shard_map/ppermute | solution.py:21
  59.9 1.2 %copy-start.8 = (s32[16]{0:T(128)S(1)}, s32[16]{0:T(128)}, u32[]{:S(2)}) copy-start(s32[16]{0:T(128)} %copy-done.7) | copy-start | bytes 196
  59.9 7.5 %copy-start.6 = (f32[2]{0:T(128)S(1)}, f32[2]{0:T(128)}, u32[]{:S(2)}) copy-start(f32[2]{0:T(128)} %and_convert_fusion) | copy-start | bytes 28
  60.0 8.5 %copy-start.5 = (f32[16]{0:T(128)S(1)}, f32[16]{0:T(128)}, u32[]{:S(2)}) copy-start(f32[16]{0:T(128)} %get-tuple-element.53) | copy-start | bytes 196
  62.0 5.3 %collective-permute-start.9 = (f32[2,16,256]{2,1,0:T(8,128)S(1)}, f32[2,16,256]{2,1,0:T(8,128)S(1)}, u32[]{:S(2)}, u32[]{:S(2)}) collective-permute-start(f32[2,16,256]{2,1,0:T(8,128)S(1)} %get-tuple-element.44), channel_id=1, source_target_pairs={{4,0},{8,4},{12,8},{5,1},{9,5},{13,9},{6,2},{10,6},{14,10},{7,3},{... | collective-permute-start | bytes 98312 | tf_op jit(solution)/shard_map/ppermute | solution.py:29
  63.3 5.2 %collective-permute-start.8 = (f32[3,16,256]{2,1,0:T(8,128)S(1)}, f32[3,16,256]{2,1,0:T(8,128)S(1)}, u32[]{:S(2)}, u32[]{:S(2)}) collective-permute-start(f32[3,16,256]{2,1,0:T(8,128)S(1)} %pad_maximum_fusion.19), channel_id=1, source_target_pairs={{0,4},{4,8},{8,12},{1,5},{5,9},{9,13},{2,6},{6,10},{10,14},{3,7},{... | collective-permute-start | bytes 147464 | tf_op jit(solution)/shard_map/ppermute | solution.py:29
  68.7 4.8 %collective-permute-start.10 = (f32[20,2,256]{2,1,0:T(2,128)S(1)}, f32[20,2,256]{2,1,0:T(2,128)S(1)}, u32[]{:S(2)}, u32[]{:S(2)}) collective-permute-start(f32[20,2,256]{2,1,0:T(2,128)S(1)} %get-tuple-element.41), channel_id=1, source_target_pairs={{0,1},{1,2},{2,3},{4,5},{5,6},{6,7},{8,9},{9,10},{10,11},{12,13},{... | collective-permute-start | bytes 122888 | tf_op jit(solution)/shard_map/ppermute | solution.py:20
  71.5 5.3 %collective-permute-start.11 = (f32[20,2,256]{2,1,0:T(2,128)S(1)}, f32[20,2,256]{2,1,0:T(2,128)S(1)}, u32[]{:S(2)}, u32[]{:S(2)}) collective-permute-start(f32[20,2,256]{2,1,0:T(2,128)S(1)} %get-tuple-element.42), channel_id=1, source_target_pairs={{1,0},{2,1},{3,2},{5,4},{6,5},{7,6},{9,8},{10,9},{11,10},{13,12},{... | collective-permute-start | bytes 122888 | tf_op jit(solution)/shard_map/ppermute | solution.py:21

commit v7 on v6

--- a/solution.py
+++ b/solution.py
@@ -1,3 +1,4 @@
+import numpy as np
 import jax
 import jax.numpy as jnp
 from jax import lax
@@ -148,10 +149,10 @@
     face_north = faces_zero[3]
     face_above = faces_zero[5]
     boundary = faces_zero[6]
-    index_z = jnp.arange(depth_cells)[:, None]
-    coarse_z = jnp.arange(half_z)[None, :]
-    pair_z = (index_z // 2 == coarse_z).astype(jnp.float32)
-    odd_z = (index_z == 2 * coarse_z + 1).astype(jnp.float32)
+    index_z = np.arange(depth_cells)[:, None]
+    coarse_z = np.arange(half_z)[None, :]
+    pair_z = jnp.asarray((index_z // 2 == coarse_z).astype(np.float32))
+    odd_z = jnp.asarray((index_z == 2 * coarse_z + 1).astype(np.float32))
     cells = width_x * width_y
 
     def z_sum(block_in, pick_z):
@@ -167,21 +168,26 @@
             z_sum(boundary, pair_z),
         ]
     )
-    slot_wide = jnp.arange(width_x + 1)
-    owner_wide = ((slot_ids + 1)[:, None] == slot_wide[None, :]).astype(jnp.float32)
-    index_y = jnp.arange(width_y)[:, None]
-    coarse_y = jnp.arange(half_y)[None, :]
-    pair_y = (index_y // 2 == coarse_y).astype(jnp.float32)
-    odd_y = (index_y == 2 * coarse_y + 1).astype(jnp.float32)
-
-    def xy_map(pick_y):
-        joint = owner_wide[:, None, :, None] * pick_y[None, :, None, :]
-        return joint.reshape(cells, (width_x + 1) * half_y)
-
-    spread_map = xy_map(pair_y)
-    north_map = xy_map(odd_y)
-    maps = jnp.stack([spread_map, spread_map, north_map, spread_map, spread_map])
-    slot_sums = jnp.einsum("qnm,qnl->qml", maps, z_parts, precision=lax.Precision.HIGHEST)
+    index_y = np.arange(width_y)[:, None]
+    coarse_y = np.arange(half_y)[None, :]
+    pair_y = jnp.asarray((index_y // 2 == coarse_y).astype(np.float32))
+    row_y = np.tile(np.arange(width_y), width_x)
+    col_slot = np.repeat(np.arange(width_x + 1), half_y)
+    col_y = np.tile(np.arange(half_y), width_x + 1)
+    row_slot = jnp.repeat(slot_ids + 1, width_y)
+    same_slot = row_slot[:, None] == jnp.asarray(col_slot.astype(np.float32))[None, :]
+    pair_rows = row_y[:, None] // 2 == col_y[None, :]
+    odd_rows = row_y[:, None] == 2 * col_y[None, :] + 1
+    spread_map = (same_slot & pair_rows).astype(jnp.float32)
+    gather_map = (same_slot.T & pair_rows.T).astype(jnp.float32)
+    north_gather = (same_slot.T & odd_rows.T).astype(jnp.float32)
+    paired = jnp.dot(
+        gather_map,
+        jnp.concatenate([z_parts[0], z_parts[1], z_parts[3], z_parts[4]], axis=1),
+        precision=lax.Precision.HIGHEST,
+    ).reshape((width_x + 1) * half_y, 4, half_z)
+    north_sums = jnp.dot(north_gather, z_parts[2], precision=lax.Precision.HIGHEST)
+    slot_sums = jnp.stack([paired[:, 0], paired[:, 1], north_sums, paired[:, 2], paired[:, 3]])
     slot_sums = slot_sums.reshape(5, width_x + 1, half_y, half_z)
     coarse = slot_sums[:, 1:]
     edge_sums = slot_sums[:, 0]

time: 80 us -> 77.9 us (0.974)
  local copies, waits for them, and re-layouts: 7.72 us -> 4.4 us
  other arithmetic: 15.1 us -> 11.9 us
  waiting for transfers between devices: 17.2 us -> 19.7 us
  matrix products: 4.32 us -> 5.99 us
    mul x7 -> x0, local copies, waits for them, and re-layouts: 4.08 us -> none  [the longest x6 4.08 us: xy_map(): joint = owner_wide[:, None, :, None] * pick_y[None, :, None, :]]
    ppermute x4, waiting for transfers between devices: 10.6 us -> 12.2 us  [padded(): after = lax.ppermute(leading, axis, down)]
    dot_general x5, matrix products: 1.65 us -> 2.9 us  [z_sum(): return jnp.dot(flat, pick_z, precision=lax.Precision.HIGHEST)]
    concatenate x3, other arithmetic: 1.46 us -> 0.4 us  [padded(): array = jnp.concatenate([before, array, after], axis=dim)]
    reshape x0 -> x1, local copies, waits for them, and re-layouts: none -> 1.05 us  [body(): paired = jnp.dot(gather_map, jnp.concatenate([z_parts[0], z_parts[1], z_p...]
    ppermute x4, waiting for transfers between devices: 0.85 us -> 1.82 us  [padded(): before = lax.ppermute(last, axis, up)]
  transfers between devices with their start and end apart: 12 -> 12, of which waited for: 7 -> 8; matrix products, arithmetic and copies ran while one was open for 12% -> 5% of each run, Pallas kernels for 0% -> 0%
where the time goes in v7:
time: 77.9 us; the launch traced here: 77.3 us
  starting transfers between devices  32 us (41%)
  waiting for transfers between devices  19.7 us (25%)
  other arithmetic  11.9 us (15%)
  matrix products  5.99 us (8%)
  local copies, waits for them, and re-layouts  4.4 us (6%)
  between operations  3.23 us (4%)
    ppermute x4, starting transfers between devices, padded(): before = lax.ppermute(last, axis, up)  14.6 us
    ppermute x4, waiting for transfers between devices, padded(): after = lax.ppermute(leading, axis, down)  12.2 us
    ppermute x4, starting transfers between devices, passed_along(): return lax.ppermute(array, axis, pairs)  10.3 us
    ppermute x4, starting transfers between devices, padded(): after = lax.ppermute(leading, axis, down)  7.05 us
    ppermute x4, waiting for transfers between devices, passed_along(): return lax.ppermute(array, axis, pairs)  5.75 us
    add x4, other arithmetic, sweeps(): field_ext = center + OMEGA * (source_now - product) / faces_now[7]  3.75 us
    dot_general x5, matrix products, z_sum(): return jnp.dot(flat, pick_z, precision=lax.Precision.HIGHEST)  2.9 us
    slice x3, other arithmetic, padded(): last = lax.slice_in_dim(array, length - width, length, axis=dim)  2.35 us
  transfers between devices with their start and end apart: 12, of which 8 were waited for; matrix products, arithmetic and copies ran while one was open for 5% of the time, Pallas kernels for 0%

profile of v7, /device:TPU:1, one launch (start us, length us, event | category | flops | bytes accessed | tf_op | source)
XLA Modules:
  0.0 77.3 jit_solution(3713941683034690515)
XLA Ops:
  0.0 1.0 %pad_maximum_fusion.17 = (f32[3,3,16,256]{3,2,1,0:T(8,128)S(1)}, f32[3,3,16,256]{3,2,1,0:T(8,128)S(1)}) fusion(f32[1,16,16,256]{3,2,1,0:T(8,128)} %bitcast.221, f32[1,16,16,256]{3,2,1,0:T(8,128)} %bitcast.218, f32[1,16,16,256]{3,2,1,0:T(8,128)} %bitcast.224), kind=kLoop, calls=%fused_computation.160 | loop fusion | flops 147456 | bytes 1081344 | tf_op jit(solution)/shard_map/slice | solution.py:19
  1.0 4.0 %collective-permute-start = (f32[3,3,16,256]{3,2,1,0:T(8,128)S(1)}, f32[3,3,16,256]{3,2,1,0:T(8,128)S(1)}, u32[]{:S(2)}, u32[]{:S(2)}) collective-permute-start(f32[3,3,16,256]{3,2,1,0:T(8,128)S(1)} %get-tuple-element.19), channel_id=1, source_target_pairs={{0,4},{4,8},{8,12},{1,5},{5,9},{9,13},{2,6},{6,10},{10,14},{3,7},{... | collective-permute-start | bytes 442376 | tf_op jit(solution)/shard_map/ppermute | solution.py:21
  5.1 1.3 %collective-permute-start.1 = (f32[3,3,16,256]{3,2,1,0:T(8,128)S(1)}, f32[3,3,16,256]{3,2,1,0:T(8,128)S(1)}, u32[]{:S(2)}, u32[]{:S(2)}) collective-permute-start(f32[3,3,16,256]{3,2,1,0:T(8,128)S(1)} %get-tuple-element.20), channel_id=1, source_target_pairs={{4,0},{8,4},{12,8},{5,1},{9,5},{13,9},{6,2},{10,6},{14,10},{7,3},{... | collective-permute-start | bytes 442376 | tf_op jit(solution)/shard_map/ppermute | solution.py:22
  7.0 0.7 convert_element_type.113
  7.6 0.2 select_reduce_fusion
  7.8 0.7 fusion.141
  11.7 1.3 %pad_maximum_fusion.13 = (f32[3,22,3,256]{3,2,1,0:T(4,128)S(1)}, f32[3,22,3,256]{3,2,1,0:T(4,128)S(1)}) fusion(f32[3,3,16,256]{3,2,1,0:T(8,128)S(1)} %collective-permute-done.1, f32[3,3,16,256]{3,2,1,0:T(8,128)S(1)} %collective-permute-done, f32[1,16,16,256]{3,2,1,0:T(8,128)} %bitcast.222, f32[1,16,16,256]{3,2,1,0:T(8,128)} %bitcast.219, ...), kind=kLoop, calls=%fused_computation.85 | loop fusion | flops 405504 | bytes 1486848 | tf_op jit(solution)/shard_map/slice | solution.py:19
  13.0 4.5 %collective-permute-start.2 = (f32[3,22,3,256]{3,2,1,0:T(4,128)S(1)}, f32[3,22,3,256]{3,2,1,0:T(4,128)S(1)}, u32[]{:S(2)}, u32[]{:S(2)}) collective-permute-start(f32[3,22,3,256]{3,2,1,0:T(4,128)S(1)} %get-tuple-element.17), channel_id=1, source_target_pairs={{0,1},{1,2},{2,3},{4,5},{5,6},{6,7},{8,9},{9,10},{10,11},{12,13},{... | collective-permute-start | bytes 608264 | tf_op jit(solution)/shard_map/ppermute | solution.py:21
  17.5 1.9 %collective-permute-start.3 = (f32[3,22,3,256]{3,2,1,0:T(4,128)S(1)}, f32[3,22,3,256]{3,2,1,0:T(4,128)S(1)}, u32[]{:S(2)}, u32[]{:S(2)}) collective-permute-start(f32[3,22,3,256]{3,2,1,0:T(4,128)S(1)} %get-tuple-element.18), channel_id=1, source_target_pairs={{1,0},{2,1},{3,2},{5,4},{6,5},{7,6},{9,8},{10,9},{11,10},{13,12},{... | collective-permute-start | bytes 608264 | tf_op jit(solution)/shard_map/ppermute | solution.py:22
  19.5 1.4 %collective-permute-done.2 = f32[3,22,3,256]{3,2,1,0:T(4,128)S(1)} collective-permute-done((f32[3,22,3,256]{3,2,1,0:T(4,128)S(1)}, f32[3,22,3,256]{3,2,1,0:T(4,128)S(1)}, u32[]{:S(2)}, u32[]{:S(2)}) %collective-permute-start.2) | collective-permute-done | bytes 202784 | tf_op jit(solution)/shard_map/ppermute | solution.py:21
  20.9 4.4 %collective-permute-done.3 = f32[3,22,3,256]{3,2,1,0:T(4,128)S(1)} collective-permute-done((f32[3,22,3,256]{3,2,1,0:T(4,128)S(1)}, f32[3,22,3,256]{3,2,1,0:T(4,128)S(1)}, u32[]{:S(2)}, u32[]{:S(2)}) %collective-permute-start.3) | collective-permute-done | bytes 202784 | tf_op jit(solution)/shard_map/ppermute | solution.py:22
  25.3 0.3 pad_maximum_fusion
  25.6 0.1 slice_bitcast_fusion
  25.7 0.2 fusion.129
  25.9 0.2 divide_select_fusion
  26.1 0.2 divide_select_fusion.1
  26.3 0.2 fusion.130
  26.5 0.2 divide_select_fusion.2
  26.7 1.0 %fusion.15 = (f32[20,20,256]{2,1,0:T(8,128)S(1)}, f32[20,20,256]{2,1,0:T(8,128)S(1)}, f32[20,20,256]{2,1,0:T(8,128)S(1)}) fusion(f32[22,22,256]{2,1,0:T(8,128)S(1)} %get-tuple-element.16, f32[22,22,256]{2,1,0:T(8,128)S(1)} %get-tuple-element.15, f32[20,20,255]{2,1,0:T(8,128)S(1)} %get-tuple-element.26, f32[20,20,255]{2,1,0:T(8,128)S(1)} %get-tuple-element.25, ...), kind=kLoop, calls=%fused_computation.29 | loop fusion | flops 2764800 | bytes 6961424 | tf_op jit(solution)/shard_map/add | solution.py:106
  27.7 0.2 fusion.133
  27.9 0.8 fusion.38
  28.7 0.1 fusion.135
  28.8 1.1 %fusion.128 = (f32[16,16,256]{2,1,0:T(8,128)}, f32[16,16,256]{2,1,0:T(8,128)S(1)}, f32[16,16,256]{2,1,0:T(8,128)S(1)}, f32[16,16,256]{2,1,0:T(8,128)S(1)}) fusion(f32[22,21,256]{2,1,0:T(8,128)S(1)} %divide_select_fusion, f32[16,16,256]{2,1,0:T(8,128)S(1)} %copy-done.1, f32[16,16,255]{2,1,0:T(8,128)S(1)} %get-tuple-element.38, ...), kind=kLoop, calls=%fused_computation.271 | loop fusion | flops 983040 | bytes 4862464 | tf_op jit(solution)/shard_map/slice | solution.py:94
  30.0 0.4 fusion.142
  30.4 0.4 fusion.143
  30.8 0.4 fusion.145
  31.2 0.4 fusion.144
  31.7 1.2 %fusion = f32[136,512]{1,0:T(8,128)} fusion(f32[256,128]{0,1:T(8,128)S(1)} %fusion.145, f32[256,128]{0,1:T(8,128)S(1)} %fusion.144, f32[256,128]{0,1:T(8,128)S(1)} %fusion.143, f32[256,128]{0,1:T(8,128)S(1)} %fusion.142, pred[136,256]{1,0:T(8,128)(4,1)S(1)} %copy-done.9, f32[256]{0:T(256)S(1)} %eq.138, f32[136]{0:T(256)S(1)} %copy-done.8), kind=kOutput, calls=%fused_computation.9 | convolution fusion | flops 214372352 | bytes 839200 | tf_op jit(solution)/shard_map/dot_general | solution.py:184
  32.8 1.0 %reshape.280 = f32[136,4,128]{2,1,0:T(4,128)S(1)} reshape(f32[136,512]{1,0:T(8,128)} %fusion) | data formatting | bytes 557056 | tf_op jit(solution)/shard_map/reshape | solution.py:188
  33.9 0.2 fusion.136
  34.1 1.3 %fusion.146 = f32[256,128]{1,0:T(8,128)S(1)} fusion(f32[256,256]{1,0:T(8,128)} %bitcast.228, f32[256,128]{1,0:T(8,128)S(1)} %copy-done), kind=kOutput, calls=%fused_computation.289 | convolution fusion | flops 100663296 | bytes 524288 | tf_op jit(solution)/shard_map/dot_general | solution.py:160
  35.5 0.3 convolution_bitcast_fusion.2
  35.9 0.3 convolution_bitcast_fusion.1
  36.2 3.7 %collective-permute-start.4 = (f32[5,4,8,128]{3,1,2,0:T(4,128)S(1)}, f32[5,4,8,128]{3,1,2,0:T(4,128)S(1)}, u32[]{:S(2)}, u32[]{:S(2)}) collective-permute-start(f32[5,4,8,128]{3,1,2,0:T(4,128)S(1)} %convolution_bitcast_fusion.1), channel_id=1, source_target_pairs={{0,4},{4,8},{8,12},{1,5},{5,9},{9,13},{2,6},{6,10},{10,14},{3,7},{... | collective-permute-start | bytes 245768 | tf_op jit(solution)/shard_map/ppermute | solution.py:30
  39.9 1.3 %collective-permute-start.5 = (f32[5,5,8,128]{3,1,2,0:T(8,128)S(1)}, f32[5,5,8,128]{3,1,2,0:T(8,128)S(1)}, u32[]{:S(2)}, u32[]{:S(2)}) collective-permute-start(f32[5,5,8,128]{3,1,2,0:T(8,128)S(1)} %pad_maximum_fusion.14), channel_id=1, source_target_pairs={{4,0},{8,4},{12,8},{5,1},{9,5},{13,9},{6,2},{10,6},{14,10},{7,3},{... | collective-permute-start | bytes 307208 | tf_op jit(solution)/shard_map/ppermute | solution.py:30
  41.2 0.1 collective-permute-done.4
  41.4 4.5 %collective-permute-done.5 = f32[5,5,8,128]{3,1,2,0:T(8,128)S(1)} collective-permute-done((f32[5,5,8,128]{3,1,2,0:T(8,128)S(1)}, f32[5,5,8,128]{3,1,2,0:T(8,128)S(1)}, u32[]{:S(2)}, u32[]{:S(2)}) %collective-permute-start.5) | collective-permute-done | bytes 102432 | tf_op jit(solution)/shard_map/ppermute | solution.py:30
  46.0 0.1 multiply_add_fusion
  46.1 0.5 maximum_add_fusion
  46.6 3.2 %collective-permute-start.6 = (f32[5,24,4,128]{3,1,2,0:T(8,128)S(1)}, f32[5,24,4,128]{3,1,2,0:T(8,128)S(1)}, u32[]{:S(2)}, u32[]{:S(2)}) collective-permute-start(f32[5,24,4,128]{3,1,2,0:T(8,128)S(1)} %get-tuple-element.31), channel_id=1, source_target_pairs={{0,1},{1,2},{2,3},{4,5},{5,6},{6,7},{8,9},{9,10},{10,11},{12,13},{... | collective-permute-start | bytes 737288 | tf_op jit(solution)/shard_map/ppermute | solution.py:21
  49.8 1.9 %collective-permute-start.7 = (f32[5,24,4,128]{3,1,2,0:T(8,128)S(1)}, f32[5,24,4,128]{3,1,2,0:T(8,128)S(1)}, u32[]{:S(2)}, u32[]{:S(2)}) collective-permute-start(f32[5,24,4,128]{3,1,2,0:T(8,128)S(1)} %get-tuple-element.32), channel_id=1, source_target_pairs={{1,0},{2,1},{3,2},{5,4},{6,5},{7,6},{9,8},{10,9},{11,10},{13,12},{... | collective-permute-start | bytes 737288 | tf_op jit(solution)/shard_map/ppermute | solution.py:22
  51.7 0.7 and_convert_fusion
  52.5 0.4 collective-permute-done.6
  52.9 4.4 %collective-permute-done.7 = f32[5,24,4,128]{3,1,2,0:T(8,128)S(1)} collective-permute-done((f32[5,24,4,128]{3,1,2,0:T(8,128)S(1)}, f32[5,24,4,128]{3,1,2,0:T(8,128)S(1)}, u32[]{:S(2)}, u32[]{:S(2)}) %collective-permute-start.7) | collective-permute-done | bytes 245792 | tf_op jit(solution)/shard_map/ppermute | solution.py:22
  57.5 0.2 fusion.62
  57.7 0.1 fusion.138
  57.8 0.3 fusion.70
  58.2 0.3 fusion.83
  58.6 0.1 multiply_reduce_fusion
  58.7 0.3 fusion.96
  59.0 0.3 copy-done.5
  59.3 0.3 fusion.59
  59.7 0.2 fusion.147
  59.8 1.3 %collective-permute-start.9 = (f32[2,16,256]{2,1,0:T(8,128)S(1)}, f32[2,16,256]{2,1,0:T(8,128)S(1)}, u32[]{:S(2)}, u32[]{:S(2)}) collective-permute-start(f32[2,16,256]{2,1,0:T(8,128)S(1)} %get-tuple-element.46), channel_id=1, source_target_pairs={{4,0},{8,4},{12,8},{5,1},{9,5},{13,9},{6,2},{10,6},{14,10},{7,3},{... | collective-permute-start | bytes 98312 | tf_op jit(solution)/shard_map/ppermute | solution.py:30
  61.2 0.1 fusion.148
  61.3 4.0 %collective-permute-start.8 = (f32[3,16,256]{2,1,0:T(8,128)S(1)}, f32[3,16,256]{2,1,0:T(8,128)S(1)}, u32[]{:S(2)}, u32[]{:S(2)}) collective-permute-start(f32[3,16,256]{2,1,0:T(8,128)S(1)} %pad_maximum_fusion.19), channel_id=1, source_target_pairs={{0,4},{4,8},{8,12},{1,5},{5,9},{9,13},{2,6},{6,10},{10,14},{3,7},{... | collective-permute-start | bytes 147464 | tf_op jit(solution)/shard_map/ppermute | solution.py:30
  65.4 1.1 %collective-permute-done.8 = f32[3,16,256]{2,1,0:T(8,128)S(1)} collective-permute-done((f32[3,16,256]{2,1,0:T(8,128)S(1)}, f32[3,16,256]{2,1,0:T(8,128)S(1)}, u32[]{:S(2)}, u32[]{:S(2)}) %collective-permute-start.8) | collective-permute-done | bytes 49184 | tf_op jit(solution)/shard_map/ppermute | solution.py:30
  66.7 2.9 %collective-permute-start.10 = (f32[20,2,256]{2,1,0:T(2,128)S(1)}, f32[20,2,256]{2,1,0:T(2,128)S(1)}, u32[]{:S(2)}, u32[]{:S(2)}) collective-permute-start(f32[20,2,256]{2,1,0:T(2,128)S(1)} %get-tuple-element.39), channel_id=1, source_target_pairs={{0,1},{1,2},{2,3},{4,5},{5,6},{6,7},{8,9},{9,10},{10,11},{12,13},{... | collective-permute-start | bytes 122888 | tf_op jit(solution)/shard_map/ppermute | solution.py:21
  69.5 1.9 %collective-permute-start.11 = (f32[20,2,256]{2,1,0:T(2,128)S(1)}, f32[20,2,256]{2,1,0:T(2,128)S(1)}, u32[]{:S(2)}, u32[]{:S(2)}) collective-permute-start(f32[20,2,256]{2,1,0:T(2,128)S(1)} %get-tuple-element.40), channel_id=1, source_target_pairs={{1,0},{2,1},{3,2},{5,4},{6,5},{7,6},{9,8},{10,9},{11,10},{13,12},{... | collective-permute-start | bytes 122888 | tf_op jit(solution)/shard_map/ppermute | solution.py:22
  71.5 3.4 %collective-permute-done.11 = f32[20,2,256]{2,1,0:T(2,128)S(1)} collective-permute-done((f32[20,2,256]{2,1,0:T(2,128)S(1)}, f32[20,2,256]{2,1,0:T(2,128)S(1)}, u32[]{:S(2)}, u32[]{:S(2)}) %collective-permute-start.11) | collective-permute-done | bytes 40992 | tf_op jit(solution)/shard_map/ppermute | solution.py:22
  74.9 0.2 fusion.131
  75.1 0.8 %fusion.27 = f32[18,18,256]{2,1,0:T(8,128)S(1)} fusion(f32[20,2,256]{2,1,0:T(2,128)S(1)} %collective-permute-done.11, f32[2,16,256]{2,1,0:T(8,128)S(1)} %multiply_add_fusion.3, f32[16,16,256]{2,1,0:T(8,128)S(1)} %multiply_add_fusion.1, f32[2,16,256]{2,1,0:T(8,128)S(1)} %slice.846, f32[20,2,256]{2,1,0:T(2,128)S(1)} %collective-permute-done.10, ...), kind=kLoop, calls=%fused_computation.50 | loop fusion | flops 1907712 | bytes 4796320 | tf_op jit(solution)/shard_map/add | solution.py:106
  76.0 0.1 fusion.134
  76.1 1.2 %fusion.49 = f32[16,16,256]{2,1,0:T(8,128)} fusion(f32[18,18,256]{2,1,0:T(8,128)S(1)} %fusion.27, f32[22,22,256]{2,1,0:T(8,128)S(1)} %get-tuple-element.15, f32[16,16,255]{2,1,0:T(8,128)S(1)} %get-tuple-element.36, f32[16,16,255]{2,1,0:T(8,128)S(1)} %get-tuple-element.35, f32[22,21,256]{2,1,0:T(8,128)S(1)} %divide_select_fusion, ...), kind=kLoop, calls=%fused_computation.94 | loop fusion | flops 1114112 | bytes 4075968 | tf_op jit(solution)/shard_map/add | solution.py:106
  (80 shorter events, 2.3 us)
Async XLA Ops:
  0.0 25.3 %copy-start.3 = (f32[16,16,256]{2,1,0:T(8,128)S(1)}, f32[16,16,256]{2,1,0:T(8,128)}, u32[]{:S(2)}) copy-start(f32[16,16,256]{2,1,0:T(8,128)} %param.11) | copy-start | bytes 786436
  0.0 25.3 %copy-start.1 = (f32[16,16,256]{2,1,0:T(8,128)S(1)}, f32[16,16,256]{2,1,0:T(8,128)}, u32[]{:S(2)}) copy-start(f32[16,16,256]{2,1,0:T(8,128)} %param.12) | copy-start | bytes 786436
  0.0 25.3 %copy-start.2 = (f32[16,16,256]{2,1,0:T(8,128)S(1)}, f32[16,16,256]{2,1,0:T(8,128)}, u32[]{:S(2)}) copy-start(f32[16,16,256]{2,1,0:T(8,128)} %param.13) | copy-start | bytes 786436
  1.0 10.6 %collective-permute-start = (f32[3,3,16,256]{3,2,1,0:T(8,128)S(1)}, f32[3,3,16,256]{3,2,1,0:T(8,128)S(1)}, u32[]{:S(2)}, u32[]{:S(2)}) collective-permute-start(f32[3,3,16,256]{3,2,1,0:T(8,128)S(1)} %get-tuple-element.19), channel_id=1, source_target_pairs={{0,4},{4,8},{8,12},{1,5},{5,9},{9,13},{2,6},{6,10},{10,14},{3,7},{... | collective-permute-start | bytes 442376 | tf_op jit(solution)/shard_map/ppermute | solution.py:21
  5.1 6.6 %collective-permute-start.1 = (f32[3,3,16,256]{3,2,1,0:T(8,128)S(1)}, f32[3,3,16,256]{3,2,1,0:T(8,128)S(1)}, u32[]{:S(2)}, u32[]{:S(2)}) collective-permute-start(f32[3,3,16,256]{3,2,1,0:T(8,128)S(1)} %get-tuple-element.20), channel_id=1, source_target_pairs={{4,0},{8,4},{12,8},{5,1},{9,5},{13,9},{6,2},{10,6},{14,10},{7,3},{... | collective-permute-start | bytes 442376 | tf_op jit(solution)/shard_map/ppermute | solution.py:22
  13.0 7.9 %collective-permute-start.2 = (f32[3,22,3,256]{3,2,1,0:T(4,128)S(1)}, f32[3,22,3,256]{3,2,1,0:T(4,128)S(1)}, u32[]{:S(2)}, u32[]{:S(2)}) collective-permute-start(f32[3,22,3,256]{3,2,1,0:T(4,128)S(1)} %get-tuple-element.17), channel_id=1, source_target_pairs={{0,1},{1,2},{2,3},{4,5},{5,6},{6,7},{8,9},{9,10},{10,11},{12,13},{... | collective-permute-start | bytes 608264 | tf_op jit(solution)/shard_map/ppermute | solution.py:21
  17.5 7.8 %collective-permute-start.3 = (f32[3,22,3,256]{3,2,1,0:T(4,128)S(1)}, f32[3,22,3,256]{3,2,1,0:T(4,128)S(1)}, u32[]{:S(2)}, u32[]{:S(2)}) collective-permute-start(f32[3,22,3,256]{3,2,1,0:T(4,128)S(1)} %get-tuple-element.18), channel_id=1, source_target_pairs={{1,0},{2,1},{3,2},{5,4},{6,5},{7,6},{9,8},{10,9},{11,10},{13,12},{... | collective-permute-start | bytes 608264 | tf_op jit(solution)/shard_map/ppermute | solution.py:22
  28.8 1.2 %copy-start = (f32[256,128]{1,0:T(8,128)S(1)}, f32[256,128]{1,0:T(8,128)}, u32[]{:S(2)}) copy-start(f32[256,128]{1,0:T(8,128)} %constant.45.clone) | copy-start | bytes 393220
  30.0 1.3 %copy-start.4 = (f32[256,128]{1,0:T(8,128)S(1)}, f32[256,128]{1,0:T(8,128)}, u32[]{:S(2)}) copy-start(f32[256,128]{1,0:T(8,128)} %constant.46.clone) | copy-start | bytes 393220
  30.0 1.7 %copy-start.8 = (f32[136]{0:T(256)S(1)}, f32[136]{0:T(256)}, u32[]{:S(2)}) copy-start(f32[136]{0:T(256)} %constant.48.clone) | copy-start | bytes 1636
  30.0 1.7 %copy-start.9 = (pred[136,256]{1,0:T(8,128)(4,1)S(1)}, pred[136,256]{1,0:T(8,128)(4,1)}, u32[]{:S(2)}) copy-start(pred[136,256]{1,0:T(8,128)(4,1)} %constant.50.clone) | copy-start | bytes 104452
  31.7 3.8 %copy-start.6 = (pred[136,256]{1,0:T(8,128)(4,1)S(1)}, pred[136,256]{1,0:T(8,128)(4,1)}, u32[]{:S(2)}) copy-start(pred[136,256]{1,0:T(8,128)(4,1)} %constant.51.clone) | copy-start | bytes 104452
  36.2 5.2 %collective-permute-start.4 = (f32[5,4,8,128]{3,1,2,0:T(4,128)S(1)}, f32[5,4,8,128]{3,1,2,0:T(4,128)S(1)}, u32[]{:S(2)}, u32[]{:S(2)}) collective-permute-start(f32[5,4,8,128]{3,1,2,0:T(4,128)S(1)} %convolution_bitcast_fusion.1), channel_id=1, source_target_pairs={{0,4},{4,8},{8,12},{1,5},{5,9},{9,13},{2,6},{6,10},{10,14},{3,7},{... | collective-permute-start | bytes 245768 | tf_op jit(solution)/shard_map/ppermute | solution.py:30
  39.9 6.1 %collective-permute-start.5 = (f32[5,5,8,128]{3,1,2,0:T(8,128)S(1)}, f32[5,5,8,128]{3,1,2,0:T(8,128)S(1)}, u32[]{:S(2)}, u32[]{:S(2)}) collective-permute-start(f32[5,5,8,128]{3,1,2,0:T(8,128)S(1)} %pad_maximum_fusion.14), channel_id=1, source_target_pairs={{4,0},{8,4},{12,8},{5,1},{9,5},{13,9},{6,2},{10,6},{14,10},{7,3},{... | collective-permute-start | bytes 307208 | tf_op jit(solution)/shard_map/ppermute | solution.py:30
  46.6 6.3 %collective-permute-start.6 = (f32[5,24,4,128]{3,1,2,0:T(8,128)S(1)}, f32[5,24,4,128]{3,1,2,0:T(8,128)S(1)}, u32[]{:S(2)}, u32[]{:S(2)}) collective-permute-start(f32[5,24,4,128]{3,1,2,0:T(8,128)S(1)} %get-tuple-element.31), channel_id=1, source_target_pairs={{0,1},{1,2},{2,3},{4,5},{5,6},{6,7},{8,9},{9,10},{10,11},{12,13},{... | collective-permute-start | bytes 737288 | tf_op jit(solution)/shard_map/ppermute | solution.py:21
  49.8 7.5 %collective-permute-start.7 = (f32[5,24,4,128]{3,1,2,0:T(8,128)S(1)}, f32[5,24,4,128]{3,1,2,0:T(8,128)S(1)}, u32[]{:S(2)}, u32[]{:S(2)}) collective-permute-start(f32[5,24,4,128]{3,1,2,0:T(8,128)S(1)} %get-tuple-element.32), channel_id=1, source_target_pairs={{1,0},{2,1},{3,2},{5,4},{6,5},{7,6},{9,8},{10,9},{11,10},{13,12},{... | collective-permute-start | bytes 737288 | tf_op jit(solution)/shard_map/ppermute | solution.py:22
  58.4 0.8 %copy-start.5 = (pred[256,136]{1,0:T(32,128)(4,1)S(1)}, pred[256,136]{1,0:T(32,128)(4,1)}, u32[]{:S(2)}) copy-start(pred[256,136]{1,0:T(32,128)(4,1)} %constant.49.clone) | copy-start | bytes 104452
  58.5 2.6 %copy-start.7 = (f32[16,8]{1,0:T(8,128)S(1)}, f32[16,8]{1,0:T(8,128)}, u32[]{:S(2)}) copy-start(f32[16,8]{1,0:T(8,128)} %constant.47.clone) | copy-start | bytes 1540
  59.8 5.5 %collective-permute-start.9 = (f32[2,16,256]{2,1,0:T(8,128)S(1)}, f32[2,16,256]{2,1,0:T(8,128)S(1)}, u32[]{:S(2)}, u32[]{:S(2)}) collective-permute-start(f32[2,16,256]{2,1,0:T(8,128)S(1)} %get-tuple-element.46), channel_id=1, source_target_pairs={{4,0},{8,4},{12,8},{5,1},{9,5},{13,9},{6,2},{10,6},{14,10},{7,3},{... | collective-permute-start | bytes 98312 | tf_op jit(solution)/shard_map/ppermute | solution.py:30
  61.3 5.2 %collective-permute-start.8 = (f32[3,16,256]{2,1,0:T(8,128)S(1)}, f32[3,16,256]{2,1,0:T(8,128)S(1)}, u32[]{:S(2)}, u32[]{:S(2)}) collective-permute-start(f32[3,16,256]{2,1,0:T(8,128)S(1)} %pad_maximum_fusion.19), channel_id=1, source_target_pairs={{0,4},{4,8},{8,12},{1,5},{5,9},{9,13},{2,6},{6,10},{10,14},{3,7},{... | collective-permute-start | bytes 147464 | tf_op jit(solution)/shard_map/ppermute | solution.py:30
  66.7 4.8 %collective-permute-start.10 = (f32[20,2,256]{2,1,0:T(2,128)S(1)}, f32[20,2,256]{2,1,0:T(2,128)S(1)}, u32[]{:S(2)}, u32[]{:S(2)}) collective-permute-start(f32[20,2,256]{2,1,0:T(2,128)S(1)} %get-tuple-element.39), channel_id=1, source_target_pairs={{0,1},{1,2},{2,3},{4,5},{5,6},{6,7},{8,9},{9,10},{10,11},{12,13},{... | collective-permute-start | bytes 122888 | tf_op jit(solution)/shard_map/ppermute | solution.py:21
  69.5 5.3 %collective-permute-start.11 = (f32[20,2,256]{2,1,0:T(2,128)S(1)}, f32[20,2,256]{2,1,0:T(2,128)S(1)}, u32[]{:S(2)}, u32[]{:S(2)}) collective-permute-start(f32[20,2,256]{2,1,0:T(2,128)S(1)} %get-tuple-element.40), channel_id=1, source_target_pairs={{1,0},{2,1},{3,2},{5,4},{6,5},{7,6},{9,8},{10,9},{11,10},{13,12},{... | collective-permute-start | bytes 122888 | tf_op jit(solution)/shard_map/ppermute | solution.py:22

commit v8 on v7

--- a/solution.py
+++ b/solution.py
@@ -185,9 +185,13 @@
         gather_map,
         jnp.concatenate([z_parts[0], z_parts[1], z_parts[3], z_parts[4]], axis=1),
         precision=lax.Precision.HIGHEST,
-    ).reshape((width_x + 1) * half_y, 4, half_z)
+    )
     north_sums = jnp.dot(north_gather, z_parts[2], precision=lax.Precision.HIGHEST)
-    slot_sums = jnp.stack([paired[:, 0], paired[:, 1], north_sums, paired[:, 2], paired[:, 3]])
+
+    def column(index):
+        return paired[:, index * half_z : (index + 1) * half_z]
+
+    slot_sums = jnp.stack([column(0), column(1), north_sums, column(2), column(3)])
     slot_sums = slot_sums.reshape(5, width_x + 1, half_y, half_z)
     coarse = slot_sums[:, 1:]
     edge_sums = slot_sums[:, 0]

time: 77.9 us -> 74.6 us (0.958)
  matrix products: 5.99 us -> 4.33 us
  local copies, waits for them, and re-layouts: 4.4 us -> 3.57 us
  other arithmetic: 11.9 us -> 11.1 us
    reshape x1 -> x0, local copies, waits for them, and re-layouts: 1.05 us -> none  [body(): paired = jnp.dot(gather_map, jnp.concatenate([z_parts[0], z_parts[1], z_p...]
    dot_general x5, matrix products: 2.9 us -> 1.95 us  [z_sum(): return jnp.dot(flat, pick_z, precision=lax.Precision.HIGHEST)]
where the time goes in v8:
time: 74.6 us; the launch traced here: 74 us
  starting transfers between devices  32 us (43%)
  waiting for transfers between devices  19.8 us (27%)
  other arithmetic  11.1 us (15%)
  matrix products  4.33 us (6%)
  local copies, waits for them, and re-layouts  3.57 us (5%)
  between operations  3.21 us (4%)
    ppermute x4, starting transfers between devices, padded(): before = lax.ppermute(last, axis, up)  14.7 us
    ppermute x4, waiting for transfers between devices, padded(): after = lax.ppermute(leading, axis, down)  12.2 us
    ppermute x4, starting transfers between devices, passed_along(): return lax.ppermute(array, axis, pairs)  10.2 us
    ppermute x4, starting transfers between devices, padded(): after = lax.ppermute(leading, axis, down)  7.05 us
    ppermute x4, waiting for transfers between devices, passed_along(): return lax.ppermute(array, axis, pairs)  5.75 us
    add x4, other arithmetic, sweeps(): field_ext = center + OMEGA * (source_now - product) / faces_now[7]  3.67 us
    slice x3, other arithmetic, padded(): last = lax.slice_in_dim(array, length - width, length, axis=dim)  2.35 us
    dot_general x5, matrix products, z_sum(): return jnp.dot(flat, pick_z, precision=lax.Precision.HIGHEST)  1.95 us
  transfers between devices with their start and end apart: 12, of which 8 were waited for; matrix products, arithmetic and copies ran while one was open for 5% of the time, Pallas kernels for 0%

profile of v8, /device:TPU:1, one launch (start us, length us, event | category | flops | bytes accessed | tf_op | source)
XLA Modules:
  0.0 74.0 jit_solution(8547274897416651141)
XLA Ops:
  0.0 1.0 %pad_maximum_fusion.17 = (f32[3,3,16,256]{3,2,1,0:T(8,128)S(1)}, f32[3,3,16,256]{3,2,1,0:T(8,128)S(1)}) fusion(f32[1,16,16,256]{3,2,1,0:T(8,128)} %bitcast.217, f32[1,16,16,256]{3,2,1,0:T(8,128)} %bitcast.214, f32[1,16,16,256]{3,2,1,0:T(8,128)} %bitcast.220), kind=kLoop, calls=%fused_computation.160 | loop fusion | flops 147456 | bytes 1081344 | tf_op jit(solution)/shard_map/slice | solution.py:19
  1.0 4.0 %collective-permute-start = (f32[3,3,16,256]{3,2,1,0:T(8,128)S(1)}, f32[3,3,16,256]{3,2,1,0:T(8,128)S(1)}, u32[]{:S(2)}, u32[]{:S(2)}) collective-permute-start(f32[3,3,16,256]{3,2,1,0:T(8,128)S(1)} %get-tuple-element.19), channel_id=1, source_target_pairs={{0,4},{4,8},{8,12},{1,5},{5,9},{9,13},{2,6},{6,10},{10,14},{3,7},{... | collective-permute-start | bytes 442376 | tf_op jit(solution)/shard_map/ppermute | solution.py:21
  5.1 1.3 %collective-permute-start.1 = (f32[3,3,16,256]{3,2,1,0:T(8,128)S(1)}, f32[3,3,16,256]{3,2,1,0:T(8,128)S(1)}, u32[]{:S(2)}, u32[]{:S(2)}) collective-permute-start(f32[3,3,16,256]{3,2,1,0:T(8,128)S(1)} %get-tuple-element.20), channel_id=1, source_target_pairs={{4,0},{8,4},{12,8},{5,1},{9,5},{13,9},{6,2},{10,6},{14,10},{7,3},{... | collective-permute-start | bytes 442376 | tf_op jit(solution)/shard_map/ppermute | solution.py:22
  7.0 0.7 convert_element_type.113
  7.6 0.2 select_reduce_fusion
  7.8 0.6 fusion.140
  11.6 1.3 %pad_maximum_fusion.13 = (f32[3,22,3,256]{3,2,1,0:T(4,128)S(1)}, f32[3,22,3,256]{3,2,1,0:T(4,128)S(1)}) fusion(f32[3,3,16,256]{3,2,1,0:T(8,128)S(1)} %collective-permute-done.1, f32[3,3,16,256]{3,2,1,0:T(8,128)S(1)} %collective-permute-done, f32[1,16,16,256]{3,2,1,0:T(8,128)} %bitcast.218, f32[1,16,16,256]{3,2,1,0:T(8,128)} %bitcast.215, ...), kind=kLoop, calls=%fused_computation.85 | loop fusion | flops 405504 | bytes 1486848 | tf_op jit(solution)/shard_map/slice | solution.py:19
  12.9 4.6 %collective-permute-start.2 = (f32[3,22,3,256]{3,2,1,0:T(4,128)S(1)}, f32[3,22,3,256]{3,2,1,0:T(4,128)S(1)}, u32[]{:S(2)}, u32[]{:S(2)}) collective-permute-start(f32[3,22,3,256]{3,2,1,0:T(4,128)S(1)} %get-tuple-element.17), channel_id=1, source_target_pairs={{0,1},{1,2},{2,3},{4,5},{5,6},{6,7},{8,9},{9,10},{10,11},{12,13},{... | collective-permute-start | bytes 608264 | tf_op jit(solution)/shard_map/ppermute | solution.py:21
  17.5 1.9 %collective-permute-start.3 = (f32[3,22,3,256]{3,2,1,0:T(4,128)S(1)}, f32[3,22,3,256]{3,2,1,0:T(4,128)S(1)}, u32[]{:S(2)}, u32[]{:S(2)}) collective-permute-start(f32[3,22,3,256]{3,2,1,0:T(4,128)S(1)} %get-tuple-element.18), channel_id=1, source_target_pairs={{1,0},{2,1},{3,2},{5,4},{6,5},{7,6},{9,8},{10,9},{11,10},{13,12},{... | collective-permute-start | bytes 608264 | tf_op jit(solution)/shard_map/ppermute | solution.py:22
  19.5 1.4 %collective-permute-done.2 = f32[3,22,3,256]{3,2,1,0:T(4,128)S(1)} collective-permute-done((f32[3,22,3,256]{3,2,1,0:T(4,128)S(1)}, f32[3,22,3,256]{3,2,1,0:T(4,128)S(1)}, u32[]{:S(2)}, u32[]{:S(2)}) %collective-permute-start.2) | collective-permute-done | bytes 202784 | tf_op jit(solution)/shard_map/ppermute | solution.py:21
  20.9 4.4 %collective-permute-done.3 = f32[3,22,3,256]{3,2,1,0:T(4,128)S(1)} collective-permute-done((f32[3,22,3,256]{3,2,1,0:T(4,128)S(1)}, f32[3,22,3,256]{3,2,1,0:T(4,128)S(1)}, u32[]{:S(2)}, u32[]{:S(2)}) %collective-permute-start.3) | collective-permute-done | bytes 202784 | tf_op jit(solution)/shard_map/ppermute | solution.py:22
  25.3 0.3 pad_maximum_fusion
  25.6 0.1 slice_bitcast_fusion
  25.7 0.2 fusion.129
  25.9 0.2 divide_select_fusion
  26.1 0.2 divide_select_fusion.1
  26.3 0.2 fusion.130
  26.5 0.2 divide_select_fusion.2
  26.7 1.0 %fusion.15 = (f32[20,20,256]{2,1,0:T(8,128)S(1)}, f32[20,20,256]{2,1,0:T(8,128)S(1)}, f32[20,20,256]{2,1,0:T(8,128)S(1)}) fusion(f32[22,22,256]{2,1,0:T(8,128)S(1)} %get-tuple-element.16, f32[22,22,256]{2,1,0:T(8,128)S(1)} %get-tuple-element.15, f32[20,20,255]{2,1,0:T(8,128)S(1)} %get-tuple-element.26, f32[20,20,255]{2,1,0:T(8,128)S(1)} %get-tuple-element.25, ...), kind=kLoop, calls=%fused_computation.29 | loop fusion | flops 2764800 | bytes 6961424 | tf_op jit(solution)/shard_map/add | solution.py:106
  27.7 0.2 fusion.133
  27.9 0.8 %fusion.38 = f32[18,18,256]{2,1,0:T(8,128)S(1)} fusion(f32[20,20,256]{2,1,0:T(8,128)S(1)} %get-tuple-element.11, f32[18,18,255]{2,1,0:T(8,128)S(1)} %get-tuple-element.34, f32[18,18,255]{2,1,0:T(8,128)S(1)} %get-tuple-element.33, f32[22,21,256]{2,1,0:T(8,128)S(1)} %divide_select_fusion, f32[21,22,256]{2,1,0:T(8,128)S(1)} %divide_select_fusion.1, ...), kind=kLoop, calls=%fused_computation.69 | loop fusion | flops 1410048 | bytes 5050272 | tf_op jit(solution)/shard_map/add | solution.py:106
  28.7 0.1 fusion.135
  28.8 0.5 fusion.128
  29.4 0.4 copy-done
  29.7 0.4 fusion.141
  30.1 0.4 fusion.142
  30.6 0.4 fusion.144
  31.0 0.4 fusion.143
  31.4 0.4 fusion
  31.9 0.4 fusion.145
  32.3 0.3 convolution_bitcast_fusion.2
  32.8 0.3 convolution_bitcast_fusion.1
  33.1 3.6 %collective-permute-start.4 = (f32[5,4,8,128]{3,1,2,0:T(4,128)S(1)}, f32[5,4,8,128]{3,1,2,0:T(4,128)S(1)}, u32[]{:S(2)}, u32[]{:S(2)}) collective-permute-start(f32[5,4,8,128]{3,1,2,0:T(4,128)S(1)} %convolution_bitcast_fusion.1), channel_id=1, source_target_pairs={{0,4},{4,8},{8,12},{1,5},{5,9},{9,13},{2,6},{6,10},{10,14},{3,7},{... | collective-permute-start | bytes 245768 | tf_op jit(solution)/shard_map/ppermute | solution.py:30
  36.7 1.3 %collective-permute-start.5 = (f32[5,5,8,128]{3,1,2,0:T(8,128)S(1)}, f32[5,5,8,128]{3,1,2,0:T(8,128)S(1)}, u32[]{:S(2)}, u32[]{:S(2)}) collective-permute-start(f32[5,5,8,128]{3,1,2,0:T(8,128)S(1)} %pad_maximum_fusion.14), channel_id=1, source_target_pairs={{4,0},{8,4},{12,8},{5,1},{9,5},{13,9},{6,2},{10,6},{14,10},{7,3},{... | collective-permute-start | bytes 307208 | tf_op jit(solution)/shard_map/ppermute | solution.py:30
  38.0 0.1 collective-permute-done.4
  38.2 4.5 %collective-permute-done.5 = f32[5,5,8,128]{3,1,2,0:T(8,128)S(1)} collective-permute-done((f32[5,5,8,128]{3,1,2,0:T(8,128)S(1)}, f32[5,5,8,128]{3,1,2,0:T(8,128)S(1)}, u32[]{:S(2)}, u32[]{:S(2)}) %collective-permute-start.5) | collective-permute-done | bytes 102432 | tf_op jit(solution)/shard_map/ppermute | solution.py:30
  42.8 0.1 multiply_add_fusion
  42.9 0.5 maximum_add_fusion
  43.5 3.2 %collective-permute-start.6 = (f32[5,24,4,128]{3,1,2,0:T(8,128)S(1)}, f32[5,24,4,128]{3,1,2,0:T(8,128)S(1)}, u32[]{:S(2)}, u32[]{:S(2)}) collective-permute-start(f32[5,24,4,128]{3,1,2,0:T(8,128)S(1)} %get-tuple-element.31), channel_id=1, source_target_pairs={{0,1},{1,2},{2,3},{4,5},{5,6},{6,7},{8,9},{9,10},{10,11},{12,13},{... | collective-permute-start | bytes 737288 | tf_op jit(solution)/shard_map/ppermute | solution.py:21
  46.6 1.9 %collective-permute-start.7 = (f32[5,24,4,128]{3,1,2,0:T(8,128)S(1)}, f32[5,24,4,128]{3,1,2,0:T(8,128)S(1)}, u32[]{:S(2)}, u32[]{:S(2)}) collective-permute-start(f32[5,24,4,128]{3,1,2,0:T(8,128)S(1)} %get-tuple-element.32), channel_id=1, source_target_pairs={{1,0},{2,1},{3,2},{5,4},{6,5},{7,6},{9,8},{10,9},{11,10},{13,12},{... | collective-permute-start | bytes 737288 | tf_op jit(solution)/shard_map/ppermute | solution.py:22
  48.6 0.7 and_convert_fusion
  49.3 0.5 collective-permute-done.6
  49.8 4.4 %collective-permute-done.7 = f32[5,24,4,128]{3,1,2,0:T(8,128)S(1)} collective-permute-done((f32[5,24,4,128]{3,1,2,0:T(8,128)S(1)}, f32[5,24,4,128]{3,1,2,0:T(8,128)S(1)}, u32[]{:S(2)}, u32[]{:S(2)}) %collective-permute-start.7) | collective-permute-done | bytes 245792 | tf_op jit(solution)/shard_map/ppermute | solution.py:22
  54.3 0.2 fusion.62
  54.5 0.1 fusion.137
  54.6 0.3 fusion.70
  54.9 0.1 fusion.138
  55.0 0.3 fusion.83
  55.4 0.1 multiply_reduce_fusion
  55.6 0.3 fusion.96
  55.9 0.3 copy-done.5
  56.1 0.3 fusion.59
  56.5 0.2 fusion.146
  56.7 1.3 %collective-permute-start.9 = (f32[2,16,256]{2,1,0:T(8,128)S(1)}, f32[2,16,256]{2,1,0:T(8,128)S(1)}, u32[]{:S(2)}, u32[]{:S(2)}) collective-permute-start(f32[2,16,256]{2,1,0:T(8,128)S(1)} %get-tuple-element.46), channel_id=1, source_target_pairs={{4,0},{8,4},{12,8},{5,1},{9,5},{13,9},{6,2},{10,6},{14,10},{7,3},{... | collective-permute-start | bytes 98312 | tf_op jit(solution)/shard_map/ppermute | solution.py:30
  58.0 0.1 fusion.147
  58.2 4.0 %collective-permute-start.8 = (f32[3,16,256]{2,1,0:T(8,128)S(1)}, f32[3,16,256]{2,1,0:T(8,128)S(1)}, u32[]{:S(2)}, u32[]{:S(2)}) collective-permute-start(f32[3,16,256]{2,1,0:T(8,128)S(1)} %pad_maximum_fusion.19), channel_id=1, source_target_pairs={{0,4},{4,8},{8,12},{1,5},{5,9},{9,13},{2,6},{6,10},{10,14},{3,7},{... | collective-permute-start | bytes 147464 | tf_op jit(solution)/shard_map/ppermute | solution.py:30
  62.3 1.1 %collective-permute-done.8 = f32[3,16,256]{2,1,0:T(8,128)S(1)} collective-permute-done((f32[3,16,256]{2,1,0:T(8,128)S(1)}, f32[3,16,256]{2,1,0:T(8,128)S(1)}, u32[]{:S(2)}, u32[]{:S(2)}) %collective-permute-start.8) | collective-permute-done | bytes 49184 | tf_op jit(solution)/shard_map/ppermute | solution.py:30
  63.5 2.9 %collective-permute-start.10 = (f32[20,2,256]{2,1,0:T(2,128)S(1)}, f32[20,2,256]{2,1,0:T(2,128)S(1)}, u32[]{:S(2)}, u32[]{:S(2)}) collective-permute-start(f32[20,2,256]{2,1,0:T(2,128)S(1)} %get-tuple-element.39), channel_id=1, source_target_pairs={{0,1},{1,2},{2,3},{4,5},{5,6},{6,7},{8,9},{9,10},{10,11},{12,13},{... | collective-permute-start | bytes 122888 | tf_op jit(solution)/shard_map/ppermute | solution.py:21
  66.4 1.9 %collective-permute-start.11 = (f32[20,2,256]{2,1,0:T(2,128)S(1)}, f32[20,2,256]{2,1,0:T(2,128)S(1)}, u32[]{:S(2)}, u32[]{:S(2)}) collective-permute-start(f32[20,2,256]{2,1,0:T(2,128)S(1)} %get-tuple-element.40), channel_id=1, source_target_pairs={{1,0},{2,1},{3,2},{5,4},{6,5},{7,6},{9,8},{10,9},{11,10},{13,12},{... | collective-permute-start | bytes 122888 | tf_op jit(solution)/shard_map/ppermute | solution.py:22
  68.3 3.4 %collective-permute-done.11 = f32[20,2,256]{2,1,0:T(2,128)S(1)} collective-permute-done((f32[20,2,256]{2,1,0:T(2,128)S(1)}, f32[20,2,256]{2,1,0:T(2,128)S(1)}, u32[]{:S(2)}, u32[]{:S(2)}) %collective-permute-start.11) | collective-permute-done | bytes 40992 | tf_op jit(solution)/shard_map/ppermute | solution.py:22
  71.8 0.2 fusion.131
  72.0 0.8 %fusion.27 = f32[18,18,256]{2,1,0:T(8,128)S(1)} fusion(f32[20,2,256]{2,1,0:T(2,128)S(1)} %collective-permute-done.11, f32[2,16,256]{2,1,0:T(8,128)S(1)} %multiply_add_fusion.3, f32[16,16,256]{2,1,0:T(8,128)S(1)} %multiply_add_fusion.1, f32[2,16,256]{2,1,0:T(8,128)S(1)} %slice.846, f32[20,2,256]{2,1,0:T(2,128)S(1)} %collective-permute-done.10, ...), kind=kLoop, calls=%fused_computation.50 | loop fusion | flops 1907712 | bytes 4796320 | tf_op jit(solution)/shard_map/add | solution.py:106
  72.8 0.1 fusion.134
  72.9 1.1 %fusion.49 = f32[16,16,256]{2,1,0:T(8,128)} fusion(f32[18,18,256]{2,1,0:T(8,128)S(1)} %fusion.27, f32[22,22,256]{2,1,0:T(8,128)S(1)} %get-tuple-element.15, f32[16,16,255]{2,1,0:T(8,128)S(1)} %get-tuple-element.36, f32[16,16,255]{2,1,0:T(8,128)S(1)} %get-tuple-element.35, f32[22,21,256]{2,1,0:T(8,128)S(1)} %divide_select_fusion, ...), kind=kLoop, calls=%fused_computation.94 | loop fusion | flops 1114112 | bytes 4075968 | tf_op jit(solution)/shard_map/add | solution.py:106
  (79 shorter events, 2.2 us)
Async XLA Ops:
  0.0 25.3 %copy-start.3 = (f32[16,16,256]{2,1,0:T(8,128)S(1)}, f32[16,16,256]{2,1,0:T(8,128)}, u32[]{:S(2)}) copy-start(f32[16,16,256]{2,1,0:T(8,128)} %param.11) | copy-start | bytes 786436
  0.0 25.3 %copy-start.1 = (f32[16,16,256]{2,1,0:T(8,128)S(1)}, f32[16,16,256]{2,1,0:T(8,128)}, u32[]{:S(2)}) copy-start(f32[16,16,256]{2,1,0:T(8,128)} %param.12) | copy-start | bytes 786436
  0.0 25.3 %copy-start.2 = (f32[16,16,256]{2,1,0:T(8,128)S(1)}, f32[16,16,256]{2,1,0:T(8,128)}, u32[]{:S(2)}) copy-start(f32[16,16,256]{2,1,0:T(8,128)} %param.13) | copy-start | bytes 786436
  1.0 10.6 %collective-permute-start = (f32[3,3,16,256]{3,2,1,0:T(8,128)S(1)}, f32[3,3,16,256]{3,2,1,0:T(8,128)S(1)}, u32[]{:S(2)}, u32[]{:S(2)}) collective-permute-start(f32[3,3,16,256]{3,2,1,0:T(8,128)S(1)} %get-tuple-element.19), channel_id=1, source_target_pairs={{0,4},{4,8},{8,12},{1,5},{5,9},{9,13},{2,6},{6,10},{10,14},{3,7},{... | collective-permute-start | bytes 442376 | tf_op jit(solution)/shard_map/ppermute | solution.py:21
  5.1 6.5 %collective-permute-start.1 = (f32[3,3,16,256]{3,2,1,0:T(8,128)S(1)}, f32[3,3,16,256]{3,2,1,0:T(8,128)S(1)}, u32[]{:S(2)}, u32[]{:S(2)}) collective-permute-start(f32[3,3,16,256]{3,2,1,0:T(8,128)S(1)} %get-tuple-element.20), channel_id=1, source_target_pairs={{4,0},{8,4},{12,8},{5,1},{9,5},{13,9},{6,2},{10,6},{14,10},{7,3},{... | collective-permute-start | bytes 442376 | tf_op jit(solution)/shard_map/ppermute | solution.py:22
  12.9 8.0 %collective-permute-start.2 = (f32[3,22,3,256]{3,2,1,0:T(4,128)S(1)}, f32[3,22,3,256]{3,2,1,0:T(4,128)S(1)}, u32[]{:S(2)}, u32[]{:S(2)}) collective-permute-start(f32[3,22,3,256]{3,2,1,0:T(4,128)S(1)} %get-tuple-element.17), channel_id=1, source_target_pairs={{0,1},{1,2},{2,3},{4,5},{5,6},{6,7},{8,9},{9,10},{10,11},{12,13},{... | collective-permute-start | bytes 608264 | tf_op jit(solution)/shard_map/ppermute | solution.py:21
  17.5 7.8 %collective-permute-start.3 = (f32[3,22,3,256]{3,2,1,0:T(4,128)S(1)}, f32[3,22,3,256]{3,2,1,0:T(4,128)S(1)}, u32[]{:S(2)}, u32[]{:S(2)}) collective-permute-start(f32[3,22,3,256]{3,2,1,0:T(4,128)S(1)} %get-tuple-element.18), channel_id=1, source_target_pairs={{1,0},{2,1},{3,2},{5,4},{6,5},{7,6},{9,8},{10,9},{11,10},{13,12},{... | collective-permute-start | bytes 608264 | tf_op jit(solution)/shard_map/ppermute | solution.py:22
  28.8 0.9 %copy-start = (f32[256,128]{1,0:T(8,128)S(1)}, f32[256,128]{1,0:T(8,128)}, u32[]{:S(2)}) copy-start(f32[256,128]{1,0:T(8,128)} %constant.45.clone) | copy-start | bytes 393220
  29.3 1.7 %copy-start.4 = (f32[256,128]{1,0:T(8,128)S(1)}, f32[256,128]{1,0:T(8,128)}, u32[]{:S(2)}) copy-start(f32[256,128]{1,0:T(8,128)} %constant.46.clone) | copy-start | bytes 393220
  29.3 2.1 %copy-start.8 = (f32[136]{0:T(256)S(1)}, f32[136]{0:T(256)}, u32[]{:S(2)}) copy-start(f32[136]{0:T(256)} %constant.48.clone) | copy-start | bytes 1636
  29.3 2.1 %copy-start.9 = (pred[136,256]{1,0:T(8,128)(4,1)S(1)}, pred[136,256]{1,0:T(8,128)(4,1)}, u32[]{:S(2)}) copy-start(pred[136,256]{1,0:T(8,128)(4,1)} %constant.50.clone) | copy-start | bytes 104452
  31.0 1.4 %copy-start.6 = (pred[136,256]{1,0:T(8,128)(4,1)S(1)}, pred[136,256]{1,0:T(8,128)(4,1)}, u32[]{:S(2)}) copy-start(pred[136,256]{1,0:T(8,128)(4,1)} %constant.51.clone) | copy-start | bytes 104452
  33.1 5.1 %collective-permute-start.4 = (f32[5,4,8,128]{3,1,2,0:T(4,128)S(1)}, f32[5,4,8,128]{3,1,2,0:T(4,128)S(1)}, u32[]{:S(2)}, u32[]{:S(2)}) collective-permute-start(f32[5,4,8,128]{3,1,2,0:T(4,128)S(1)} %convolution_bitcast_fusion.1), channel_id=1, source_target_pairs={{0,4},{4,8},{8,12},{1,5},{5,9},{9,13},{2,6},{6,10},{10,14},{3,7},{... | collective-permute-start | bytes 245768 | tf_op jit(solution)/shard_map/ppermute | solution.py:30
  36.7 6.1 %collective-permute-start.5 = (f32[5,5,8,128]{3,1,2,0:T(8,128)S(1)}, f32[5,5,8,128]{3,1,2,0:T(8,128)S(1)}, u32[]{:S(2)}, u32[]{:S(2)}) collective-permute-start(f32[5,5,8,128]{3,1,2,0:T(8,128)S(1)} %pad_maximum_fusion.14), channel_id=1, source_target_pairs={{4,0},{8,4},{12,8},{5,1},{9,5},{13,9},{6,2},{10,6},{14,10},{7,3},{... | collective-permute-start | bytes 307208 | tf_op jit(solution)/shard_map/ppermute | solution.py:30
  43.5 6.3 %collective-permute-start.6 = (f32[5,24,4,128]{3,1,2,0:T(8,128)S(1)}, f32[5,24,4,128]{3,1,2,0:T(8,128)S(1)}, u32[]{:S(2)}, u32[]{:S(2)}) collective-permute-start(f32[5,24,4,128]{3,1,2,0:T(8,128)S(1)} %get-tuple-element.31), channel_id=1, source_target_pairs={{0,1},{1,2},{2,3},{4,5},{5,6},{6,7},{8,9},{9,10},{10,11},{12,13},{... | collective-permute-start | bytes 737288 | tf_op jit(solution)/shard_map/ppermute | solution.py:21
  46.6 7.5 %collective-permute-start.7 = (f32[5,24,4,128]{3,1,2,0:T(8,128)S(1)}, f32[5,24,4,128]{3,1,2,0:T(8,128)S(1)}, u32[]{:S(2)}, u32[]{:S(2)}) collective-permute-start(f32[5,24,4,128]{3,1,2,0:T(8,128)S(1)} %get-tuple-element.32), channel_id=1, source_target_pairs={{1,0},{2,1},{3,2},{5,4},{6,5},{7,6},{9,8},{10,9},{11,10},{13,12},{... | collective-permute-start | bytes 737288 | tf_op jit(solution)/shard_map/ppermute | solution.py:22
  55.3 0.8 %copy-start.5 = (pred[256,136]{1,0:T(32,128)(4,1)S(1)}, pred[256,136]{1,0:T(32,128)(4,1)}, u32[]{:S(2)}) copy-start(pred[256,136]{1,0:T(32,128)(4,1)} %constant.49.clone) | copy-start | bytes 104452
  55.4 2.6 %copy-start.7 = (f32[16,8]{1,0:T(8,128)S(1)}, f32[16,8]{1,0:T(8,128)}, u32[]{:S(2)}) copy-start(f32[16,8]{1,0:T(8,128)} %constant.47.clone) | copy-start | bytes 1540
  56.7 5.5 %collective-permute-start.9 = (f32[2,16,256]{2,1,0:T(8,128)S(1)}, f32[2,16,256]{2,1,0:T(8,128)S(1)}, u32[]{:S(2)}, u32[]{:S(2)}) collective-permute-start(f32[2,16,256]{2,1,0:T(8,128)S(1)} %get-tuple-element.46), channel_id=1, source_target_pairs={{4,0},{8,4},{12,8},{5,1},{9,5},{13,9},{6,2},{10,6},{14,10},{7,3},{... | collective-permute-start | bytes 98312 | tf_op jit(solution)/shard_map/ppermute | solution.py:30
  58.2 5.2 %collective-permute-start.8 = (f32[3,16,256]{2,1,0:T(8,128)S(1)}, f32[3,16,256]{2,1,0:T(8,128)S(1)}, u32[]{:S(2)}, u32[]{:S(2)}) collective-permute-start(f32[3,16,256]{2,1,0:T(8,128)S(1)} %pad_maximum_fusion.19), channel_id=1, source_target_pairs={{0,4},{4,8},{8,12},{1,5},{5,9},{9,13},{2,6},{6,10},{10,14},{3,7},{... | collective-permute-start | bytes 147464 | tf_op jit(solution)/shard_map/ppermute | solution.py:30
  63.5 4.8 %collective-permute-start.10 = (f32[20,2,256]{2,1,0:T(2,128)S(1)}, f32[20,2,256]{2,1,0:T(2,128)S(1)}, u32[]{:S(2)}, u32[]{:S(2)}) collective-permute-start(f32[20,2,256]{2,1,0:T(2,128)S(1)} %get-tuple-element.39), channel_id=1, source_target_pairs={{0,1},{1,2},{2,3},{4,5},{5,6},{6,7},{8,9},{9,10},{10,11},{12,13},{... | collective-permute-start | bytes 122888 | tf_op jit(solution)/shard_map/ppermute | solution.py:21
  66.4 5.3 %collective-permute-start.11 = (f32[20,2,256]{2,1,0:T(2,128)S(1)}, f32[20,2,256]{2,1,0:T(2,128)S(1)}, u32[]{:S(2)}, u32[]{:S(2)}) collective-permute-start(f32[20,2,256]{2,1,0:T(2,128)S(1)} %get-tuple-element.40), channel_id=1, source_target_pairs={{1,0},{2,1},{3,2},{5,4},{6,5},{7,6},{9,8},{10,9},{11,10},{13,12},{... | collective-permute-start | bytes 122888 | tf_op jit(solution)/shard_map/ppermute | solution.py:22

commit v9 on v8

--- a/solution.py
+++ b/solution.py
@@ -107,6 +107,14 @@
     return field_ext
 
 
+def shifted(array, axis, step):
+    zero = jnp.zeros_like(lax.slice_in_dim(array, 0, 1, axis=axis))
+    size = array.shape[axis]
+    if step > 0:
+        return jnp.concatenate([lax.slice_in_dim(array, 1, size, axis=axis), zero], axis=axis)
+    return jnp.concatenate([zero, lax.slice_in_dim(array, 0, size - 1, axis=axis)], axis=axis)
+
+
 def body(permeability, source, pressure, aggregate):
     width_x, width_y, depth_cells = permeability.shape
     slab_index = lax.axis_index("slab")
@@ -115,9 +123,8 @@
     row_count = lax.axis_size(("pencil", "sub"))
     total_x = width_x * slab_count
     total_y = width_y * row_count
-    sides = (("slab", 0), (("pencil", "sub"), 1))
     stacked_sides = (("slab", 1), (("pencil", "sub"), 2))
-    fine_rim = NU + 1
+    fine_rim = 2 * NU
     ext_all = padded(jnp.stack([permeability, source, pressure]), stacked_sides, fine_rim)
     perm_ext = ext_all[0]
     source_ext = crop(ext_all[1], 1)
@@ -128,23 +135,41 @@
     faces_ext = geometry(perm_ext, glob_x, glob_y, inside_x, inside_y, total_x, total_y)
     smooth_ext = sweeps(ext_all[2], source_ext, faces_ext, NU, width_x)
     faces_zero = tuple(crop(member, fine_rim - 1) for member in faces_ext)
-    pressure = crop(smooth_ext, 1)
-    center, product = apply_fine(smooth_ext, faces_zero)
+    center, product = apply_fine(crop(smooth_ext, NU - 1), faces_zero)
     residual = source - product
     half_y = width_y // 2
     half_z = depth_cells // 2
 
     plane_count = aggregate.shape[0]
-    ext_pos = slab_index * width_x - 1 + jnp.arange(width_x + 1 + NU)
-    pick_ids = ext_pos[:, None] == jnp.arange(plane_count)[None, :]
-    ext_ids = jnp.sum(jnp.where(pick_ids, aggregate.astype(jnp.float32)[None, :], 0.0), axis=1)
-    local_ids = ext_ids[1 : width_x + 1]
-    straddles = (slab_index > 0) & (ext_ids[0] == local_ids[0])
+    agg_f = aggregate.astype(jnp.float32)
+    plane_range = jnp.arange(plane_count)
+
+    def ids_at(positions):
+        pick = positions[:, None] == plane_range[None, :]
+        return jnp.sum(jnp.where(pick, agg_f[None, :], 0.0), axis=1)
+
+    ext_pos = slab_index * width_x - NU + jnp.arange(width_x + 2 * NU)
+    ext_ids = ids_at(ext_pos)
+    local_ids = ext_ids[NU : NU + width_x]
+    straddles = (slab_index > 0) & (ext_ids[NU - 1] == local_ids[0])
     first_id = local_ids[0] + straddles.astype(jnp.float32)
     count_live = local_ids[-1] - first_id + 1
     slot_ids = local_ids - first_id
-    has_next = ext_pos[2 : width_x + 2] < plane_count
-    crossing = ((local_ids != ext_ids[2 : width_x + 2]) & has_next).astype(jnp.float32)
+    has_next = ext_pos[NU + 1 : NU + 1 + width_x] < plane_count
+    crossing = ((local_ids != ext_ids[NU + 1 : NU + 1 + width_x]) & has_next).astype(jnp.float32)
+    side_pos = jnp.stack(
+        [
+            (slab_index - 1) * width_x - 1,
+            (slab_index - 1) * width_x,
+            slab_index * width_x - 1,
+            (slab_index + 1) * width_x + width_x - 1,
+        ]
+    )
+    side_ids = ids_at(side_pos)
+    prev_first = side_ids[1] + ((slab_index > 1) & (side_ids[0] == side_ids[1])).astype(jnp.float32)
+    count_prev = side_ids[2] - prev_first + 1
+    count_next = side_ids[3] - (local_ids[-1] + 1) + 1
+
     face_east = faces_zero[1]
     face_north = faces_zero[3]
     face_above = faces_zero[5]
@@ -168,9 +193,6 @@
             z_sum(boundary, pair_z),
         ]
     )
-    index_y = np.arange(width_y)[:, None]
-    coarse_y = np.arange(half_y)[None, :]
-    pair_y = jnp.asarray((index_y // 2 == coarse_y).astype(np.float32))
     row_y = np.tile(np.arange(width_y), width_x)
     col_slot = np.repeat(np.arange(width_x + 1), half_y)
     col_y = np.tile(np.arange(half_y), width_x + 1)
@@ -178,7 +200,6 @@
     same_slot = row_slot[:, None] == jnp.asarray(col_slot.astype(np.float32))[None, :]
     pair_rows = row_y[:, None] // 2 == col_y[None, :]
     odd_rows = row_y[:, None] == 2 * col_y[None, :] + 1
-    spread_map = (same_slot & pair_rows).astype(jnp.float32)
     gather_map = (same_slot.T & pair_rows.T).astype(jnp.float32)
     north_gather = (same_slot.T & odd_rows.T).astype(jnp.float32)
     paired = jnp.dot(
@@ -196,90 +217,93 @@
     coarse = slot_sums[:, 1:]
     edge_sums = slot_sums[:, 0]
     slot_range = jnp.arange(width_x)
+
+    def pick_slots(first_slot, count):
+        chosen = slot_range[None, :] == first_slot + jnp.arange(count)[:, None]
+        return jnp.einsum(
+            "ks,qsjl->qkjl", chosen.astype(jnp.float32), coarse, precision=lax.Precision.HIGHEST
+        )
+
+    low_rim = NCS + NU
+    up_one = jnp.concatenate([pick_slots(count_live - low_rim, low_rim), edge_sums[:, None]], axis=1)
+    up_two = pick_slots(count_live - NU, NU)
+    down_one = jnp.concatenate([coarse[:, :NCS], edge_sums[:, None]], axis=1)
+    down_two = edge_sums
+    up_one, up_two, down_one, down_two = lax.optimization_barrier((up_one, up_two, down_one, down_two))
+    from_prev = passed_along(up_one, "slab", 1)
+    from_prev_two = passed_along(up_two, "slab", 2)
+    from_next = passed_along(down_one, "slab", -1)
+    from_next_two = passed_along(down_two, "slab", -2)
     last_slot = (slot_range == count_live - 1).astype(jnp.float32)
-    tail_pick = (slot_range[None, :] == count_live - NCS + jnp.arange(NCS)[:, None]).astype(jnp.float32)
-    tail_planes = jnp.einsum("ks,qsjl->qkjl", tail_pick, coarse, precision=lax.Precision.HIGHEST)
-    head_planes = jnp.concatenate([coarse[:, :NCS], edge_sums[:, None]], axis=1)
-    tail_planes, head_planes = lax.optimization_barrier((tail_planes, head_planes))
-    from_prev = passed_along(tail_planes, "slab", 1)
-    from_next = passed_along(head_planes, "slab", -1)
     coarse = coarse + from_next[:, NCS][:, None] * last_slot[None, :, None, None]
-    prev_last = (jnp.arange(NCS) == NCS - 1).astype(jnp.float32)
-    from_prev = from_prev + edge_sums[:, None] * prev_last[None, :, None, None]
-    x_ext = jnp.concatenate([from_prev, coarse, jnp.zeros_like(tail_planes)], axis=1)
-    wide_range = jnp.arange(width_x + 2 * NCS)[:, None]
-    place = (wide_range == NCS + count_live + jnp.arange(NCS)[None, :]).astype(jnp.float32)
-    x_ext = x_ext + jnp.einsum("tk,qkjl->qtjl", place, from_next[:, :NCS], precision=lax.Precision.HIGHEST)
-    coarse_rim = NCS
-    coef_ext = padded(x_ext, ((("pencil", "sub"), 2),), coarse_rim)
-    coarse_corr = jnp.zeros((width_x + 2 * NCS, half_y + 2 * NCS, half_z), jnp.float32)
+    prev_last = (jnp.arange(NU) == NU - 1).astype(jnp.float32)
+    before_prev = from_prev_two + from_prev[:, low_rim][:, None] * prev_last[None, :, None, None]
+    rim_range = jnp.arange(low_rim)[:, None]
+    from_before = (jnp.arange(NU)[None, :] == rim_range - (low_rim - NU) + count_prev) & (
+        rim_range < low_rim - count_prev
+    )
+    low_part = from_prev[:, :low_rim] + jnp.einsum(
+        "kj,qjyl->qkyl", from_before.astype(jnp.float32), before_prev, precision=lax.Precision.HIGHEST
+    )
+    own_fix = (jnp.arange(low_rim) == low_rim - 1).astype(jnp.float32)
+    low_part = low_part + edge_sums[:, None] * own_fix[None, :, None, None]
+    next_last = (jnp.arange(NCS) == count_next - 1).astype(jnp.float32)
+    high_part = from_next[:, :NCS] + from_next_two[:, None] * next_last[None, :, None, None]
+    x_ext = jnp.concatenate([low_part, coarse, jnp.zeros_like(high_part)], axis=1)
+    wide_range = jnp.arange(low_rim + width_x + NCS)[:, None]
+    place = (wide_range == low_rim + count_live + jnp.arange(NCS)[None, :]).astype(jnp.float32)
+    x_ext = x_ext + jnp.einsum("tk,qkjl->qtjl", place, high_part, precision=lax.Precision.HIGHEST)
+    y_rim = NCS + 1
+    coef_ext = padded(x_ext, ((("pencil", "sub"), 2),), y_rim)
+    coarse_rhs = coef_ext[0]
+    coarse_east = coef_ext[1]
+    coarse_north = coef_ext[2]
+    coarse_above = coef_ext[3]
+    coarse_bound = coef_ext[4]
+    coarse_west = shifted(coarse_east, 0, -1)
+    coarse_south = shifted(coarse_north, 1, -1)
+    coarse_below = shifted(coarse_above, 2, -1)
+    diag_coarse = (
+        coarse_east
+        + coarse_west
+        + coarse_north
+        + coarse_south
+        + coarse_above
+        + coarse_below
+        + coarse_bound
+    )
+    safe_coarse = jnp.where(diag_coarse > 0, diag_coarse, 1.0)
+    coarse_corr = jnp.zeros_like(coarse_rhs)
     for sweep_index in range(NCS):
-        out_rim = NCS - 1 - sweep_index
-        start_at = coarse_rim - out_rim
-        size_x = width_x + 2 * out_rim
-        size_y = half_y + 2 * out_rim
-
-        def region(offset_x, offset_y):
-            return coef_ext[
-                :,
-                start_at + offset_x : start_at + offset_x + size_x,
-                start_at + offset_y : start_at + offset_y + size_y,
-            ]
-
-        here_coef = region(0, 0)
-        coarse_rhs = here_coef[0]
-        coarse_east = here_coef[1]
-        coarse_north = here_coef[2]
-        coarse_above = here_coef[3]
-        coarse_bound = here_coef[4]
-        coarse_west = region(-1, 0)[1]
-        coarse_south = region(0, -1)[2]
-        zero_plane = jnp.zeros_like(coarse_above[:, :, :1])
-        coarse_below = jnp.concatenate([zero_plane, coarse_above[:, :, :-1]], axis=2)
-        diag_coarse = (
-            coarse_east
-            + coarse_west
-            + coarse_north
-            + coarse_south
-            + coarse_above
-            + coarse_below
-            + coarse_bound
-        )
-        safe_coarse = jnp.where(diag_coarse > 0, diag_coarse, 1.0)
-        coarse_center = coarse_corr[1:-1, 1:-1]
-        above_vals = jnp.concatenate([coarse_center[:, :, 1:], zero_plane], axis=2)
-        below_vals = jnp.concatenate([zero_plane, coarse_center[:, :, :-1]], axis=2)
-        beside_all = coarse_east * coarse_corr[2:, 1:-1] + coarse_west * coarse_corr[:-2, 1:-1]
+        beside_all = coarse_east * shifted(coarse_corr, 0, 1) + coarse_west * shifted(coarse_corr, 0, -1)
         beside_all = (
             beside_all
-            + coarse_north * coarse_corr[1:-1, 2:]
-            + coarse_south * coarse_corr[1:-1, :-2]
+            + coarse_north * shifted(coarse_corr, 1, 1)
+            + coarse_south * shifted(coarse_corr, 1, -1)
         )
-        beside_all = beside_all + coarse_above * above_vals + coarse_below * below_vals
+        beside_all = (
+            beside_all
+            + coarse_above * shifted(coarse_corr, 2, 1)
+            + coarse_below * shifted(coarse_corr, 2, -1)
+        )
         coarse_corr = (
-            coarse_center
-            + OMEGA * (coarse_rhs - (diag_coarse * coarse_center - beside_all)) / safe_coarse
+            coarse_corr
+            + OMEGA * (coarse_rhs - (diag_coarse * coarse_corr - beside_all)) / safe_coarse
         )
-    last_corr = jnp.sum(last_slot[:, None, None] * coarse_corr, axis=0)
-    corr_wide = jnp.concatenate([jnp.zeros_like(last_corr)[None], coarse_corr], axis=0)
+    span = width_x + 2 * NU
+    coarse_rows = coarse_corr.shape[1]
+    coarse_planes = coarse_corr.shape[0]
     corr_z = jnp.dot(
-        corr_wide.reshape((width_x + 1) * half_y, half_z), pair_z.T, precision=lax.Precision.HIGHEST
-    )
-    correction = jnp.dot(spread_map, corr_z, precision=lax.Precision.HIGHEST)
-    base = pressure + correction.reshape(width_x, width_y, depth_cells)
-    last_z = jnp.dot(last_corr, pair_z.T, precision=lax.Precision.HIGHEST)
-    last_fine = jnp.dot(pair_y, last_z, precision=lax.Precision.HIGHEST)
-    up_block = jnp.concatenate([base[width_x - NU :], last_fine[None]], axis=0)
-    below_prev = passed_along(up_block, "slab", 1)
-    above_next = passed_along(base[:NU], "slab", -1)
-    from_owner = (slot_ids == -1).astype(jnp.float32)
-    own = base + from_owner[:, None, None] * below_prev[NU][None]
-    next_ids = ext_ids[width_x + 1 :]
-    next_in = ext_pos[width_x + 1 :] < plane_count
-    to_owner = ((next_ids == local_ids[-1]) & next_in).astype(jnp.float32)
-    high_halo = above_next + to_owner[:, None, None] * last_fine[None]
-    post_x = jnp.concatenate([below_prev[:NU], own, high_halo], axis=0)
-    post_ext = padded(post_x, ((("pencil", "sub"), 1),), NU)
+        coarse_corr.reshape(coarse_planes * coarse_rows, half_z), pair_z.T, precision=lax.Precision.HIGHEST
+    )
+    fine_rows = np.tile(np.arange(span) - NU, span)
+    col_plane = np.repeat(np.arange(coarse_planes), coarse_rows)
+    col_row = np.tile(np.arange(coarse_rows), coarse_planes)
+    row_match = (fine_rows[:, None] // 2 + y_rim) == col_row[None, :]
+    plane_slot = jnp.repeat(ext_ids - first_id + low_rim, span)
+    spread_map = (plane_slot[:, None] == jnp.asarray(col_plane.astype(np.float32))[None, :]) & row_match
+    correction = jnp.dot(spread_map.astype(jnp.float32), corr_z, precision=lax.Precision.HIGHEST)
+    post_ext = smooth_ext + correction.reshape(span, span, depth_cells)
     return sweeps(post_ext, source_ext, faces_ext, NU, width_x)
 
 

time: 74.6 us -> 86.2 us (1.16)
  local copies, waits for them, and re-layouts: 3.57 us -> 10.8 us
  between operations: 3.21 us -> 6.88 us
  matrix products: 4.33 us -> 7.93 us
  starting transfers between devices: 32 us -> 28.9 us
  other arithmetic: 11.1 us -> 14.1 us
  waiting for transfers between devices: 19.8 us -> 16.9 us
    dot_general x6, matrix products: 1.67 us -> 5.27 us  [the longest x1 2.33 us: body(): jnp.dot(spread_map.astype(jnp.float32), corr_z, precision=lax.Precision.H...]
    reshape x0 -> x2, local copies, waits for them, and re-layouts: none -> 3.49 us  [the longest x1 1.81 us: body(): post_ext = smooth_ext + correction.reshape(span, span, depth_cells)]
    ppermute x4 -> x3, waiting for transfers between devices: 12.2 us -> 8.8 us  [padded(): after = lax.ppermute(leading, axis, down)]
    ppermute x4 -> x3, starting transfers between devices: 14.7 us -> 11.7 us  [padded(): before = lax.ppermute(last, axis, up)]
    ppermute x4 -> x3, waiting for transfers between devices: 1.87 us -> 4.53 us  [padded(): before = lax.ppermute(last, axis, up)]
    ppermute x4, waiting for transfers between devices: 5.75 us -> 3.58 us  [passed_along(): return lax.ppermute(array, axis, pairs)]
    add x9 -> x10, other arithmetic: 0.86 us -> 2.72 us  [the longest x3 1.6 us: body(): coarse_corr + OMEGA * (coarse_rhs - (diag_coarse * coarse_corr - beside_a...]
    ppermute x4 -> x3, starting transfers between devices: 7.05 us -> 5.31 us  [padded(): after = lax.ppermute(leading, axis, down)]
  transfers between devices with their start and end apart: 12 -> 10, of which waited for: 8 -> 5; matrix products, arithmetic and copies ran while one was open for 5% -> 5% of each run, Pallas kernels for 0% -> 0%
where the time goes in v9:
time: 86.2 us; the launch traced here: 85.5 us
  starting transfers between devices  28.9 us (34%)
  waiting for transfers between devices  16.9 us (20%)
  other arithmetic  14.1 us (16%)
  local copies, waits for them, and re-layouts  10.8 us (13%)
  matrix products  7.93 us (9%)
  between operations  6.88 us (8%)
    ppermute x4, starting transfers between devices, passed_along(): return lax.ppermute(array, axis, pairs)  11.9 us
    ppermute x3, starting transfers between devices, padded(): before = lax.ppermute(last, axis, up)  11.7 us
    ppermute x3, waiting for transfers between devices, padded(): after = lax.ppermute(leading, axis, down)  8.8 us
    ppermute x3, starting transfers between devices, padded(): after = lax.ppermute(leading, axis, down)  5.31 us
    ppermute x3, waiting for transfers between devices, padded(): before = lax.ppermute(last, axis, up)  4.53 us
    add x4, other arithmetic, sweeps(): field_ext = center + OMEGA * (source_now - product) / faces_now[7]  3.78 us
    ppermute x4, waiting for transfers between devices, passed_along(): return lax.ppermute(array, axis, pairs)  3.58 us
    slice x2, other arithmetic, padded(): last = lax.slice_in_dim(array, length - width, length, axis=dim)  2.41 us
  transfers between devices with their start and end apart: 10, of which 5 were waited for; matrix products, arithmetic and copies ran while one was open for 5% of the time, Pallas kernels for 0%

profile of v9, /device:TPU:1, one launch (start us, length us, event | category | flops | bytes accessed | tf_op | source)
XLA Modules:
  0.0 85.5 jit_solution(13574138458811484417)
XLA Ops:
  0.0 1.1 %pad_maximum_fusion.9 = (f32[3,4,16,256]{3,2,1,0:T(8,128)S(1)}, f32[3,4,16,256]{3,2,1,0:T(8,128)S(1)}) fusion(f32[1,16,16,256]{3,2,1,0:T(8,128)} %bitcast.161, f32[1,16,16,256]{3,2,1,0:T(8,128)} %bitcast.158, f32[1,16,16,256]{3,2,1,0:T(8,128)} %bitcast.164), kind=kLoop, calls=%fused_computation.129 | loop fusion | flops 196608 | bytes 1179648 | tf_op jit(solution)/shard_map/slice | solution.py:19
  1.1 4.0 %collective-permute-start = (f32[3,4,16,256]{3,2,1,0:T(8,128)S(1)}, f32[3,4,16,256]{3,2,1,0:T(8,128)S(1)}, u32[]{:S(2)}, u32[]{:S(2)}) collective-permute-start(f32[3,4,16,256]{3,2,1,0:T(8,128)S(1)} %get-tuple-element.25), channel_id=1, source_target_pairs={{0,4},{4,8},{8,12},{1,5},{5,9},{9,13},{2,6},{6,10},{10,14},{3,7},{... | collective-permute-start | bytes 589832 | tf_op jit(solution)/shard_map/ppermute | solution.py:21
  5.2 1.3 %collective-permute-start.1 = (f32[3,4,16,256]{3,2,1,0:T(8,128)S(1)}, f32[3,4,16,256]{3,2,1,0:T(8,128)S(1)}, u32[]{:S(2)}, u32[]{:S(2)}) collective-permute-start(f32[3,4,16,256]{3,2,1,0:T(8,128)S(1)} %get-tuple-element.26), channel_id=1, source_target_pairs={{4,0},{8,4},{12,8},{5,1},{9,5},{13,9},{6,2},{10,6},{14,10},{7,3},{... | collective-permute-start | bytes 589832 | tf_op jit(solution)/shard_map/ppermute | solution.py:22
  7.2 0.7 convert_element_type.158
  7.8 0.2 select_reduce_fusion
  8.0 0.7 fusion.123
  11.4 0.2 select_reduce_fusion.1
  11.6 0.7 fusion.122
  16.3 1.3 %pad_maximum_fusion.6 = (f32[3,24,4,256]{3,2,1,0:T(4,128)S(1)}, f32[3,24,4,256]{3,2,1,0:T(4,128)S(1)}) fusion(f32[3,4,16,256]{3,2,1,0:T(8,128)S(1)} %collective-permute-done.1, f32[3,4,16,256]{3,2,1,0:T(8,128)S(1)} %collective-permute-done, f32[1,16,16,256]{3,2,1,0:T(8,128)} %bitcast.162, f32[1,16,16,256]{3,2,1,0:T(8,128)} %bitcast.159, ...), kind=kLoop, calls=%fused_computation.89 | loop fusion | flops 589824 | bytes 1769472 | tf_op jit(solution)/shard_map/slice | solution.py:19
  17.6 4.0 %collective-permute-start.2 = (f32[3,24,4,256]{3,2,1,0:T(4,128)S(1)}, f32[3,24,4,256]{3,2,1,0:T(4,128)S(1)}, u32[]{:S(2)}, u32[]{:S(2)}) collective-permute-start(f32[3,24,4,256]{3,2,1,0:T(4,128)S(1)} %get-tuple-element.23), channel_id=1, source_target_pairs={{0,1},{1,2},{2,3},{4,5},{5,6},{6,7},{8,9},{9,10},{10,11},{12,13},{... | collective-permute-start | bytes 884744 | tf_op jit(solution)/shard_map/ppermute | solution.py:21
  21.6 1.9 %collective-permute-start.3 = (f32[3,24,4,256]{3,2,1,0:T(4,128)S(1)}, f32[3,24,4,256]{3,2,1,0:T(4,128)S(1)}, u32[]{:S(2)}, u32[]{:S(2)}) collective-permute-start(f32[3,24,4,256]{3,2,1,0:T(4,128)S(1)} %get-tuple-element.24), channel_id=1, source_target_pairs={{1,0},{2,1},{3,2},{5,4},{6,5},{7,6},{9,8},{10,9},{11,10},{13,12},{... | collective-permute-start | bytes 884744 | tf_op jit(solution)/shard_map/ppermute | solution.py:22
  23.6 1.6 %collective-permute-done.2 = f32[3,24,4,256]{3,2,1,0:T(4,128)S(1)} collective-permute-done((f32[3,24,4,256]{3,2,1,0:T(4,128)S(1)}, f32[3,24,4,256]{3,2,1,0:T(4,128)S(1)}, u32[]{:S(2)}, u32[]{:S(2)}) %collective-permute-start.2) | collective-permute-done | bytes 294944 | tf_op jit(solution)/shard_map/ppermute | solution.py:21
  25.3 4.4 %collective-permute-done.3 = f32[3,24,4,256]{3,2,1,0:T(4,128)S(1)} collective-permute-done((f32[3,24,4,256]{3,2,1,0:T(4,128)S(1)}, f32[3,24,4,256]{3,2,1,0:T(4,128)S(1)}, u32[]{:S(2)}, u32[]{:S(2)}) %collective-permute-start.3) | collective-permute-done | bytes 294944 | tf_op jit(solution)/shard_map/ppermute | solution.py:22
  29.7 0.3 pad_maximum_fusion
  30.1 0.2 fusion.107
  30.3 0.2 divide_select_fusion
  30.5 0.2 divide_select_fusion.1
  30.7 0.2 fusion.108
  30.9 0.2 divide_select_fusion.2
  31.2 1.1 %fusion.11 = (f32[22,22,256]{2,1,0:T(8,128)S(1)}, f32[22,22,256]{2,1,0:T(8,128)S(1)}, f32[22,22,256]{2,1,0:T(8,128)S(1)}) fusion(f32[24,24,256]{2,1,0:T(8,128)S(1)} %get-tuple-element.20, f32[24,24,256]{2,1,0:T(8,128)S(1)} %get-tuple-element.19, f32[22,22,255]{2,1,0:T(8,128)S(1)} %get-tuple-element.34, f32[22,22,255]{2,1,0:T(8,128)S(1)} %get-tuple-element.33, ...), kind=kLoop, calls=%fused_computation.27 | loop fusion | flops 3345408 | bytes 8423108 | tf_op jit(solution)/shard_map/add | solution.py:106
  32.2 0.2 fusion.109
  32.5 0.8 fusion.30
  33.5 0.5 fusion.106
  34.0 0.4 copy-done.3
  34.4 0.4 fusion.124
  34.8 0.4 fusion.125
  35.2 0.4 fusion.127
  35.6 0.4 fusion.126
  36.1 0.4 fusion.15
  36.6 0.4 fusion.128
  37.0 0.3 convolution_bitcast_fusion.3
  37.4 0.3 convolution_bitcast_fusion.2
  37.7 0.3 convolution_bitcast_fusion.4
  38.0 1.3 %collective-permute-start.6 = (f32[5,5,8,128]{3,1,2,0:T(8,128)S(1)}, f32[5,5,8,128]{3,1,2,0:T(8,128)S(1)}, u32[]{:S(2)}, u32[]{:S(2)}) collective-permute-start(f32[5,5,8,128]{3,1,2,0:T(8,128)S(1)} %pad_maximum_fusion.11), channel_id=1, source_target_pairs={{4,0},{8,4},{12,8},{5,1},{9,5},{13,9},{6,2},{10,6},{14,10},{7,3},{... | collective-permute-start | bytes 307208 | tf_op jit(solution)/shard_map/ppermute | solution.py:30
  39.3 4.9 %collective-permute-start.4 = (f32[5,7,8,128]{3,1,2,0:T(8,128)S(1)}, f32[5,7,8,128]{3,1,2,0:T(8,128)S(1)}, u32[]{:S(2)}, u32[]{:S(2)}) collective-permute-start(f32[5,7,8,128]{3,1,2,0:T(8,128)S(1)} %pad_maximum_fusion.10), channel_id=1, source_target_pairs={{0,4},{4,8},{8,12},{1,5},{5,9},{9,13},{2,6},{6,10},{10,14},{3,7},{... | collective-permute-start | bytes 430088 | tf_op jit(solution)/shard_map/ppermute | solution.py:30
  44.2 4.4 %collective-permute-start.5 = (f32[5,2,8,128]{3,1,2,0:T(2,128)S(1)}, f32[5,2,8,128]{3,1,2,0:T(2,128)S(1)}, u32[]{:S(2)}, u32[]{:S(2)}) collective-permute-start(f32[5,2,8,128]{3,1,2,0:T(2,128)S(1)} %convolution_bitcast_fusion.4), channel_id=1, source_target_pairs={{0,8},{4,12},{1,9},{5,13},{2,10},{6,14},{3,11},{7,15},{16,24},{20,... | collective-permute-start | bytes 122888 | tf_op jit(solution)/shard_map/ppermute | solution.py:30
  48.6 1.3 %collective-permute-start.7 = (f32[5,8,128]{2,1,0:T(8,128)S(1)}, f32[5,8,128]{2,1,0:T(8,128)S(1)}, u32[]{:S(2)}, u32[]{:S(2)}) collective-permute-start(f32[5,8,128]{2,1,0:T(8,128)S(1)} %bitcast.172), channel_id=1, source_target_pairs={{8,0},{12,4},{9,1},{13,5},{10,2},{14,6},{11,3},{15,7},{24,16},{28,... | collective-permute-start | bytes 61448 | tf_op jit(solution)/shard_map/ppermute | solution.py:30
  50.1 0.3 fusion.68
  50.5 3.6 %collective-permute-done.7 = f32[5,8,128]{2,1,0:T(8,128)S(1)} collective-permute-done((f32[5,8,128]{2,1,0:T(8,128)S(1)}, f32[5,8,128]{2,1,0:T(8,128)S(1)}, u32[]{:S(2)}, u32[]{:S(2)}) %collective-permute-start.7) | collective-permute-done | bytes 20512 | tf_op jit(solution)/shard_map/ppermute | solution.py:30
  54.0 0.6 fusion
  54.6 0.8 copy-done
  55.4 1.0 %fusion.105 = (f32[5,26,5,128]{3,1,2,0:T(8,128)}, f32[5,26,5,128]{3,1,2,0:T(8,128)}) fusion(f32[5,26,8,128]{3,1,2,0:T(8,128)S(1)} %fusion), kind=kLoop, calls=%fused_computation.217 | loop fusion | bytes 1331200 | tf_op jit(solution)/shard_map/slice | solution.py:19
  56.4 3.7 %collective-permute-start.8 = (f32[5,26,5,128]{3,1,2,0:T(8,128)}, f32[5,26,5,128]{3,1,2,0:T(8,128)}, u32[]{:S(2)}, u32[]{:S(2)}) collective-permute-start(f32[5,26,5,128]{3,1,2,0:T(8,128)} %get-tuple-element.27), channel_id=1, source_target_pairs={{0,1},{1,2},{2,3},{4,5},{5,6},{6,7},{8,9},{9,10},{10,11},{12,13},{... | collective-permute-start | bytes 998408 | tf_op jit(solution)/shard_map/ppermute | solution.py:21
  60.2 2.1 %collective-permute-start.9 = (f32[5,26,5,128]{3,1,2,0:T(8,128)}, f32[5,26,5,128]{3,1,2,0:T(8,128)}, u32[]{:S(2)}, u32[]{:S(2)}) collective-permute-start(f32[5,26,5,128]{3,1,2,0:T(8,128)} %get-tuple-element.28), channel_id=1, source_target_pairs={{1,0},{2,1},{3,2},{5,4},{6,5},{7,6},{9,8},{10,9},{11,10},{13,12},{... | collective-permute-start | bytes 998408 | tf_op jit(solution)/shard_map/ppermute | solution.py:22
  62.5 2.9 %collective-permute-done.8 = f32[5,26,5,128]{3,1,2,0:T(8,128)} collective-permute-done((f32[5,26,5,128]{3,1,2,0:T(8,128)}, f32[5,26,5,128]{3,1,2,0:T(8,128)}, u32[]{:S(2)}, u32[]{:S(2)}) %collective-permute-start.8) | collective-permute-done | bytes 332832 | tf_op jit(solution)/shard_map/ppermute | solution.py:21
  65.4 4.4 %collective-permute-done.9 = f32[5,26,5,128]{3,1,2,0:T(8,128)} collective-permute-done((f32[5,26,5,128]{3,1,2,0:T(8,128)}, f32[5,26,5,128]{3,1,2,0:T(8,128)}, u32[]{:S(2)}, u32[]{:S(2)}) %collective-permute-start.9) | collective-permute-done | bytes 332832 | tf_op jit(solution)/shard_map/ppermute | solution.py:22
  69.8 1.4 %pad_maximum_fusion.1 = f32[5,26,18,128]{3,1,2,0:T(8,128)S(1)} fusion(f32[5,26,5,128]{3,1,2,0:T(8,128)} %collective-permute-done.9, f32[5,26,8,128]{3,1,2,0:T(8,128)} %copy-done, f32[5,26,5,128]{3,1,2,0:T(8,128)} %collective-permute-done.8), kind=kLoop, calls=%fused_computation.1 | loop fusion | flops 599040 | bytes 2396160 | tf_op jit(solution)/shard_map/concatenate | solution.py:23
  71.3 0.3 fusion.48
  71.7 0.1 fusion.121
  71.9 0.5 divide_add_fusion.2
  72.5 0.1 fusion.118
  72.7 0.5 divide_add_fusion.1
  73.3 0.1 fusion.115
  73.5 0.5 divide_add_fusion
  74.0 0.9 %copy.28 = f32[26,18,128]{2,1,0:T(8,128)} copy(f32[26,18,128]{2,0,1:T(8,128)S(1)} %divide_add_fusion) | data formatting | bytes 479232 | tf_op jit(solution)/shard_map/add | solution.py:290
  74.9 1.7 %reshape.295 = f32[468,128]{1,0:T(8,128)} reshape(f32[26,18,128]{2,1,0:T(8,128)} %copy.28) | data formatting | bytes 479232 | tf_op jit(solution)/shard_map/reshape | solution.py:297
  76.6 1.5 %fusion.129 = f32[468,256]{1,0:T(8,128)S(1)} fusion(f32[468,128]{1,0:T(8,128)} %reshape.295, f32[256,128]{1,0:T(8,128)S(1)} %copy-done.3), kind=kOutput, calls=%fused_computation.241 | convolution fusion | flops 184025088 | bytes 849920 | tf_op jit(solution)/shard_map/dot_general | solution.py:296
  78.1 2.3 %fusion.1 = f32[400,256]{1,0:T(8,128)} fusion(f32[468,256]{1,0:T(8,128)S(1)} %fusion.129, pred[400,468]{1,0:T(8,128)(4,1)} %constant.108.clone, f32[468]{0:T(512)S(1)} %copy-done.8, f32[400]{0:T(512)S(1)} %eq.193), kind=kOutput, calls=%fused_computation.9 | convolution fusion | flops 575452800 | bytes 1079504 | tf_op jit(solution)/shard_map/dot_general | solution.py:305
  80.4 1.8 %reshape.296 = f32[20,20,256]{2,1,0:T(8,128)} reshape(f32[400,256]{1,0:T(8,128)} %fusion.1) | data formatting | bytes 819200 | tf_op jit(solution)/shard_map/reshape | solution.py:306
  82.2 1.1 %add.558 = f32[20,20,256]{2,1,0:T(8,128)S(1)} add(f32[20,20,256]{2,1,0:T(8,128)S(1)} %fusion.30, f32[20,20,256]{2,1,0:T(8,128)} %reshape.296) | non-fusion elementwise | flops 102400 | bytes 1228800 | tf_op jit(solution)/shard_map/add | solution.py:306
  83.3 0.2 fusion.110
  83.5 0.7 fusion.40
  84.2 0.1 fusion.112
  84.4 1.1 %fusion.58 = f32[16,16,256]{2,1,0:T(8,128)} fusion(f32[18,18,256]{2,1,0:T(8,128)S(1)} %fusion.40, f32[24,24,256]{2,1,0:T(8,128)S(1)} %get-tuple-element.19, f32[16,16,255]{2,1,0:T(8,128)S(1)} %get-tuple-element.44, f32[16,16,255]{2,1,0:T(8,128)S(1)} %get-tuple-element.43, f32[24,23,256]{2,1,0:T(8,128)S(1)} %divide_select_fusion, ...), kind=kLoop, calls=%fused_computation.108 | loop fusion | flops 1114112 | bytes 4161648 | tf_op jit(solution)/shard_map/add | solution.py:106
  (87 shorter events, 2.6 us)
Async XLA Ops:
  0.0 29.7 %copy-start.5 = (f32[16,16,256]{2,1,0:T(8,128)S(1)}, f32[16,16,256]{2,1,0:T(8,128)}, u32[]{:S(2)}) copy-start(f32[16,16,256]{2,1,0:T(8,128)} %param.11) | copy-start | bytes 786436
  0.0 29.7 %copy-start.1 = (f32[16,16,256]{2,1,0:T(8,128)S(1)}, f32[16,16,256]{2,1,0:T(8,128)}, u32[]{:S(2)}) copy-start(f32[16,16,256]{2,1,0:T(8,128)} %param.12) | copy-start | bytes 786436
  0.0 29.7 %copy-start.4 = (f32[16,16,256]{2,1,0:T(8,128)S(1)}, f32[16,16,256]{2,1,0:T(8,128)}, u32[]{:S(2)}) copy-start(f32[16,16,256]{2,1,0:T(8,128)} %param.13) | copy-start | bytes 786436
  1.1 15.2 %collective-permute-start = (f32[3,4,16,256]{3,2,1,0:T(8,128)S(1)}, f32[3,4,16,256]{3,2,1,0:T(8,128)S(1)}, u32[]{:S(2)}, u32[]{:S(2)}) collective-permute-start(f32[3,4,16,256]{3,2,1,0:T(8,128)S(1)} %get-tuple-element.25), channel_id=1, source_target_pairs={{0,4},{4,8},{8,12},{1,5},{5,9},{9,13},{2,6},{6,10},{10,14},{3,7},{... | collective-permute-start | bytes 589832 | tf_op jit(solution)/shard_map/ppermute | solution.py:21
  5.2 11.2 %collective-permute-start.1 = (f32[3,4,16,256]{3,2,1,0:T(8,128)S(1)}, f32[3,4,16,256]{3,2,1,0:T(8,128)S(1)}, u32[]{:S(2)}, u32[]{:S(2)}) collective-permute-start(f32[3,4,16,256]{3,2,1,0:T(8,128)S(1)} %get-tuple-element.26), channel_id=1, source_target_pairs={{4,0},{8,4},{12,8},{5,1},{9,5},{13,9},{6,2},{10,6},{14,10},{7,3},{... | collective-permute-start | bytes 589832 | tf_op jit(solution)/shard_map/ppermute | solution.py:22
  17.6 7.6 %collective-permute-start.2 = (f32[3,24,4,256]{3,2,1,0:T(4,128)S(1)}, f32[3,24,4,256]{3,2,1,0:T(4,128)S(1)}, u32[]{:S(2)}, u32[]{:S(2)}) collective-permute-start(f32[3,24,4,256]{3,2,1,0:T(4,128)S(1)} %get-tuple-element.23), channel_id=1, source_target_pairs={{0,1},{1,2},{2,3},{4,5},{5,6},{6,7},{8,9},{9,10},{10,11},{12,13},{... | collective-permute-start | bytes 884744 | tf_op jit(solution)/shard_map/ppermute | solution.py:21
  21.6 8.0 %collective-permute-start.3 = (f32[3,24,4,256]{3,2,1,0:T(4,128)S(1)}, f32[3,24,4,256]{3,2,1,0:T(4,128)S(1)}, u32[]{:S(2)}, u32[]{:S(2)}) collective-permute-start(f32[3,24,4,256]{3,2,1,0:T(4,128)S(1)} %get-tuple-element.24), channel_id=1, source_target_pairs={{1,0},{2,1},{3,2},{5,4},{6,5},{7,6},{9,8},{10,9},{11,10},{13,12},{... | collective-permute-start | bytes 884744 | tf_op jit(solution)/shard_map/ppermute | solution.py:22
  32.5 1.0 %copy-start.2 = (f32[16,16,256]{2,1,0:T(8,128)S(1)}, f32[16,16,256]{2,1,0:T(8,128)}, u32[]{:S(2)}) copy-start(f32[16,16,256]{2,1,0:T(8,128)} %param.12) | copy-start | bytes 786436
  33.5 0.9 %copy-start.3 = (f32[256,128]{1,0:T(8,128)S(1)}, f32[256,128]{1,0:T(8,128)}, u32[]{:S(2)}) copy-start(f32[256,128]{1,0:T(8,128)} %constant.102.clone) | copy-start | bytes 393220
  34.0 1.6 %copy-start.6 = (f32[256,128]{1,0:T(8,128)S(1)}, f32[256,128]{1,0:T(8,128)}, u32[]{:S(2)}) copy-start(f32[256,128]{1,0:T(8,128)} %constant.103.clone) | copy-start | bytes 393220
  34.0 2.0 %copy-start.9 = (f32[136]{0:T(256)S(1)}, f32[136]{0:T(256)}, u32[]{:S(2)}) copy-start(f32[136]{0:T(256)} %constant.104.clone) | copy-start | bytes 1636
  34.0 2.0 %copy-start.10 = (pred[136,256]{1,0:T(8,128)(4,1)S(1)}, pred[136,256]{1,0:T(8,128)(4,1)}, u32[]{:S(2)}) copy-start(pred[136,256]{1,0:T(8,128)(4,1)} %constant.105.clone) | copy-start | bytes 104452
  35.2 1.8 %copy-start.7 = (pred[136,256]{1,0:T(8,128)(4,1)S(1)}, pred[136,256]{1,0:T(8,128)(4,1)}, u32[]{:S(2)}) copy-start(pred[136,256]{1,0:T(8,128)(4,1)} %constant.106.clone) | copy-start | bytes 104452
  38.0 11.9 %collective-permute-start.6 = (f32[5,5,8,128]{3,1,2,0:T(8,128)S(1)}, f32[5,5,8,128]{3,1,2,0:T(8,128)S(1)}, u32[]{:S(2)}, u32[]{:S(2)}) collective-permute-start(f32[5,5,8,128]{3,1,2,0:T(8,128)S(1)} %pad_maximum_fusion.11), channel_id=1, source_target_pairs={{4,0},{8,4},{12,8},{5,1},{9,5},{13,9},{6,2},{10,6},{14,10},{7,3},{... | collective-permute-start | bytes 307208 | tf_op jit(solution)/shard_map/ppermute | solution.py:30
  39.3 10.7 %collective-permute-start.4 = (f32[5,7,8,128]{3,1,2,0:T(8,128)S(1)}, f32[5,7,8,128]{3,1,2,0:T(8,128)S(1)}, u32[]{:S(2)}, u32[]{:S(2)}) collective-permute-start(f32[5,7,8,128]{3,1,2,0:T(8,128)S(1)} %pad_maximum_fusion.10), channel_id=1, source_target_pairs={{0,4},{4,8},{8,12},{1,5},{5,9},{9,13},{2,6},{6,10},{10,14},{3,7},{... | collective-permute-start | bytes 430088 | tf_op jit(solution)/shard_map/ppermute | solution.py:30
  44.2 5.9 %collective-permute-start.5 = (f32[5,2,8,128]{3,1,2,0:T(2,128)S(1)}, f32[5,2,8,128]{3,1,2,0:T(2,128)S(1)}, u32[]{:S(2)}, u32[]{:S(2)}) collective-permute-start(f32[5,2,8,128]{3,1,2,0:T(2,128)S(1)} %convolution_bitcast_fusion.4), channel_id=1, source_target_pairs={{0,8},{4,12},{1,9},{5,13},{2,10},{6,14},{3,11},{7,15},{16,24},{20,... | collective-permute-start | bytes 122888 | tf_op jit(solution)/shard_map/ppermute | solution.py:30
  48.6 5.4 %collective-permute-start.7 = (f32[5,8,128]{2,1,0:T(8,128)S(1)}, f32[5,8,128]{2,1,0:T(8,128)S(1)}, u32[]{:S(2)}, u32[]{:S(2)}) collective-permute-start(f32[5,8,128]{2,1,0:T(8,128)S(1)} %bitcast.172), channel_id=1, source_target_pairs={{8,0},{12,4},{9,1},{13,5},{10,2},{14,6},{11,3},{15,7},{24,16},{28,... | collective-permute-start | bytes 61448 | tf_op jit(solution)/shard_map/ppermute | solution.py:30
  54.6 0.8 copy-start
  56.4 8.9 %collective-permute-start.8 = (f32[5,26,5,128]{3,1,2,0:T(8,128)}, f32[5,26,5,128]{3,1,2,0:T(8,128)}, u32[]{:S(2)}, u32[]{:S(2)}) collective-permute-start(f32[5,26,5,128]{3,1,2,0:T(8,128)} %get-tuple-element.27), channel_id=1, source_target_pairs={{0,1},{1,2},{2,3},{4,5},{5,6},{6,7},{8,9},{9,10},{10,11},{12,13},{... | collective-permute-start | bytes 998408 | tf_op jit(solution)/shard_map/ppermute | solution.py:21
  60.2 9.6 %collective-permute-start.9 = (f32[5,26,5,128]{3,1,2,0:T(8,128)}, f32[5,26,5,128]{3,1,2,0:T(8,128)}, u32[]{:S(2)}, u32[]{:S(2)}) collective-permute-start(f32[5,26,5,128]{3,1,2,0:T(8,128)} %get-tuple-element.28), channel_id=1, source_target_pairs={{1,0},{2,1},{3,2},{5,4},{6,5},{7,6},{9,8},{10,9},{11,10},{13,12},{... | collective-permute-start | bytes 998408 | tf_op jit(solution)/shard_map/ppermute | solution.py:22
  74.0 4.1 %copy-start.8 = (f32[468]{0:T(512)S(1)}, f32[468]{0:T(512)}, u32[]{:S(2)}) copy-start(f32[468]{0:T(512)} %constant.107.clone) | copy-start | bytes 5620

commit v10 on v8

--- a/solution.py
+++ b/solution.py
@@ -118,7 +118,9 @@
     sides = (("slab", 0), (("pencil", "sub"), 1))
     stacked_sides = (("slab", 1), (("pencil", "sub"), 2))
     fine_rim = NU + 1
-    ext_all = padded(jnp.stack([permeability, source, pressure]), stacked_sides, fine_rim)
+    ext_x = padded(jnp.stack([permeability, source, pressure]), (("slab", 1),), fine_rim)
+    ext_x, aggregate = lax.optimization_barrier((ext_x, aggregate))
+    ext_all = padded(ext_x, ((("pencil", "sub"), 2),), fine_rim)
     perm_ext = ext_all[0]
     source_ext = crop(ext_all[1], 1)
     glob_x = slab_index * width_x - fine_rim + jnp.arange(width_x + 2 * fine_rim)

time: 74.6 us -> 73.2 us (0.981)
  other arithmetic: 11.1 us -> 9.24 us
    ppermute x4, waiting for transfers between devices: 12.2 us -> 13.7 us  [padded(): after = lax.ppermute(leading, axis, down)]
    slice x3 -> x2, other arithmetic: 2.35 us -> 1.04 us  [padded(): last = lax.slice_in_dim(array, length - width, length, axis=dim)]
    ppermute x4, waiting for transfers between devices: 1.87 us -> 0.7 us  [padded(): before = lax.ppermute(last, axis, up)]
  transfers between devices with their start and end apart: 12 -> 12, of which waited for: 8 -> 9; matrix products, arithmetic and copies ran while one was open for 5% -> 4% of each run, Pallas kernels for 0% -> 0%
where the time goes in v10:
time: 73.2 us; the launch traced here: 72.6 us
  starting transfers between devices  31.8 us (43%)
  waiting for transfers between devices  20.1 us (27%)
  other arithmetic  9.24 us (13%)
  matrix products  4.33 us (6%)
  local copies, waits for them, and re-layouts  3.82 us (5%)
  between operations  3.28 us (4%)
    ppermute x4, starting transfers between devices, padded(): before = lax.ppermute(last, axis, up)  15 us
    ppermute x4, waiting for transfers between devices, padded(): after = lax.ppermute(leading, axis, down)  13.7 us
    ppermute x4, starting transfers between devices, passed_along(): return lax.ppermute(array, axis, pairs)  9.81 us
    ppermute x4, starting transfers between devices, padded(): after = lax.ppermute(leading, axis, down)  7.05 us
    ppermute x4, waiting for transfers between devices, passed_along(): return lax.ppermute(array, axis, pairs)  5.75 us
    add x4, other arithmetic, sweeps(): field_ext = center + OMEGA * (source_now - product) / faces_now[7]  3.67 us
    dot_general x5, matrix products, z_sum(): return jnp.dot(flat, pick_z, precision=lax.Precision.HIGHEST)  1.95 us
  transfers between devices with their start and end apart: 12, of which 9 were waited for; matrix products, arithmetic and copies ran while one was open for 4% of the time, Pallas kernels for 0%

profile of v10, /device:TPU:1, one launch (start us, length us, event | category | flops | bytes accessed | tf_op | source)
XLA Modules:
  0.0 72.6 jit_solution(8828868014399380364)
XLA Ops:
  0.0 1.0 %pad_maximum_fusion.13 = (f32[3,3,16,256]{3,2,1,0:T(8,128)S(1)}, f32[3,3,16,256]{3,2,1,0:T(8,128)S(1)}) fusion(f32[1,16,16,256]{3,2,1,0:T(8,128)} %bitcast.221, f32[1,16,16,256]{3,2,1,0:T(8,128)} %bitcast.214, f32[1,16,16,256]{3,2,1,0:T(8,128)} %bitcast.223), kind=kLoop, calls=%fused_computation.156 | loop fusion | flops 147456 | bytes 1081344 | tf_op jit(solution)/shard_map/slice | solution.py:19
  1.0 4.0 %collective-permute-start = (f32[3,3,16,256]{3,2,1,0:T(8,128)S(1)}, f32[3,3,16,256]{3,2,1,0:T(8,128)S(1)}, u32[]{:S(2)}, u32[]{:S(2)}) collective-permute-start(f32[3,3,16,256]{3,2,1,0:T(8,128)S(1)} %get-tuple-element.23), channel_id=1, source_target_pairs={{0,4},{4,8},{8,12},{1,5},{5,9},{9,13},{2,6},{6,10},{10,14},{3,7},{... | collective-permute-start | bytes 442376 | tf_op jit(solution)/shard_map/ppermute | solution.py:21
  5.1 1.3 %collective-permute-start.1 = (f32[3,3,16,256]{3,2,1,0:T(8,128)S(1)}, f32[3,3,16,256]{3,2,1,0:T(8,128)S(1)}, u32[]{:S(2)}, u32[]{:S(2)}) collective-permute-start(f32[3,3,16,256]{3,2,1,0:T(8,128)S(1)} %get-tuple-element.24), channel_id=1, source_target_pairs={{4,0},{8,4},{12,8},{5,1},{9,5},{13,9},{6,2},{10,6},{14,10},{7,3},{... | collective-permute-start | bytes 442376 | tf_op jit(solution)/shard_map/ppermute | solution.py:22
  7.3 0.2 collective-permute-done
  7.6 3.8 %collective-permute-done.1 = f32[3,3,16,256]{3,2,1,0:T(8,128)S(1)} collective-permute-done((f32[3,3,16,256]{3,2,1,0:T(8,128)S(1)}, f32[3,3,16,256]{3,2,1,0:T(8,128)S(1)}, u32[]{:S(2)}, u32[]{:S(2)}) %collective-permute-start.1) | collective-permute-done | bytes 147488 | tf_op jit(solution)/shard_map/ppermute | solution.py:22
  11.5 0.1 fusion.128
  11.6 4.9 %collective-permute-start.2 = (f32[3,22,3,256]{3,2,1,0:T(4,128)S(1)}, f32[3,22,3,256]{3,2,1,0:T(4,128)S(1)}, u32[]{:S(2)}, u32[]{:S(2)}) collective-permute-start(f32[3,22,3,256]{3,2,1,0:T(4,128)S(1)} %get-tuple-element.21), channel_id=1, source_target_pairs={{0,1},{1,2},{2,3},{4,5},{5,6},{6,7},{8,9},{9,10},{10,11},{12,13},{... | collective-permute-start | bytes 608264 | tf_op jit(solution)/shard_map/ppermute | solution.py:21
  16.4 1.9 %collective-permute-start.3 = (f32[3,22,3,256]{3,2,1,0:T(4,128)S(1)}, f32[3,22,3,256]{3,2,1,0:T(4,128)S(1)}, u32[]{:S(2)}, u32[]{:S(2)}) collective-permute-start(f32[3,22,3,256]{3,2,1,0:T(4,128)S(1)} %get-tuple-element.22), channel_id=1, source_target_pairs={{1,0},{2,1},{3,2},{5,4},{6,5},{7,6},{9,8},{10,9},{11,10},{13,12},{... | collective-permute-start | bytes 608264 | tf_op jit(solution)/shard_map/ppermute | solution.py:22
  18.4 0.2 select_reduce_fusion
  18.6 0.6 fusion.141
  22.1 2.1 %collective-permute-done.3 = f32[3,22,3,256]{3,2,1,0:T(4,128)S(1)} collective-permute-done((f32[3,22,3,256]{3,2,1,0:T(4,128)S(1)}, f32[3,22,3,256]{3,2,1,0:T(4,128)S(1)}, u32[]{:S(2)}, u32[]{:S(2)}) %collective-permute-start.3) | collective-permute-done | bytes 202784 | tf_op jit(solution)/shard_map/ppermute | solution.py:22
  24.2 0.3 pad_maximum_fusion
  24.5 0.1 slice_bitcast_fusion
  24.6 0.2 fusion.130
  24.8 0.2 divide_select_fusion
  25.0 0.2 divide_select_fusion.1
  25.2 0.2 fusion.131
  25.4 0.2 divide_select_fusion.2
  25.6 1.0 %fusion.15 = (f32[20,20,256]{2,1,0:T(8,128)S(1)}, f32[20,20,256]{2,1,0:T(8,128)S(1)}, f32[20,20,256]{2,1,0:T(8,128)S(1)}) fusion(f32[22,22,256]{2,1,0:T(8,128)S(1)} %get-tuple-element.20, f32[22,22,256]{2,1,0:T(8,128)S(1)} %get-tuple-element.19, f32[20,20,255]{2,1,0:T(8,128)S(1)} %get-tuple-element.30, f32[20,20,255]{2,1,0:T(8,128)S(1)} %get-tuple-element.29, ...), kind=kLoop, calls=%fused_computation.30 | loop fusion | flops 2764800 | bytes 6961424 | tf_op jit(solution)/shard_map/add | solution.py:106
  26.6 0.2 fusion.134
  26.8 0.8 %fusion.38 = f32[18,18,256]{2,1,0:T(8,128)S(1)} fusion(f32[20,20,256]{2,1,0:T(8,128)S(1)} %get-tuple-element.15, f32[18,18,255]{2,1,0:T(8,128)S(1)} %get-tuple-element.38, f32[18,18,255]{2,1,0:T(8,128)S(1)} %get-tuple-element.37, f32[22,21,256]{2,1,0:T(8,128)S(1)} %divide_select_fusion, f32[21,22,256]{2,1,0:T(8,128)S(1)} %divide_select_fusion.1, ...), kind=kLoop, calls=%fused_computation.70 | loop fusion | flops 1410048 | bytes 5050272 | tf_op jit(solution)/shard_map/add | solution.py:106
  27.6 0.1 fusion.136
  27.7 0.5 fusion.129
  28.2 0.4 copy-done
  28.6 0.4 fusion.146
  29.0 0.4 fusion.142
  29.5 0.4 fusion.143
  29.9 0.4 fusion.145
  30.3 0.4 fusion.144
  30.7 0.4 fusion
  31.3 0.3 convolution_bitcast_fusion.2
  31.7 0.3 convolution_bitcast_fusion.1
  32.0 3.2 %collective-permute-start.4 = (f32[5,4,8,128]{3,1,2,0:T(4,128)S(1)}, f32[5,4,8,128]{3,1,2,0:T(4,128)S(1)}, u32[]{:S(2)}, u32[]{:S(2)}) collective-permute-start(f32[5,4,8,128]{3,1,2,0:T(4,128)S(1)} %convolution_bitcast_fusion.1), channel_id=1, source_target_pairs={{0,4},{4,8},{8,12},{1,5},{5,9},{9,13},{2,6},{6,10},{10,14},{3,7},{... | collective-permute-start | bytes 245768 | tf_op jit(solution)/shard_map/ppermute | solution.py:30
  35.2 1.3 %collective-permute-start.5 = (f32[5,5,8,128]{3,1,2,0:T(8,128)S(1)}, f32[5,5,8,128]{3,1,2,0:T(8,128)S(1)}, u32[]{:S(2)}, u32[]{:S(2)}) collective-permute-start(f32[5,5,8,128]{3,1,2,0:T(8,128)S(1)} %pad_maximum_fusion.10), channel_id=1, source_target_pairs={{4,0},{8,4},{12,8},{5,1},{9,5},{13,9},{6,2},{10,6},{14,10},{7,3},{... | collective-permute-start | bytes 307208 | tf_op jit(solution)/shard_map/ppermute | solution.py:30
  36.5 0.1 collective-permute-done.4
  36.8 4.5 %collective-permute-done.5 = f32[5,5,8,128]{3,1,2,0:T(8,128)S(1)} collective-permute-done((f32[5,5,8,128]{3,1,2,0:T(8,128)S(1)}, f32[5,5,8,128]{3,1,2,0:T(8,128)S(1)}, u32[]{:S(2)}, u32[]{:S(2)}) %collective-permute-start.5) | collective-permute-done | bytes 102432 | tf_op jit(solution)/shard_map/ppermute | solution.py:30
  41.3 0.1 multiply_add_fusion
  41.4 0.5 maximum_add_fusion
  42.0 3.2 %collective-permute-start.6 = (f32[5,24,4,128]{3,1,2,0:T(8,128)S(1)}, f32[5,24,4,128]{3,1,2,0:T(8,128)S(1)}, u32[]{:S(2)}, u32[]{:S(2)}) collective-permute-start(f32[5,24,4,128]{3,1,2,0:T(8,128)S(1)} %get-tuple-element.35), channel_id=1, source_target_pairs={{0,1},{1,2},{2,3},{4,5},{5,6},{6,7},{8,9},{9,10},{10,11},{12,13},{... | collective-permute-start | bytes 737288 | tf_op jit(solution)/shard_map/ppermute | solution.py:21
  45.2 1.9 %collective-permute-start.7 = (f32[5,24,4,128]{3,1,2,0:T(8,128)S(1)}, f32[5,24,4,128]{3,1,2,0:T(8,128)S(1)}, u32[]{:S(2)}, u32[]{:S(2)}) collective-permute-start(f32[5,24,4,128]{3,1,2,0:T(8,128)S(1)} %get-tuple-element.36), channel_id=1, source_target_pairs={{1,0},{2,1},{3,2},{5,4},{6,5},{7,6},{9,8},{10,9},{11,10},{13,12},{... | collective-permute-start | bytes 737288 | tf_op jit(solution)/shard_map/ppermute | solution.py:22
  47.1 0.7 and_convert_fusion
  47.8 0.5 collective-permute-done.6
  48.3 4.4 %collective-permute-done.7 = f32[5,24,4,128]{3,1,2,0:T(8,128)S(1)} collective-permute-done((f32[5,24,4,128]{3,1,2,0:T(8,128)S(1)}, f32[5,24,4,128]{3,1,2,0:T(8,128)S(1)}, u32[]{:S(2)}, u32[]{:S(2)}) %collective-permute-start.7) | collective-permute-done | bytes 245792 | tf_op jit(solution)/shard_map/ppermute | solution.py:22
  52.8 0.2 fusion.62
  53.0 0.1 fusion.138
  53.1 0.3 fusion.70
  53.4 0.1 fusion.139
  53.5 0.3 fusion.83
  53.9 0.1 multiply_reduce_fusion
  54.1 0.3 fusion.96
  54.4 0.3 copy-done.5
  54.7 0.3 fusion.59
  55.1 0.2 fusion.147
  55.3 1.3 %collective-permute-start.9 = (f32[2,16,256]{2,1,0:T(8,128)S(1)}, f32[2,16,256]{2,1,0:T(8,128)S(1)}, u32[]{:S(2)}, u32[]{:S(2)}) collective-permute-start(f32[2,16,256]{2,1,0:T(8,128)S(1)} %get-tuple-element.50), channel_id=1, source_target_pairs={{4,0},{8,4},{12,8},{5,1},{9,5},{13,9},{6,2},{10,6},{14,10},{7,3},{... | collective-permute-start | bytes 98312 | tf_op jit(solution)/shard_map/ppermute | solution.py:30
  56.6 0.1 fusion.148
  56.8 4.0 %collective-permute-start.8 = (f32[3,16,256]{2,1,0:T(8,128)S(1)}, f32[3,16,256]{2,1,0:T(8,128)S(1)}, u32[]{:S(2)}, u32[]{:S(2)}) collective-permute-start(f32[3,16,256]{2,1,0:T(8,128)S(1)} %pad_maximum_fusion.15), channel_id=1, source_target_pairs={{0,4},{4,8},{8,12},{1,5},{5,9},{9,13},{2,6},{6,10},{10,14},{3,7},{... | collective-permute-start | bytes 147464 | tf_op jit(solution)/shard_map/ppermute | solution.py:30
  60.9 1.1 %collective-permute-done.8 = f32[3,16,256]{2,1,0:T(8,128)S(1)} collective-permute-done((f32[3,16,256]{2,1,0:T(8,128)S(1)}, f32[3,16,256]{2,1,0:T(8,128)S(1)}, u32[]{:S(2)}, u32[]{:S(2)}) %collective-permute-start.8) | collective-permute-done | bytes 49184 | tf_op jit(solution)/shard_map/ppermute | solution.py:30
  62.1 2.9 %collective-permute-start.10 = (f32[20,2,256]{2,1,0:T(2,128)S(1)}, f32[20,2,256]{2,1,0:T(2,128)S(1)}, u32[]{:S(2)}, u32[]{:S(2)}) collective-permute-start(f32[20,2,256]{2,1,0:T(2,128)S(1)} %get-tuple-element.43), channel_id=1, source_target_pairs={{0,1},{1,2},{2,3},{4,5},{5,6},{6,7},{8,9},{9,10},{10,11},{12,13},{... | collective-permute-start | bytes 122888 | tf_op jit(solution)/shard_map/ppermute | solution.py:21
  65.0 1.9 %collective-permute-start.11 = (f32[20,2,256]{2,1,0:T(2,128)S(1)}, f32[20,2,256]{2,1,0:T(2,128)S(1)}, u32[]{:S(2)}, u32[]{:S(2)}) collective-permute-start(f32[20,2,256]{2,1,0:T(2,128)S(1)} %get-tuple-element.44), channel_id=1, source_target_pairs={{1,0},{2,1},{3,2},{5,4},{6,5},{7,6},{9,8},{10,9},{11,10},{13,12},{... | collective-permute-start | bytes 122888 | tf_op jit(solution)/shard_map/ppermute | solution.py:22
  66.9 3.4 %collective-permute-done.11 = f32[20,2,256]{2,1,0:T(2,128)S(1)} collective-permute-done((f32[20,2,256]{2,1,0:T(2,128)S(1)}, f32[20,2,256]{2,1,0:T(2,128)S(1)}, u32[]{:S(2)}, u32[]{:S(2)}) %collective-permute-start.11) | collective-permute-done | bytes 40992 | tf_op jit(solution)/shard_map/ppermute | solution.py:22
  70.4 0.2 fusion.132
  70.6 0.8 %fusion.27 = f32[18,18,256]{2,1,0:T(8,128)S(1)} fusion(f32[20,2,256]{2,1,0:T(2,128)S(1)} %collective-permute-done.11, f32[2,16,256]{2,1,0:T(8,128)S(1)} %multiply_add_fusion.3, f32[16,16,256]{2,1,0:T(8,128)S(1)} %multiply_add_fusion.1, f32[2,16,256]{2,1,0:T(8,128)S(1)} %slice.846, f32[20,2,256]{2,1,0:T(2,128)S(1)} %collective-permute-done.10, ...), kind=kLoop, calls=%fused_computation.51 | loop fusion | flops 1907712 | bytes 4796320 | tf_op jit(solution)/shard_map/add | solution.py:106
  71.4 0.1 fusion.135
  71.5 1.1 %fusion.49 = f32[16,16,256]{2,1,0:T(8,128)} fusion(f32[18,18,256]{2,1,0:T(8,128)S(1)} %fusion.27, f32[22,22,256]{2,1,0:T(8,128)S(1)} %get-tuple-element.19, f32[16,16,255]{2,1,0:T(8,128)S(1)} %get-tuple-element.40, f32[16,16,255]{2,1,0:T(8,128)S(1)} %get-tuple-element.39, f32[22,21,256]{2,1,0:T(8,128)S(1)} %divide_select_fusion, ...), kind=kLoop, calls=%fused_computation.90 | loop fusion | flops 1114112 | bytes 4075968 | tf_op jit(solution)/shard_map/add | solution.py:106
  (82 shorter events, 2.3 us)
Async XLA Ops:
  0.0 11.4 %copy-start.3 = (f32[16,16,256]{2,1,0:T(8,128)S(1)}, f32[16,16,256]{2,1,0:T(8,128)}, u32[]{:S(2)}) copy-start(f32[16,16,256]{2,1,0:T(8,128)} %param.11) | copy-start | bytes 786436
  0.0 11.4 %copy-start.1 = (f32[16,16,256]{2,1,0:T(8,128)S(1)}, f32[16,16,256]{2,1,0:T(8,128)}, u32[]{:S(2)}) copy-start(f32[16,16,256]{2,1,0:T(8,128)} %param.12) | copy-start | bytes 786436
  0.0 11.4 %copy-start.2 = (f32[16,16,256]{2,1,0:T(8,128)S(1)}, f32[16,16,256]{2,1,0:T(8,128)}, u32[]{:S(2)}) copy-start(f32[16,16,256]{2,1,0:T(8,128)} %param.13) | copy-start | bytes 786436
  1.0 6.5 %collective-permute-start = (f32[3,3,16,256]{3,2,1,0:T(8,128)S(1)}, f32[3,3,16,256]{3,2,1,0:T(8,128)S(1)}, u32[]{:S(2)}, u32[]{:S(2)}) collective-permute-start(f32[3,3,16,256]{3,2,1,0:T(8,128)S(1)} %get-tuple-element.23), channel_id=1, source_target_pairs={{0,4},{4,8},{8,12},{1,5},{5,9},{9,13},{2,6},{6,10},{10,14},{3,7},{... | collective-permute-start | bytes 442376 | tf_op jit(solution)/shard_map/ppermute | solution.py:21
  5.1 6.3 %collective-permute-start.1 = (f32[3,3,16,256]{3,2,1,0:T(8,128)S(1)}, f32[3,3,16,256]{3,2,1,0:T(8,128)S(1)}, u32[]{:S(2)}, u32[]{:S(2)}) collective-permute-start(f32[3,3,16,256]{3,2,1,0:T(8,128)S(1)} %get-tuple-element.24), channel_id=1, source_target_pairs={{4,0},{8,4},{12,8},{5,1},{9,5},{13,9},{6,2},{10,6},{14,10},{7,3},{... | collective-permute-start | bytes 442376 | tf_op jit(solution)/shard_map/ppermute | solution.py:22
  11.5 6.9 %copy-start.9 = (s32[64]{0:T(128)S(1)}, s32[64]{0:T(128)}, u32[]{:S(2)}) copy-start(s32[64]{0:T(128)} %param.14) | copy-start | bytes 772
  11.6 10.5 %collective-permute-start.2 = (f32[3,22,3,256]{3,2,1,0:T(4,128)S(1)}, f32[3,22,3,256]{3,2,1,0:T(4,128)S(1)}, u32[]{:S(2)}, u32[]{:S(2)}) collective-permute-start(f32[3,22,3,256]{3,2,1,0:T(4,128)S(1)} %get-tuple-element.21), channel_id=1, source_target_pairs={{0,1},{1,2},{2,3},{4,5},{5,6},{6,7},{8,9},{9,10},{10,11},{12,13},{... | collective-permute-start | bytes 608264 | tf_op jit(solution)/shard_map/ppermute | solution.py:21
  16.4 7.8 %collective-permute-start.3 = (f32[3,22,3,256]{3,2,1,0:T(4,128)S(1)}, f32[3,22,3,256]{3,2,1,0:T(4,128)S(1)}, u32[]{:S(2)}, u32[]{:S(2)}) collective-permute-start(f32[3,22,3,256]{3,2,1,0:T(4,128)S(1)} %get-tuple-element.22), channel_id=1, source_target_pairs={{1,0},{2,1},{3,2},{5,4},{6,5},{7,6},{9,8},{10,9},{11,10},{13,12},{... | collective-permute-start | bytes 608264 | tf_op jit(solution)/shard_map/ppermute | solution.py:22
  27.7 0.9 %copy-start = (f32[256,128]{1,0:T(8,128)S(1)}, f32[256,128]{1,0:T(8,128)}, u32[]{:S(2)}) copy-start(f32[256,128]{1,0:T(8,128)} %constant.45.clone) | copy-start | bytes 393220
  29.0 1.3 %copy-start.4 = (f32[256,128]{1,0:T(8,128)S(1)}, f32[256,128]{1,0:T(8,128)}, u32[]{:S(2)}) copy-start(f32[256,128]{1,0:T(8,128)} %constant.46.clone) | copy-start | bytes 393220
  29.4 1.3 %copy-start.8 = (f32[136]{0:T(256)S(1)}, f32[136]{0:T(256)}, u32[]{:S(2)}) copy-start(f32[136]{0:T(256)} %constant.48.clone) | copy-start | bytes 1636
  29.4 1.3 %copy-start.10 = (pred[136,256]{1,0:T(8,128)(4,1)S(1)}, pred[136,256]{1,0:T(8,128)(4,1)}, u32[]{:S(2)}) copy-start(pred[136,256]{1,0:T(8,128)(4,1)} %constant.50.clone) | copy-start | bytes 104452
  30.3 0.9 %copy-start.6 = (pred[136,256]{1,0:T(8,128)(4,1)S(1)}, pred[136,256]{1,0:T(8,128)(4,1)}, u32[]{:S(2)}) copy-start(pred[136,256]{1,0:T(8,128)(4,1)} %constant.51.clone) | copy-start | bytes 104452
  32.0 4.7 %collective-permute-start.4 = (f32[5,4,8,128]{3,1,2,0:T(4,128)S(1)}, f32[5,4,8,128]{3,1,2,0:T(4,128)S(1)}, u32[]{:S(2)}, u32[]{:S(2)}) collective-permute-start(f32[5,4,8,128]{3,1,2,0:T(4,128)S(1)} %convolution_bitcast_fusion.1), channel_id=1, source_target_pairs={{0,4},{4,8},{8,12},{1,5},{5,9},{9,13},{2,6},{6,10},{10,14},{3,7},{... | collective-permute-start | bytes 245768 | tf_op jit(solution)/shard_map/ppermute | solution.py:30
  35.2 6.1 %collective-permute-start.5 = (f32[5,5,8,128]{3,1,2,0:T(8,128)S(1)}, f32[5,5,8,128]{3,1,2,0:T(8,128)S(1)}, u32[]{:S(2)}, u32[]{:S(2)}) collective-permute-start(f32[5,5,8,128]{3,1,2,0:T(8,128)S(1)} %pad_maximum_fusion.10), channel_id=1, source_target_pairs={{4,0},{8,4},{12,8},{5,1},{9,5},{13,9},{6,2},{10,6},{14,10},{7,3},{... | collective-permute-start | bytes 307208 | tf_op jit(solution)/shard_map/ppermute | solution.py:30
  42.0 6.3 %collective-permute-start.6 = (f32[5,24,4,128]{3,1,2,0:T(8,128)S(1)}, f32[5,24,4,128]{3,1,2,0:T(8,128)S(1)}, u32[]{:S(2)}, u32[]{:S(2)}) collective-permute-start(f32[5,24,4,128]{3,1,2,0:T(8,128)S(1)} %get-tuple-element.35), channel_id=1, source_target_pairs={{0,1},{1,2},{2,3},{4,5},{5,6},{6,7},{8,9},{9,10},{10,11},{12,13},{... | collective-permute-start | bytes 737288 | tf_op jit(solution)/shard_map/ppermute | solution.py:21
  45.2 7.5 %collective-permute-start.7 = (f32[5,24,4,128]{3,1,2,0:T(8,128)S(1)}, f32[5,24,4,128]{3,1,2,0:T(8,128)S(1)}, u32[]{:S(2)}, u32[]{:S(2)}) collective-permute-start(f32[5,24,4,128]{3,1,2,0:T(8,128)S(1)} %get-tuple-element.36), channel_id=1, source_target_pairs={{1,0},{2,1},{3,2},{5,4},{6,5},{7,6},{9,8},{10,9},{11,10},{13,12},{... | collective-permute-start | bytes 737288 | tf_op jit(solution)/shard_map/ppermute | solution.py:22
  53.9 0.8 %copy-start.5 = (pred[256,136]{1,0:T(32,128)(4,1)S(1)}, pred[256,136]{1,0:T(32,128)(4,1)}, u32[]{:S(2)}) copy-start(pred[256,136]{1,0:T(32,128)(4,1)} %constant.49.clone) | copy-start | bytes 104452
  54.0 2.6 %copy-start.7 = (f32[16,8]{1,0:T(8,128)S(1)}, f32[16,8]{1,0:T(8,128)}, u32[]{:S(2)}) copy-start(f32[16,8]{1,0:T(8,128)} %constant.47.clone) | copy-start | bytes 1540
  55.3 5.5 %collective-permute-start.9 = (f32[2,16,256]{2,1,0:T(8,128)S(1)}, f32[2,16,256]{2,1,0:T(8,128)S(1)}, u32[]{:S(2)}, u32[]{:S(2)}) collective-permute-start(f32[2,16,256]{2,1,0:T(8,128)S(1)} %get-tuple-element.50), channel_id=1, source_target_pairs={{4,0},{8,4},{12,8},{5,1},{9,5},{13,9},{6,2},{10,6},{14,10},{7,3},{... | collective-permute-start | bytes 98312 | tf_op jit(solution)/shard_map/ppermute | solution.py:30
  56.8 5.2 %collective-permute-start.8 = (f32[3,16,256]{2,1,0:T(8,128)S(1)}, f32[3,16,256]{2,1,0:T(8,128)S(1)}, u32[]{:S(2)}, u32[]{:S(2)}) collective-permute-start(f32[3,16,256]{2,1,0:T(8,128)S(1)} %pad_maximum_fusion.15), channel_id=1, source_target_pairs={{0,4},{4,8},{8,12},{1,5},{5,9},{9,13},{2,6},{6,10},{10,14},{3,7},{... | collective-permute-start | bytes 147464 | tf_op jit(solution)/shard_map/ppermute | solution.py:30
  62.1 4.8 %collective-permute-start.10 = (f32[20,2,256]{2,1,0:T(2,128)S(1)}, f32[20,2,256]{2,1,0:T(2,128)S(1)}, u32[]{:S(2)}, u32[]{:S(2)}) collective-permute-start(f32[20,2,256]{2,1,0:T(2,128)S(1)} %get-tuple-element.43), channel_id=1, source_target_pairs={{0,1},{1,2},{2,3},{4,5},{5,6},{6,7},{8,9},{9,10},{10,11},{12,13},{... | collective-permute-start | bytes 122888 | tf_op jit(solution)/shard_map/ppermute | solution.py:21
  65.0 5.3 %collective-permute-start.11 = (f32[20,2,256]{2,1,0:T(2,128)S(1)}, f32[20,2,256]{2,1,0:T(2,128)S(1)}, u32[]{:S(2)}, u32[]{:S(2)}) collective-permute-start(f32[20,2,256]{2,1,0:T(2,128)S(1)} %get-tuple-element.44), channel_id=1, source_target_pairs={{1,0},{2,1},{3,2},{5,4},{6,5},{7,6},{9,8},{10,9},{11,10},{13,12},{... | collective-permute-start | bytes 122888 | tf_op jit(solution)/shard_map/ppermute | solution.py:22

commit v11 on v10

--- a/solution.py
+++ b/solution.py
@@ -117,7 +117,7 @@
     total_y = width_y * row_count
     sides = (("slab", 0), (("pencil", "sub"), 1))
     stacked_sides = (("slab", 1), (("pencil", "sub"), 2))
-    fine_rim = NU + 1
+    fine_rim = 2 * NU
     ext_x = padded(jnp.stack([permeability, source, pressure]), (("slab", 1),), fine_rim)
     ext_x, aggregate = lax.optimization_barrier((ext_x, aggregate))
     ext_all = padded(ext_x, ((("pencil", "sub"), 2),), fine_rim)
@@ -130,8 +130,8 @@
     faces_ext = geometry(perm_ext, glob_x, glob_y, inside_x, inside_y, total_x, total_y)
     smooth_ext = sweeps(ext_all[2], source_ext, faces_ext, NU, width_x)
     faces_zero = tuple(crop(member, fine_rim - 1) for member in faces_ext)
-    pressure = crop(smooth_ext, 1)
-    center, product = apply_fine(smooth_ext, faces_zero)
+    smooth_rows = smooth_ext[NU : NU + width_x]
+    center, product = apply_fine(crop(smooth_ext, NU - 1), faces_zero)
     residual = source - product
     half_y = width_y // 2
     half_z = depth_cells // 2
@@ -213,19 +213,21 @@
     place = (wide_range == NCS + count_live + jnp.arange(NCS)[None, :]).astype(jnp.float32)
     x_ext = x_ext + jnp.einsum("tk,qkjl->qtjl", place, from_next[:, :NCS], precision=lax.Precision.HIGHEST)
     coarse_rim = NCS
-    coef_ext = padded(x_ext, ((("pencil", "sub"), 2),), coarse_rim)
-    coarse_corr = jnp.zeros((width_x + 2 * NCS, half_y + 2 * NCS, half_z), jnp.float32)
+    rim_y = NCS + 1
+    coef_ext = padded(x_ext, ((("pencil", "sub"), 2),), rim_y)
+    coarse_corr = jnp.zeros((width_x + 2 * NCS, half_y + 2 * rim_y, half_z), jnp.float32)
     for sweep_index in range(NCS):
         out_rim = NCS - 1 - sweep_index
         start_at = coarse_rim - out_rim
+        start_y = start_at
         size_x = width_x + 2 * out_rim
-        size_y = half_y + 2 * out_rim
+        size_y = half_y + 2 * (out_rim + 1)
 
         def region(offset_x, offset_y):
             return coef_ext[
                 :,
                 start_at + offset_x : start_at + offset_x + size_x,
-                start_at + offset_y : start_at + offset_y + size_y,
+                start_y + offset_y : start_y + offset_y + size_y,
             ]
 
         here_coef = region(0, 0)
@@ -264,13 +266,25 @@
         )
     last_corr = jnp.sum(last_slot[:, None, None] * coarse_corr, axis=0)
     corr_wide = jnp.concatenate([jnp.zeros_like(last_corr)[None], coarse_corr], axis=0)
+    corr_core = corr_wide[:, 1 : 1 + half_y]
     corr_z = jnp.dot(
-        corr_wide.reshape((width_x + 1) * half_y, half_z), pair_z.T, precision=lax.Precision.HIGHEST
+        corr_core.reshape((width_x + 1) * half_y, half_z), pair_z.T, precision=lax.Precision.HIGHEST
     )
     correction = jnp.dot(spread_map, corr_z, precision=lax.Precision.HIGHEST)
-    base = pressure + correction.reshape(width_x, width_y, depth_cells)
+    correction = correction.reshape(width_x, width_y, depth_cells)
+    owner_rows = (slot_ids[:, None] + 1 == jnp.arange(width_x + 1)[None, :]).astype(jnp.float32)
+
+    def rim_rows(coarse_row):
+        row_z = jnp.dot(corr_wide[:, coarse_row], pair_z.T, precision=lax.Precision.HIGHEST)
+        row_fine = jnp.dot(owner_rows, row_z, precision=lax.Precision.HIGHEST)
+        return jnp.broadcast_to(row_fine[:, None], (width_x, NU, depth_cells))
+
+    correction = jnp.concatenate([rim_rows(0), correction, rim_rows(half_y + 1)], axis=1)
+    base = smooth_rows + correction
     last_z = jnp.dot(last_corr, pair_z.T, precision=lax.Precision.HIGHEST)
-    last_fine = jnp.dot(pair_y, last_z, precision=lax.Precision.HIGHEST)
+    fine_y = np.arange(width_y + 2 * NU) - NU
+    rows_ext = jnp.asarray((fine_y[:, None] // 2 + 1 == np.arange(half_y + 2)[None, :]).astype(np.float32))
+    last_fine = jnp.dot(rows_ext, last_z, precision=lax.Precision.HIGHEST)
     up_block = jnp.concatenate([base[width_x - NU :], last_fine[None]], axis=0)
     below_prev = passed_along(up_block, "slab", 1)
     above_next = passed_along(base[:NU], "slab", -1)
@@ -280,8 +294,7 @@
     next_in = ext_pos[width_x + 1 :] < plane_count
     to_owner = ((next_ids == local_ids[-1]) & next_in).astype(jnp.float32)
     high_halo = above_next + to_owner[:, None, None] * last_fine[None]
-    post_x = jnp.concatenate([below_prev[:NU], own, high_halo], axis=0)
-    post_ext = padded(post_x, ((("pencil", "sub"), 1),), NU)
+    post_ext = jnp.concatenate([below_prev[:NU], own, high_halo], axis=0)
     return sweeps(post_ext, source_ext, faces_ext, NU, width_x)
 
 

time: 73.2 us -> 68.2 us (0.932)
  starting transfers between devices: 31.8 us -> 27 us
  waiting for transfers between devices: 20.1 us -> 19 us
  matrix products: 4.33 us -> 5.2 us
    ppermute x4 -> x3, waiting for transfers between devices: 13.7 us -> 10.6 us  [padded(): after = lax.ppermute(leading, axis, down)]
    ppermute x4 -> x3, starting transfers between devices: 15 us -> 12.1 us  [padded(): before = lax.ppermute(last, axis, up)]
    ppermute x4 -> x3, starting transfers between devices: 7.05 us -> 5.13 us  [padded(): after = lax.ppermute(leading, axis, down)]
    ppermute x4 -> x3, waiting for transfers between devices: 0.7 us -> 2.35 us  [padded(): before = lax.ppermute(last, axis, up)]
    dot_general x2 -> x6, matrix products: 0.41 us -> 1.26 us  [the longest x2 0.45 us: rim_rows(): jnp.dot(corr_wide[:, coarse_row], pair_z.T, precision=lax.Precision.HIGHEST)]
  transfers between devices with their start and end apart: 12 -> 10, of which waited for: 9 -> 8; matrix products, arithmetic and copies ran while one was open for 4% -> 5% of each run, Pallas kernels for 0% -> 0%
where the time goes in v11:
time: 68.2 us; the launch traced here: 67.8 us
  starting transfers between devices  27 us (40%)
  waiting for transfers between devices  19 us (28%)
  other arithmetic  9.81 us (14%)
  matrix products  5.2 us (8%)
  local copies, waits for them, and re-layouts  3.57 us (5%)
  between operations  3.24 us (5%)
    ppermute x3, starting transfers between devices, padded(): before = lax.ppermute(last, axis, up)  12.1 us
    ppermute x3, waiting for transfers between devices, padded(): after = lax.ppermute(leading, axis, down)  10.6 us
    ppermute x4, starting transfers between devices, passed_along(): return lax.ppermute(array, axis, pairs)  9.79 us
    ppermute x4, waiting for transfers between devices, passed_along(): return lax.ppermute(array, axis, pairs)  5.98 us
    ppermute x3, starting transfers between devices, padded(): after = lax.ppermute(leading, axis, down)  5.13 us
    add x4, other arithmetic, sweeps(): field_ext = center + OMEGA * (source_now - product) / faces_now[7]  3.86 us
    ppermute x3, waiting for transfers between devices, padded(): before = lax.ppermute(last, axis, up)  2.35 us
    dot_general x5, matrix products, z_sum(): return jnp.dot(flat, pick_z, precision=lax.Precision.HIGHEST)  1.96 us
  transfers between devices with their start and end apart: 10, of which 8 were waited for; matrix products, arithmetic and copies ran while one was open for 5% of the time, Pallas kernels for 0%

profile of v11, /device:TPU:1, one launch (start us, length us, event | category | flops | bytes accessed | tf_op | source)
XLA Modules:
  0.0 67.8 jit_solution(16389567500703272335)
XLA Ops:
  0.0 1.1 %pad_maximum_fusion.8 = (f32[3,4,16,256]{3,2,1,0:T(8,128)S(1)}, f32[3,4,16,256]{3,2,1,0:T(8,128)S(1)}) fusion(f32[1,16,16,256]{3,2,1,0:T(8,128)} %bitcast.231, f32[1,16,16,256]{3,2,1,0:T(8,128)} %bitcast.224, f32[1,16,16,256]{3,2,1,0:T(8,128)} %bitcast.233), kind=kLoop, calls=%fused_computation.123 | loop fusion | flops 196608 | bytes 1179648 | tf_op jit(solution)/shard_map/slice | solution.py:19
  1.1 4.0 %collective-permute-start = (f32[3,4,16,256]{3,2,1,0:T(8,128)S(1)}, f32[3,4,16,256]{3,2,1,0:T(8,128)S(1)}, u32[]{:S(2)}, u32[]{:S(2)}) collective-permute-start(f32[3,4,16,256]{3,2,1,0:T(8,128)S(1)} %get-tuple-element.23), channel_id=1, source_target_pairs={{0,4},{4,8},{8,12},{1,5},{5,9},{9,13},{2,6},{6,10},{10,14},{3,7},{... | collective-permute-start | bytes 589832 | tf_op jit(solution)/shard_map/ppermute | solution.py:21
  5.2 1.3 %collective-permute-start.1 = (f32[3,4,16,256]{3,2,1,0:T(8,128)S(1)}, f32[3,4,16,256]{3,2,1,0:T(8,128)S(1)}, u32[]{:S(2)}, u32[]{:S(2)}) collective-permute-start(f32[3,4,16,256]{3,2,1,0:T(8,128)S(1)} %get-tuple-element.24), channel_id=1, source_target_pairs={{4,0},{8,4},{12,8},{5,1},{9,5},{13,9},{6,2},{10,6},{14,10},{7,3},{... | collective-permute-start | bytes 589832 | tf_op jit(solution)/shard_map/ppermute | solution.py:22
  7.4 1.3 %collective-permute-done = f32[3,4,16,256]{3,2,1,0:T(8,128)S(1)} collective-permute-done((f32[3,4,16,256]{3,2,1,0:T(8,128)S(1)}, f32[3,4,16,256]{3,2,1,0:T(8,128)S(1)}, u32[]{:S(2)}, u32[]{:S(2)}) %collective-permute-start) | collective-permute-done | bytes 196640 | tf_op jit(solution)/shard_map/ppermute | solution.py:21
  8.7 3.8 %collective-permute-done.1 = f32[3,4,16,256]{3,2,1,0:T(8,128)S(1)} collective-permute-done((f32[3,4,16,256]{3,2,1,0:T(8,128)S(1)}, f32[3,4,16,256]{3,2,1,0:T(8,128)S(1)}, u32[]{:S(2)}, u32[]{:S(2)}) %collective-permute-start.1) | collective-permute-done | bytes 196640 | tf_op jit(solution)/shard_map/ppermute | solution.py:22
  12.6 0.1 fusion.145
  12.7 4.9 %collective-permute-start.2 = (f32[3,24,4,256]{3,2,1,0:T(4,128)S(1)}, f32[3,24,4,256]{3,2,1,0:T(4,128)S(1)}, u32[]{:S(2)}, u32[]{:S(2)}) collective-permute-start(f32[3,24,4,256]{3,2,1,0:T(4,128)S(1)} %get-tuple-element.21), channel_id=1, source_target_pairs={{0,1},{1,2},{2,3},{4,5},{5,6},{6,7},{8,9},{9,10},{10,11},{12,13},{... | collective-permute-start | bytes 884744 | tf_op jit(solution)/shard_map/ppermute | solution.py:21
  17.6 1.9 %collective-permute-start.3 = (f32[3,24,4,256]{3,2,1,0:T(4,128)S(1)}, f32[3,24,4,256]{3,2,1,0:T(4,128)S(1)}, u32[]{:S(2)}, u32[]{:S(2)}) collective-permute-start(f32[3,24,4,256]{3,2,1,0:T(4,128)S(1)} %get-tuple-element.22), channel_id=1, source_target_pairs={{1,0},{2,1},{3,2},{5,4},{6,5},{7,6},{9,8},{10,9},{11,10},{13,12},{... | collective-permute-start | bytes 884744 | tf_op jit(solution)/shard_map/ppermute | solution.py:22
  19.6 0.2 select_reduce_fusion
  19.7 0.7 fusion.158
  23.2 2.4 %collective-permute-done.3 = f32[3,24,4,256]{3,2,1,0:T(4,128)S(1)} collective-permute-done((f32[3,24,4,256]{3,2,1,0:T(4,128)S(1)}, f32[3,24,4,256]{3,2,1,0:T(4,128)S(1)}, u32[]{:S(2)}, u32[]{:S(2)}) %collective-permute-start.3) | collective-permute-done | bytes 294944 | tf_op jit(solution)/shard_map/ppermute | solution.py:22
  25.7 0.3 pad_maximum_fusion
  25.9 0.1 slice_bitcast_fusion
  26.1 0.2 fusion.147
  26.3 0.2 divide_select_fusion
  26.5 0.2 divide_select_fusion.1
  26.7 0.2 fusion.148
  26.9 0.2 divide_select_fusion.2
  27.2 1.1 %fusion.7 = (f32[22,22,256]{2,1,0:T(8,128)S(1)}, f32[22,22,256]{2,1,0:T(8,128)S(1)}, f32[22,22,256]{2,1,0:T(8,128)S(1)}) fusion(f32[24,24,256]{2,1,0:T(8,128)S(1)} %get-tuple-element.20, f32[24,24,256]{2,1,0:T(8,128)S(1)} %get-tuple-element.19, f32[22,22,255]{2,1,0:T(8,128)S(1)} %get-tuple-element.30, f32[22,22,255]{2,1,0:T(8,128)S(1)} %get-tuple-element.29, ...), kind=kLoop, calls=%fused_computation.22 | loop fusion | flops 3345408 | bytes 8423108 | tf_op jit(solution)/shard_map/add | solution.py:106
  28.3 0.2 fusion.149
  28.5 0.8 %fusion.26 = f32[20,20,256]{2,1,0:T(8,128)S(1)} fusion(f32[22,22,256]{2,1,0:T(8,128)S(1)} %get-tuple-element.15, f32[24,23,256]{2,1,0:T(8,128)S(1)} %divide_select_fusion, f32[23,24,256]{2,1,0:T(8,128)S(1)} %divide_select_fusion.1, f32[24,24,256]{2,1,0:T(8,128)S(1)} %get-tuple-element.19, f32[20,20,255]{2,1,0:T(8,128)S(1)} %get-tuple-element.34, ...), kind=kLoop, calls=%fused_computation.49 | loop fusion | flops 1740800 | bytes 6224880 | tf_op jit(solution)/shard_map/add | solution.py:106
  29.3 0.1 fusion.152
  29.4 0.5 fusion.146
  29.9 0.4 copy-done
  30.3 0.4 fusion.163
  30.7 0.4 fusion.159
  31.2 0.4 fusion.160
  31.6 0.4 fusion.162
  32.0 0.4 fusion.161
  32.5 0.4 fusion.11
  33.0 0.3 convolution_bitcast_fusion.2
  33.4 0.3 convolution_bitcast_fusion.1
  33.7 3.2 %collective-permute-start.4 = (f32[5,4,8,128]{3,1,2,0:T(4,128)S(1)}, f32[5,4,8,128]{3,1,2,0:T(4,128)S(1)}, u32[]{:S(2)}, u32[]{:S(2)}) collective-permute-start(f32[5,4,8,128]{3,1,2,0:T(4,128)S(1)} %convolution_bitcast_fusion.1), channel_id=1, source_target_pairs={{0,4},{4,8},{8,12},{1,5},{5,9},{9,13},{2,6},{6,10},{10,14},{3,7},{... | collective-permute-start | bytes 245768 | tf_op jit(solution)/shard_map/ppermute | solution.py:30
  36.9 1.3 %collective-permute-start.5 = (f32[5,5,8,128]{3,1,2,0:T(8,128)S(1)}, f32[5,5,8,128]{3,1,2,0:T(8,128)S(1)}, u32[]{:S(2)}, u32[]{:S(2)}) collective-permute-start(f32[5,5,8,128]{3,1,2,0:T(8,128)S(1)} %pad_maximum_fusion.9), channel_id=1, source_target_pairs={{4,0},{8,4},{12,8},{5,1},{9,5},{13,9},{6,2},{10,6},{14,10},{7,3},{... | collective-permute-start | bytes 307208 | tf_op jit(solution)/shard_map/ppermute | solution.py:30
  38.2 0.1 collective-permute-done.4
  38.5 4.5 %collective-permute-done.5 = f32[5,5,8,128]{3,1,2,0:T(8,128)S(1)} collective-permute-done((f32[5,5,8,128]{3,1,2,0:T(8,128)S(1)}, f32[5,5,8,128]{3,1,2,0:T(8,128)S(1)}, u32[]{:S(2)}, u32[]{:S(2)}) %collective-permute-start.5) | collective-permute-done | bytes 102432 | tf_op jit(solution)/shard_map/ppermute | solution.py:30
  43.0 0.1 multiply_add_fusion.1
  43.1 0.5 maximum_add_fusion
  43.7 3.2 %collective-permute-start.6 = (f32[5,24,5,128]{3,1,2,0:T(8,128)S(1)}, f32[5,24,5,128]{3,1,2,0:T(8,128)S(1)}, u32[]{:S(2)}, u32[]{:S(2)}) collective-permute-start(f32[5,24,5,128]{3,1,2,0:T(8,128)S(1)} %get-tuple-element.37), channel_id=1, source_target_pairs={{0,1},{1,2},{2,3},{4,5},{5,6},{6,7},{8,9},{9,10},{10,11},{12,13},{... | collective-permute-start | bytes 921608 | tf_op jit(solution)/shard_map/ppermute | solution.py:21
  46.9 1.9 %collective-permute-start.7 = (f32[5,24,5,128]{3,1,2,0:T(8,128)S(1)}, f32[5,24,5,128]{3,1,2,0:T(8,128)S(1)}, u32[]{:S(2)}, u32[]{:S(2)}) collective-permute-start(f32[5,24,5,128]{3,1,2,0:T(8,128)S(1)} %get-tuple-element.38), channel_id=1, source_target_pairs={{1,0},{2,1},{3,2},{5,4},{6,5},{7,6},{9,8},{10,9},{11,10},{13,12},{... | collective-permute-start | bytes 921608 | tf_op jit(solution)/shard_map/ppermute | solution.py:22
  48.8 0.8 %and_convert_fusion = f32[2]{0:T(128)S(1)} fusion(s32[19]{0:T(128)S(1)} %iota_add_fusion, f32[19]{0:T(128)S(1)} %select_reduce_fusion, f32[]{:T(128)} %bitcast.21), kind=kLoop, calls=%fused_computation.247 | loop fusion | flops 8 | bytes 28 | tf_op jit(solution)/shard_map/convert_element_type | solution.py:295
  49.6 1.1 %collective-permute-done.6 = f32[5,24,5,128]{3,1,2,0:T(8,128)S(1)} collective-permute-done((f32[5,24,5,128]{3,1,2,0:T(8,128)S(1)}, f32[5,24,5,128]{3,1,2,0:T(8,128)S(1)}, u32[]{:S(2)}, u32[]{:S(2)}) %collective-permute-start.6) | collective-permute-done | bytes 307232 | tf_op jit(solution)/shard_map/ppermute | solution.py:21
  50.6 4.4 %collective-permute-done.7 = f32[5,24,5,128]{3,1,2,0:T(8,128)S(1)} collective-permute-done((f32[5,24,5,128]{3,1,2,0:T(8,128)S(1)}, f32[5,24,5,128]{3,1,2,0:T(8,128)S(1)}, u32[]{:S(2)}, u32[]{:S(2)}) %collective-permute-start.7) | collective-permute-done | bytes 307232 | tf_op jit(solution)/shard_map/ppermute | solution.py:22
  55.2 0.2 fusion.62
  55.4 0.1 fusion.155
  55.6 0.3 fusion.70
  55.9 0.1 fusion.156
  56.0 0.3 fusion.81
  56.4 0.2 multiply_reduce_fusion
  56.6 0.2 fusion.119
  56.9 0.2 fusion.117
  57.1 0.3 fusion.108
  57.4 0.2 fusion.123
  57.6 0.2 fusion.121
  57.8 0.3 fusion.59
  58.3 0.2 fusion.164
  58.5 1.3 %collective-permute-start.9 = (f32[2,20,256]{2,1,0:T(8,128)S(1)}, f32[2,20,256]{2,1,0:T(8,128)S(1)}, u32[]{:S(2)}, u32[]{:S(2)}) collective-permute-start(f32[2,20,256]{2,1,0:T(8,128)S(1)} %get-tuple-element.44), channel_id=1, source_target_pairs={{4,0},{8,4},{12,8},{5,1},{9,5},{13,9},{6,2},{10,6},{14,10},{7,3},{... | collective-permute-start | bytes 122888 | tf_op jit(solution)/shard_map/ppermute | solution.py:30
  59.8 0.1 fusion.165
  60.0 4.0 %collective-permute-start.8 = (f32[3,20,256]{2,1,0:T(8,128)S(1)}, f32[3,20,256]{2,1,0:T(8,128)S(1)}, u32[]{:S(2)}, u32[]{:S(2)}) collective-permute-start(f32[3,20,256]{2,1,0:T(8,128)S(1)} %pad_maximum_fusion.11), channel_id=1, source_target_pairs={{0,4},{4,8},{8,12},{1,5},{5,9},{9,13},{2,6},{6,10},{10,14},{3,7},{... | collective-permute-start | bytes 184328 | tf_op jit(solution)/shard_map/ppermute | solution.py:30
  64.0 1.3 %collective-permute-done.8 = f32[3,20,256]{2,1,0:T(8,128)S(1)} collective-permute-done((f32[3,20,256]{2,1,0:T(8,128)S(1)}, f32[3,20,256]{2,1,0:T(8,128)S(1)}, u32[]{:S(2)}, u32[]{:S(2)}) %collective-permute-start.8) | collective-permute-done | bytes 61472 | tf_op jit(solution)/shard_map/ppermute | solution.py:30
  65.5 0.2 fusion.150
  65.7 0.8 %fusion.36 = f32[18,18,256]{2,1,0:T(8,128)S(1)} fusion(f32[20,20,256]{2,1,0:T(8,128)S(1)} %pad_maximum_fusion.3, f32[24,23,256]{2,1,0:T(8,128)S(1)} %divide_select_fusion, f32[2,20,256]{2,1,0:T(8,128)S(1)} %multiply_add_fusion.3, f32[16,20,256]{2,1,0:T(8,128)S(1)} %multiply_add_fusion, f32[23,24,256]{2,1,0:T(8,128)S(1)} %divide_select_fusion.1, ...), kind=kLoop, calls=%fused_computation.65 | loop fusion | flops 1575936 | bytes 4882000 | tf_op jit(solution)/shard_map/add | solution.py:106
  66.5 0.1 fusion.153
  66.7 1.1 %fusion.49 = f32[16,16,256]{2,1,0:T(8,128)} fusion(f32[18,18,256]{2,1,0:T(8,128)S(1)} %fusion.36, f32[24,24,256]{2,1,0:T(8,128)S(1)} %get-tuple-element.19, f32[16,16,255]{2,1,0:T(8,128)S(1)} %get-tuple-element.42, f32[16,16,255]{2,1,0:T(8,128)S(1)} %get-tuple-element.41, f32[24,23,256]{2,1,0:T(8,128)S(1)} %divide_select_fusion, ...), kind=kLoop, calls=%fused_computation.88 | loop fusion | flops 1114112 | bytes 4161648 | tf_op jit(solution)/shard_map/add | solution.py:106
  (84 shorter events, 2.3 us)
Async XLA Ops:
  0.0 12.5 %copy-start.3 = (f32[16,16,256]{2,1,0:T(8,128)S(1)}, f32[16,16,256]{2,1,0:T(8,128)}, u32[]{:S(2)}) copy-start(f32[16,16,256]{2,1,0:T(8,128)} %param.11) | copy-start | bytes 786436
  0.0 12.5 %copy-start.1 = (f32[16,16,256]{2,1,0:T(8,128)S(1)}, f32[16,16,256]{2,1,0:T(8,128)}, u32[]{:S(2)}) copy-start(f32[16,16,256]{2,1,0:T(8,128)} %param.12) | copy-start | bytes 786436
  0.0 12.5 %copy-start.2 = (f32[16,16,256]{2,1,0:T(8,128)S(1)}, f32[16,16,256]{2,1,0:T(8,128)}, u32[]{:S(2)}) copy-start(f32[16,16,256]{2,1,0:T(8,128)} %param.13) | copy-start | bytes 786436
  1.1 7.6 %collective-permute-start = (f32[3,4,16,256]{3,2,1,0:T(8,128)S(1)}, f32[3,4,16,256]{3,2,1,0:T(8,128)S(1)}, u32[]{:S(2)}, u32[]{:S(2)}) collective-permute-start(f32[3,4,16,256]{3,2,1,0:T(8,128)S(1)} %get-tuple-element.23), channel_id=1, source_target_pairs={{0,4},{4,8},{8,12},{1,5},{5,9},{9,13},{2,6},{6,10},{10,14},{3,7},{... | collective-permute-start | bytes 589832 | tf_op jit(solution)/shard_map/ppermute | solution.py:21
  5.2 7.3 %collective-permute-start.1 = (f32[3,4,16,256]{3,2,1,0:T(8,128)S(1)}, f32[3,4,16,256]{3,2,1,0:T(8,128)S(1)}, u32[]{:S(2)}, u32[]{:S(2)}) collective-permute-start(f32[3,4,16,256]{3,2,1,0:T(8,128)S(1)} %get-tuple-element.24), channel_id=1, source_target_pairs={{4,0},{8,4},{12,8},{5,1},{9,5},{13,9},{6,2},{10,6},{14,10},{7,3},{... | collective-permute-start | bytes 589832 | tf_op jit(solution)/shard_map/ppermute | solution.py:22
  12.6 6.9 %copy-start.9 = (s32[64]{0:T(128)S(1)}, s32[64]{0:T(128)}, u32[]{:S(2)}) copy-start(s32[64]{0:T(128)} %param.14) | copy-start | bytes 772
  12.7 10.5 %collective-permute-start.2 = (f32[3,24,4,256]{3,2,1,0:T(4,128)S(1)}, f32[3,24,4,256]{3,2,1,0:T(4,128)S(1)}, u32[]{:S(2)}, u32[]{:S(2)}) collective-permute-start(f32[3,24,4,256]{3,2,1,0:T(4,128)S(1)} %get-tuple-element.21), channel_id=1, source_target_pairs={{0,1},{1,2},{2,3},{4,5},{5,6},{6,7},{8,9},{9,10},{10,11},{12,13},{... | collective-permute-start | bytes 884744 | tf_op jit(solution)/shard_map/ppermute | solution.py:21
  17.6 8.0 %collective-permute-start.3 = (f32[3,24,4,256]{3,2,1,0:T(4,128)S(1)}, f32[3,24,4,256]{3,2,1,0:T(4,128)S(1)}, u32[]{:S(2)}, u32[]{:S(2)}) collective-permute-start(f32[3,24,4,256]{3,2,1,0:T(4,128)S(1)} %get-tuple-element.22), channel_id=1, source_target_pairs={{1,0},{2,1},{3,2},{5,4},{6,5},{7,6},{9,8},{10,9},{11,10},{13,12},{... | collective-permute-start | bytes 884744 | tf_op jit(solution)/shard_map/ppermute | solution.py:22
  29.4 0.9 %copy-start = (f32[256,128]{1,0:T(8,128)S(1)}, f32[256,128]{1,0:T(8,128)}, u32[]{:S(2)}) copy-start(f32[256,128]{1,0:T(8,128)} %constant.45.clone) | copy-start | bytes 393220
  30.7 1.3 %copy-start.4 = (f32[256,128]{1,0:T(8,128)S(1)}, f32[256,128]{1,0:T(8,128)}, u32[]{:S(2)}) copy-start(f32[256,128]{1,0:T(8,128)} %constant.46.clone) | copy-start | bytes 393220
  31.1 1.3 %copy-start.8 = (f32[136]{0:T(256)S(1)}, f32[136]{0:T(256)}, u32[]{:S(2)}) copy-start(f32[136]{0:T(256)} %constant.47.clone) | copy-start | bytes 1636
  31.2 1.3 %copy-start.10 = (pred[136,256]{1,0:T(8,128)(4,1)S(1)}, pred[136,256]{1,0:T(8,128)(4,1)}, u32[]{:S(2)}) copy-start(pred[136,256]{1,0:T(8,128)(4,1)} %constant.49.clone) | copy-start | bytes 104452
  32.0 0.9 %copy-start.6 = (pred[136,256]{1,0:T(8,128)(4,1)S(1)}, pred[136,256]{1,0:T(8,128)(4,1)}, u32[]{:S(2)}) copy-start(pred[136,256]{1,0:T(8,128)(4,1)} %constant.50.clone) | copy-start | bytes 104452
  33.7 4.7 %collective-permute-start.4 = (f32[5,4,8,128]{3,1,2,0:T(4,128)S(1)}, f32[5,4,8,128]{3,1,2,0:T(4,128)S(1)}, u32[]{:S(2)}, u32[]{:S(2)}) collective-permute-start(f32[5,4,8,128]{3,1,2,0:T(4,128)S(1)} %convolution_bitcast_fusion.1), channel_id=1, source_target_pairs={{0,4},{4,8},{8,12},{1,5},{5,9},{9,13},{2,6},{6,10},{10,14},{3,7},{... | collective-permute-start | bytes 245768 | tf_op jit(solution)/shard_map/ppermute | solution.py:30
  36.9 6.1 %collective-permute-start.5 = (f32[5,5,8,128]{3,1,2,0:T(8,128)S(1)}, f32[5,5,8,128]{3,1,2,0:T(8,128)S(1)}, u32[]{:S(2)}, u32[]{:S(2)}) collective-permute-start(f32[5,5,8,128]{3,1,2,0:T(8,128)S(1)} %pad_maximum_fusion.9), channel_id=1, source_target_pairs={{4,0},{8,4},{12,8},{5,1},{9,5},{13,9},{6,2},{10,6},{14,10},{7,3},{... | collective-permute-start | bytes 307208 | tf_op jit(solution)/shard_map/ppermute | solution.py:30
  43.7 7.0 %collective-permute-start.6 = (f32[5,24,5,128]{3,1,2,0:T(8,128)S(1)}, f32[5,24,5,128]{3,1,2,0:T(8,128)S(1)}, u32[]{:S(2)}, u32[]{:S(2)}) collective-permute-start(f32[5,24,5,128]{3,1,2,0:T(8,128)S(1)} %get-tuple-element.37), channel_id=1, source_target_pairs={{0,1},{1,2},{2,3},{4,5},{5,6},{6,7},{8,9},{9,10},{10,11},{12,13},{... | collective-permute-start | bytes 921608 | tf_op jit(solution)/shard_map/ppermute | solution.py:21
  46.9 8.2 %collective-permute-start.7 = (f32[5,24,5,128]{3,1,2,0:T(8,128)S(1)}, f32[5,24,5,128]{3,1,2,0:T(8,128)S(1)}, u32[]{:S(2)}, u32[]{:S(2)}) collective-permute-start(f32[5,24,5,128]{3,1,2,0:T(8,128)S(1)} %get-tuple-element.38), channel_id=1, source_target_pairs={{1,0},{2,1},{3,2},{5,4},{6,5},{7,6},{9,8},{10,9},{11,10},{13,12},{... | collective-permute-start | bytes 921608 | tf_op jit(solution)/shard_map/ppermute | solution.py:22
  56.4 1.4 %copy-start.5 = (pred[256,136]{1,0:T(32,128)(4,1)S(1)}, pred[256,136]{1,0:T(32,128)(4,1)}, u32[]{:S(2)}) copy-start(pred[256,136]{1,0:T(32,128)(4,1)} %constant.48.clone) | copy-start | bytes 104452
  57.1 2.7 %copy-start.7 = (f32[20,10]{1,0:T(8,128)S(1)}, f32[20,10]{1,0:T(8,128)}, u32[]{:S(2)}) copy-start(f32[20,10]{1,0:T(8,128)} %constant.51.clone) | copy-start | bytes 2404
  58.5 5.5 %collective-permute-start.9 = (f32[2,20,256]{2,1,0:T(8,128)S(1)}, f32[2,20,256]{2,1,0:T(8,128)S(1)}, u32[]{:S(2)}, u32[]{:S(2)}) collective-permute-start(f32[2,20,256]{2,1,0:T(8,128)S(1)} %get-tuple-element.44), channel_id=1, source_target_pairs={{4,0},{8,4},{12,8},{5,1},{9,5},{13,9},{6,2},{10,6},{14,10},{7,3},{... | collective-permute-start | bytes 122888 | tf_op jit(solution)/shard_map/ppermute | solution.py:30
  60.0 5.4 %collective-permute-start.8 = (f32[3,20,256]{2,1,0:T(8,128)S(1)}, f32[3,20,256]{2,1,0:T(8,128)S(1)}, u32[]{:S(2)}, u32[]{:S(2)}) collective-permute-start(f32[3,20,256]{2,1,0:T(8,128)S(1)} %pad_maximum_fusion.11), channel_id=1, source_target_pairs={{0,4},{4,8},{8,12},{1,5},{5,9},{9,13},{2,6},{6,10},{10,14},{3,7},{... | collective-permute-start | bytes 184328 | tf_op jit(solution)/shard_map/ppermute | solution.py:30

commit v12 on v11

--- a/solution.py
+++ b/solution.py
@@ -161,15 +161,19 @@
         flat = block_in.reshape(cells, depth_cells)
         return jnp.dot(flat, pick_z, precision=lax.Precision.HIGHEST)
 
-    z_parts = jnp.stack(
+    z_rows = jnp.concatenate(
         [
-            z_sum(residual, pair_z),
-            z_sum(face_east * crossing[:, None, None], pair_z),
-            z_sum(face_north, pair_z),
-            z_sum(face_above, odd_z),
-            z_sum(boundary, pair_z),
-        ]
-    )
+            block_in.reshape(cells, depth_cells)
+            for block_in in (residual, face_east * crossing[:, None, None], face_north, face_above, boundary)
+        ],
+        axis=0,
+    )
+    z_all = jnp.dot(z_rows, jnp.concatenate([pair_z, odd_z], axis=1), precision=lax.Precision.HIGHEST)
+
+    def z_part(index, odd):
+        return z_all[index * cells : (index + 1) * cells, odd * half_z : (odd + 1) * half_z]
+
+    z_parts = [z_part(0, 0), z_part(1, 0), z_part(2, 0), z_part(3, 1), z_part(4, 0)]
     index_y = np.arange(width_y)[:, None]
     coarse_y = np.arange(half_y)[None, :]
     pair_y = jnp.asarray((index_y // 2 == coarse_y).astype(np.float32))

time: 68.2 us -> 72.2 us (1.059)
  waiting for transfers between devices: 19 us -> 22.7 us
  local copies, waits for them, and re-layouts: 3.57 us -> 4.61 us
    ppermute x3, waiting for transfers between devices: 10.6 us -> 12.6 us  [padded(): after = lax.ppermute(leading, axis, down)]
    ppermute x3, waiting for transfers between devices: 2.35 us -> 4.08 us  [padded(): before = lax.ppermute(last, axis, up)]
    unnamed x26 -> x30, local copies, waits for them, and re-layouts: 0.54 us -> 1.57 us
    dot_general x5 -> x1, matrix products: 1.96 us -> 1.3 us  [body(): jnp.dot(z_rows, jnp.concatenate([pair_z, odd_z], axis=1), precision=lax.P...]
  transfers between devices with their start and end apart: 10 -> 10, of which waited for: 8 -> 9; matrix products, arithmetic and copies ran while one was open for 5% -> 3% of each run, Pallas kernels for 0% -> 0%
where the time goes in v12:
time: 72.2 us; the launch traced here: 71.8 us
  starting transfers between devices  27 us (37%)
  waiting for transfers between devices  22.7 us (31%)
  other arithmetic  9.73 us (13%)
  local copies, waits for them, and re-layouts  4.61 us (6%)
  matrix products  4.57 us (6%)
  between operations  3.21 us (4%)
    ppermute x3, waiting for transfers between devices, padded(): after = lax.ppermute(leading, axis, down)  12.6 us
    ppermute x3, starting transfers between devices, padded(): before = lax.ppermute(last, axis, up)  12.1 us
    ppermute x4, starting transfers between devices, passed_along(): return lax.ppermute(array, axis, pairs)  9.77 us
    ppermute x4, waiting for transfers between devices, passed_along(): return lax.ppermute(array, axis, pairs)  5.98 us
    ppermute x3, starting transfers between devices, padded(): after = lax.ppermute(leading, axis, down)  5.13 us
    ppermute x3, waiting for transfers between devices, padded(): before = lax.ppermute(last, axis, up)  4.08 us
    add x4, other arithmetic, sweeps(): field_ext = center + OMEGA * (source_now - product) / faces_now[7]  3.86 us
    unnamed x30, local copies, waits for them, and re-layouts  1.57 us
  transfers between devices with their start and end apart: 10, of which 9 were waited for; matrix products, arithmetic and copies ran while one was open for 3% of the time, Pallas kernels for 0%

profile of v12, /device:TPU:1, one launch (start us, length us, event | category | flops | bytes accessed | tf_op | source)
XLA Modules:
  0.0 71.8 jit_solution(15583273955247909417)
XLA Ops:
  0.0 1.1 %pad_maximum_fusion.8 = (f32[3,4,16,256]{3,2,1,0:T(8,128)S(1)}, f32[3,4,16,256]{3,2,1,0:T(8,128)S(1)}) fusion(f32[1,16,16,256]{3,2,1,0:T(8,128)} %bitcast.222, f32[1,16,16,256]{3,2,1,0:T(8,128)} %bitcast.215, f32[1,16,16,256]{3,2,1,0:T(8,128)} %bitcast.224), kind=kLoop, calls=%fused_computation.123 | loop fusion | flops 196608 | bytes 1179648 | tf_op jit(solution)/shard_map/slice | solution.py:19
  1.1 4.0 %collective-permute-start = (f32[3,4,16,256]{3,2,1,0:T(8,128)S(1)}, f32[3,4,16,256]{3,2,1,0:T(8,128)S(1)}, u32[]{:S(2)}, u32[]{:S(2)}) collective-permute-start(f32[3,4,16,256]{3,2,1,0:T(8,128)S(1)} %get-tuple-element.27), channel_id=1, source_target_pairs={{0,4},{4,8},{8,12},{1,5},{5,9},{9,13},{2,6},{6,10},{10,14},{3,7},{... | collective-permute-start | bytes 589832 | tf_op jit(solution)/shard_map/ppermute | solution.py:21
  5.2 1.3 %collective-permute-start.1 = (f32[3,4,16,256]{3,2,1,0:T(8,128)S(1)}, f32[3,4,16,256]{3,2,1,0:T(8,128)S(1)}, u32[]{:S(2)}, u32[]{:S(2)}) collective-permute-start(f32[3,4,16,256]{3,2,1,0:T(8,128)S(1)} %get-tuple-element.28), channel_id=1, source_target_pairs={{4,0},{8,4},{12,8},{5,1},{9,5},{13,9},{6,2},{10,6},{14,10},{7,3},{... | collective-permute-start | bytes 589832 | tf_op jit(solution)/shard_map/ppermute | solution.py:22
  7.5 1.3 %collective-permute-done = f32[3,4,16,256]{3,2,1,0:T(8,128)S(1)} collective-permute-done((f32[3,4,16,256]{3,2,1,0:T(8,128)S(1)}, f32[3,4,16,256]{3,2,1,0:T(8,128)S(1)}, u32[]{:S(2)}, u32[]{:S(2)}) %collective-permute-start) | collective-permute-done | bytes 196640 | tf_op jit(solution)/shard_map/ppermute | solution.py:21
  8.7 3.8 %collective-permute-done.1 = f32[3,4,16,256]{3,2,1,0:T(8,128)S(1)} collective-permute-done((f32[3,4,16,256]{3,2,1,0:T(8,128)S(1)}, f32[3,4,16,256]{3,2,1,0:T(8,128)S(1)}, u32[]{:S(2)}, u32[]{:S(2)}) %collective-permute-start.1) | collective-permute-done | bytes 196640 | tf_op jit(solution)/shard_map/ppermute | solution.py:22
  12.6 0.2 select_reduce_fusion
  12.8 0.6 fusion.160
  16.1 0.1 fusion.147
  16.3 4.9 %collective-permute-start.2 = (f32[3,24,4,256]{3,2,1,0:T(4,128)S(1)}, f32[3,24,4,256]{3,2,1,0:T(4,128)S(1)}, u32[]{:S(2)}, u32[]{:S(2)}) collective-permute-start(f32[3,24,4,256]{3,2,1,0:T(4,128)S(1)} %get-tuple-element.25), channel_id=1, source_target_pairs={{0,1},{1,2},{2,3},{4,5},{5,6},{6,7},{8,9},{9,10},{10,11},{12,13},{... | collective-permute-start | bytes 884744 | tf_op jit(solution)/shard_map/ppermute | solution.py:21
  21.1 1.9 %collective-permute-start.3 = (f32[3,24,4,256]{3,2,1,0:T(4,128)S(1)}, f32[3,24,4,256]{3,2,1,0:T(4,128)S(1)}, u32[]{:S(2)}, u32[]{:S(2)}) collective-permute-start(f32[3,24,4,256]{3,2,1,0:T(4,128)S(1)} %get-tuple-element.26), channel_id=1, source_target_pairs={{1,0},{2,1},{3,2},{5,4},{6,5},{7,6},{9,8},{10,9},{11,10},{13,12},{... | collective-permute-start | bytes 884744 | tf_op jit(solution)/shard_map/ppermute | solution.py:22
  23.1 1.6 %collective-permute-done.2 = f32[3,24,4,256]{3,2,1,0:T(4,128)S(1)} collective-permute-done((f32[3,24,4,256]{3,2,1,0:T(4,128)S(1)}, f32[3,24,4,256]{3,2,1,0:T(4,128)S(1)}, u32[]{:S(2)}, u32[]{:S(2)}) %collective-permute-start.2) | collective-permute-done | bytes 294944 | tf_op jit(solution)/shard_map/ppermute | solution.py:21
  24.8 4.4 %collective-permute-done.3 = f32[3,24,4,256]{3,2,1,0:T(4,128)S(1)} collective-permute-done((f32[3,24,4,256]{3,2,1,0:T(4,128)S(1)}, f32[3,24,4,256]{3,2,1,0:T(4,128)S(1)}, u32[]{:S(2)}, u32[]{:S(2)}) %collective-permute-start.3) | collective-permute-done | bytes 294944 | tf_op jit(solution)/shard_map/ppermute | solution.py:22
  29.2 0.3 pad_maximum_fusion
  29.5 0.1 slice_bitcast_fusion
  29.6 0.2 divide_select_fusion.1
  29.8 0.2 fusion.149
  30.0 0.2 divide_select_fusion
  30.2 0.2 fusion.150
  30.5 0.2 divide_select_fusion.2
  30.7 1.1 %fusion.7 = (f32[22,22,256]{2,1,0:T(8,128)S(1)}, f32[22,22,256]{2,1,0:T(8,128)S(1)}, f32[22,22,256]{2,1,0:T(8,128)S(1)}) fusion(f32[24,24,256]{2,1,0:T(8,128)S(1)} %get-tuple-element.20, f32[24,24,256]{2,1,0:T(8,128)S(1)} %get-tuple-element.19, f32[22,22,255]{2,1,0:T(8,128)S(1)} %get-tuple-element.34, f32[22,22,255]{2,1,0:T(8,128)S(1)} %get-tuple-element.33, ...), kind=kLoop, calls=%fused_computation.22 | loop fusion | flops 3345408 | bytes 8423108 | tf_op jit(solution)/shard_map/add | solution.py:106
  31.8 0.2 fusion.151
  32.0 0.8 %fusion.26 = f32[20,20,256]{2,1,0:T(8,128)S(1)} fusion(f32[22,22,256]{2,1,0:T(8,128)S(1)} %get-tuple-element.15, f32[24,23,256]{2,1,0:T(8,128)S(1)} %divide_select_fusion, f32[23,24,256]{2,1,0:T(8,128)S(1)} %divide_select_fusion.1, f32[24,24,256]{2,1,0:T(8,128)S(1)} %get-tuple-element.19, f32[20,20,255]{2,1,0:T(8,128)S(1)} %get-tuple-element.38, ...), kind=kLoop, calls=%fused_computation.49 | loop fusion | flops 1740800 | bytes 6224880 | tf_op jit(solution)/shard_map/add | solution.py:106
  32.9 0.1 fusion.154
  33.0 0.5 fusion.148
  33.7 0.8 %copy-done.4 = f32[256,256]{1,0:T(8,128)S(1)} copy-done((f32[256,256]{1,0:T(8,128)S(1)}, f32[256,256]{1,0:T(8,128)}, u32[]{:S(2)}) %copy-start.4) | copy-done | bytes 262168
  34.5 1.3 %fusion.161 = f32[1280,256]{0,1:T(8,128)S(1)} fusion(f32[1280,256]{1,0:T(8,128)S(1)} %constant_dynamic-update-slice_fusion, f32[256,256]{1,0:T(8,128)S(1)} %copy-done.4), kind=kOutput, calls=%fused_computation.304 | convolution fusion | flops 1006632960 | bytes 2883584 | tf_op jit(solution)/shard_map/dot_general | solution.py:171
  35.8 0.3 convolution_bitcast_fusion.2
  36.1 0.4 fusion.11
  36.8 0.3 convolution_bitcast_fusion.1
  37.1 3.2 %collective-permute-start.4 = (f32[5,4,8,128]{3,1,2,0:T(4,128)S(1)}, f32[5,4,8,128]{3,1,2,0:T(4,128)S(1)}, u32[]{:S(2)}, u32[]{:S(2)}) collective-permute-start(f32[5,4,8,128]{3,1,2,0:T(4,128)S(1)} %convolution_bitcast_fusion.1), channel_id=1, source_target_pairs={{0,4},{4,8},{8,12},{1,5},{5,9},{9,13},{2,6},{6,10},{10,14},{3,7},{... | collective-permute-start | bytes 245768 | tf_op jit(solution)/shard_map/ppermute | solution.py:30
  40.3 1.3 %collective-permute-start.5 = (f32[5,5,8,128]{3,1,2,0:T(8,128)S(1)}, f32[5,5,8,128]{3,1,2,0:T(8,128)S(1)}, u32[]{:S(2)}, u32[]{:S(2)}) collective-permute-start(f32[5,5,8,128]{3,1,2,0:T(8,128)S(1)} %pad_maximum_fusion.9), channel_id=1, source_target_pairs={{4,0},{8,4},{12,8},{5,1},{9,5},{13,9},{6,2},{10,6},{14,10},{7,3},{... | collective-permute-start | bytes 307208 | tf_op jit(solution)/shard_map/ppermute | solution.py:30
  41.6 0.1 collective-permute-done.4
  41.8 4.5 %collective-permute-done.5 = f32[5,5,8,128]{3,1,2,0:T(8,128)S(1)} collective-permute-done((f32[5,5,8,128]{3,1,2,0:T(8,128)S(1)}, f32[5,5,8,128]{3,1,2,0:T(8,128)S(1)}, u32[]{:S(2)}, u32[]{:S(2)}) %collective-permute-start.5) | collective-permute-done | bytes 102432 | tf_op jit(solution)/shard_map/ppermute | solution.py:30
  46.4 0.1 multiply_add_fusion.1
  46.5 0.5 maximum_add_fusion
  47.1 3.2 %collective-permute-start.6 = (f32[5,24,5,128]{3,1,2,0:T(8,128)S(1)}, f32[5,24,5,128]{3,1,2,0:T(8,128)S(1)}, u32[]{:S(2)}, u32[]{:S(2)}) collective-permute-start(f32[5,24,5,128]{3,1,2,0:T(8,128)S(1)} %get-tuple-element.41), channel_id=1, source_target_pairs={{0,1},{1,2},{2,3},{4,5},{5,6},{6,7},{8,9},{9,10},{10,11},{12,13},{... | collective-permute-start | bytes 921608 | tf_op jit(solution)/shard_map/ppermute | solution.py:21
  50.2 1.9 %collective-permute-start.7 = (f32[5,24,5,128]{3,1,2,0:T(8,128)S(1)}, f32[5,24,5,128]{3,1,2,0:T(8,128)S(1)}, u32[]{:S(2)}, u32[]{:S(2)}) collective-permute-start(f32[5,24,5,128]{3,1,2,0:T(8,128)S(1)} %get-tuple-element.42), channel_id=1, source_target_pairs={{1,0},{2,1},{3,2},{5,4},{6,5},{7,6},{9,8},{10,9},{11,10},{13,12},{... | collective-permute-start | bytes 921608 | tf_op jit(solution)/shard_map/ppermute | solution.py:22
  52.2 0.6 and_convert_fusion
  52.8 1.2 %collective-permute-done.6 = f32[5,24,5,128]{3,1,2,0:T(8,128)S(1)} collective-permute-done((f32[5,24,5,128]{3,1,2,0:T(8,128)S(1)}, f32[5,24,5,128]{3,1,2,0:T(8,128)S(1)}, u32[]{:S(2)}, u32[]{:S(2)}) %collective-permute-start.6) | collective-permute-done | bytes 307232 | tf_op jit(solution)/shard_map/ppermute | solution.py:21
  54.0 4.4 %collective-permute-done.7 = f32[5,24,5,128]{3,1,2,0:T(8,128)S(1)} collective-permute-done((f32[5,24,5,128]{3,1,2,0:T(8,128)S(1)}, f32[5,24,5,128]{3,1,2,0:T(8,128)S(1)}, u32[]{:S(2)}, u32[]{:S(2)}) %collective-permute-start.7) | collective-permute-done | bytes 307232 | tf_op jit(solution)/shard_map/ppermute | solution.py:22
  58.6 0.2 fusion.62
  58.8 0.1 fusion.157
  58.9 0.3 fusion.70
  59.3 0.1 fusion.158
  59.4 0.3 fusion.81
  59.7 0.1 fusion.159
  59.8 0.2 multiply_reduce_fusion
  60.0 0.6 copy-done.1
  60.6 0.2 fusion.118
  60.8 0.2 fusion.120
  61.1 0.2 fusion.162
  61.3 0.2 fusion.122
  61.5 0.2 fusion.124
  61.7 0.3 fusion.109
  62.0 0.3 fusion.59
  62.5 1.3 %collective-permute-start.9 = (f32[2,20,256]{2,1,0:T(8,128)S(1)}, f32[2,20,256]{2,1,0:T(8,128)S(1)}, u32[]{:S(2)}, u32[]{:S(2)}) collective-permute-start(f32[2,20,256]{2,1,0:T(8,128)S(1)} %get-tuple-element.48), channel_id=1, source_target_pairs={{4,0},{8,4},{12,8},{5,1},{9,5},{13,9},{6,2},{10,6},{14,10},{7,3},{... | collective-permute-start | bytes 122888 | tf_op jit(solution)/shard_map/ppermute | solution.py:30
  63.8 0.1 fusion.163
  63.9 4.0 %collective-permute-start.8 = (f32[3,20,256]{2,1,0:T(8,128)S(1)}, f32[3,20,256]{2,1,0:T(8,128)S(1)}, u32[]{:S(2)}, u32[]{:S(2)}) collective-permute-start(f32[3,20,256]{2,1,0:T(8,128)S(1)} %pad_maximum_fusion.11), channel_id=1, source_target_pairs={{0,4},{4,8},{8,12},{1,5},{5,9},{9,13},{2,6},{6,10},{10,14},{3,7},{... | collective-permute-start | bytes 184328 | tf_op jit(solution)/shard_map/ppermute | solution.py:30
  68.0 1.3 %collective-permute-done.8 = f32[3,20,256]{2,1,0:T(8,128)S(1)} collective-permute-done((f32[3,20,256]{2,1,0:T(8,128)S(1)}, f32[3,20,256]{2,1,0:T(8,128)S(1)}, u32[]{:S(2)}, u32[]{:S(2)}) %collective-permute-start.8) | collective-permute-done | bytes 61472 | tf_op jit(solution)/shard_map/ppermute | solution.py:30
  69.3 0.1 multiply_add_fusion
  69.5 0.2 fusion.152
  69.7 0.8 %fusion.36 = f32[18,18,256]{2,1,0:T(8,128)S(1)} fusion(f32[20,20,256]{2,1,0:T(8,128)S(1)} %pad_maximum_fusion.3, f32[24,23,256]{2,1,0:T(8,128)S(1)} %divide_select_fusion, f32[2,20,256]{2,1,0:T(8,128)S(1)} %multiply_add_fusion.3, f32[16,20,256]{2,1,0:T(8,128)S(1)} %multiply_add_fusion, f32[23,24,256]{2,1,0:T(8,128)S(1)} %divide_select_fusion.1, ...), kind=kLoop, calls=%fused_computation.65 | loop fusion | flops 1575936 | bytes 4882000 | tf_op jit(solution)/shard_map/add | solution.py:106
  70.5 0.1 fusion.155
  70.6 1.1 %fusion.49 = f32[16,16,256]{2,1,0:T(8,128)} fusion(f32[18,18,256]{2,1,0:T(8,128)S(1)} %fusion.36, f32[24,24,256]{2,1,0:T(8,128)S(1)} %get-tuple-element.19, f32[16,16,255]{2,1,0:T(8,128)S(1)} %get-tuple-element.46, f32[16,16,255]{2,1,0:T(8,128)S(1)} %get-tuple-element.45, f32[24,23,256]{2,1,0:T(8,128)S(1)} %divide_select_fusion, ...), kind=kLoop, calls=%fused_computation.88 | loop fusion | flops 1114112 | bytes 4161648 | tf_op jit(solution)/shard_map/add | solution.py:106
  (86 shorter events, 2.3 us)
Async XLA Ops:
  0.0 12.5 %copy-start = (f32[16,16,256]{2,1,0:T(8,128)S(1)}, f32[16,16,256]{2,1,0:T(8,128)}, u32[]{:S(2)}) copy-start(f32[16,16,256]{2,1,0:T(8,128)} %param.12) | copy-start | bytes 786436
  0.0 12.5 %copy-start.2 = (f32[16,16,256]{2,1,0:T(8,128)S(1)}, f32[16,16,256]{2,1,0:T(8,128)}, u32[]{:S(2)}) copy-start(f32[16,16,256]{2,1,0:T(8,128)} %param.13) | copy-start | bytes 786436
  0.0 12.5 %copy-start.3 = (f32[16,16,256]{2,1,0:T(8,128)S(1)}, f32[16,16,256]{2,1,0:T(8,128)}, u32[]{:S(2)}) copy-start(f32[16,16,256]{2,1,0:T(8,128)} %param.11) | copy-start | bytes 786436
  1.1 11.5 %copy-start.9 = (s32[64]{0:T(128)S(1)}, s32[64]{0:T(128)}, u32[]{:S(2)}) copy-start(s32[64]{0:T(128)} %param.14) | copy-start | bytes 772
  1.1 7.6 %collective-permute-start = (f32[3,4,16,256]{3,2,1,0:T(8,128)S(1)}, f32[3,4,16,256]{3,2,1,0:T(8,128)S(1)}, u32[]{:S(2)}, u32[]{:S(2)}) collective-permute-start(f32[3,4,16,256]{3,2,1,0:T(8,128)S(1)} %get-tuple-element.27), channel_id=1, source_target_pairs={{0,4},{4,8},{8,12},{1,5},{5,9},{9,13},{2,6},{6,10},{10,14},{3,7},{... | collective-permute-start | bytes 589832 | tf_op jit(solution)/shard_map/ppermute | solution.py:21
  5.2 7.3 %collective-permute-start.1 = (f32[3,4,16,256]{3,2,1,0:T(8,128)S(1)}, f32[3,4,16,256]{3,2,1,0:T(8,128)S(1)}, u32[]{:S(2)}, u32[]{:S(2)}) collective-permute-start(f32[3,4,16,256]{3,2,1,0:T(8,128)S(1)} %get-tuple-element.28), channel_id=1, source_target_pairs={{4,0},{8,4},{12,8},{5,1},{9,5},{13,9},{6,2},{10,6},{14,10},{7,3},{... | collective-permute-start | bytes 589832 | tf_op jit(solution)/shard_map/ppermute | solution.py:22
  16.3 8.5 %collective-permute-start.2 = (f32[3,24,4,256]{3,2,1,0:T(4,128)S(1)}, f32[3,24,4,256]{3,2,1,0:T(4,128)S(1)}, u32[]{:S(2)}, u32[]{:S(2)}) collective-permute-start(f32[3,24,4,256]{3,2,1,0:T(4,128)S(1)} %get-tuple-element.25), channel_id=1, source_target_pairs={{0,1},{1,2},{2,3},{4,5},{5,6},{6,7},{8,9},{9,10},{10,11},{12,13},{... | collective-permute-start | bytes 884744 | tf_op jit(solution)/shard_map/ppermute | solution.py:21
  21.1 8.0 %collective-permute-start.3 = (f32[3,24,4,256]{3,2,1,0:T(4,128)S(1)}, f32[3,24,4,256]{3,2,1,0:T(4,128)S(1)}, u32[]{:S(2)}, u32[]{:S(2)}) collective-permute-start(f32[3,24,4,256]{3,2,1,0:T(4,128)S(1)} %get-tuple-element.26), channel_id=1, source_target_pairs={{1,0},{2,1},{3,2},{5,4},{6,5},{7,6},{9,8},{10,9},{11,10},{13,12},{... | collective-permute-start | bytes 884744 | tf_op jit(solution)/shard_map/ppermute | solution.py:22
  33.5 1.0 %copy-start.4 = (f32[256,256]{1,0:T(8,128)S(1)}, f32[256,256]{1,0:T(8,128)}, u32[]{:S(2)}) copy-start(f32[256,256]{1,0:T(8,128)} %constant.148) | copy-start | bytes 786436
  34.5 1.4 %copy-start.6 = (pred[136,256]{1,0:T(8,128)(4,1)S(1)}, pred[136,256]{1,0:T(8,128)(4,1)}, u32[]{:S(2)}) copy-start(pred[136,256]{1,0:T(8,128)(4,1)} %constant.50.clone) | copy-start | bytes 104452
  34.5 1.4 %copy-start.8 = (f32[136]{0:T(256)S(1)}, f32[136]{0:T(256)}, u32[]{:S(2)}) copy-start(f32[136]{0:T(256)} %constant.47.clone) | copy-start | bytes 1636
  34.5 1.7 %copy-start.10 = (pred[136,256]{1,0:T(8,128)(4,1)S(1)}, pred[136,256]{1,0:T(8,128)(4,1)}, u32[]{:S(2)}) copy-start(pred[136,256]{1,0:T(8,128)(4,1)} %constant.49.clone) | copy-start | bytes 104452
  37.1 4.7 %collective-permute-start.4 = (f32[5,4,8,128]{3,1,2,0:T(4,128)S(1)}, f32[5,4,8,128]{3,1,2,0:T(4,128)S(1)}, u32[]{:S(2)}, u32[]{:S(2)}) collective-permute-start(f32[5,4,8,128]{3,1,2,0:T(4,128)S(1)} %convolution_bitcast_fusion.1), channel_id=1, source_target_pairs={{0,4},{4,8},{8,12},{1,5},{5,9},{9,13},{2,6},{6,10},{10,14},{3,7},{... | collective-permute-start | bytes 245768 | tf_op jit(solution)/shard_map/ppermute | solution.py:30
  40.3 6.1 %collective-permute-start.5 = (f32[5,5,8,128]{3,1,2,0:T(8,128)S(1)}, f32[5,5,8,128]{3,1,2,0:T(8,128)S(1)}, u32[]{:S(2)}, u32[]{:S(2)}) collective-permute-start(f32[5,5,8,128]{3,1,2,0:T(8,128)S(1)} %pad_maximum_fusion.9), channel_id=1, source_target_pairs={{4,0},{8,4},{12,8},{5,1},{9,5},{13,9},{6,2},{10,6},{14,10},{7,3},{... | collective-permute-start | bytes 307208 | tf_op jit(solution)/shard_map/ppermute | solution.py:30
  47.1 7.0 %collective-permute-start.6 = (f32[5,24,5,128]{3,1,2,0:T(8,128)S(1)}, f32[5,24,5,128]{3,1,2,0:T(8,128)S(1)}, u32[]{:S(2)}, u32[]{:S(2)}) collective-permute-start(f32[5,24,5,128]{3,1,2,0:T(8,128)S(1)} %get-tuple-element.41), channel_id=1, source_target_pairs={{0,1},{1,2},{2,3},{4,5},{5,6},{6,7},{8,9},{9,10},{10,11},{12,13},{... | collective-permute-start | bytes 921608 | tf_op jit(solution)/shard_map/ppermute | solution.py:21
  50.2 8.2 %collective-permute-start.7 = (f32[5,24,5,128]{3,1,2,0:T(8,128)S(1)}, f32[5,24,5,128]{3,1,2,0:T(8,128)S(1)}, u32[]{:S(2)}, u32[]{:S(2)}) collective-permute-start(f32[5,24,5,128]{3,1,2,0:T(8,128)S(1)} %get-tuple-element.42), channel_id=1, source_target_pairs={{1,0},{2,1},{3,2},{5,4},{6,5},{7,6},{9,8},{10,9},{11,10},{13,12},{... | collective-permute-start | bytes 921608 | tf_op jit(solution)/shard_map/ppermute | solution.py:22
  59.7 0.9 %copy-start.1 = (f32[256,128]{1,0:T(8,128)S(1)}, f32[256,128]{1,0:T(8,128)}, u32[]{:S(2)}) copy-start(f32[256,128]{1,0:T(8,128)} %constant.45.clone) | copy-start | bytes 393220
  59.8 2.2 %copy-start.5 = (pred[256,136]{1,0:T(32,128)(4,1)S(1)}, pred[256,136]{1,0:T(32,128)(4,1)}, u32[]{:S(2)}) copy-start(pred[256,136]{1,0:T(32,128)(4,1)} %constant.48.clone) | copy-start | bytes 104452
  61.0 2.7 %copy-start.7 = (f32[20,10]{1,0:T(8,128)S(1)}, f32[20,10]{1,0:T(8,128)}, u32[]{:S(2)}) copy-start(f32[20,10]{1,0:T(8,128)} %constant.51.clone) | copy-start | bytes 2404
  62.5 5.5 %collective-permute-start.9 = (f32[2,20,256]{2,1,0:T(8,128)S(1)}, f32[2,20,256]{2,1,0:T(8,128)S(1)}, u32[]{:S(2)}, u32[]{:S(2)}) collective-permute-start(f32[2,20,256]{2,1,0:T(8,128)S(1)} %get-tuple-element.48), channel_id=1, source_target_pairs={{4,0},{8,4},{12,8},{5,1},{9,5},{13,9},{6,2},{10,6},{14,10},{7,3},{... | collective-permute-start | bytes 122888 | tf_op jit(solution)/shard_map/ppermute | solution.py:30
  63.9 5.4 %collective-permute-start.8 = (f32[3,20,256]{2,1,0:T(8,128)S(1)}, f32[3,20,256]{2,1,0:T(8,128)S(1)}, u32[]{:S(2)}, u32[]{:S(2)}) collective-permute-start(f32[3,20,256]{2,1,0:T(8,128)S(1)} %pad_maximum_fusion.11), channel_id=1, source_target_pairs={{0,4},{4,8},{8,12},{1,5},{5,9},{9,13},{2,6},{6,10},{10,14},{3,7},{... | collective-permute-start | bytes 184328 | tf_op jit(solution)/shard_map/ppermute | solution.py:30

commit v13 on v11

--- a/solution.py
+++ b/solution.py
@@ -118,9 +118,9 @@
     sides = (("slab", 0), (("pencil", "sub"), 1))
     stacked_sides = (("slab", 1), (("pencil", "sub"), 2))
     fine_rim = 2 * NU
-    ext_x = padded(jnp.stack([permeability, source, pressure]), (("slab", 1),), fine_rim)
-    ext_x, aggregate = lax.optimization_barrier((ext_x, aggregate))
-    ext_all = padded(ext_x, ((("pencil", "sub"), 2),), fine_rim)
+    ext_y = padded(jnp.stack([permeability, source, pressure]), ((("pencil", "sub"), 2),), fine_rim)
+    ext_y, aggregate = lax.optimization_barrier((ext_y, aggregate))
+    ext_all = padded(ext_y, (("slab", 1),), fine_rim)
     perm_ext = ext_all[0]
     source_ext = crop(ext_all[1], 1)
     glob_x = slab_index * width_x - fine_rim + jnp.arange(width_x + 2 * fine_rim)

time: 68.2 us -> 69.7 us (1.022)
  starting transfers between devices: 27 us -> 28.2 us
    ppermute x3, waiting for transfers between devices: 2.35 us -> 4.76 us  [padded(): before = lax.ppermute(last, axis, up)]
    ppermute x3, waiting for transfers between devices: 10.6 us -> 8.44 us  [padded(): after = lax.ppermute(leading, axis, down)]
  transfers between devices with their start and end apart: 10 -> 10, of which waited for: 8 -> 7; matrix products, arithmetic and copies ran while one was open for 5% -> 3% of each run, Pallas kernels for 0% -> 0%
where the time goes in v13:
time: 69.7 us; the launch traced here: 69.3 us
  starting transfers between devices  28.2 us (40%)
  waiting for transfers between devices  19.4 us (28%)
  other arithmetic  10 us (14%)
  matrix products  5.2 us (7%)
  between operations  3.47 us (5%)
  local copies, waits for them, and re-layouts  3.04 us (4%)
    ppermute x3, starting transfers between devices, padded(): before = lax.ppermute(last, axis, up)  12.6 us
    ppermute x4, starting transfers between devices, passed_along(): return lax.ppermute(array, axis, pairs)  10.4 us
    ppermute x3, waiting for transfers between devices, padded(): after = lax.ppermute(leading, axis, down)  8.44 us
    ppermute x4, waiting for transfers between devices, passed_along(): return lax.ppermute(array, axis, pairs)  6.2 us
    ppermute x3, starting transfers between devices, padded(): after = lax.ppermute(leading, axis, down)  5.13 us
    ppermute x3, waiting for transfers between devices, padded(): before = lax.ppermute(last, axis, up)  4.76 us
    add x4, other arithmetic, sweeps(): field_ext = center + OMEGA * (source_now - product) / faces_now[7]  3.86 us
    dot_general x5, matrix products, z_sum(): return jnp.dot(flat, pick_z, precision=lax.Precision.HIGHEST)  1.96 us
  transfers between devices with their start and end apart: 10, of which 7 were waited for; matrix products, arithmetic and copies ran while one was open for 3% of the time, Pallas kernels for 0%

profile of v13, /device:TPU:1, one launch (start us, length us, event | category | flops | bytes accessed | tf_op | source)
XLA Modules:
  0.0 69.3 jit_solution(16401999312273219129)
XLA Ops:
  0.0 1.3 %pad_maximum_fusion.7 = (f32[3,16,4,256]{3,2,1,0:T(4,128)S(1)}, f32[3,16,4,256]{3,2,1,0:T(4,128)S(1)}) fusion(f32[1,16,16,256]{3,2,1,0:T(8,128)} %bitcast.231, f32[1,16,16,256]{3,2,1,0:T(8,128)} %bitcast.224, f32[1,16,16,256]{3,2,1,0:T(8,128)} %bitcast.233), kind=kLoop, calls=%fused_computation.122 | loop fusion | flops 196608 | bytes 1179648 | tf_op jit(solution)/shard_map/slice | solution.py:19
  1.4 4.5 %collective-permute-start = (f32[3,16,4,256]{3,2,1,0:T(4,128)S(1)}, f32[3,16,4,256]{3,2,1,0:T(4,128)S(1)}, u32[]{:S(2)}, u32[]{:S(2)}) collective-permute-start(f32[3,16,4,256]{3,2,1,0:T(4,128)S(1)} %get-tuple-element.23), channel_id=1, source_target_pairs={{0,1},{1,2},{2,3},{4,5},{5,6},{6,7},{8,9},{9,10},{10,11},{12,13},{... | collective-permute-start | bytes 589832 | tf_op jit(solution)/shard_map/ppermute | solution.py:21
  5.9 1.9 %collective-permute-start.1 = (f32[3,16,4,256]{3,2,1,0:T(4,128)S(1)}, f32[3,16,4,256]{3,2,1,0:T(4,128)S(1)}, u32[]{:S(2)}, u32[]{:S(2)}) collective-permute-start(f32[3,16,4,256]{3,2,1,0:T(4,128)S(1)} %get-tuple-element.24), channel_id=1, source_target_pairs={{1,0},{2,1},{3,2},{5,4},{6,5},{7,6},{9,8},{10,9},{11,10},{13,12},{... | collective-permute-start | bytes 589832 | tf_op jit(solution)/shard_map/ppermute | solution.py:22
  8.8 4.0 %collective-permute-done.1 = f32[3,16,4,256]{3,2,1,0:T(4,128)S(1)} collective-permute-done((f32[3,16,4,256]{3,2,1,0:T(4,128)S(1)}, f32[3,16,4,256]{3,2,1,0:T(4,128)S(1)}, u32[]{:S(2)}, u32[]{:S(2)}) %collective-permute-start.1) | collective-permute-done | bytes 196640 | tf_op jit(solution)/shard_map/ppermute | solution.py:22
  12.9 0.2 pad_maximum_fusion
  13.1 0.2 select_reduce_fusion
  13.3 0.7 fusion.158
  16.8 1.3 %collective-permute-start.3 = (f32[3,4,24,256]{3,2,1,0:T(8,128)S(1)}, f32[3,4,24,256]{3,2,1,0:T(8,128)S(1)}, u32[]{:S(2)}, u32[]{:S(2)}) collective-permute-start(f32[3,4,24,256]{3,2,1,0:T(8,128)S(1)} %get-tuple-element.21), channel_id=1, source_target_pairs={{4,0},{8,4},{12,8},{5,1},{9,5},{13,9},{6,2},{10,6},{14,10},{7,3},{... | collective-permute-start | bytes 884744 | tf_op jit(solution)/shard_map/ppermute | solution.py:22
  18.1 4.0 %collective-permute-start.2 = (f32[3,4,24,256]{3,2,1,0:T(8,128)S(1)}, f32[3,4,24,256]{3,2,1,0:T(8,128)S(1)}, u32[]{:S(2)}, u32[]{:S(2)}) collective-permute-start(f32[3,4,24,256]{3,2,1,0:T(8,128)S(1)} %get-tuple-element.22), channel_id=1, source_target_pairs={{0,4},{4,8},{8,12},{1,5},{5,9},{9,13},{2,6},{6,10},{10,14},{3,7},{... | collective-permute-start | bytes 884744 | tf_op jit(solution)/shard_map/ppermute | solution.py:21
  22.2 0.1 eq.154
  22.3 3.7 %collective-permute-done.2 = f32[3,4,24,256]{3,2,1,0:T(8,128)S(1)} collective-permute-done((f32[3,4,24,256]{3,2,1,0:T(8,128)S(1)}, f32[3,4,24,256]{3,2,1,0:T(8,128)S(1)}, u32[]{:S(2)}, u32[]{:S(2)}) %collective-permute-start.2) | collective-permute-done | bytes 294944 | tf_op jit(solution)/shard_map/ppermute | solution.py:21
  26.1 0.1 slice_bitcast_fusion
  26.3 0.2 divide_select_fusion.1
  26.4 0.2 fusion.147
  26.7 0.2 divide_select_fusion
  26.9 0.4 fusion.148
  27.3 1.1 %fusion.7 = (f32[22,22,256]{2,1,0:T(8,128)S(1)}, f32[22,22,256]{2,1,0:T(8,128)S(1)}, f32[22,22,256]{2,1,0:T(8,128)S(1)}) fusion(f32[24,24,256]{2,1,0:T(8,128)S(1)} %get-tuple-element.20, f32[24,24,256]{2,1,0:T(8,128)S(1)} %get-tuple-element.19, f32[22,22,255]{2,1,0:T(8,128)S(1)} %get-tuple-element.30, f32[22,22,255]{2,1,0:T(8,128)S(1)} %get-tuple-element.29, ...), kind=kLoop, calls=%fused_computation.21 | loop fusion | flops 3345408 | bytes 8423108 | tf_op jit(solution)/shard_map/add | solution.py:106
  28.4 0.2 fusion.149
  28.6 0.8 %fusion.26 = f32[20,20,256]{2,1,0:T(8,128)S(1)} fusion(f32[22,22,256]{2,1,0:T(8,128)S(1)} %get-tuple-element.15, f32[24,23,256]{2,1,0:T(8,128)S(1)} %divide_select_fusion, f32[23,24,256]{2,1,0:T(8,128)S(1)} %divide_select_fusion.1, f32[24,24,256]{2,1,0:T(8,128)S(1)} %get-tuple-element.19, f32[20,20,255]{2,1,0:T(8,128)S(1)} %get-tuple-element.34, ...), kind=kLoop, calls=%fused_computation.48 | loop fusion | flops 1740800 | bytes 6224880 | tf_op jit(solution)/shard_map/add | solution.py:106
  29.4 0.1 fusion.152
  29.6 0.4 fusion.162
  30.0 0.5 fusion.146
  30.5 0.4 fusion.163
  30.9 0.4 fusion.159
  31.3 0.4 fusion.160
  31.7 0.4 fusion.161
  32.2 0.4 fusion.11
  32.7 0.3 convolution_bitcast_fusion.2
  33.1 0.3 convolution_bitcast_fusion.1
  33.4 3.8 %collective-permute-start.4 = (f32[5,4,8,128]{3,1,2,0:T(4,128)S(1)}, f32[5,4,8,128]{3,1,2,0:T(4,128)S(1)}, u32[]{:S(2)}, u32[]{:S(2)}) collective-permute-start(f32[5,4,8,128]{3,1,2,0:T(4,128)S(1)} %convolution_bitcast_fusion.1), channel_id=1, source_target_pairs={{0,4},{4,8},{8,12},{1,5},{5,9},{9,13},{2,6},{6,10},{10,14},{3,7},{... | collective-permute-start | bytes 245768 | tf_op jit(solution)/shard_map/ppermute | solution.py:30
  37.2 1.3 %collective-permute-start.5 = (f32[5,5,8,128]{3,1,2,0:T(8,128)S(1)}, f32[5,5,8,128]{3,1,2,0:T(8,128)S(1)}, u32[]{:S(2)}, u32[]{:S(2)}) collective-permute-start(f32[5,5,8,128]{3,1,2,0:T(8,128)S(1)} %pad_maximum_fusion.8), channel_id=1, source_target_pairs={{4,0},{8,4},{12,8},{5,1},{9,5},{13,9},{6,2},{10,6},{14,10},{7,3},{... | collective-permute-start | bytes 307208 | tf_op jit(solution)/shard_map/ppermute | solution.py:30
  38.5 0.1 collective-permute-done.4
  38.7 0.1 multiply_add_fusion.2
  38.8 4.7 %collective-permute-done.5 = f32[5,5,8,128]{3,1,2,0:T(8,128)S(1)} collective-permute-done((f32[5,5,8,128]{3,1,2,0:T(8,128)S(1)}, f32[5,5,8,128]{3,1,2,0:T(8,128)S(1)}, u32[]{:S(2)}, u32[]{:S(2)}) %collective-permute-start.5) | collective-permute-done | bytes 102432 | tf_op jit(solution)/shard_map/ppermute | solution.py:30
  43.6 0.1 multiply_add_fusion.1
  43.7 0.5 maximum_add_fusion
  44.2 4.1 %collective-permute-start.6 = (f32[5,24,5,128]{3,1,2,0:T(8,128)S(1)}, f32[5,24,5,128]{3,1,2,0:T(8,128)S(1)}, u32[]{:S(2)}, u32[]{:S(2)}) collective-permute-start(f32[5,24,5,128]{3,1,2,0:T(8,128)S(1)} %get-tuple-element.37), channel_id=1, source_target_pairs={{0,1},{1,2},{2,3},{4,5},{5,6},{6,7},{8,9},{9,10},{10,11},{12,13},{... | collective-permute-start | bytes 921608 | tf_op jit(solution)/shard_map/ppermute | solution.py:21
  48.4 1.9 %collective-permute-start.7 = (f32[5,24,5,128]{3,1,2,0:T(8,128)S(1)}, f32[5,24,5,128]{3,1,2,0:T(8,128)S(1)}, u32[]{:S(2)}, u32[]{:S(2)}) collective-permute-start(f32[5,24,5,128]{3,1,2,0:T(8,128)S(1)} %get-tuple-element.38), channel_id=1, source_target_pairs={{1,0},{2,1},{3,2},{5,4},{6,5},{7,6},{9,8},{10,9},{11,10},{13,12},{... | collective-permute-start | bytes 921608 | tf_op jit(solution)/shard_map/ppermute | solution.py:22
  50.3 0.7 %and_convert_fusion = f32[2]{0:T(128)S(1)} fusion(s32[19]{0:T(128)S(1)} %iota_add_fusion, f32[19]{0:T(128)S(1)} %select_reduce_fusion, f32[]{:T(128)} %bitcast.21), kind=kLoop, calls=%fused_computation.249 | loop fusion | flops 8 | bytes 28 | tf_op jit(solution)/shard_map/convert_element_type | solution.py:295
  51.0 1.1 %collective-permute-done.6 = f32[5,24,5,128]{3,1,2,0:T(8,128)S(1)} collective-permute-done((f32[5,24,5,128]{3,1,2,0:T(8,128)S(1)}, f32[5,24,5,128]{3,1,2,0:T(8,128)S(1)}, u32[]{:S(2)}, u32[]{:S(2)}) %collective-permute-start.6) | collective-permute-done | bytes 307232 | tf_op jit(solution)/shard_map/ppermute | solution.py:21
  52.1 4.4 %collective-permute-done.7 = f32[5,24,5,128]{3,1,2,0:T(8,128)S(1)} collective-permute-done((f32[5,24,5,128]{3,1,2,0:T(8,128)S(1)}, f32[5,24,5,128]{3,1,2,0:T(8,128)S(1)}, u32[]{:S(2)}, u32[]{:S(2)}) %collective-permute-start.7) | collective-permute-done | bytes 307232 | tf_op jit(solution)/shard_map/ppermute | solution.py:22
  56.7 0.2 fusion.62
  56.9 0.1 fusion.155
  57.0 0.3 fusion.70
  57.4 0.1 fusion.156
  57.5 0.3 fusion.81
  57.8 0.1 fusion.157
  57.9 0.2 multiply_reduce_fusion
  58.1 0.2 fusion.117
  58.3 0.2 fusion.119
  58.6 0.2 fusion.164
  58.8 0.2 fusion.121
  59.0 0.2 fusion.123
  59.2 0.3 fusion.108
  59.5 0.3 fusion.59
  60.0 1.3 %collective-permute-start.9 = (f32[2,20,256]{2,1,0:T(8,128)S(1)}, f32[2,20,256]{2,1,0:T(8,128)S(1)}, u32[]{:S(2)}, u32[]{:S(2)}) collective-permute-start(f32[2,20,256]{2,1,0:T(8,128)S(1)} %get-tuple-element.44), channel_id=1, source_target_pairs={{4,0},{8,4},{12,8},{5,1},{9,5},{13,9},{6,2},{10,6},{14,10},{7,3},{... | collective-permute-start | bytes 122888 | tf_op jit(solution)/shard_map/ppermute | solution.py:30
  61.3 0.1 fusion.165
  61.4 4.0 %collective-permute-start.8 = (f32[3,20,256]{2,1,0:T(8,128)S(1)}, f32[3,20,256]{2,1,0:T(8,128)S(1)}, u32[]{:S(2)}, u32[]{:S(2)}) collective-permute-start(f32[3,20,256]{2,1,0:T(8,128)S(1)} %pad_maximum_fusion.10), channel_id=1, source_target_pairs={{0,4},{4,8},{8,12},{1,5},{5,9},{9,13},{2,6},{6,10},{10,14},{3,7},{... | collective-permute-start | bytes 184328 | tf_op jit(solution)/shard_map/ppermute | solution.py:30
  65.5 1.3 %collective-permute-done.8 = f32[3,20,256]{2,1,0:T(8,128)S(1)} collective-permute-done((f32[3,20,256]{2,1,0:T(8,128)S(1)}, f32[3,20,256]{2,1,0:T(8,128)S(1)}, u32[]{:S(2)}, u32[]{:S(2)}) %collective-permute-start.8) | collective-permute-done | bytes 61472 | tf_op jit(solution)/shard_map/ppermute | solution.py:30
  66.8 0.1 multiply_add_fusion
  67.0 0.2 fusion.150
  67.2 0.8 %fusion.36 = f32[18,18,256]{2,1,0:T(8,128)S(1)} fusion(f32[20,20,256]{2,1,0:T(8,128)S(1)} %pad_maximum_fusion.2, f32[24,23,256]{2,1,0:T(8,128)S(1)} %divide_select_fusion, f32[2,20,256]{2,1,0:T(8,128)S(1)} %multiply_add_fusion.3, f32[16,20,256]{2,1,0:T(8,128)S(1)} %multiply_add_fusion, f32[23,24,256]{2,1,0:T(8,128)S(1)} %divide_select_fusion.1, ...), kind=kLoop, calls=%fused_computation.64 | loop fusion | flops 1575936 | bytes 4882000 | tf_op jit(solution)/shard_map/add | solution.py:106
  68.0 0.1 fusion.153
  68.1 1.1 %fusion.49 = f32[16,16,256]{2,1,0:T(8,128)} fusion(f32[18,18,256]{2,1,0:T(8,128)S(1)} %fusion.36, f32[24,24,256]{2,1,0:T(8,128)S(1)} %get-tuple-element.19, f32[16,16,255]{2,1,0:T(8,128)S(1)} %get-tuple-element.42, f32[16,16,255]{2,1,0:T(8,128)S(1)} %get-tuple-element.41, f32[24,23,256]{2,1,0:T(8,128)S(1)} %divide_select_fusion, ...), kind=kLoop, calls=%fused_computation.87 | loop fusion | flops 1114112 | bytes 4161648 | tf_op jit(solution)/shard_map/add | solution.py:106
  (86 shorter events, 2.1 us)
Async XLA Ops:
  0.0 12.9 %copy-start.1 = (f32[16,16,256]{2,1,0:T(8,128)S(1)}, f32[16,16,256]{2,1,0:T(8,128)}, u32[]{:S(2)}) copy-start(f32[16,16,256]{2,1,0:T(8,128)} %param.12) | copy-start | bytes 786436
  0.0 12.9 %copy-start.2 = (f32[16,16,256]{2,1,0:T(8,128)S(1)}, f32[16,16,256]{2,1,0:T(8,128)}, u32[]{:S(2)}) copy-start(f32[16,16,256]{2,1,0:T(8,128)} %param.13) | copy-start | bytes 786436
  0.0 12.9 %copy-start.3 = (f32[16,16,256]{2,1,0:T(8,128)S(1)}, f32[16,16,256]{2,1,0:T(8,128)}, u32[]{:S(2)}) copy-start(f32[16,16,256]{2,1,0:T(8,128)} %param.11) | copy-start | bytes 786436
  1.4 7.5 %collective-permute-start = (f32[3,16,4,256]{3,2,1,0:T(4,128)S(1)}, f32[3,16,4,256]{3,2,1,0:T(4,128)S(1)}, u32[]{:S(2)}, u32[]{:S(2)}) collective-permute-start(f32[3,16,4,256]{3,2,1,0:T(4,128)S(1)} %get-tuple-element.23), channel_id=1, source_target_pairs={{0,1},{1,2},{2,3},{4,5},{5,6},{6,7},{8,9},{9,10},{10,11},{12,13},{... | collective-permute-start | bytes 589832 | tf_op jit(solution)/shard_map/ppermute | solution.py:21
  5.9 7.0 %collective-permute-start.1 = (f32[3,16,4,256]{3,2,1,0:T(4,128)S(1)}, f32[3,16,4,256]{3,2,1,0:T(4,128)S(1)}, u32[]{:S(2)}, u32[]{:S(2)}) collective-permute-start(f32[3,16,4,256]{3,2,1,0:T(4,128)S(1)} %get-tuple-element.24), channel_id=1, source_target_pairs={{1,0},{2,1},{3,2},{5,4},{6,5},{7,6},{9,8},{10,9},{11,10},{13,12},{... | collective-permute-start | bytes 589832 | tf_op jit(solution)/shard_map/ppermute | solution.py:22
  8.8 4.3 %copy-start.9 = (s32[64]{0:T(128)S(1)}, s32[64]{0:T(128)}, u32[]{:S(2)}) copy-start(s32[64]{0:T(128)} %param.14) | copy-start | bytes 772
  16.8 9.3 %collective-permute-start.3 = (f32[3,4,24,256]{3,2,1,0:T(8,128)S(1)}, f32[3,4,24,256]{3,2,1,0:T(8,128)S(1)}, u32[]{:S(2)}, u32[]{:S(2)}) collective-permute-start(f32[3,4,24,256]{3,2,1,0:T(8,128)S(1)} %get-tuple-element.21), channel_id=1, source_target_pairs={{4,0},{8,4},{12,8},{5,1},{9,5},{13,9},{6,2},{10,6},{14,10},{7,3},{... | collective-permute-start | bytes 884744 | tf_op jit(solution)/shard_map/ppermute | solution.py:22
  18.1 7.9 %collective-permute-start.2 = (f32[3,4,24,256]{3,2,1,0:T(8,128)S(1)}, f32[3,4,24,256]{3,2,1,0:T(8,128)S(1)}, u32[]{:S(2)}, u32[]{:S(2)}) collective-permute-start(f32[3,4,24,256]{3,2,1,0:T(8,128)S(1)} %get-tuple-element.22), channel_id=1, source_target_pairs={{0,4},{4,8},{8,12},{1,5},{5,9},{9,13},{2,6},{6,10},{10,14},{3,7},{... | collective-permute-start | bytes 884744 | tf_op jit(solution)/shard_map/ppermute | solution.py:21
  28.6 1.0 %copy-start = (f32[256,128]{1,0:T(8,128)S(1)}, f32[256,128]{1,0:T(8,128)}, u32[]{:S(2)}) copy-start(f32[256,128]{1,0:T(8,128)} %constant.45.clone) | copy-start | bytes 393220
  30.5 1.2 %copy-start.4 = (f32[256,128]{1,0:T(8,128)S(1)}, f32[256,128]{1,0:T(8,128)}, u32[]{:S(2)}) copy-start(f32[256,128]{1,0:T(8,128)} %constant.46.clone) | copy-start | bytes 393220
  30.5 1.6 %copy-start.8 = (f32[136]{0:T(256)S(1)}, f32[136]{0:T(256)}, u32[]{:S(2)}) copy-start(f32[136]{0:T(256)} %constant.47.clone) | copy-start | bytes 1636
  30.5 1.6 %copy-start.10 = (pred[136,256]{1,0:T(8,128)(4,1)S(1)}, pred[136,256]{1,0:T(8,128)(4,1)}, u32[]{:S(2)}) copy-start(pred[136,256]{1,0:T(8,128)(4,1)} %constant.49.clone) | copy-start | bytes 104452
  31.7 0.9 %copy-start.6 = (pred[136,256]{1,0:T(8,128)(4,1)S(1)}, pred[136,256]{1,0:T(8,128)(4,1)}, u32[]{:S(2)}) copy-start(pred[136,256]{1,0:T(8,128)(4,1)} %constant.50.clone) | copy-start | bytes 104452
  33.4 5.3 %collective-permute-start.4 = (f32[5,4,8,128]{3,1,2,0:T(4,128)S(1)}, f32[5,4,8,128]{3,1,2,0:T(4,128)S(1)}, u32[]{:S(2)}, u32[]{:S(2)}) collective-permute-start(f32[5,4,8,128]{3,1,2,0:T(4,128)S(1)} %convolution_bitcast_fusion.1), channel_id=1, source_target_pairs={{0,4},{4,8},{8,12},{1,5},{5,9},{9,13},{2,6},{6,10},{10,14},{3,7},{... | collective-permute-start | bytes 245768 | tf_op jit(solution)/shard_map/ppermute | solution.py:30
  37.2 6.3 %collective-permute-start.5 = (f32[5,5,8,128]{3,1,2,0:T(8,128)S(1)}, f32[5,5,8,128]{3,1,2,0:T(8,128)S(1)}, u32[]{:S(2)}, u32[]{:S(2)}) collective-permute-start(f32[5,5,8,128]{3,1,2,0:T(8,128)S(1)} %pad_maximum_fusion.8), channel_id=1, source_target_pairs={{4,0},{8,4},{12,8},{5,1},{9,5},{13,9},{6,2},{10,6},{14,10},{7,3},{... | collective-permute-start | bytes 307208 | tf_op jit(solution)/shard_map/ppermute | solution.py:30
  44.2 7.9 %collective-permute-start.6 = (f32[5,24,5,128]{3,1,2,0:T(8,128)S(1)}, f32[5,24,5,128]{3,1,2,0:T(8,128)S(1)}, u32[]{:S(2)}, u32[]{:S(2)}) collective-permute-start(f32[5,24,5,128]{3,1,2,0:T(8,128)S(1)} %get-tuple-element.37), channel_id=1, source_target_pairs={{0,1},{1,2},{2,3},{4,5},{5,6},{6,7},{8,9},{9,10},{10,11},{12,13},{... | collective-permute-start | bytes 921608 | tf_op jit(solution)/shard_map/ppermute | solution.py:21
  48.4 8.2 %collective-permute-start.7 = (f32[5,24,5,128]{3,1,2,0:T(8,128)S(1)}, f32[5,24,5,128]{3,1,2,0:T(8,128)S(1)}, u32[]{:S(2)}, u32[]{:S(2)}) collective-permute-start(f32[5,24,5,128]{3,1,2,0:T(8,128)S(1)} %get-tuple-element.38), channel_id=1, source_target_pairs={{1,0},{2,1},{3,2},{5,4},{6,5},{7,6},{9,8},{10,9},{11,10},{13,12},{... | collective-permute-start | bytes 921608 | tf_op jit(solution)/shard_map/ppermute | solution.py:22
  57.9 1.6 %copy-start.5 = (pred[256,136]{1,0:T(32,128)(4,1)S(1)}, pred[256,136]{1,0:T(32,128)(4,1)}, u32[]{:S(2)}) copy-start(pred[256,136]{1,0:T(32,128)(4,1)} %constant.48.clone) | copy-start | bytes 104452
  58.8 2.5 %copy-start.7 = (f32[20,10]{1,0:T(8,128)S(1)}, f32[20,10]{1,0:T(8,128)}, u32[]{:S(2)}) copy-start(f32[20,10]{1,0:T(8,128)} %constant.51.clone) | copy-start | bytes 2404
  60.0 5.5 %collective-permute-start.9 = (f32[2,20,256]{2,1,0:T(8,128)S(1)}, f32[2,20,256]{2,1,0:T(8,128)S(1)}, u32[]{:S(2)}, u32[]{:S(2)}) collective-permute-start(f32[2,20,256]{2,1,0:T(8,128)S(1)} %get-tuple-element.44), channel_id=1, source_target_pairs={{4,0},{8,4},{12,8},{5,1},{9,5},{13,9},{6,2},{10,6},{14,10},{7,3},{... | collective-permute-start | bytes 122888 | tf_op jit(solution)/shard_map/ppermute | solution.py:30
  61.4 5.4 %collective-permute-start.8 = (f32[3,20,256]{2,1,0:T(8,128)S(1)}, f32[3,20,256]{2,1,0:T(8,128)S(1)}, u32[]{:S(2)}, u32[]{:S(2)}) collective-permute-start(f32[3,20,256]{2,1,0:T(8,128)S(1)} %pad_maximum_fusion.10), channel_id=1, source_target_pairs={{0,4},{4,8},{8,12},{1,5},{5,9},{9,13},{2,6},{6,10},{10,14},{3,7},{... | collective-permute-start | bytes 184328 | tf_op jit(solution)/shard_map/ppermute | solution.py:30

commit v14 on v11

--- a/solution.py
+++ b/solution.py
@@ -159,7 +159,7 @@
 
     def z_sum(block_in, pick_z):
         flat = block_in.reshape(cells, depth_cells)
-        return jnp.dot(flat, pick_z, precision=lax.Precision.HIGHEST)
+        return jnp.dot(flat, pick_z, precision=lax.Precision.HIGH)
 
     z_parts = jnp.stack(
         [

time: 68.2 us -> 67.7 us (level)
  no operation moved by 1% of the time
where the time goes in v14:
time: 67.7 us; the launch traced here: 67.3 us
  starting transfers between devices  27 us (40%)
  waiting for transfers between devices  19 us (28%)
  other arithmetic  9.81 us (14%)
  matrix products  4.72 us (7%)
  local copies, waits for them, and re-layouts  3.57 us (5%)
  between operations  3.24 us (5%)
    ppermute x3, starting transfers between devices, padded(): before = lax.ppermute(last, axis, up)  12.1 us
    ppermute x3, waiting for transfers between devices, padded(): after = lax.ppermute(leading, axis, down)  10.6 us
    ppermute x4, starting transfers between devices, passed_along(): return lax.ppermute(array, axis, pairs)  9.79 us
    ppermute x4, waiting for transfers between devices, passed_along(): return lax.ppermute(array, axis, pairs)  5.98 us
    ppermute x3, starting transfers between devices, padded(): after = lax.ppermute(leading, axis, down)  5.13 us
    add x4, other arithmetic, sweeps(): field_ext = center + OMEGA * (source_now - product) / faces_now[7]  3.86 us
    ppermute x3, waiting for transfers between devices, padded(): before = lax.ppermute(last, axis, up)  2.35 us
    dot_general x5, matrix products, z_sum(): return jnp.dot(flat, pick_z, precision=lax.Precision.HIGH)  1.48 us
  transfers between devices with their start and end apart: 10, of which 8 were waited for; matrix products, arithmetic and copies ran while one was open for 5% of the time, Pallas kernels for 0%

profile of v14, /device:TPU:1, one launch (start us, length us, event | category | flops | bytes accessed | tf_op | source)
XLA Modules:
  0.0 67.3 jit_solution(14326401471048451914)
XLA Ops:
  0.0 1.1 %pad_maximum_fusion.8 = (f32[3,4,16,256]{3,2,1,0:T(8,128)S(1)}, f32[3,4,16,256]{3,2,1,0:T(8,128)S(1)}) fusion(f32[1,16,16,256]{3,2,1,0:T(8,128)} %bitcast.231, f32[1,16,16,256]{3,2,1,0:T(8,128)} %bitcast.224, f32[1,16,16,256]{3,2,1,0:T(8,128)} %bitcast.233), kind=kLoop, calls=%fused_computation.123 | loop fusion | flops 196608 | bytes 1179648 | tf_op jit(solution)/shard_map/slice | solution.py:19
  1.1 4.0 %collective-permute-start = (f32[3,4,16,256]{3,2,1,0:T(8,128)S(1)}, f32[3,4,16,256]{3,2,1,0:T(8,128)S(1)}, u32[]{:S(2)}, u32[]{:S(2)}) collective-permute-start(f32[3,4,16,256]{3,2,1,0:T(8,128)S(1)} %get-tuple-element.23), channel_id=1, source_target_pairs={{0,4},{4,8},{8,12},{1,5},{5,9},{9,13},{2,6},{6,10},{10,14},{3,7},{... | collective-permute-start | bytes 589832 | tf_op jit(solution)/shard_map/ppermute | solution.py:21
  5.2 1.3 %collective-permute-start.1 = (f32[3,4,16,256]{3,2,1,0:T(8,128)S(1)}, f32[3,4,16,256]{3,2,1,0:T(8,128)S(1)}, u32[]{:S(2)}, u32[]{:S(2)}) collective-permute-start(f32[3,4,16,256]{3,2,1,0:T(8,128)S(1)} %get-tuple-element.24), channel_id=1, source_target_pairs={{4,0},{8,4},{12,8},{5,1},{9,5},{13,9},{6,2},{10,6},{14,10},{7,3},{... | collective-permute-start | bytes 589832 | tf_op jit(solution)/shard_map/ppermute | solution.py:22
  7.4 1.3 %collective-permute-done = f32[3,4,16,256]{3,2,1,0:T(8,128)S(1)} collective-permute-done((f32[3,4,16,256]{3,2,1,0:T(8,128)S(1)}, f32[3,4,16,256]{3,2,1,0:T(8,128)S(1)}, u32[]{:S(2)}, u32[]{:S(2)}) %collective-permute-start) | collective-permute-done | bytes 196640 | tf_op jit(solution)/shard_map/ppermute | solution.py:21
  8.7 3.8 %collective-permute-done.1 = f32[3,4,16,256]{3,2,1,0:T(8,128)S(1)} collective-permute-done((f32[3,4,16,256]{3,2,1,0:T(8,128)S(1)}, f32[3,4,16,256]{3,2,1,0:T(8,128)S(1)}, u32[]{:S(2)}, u32[]{:S(2)}) %collective-permute-start.1) | collective-permute-done | bytes 196640 | tf_op jit(solution)/shard_map/ppermute | solution.py:22
  12.6 0.1 fusion.145
  12.7 4.9 %collective-permute-start.2 = (f32[3,24,4,256]{3,2,1,0:T(4,128)S(1)}, f32[3,24,4,256]{3,2,1,0:T(4,128)S(1)}, u32[]{:S(2)}, u32[]{:S(2)}) collective-permute-start(f32[3,24,4,256]{3,2,1,0:T(4,128)S(1)} %get-tuple-element.21), channel_id=1, source_target_pairs={{0,1},{1,2},{2,3},{4,5},{5,6},{6,7},{8,9},{9,10},{10,11},{12,13},{... | collective-permute-start | bytes 884744 | tf_op jit(solution)/shard_map/ppermute | solution.py:21
  17.6 1.9 %collective-permute-start.3 = (f32[3,24,4,256]{3,2,1,0:T(4,128)S(1)}, f32[3,24,4,256]{3,2,1,0:T(4,128)S(1)}, u32[]{:S(2)}, u32[]{:S(2)}) collective-permute-start(f32[3,24,4,256]{3,2,1,0:T(4,128)S(1)} %get-tuple-element.22), channel_id=1, source_target_pairs={{1,0},{2,1},{3,2},{5,4},{6,5},{7,6},{9,8},{10,9},{11,10},{13,12},{... | collective-permute-start | bytes 884744 | tf_op jit(solution)/shard_map/ppermute | solution.py:22
  19.6 0.2 select_reduce_fusion
  19.7 0.7 fusion.158
  23.2 2.4 %collective-permute-done.3 = f32[3,24,4,256]{3,2,1,0:T(4,128)S(1)} collective-permute-done((f32[3,24,4,256]{3,2,1,0:T(4,128)S(1)}, f32[3,24,4,256]{3,2,1,0:T(4,128)S(1)}, u32[]{:S(2)}, u32[]{:S(2)}) %collective-permute-start.3) | collective-permute-done | bytes 294944 | tf_op jit(solution)/shard_map/ppermute | solution.py:22
  25.7 0.3 pad_maximum_fusion
  25.9 0.1 slice_bitcast_fusion
  26.1 0.2 fusion.147
  26.3 0.2 divide_select_fusion
  26.5 0.2 divide_select_fusion.1
  26.7 0.2 fusion.148
  26.9 0.2 divide_select_fusion.2
  27.2 1.1 %fusion.7 = (f32[22,22,256]{2,1,0:T(8,128)S(1)}, f32[22,22,256]{2,1,0:T(8,128)S(1)}, f32[22,22,256]{2,1,0:T(8,128)S(1)}) fusion(f32[24,24,256]{2,1,0:T(8,128)S(1)} %get-tuple-element.20, f32[24,24,256]{2,1,0:T(8,128)S(1)} %get-tuple-element.19, f32[22,22,255]{2,1,0:T(8,128)S(1)} %get-tuple-element.30, f32[22,22,255]{2,1,0:T(8,128)S(1)} %get-tuple-element.29, ...), kind=kLoop, calls=%fused_computation.22 | loop fusion | flops 3345408 | bytes 8423108 | tf_op jit(solution)/shard_map/add | solution.py:106
  28.3 0.2 fusion.149
  28.5 0.8 %fusion.26 = f32[20,20,256]{2,1,0:T(8,128)S(1)} fusion(f32[22,22,256]{2,1,0:T(8,128)S(1)} %get-tuple-element.15, f32[24,23,256]{2,1,0:T(8,128)S(1)} %divide_select_fusion, f32[23,24,256]{2,1,0:T(8,128)S(1)} %divide_select_fusion.1, f32[24,24,256]{2,1,0:T(8,128)S(1)} %get-tuple-element.19, f32[20,20,255]{2,1,0:T(8,128)S(1)} %get-tuple-element.34, ...), kind=kLoop, calls=%fused_computation.49 | loop fusion | flops 1740800 | bytes 6224880 | tf_op jit(solution)/shard_map/add | solution.py:106
  29.3 0.1 fusion.152
  29.4 0.5 fusion.146
  29.9 0.4 copy-done
  30.3 0.3 fusion.163
  30.6 0.3 fusion.159
  31.0 0.3 fusion.160
  31.3 0.3 fusion.162
  31.7 0.3 fusion.161
  32.0 0.4 fusion.11
  32.5 0.3 convolution_bitcast_fusion.2
  33.0 0.3 convolution_bitcast_fusion.1
  33.2 3.2 %collective-permute-start.4 = (f32[5,4,8,128]{3,1,2,0:T(4,128)S(1)}, f32[5,4,8,128]{3,1,2,0:T(4,128)S(1)}, u32[]{:S(2)}, u32[]{:S(2)}) collective-permute-start(f32[5,4,8,128]{3,1,2,0:T(4,128)S(1)} %convolution_bitcast_fusion.1), channel_id=1, source_target_pairs={{0,4},{4,8},{8,12},{1,5},{5,9},{9,13},{2,6},{6,10},{10,14},{3,7},{... | collective-permute-start | bytes 245768 | tf_op jit(solution)/shard_map/ppermute | solution.py:30
  36.5 1.3 %collective-permute-start.5 = (f32[5,5,8,128]{3,1,2,0:T(8,128)S(1)}, f32[5,5,8,128]{3,1,2,0:T(8,128)S(1)}, u32[]{:S(2)}, u32[]{:S(2)}) collective-permute-start(f32[5,5,8,128]{3,1,2,0:T(8,128)S(1)} %pad_maximum_fusion.9), channel_id=1, source_target_pairs={{4,0},{8,4},{12,8},{5,1},{9,5},{13,9},{6,2},{10,6},{14,10},{7,3},{... | collective-permute-start | bytes 307208 | tf_op jit(solution)/shard_map/ppermute | solution.py:30
  37.8 0.1 collective-permute-done.4
  38.0 4.5 %collective-permute-done.5 = f32[5,5,8,128]{3,1,2,0:T(8,128)S(1)} collective-permute-done((f32[5,5,8,128]{3,1,2,0:T(8,128)S(1)}, f32[5,5,8,128]{3,1,2,0:T(8,128)S(1)}, u32[]{:S(2)}, u32[]{:S(2)}) %collective-permute-start.5) | collective-permute-done | bytes 102432 | tf_op jit(solution)/shard_map/ppermute | solution.py:30
  42.5 0.1 multiply_add_fusion.1
  42.6 0.5 maximum_add_fusion
  43.2 3.2 %collective-permute-start.6 = (f32[5,24,5,128]{3,1,2,0:T(8,128)S(1)}, f32[5,24,5,128]{3,1,2,0:T(8,128)S(1)}, u32[]{:S(2)}, u32[]{:S(2)}) collective-permute-start(f32[5,24,5,128]{3,1,2,0:T(8,128)S(1)} %get-tuple-element.37), channel_id=1, source_target_pairs={{0,1},{1,2},{2,3},{4,5},{5,6},{6,7},{8,9},{9,10},{10,11},{12,13},{... | collective-permute-start | bytes 921608 | tf_op jit(solution)/shard_map/ppermute | solution.py:21
  46.4 1.9 %collective-permute-start.7 = (f32[5,24,5,128]{3,1,2,0:T(8,128)S(1)}, f32[5,24,5,128]{3,1,2,0:T(8,128)S(1)}, u32[]{:S(2)}, u32[]{:S(2)}) collective-permute-start(f32[5,24,5,128]{3,1,2,0:T(8,128)S(1)} %get-tuple-element.38), channel_id=1, source_target_pairs={{1,0},{2,1},{3,2},{5,4},{6,5},{7,6},{9,8},{10,9},{11,10},{13,12},{... | collective-permute-start | bytes 921608 | tf_op jit(solution)/shard_map/ppermute | solution.py:22
  48.3 0.8 %and_convert_fusion = f32[2]{0:T(128)S(1)} fusion(s32[19]{0:T(128)S(1)} %iota_add_fusion, f32[19]{0:T(128)S(1)} %select_reduce_fusion, f32[]{:T(128)} %bitcast.21), kind=kLoop, calls=%fused_computation.247 | loop fusion | flops 8 | bytes 28 | tf_op jit(solution)/shard_map/convert_element_type | solution.py:295
  49.1 1.1 %collective-permute-done.6 = f32[5,24,5,128]{3,1,2,0:T(8,128)S(1)} collective-permute-done((f32[5,24,5,128]{3,1,2,0:T(8,128)S(1)}, f32[5,24,5,128]{3,1,2,0:T(8,128)S(1)}, u32[]{:S(2)}, u32[]{:S(2)}) %collective-permute-start.6) | collective-permute-done | bytes 307232 | tf_op jit(solution)/shard_map/ppermute | solution.py:21
  50.2 4.4 %collective-permute-done.7 = f32[5,24,5,128]{3,1,2,0:T(8,128)S(1)} collective-permute-done((f32[5,24,5,128]{3,1,2,0:T(8,128)S(1)}, f32[5,24,5,128]{3,1,2,0:T(8,128)S(1)}, u32[]{:S(2)}, u32[]{:S(2)}) %collective-permute-start.7) | collective-permute-done | bytes 307232 | tf_op jit(solution)/shard_map/ppermute | solution.py:22
  54.7 0.2 fusion.62
  55.0 0.1 fusion.155
  55.1 0.3 fusion.70
  55.4 0.1 fusion.156
  55.5 0.3 fusion.81
  55.9 0.2 multiply_reduce_fusion
  56.1 0.2 fusion.119
  56.4 0.2 fusion.117
  56.6 0.3 fusion.108
  56.9 0.2 fusion.123
  57.1 0.2 fusion.121
  57.3 0.3 fusion.59
  57.8 0.2 fusion.164
  58.0 1.3 %collective-permute-start.9 = (f32[2,20,256]{2,1,0:T(8,128)S(1)}, f32[2,20,256]{2,1,0:T(8,128)S(1)}, u32[]{:S(2)}, u32[]{:S(2)}) collective-permute-start(f32[2,20,256]{2,1,0:T(8,128)S(1)} %get-tuple-element.44), channel_id=1, source_target_pairs={{4,0},{8,4},{12,8},{5,1},{9,5},{13,9},{6,2},{10,6},{14,10},{7,3},{... | collective-permute-start | bytes 122888 | tf_op jit(solution)/shard_map/ppermute | solution.py:30
  59.3 0.1 fusion.165
  59.5 4.0 %collective-permute-start.8 = (f32[3,20,256]{2,1,0:T(8,128)S(1)}, f32[3,20,256]{2,1,0:T(8,128)S(1)}, u32[]{:S(2)}, u32[]{:S(2)}) collective-permute-start(f32[3,20,256]{2,1,0:T(8,128)S(1)} %pad_maximum_fusion.11), channel_id=1, source_target_pairs={{0,4},{4,8},{8,12},{1,5},{5,9},{9,13},{2,6},{6,10},{10,14},{3,7},{... | collective-permute-start | bytes 184328 | tf_op jit(solution)/shard_map/ppermute | solution.py:30
  63.6 1.3 %collective-permute-done.8 = f32[3,20,256]{2,1,0:T(8,128)S(1)} collective-permute-done((f32[3,20,256]{2,1,0:T(8,128)S(1)}, f32[3,20,256]{2,1,0:T(8,128)S(1)}, u32[]{:S(2)}, u32[]{:S(2)}) %collective-permute-start.8) | collective-permute-done | bytes 61472 | tf_op jit(solution)/shard_map/ppermute | solution.py:30
  65.0 0.2 fusion.150
  65.2 0.8 %fusion.36 = f32[18,18,256]{2,1,0:T(8,128)S(1)} fusion(f32[20,20,256]{2,1,0:T(8,128)S(1)} %pad_maximum_fusion.3, f32[24,23,256]{2,1,0:T(8,128)S(1)} %divide_select_fusion, f32[2,20,256]{2,1,0:T(8,128)S(1)} %multiply_add_fusion.3, f32[16,20,256]{2,1,0:T(8,128)S(1)} %multiply_add_fusion, f32[23,24,256]{2,1,0:T(8,128)S(1)} %divide_select_fusion.1, ...), kind=kLoop, calls=%fused_computation.65 | loop fusion | flops 1575936 | bytes 4882000 | tf_op jit(solution)/shard_map/add | solution.py:106
  66.0 0.1 fusion.153
  66.2 1.1 %fusion.49 = f32[16,16,256]{2,1,0:T(8,128)} fusion(f32[18,18,256]{2,1,0:T(8,128)S(1)} %fusion.36, f32[24,24,256]{2,1,0:T(8,128)S(1)} %get-tuple-element.19, f32[16,16,255]{2,1,0:T(8,128)S(1)} %get-tuple-element.42, f32[16,16,255]{2,1,0:T(8,128)S(1)} %get-tuple-element.41, f32[24,23,256]{2,1,0:T(8,128)S(1)} %divide_select_fusion, ...), kind=kLoop, calls=%fused_computation.88 | loop fusion | flops 1114112 | bytes 4161648 | tf_op jit(solution)/shard_map/add | solution.py:106
  (84 shorter events, 2.3 us)
Async XLA Ops:
  0.0 12.5 %copy-start.3 = (f32[16,16,256]{2,1,0:T(8,128)S(1)}, f32[16,16,256]{2,1,0:T(8,128)}, u32[]{:S(2)}) copy-start(f32[16,16,256]{2,1,0:T(8,128)} %param.11) | copy-start | bytes 786436
  0.0 12.5 %copy-start.1 = (f32[16,16,256]{2,1,0:T(8,128)S(1)}, f32[16,16,256]{2,1,0:T(8,128)}, u32[]{:S(2)}) copy-start(f32[16,16,256]{2,1,0:T(8,128)} %param.12) | copy-start | bytes 786436
  0.0 12.5 %copy-start.2 = (f32[16,16,256]{2,1,0:T(8,128)S(1)}, f32[16,16,256]{2,1,0:T(8,128)}, u32[]{:S(2)}) copy-start(f32[16,16,256]{2,1,0:T(8,128)} %param.13) | copy-start | bytes 786436
  1.1 7.6 %collective-permute-start = (f32[3,4,16,256]{3,2,1,0:T(8,128)S(1)}, f32[3,4,16,256]{3,2,1,0:T(8,128)S(1)}, u32[]{:S(2)}, u32[]{:S(2)}) collective-permute-start(f32[3,4,16,256]{3,2,1,0:T(8,128)S(1)} %get-tuple-element.23), channel_id=1, source_target_pairs={{0,4},{4,8},{8,12},{1,5},{5,9},{9,13},{2,6},{6,10},{10,14},{3,7},{... | collective-permute-start | bytes 589832 | tf_op jit(solution)/shard_map/ppermute | solution.py:21
  5.2 7.3 %collective-permute-start.1 = (f32[3,4,16,256]{3,2,1,0:T(8,128)S(1)}, f32[3,4,16,256]{3,2,1,0:T(8,128)S(1)}, u32[]{:S(2)}, u32[]{:S(2)}) collective-permute-start(f32[3,4,16,256]{3,2,1,0:T(8,128)S(1)} %get-tuple-element.24), channel_id=1, source_target_pairs={{4,0},{8,4},{12,8},{5,1},{9,5},{13,9},{6,2},{10,6},{14,10},{7,3},{... | collective-permute-start | bytes 589832 | tf_op jit(solution)/shard_map/ppermute | solution.py:22
  12.6 6.9 %copy-start.9 = (s32[64]{0:T(128)S(1)}, s32[64]{0:T(128)}, u32[]{:S(2)}) copy-start(s32[64]{0:T(128)} %param.14) | copy-start | bytes 772
  12.7 10.5 %collective-permute-start.2 = (f32[3,24,4,256]{3,2,1,0:T(4,128)S(1)}, f32[3,24,4,256]{3,2,1,0:T(4,128)S(1)}, u32[]{:S(2)}, u32[]{:S(2)}) collective-permute-start(f32[3,24,4,256]{3,2,1,0:T(4,128)S(1)} %get-tuple-element.21), channel_id=1, source_target_pairs={{0,1},{1,2},{2,3},{4,5},{5,6},{6,7},{8,9},{9,10},{10,11},{12,13},{... | collective-permute-start | bytes 884744 | tf_op jit(solution)/shard_map/ppermute | solution.py:21
  17.6 8.0 %collective-permute-start.3 = (f32[3,24,4,256]{3,2,1,0:T(4,128)S(1)}, f32[3,24,4,256]{3,2,1,0:T(4,128)S(1)}, u32[]{:S(2)}, u32[]{:S(2)}) collective-permute-start(f32[3,24,4,256]{3,2,1,0:T(4,128)S(1)} %get-tuple-element.22), channel_id=1, source_target_pairs={{1,0},{2,1},{3,2},{5,4},{6,5},{7,6},{9,8},{10,9},{11,10},{13,12},{... | collective-permute-start | bytes 884744 | tf_op jit(solution)/shard_map/ppermute | solution.py:22
  29.4 0.9 %copy-start = (f32[256,128]{1,0:T(8,128)S(1)}, f32[256,128]{1,0:T(8,128)}, u32[]{:S(2)}) copy-start(f32[256,128]{1,0:T(8,128)} %constant.45.clone) | copy-start | bytes 393220
  30.6 1.0 %copy-start.4 = (f32[256,128]{1,0:T(8,128)S(1)}, f32[256,128]{1,0:T(8,128)}, u32[]{:S(2)}) copy-start(f32[256,128]{1,0:T(8,128)} %constant.46.clone) | copy-start | bytes 393220
  31.0 1.0 %copy-start.8 = (f32[136]{0:T(256)S(1)}, f32[136]{0:T(256)}, u32[]{:S(2)}) copy-start(f32[136]{0:T(256)} %constant.47.clone) | copy-start | bytes 1636
  31.0 1.0 %copy-start.10 = (pred[136,256]{1,0:T(8,128)(4,1)S(1)}, pred[136,256]{1,0:T(8,128)(4,1)}, u32[]{:S(2)}) copy-start(pred[136,256]{1,0:T(8,128)(4,1)} %constant.49.clone) | copy-start | bytes 104452
  31.6 0.9 %copy-start.6 = (pred[136,256]{1,0:T(8,128)(4,1)S(1)}, pred[136,256]{1,0:T(8,128)(4,1)}, u32[]{:S(2)}) copy-start(pred[136,256]{1,0:T(8,128)(4,1)} %constant.50.clone) | copy-start | bytes 104452
  33.2 4.7 %collective-permute-start.4 = (f32[5,4,8,128]{3,1,2,0:T(4,128)S(1)}, f32[5,4,8,128]{3,1,2,0:T(4,128)S(1)}, u32[]{:S(2)}, u32[]{:S(2)}) collective-permute-start(f32[5,4,8,128]{3,1,2,0:T(4,128)S(1)} %convolution_bitcast_fusion.1), channel_id=1, source_target_pairs={{0,4},{4,8},{8,12},{1,5},{5,9},{9,13},{2,6},{6,10},{10,14},{3,7},{... | collective-permute-start | bytes 245768 | tf_op jit(solution)/shard_map/ppermute | solution.py:30
  36.5 6.1 %collective-permute-start.5 = (f32[5,5,8,128]{3,1,2,0:T(8,128)S(1)}, f32[5,5,8,128]{3,1,2,0:T(8,128)S(1)}, u32[]{:S(2)}, u32[]{:S(2)}) collective-permute-start(f32[5,5,8,128]{3,1,2,0:T(8,128)S(1)} %pad_maximum_fusion.9), channel_id=1, source_target_pairs={{4,0},{8,4},{12,8},{5,1},{9,5},{13,9},{6,2},{10,6},{14,10},{7,3},{... | collective-permute-start | bytes 307208 | tf_op jit(solution)/shard_map/ppermute | solution.py:30
  43.2 7.0 %collective-permute-start.6 = (f32[5,24,5,128]{3,1,2,0:T(8,128)S(1)}, f32[5,24,5,128]{3,1,2,0:T(8,128)S(1)}, u32[]{:S(2)}, u32[]{:S(2)}) collective-permute-start(f32[5,24,5,128]{3,1,2,0:T(8,128)S(1)} %get-tuple-element.37), channel_id=1, source_target_pairs={{0,1},{1,2},{2,3},{4,5},{5,6},{6,7},{8,9},{9,10},{10,11},{12,13},{... | collective-permute-start | bytes 921608 | tf_op jit(solution)/shard_map/ppermute | solution.py:21
  46.4 8.2 %collective-permute-start.7 = (f32[5,24,5,128]{3,1,2,0:T(8,128)S(1)}, f32[5,24,5,128]{3,1,2,0:T(8,128)S(1)}, u32[]{:S(2)}, u32[]{:S(2)}) collective-permute-start(f32[5,24,5,128]{3,1,2,0:T(8,128)S(1)} %get-tuple-element.38), channel_id=1, source_target_pairs={{1,0},{2,1},{3,2},{5,4},{6,5},{7,6},{9,8},{10,9},{11,10},{13,12},{... | collective-permute-start | bytes 921608 | tf_op jit(solution)/shard_map/ppermute | solution.py:22
  55.9 1.4 %copy-start.5 = (pred[256,136]{1,0:T(32,128)(4,1)S(1)}, pred[256,136]{1,0:T(32,128)(4,1)}, u32[]{:S(2)}) copy-start(pred[256,136]{1,0:T(32,128)(4,1)} %constant.48.clone) | copy-start | bytes 104452
  56.6 2.7 %copy-start.7 = (f32[20,10]{1,0:T(8,128)S(1)}, f32[20,10]{1,0:T(8,128)}, u32[]{:S(2)}) copy-start(f32[20,10]{1,0:T(8,128)} %constant.51.clone) | copy-start | bytes 2404
  58.0 5.5 %collective-permute-start.9 = (f32[2,20,256]{2,1,0:T(8,128)S(1)}, f32[2,20,256]{2,1,0:T(8,128)S(1)}, u32[]{:S(2)}, u32[]{:S(2)}) collective-permute-start(f32[2,20,256]{2,1,0:T(8,128)S(1)} %get-tuple-element.44), channel_id=1, source_target_pairs={{4,0},{8,4},{12,8},{5,1},{9,5},{13,9},{6,2},{10,6},{14,10},{7,3},{... | collective-permute-start | bytes 122888 | tf_op jit(solution)/shard_map/ppermute | solution.py:30
  59.5 5.4 %collective-permute-start.8 = (f32[3,20,256]{2,1,0:T(8,128)S(1)}, f32[3,20,256]{2,1,0:T(8,128)S(1)}, u32[]{:S(2)}, u32[]{:S(2)}) collective-permute-start(f32[3,20,256]{2,1,0:T(8,128)S(1)} %pad_maximum_fusion.11), channel_id=1, source_target_pairs={{0,4},{4,8},{8,12},{1,5},{5,9},{9,13},{2,6},{6,10},{10,14},{3,7},{... | collective-permute-start | bytes 184328 | tf_op jit(solution)/shard_map/ppermute | solution.py:30

commit v15 on v11

--- a/solution.py
+++ b/solution.py
@@ -295,7 +295,22 @@
     to_owner = ((next_ids == local_ids[-1]) & next_in).astype(jnp.float32)
     high_halo = above_next + to_owner[:, None, None] * last_fine[None]
     post_ext = jnp.concatenate([below_prev[:NU], own, high_halo], axis=0)
-    return sweeps(post_ext, source_ext, faces_ext, NU, width_x)
+    face_rim = fine_rim - 1
+
+    def piece(field, low, high, rim):
+        window = (slice(low + face_rim, high + face_rim), slice(face_rim - rim, face_rim + width_y + rim))
+        faces_now = tuple(member[window] for member in faces_ext)
+        center, product = apply_fine(field, faces_now)
+        return center + OMEGA * (source_ext[window] - product) / faces_now[7]
+
+    settled = 3
+    first_mid = piece(base[settled:], settled + 1, width_x - 1, 1)
+    second_mid = piece(first_mid, settled + 2, width_x - 2, 0)
+    first_low = piece(post_ext[: settled + 4], -1, settled + 1, 1)
+    first_high = piece(post_ext[width_x:], width_x - 1, width_x + 1, 1)
+    second_low = piece(jnp.concatenate([first_low, first_mid[:2]], axis=0), 0, settled + 2, 0)
+    second_high = piece(jnp.concatenate([first_mid[-2:], first_high], axis=0), width_x - 2, width_x, 0)
+    return jnp.concatenate([second_low, second_mid, second_high], axis=0)
 
 
 def solution(mesh):

time: 68.2 us -> 69.9 us (1.025)
  waiting for transfers between devices: 19 us -> 21.1 us
  starting transfers between devices: 27 us -> 26.2 us
    ppermute x4, waiting for transfers between devices: 5.98 us -> 7.92 us  [passed_along(): return lax.ppermute(array, axis, pairs)]
    add x4 -> x2, other arithmetic: 3.86 us -> 1.98 us  [sweeps(): field_ext = center + OMEGA * (source_now - product) / faces_now[7]]
    add x0 -> x6, other arithmetic: none -> 1.4 us  [piece(): return center + OMEGA * (source_ext[window] - product) / faces_now[7]]
    ppermute x4, starting transfers between devices: 9.79 us -> 8.98 us  [passed_along(): return lax.ppermute(array, axis, pairs)]
    concatenate x0 -> x3, other arithmetic: none -> 0.74 us  [the longest x1 0.72 us: body(): return jnp.concatenate([second_low, second_mid, second_high], axis=0)]
where the time goes in v15:
time: 69.9 us; the launch traced here: 69.4 us
  starting transfers between devices  26.2 us (37%)
  waiting for transfers between devices  21.1 us (30%)
  other arithmetic  9.98 us (14%)
  matrix products  5.19 us (7%)
  local copies, waits for them, and re-layouts  3.68 us (5%)
  between operations  3.25 us (5%)
    ppermute x3, starting transfers between devices, padded(): before = lax.ppermute(last, axis, up)  12.1 us
    ppermute x3, waiting for transfers between devices, padded(): after = lax.ppermute(leading, axis, down)  10.7 us
    ppermute x4, starting transfers between devices, passed_along(): return lax.ppermute(array, axis, pairs)  8.98 us
    ppermute x4, waiting for transfers between devices, passed_along(): return lax.ppermute(array, axis, pairs)  7.92 us
    ppermute x3, starting transfers between devices, padded(): after = lax.ppermute(leading, axis, down)  5.13 us
    ppermute x3, waiting for transfers between devices, padded(): before = lax.ppermute(last, axis, up)  2.46 us
    add x2, other arithmetic, sweeps(): field_ext = center + OMEGA * (source_now - product) / faces_now[7]  1.98 us
    dot_general x5, matrix products, z_sum(): return jnp.dot(flat, pick_z, precision=lax.Precision.HIGHEST)  1.95 us
  transfers between devices with their start and end apart: 10, of which 8 were waited for; matrix products, arithmetic and copies ran while one was open for 5% of the time, Pallas kernels for 0%

profile of v15, /device:TPU:1, one launch (start us, length us, event | category | flops | bytes accessed | tf_op | source)
XLA Modules:
  0.0 69.4 jit_solution(1375007594352210448)
XLA Ops:
  0.0 1.1 %pad_maximum_fusion.6 = (f32[3,4,16,256]{3,2,1,0:T(8,128)S(1)}, f32[3,4,16,256]{3,2,1,0:T(8,128)S(1)}) fusion(f32[1,16,16,256]{3,2,1,0:T(8,128)} %bitcast.231, f32[1,16,16,256]{3,2,1,0:T(8,128)} %bitcast.224, f32[1,16,16,256]{3,2,1,0:T(8,128)} %bitcast.233), kind=kLoop, calls=%fused_computation.136 | loop fusion | flops 196608 | bytes 1179648 | tf_op jit(solution)/shard_map/slice | solution.py:19
  1.1 4.0 %collective-permute-start = (f32[3,4,16,256]{3,2,1,0:T(8,128)S(1)}, f32[3,4,16,256]{3,2,1,0:T(8,128)S(1)}, u32[]{:S(2)}, u32[]{:S(2)}) collective-permute-start(f32[3,4,16,256]{3,2,1,0:T(8,128)S(1)} %get-tuple-element.23), channel_id=1, source_target_pairs={{0,4},{4,8},{8,12},{1,5},{5,9},{9,13},{2,6},{6,10},{10,14},{3,7},{... | collective-permute-start | bytes 589832 | tf_op jit(solution)/shard_map/ppermute | solution.py:21
  5.2 1.3 %collective-permute-start.1 = (f32[3,4,16,256]{3,2,1,0:T(8,128)S(1)}, f32[3,4,16,256]{3,2,1,0:T(8,128)S(1)}, u32[]{:S(2)}, u32[]{:S(2)}) collective-permute-start(f32[3,4,16,256]{3,2,1,0:T(8,128)S(1)} %get-tuple-element.24), channel_id=1, source_target_pairs={{4,0},{8,4},{12,8},{5,1},{9,5},{13,9},{6,2},{10,6},{14,10},{7,3},{... | collective-permute-start | bytes 589832 | tf_op jit(solution)/shard_map/ppermute | solution.py:22
  7.4 1.3 %collective-permute-done = f32[3,4,16,256]{3,2,1,0:T(8,128)S(1)} collective-permute-done((f32[3,4,16,256]{3,2,1,0:T(8,128)S(1)}, f32[3,4,16,256]{3,2,1,0:T(8,128)S(1)}, u32[]{:S(2)}, u32[]{:S(2)}) %collective-permute-start) | collective-permute-done | bytes 196640 | tf_op jit(solution)/shard_map/ppermute | solution.py:21
  8.7 3.8 %collective-permute-done.1 = f32[3,4,16,256]{3,2,1,0:T(8,128)S(1)} collective-permute-done((f32[3,4,16,256]{3,2,1,0:T(8,128)S(1)}, f32[3,4,16,256]{3,2,1,0:T(8,128)S(1)}, u32[]{:S(2)}, u32[]{:S(2)}) %collective-permute-start.1) | collective-permute-done | bytes 196640 | tf_op jit(solution)/shard_map/ppermute | solution.py:22
  12.7 4.9 %collective-permute-start.2 = (f32[3,24,4,256]{3,2,1,0:T(4,128)S(1)}, f32[3,24,4,256]{3,2,1,0:T(4,128)S(1)}, u32[]{:S(2)}, u32[]{:S(2)}) collective-permute-start(f32[3,24,4,256]{3,2,1,0:T(4,128)S(1)} %get-tuple-element.21), channel_id=1, source_target_pairs={{0,1},{1,2},{2,3},{4,5},{5,6},{6,7},{8,9},{9,10},{10,11},{12,13},{... | collective-permute-start | bytes 884744 | tf_op jit(solution)/shard_map/ppermute | solution.py:21
  17.6 1.9 %collective-permute-start.3 = (f32[3,24,4,256]{3,2,1,0:T(4,128)S(1)}, f32[3,24,4,256]{3,2,1,0:T(4,128)S(1)}, u32[]{:S(2)}, u32[]{:S(2)}) collective-permute-start(f32[3,24,4,256]{3,2,1,0:T(4,128)S(1)} %get-tuple-element.22), channel_id=1, source_target_pairs={{1,0},{2,1},{3,2},{5,4},{6,5},{7,6},{9,8},{10,9},{11,10},{13,12},{... | collective-permute-start | bytes 884744 | tf_op jit(solution)/shard_map/ppermute | solution.py:22
  19.6 0.2 select_reduce_fusion
  19.7 0.6 fusion.223
  23.2 2.5 %collective-permute-done.3 = f32[3,24,4,256]{3,2,1,0:T(4,128)S(1)} collective-permute-done((f32[3,24,4,256]{3,2,1,0:T(4,128)S(1)}, f32[3,24,4,256]{3,2,1,0:T(4,128)S(1)}, u32[]{:S(2)}, u32[]{:S(2)}) %collective-permute-start.3) | collective-permute-done | bytes 294944 | tf_op jit(solution)/shard_map/ppermute | solution.py:22
  25.7 0.3 pad_maximum_fusion
  25.9 0.1 slice_bitcast_fusion
  26.1 0.2 fusion.211
  26.3 0.2 divide_select_fusion
  26.5 0.2 divide_select_fusion.1
  26.7 0.2 fusion.212
  26.9 0.2 divide_select_fusion.2
  27.2 1.1 %fusion.7 = (f32[22,22,256]{2,1,0:T(8,128)S(1)}, f32[22,22,256]{2,1,0:T(8,128)S(1)}, f32[22,22,256]{2,1,0:T(8,128)S(1)}) fusion(f32[24,24,256]{2,1,0:T(8,128)S(1)} %get-tuple-element.20, f32[24,24,256]{2,1,0:T(8,128)S(1)} %get-tuple-element.19, f32[22,22,255]{2,1,0:T(8,128)S(1)} %get-tuple-element.30, f32[22,22,255]{2,1,0:T(8,128)S(1)} %get-tuple-element.29, ...), kind=kLoop, calls=%fused_computation.27 | loop fusion | flops 3345408 | bytes 8423108 | tf_op jit(solution)/shard_map/add | solution.py:106
  28.3 0.2 fusion.213
  28.5 0.9 %fusion.26 = f32[20,20,256]{2,1,0:T(8,128)S(1)} fusion(f32[22,22,256]{2,1,0:T(8,128)S(1)} %get-tuple-element.15, f32[24,23,256]{2,1,0:T(8,128)S(1)} %divide_select_fusion, f32[23,24,256]{2,1,0:T(8,128)S(1)} %divide_select_fusion.1, f32[24,24,256]{2,1,0:T(8,128)S(1)} %get-tuple-element.19, f32[20,20,255]{2,1,0:T(8,128)S(1)} %get-tuple-element.34, ...), kind=kLoop, calls=%fused_computation.54 | loop fusion | flops 1740800 | bytes 6224880 | tf_op jit(solution)/shard_map/add | solution.py:106
  29.4 0.1 fusion.215
  29.5 0.5 fusion.210
  30.0 0.4 copy-done
  30.4 0.4 fusion.228
  30.8 0.4 fusion.224
  31.2 0.4 fusion.225
  31.7 0.4 fusion.227
  32.1 0.4 fusion.226
  32.5 0.4 fusion.11
  33.0 0.3 convolution_bitcast_fusion.2
  33.5 0.3 convolution_bitcast_fusion.1
  33.8 3.2 %collective-permute-start.4 = (f32[5,4,8,128]{3,1,2,0:T(4,128)S(1)}, f32[5,4,8,128]{3,1,2,0:T(4,128)S(1)}, u32[]{:S(2)}, u32[]{:S(2)}) collective-permute-start(f32[5,4,8,128]{3,1,2,0:T(4,128)S(1)} %convolution_bitcast_fusion.1), channel_id=1, source_target_pairs={{0,4},{4,8},{8,12},{1,5},{5,9},{9,13},{2,6},{6,10},{10,14},{3,7},{... | collective-permute-start | bytes 245768 | tf_op jit(solution)/shard_map/ppermute | solution.py:30
  37.0 1.3 %collective-permute-start.5 = (f32[5,5,8,128]{3,1,2,0:T(8,128)S(1)}, f32[5,5,8,128]{3,1,2,0:T(8,128)S(1)}, u32[]{:S(2)}, u32[]{:S(2)}) collective-permute-start(f32[5,5,8,128]{3,1,2,0:T(8,128)S(1)} %pad_maximum_fusion.7), channel_id=1, source_target_pairs={{4,0},{8,4},{12,8},{5,1},{9,5},{13,9},{6,2},{10,6},{14,10},{7,3},{... | collective-permute-start | bytes 307208 | tf_op jit(solution)/shard_map/ppermute | solution.py:30
  38.3 0.1 collective-permute-done.4
  38.5 4.5 %collective-permute-done.5 = f32[5,5,8,128]{3,1,2,0:T(8,128)S(1)} collective-permute-done((f32[5,5,8,128]{3,1,2,0:T(8,128)S(1)}, f32[5,5,8,128]{3,1,2,0:T(8,128)S(1)}, u32[]{:S(2)}, u32[]{:S(2)}) %collective-permute-start.5) | collective-permute-done | bytes 102432 | tf_op jit(solution)/shard_map/ppermute | solution.py:30
  43.2 0.5 maximum_add_fusion
  43.8 3.2 %collective-permute-start.6 = (f32[5,24,5,128]{3,1,2,0:T(8,128)S(1)}, f32[5,24,5,128]{3,1,2,0:T(8,128)S(1)}, u32[]{:S(2)}, u32[]{:S(2)}) collective-permute-start(f32[5,24,5,128]{3,1,2,0:T(8,128)S(1)} %get-tuple-element.35), channel_id=1, source_target_pairs={{0,1},{1,2},{2,3},{4,5},{5,6},{6,7},{8,9},{9,10},{10,11},{12,13},{... | collective-permute-start | bytes 921608 | tf_op jit(solution)/shard_map/ppermute | solution.py:21
  46.9 1.9 %collective-permute-start.7 = (f32[5,24,5,128]{3,1,2,0:T(8,128)S(1)}, f32[5,24,5,128]{3,1,2,0:T(8,128)S(1)}, u32[]{:S(2)}, u32[]{:S(2)}) collective-permute-start(f32[5,24,5,128]{3,1,2,0:T(8,128)S(1)} %get-tuple-element.36), channel_id=1, source_target_pairs={{1,0},{2,1},{3,2},{5,4},{6,5},{7,6},{9,8},{10,9},{11,10},{13,12},{... | collective-permute-start | bytes 921608 | tf_op jit(solution)/shard_map/ppermute | solution.py:22
  48.9 0.6 and_convert_fusion
  49.5 1.2 %collective-permute-done.6 = f32[5,24,5,128]{3,1,2,0:T(8,128)S(1)} collective-permute-done((f32[5,24,5,128]{3,1,2,0:T(8,128)S(1)}, f32[5,24,5,128]{3,1,2,0:T(8,128)S(1)}, u32[]{:S(2)}, u32[]{:S(2)}) %collective-permute-start.6) | collective-permute-done | bytes 307232 | tf_op jit(solution)/shard_map/ppermute | solution.py:21
  50.7 4.4 %collective-permute-done.7 = f32[5,24,5,128]{3,1,2,0:T(8,128)S(1)} collective-permute-done((f32[5,24,5,128]{3,1,2,0:T(8,128)S(1)}, f32[5,24,5,128]{3,1,2,0:T(8,128)S(1)}, u32[]{:S(2)}, u32[]{:S(2)}) %collective-permute-start.7) | collective-permute-done | bytes 307232 | tf_op jit(solution)/shard_map/ppermute | solution.py:22
  55.3 0.2 fusion.50
  55.6 0.3 fusion.58
  56.1 0.3 fusion.78
  56.5 0.2 multiply_reduce_fusion
  56.7 0.2 fusion.183
  56.9 0.2 fusion.181
  57.2 0.3 fusion.148
  57.5 0.2 fusion.187
  57.7 0.2 fusion.185
  57.9 0.3 fusion.47
  58.4 0.1 fusion.216
  58.5 0.2 fusion.229
  58.7 0.2 copy-done.7
  58.9 0.1 fusion.230
  59.1 3.2 %collective-permute-start.8 = (f32[3,20,256]{2,1,0:T(8,128)S(1)}, f32[3,20,256]{2,1,0:T(8,128)S(1)}, u32[]{:S(2)}, u32[]{:S(2)}) collective-permute-start(f32[3,20,256]{2,1,0:T(8,128)S(1)} %pad_maximum_fusion.9), channel_id=1, source_target_pairs={{0,4},{4,8},{8,12},{1,5},{5,9},{9,13},{2,6},{6,10},{10,14},{3,7},{... | collective-permute-start | bytes 184328 | tf_op jit(solution)/shard_map/ppermute | solution.py:30
  62.3 0.5 fusion.37
  62.9 1.3 %collective-permute-start.9 = (f32[2,20,256]{2,1,0:T(8,128)S(1)}, f32[2,20,256]{2,1,0:T(8,128)S(1)}, u32[]{:S(2)}, u32[]{:S(2)}) collective-permute-start(f32[2,20,256]{2,1,0:T(8,128)S(1)} %get-tuple-element.42), channel_id=1, source_target_pairs={{4,0},{8,4},{12,8},{5,1},{9,5},{13,9},{6,2},{10,6},{14,10},{7,3},{... | collective-permute-start | bytes 122888 | tf_op jit(solution)/shard_map/ppermute | solution.py:30
  64.2 0.3 fusion.75
  64.5 3.2 %collective-permute-done.9 = f32[2,20,256]{2,1,0:T(8,128)S(1)} collective-permute-done((f32[2,20,256]{2,1,0:T(8,128)S(1)}, f32[2,20,256]{2,1,0:T(8,128)S(1)}, u32[]{:S(2)}, u32[]{:S(2)}) %collective-permute-start.9) | collective-permute-done | bytes 40992 | tf_op jit(solution)/shard_map/ppermute | solution.py:30
  68.0 0.2 fusion.100
  68.2 0.2 fusion.126
  68.4 0.1 divide_add_fusion
  68.7 0.7 %pad_maximum_fusion.3 = f32[16,16,256]{2,1,0:T(8,128)} fusion(f32[2,16,256]{2,1,0:T(8,128)S(1)} %divide_add_fusion.1, f32[9,16,256]{2,1,0:T(8,128)S(1)} %fusion.75, f32[5,16,256]{2,1,0:T(8,128)S(1)} %fusion.126), kind=kLoop, calls=%fused_computation.102 | loop fusion | flops 131072 | bytes 524288 | tf_op jit(solution)/shard_map/concatenate | solution.py:313
  (92 shorter events, 3.0 us)
Async XLA Ops:
  0.0 12.5 %copy-start.3 = (f32[16,16,256]{2,1,0:T(8,128)S(1)}, f32[16,16,256]{2,1,0:T(8,128)}, u32[]{:S(2)}) copy-start(f32[16,16,256]{2,1,0:T(8,128)} %param.11) | copy-start | bytes 786436
  0.0 12.5 %copy-start.1 = (f32[16,16,256]{2,1,0:T(8,128)S(1)}, f32[16,16,256]{2,1,0:T(8,128)}, u32[]{:S(2)}) copy-start(f32[16,16,256]{2,1,0:T(8,128)} %param.12) | copy-start | bytes 786436
  0.0 12.5 %copy-start.2 = (f32[16,16,256]{2,1,0:T(8,128)S(1)}, f32[16,16,256]{2,1,0:T(8,128)}, u32[]{:S(2)}) copy-start(f32[16,16,256]{2,1,0:T(8,128)} %param.13) | copy-start | bytes 786436
  1.1 7.6 %collective-permute-start = (f32[3,4,16,256]{3,2,1,0:T(8,128)S(1)}, f32[3,4,16,256]{3,2,1,0:T(8,128)S(1)}, u32[]{:S(2)}, u32[]{:S(2)}) collective-permute-start(f32[3,4,16,256]{3,2,1,0:T(8,128)S(1)} %get-tuple-element.23), channel_id=1, source_target_pairs={{0,4},{4,8},{8,12},{1,5},{5,9},{9,13},{2,6},{6,10},{10,14},{3,7},{... | collective-permute-start | bytes 589832 | tf_op jit(solution)/shard_map/ppermute | solution.py:21
  5.2 7.3 %collective-permute-start.1 = (f32[3,4,16,256]{3,2,1,0:T(8,128)S(1)}, f32[3,4,16,256]{3,2,1,0:T(8,128)S(1)}, u32[]{:S(2)}, u32[]{:S(2)}) collective-permute-start(f32[3,4,16,256]{3,2,1,0:T(8,128)S(1)} %get-tuple-element.24), channel_id=1, source_target_pairs={{4,0},{8,4},{12,8},{5,1},{9,5},{13,9},{6,2},{10,6},{14,10},{7,3},{... | collective-permute-start | bytes 589832 | tf_op jit(solution)/shard_map/ppermute | solution.py:22
  12.6 6.9 %copy-start.9 = (s32[64]{0:T(128)S(1)}, s32[64]{0:T(128)}, u32[]{:S(2)}) copy-start(s32[64]{0:T(128)} %param.14) | copy-start | bytes 772
  12.7 10.4 %collective-permute-start.2 = (f32[3,24,4,256]{3,2,1,0:T(4,128)S(1)}, f32[3,24,4,256]{3,2,1,0:T(4,128)S(1)}, u32[]{:S(2)}, u32[]{:S(2)}) collective-permute-start(f32[3,24,4,256]{3,2,1,0:T(4,128)S(1)} %get-tuple-element.21), channel_id=1, source_target_pairs={{0,1},{1,2},{2,3},{4,5},{5,6},{6,7},{8,9},{9,10},{10,11},{12,13},{... | collective-permute-start | bytes 884744 | tf_op jit(solution)/shard_map/ppermute | solution.py:21
  17.6 8.0 %collective-permute-start.3 = (f32[3,24,4,256]{3,2,1,0:T(4,128)S(1)}, f32[3,24,4,256]{3,2,1,0:T(4,128)S(1)}, u32[]{:S(2)}, u32[]{:S(2)}) collective-permute-start(f32[3,24,4,256]{3,2,1,0:T(4,128)S(1)} %get-tuple-element.22), channel_id=1, source_target_pairs={{1,0},{2,1},{3,2},{5,4},{6,5},{7,6},{9,8},{10,9},{11,10},{13,12},{... | collective-permute-start | bytes 884744 | tf_op jit(solution)/shard_map/ppermute | solution.py:22
  29.5 0.9 %copy-start = (f32[256,128]{1,0:T(8,128)S(1)}, f32[256,128]{1,0:T(8,128)}, u32[]{:S(2)}) copy-start(f32[256,128]{1,0:T(8,128)} %constant.45.clone) | copy-start | bytes 393220
  30.8 1.3 %copy-start.4 = (f32[256,128]{1,0:T(8,128)S(1)}, f32[256,128]{1,0:T(8,128)}, u32[]{:S(2)}) copy-start(f32[256,128]{1,0:T(8,128)} %constant.46.clone) | copy-start | bytes 393220
  31.2 1.3 %copy-start.8 = (f32[136]{0:T(256)S(1)}, f32[136]{0:T(256)}, u32[]{:S(2)}) copy-start(f32[136]{0:T(256)} %constant.47.clone) | copy-start | bytes 1636
  31.2 1.3 %copy-start.10 = (pred[136,256]{1,0:T(8,128)(4,1)S(1)}, pred[136,256]{1,0:T(8,128)(4,1)}, u32[]{:S(2)}) copy-start(pred[136,256]{1,0:T(8,128)(4,1)} %constant.49.clone) | copy-start | bytes 104452
  32.1 0.9 %copy-start.6 = (pred[136,256]{1,0:T(8,128)(4,1)S(1)}, pred[136,256]{1,0:T(8,128)(4,1)}, u32[]{:S(2)}) copy-start(pred[136,256]{1,0:T(8,128)(4,1)} %constant.50.clone) | copy-start | bytes 104452
  33.8 4.7 %collective-permute-start.4 = (f32[5,4,8,128]{3,1,2,0:T(4,128)S(1)}, f32[5,4,8,128]{3,1,2,0:T(4,128)S(1)}, u32[]{:S(2)}, u32[]{:S(2)}) collective-permute-start(f32[5,4,8,128]{3,1,2,0:T(4,128)S(1)} %convolution_bitcast_fusion.1), channel_id=1, source_target_pairs={{0,4},{4,8},{8,12},{1,5},{5,9},{9,13},{2,6},{6,10},{10,14},{3,7},{... | collective-permute-start | bytes 245768 | tf_op jit(solution)/shard_map/ppermute | solution.py:30
  37.0 6.1 %collective-permute-start.5 = (f32[5,5,8,128]{3,1,2,0:T(8,128)S(1)}, f32[5,5,8,128]{3,1,2,0:T(8,128)S(1)}, u32[]{:S(2)}, u32[]{:S(2)}) collective-permute-start(f32[5,5,8,128]{3,1,2,0:T(8,128)S(1)} %pad_maximum_fusion.7), channel_id=1, source_target_pairs={{4,0},{8,4},{12,8},{5,1},{9,5},{13,9},{6,2},{10,6},{14,10},{7,3},{... | collective-permute-start | bytes 307208 | tf_op jit(solution)/shard_map/ppermute | solution.py:30
  43.8 7.0 %collective-permute-start.6 = (f32[5,24,5,128]{3,1,2,0:T(8,128)S(1)}, f32[5,24,5,128]{3,1,2,0:T(8,128)S(1)}, u32[]{:S(2)}, u32[]{:S(2)}) collective-permute-start(f32[5,24,5,128]{3,1,2,0:T(8,128)S(1)} %get-tuple-element.35), channel_id=1, source_target_pairs={{0,1},{1,2},{2,3},{4,5},{5,6},{6,7},{8,9},{9,10},{10,11},{12,13},{... | collective-permute-start | bytes 921608 | tf_op jit(solution)/shard_map/ppermute | solution.py:21
  46.9 8.2 %collective-permute-start.7 = (f32[5,24,5,128]{3,1,2,0:T(8,128)S(1)}, f32[5,24,5,128]{3,1,2,0:T(8,128)S(1)}, u32[]{:S(2)}, u32[]{:S(2)}) collective-permute-start(f32[5,24,5,128]{3,1,2,0:T(8,128)S(1)} %get-tuple-element.36), channel_id=1, source_target_pairs={{1,0},{2,1},{3,2},{5,4},{6,5},{7,6},{9,8},{10,9},{11,10},{13,12},{... | collective-permute-start | bytes 921608 | tf_op jit(solution)/shard_map/ppermute | solution.py:22
  56.5 1.4 %copy-start.5 = (pred[256,136]{1,0:T(32,128)(4,1)S(1)}, pred[256,136]{1,0:T(32,128)(4,1)}, u32[]{:S(2)}) copy-start(pred[256,136]{1,0:T(32,128)(4,1)} %constant.48.clone) | copy-start | bytes 104452
  58.2 0.7 %copy-start.7 = (f32[20,10]{1,0:T(8,128)S(1)}, f32[20,10]{1,0:T(8,128)}, u32[]{:S(2)}) copy-start(f32[20,10]{1,0:T(8,128)} %constant.51.clone) | copy-start | bytes 2404
  59.1 8.7 %collective-permute-start.8 = (f32[3,20,256]{2,1,0:T(8,128)S(1)}, f32[3,20,256]{2,1,0:T(8,128)S(1)}, u32[]{:S(2)}, u32[]{:S(2)}) collective-permute-start(f32[3,20,256]{2,1,0:T(8,128)S(1)} %pad_maximum_fusion.9), channel_id=1, source_target_pairs={{0,4},{4,8},{8,12},{1,5},{5,9},{9,13},{2,6},{6,10},{10,14},{3,7},{... | collective-permute-start | bytes 184328 | tf_op jit(solution)/shard_map/ppermute | solution.py:30
  62.9 4.8 %collective-permute-start.9 = (f32[2,20,256]{2,1,0:T(8,128)S(1)}, f32[2,20,256]{2,1,0:T(8,128)S(1)}, u32[]{:S(2)}, u32[]{:S(2)}) collective-permute-start(f32[2,20,256]{2,1,0:T(8,128)S(1)} %get-tuple-element.42), channel_id=1, source_target_pairs={{4,0},{8,4},{12,8},{5,1},{9,5},{13,9},{6,2},{10,6},{14,10},{7,3},{... | collective-permute-start | bytes 122888 | tf_op jit(solution)/shard_map/ppermute | solution.py:30

commit v16 on v14

--- a/solution.py
+++ b/solution.py
@@ -186,9 +186,9 @@
     paired = jnp.dot(
         gather_map,
         jnp.concatenate([z_parts[0], z_parts[1], z_parts[3], z_parts[4]], axis=1),
-        precision=lax.Precision.HIGHEST,
-    )
-    north_sums = jnp.dot(north_gather, z_parts[2], precision=lax.Precision.HIGHEST)
+        precision=lax.Precision.HIGH,
+    )
+    north_sums = jnp.dot(north_gather, z_parts[2], precision=lax.Precision.HIGH)
 
     def column(index):
         return paired[:, index * half_z : (index + 1) * half_z]
@@ -268,9 +268,9 @@
     corr_wide = jnp.concatenate([jnp.zeros_like(last_corr)[None], coarse_corr], axis=0)
     corr_core = corr_wide[:, 1 : 1 + half_y]
     corr_z = jnp.dot(
-        corr_core.reshape((width_x + 1) * half_y, half_z), pair_z.T, precision=lax.Precision.HIGHEST
-    )
-    correction = jnp.dot(spread_map, corr_z, precision=lax.Precision.HIGHEST)
+        corr_core.reshape((width_x + 1) * half_y, half_z), pair_z.T, precision=lax.Precision.HIGH
+    )
+    correction = jnp.dot(spread_map, corr_z, precision=lax.Precision.HIGH)
     correction = correction.reshape(width_x, width_y, depth_cells)
     owner_rows = (slot_ids[:, None] + 1 == jnp.arange(width_x + 1)[None, :]).astype(jnp.float32)
 

time: 67.7 us -> 67.6 us (level)
  no operation moved by 1% of the time
where the time goes in v16:
time: 67.6 us; the launch traced here: 67.1 us
  starting transfers between devices  27 us (40%)
  waiting for transfers between devices  19 us (28%)
  other arithmetic  9.81 us (15%)
  matrix products  4.5 us (7%)
  local copies, waits for them, and re-layouts  3.6 us (5%)
  between operations  3.23 us (5%)
    ppermute x3, starting transfers between devices, padded(): before = lax.ppermute(last, axis, up)  12.1 us
    ppermute x3, waiting for transfers between devices, padded(): after = lax.ppermute(leading, axis, down)  10.6 us
    ppermute x4, starting transfers between devices, passed_along(): return lax.ppermute(array, axis, pairs)  9.79 us
    ppermute x4, waiting for transfers between devices, passed_along(): return lax.ppermute(array, axis, pairs)  5.98 us
    ppermute x3, starting transfers between devices, padded(): after = lax.ppermute(leading, axis, down)  5.13 us
    add x4, other arithmetic, sweeps(): field_ext = center + OMEGA * (source_now - product) / faces_now[7]  3.86 us
    ppermute x3, waiting for transfers between devices, padded(): before = lax.ppermute(last, axis, up)  2.35 us
    dot_general x5, matrix products, z_sum(): return jnp.dot(flat, pick_z, precision=lax.Precision.HIGH)  1.48 us
  transfers between devices with their start and end apart: 10, of which 8 were waited for; matrix products, arithmetic and copies ran while one was open for 5% of the time, Pallas kernels for 0%

profile of v16, /device:TPU:1, one launch (start us, length us, event | category | flops | bytes accessed | tf_op | source)
XLA Modules:
  0.0 67.1 jit_solution(7766009190880403654)
XLA Ops:
  0.0 1.1 %pad_maximum_fusion.8 = (f32[3,4,16,256]{3,2,1,0:T(8,128)S(1)}, f32[3,4,16,256]{3,2,1,0:T(8,128)S(1)}) fusion(f32[1,16,16,256]{3,2,1,0:T(8,128)} %bitcast.231, f32[1,16,16,256]{3,2,1,0:T(8,128)} %bitcast.224, f32[1,16,16,256]{3,2,1,0:T(8,128)} %bitcast.233), kind=kLoop, calls=%fused_computation.123 | loop fusion | flops 196608 | bytes 1179648 | tf_op jit(solution)/shard_map/slice | solution.py:19
  1.1 4.0 %collective-permute-start = (f32[3,4,16,256]{3,2,1,0:T(8,128)S(1)}, f32[3,4,16,256]{3,2,1,0:T(8,128)S(1)}, u32[]{:S(2)}, u32[]{:S(2)}) collective-permute-start(f32[3,4,16,256]{3,2,1,0:T(8,128)S(1)} %get-tuple-element.23), channel_id=1, source_target_pairs={{0,4},{4,8},{8,12},{1,5},{5,9},{9,13},{2,6},{6,10},{10,14},{3,7},{... | collective-permute-start | bytes 589832 | tf_op jit(solution)/shard_map/ppermute | solution.py:21
  5.2 1.3 %collective-permute-start.1 = (f32[3,4,16,256]{3,2,1,0:T(8,128)S(1)}, f32[3,4,16,256]{3,2,1,0:T(8,128)S(1)}, u32[]{:S(2)}, u32[]{:S(2)}) collective-permute-start(f32[3,4,16,256]{3,2,1,0:T(8,128)S(1)} %get-tuple-element.24), channel_id=1, source_target_pairs={{4,0},{8,4},{12,8},{5,1},{9,5},{13,9},{6,2},{10,6},{14,10},{7,3},{... | collective-permute-start | bytes 589832 | tf_op jit(solution)/shard_map/ppermute | solution.py:22
  7.4 1.3 %collective-permute-done = f32[3,4,16,256]{3,2,1,0:T(8,128)S(1)} collective-permute-done((f32[3,4,16,256]{3,2,1,0:T(8,128)S(1)}, f32[3,4,16,256]{3,2,1,0:T(8,128)S(1)}, u32[]{:S(2)}, u32[]{:S(2)}) %collective-permute-start) | collective-permute-done | bytes 196640 | tf_op jit(solution)/shard_map/ppermute | solution.py:21
  8.7 3.8 %collective-permute-done.1 = f32[3,4,16,256]{3,2,1,0:T(8,128)S(1)} collective-permute-done((f32[3,4,16,256]{3,2,1,0:T(8,128)S(1)}, f32[3,4,16,256]{3,2,1,0:T(8,128)S(1)}, u32[]{:S(2)}, u32[]{:S(2)}) %collective-permute-start.1) | collective-permute-done | bytes 196640 | tf_op jit(solution)/shard_map/ppermute | solution.py:22
  12.6 0.1 fusion.145
  12.7 4.9 %collective-permute-start.2 = (f32[3,24,4,256]{3,2,1,0:T(4,128)S(1)}, f32[3,24,4,256]{3,2,1,0:T(4,128)S(1)}, u32[]{:S(2)}, u32[]{:S(2)}) collective-permute-start(f32[3,24,4,256]{3,2,1,0:T(4,128)S(1)} %get-tuple-element.21), channel_id=1, source_target_pairs={{0,1},{1,2},{2,3},{4,5},{5,6},{6,7},{8,9},{9,10},{10,11},{12,13},{... | collective-permute-start | bytes 884744 | tf_op jit(solution)/shard_map/ppermute | solution.py:21
  17.6 1.9 %collective-permute-start.3 = (f32[3,24,4,256]{3,2,1,0:T(4,128)S(1)}, f32[3,24,4,256]{3,2,1,0:T(4,128)S(1)}, u32[]{:S(2)}, u32[]{:S(2)}) collective-permute-start(f32[3,24,4,256]{3,2,1,0:T(4,128)S(1)} %get-tuple-element.22), channel_id=1, source_target_pairs={{1,0},{2,1},{3,2},{5,4},{6,5},{7,6},{9,8},{10,9},{11,10},{13,12},{... | collective-permute-start | bytes 884744 | tf_op jit(solution)/shard_map/ppermute | solution.py:22
  19.6 0.2 select_reduce_fusion
  19.7 0.7 fusion.158
  23.2 2.4 %collective-permute-done.3 = f32[3,24,4,256]{3,2,1,0:T(4,128)S(1)} collective-permute-done((f32[3,24,4,256]{3,2,1,0:T(4,128)S(1)}, f32[3,24,4,256]{3,2,1,0:T(4,128)S(1)}, u32[]{:S(2)}, u32[]{:S(2)}) %collective-permute-start.3) | collective-permute-done | bytes 294944 | tf_op jit(solution)/shard_map/ppermute | solution.py:22
  25.7 0.3 pad_maximum_fusion
  25.9 0.1 slice_bitcast_fusion
  26.1 0.2 fusion.147
  26.3 0.2 divide_select_fusion
  26.5 0.2 divide_select_fusion.1
  26.7 0.2 fusion.148
  26.9 0.2 divide_select_fusion.2
  27.2 1.1 %fusion.7 = (f32[22,22,256]{2,1,0:T(8,128)S(1)}, f32[22,22,256]{2,1,0:T(8,128)S(1)}, f32[22,22,256]{2,1,0:T(8,128)S(1)}) fusion(f32[24,24,256]{2,1,0:T(8,128)S(1)} %get-tuple-element.20, f32[24,24,256]{2,1,0:T(8,128)S(1)} %get-tuple-element.19, f32[22,22,255]{2,1,0:T(8,128)S(1)} %get-tuple-element.30, f32[22,22,255]{2,1,0:T(8,128)S(1)} %get-tuple-element.29, ...), kind=kLoop, calls=%fused_computation.22 | loop fusion | flops 3345408 | bytes 8423108 | tf_op jit(solution)/shard_map/add | solution.py:106
  28.3 0.2 fusion.149
  28.5 0.8 %fusion.26 = f32[20,20,256]{2,1,0:T(8,128)S(1)} fusion(f32[22,22,256]{2,1,0:T(8,128)S(1)} %get-tuple-element.15, f32[24,23,256]{2,1,0:T(8,128)S(1)} %divide_select_fusion, f32[23,24,256]{2,1,0:T(8,128)S(1)} %divide_select_fusion.1, f32[24,24,256]{2,1,0:T(8,128)S(1)} %get-tuple-element.19, f32[20,20,255]{2,1,0:T(8,128)S(1)} %get-tuple-element.34, ...), kind=kLoop, calls=%fused_computation.49 | loop fusion | flops 1740800 | bytes 6224880 | tf_op jit(solution)/shard_map/add | solution.py:106
  29.3 0.1 fusion.152
  29.4 0.5 fusion.146
  29.9 0.4 copy-done
  30.3 0.3 fusion.163
  30.6 0.3 fusion.159
  31.0 0.3 fusion.160
  31.3 0.3 fusion.162
  31.7 0.3 fusion.161
  32.0 0.3 fusion.11
  32.4 0.2 convolution_bitcast_fusion.2
  32.8 0.3 convolution_bitcast_fusion.1
  33.1 3.2 %collective-permute-start.4 = (f32[5,4,8,128]{3,1,2,0:T(4,128)S(1)}, f32[5,4,8,128]{3,1,2,0:T(4,128)S(1)}, u32[]{:S(2)}, u32[]{:S(2)}) collective-permute-start(f32[5,4,8,128]{3,1,2,0:T(4,128)S(1)} %convolution_bitcast_fusion.1), channel_id=1, source_target_pairs={{0,4},{4,8},{8,12},{1,5},{5,9},{9,13},{2,6},{6,10},{10,14},{3,7},{... | collective-permute-start | bytes 245768 | tf_op jit(solution)/shard_map/ppermute | solution.py:30
  36.3 1.3 %collective-permute-start.5 = (f32[5,5,8,128]{3,1,2,0:T(8,128)S(1)}, f32[5,5,8,128]{3,1,2,0:T(8,128)S(1)}, u32[]{:S(2)}, u32[]{:S(2)}) collective-permute-start(f32[5,5,8,128]{3,1,2,0:T(8,128)S(1)} %pad_maximum_fusion.9), channel_id=1, source_target_pairs={{4,0},{8,4},{12,8},{5,1},{9,5},{13,9},{6,2},{10,6},{14,10},{7,3},{... | collective-permute-start | bytes 307208 | tf_op jit(solution)/shard_map/ppermute | solution.py:30
  37.6 0.1 collective-permute-done.4
  37.9 4.5 %collective-permute-done.5 = f32[5,5,8,128]{3,1,2,0:T(8,128)S(1)} collective-permute-done((f32[5,5,8,128]{3,1,2,0:T(8,128)S(1)}, f32[5,5,8,128]{3,1,2,0:T(8,128)S(1)}, u32[]{:S(2)}, u32[]{:S(2)}) %collective-permute-start.5) | collective-permute-done | bytes 102432 | tf_op jit(solution)/shard_map/ppermute | solution.py:30
  42.4 0.1 multiply_add_fusion.1
  42.5 0.5 maximum_add_fusion
  43.1 3.2 %collective-permute-start.6 = (f32[5,24,5,128]{3,1,2,0:T(8,128)S(1)}, f32[5,24,5,128]{3,1,2,0:T(8,128)S(1)}, u32[]{:S(2)}, u32[]{:S(2)}) collective-permute-start(f32[5,24,5,128]{3,1,2,0:T(8,128)S(1)} %get-tuple-element.37), channel_id=1, source_target_pairs={{0,1},{1,2},{2,3},{4,5},{5,6},{6,7},{8,9},{9,10},{10,11},{12,13},{... | collective-permute-start | bytes 921608 | tf_op jit(solution)/shard_map/ppermute | solution.py:21
  46.3 1.9 %collective-permute-start.7 = (f32[5,24,5,128]{3,1,2,0:T(8,128)S(1)}, f32[5,24,5,128]{3,1,2,0:T(8,128)S(1)}, u32[]{:S(2)}, u32[]{:S(2)}) collective-permute-start(f32[5,24,5,128]{3,1,2,0:T(8,128)S(1)} %get-tuple-element.38), channel_id=1, source_target_pairs={{1,0},{2,1},{3,2},{5,4},{6,5},{7,6},{9,8},{10,9},{11,10},{13,12},{... | collective-permute-start | bytes 921608 | tf_op jit(solution)/shard_map/ppermute | solution.py:22
  48.2 0.8 %and_convert_fusion = f32[2]{0:T(128)S(1)} fusion(s32[19]{0:T(128)S(1)} %iota_add_fusion, f32[19]{0:T(128)S(1)} %select_reduce_fusion, f32[]{:T(128)} %bitcast.21), kind=kLoop, calls=%fused_computation.247 | loop fusion | flops 8 | bytes 28 | tf_op jit(solution)/shard_map/convert_element_type | solution.py:295
  49.0 1.1 %collective-permute-done.6 = f32[5,24,5,128]{3,1,2,0:T(8,128)S(1)} collective-permute-done((f32[5,24,5,128]{3,1,2,0:T(8,128)S(1)}, f32[5,24,5,128]{3,1,2,0:T(8,128)S(1)}, u32[]{:S(2)}, u32[]{:S(2)}) %collective-permute-start.6) | collective-permute-done | bytes 307232 | tf_op jit(solution)/shard_map/ppermute | solution.py:21
  50.0 4.4 %collective-permute-done.7 = f32[5,24,5,128]{3,1,2,0:T(8,128)S(1)} collective-permute-done((f32[5,24,5,128]{3,1,2,0:T(8,128)S(1)}, f32[5,24,5,128]{3,1,2,0:T(8,128)S(1)}, u32[]{:S(2)}, u32[]{:S(2)}) %collective-permute-start.7) | collective-permute-done | bytes 307232 | tf_op jit(solution)/shard_map/ppermute | solution.py:22
  54.6 0.2 fusion.62
  54.8 0.1 fusion.155
  55.0 0.3 fusion.70
  55.3 0.1 fusion.156
  55.4 0.3 fusion.81
  55.8 0.2 multiply_reduce_fusion
  56.0 0.2 fusion.119
  56.3 0.2 fusion.117
  56.5 0.2 fusion.108
  56.8 0.2 fusion.123
  56.9 0.2 fusion.121
  57.2 0.3 fusion.59
  57.6 0.2 fusion.164
  57.8 1.3 %collective-permute-start.9 = (f32[2,20,256]{2,1,0:T(8,128)S(1)}, f32[2,20,256]{2,1,0:T(8,128)S(1)}, u32[]{:S(2)}, u32[]{:S(2)}) collective-permute-start(f32[2,20,256]{2,1,0:T(8,128)S(1)} %get-tuple-element.44), channel_id=1, source_target_pairs={{4,0},{8,4},{12,8},{5,1},{9,5},{13,9},{6,2},{10,6},{14,10},{7,3},{... | collective-permute-start | bytes 122888 | tf_op jit(solution)/shard_map/ppermute | solution.py:30
  59.1 0.1 fusion.165
  59.3 4.0 %collective-permute-start.8 = (f32[3,20,256]{2,1,0:T(8,128)S(1)}, f32[3,20,256]{2,1,0:T(8,128)S(1)}, u32[]{:S(2)}, u32[]{:S(2)}) collective-permute-start(f32[3,20,256]{2,1,0:T(8,128)S(1)} %pad_maximum_fusion.11), channel_id=1, source_target_pairs={{0,4},{4,8},{8,12},{1,5},{5,9},{9,13},{2,6},{6,10},{10,14},{3,7},{... | collective-permute-start | bytes 184328 | tf_op jit(solution)/shard_map/ppermute | solution.py:30
  63.4 1.3 %collective-permute-done.8 = f32[3,20,256]{2,1,0:T(8,128)S(1)} collective-permute-done((f32[3,20,256]{2,1,0:T(8,128)S(1)}, f32[3,20,256]{2,1,0:T(8,128)S(1)}, u32[]{:S(2)}, u32[]{:S(2)}) %collective-permute-start.8) | collective-permute-done | bytes 61472 | tf_op jit(solution)/shard_map/ppermute | solution.py:30
  64.8 0.2 fusion.150
  65.0 0.8 %fusion.36 = f32[18,18,256]{2,1,0:T(8,128)S(1)} fusion(f32[20,20,256]{2,1,0:T(8,128)S(1)} %pad_maximum_fusion.3, f32[24,23,256]{2,1,0:T(8,128)S(1)} %divide_select_fusion, f32[2,20,256]{2,1,0:T(8,128)S(1)} %multiply_add_fusion.3, f32[16,20,256]{2,1,0:T(8,128)S(1)} %multiply_add_fusion, f32[23,24,256]{2,1,0:T(8,128)S(1)} %divide_select_fusion.1, ...), kind=kLoop, calls=%fused_computation.65 | loop fusion | flops 1575936 | bytes 4882000 | tf_op jit(solution)/shard_map/add | solution.py:106
  65.8 0.1 fusion.153
  66.0 1.1 %fusion.49 = f32[16,16,256]{2,1,0:T(8,128)} fusion(f32[18,18,256]{2,1,0:T(8,128)S(1)} %fusion.36, f32[24,24,256]{2,1,0:T(8,128)S(1)} %get-tuple-element.19, f32[16,16,255]{2,1,0:T(8,128)S(1)} %get-tuple-element.42, f32[16,16,255]{2,1,0:T(8,128)S(1)} %get-tuple-element.41, f32[24,23,256]{2,1,0:T(8,128)S(1)} %divide_select_fusion, ...), kind=kLoop, calls=%fused_computation.88 | loop fusion | flops 1114112 | bytes 4161648 | tf_op jit(solution)/shard_map/add | solution.py:106
  (84 shorter events, 2.4 us)
Async XLA Ops:
  0.0 12.5 %copy-start.3 = (f32[16,16,256]{2,1,0:T(8,128)S(1)}, f32[16,16,256]{2,1,0:T(8,128)}, u32[]{:S(2)}) copy-start(f32[16,16,256]{2,1,0:T(8,128)} %param.11) | copy-start | bytes 786436
  0.0 12.5 %copy-start.1 = (f32[16,16,256]{2,1,0:T(8,128)S(1)}, f32[16,16,256]{2,1,0:T(8,128)}, u32[]{:S(2)}) copy-start(f32[16,16,256]{2,1,0:T(8,128)} %param.12) | copy-start | bytes 786436
  0.0 12.5 %copy-start.2 = (f32[16,16,256]{2,1,0:T(8,128)S(1)}, f32[16,16,256]{2,1,0:T(8,128)}, u32[]{:S(2)}) copy-start(f32[16,16,256]{2,1,0:T(8,128)} %param.13) | copy-start | bytes 786436
  1.1 7.6 %collective-permute-start = (f32[3,4,16,256]{3,2,1,0:T(8,128)S(1)}, f32[3,4,16,256]{3,2,1,0:T(8,128)S(1)}, u32[]{:S(2)}, u32[]{:S(2)}) collective-permute-start(f32[3,4,16,256]{3,2,1,0:T(8,128)S(1)} %get-tuple-element.23), channel_id=1, source_target_pairs={{0,4},{4,8},{8,12},{1,5},{5,9},{9,13},{2,6},{6,10},{10,14},{3,7},{... | collective-permute-start | bytes 589832 | tf_op jit(solution)/shard_map/ppermute | solution.py:21
  5.2 7.3 %collective-permute-start.1 = (f32[3,4,16,256]{3,2,1,0:T(8,128)S(1)}, f32[3,4,16,256]{3,2,1,0:T(8,128)S(1)}, u32[]{:S(2)}, u32[]{:S(2)}) collective-permute-start(f32[3,4,16,256]{3,2,1,0:T(8,128)S(1)} %get-tuple-element.24), channel_id=1, source_target_pairs={{4,0},{8,4},{12,8},{5,1},{9,5},{13,9},{6,2},{10,6},{14,10},{7,3},{... | collective-permute-start | bytes 589832 | tf_op jit(solution)/shard_map/ppermute | solution.py:22
  12.6 6.9 %copy-start.9 = (s32[64]{0:T(128)S(1)}, s32[64]{0:T(128)}, u32[]{:S(2)}) copy-start(s32[64]{0:T(128)} %param.14) | copy-start | bytes 772
  12.7 10.5 %collective-permute-start.2 = (f32[3,24,4,256]{3,2,1,0:T(4,128)S(1)}, f32[3,24,4,256]{3,2,1,0:T(4,128)S(1)}, u32[]{:S(2)}, u32[]{:S(2)}) collective-permute-start(f32[3,24,4,256]{3,2,1,0:T(4,128)S(1)} %get-tuple-element.21), channel_id=1, source_target_pairs={{0,1},{1,2},{2,3},{4,5},{5,6},{6,7},{8,9},{9,10},{10,11},{12,13},{... | collective-permute-start | bytes 884744 | tf_op jit(solution)/shard_map/ppermute | solution.py:21
  17.6 8.0 %collective-permute-start.3 = (f32[3,24,4,256]{3,2,1,0:T(4,128)S(1)}, f32[3,24,4,256]{3,2,1,0:T(4,128)S(1)}, u32[]{:S(2)}, u32[]{:S(2)}) collective-permute-start(f32[3,24,4,256]{3,2,1,0:T(4,128)S(1)} %get-tuple-element.22), channel_id=1, source_target_pairs={{1,0},{2,1},{3,2},{5,4},{6,5},{7,6},{9,8},{10,9},{11,10},{13,12},{... | collective-permute-start | bytes 884744 | tf_op jit(solution)/shard_map/ppermute | solution.py:22
  29.4 0.9 %copy-start = (f32[256,128]{1,0:T(8,128)S(1)}, f32[256,128]{1,0:T(8,128)}, u32[]{:S(2)}) copy-start(f32[256,128]{1,0:T(8,128)} %constant.45.clone) | copy-start | bytes 393220
  30.6 1.0 %copy-start.4 = (f32[256,128]{1,0:T(8,128)S(1)}, f32[256,128]{1,0:T(8,128)}, u32[]{:S(2)}) copy-start(f32[256,128]{1,0:T(8,128)} %constant.46.clone) | copy-start | bytes 393220
  31.0 1.0 %copy-start.8 = (f32[136]{0:T(256)S(1)}, f32[136]{0:T(256)}, u32[]{:S(2)}) copy-start(f32[136]{0:T(256)} %constant.47.clone) | copy-start | bytes 1636
  31.0 1.0 %copy-start.10 = (pred[136,256]{1,0:T(8,128)(4,1)S(1)}, pred[136,256]{1,0:T(8,128)(4,1)}, u32[]{:S(2)}) copy-start(pred[136,256]{1,0:T(8,128)(4,1)} %constant.49.clone) | copy-start | bytes 104452
  31.6 0.8 %copy-start.6 = (pred[136,256]{1,0:T(8,128)(4,1)S(1)}, pred[136,256]{1,0:T(8,128)(4,1)}, u32[]{:S(2)}) copy-start(pred[136,256]{1,0:T(8,128)(4,1)} %constant.50.clone) | copy-start | bytes 104452
  33.1 4.7 %collective-permute-start.4 = (f32[5,4,8,128]{3,1,2,0:T(4,128)S(1)}, f32[5,4,8,128]{3,1,2,0:T(4,128)S(1)}, u32[]{:S(2)}, u32[]{:S(2)}) collective-permute-start(f32[5,4,8,128]{3,1,2,0:T(4,128)S(1)} %convolution_bitcast_fusion.1), channel_id=1, source_target_pairs={{0,4},{4,8},{8,12},{1,5},{5,9},{9,13},{2,6},{6,10},{10,14},{3,7},{... | collective-permute-start | bytes 245768 | tf_op jit(solution)/shard_map/ppermute | solution.py:30
  36.3 6.1 %collective-permute-start.5 = (f32[5,5,8,128]{3,1,2,0:T(8,128)S(1)}, f32[5,5,8,128]{3,1,2,0:T(8,128)S(1)}, u32[]{:S(2)}, u32[]{:S(2)}) collective-permute-start(f32[5,5,8,128]{3,1,2,0:T(8,128)S(1)} %pad_maximum_fusion.9), channel_id=1, source_target_pairs={{4,0},{8,4},{12,8},{5,1},{9,5},{13,9},{6,2},{10,6},{14,10},{7,3},{... | collective-permute-start | bytes 307208 | tf_op jit(solution)/shard_map/ppermute | solution.py:30
  43.1 7.0 %collective-permute-start.6 = (f32[5,24,5,128]{3,1,2,0:T(8,128)S(1)}, f32[5,24,5,128]{3,1,2,0:T(8,128)S(1)}, u32[]{:S(2)}, u32[]{:S(2)}) collective-permute-start(f32[5,24,5,128]{3,1,2,0:T(8,128)S(1)} %get-tuple-element.37), channel_id=1, source_target_pairs={{0,1},{1,2},{2,3},{4,5},{5,6},{6,7},{8,9},{9,10},{10,11},{12,13},{... | collective-permute-start | bytes 921608 | tf_op jit(solution)/shard_map/ppermute | solution.py:21
  46.3 8.2 %collective-permute-start.7 = (f32[5,24,5,128]{3,1,2,0:T(8,128)S(1)}, f32[5,24,5,128]{3,1,2,0:T(8,128)S(1)}, u32[]{:S(2)}, u32[]{:S(2)}) collective-permute-start(f32[5,24,5,128]{3,1,2,0:T(8,128)S(1)} %get-tuple-element.38), channel_id=1, source_target_pairs={{1,0},{2,1},{3,2},{5,4},{6,5},{7,6},{9,8},{10,9},{11,10},{13,12},{... | collective-permute-start | bytes 921608 | tf_op jit(solution)/shard_map/ppermute | solution.py:22
  55.8 1.4 %copy-start.5 = (pred[256,136]{1,0:T(32,128)(4,1)S(1)}, pred[256,136]{1,0:T(32,128)(4,1)}, u32[]{:S(2)}) copy-start(pred[256,136]{1,0:T(32,128)(4,1)} %constant.48.clone) | copy-start | bytes 104452
  56.5 2.6 %copy-start.7 = (f32[20,10]{1,0:T(8,128)S(1)}, f32[20,10]{1,0:T(8,128)}, u32[]{:S(2)}) copy-start(f32[20,10]{1,0:T(8,128)} %constant.51.clone) | copy-start | bytes 2404
  57.8 5.5 %collective-permute-start.9 = (f32[2,20,256]{2,1,0:T(8,128)S(1)}, f32[2,20,256]{2,1,0:T(8,128)S(1)}, u32[]{:S(2)}, u32[]{:S(2)}) collective-permute-start(f32[2,20,256]{2,1,0:T(8,128)S(1)} %get-tuple-element.44), channel_id=1, source_target_pairs={{4,0},{8,4},{12,8},{5,1},{9,5},{13,9},{6,2},{10,6},{14,10},{7,3},{... | collective-permute-start | bytes 122888 | tf_op jit(solution)/shard_map/ppermute | solution.py:30
  59.3 5.4 %collective-permute-start.8 = (f32[3,20,256]{2,1,0:T(8,128)S(1)}, f32[3,20,256]{2,1,0:T(8,128)S(1)}, u32[]{:S(2)}, u32[]{:S(2)}) collective-permute-start(f32[3,20,256]{2,1,0:T(8,128)S(1)} %pad_maximum_fusion.11), channel_id=1, source_target_pairs={{0,4},{4,8},{8,12},{1,5},{5,9},{9,13},{2,6},{6,10},{10,14},{3,7},{... | collective-permute-start | bytes 184328 | tf_op jit(solution)/shard_map/ppermute | solution.py:30

commit v17 on v16

--- a/solution.py
+++ b/solution.py
@@ -119,7 +119,6 @@
     stacked_sides = (("slab", 1), (("pencil", "sub"), 2))
     fine_rim = 2 * NU
     ext_x = padded(jnp.stack([permeability, source, pressure]), (("slab", 1),), fine_rim)
-    ext_x, aggregate = lax.optimization_barrier((ext_x, aggregate))
     ext_all = padded(ext_x, ((("pencil", "sub"), 2),), fine_rim)
     perm_ext = ext_all[0]
     source_ext = crop(ext_all[1], 1)

time: 67.6 us -> 68.6 us (1.015)
  other arithmetic: 9.81 us -> 11.7 us
  waiting for transfers between devices: 19 us -> 18.1 us
    slice x1 -> x2, other arithmetic: 1.1 us -> 2.4 us  [padded(): last = lax.slice_in_dim(array, length - width, length, axis=dim)]
    ppermute x3, waiting for transfers between devices: 10.6 us -> 9.42 us  [padded(): after = lax.ppermute(leading, axis, down)]
  transfers between devices with their start and end apart: 10 -> 10, of which waited for: 8 -> 8; matrix products, arithmetic and copies ran while one was open for 5% -> 6% of each run, Pallas kernels for 0% -> 0%
where the time goes in v17:
time: 68.6 us; the launch traced here: 68.1 us
  starting transfers between devices  27 us (39%)
  waiting for transfers between devices  18.1 us (26%)
  other arithmetic  11.7 us (17%)
  matrix products  4.49 us (7%)
  local copies, waits for them, and re-layouts  3.4 us (5%)
  between operations  3.4 us (5%)
    ppermute x3, starting transfers between devices, padded(): before = lax.ppermute(last, axis, up)  12.1 us
    ppermute x4, starting transfers between devices, passed_along(): return lax.ppermute(array, axis, pairs)  9.79 us
    ppermute x3, waiting for transfers between devices, padded(): after = lax.ppermute(leading, axis, down)  9.42 us
    ppermute x4, waiting for transfers between devices, passed_along(): return lax.ppermute(array, axis, pairs)  5.98 us
    ppermute x3, starting transfers between devices, padded(): after = lax.ppermute(leading, axis, down)  5.13 us
    add x4, other arithmetic, sweeps(): field_ext = center + OMEGA * (source_now - product) / faces_now[7]  3.85 us
    ppermute x3, waiting for transfers between devices, padded(): before = lax.ppermute(last, axis, up)  2.73 us
    slice x2, other arithmetic, padded(): last = lax.slice_in_dim(array, length - width, length, axis=dim)  2.4 us
  transfers between devices with their start and end apart: 10, of which 8 were waited for; matrix products, arithmetic and copies ran while one was open for 6% of the time, Pallas kernels for 0%

profile of v17, /device:TPU:1, one launch (start us, length us, event | category | flops | bytes accessed | tf_op | source)
XLA Modules:
  0.0 68.1 jit_solution(2406827237897840531)
XLA Ops:
  0.0 1.1 %pad_maximum_fusion.12 = (f32[3,4,16,256]{3,2,1,0:T(8,128)S(1)}, f32[3,4,16,256]{3,2,1,0:T(8,128)S(1)}) fusion(f32[1,16,16,256]{3,2,1,0:T(8,128)} %bitcast.227, f32[1,16,16,256]{3,2,1,0:T(8,128)} %bitcast.224, f32[1,16,16,256]{3,2,1,0:T(8,128)} %bitcast.230), kind=kLoop, calls=%fused_computation.127 | loop fusion | flops 196608 | bytes 1179648 | tf_op jit(solution)/shard_map/slice | solution.py:19
  1.1 4.0 %collective-permute-start = (f32[3,4,16,256]{3,2,1,0:T(8,128)S(1)}, f32[3,4,16,256]{3,2,1,0:T(8,128)S(1)}, u32[]{:S(2)}, u32[]{:S(2)}) collective-permute-start(f32[3,4,16,256]{3,2,1,0:T(8,128)S(1)} %get-tuple-element.19), channel_id=1, source_target_pairs={{0,4},{4,8},{8,12},{1,5},{5,9},{9,13},{2,6},{6,10},{10,14},{3,7},{... | collective-permute-start | bytes 589832 | tf_op jit(solution)/shard_map/ppermute | solution.py:21
  5.2 1.3 %collective-permute-start.1 = (f32[3,4,16,256]{3,2,1,0:T(8,128)S(1)}, f32[3,4,16,256]{3,2,1,0:T(8,128)S(1)}, u32[]{:S(2)}, u32[]{:S(2)}) collective-permute-start(f32[3,4,16,256]{3,2,1,0:T(8,128)S(1)} %get-tuple-element.20), channel_id=1, source_target_pairs={{4,0},{8,4},{12,8},{5,1},{9,5},{13,9},{6,2},{10,6},{14,10},{7,3},{... | collective-permute-start | bytes 589832 | tf_op jit(solution)/shard_map/ppermute | solution.py:22
  6.9 0.7 convert_element_type.122
  7.6 0.2 select_reduce_fusion
  7.7 0.7 fusion.157
  11.9 0.6 collective-permute-done.1
  12.5 1.3 %pad_maximum_fusion.9 = (f32[3,24,4,256]{3,2,1,0:T(4,128)S(1)}, f32[3,24,4,256]{3,2,1,0:T(4,128)S(1)}) fusion(f32[3,4,16,256]{3,2,1,0:T(8,128)S(1)} %collective-permute-done.1, f32[3,4,16,256]{3,2,1,0:T(8,128)S(1)} %collective-permute-done, f32[1,16,16,256]{3,2,1,0:T(8,128)} %bitcast.228, f32[1,16,16,256]{3,2,1,0:T(8,128)} %bitcast.225, ...), kind=kLoop, calls=%fused_computation.83 | loop fusion | flops 589824 | bytes 1769472 | tf_op jit(solution)/shard_map/slice | solution.py:19
  13.8 4.9 %collective-permute-start.2 = (f32[3,24,4,256]{3,2,1,0:T(4,128)S(1)}, f32[3,24,4,256]{3,2,1,0:T(4,128)S(1)}, u32[]{:S(2)}, u32[]{:S(2)}) collective-permute-start(f32[3,24,4,256]{3,2,1,0:T(4,128)S(1)} %get-tuple-element.17), channel_id=1, source_target_pairs={{0,1},{1,2},{2,3},{4,5},{5,6},{6,7},{8,9},{9,10},{10,11},{12,13},{... | collective-permute-start | bytes 884744 | tf_op jit(solution)/shard_map/ppermute | solution.py:21
  18.7 1.9 %collective-permute-start.3 = (f32[3,24,4,256]{3,2,1,0:T(4,128)S(1)}, f32[3,24,4,256]{3,2,1,0:T(4,128)S(1)}, u32[]{:S(2)}, u32[]{:S(2)}) collective-permute-start(f32[3,24,4,256]{3,2,1,0:T(4,128)S(1)} %get-tuple-element.18), channel_id=1, source_target_pairs={{1,0},{2,1},{3,2},{5,4},{6,5},{7,6},{9,8},{10,9},{11,10},{13,12},{... | collective-permute-start | bytes 884744 | tf_op jit(solution)/shard_map/ppermute | solution.py:22
  20.7 1.6 %collective-permute-done.2 = f32[3,24,4,256]{3,2,1,0:T(4,128)S(1)} collective-permute-done((f32[3,24,4,256]{3,2,1,0:T(4,128)S(1)}, f32[3,24,4,256]{3,2,1,0:T(4,128)S(1)}, u32[]{:S(2)}, u32[]{:S(2)}) %collective-permute-start.2) | collective-permute-done | bytes 294944 | tf_op jit(solution)/shard_map/ppermute | solution.py:21
  22.3 4.4 %collective-permute-done.3 = f32[3,24,4,256]{3,2,1,0:T(4,128)S(1)} collective-permute-done((f32[3,24,4,256]{3,2,1,0:T(4,128)S(1)}, f32[3,24,4,256]{3,2,1,0:T(4,128)S(1)}, u32[]{:S(2)}, u32[]{:S(2)}) %collective-permute-start.3) | collective-permute-done | bytes 294944 | tf_op jit(solution)/shard_map/ppermute | solution.py:22
  26.7 0.3 pad_maximum_fusion
  27.1 0.1 slice_bitcast_fusion
  27.2 0.2 fusion.146
  27.4 0.2 divide_select_fusion
  27.6 0.2 divide_select_fusion.1
  27.8 0.2 fusion.147
  28.0 0.2 divide_select_fusion.2
  28.3 1.1 %fusion.7 = (f32[22,22,256]{2,1,0:T(8,128)S(1)}, f32[22,22,256]{2,1,0:T(8,128)S(1)}, f32[22,22,256]{2,1,0:T(8,128)S(1)}) fusion(f32[24,24,256]{2,1,0:T(8,128)S(1)} %get-tuple-element.16, f32[24,24,256]{2,1,0:T(8,128)S(1)} %get-tuple-element.15, f32[22,22,255]{2,1,0:T(8,128)S(1)} %get-tuple-element.26, f32[22,22,255]{2,1,0:T(8,128)S(1)} %get-tuple-element.25, ...), kind=kLoop, calls=%fused_computation.21 | loop fusion | flops 3345408 | bytes 8423108 | tf_op jit(solution)/shard_map/add | solution.py:106
  29.3 0.2 fusion.148
  29.5 0.8 %fusion.26 = f32[20,20,256]{2,1,0:T(8,128)S(1)} fusion(f32[22,22,256]{2,1,0:T(8,128)S(1)} %get-tuple-element.11, f32[24,23,256]{2,1,0:T(8,128)S(1)} %divide_select_fusion, f32[23,24,256]{2,1,0:T(8,128)S(1)} %divide_select_fusion.1, f32[24,24,256]{2,1,0:T(8,128)S(1)} %get-tuple-element.15, f32[20,20,255]{2,1,0:T(8,128)S(1)} %get-tuple-element.30, ...), kind=kLoop, calls=%fused_computation.48 | loop fusion | flops 1740800 | bytes 6224880 | tf_op jit(solution)/shard_map/add | solution.py:106
  30.4 0.1 fusion.151
  30.5 0.5 fusion.145
  31.1 0.4 copy-done
  31.4 0.3 fusion.158
  31.7 0.3 fusion.159
  32.1 0.3 fusion.161
  32.4 0.3 fusion.160
  32.7 0.3 fusion.11
  33.1 0.3 fusion.162
  33.4 0.2 convolution_bitcast_fusion.2
  33.9 0.3 convolution_bitcast_fusion.1
  34.1 3.2 %collective-permute-start.4 = (f32[5,4,8,128]{3,1,2,0:T(4,128)S(1)}, f32[5,4,8,128]{3,1,2,0:T(4,128)S(1)}, u32[]{:S(2)}, u32[]{:S(2)}) collective-permute-start(f32[5,4,8,128]{3,1,2,0:T(4,128)S(1)} %convolution_bitcast_fusion.1), channel_id=1, source_target_pairs={{0,4},{4,8},{8,12},{1,5},{5,9},{9,13},{2,6},{6,10},{10,14},{3,7},{... | collective-permute-start | bytes 245768 | tf_op jit(solution)/shard_map/ppermute | solution.py:30
  37.3 1.3 %collective-permute-start.5 = (f32[5,5,8,128]{3,1,2,0:T(8,128)S(1)}, f32[5,5,8,128]{3,1,2,0:T(8,128)S(1)}, u32[]{:S(2)}, u32[]{:S(2)}) collective-permute-start(f32[5,5,8,128]{3,1,2,0:T(8,128)S(1)} %pad_maximum_fusion.13), channel_id=1, source_target_pairs={{4,0},{8,4},{12,8},{5,1},{9,5},{13,9},{6,2},{10,6},{14,10},{7,3},{... | collective-permute-start | bytes 307208 | tf_op jit(solution)/shard_map/ppermute | solution.py:30
  38.6 0.1 collective-permute-done.4
  38.9 4.5 %collective-permute-done.5 = f32[5,5,8,128]{3,1,2,0:T(8,128)S(1)} collective-permute-done((f32[5,5,8,128]{3,1,2,0:T(8,128)S(1)}, f32[5,5,8,128]{3,1,2,0:T(8,128)S(1)}, u32[]{:S(2)}, u32[]{:S(2)}) %collective-permute-start.5) | collective-permute-done | bytes 102432 | tf_op jit(solution)/shard_map/ppermute | solution.py:30
  43.5 0.5 maximum_add_fusion
  44.1 3.2 %collective-permute-start.6 = (f32[5,24,5,128]{3,1,2,0:T(8,128)S(1)}, f32[5,24,5,128]{3,1,2,0:T(8,128)S(1)}, u32[]{:S(2)}, u32[]{:S(2)}) collective-permute-start(f32[5,24,5,128]{3,1,2,0:T(8,128)S(1)} %get-tuple-element.33), channel_id=1, source_target_pairs={{0,1},{1,2},{2,3},{4,5},{5,6},{6,7},{8,9},{9,10},{10,11},{12,13},{... | collective-permute-start | bytes 921608 | tf_op jit(solution)/shard_map/ppermute | solution.py:21
  47.3 1.9 %collective-permute-start.7 = (f32[5,24,5,128]{3,1,2,0:T(8,128)S(1)}, f32[5,24,5,128]{3,1,2,0:T(8,128)S(1)}, u32[]{:S(2)}, u32[]{:S(2)}) collective-permute-start(f32[5,24,5,128]{3,1,2,0:T(8,128)S(1)} %get-tuple-element.34), channel_id=1, source_target_pairs={{1,0},{2,1},{3,2},{5,4},{6,5},{7,6},{9,8},{10,9},{11,10},{13,12},{... | collective-permute-start | bytes 921608 | tf_op jit(solution)/shard_map/ppermute | solution.py:22
  49.2 0.7 %and_convert_fusion = f32[2]{0:T(128)S(1)} fusion(s32[19]{0:T(128)S(1)} %iota_add_fusion, f32[19]{0:T(128)S(1)} %select_reduce_fusion, f32[]{:T(128)} %bitcast.21), kind=kLoop, calls=%fused_computation.251 | loop fusion | flops 8 | bytes 28 | tf_op jit(solution)/shard_map/convert_element_type | solution.py:294
  50.0 1.1 %collective-permute-done.6 = f32[5,24,5,128]{3,1,2,0:T(8,128)S(1)} collective-permute-done((f32[5,24,5,128]{3,1,2,0:T(8,128)S(1)}, f32[5,24,5,128]{3,1,2,0:T(8,128)S(1)}, u32[]{:S(2)}, u32[]{:S(2)}) %collective-permute-start.6) | collective-permute-done | bytes 307232 | tf_op jit(solution)/shard_map/ppermute | solution.py:21
  51.1 4.4 %collective-permute-done.7 = f32[5,24,5,128]{3,1,2,0:T(8,128)S(1)} collective-permute-done((f32[5,24,5,128]{3,1,2,0:T(8,128)S(1)}, f32[5,24,5,128]{3,1,2,0:T(8,128)S(1)}, u32[]{:S(2)}, u32[]{:S(2)}) %collective-permute-start.7) | collective-permute-done | bytes 307232 | tf_op jit(solution)/shard_map/ppermute | solution.py:22
  55.6 0.2 fusion.62
  55.9 0.1 fusion.154
  56.0 0.3 fusion.70
  56.3 0.1 fusion.155
  56.4 0.3 fusion.81
  56.8 0.2 multiply_reduce_fusion
  57.1 0.2 fusion.119
  57.3 0.2 fusion.117
  57.5 0.2 fusion.108
  57.8 0.2 fusion.123
  58.0 0.2 fusion.121
  58.2 0.3 fusion.59
  58.6 0.2 fusion.163
  58.8 1.3 %collective-permute-start.9 = (f32[2,20,256]{2,1,0:T(8,128)S(1)}, f32[2,20,256]{2,1,0:T(8,128)S(1)}, u32[]{:S(2)}, u32[]{:S(2)}) collective-permute-start(f32[2,20,256]{2,1,0:T(8,128)S(1)} %get-tuple-element.40), channel_id=1, source_target_pairs={{4,0},{8,4},{12,8},{5,1},{9,5},{13,9},{6,2},{10,6},{14,10},{7,3},{... | collective-permute-start | bytes 122888 | tf_op jit(solution)/shard_map/ppermute | solution.py:30
  60.1 0.1 fusion.164
  60.3 4.0 %collective-permute-start.8 = (f32[3,20,256]{2,1,0:T(8,128)S(1)}, f32[3,20,256]{2,1,0:T(8,128)S(1)}, u32[]{:S(2)}, u32[]{:S(2)}) collective-permute-start(f32[3,20,256]{2,1,0:T(8,128)S(1)} %pad_maximum_fusion.15), channel_id=1, source_target_pairs={{0,4},{4,8},{8,12},{1,5},{5,9},{9,13},{2,6},{6,10},{10,14},{3,7},{... | collective-permute-start | bytes 184328 | tf_op jit(solution)/shard_map/ppermute | solution.py:30
  64.4 1.3 %collective-permute-done.8 = f32[3,20,256]{2,1,0:T(8,128)S(1)} collective-permute-done((f32[3,20,256]{2,1,0:T(8,128)S(1)}, f32[3,20,256]{2,1,0:T(8,128)S(1)}, u32[]{:S(2)}, u32[]{:S(2)}) %collective-permute-start.8) | collective-permute-done | bytes 61472 | tf_op jit(solution)/shard_map/ppermute | solution.py:30
  65.8 0.2 fusion.149
  66.0 0.8 %fusion.36 = f32[18,18,256]{2,1,0:T(8,128)S(1)} fusion(f32[20,20,256]{2,1,0:T(8,128)S(1)} %pad_maximum_fusion.2, f32[24,23,256]{2,1,0:T(8,128)S(1)} %divide_select_fusion, f32[2,20,256]{2,1,0:T(8,128)S(1)} %multiply_add_fusion.3, f32[16,20,256]{2,1,0:T(8,128)S(1)} %multiply_add_fusion, f32[23,24,256]{2,1,0:T(8,128)S(1)} %divide_select_fusion.1, ...), kind=kLoop, calls=%fused_computation.64 | loop fusion | flops 1575936 | bytes 4882000 | tf_op jit(solution)/shard_map/add | solution.py:106
  66.8 0.1 fusion.152
  67.0 1.1 %fusion.49 = f32[16,16,256]{2,1,0:T(8,128)} fusion(f32[18,18,256]{2,1,0:T(8,128)S(1)} %fusion.36, f32[24,24,256]{2,1,0:T(8,128)S(1)} %get-tuple-element.15, f32[16,16,255]{2,1,0:T(8,128)S(1)} %get-tuple-element.38, f32[16,16,255]{2,1,0:T(8,128)S(1)} %get-tuple-element.37, f32[24,23,256]{2,1,0:T(8,128)S(1)} %divide_select_fusion, ...), kind=kLoop, calls=%fused_computation.92 | loop fusion | flops 1114112 | bytes 4161648 | tf_op jit(solution)/shard_map/add | solution.py:106
  (81 shorter events, 2.3 us)
Async XLA Ops:
  0.0 26.7 %copy-start.3 = (f32[16,16,256]{2,1,0:T(8,128)S(1)}, f32[16,16,256]{2,1,0:T(8,128)}, u32[]{:S(2)}) copy-start(f32[16,16,256]{2,1,0:T(8,128)} %param.11) | copy-start | bytes 786436
  0.0 26.7 %copy-start.1 = (f32[16,16,256]{2,1,0:T(8,128)S(1)}, f32[16,16,256]{2,1,0:T(8,128)}, u32[]{:S(2)}) copy-start(f32[16,16,256]{2,1,0:T(8,128)} %param.12) | copy-start | bytes 786436
  0.0 26.7 %copy-start.2 = (f32[16,16,256]{2,1,0:T(8,128)S(1)}, f32[16,16,256]{2,1,0:T(8,128)}, u32[]{:S(2)}) copy-start(f32[16,16,256]{2,1,0:T(8,128)} %param.13) | copy-start | bytes 786436
  1.1 10.8 %collective-permute-start = (f32[3,4,16,256]{3,2,1,0:T(8,128)S(1)}, f32[3,4,16,256]{3,2,1,0:T(8,128)S(1)}, u32[]{:S(2)}, u32[]{:S(2)}) collective-permute-start(f32[3,4,16,256]{3,2,1,0:T(8,128)S(1)} %get-tuple-element.19), channel_id=1, source_target_pairs={{0,4},{4,8},{8,12},{1,5},{5,9},{9,13},{2,6},{6,10},{10,14},{3,7},{... | collective-permute-start | bytes 589832 | tf_op jit(solution)/shard_map/ppermute | solution.py:21
  5.2 7.3 %collective-permute-start.1 = (f32[3,4,16,256]{3,2,1,0:T(8,128)S(1)}, f32[3,4,16,256]{3,2,1,0:T(8,128)S(1)}, u32[]{:S(2)}, u32[]{:S(2)}) collective-permute-start(f32[3,4,16,256]{3,2,1,0:T(8,128)S(1)} %get-tuple-element.20), channel_id=1, source_target_pairs={{4,0},{8,4},{12,8},{5,1},{9,5},{13,9},{6,2},{10,6},{14,10},{7,3},{... | collective-permute-start | bytes 589832 | tf_op jit(solution)/shard_map/ppermute | solution.py:22
  13.8 8.5 %collective-permute-start.2 = (f32[3,24,4,256]{3,2,1,0:T(4,128)S(1)}, f32[3,24,4,256]{3,2,1,0:T(4,128)S(1)}, u32[]{:S(2)}, u32[]{:S(2)}) collective-permute-start(f32[3,24,4,256]{3,2,1,0:T(4,128)S(1)} %get-tuple-element.17), channel_id=1, source_target_pairs={{0,1},{1,2},{2,3},{4,5},{5,6},{6,7},{8,9},{9,10},{10,11},{12,13},{... | collective-permute-start | bytes 884744 | tf_op jit(solution)/shard_map/ppermute | solution.py:21
  18.7 8.0 %collective-permute-start.3 = (f32[3,24,4,256]{3,2,1,0:T(4,128)S(1)}, f32[3,24,4,256]{3,2,1,0:T(4,128)S(1)}, u32[]{:S(2)}, u32[]{:S(2)}) collective-permute-start(f32[3,24,4,256]{3,2,1,0:T(4,128)S(1)} %get-tuple-element.18), channel_id=1, source_target_pairs={{1,0},{2,1},{3,2},{5,4},{6,5},{7,6},{9,8},{10,9},{11,10},{13,12},{... | collective-permute-start | bytes 884744 | tf_op jit(solution)/shard_map/ppermute | solution.py:22
  30.5 0.9 %copy-start = (f32[256,128]{1,0:T(8,128)S(1)}, f32[256,128]{1,0:T(8,128)}, u32[]{:S(2)}) copy-start(f32[256,128]{1,0:T(8,128)} %constant.45.clone) | copy-start | bytes 393220
  31.0 1.4 %copy-start.4 = (f32[256,128]{1,0:T(8,128)S(1)}, f32[256,128]{1,0:T(8,128)}, u32[]{:S(2)}) copy-start(f32[256,128]{1,0:T(8,128)} %constant.46.clone) | copy-start | bytes 393220
  31.0 1.7 %copy-start.8 = (f32[136]{0:T(256)S(1)}, f32[136]{0:T(256)}, u32[]{:S(2)}) copy-start(f32[136]{0:T(256)} %constant.47.clone) | copy-start | bytes 1636
  31.0 1.7 %copy-start.9 = (pred[136,256]{1,0:T(8,128)(4,1)S(1)}, pred[136,256]{1,0:T(8,128)(4,1)}, u32[]{:S(2)}) copy-start(pred[136,256]{1,0:T(8,128)(4,1)} %constant.49.clone) | copy-start | bytes 104452
  32.1 1.4 %copy-start.6 = (pred[136,256]{1,0:T(8,128)(4,1)S(1)}, pred[136,256]{1,0:T(8,128)(4,1)}, u32[]{:S(2)}) copy-start(pred[136,256]{1,0:T(8,128)(4,1)} %constant.50.clone) | copy-start | bytes 104452
  34.1 4.7 %collective-permute-start.4 = (f32[5,4,8,128]{3,1,2,0:T(4,128)S(1)}, f32[5,4,8,128]{3,1,2,0:T(4,128)S(1)}, u32[]{:S(2)}, u32[]{:S(2)}) collective-permute-start(f32[5,4,8,128]{3,1,2,0:T(4,128)S(1)} %convolution_bitcast_fusion.1), channel_id=1, source_target_pairs={{0,4},{4,8},{8,12},{1,5},{5,9},{9,13},{2,6},{6,10},{10,14},{3,7},{... | collective-permute-start | bytes 245768 | tf_op jit(solution)/shard_map/ppermute | solution.py:30
  37.3 6.1 %collective-permute-start.5 = (f32[5,5,8,128]{3,1,2,0:T(8,128)S(1)}, f32[5,5,8,128]{3,1,2,0:T(8,128)S(1)}, u32[]{:S(2)}, u32[]{:S(2)}) collective-permute-start(f32[5,5,8,128]{3,1,2,0:T(8,128)S(1)} %pad_maximum_fusion.13), channel_id=1, source_target_pairs={{4,0},{8,4},{12,8},{5,1},{9,5},{13,9},{6,2},{10,6},{14,10},{7,3},{... | collective-permute-start | bytes 307208 | tf_op jit(solution)/shard_map/ppermute | solution.py:30
  44.1 7.0 %collective-permute-start.6 = (f32[5,24,5,128]{3,1,2,0:T(8,128)S(1)}, f32[5,24,5,128]{3,1,2,0:T(8,128)S(1)}, u32[]{:S(2)}, u32[]{:S(2)}) collective-permute-start(f32[5,24,5,128]{3,1,2,0:T(8,128)S(1)} %get-tuple-element.33), channel_id=1, source_target_pairs={{0,1},{1,2},{2,3},{4,5},{5,6},{6,7},{8,9},{9,10},{10,11},{12,13},{... | collective-permute-start | bytes 921608 | tf_op jit(solution)/shard_map/ppermute | solution.py:21
  47.3 8.2 %collective-permute-start.7 = (f32[5,24,5,128]{3,1,2,0:T(8,128)S(1)}, f32[5,24,5,128]{3,1,2,0:T(8,128)S(1)}, u32[]{:S(2)}, u32[]{:S(2)}) collective-permute-start(f32[5,24,5,128]{3,1,2,0:T(8,128)S(1)} %get-tuple-element.34), channel_id=1, source_target_pairs={{1,0},{2,1},{3,2},{5,4},{6,5},{7,6},{9,8},{10,9},{11,10},{13,12},{... | collective-permute-start | bytes 921608 | tf_op jit(solution)/shard_map/ppermute | solution.py:22
  56.7 1.5 %copy-start.5 = (pred[256,136]{1,0:T(32,128)(4,1)S(1)}, pred[256,136]{1,0:T(32,128)(4,1)}, u32[]{:S(2)}) copy-start(pred[256,136]{1,0:T(32,128)(4,1)} %constant.48.clone) | copy-start | bytes 104452
  57.0 3.1 %copy-start.7 = (f32[20,10]{1,0:T(8,128)S(1)}, f32[20,10]{1,0:T(8,128)}, u32[]{:S(2)}) copy-start(f32[20,10]{1,0:T(8,128)} %constant.51.clone) | copy-start | bytes 2404
  58.8 5.5 %collective-permute-start.9 = (f32[2,20,256]{2,1,0:T(8,128)S(1)}, f32[2,20,256]{2,1,0:T(8,128)S(1)}, u32[]{:S(2)}, u32[]{:S(2)}) collective-permute-start(f32[2,20,256]{2,1,0:T(8,128)S(1)} %get-tuple-element.40), channel_id=1, source_target_pairs={{4,0},{8,4},{12,8},{5,1},{9,5},{13,9},{6,2},{10,6},{14,10},{7,3},{... | collective-permute-start | bytes 122888 | tf_op jit(solution)/shard_map/ppermute | solution.py:30
  60.3 5.4 %collective-permute-start.8 = (f32[3,20,256]{2,1,0:T(8,128)S(1)}, f32[3,20,256]{2,1,0:T(8,128)S(1)}, u32[]{:S(2)}, u32[]{:S(2)}) collective-permute-start(f32[3,20,256]{2,1,0:T(8,128)S(1)} %pad_maximum_fusion.15), channel_id=1, source_target_pairs={{0,4},{4,8},{8,12},{1,5},{5,9},{9,13},{2,6},{6,10},{10,14},{3,7},{... | collective-permute-start | bytes 184328 | tf_op jit(solution)/shard_map/ppermute | solution.py:30

commit v18 on v16

--- a/solution.py
+++ b/solution.py
@@ -202,9 +202,14 @@
     tail_pick = (slot_range[None, :] == count_live - NCS + jnp.arange(NCS)[:, None]).astype(jnp.float32)
     tail_planes = jnp.einsum("ks,qsjl->qkjl", tail_pick, coarse, precision=lax.Precision.HIGHEST)
     head_planes = jnp.concatenate([coarse[:, :NCS], edge_sums[:, None]], axis=1)
-    tail_planes, head_planes = lax.optimization_barrier((tail_planes, head_planes))
-    from_prev = passed_along(tail_planes, "slab", 1)
-    from_next = passed_along(head_planes, "slab", -1)
+    tail_wide = jnp.concatenate([tail_planes, jnp.zeros_like(edge_sums[:, None])], axis=1)
+    slab_range = jnp.arange(slab_count)
+    to_next = (slab_range == slab_index + 1).astype(jnp.float32)[:, None, None, None, None]
+    to_prev = (slab_range == slab_index - 1).astype(jnp.float32)[:, None, None, None, None]
+    outgoing = to_next * tail_wide[None] + to_prev * head_planes[None]
+    incoming = lax.all_to_all(outgoing, "slab", 0, 0, tiled=False)
+    from_prev = jnp.sum(to_prev * incoming, axis=0)[:, :NCS]
+    from_next = jnp.sum(to_next * incoming, axis=0)
     coarse = coarse + from_next[:, NCS][:, None] * last_slot[None, :, None, None]
     prev_last = (jnp.arange(NCS) == NCS - 1).astype(jnp.float32)
     from_prev = from_prev + edge_sums[:, None] * prev_last[None, :, None, None]

time: 67.6 us -> 75.8 us (1.12)
  waiting for transfers between devices: 19 us -> 22.6 us
  other arithmetic: 9.81 us -> 11.9 us
  local copies, waits for them, and re-layouts: 3.6 us -> 5.13 us
  starting transfers between devices: 27 us -> 27.8 us
    all_to_all x0 -> x1, waiting for transfers between devices: none -> 8.14 us  [body(): incoming = lax.all_to_all(outgoing, 'slab', 0, 0, tiled=False)]
    ppermute x4 -> x2, waiting for transfers between devices: 5.98 us -> 1.3 us  [passed_along(): return lax.ppermute(array, axis, pairs)]
    ppermute x4 -> x2, starting transfers between devices: 9.79 us -> 5.3 us  [passed_along(): return lax.ppermute(array, axis, pairs)]
    all_to_all x0 -> x1, starting transfers between devices: none -> 4.11 us  [body(): incoming = lax.all_to_all(outgoing, 'slab', 0, 0, tiled=False)]
    unnamed x26 -> x33, local copies, waits for them, and re-layouts: 0.56 us -> 2.09 us
    reduce_sum x0 -> x1, other arithmetic: none -> 1.2 us  [body(): from_prev = jnp.sum(to_prev * incoming, axis=0)[:, :NCS]]
    ppermute x3, starting transfers between devices: 12.1 us -> 13.3 us  [padded(): before = lax.ppermute(last, axis, up)]
    add x0 -> x1, other arithmetic: none -> 0.86 us  [body(): outgoing = to_next * tail_wide[None] + to_prev * head_planes[None]]
  transfers between devices with their start and end apart: 10 -> 9, of which waited for: 8 -> 7; matrix products, arithmetic and copies ran while one was open for 5% -> 4% of each run, Pallas kernels for 0% -> 0%
where the time goes in v18:
time: 75.8 us; the launch traced here: 75.2 us
  starting transfers between devices  27.8 us (37%)
  waiting for transfers between devices  22.6 us (30%)
  other arithmetic  11.9 us (16%)
  local copies, waits for them, and re-layouts  5.13 us (7%)
  matrix products  4.49 us (6%)
  between operations  3.35 us (4%)
    ppermute x3, starting transfers between devices, padded(): before = lax.ppermute(last, axis, up)  13.3 us
    ppermute x3, waiting for transfers between devices, padded(): after = lax.ppermute(leading, axis, down)  10.6 us
    all_to_all x1, waiting for transfers between devices, body(): incoming = lax.all_to_all(outgoing, 'slab', 0, 0, tiled=False)  8.14 us
    ppermute x2, starting transfers between devices, passed_along(): return lax.ppermute(array, axis, pairs)  5.3 us
    ppermute x3, starting transfers between devices, padded(): after = lax.ppermute(leading, axis, down)  5.13 us
    all_to_all x1, starting transfers between devices, body(): incoming = lax.all_to_all(outgoing, 'slab', 0, 0, tiled=False)  4.11 us
    add x4, other arithmetic, sweeps(): field_ext = center + OMEGA * (source_now - product) / faces_now[7]  3.96 us
    ppermute x3, waiting for transfers between devices, padded(): before = lax.ppermute(last, axis, up)  2.57 us
  transfers between devices with their start and end apart: 9, of which 7 were waited for; matrix products, arithmetic and copies ran while one was open for 4% of the time, Pallas kernels for 0%

profile of v18, /device:TPU:1, one launch (start us, length us, event | category | flops | bytes accessed | tf_op | source)
XLA Modules:
  0.0 75.2 jit_solution(6022395427319444373)
XLA Ops:
  0.0 1.1 %pad_maximum_fusion.8 = (f32[3,4,16,256]{3,2,1,0:T(8,128)S(1)}, f32[3,4,16,256]{3,2,1,0:T(8,128)S(1)}) fusion(f32[1,16,16,256]{3,2,1,0:T(8,128)} %bitcast.232, f32[1,16,16,256]{3,2,1,0:T(8,128)} %bitcast.225, f32[1,16,16,256]{3,2,1,0:T(8,128)} %bitcast.234), kind=kLoop, calls=%fused_computation.126 | loop fusion | flops 196608 | bytes 1179648 | tf_op jit(solution)/shard_map/slice | solution.py:19
  1.1 4.0 %collective-permute-start = (f32[3,4,16,256]{3,2,1,0:T(8,128)S(1)}, f32[3,4,16,256]{3,2,1,0:T(8,128)S(1)}, u32[]{:S(2)}, u32[]{:S(2)}) collective-permute-start(f32[3,4,16,256]{3,2,1,0:T(8,128)S(1)} %get-tuple-element.21), channel_id=1, source_target_pairs={{0,4},{4,8},{8,12},{1,5},{5,9},{9,13},{2,6},{6,10},{10,14},{3,7},{... | collective-permute-start | bytes 589832 | tf_op jit(solution)/shard_map/ppermute | solution.py:21
  5.2 1.3 %collective-permute-start.1 = (f32[3,4,16,256]{3,2,1,0:T(8,128)S(1)}, f32[3,4,16,256]{3,2,1,0:T(8,128)S(1)}, u32[]{:S(2)}, u32[]{:S(2)}) collective-permute-start(f32[3,4,16,256]{3,2,1,0:T(8,128)S(1)} %get-tuple-element.22), channel_id=1, source_target_pairs={{4,0},{8,4},{12,8},{5,1},{9,5},{13,9},{6,2},{10,6},{14,10},{7,3},{... | collective-permute-start | bytes 589832 | tf_op jit(solution)/shard_map/ppermute | solution.py:22
  7.4 1.3 %collective-permute-done = f32[3,4,16,256]{3,2,1,0:T(8,128)S(1)} collective-permute-done((f32[3,4,16,256]{3,2,1,0:T(8,128)S(1)}, f32[3,4,16,256]{3,2,1,0:T(8,128)S(1)}, u32[]{:S(2)}, u32[]{:S(2)}) %collective-permute-start) | collective-permute-done | bytes 196640 | tf_op jit(solution)/shard_map/ppermute | solution.py:21
  8.7 3.8 %collective-permute-done.1 = f32[3,4,16,256]{3,2,1,0:T(8,128)S(1)} collective-permute-done((f32[3,4,16,256]{3,2,1,0:T(8,128)S(1)}, f32[3,4,16,256]{3,2,1,0:T(8,128)S(1)}, u32[]{:S(2)}, u32[]{:S(2)}) %collective-permute-start.1) | collective-permute-done | bytes 196640 | tf_op jit(solution)/shard_map/ppermute | solution.py:22
  12.6 0.1 fusion.144
  12.7 4.9 %collective-permute-start.2 = (f32[3,24,4,256]{3,2,1,0:T(4,128)S(1)}, f32[3,24,4,256]{3,2,1,0:T(4,128)S(1)}, u32[]{:S(2)}, u32[]{:S(2)}) collective-permute-start(f32[3,24,4,256]{3,2,1,0:T(4,128)S(1)} %get-tuple-element.19), channel_id=1, source_target_pairs={{0,1},{1,2},{2,3},{4,5},{5,6},{6,7},{8,9},{9,10},{10,11},{12,13},{... | collective-permute-start | bytes 884744 | tf_op jit(solution)/shard_map/ppermute | solution.py:21
  17.6 1.9 %collective-permute-start.3 = (f32[3,24,4,256]{3,2,1,0:T(4,128)S(1)}, f32[3,24,4,256]{3,2,1,0:T(4,128)S(1)}, u32[]{:S(2)}, u32[]{:S(2)}) collective-permute-start(f32[3,24,4,256]{3,2,1,0:T(4,128)S(1)} %get-tuple-element.20), channel_id=1, source_target_pairs={{1,0},{2,1},{3,2},{5,4},{6,5},{7,6},{9,8},{10,9},{11,10},{13,12},{... | collective-permute-start | bytes 884744 | tf_op jit(solution)/shard_map/ppermute | solution.py:22
  19.6 0.2 select_reduce_fusion
  19.7 0.7 fusion.157
  23.3 2.4 %collective-permute-done.3 = f32[3,24,4,256]{3,2,1,0:T(4,128)S(1)} collective-permute-done((f32[3,24,4,256]{3,2,1,0:T(4,128)S(1)}, f32[3,24,4,256]{3,2,1,0:T(4,128)S(1)}, u32[]{:S(2)}, u32[]{:S(2)}) %collective-permute-start.3) | collective-permute-done | bytes 294944 | tf_op jit(solution)/shard_map/ppermute | solution.py:22
  25.7 0.3 pad_maximum_fusion
  25.9 0.1 slice_bitcast_fusion
  26.1 0.2 fusion.146
  26.3 0.2 divide_select_fusion
  26.5 0.2 divide_select_fusion.1
  26.7 0.2 fusion.147
  26.9 0.2 divide_select_fusion.2
  27.1 1.1 %fusion.8 = (f32[22,22,256]{2,1,0:T(8,128)S(1)}, f32[22,22,256]{2,1,0:T(8,128)S(1)}, f32[22,22,256]{2,1,0:T(8,128)S(1)}) fusion(f32[24,24,256]{2,1,0:T(8,128)S(1)} %get-tuple-element.18, f32[24,24,256]{2,1,0:T(8,128)S(1)} %get-tuple-element.17, f32[22,22,255]{2,1,0:T(8,128)S(1)} %get-tuple-element.28, f32[22,22,255]{2,1,0:T(8,128)S(1)} %get-tuple-element.27, ...), kind=kLoop, calls=%fused_computation.23 | loop fusion | flops 3345408 | bytes 8423108 | tf_op jit(solution)/shard_map/add | solution.py:106
  28.2 0.2 fusion.148
  28.4 0.8 %fusion.27 = f32[20,20,256]{2,1,0:T(8,128)S(1)} fusion(f32[22,22,256]{2,1,0:T(8,128)S(1)} %get-tuple-element.13, f32[24,23,256]{2,1,0:T(8,128)S(1)} %divide_select_fusion, f32[23,24,256]{2,1,0:T(8,128)S(1)} %divide_select_fusion.1, f32[24,24,256]{2,1,0:T(8,128)S(1)} %get-tuple-element.17, f32[20,20,255]{2,1,0:T(8,128)S(1)} %get-tuple-element.32, ...), kind=kLoop, calls=%fused_computation.50 | loop fusion | flops 1740800 | bytes 6224880 | tf_op jit(solution)/shard_map/add | solution.py:106
  29.3 0.1 fusion.151
  29.4 0.8 %copy-done.2 = f32[16,16,256]{2,1,0:T(8,128)S(1)} copy-done((f32[16,16,256]{2,1,0:T(8,128)S(1)}, f32[16,16,256]{2,1,0:T(8,128)}, u32[]{:S(2)}) %copy-start.2) | copy-done | bytes 262168
  30.2 0.5 fusion.145
  30.7 0.4 copy-done
  31.1 0.3 fusion.162
  31.4 0.3 fusion.158
  31.8 0.3 fusion.159
  32.1 0.3 fusion.161
  32.5 0.3 fusion.160
  32.8 0.3 fusion.12
  33.2 0.2 convolution_bitcast_fusion.2
  33.6 0.7 copy-done.3
  34.3 0.3 convolution_bitcast_fusion.1
  34.7 0.9 %multiply_add_fusion = f32[4,5,5,8,128]{4,3,2,1,0:T(8,128)} fusion(f32[5,5,8,128]{3,2,1,0:T(8,128)S(1)} %copy.33, f32[5,5,8,128]{3,2,1,0:T(8,128)S(1)} %concatenate.120.clone, f32[4]{0:T(128)S(1)} %get-tuple-element.62, f32[4]{0:T(128)S(1)} %get-tuple-element.63), kind=kLoop, calls=%fused_computation.78 | loop fusion | flops 307200 | bytes 614432 | tf_op jit(solution)/shard_map/add | solution.py:209
  35.6 4.1 %all-to-all-start = ((f32[4,5,5,8,128]{4,3,2,1,0:T(8,128)}), f32[4,5,5,8,128]{4,3,2,1,0:T(8,128)}, u32[]{:S(2)}, u32[]{:S(2)}) async-start(f32[4,5,5,8,128]{4,3,2,1,0:T(8,128)} %multiply_add_fusion), calls=%async_computation | async-start | bytes 819200 | tf_op jit(solution)/shard_map/all_to_all | solution.py:210
  39.8 8.1 %all-to-all-done = f32[4,5,5,8,128]{4,3,2,1,0:T(8,128)} async-done(((f32[4,5,5,8,128]{4,3,2,1,0:T(8,128)}), f32[4,5,5,8,128]{4,3,2,1,0:T(8,128)}, u32[]{:S(2)}, u32[]{:S(2)}) %all-to-all-start) | async-done | bytes 409632 | tf_op jit(solution)/shard_map/all_to_all | solution.py:210
  47.9 1.2 %multiply_reduce_fusion.1 = (f32[5,5,8,128]{3,2,1,0:T(8,128)S(1)}, f32[5,5,8,128]{3,2,1,0:T(8,128)S(1)}) fusion(f32[4,5,5,8,128]{4,3,2,1,0:T(8,128)} %all-to-all-done, f32[4]{0:T(128)S(1)} %get-tuple-element.63, f32[4]{0:T(128)S(1)} %get-tuple-element.62), kind=kLoop, calls=%fused_computation.77 | loop fusion | flops 358400 | bytes 614432 | tf_op jit(solution)/shard_map/reduce_sum | solution.py:211
  49.4 0.5 fusion
  50.0 4.3 %collective-permute-start.4 = (f32[5,24,5,128]{3,1,2,0:T(8,128)S(1)}, f32[5,24,5,128]{3,1,2,0:T(8,128)S(1)}, u32[]{:S(2)}, u32[]{:S(2)}) collective-permute-start(f32[5,24,5,128]{3,1,2,0:T(8,128)S(1)} %get-tuple-element.35), channel_id=1, source_target_pairs={{0,1},{1,2},{2,3},{4,5},{5,6},{6,7},{8,9},{9,10},{10,11},{12,13},{... | collective-permute-start | bytes 921608 | tf_op jit(solution)/shard_map/ppermute | solution.py:21
  54.3 1.9 %collective-permute-start.5 = (f32[5,24,5,128]{3,1,2,0:T(8,128)S(1)}, f32[5,24,5,128]{3,1,2,0:T(8,128)S(1)}, u32[]{:S(2)}, u32[]{:S(2)}) collective-permute-start(f32[5,24,5,128]{3,1,2,0:T(8,128)S(1)} %get-tuple-element.36), channel_id=1, source_target_pairs={{1,0},{2,1},{3,2},{5,4},{6,5},{7,6},{9,8},{10,9},{11,10},{13,12},{... | collective-permute-start | bytes 921608 | tf_op jit(solution)/shard_map/ppermute | solution.py:22
  56.2 0.6 and_convert_fusion
  56.9 1.2 %collective-permute-done.4 = f32[5,24,5,128]{3,1,2,0:T(8,128)S(1)} collective-permute-done((f32[5,24,5,128]{3,1,2,0:T(8,128)S(1)}, f32[5,24,5,128]{3,1,2,0:T(8,128)S(1)}, u32[]{:S(2)}, u32[]{:S(2)}) %collective-permute-start.4) | collective-permute-done | bytes 307232 | tf_op jit(solution)/shard_map/ppermute | solution.py:21
  58.1 4.4 %collective-permute-done.5 = f32[5,24,5,128]{3,1,2,0:T(8,128)S(1)} collective-permute-done((f32[5,24,5,128]{3,1,2,0:T(8,128)S(1)}, f32[5,24,5,128]{3,1,2,0:T(8,128)S(1)}, u32[]{:S(2)}, u32[]{:S(2)}) %collective-permute-start.5) | collective-permute-done | bytes 307232 | tf_op jit(solution)/shard_map/ppermute | solution.py:22
  62.6 0.2 fusion.63
  62.9 0.1 fusion.154
  63.0 0.3 fusion.71
  63.4 0.3 fusion.82
  63.8 0.2 multiply_reduce_fusion.2
  64.1 0.2 fusion.118
  64.3 0.2 fusion.116
  64.6 0.2 fusion.107
  64.8 0.2 fusion.122
  65.0 0.2 fusion.120
  65.2 0.3 fusion.60
  65.6 0.2 fusion.163
  65.8 1.3 %collective-permute-start.7 = (f32[2,20,256]{2,1,0:T(8,128)S(1)}, f32[2,20,256]{2,1,0:T(8,128)S(1)}, u32[]{:S(2)}, u32[]{:S(2)}) collective-permute-start(f32[2,20,256]{2,1,0:T(8,128)S(1)} %get-tuple-element.42), channel_id=1, source_target_pairs={{4,0},{8,4},{12,8},{5,1},{9,5},{13,9},{6,2},{10,6},{14,10},{7,3},{... | collective-permute-start | bytes 122888 | tf_op jit(solution)/shard_map/ppermute | solution.py:30
  67.1 0.1 fusion.164
  67.3 4.0 %collective-permute-start.6 = (f32[3,20,256]{2,1,0:T(8,128)S(1)}, f32[3,20,256]{2,1,0:T(8,128)S(1)}, u32[]{:S(2)}, u32[]{:S(2)}) collective-permute-start(f32[3,20,256]{2,1,0:T(8,128)S(1)} %pad_maximum_fusion.11), channel_id=1, source_target_pairs={{0,4},{4,8},{8,12},{1,5},{5,9},{9,13},{2,6},{6,10},{10,14},{3,7},{... | collective-permute-start | bytes 184328 | tf_op jit(solution)/shard_map/ppermute | solution.py:30
  71.4 1.3 %collective-permute-done.6 = f32[3,20,256]{2,1,0:T(8,128)S(1)} collective-permute-done((f32[3,20,256]{2,1,0:T(8,128)S(1)}, f32[3,20,256]{2,1,0:T(8,128)S(1)}, u32[]{:S(2)}, u32[]{:S(2)}) %collective-permute-start.6) | collective-permute-done | bytes 61472 | tf_op jit(solution)/shard_map/ppermute | solution.py:30
  72.9 0.2 fusion.149
  73.1 0.9 %fusion.37 = f32[18,18,256]{2,1,0:T(8,128)S(1)} fusion(f32[20,20,256]{2,1,0:T(8,128)S(1)} %pad_maximum_fusion.3, f32[24,23,256]{2,1,0:T(8,128)S(1)} %divide_select_fusion, f32[2,20,256]{2,1,0:T(8,128)S(1)} %multiply_add_fusion.3, f32[16,20,256]{2,1,0:T(8,128)S(1)} %multiply_add_fusion.1, f32[23,24,256]{2,1,0:T(8,128)S(1)} %divide_select_fusion.1, ...), kind=kLoop, calls=%fused_computation.65 | loop fusion | flops 1575936 | bytes 4882000 | tf_op jit(solution)/shard_map/add | solution.py:106
  73.9 0.1 fusion.152
  74.1 1.2 %fusion.50 = f32[16,16,256]{2,1,0:T(8,128)} fusion(f32[18,18,256]{2,1,0:T(8,128)S(1)} %fusion.37, f32[24,24,256]{2,1,0:T(8,128)S(1)} %get-tuple-element.17, f32[16,16,255]{2,1,0:T(8,128)S(1)} %get-tuple-element.40, f32[16,16,255]{2,1,0:T(8,128)S(1)} %get-tuple-element.39, f32[24,23,256]{2,1,0:T(8,128)S(1)} %divide_select_fusion, ...), kind=kLoop, calls=%fused_computation.91 | loop fusion | flops 1114112 | bytes 4161648 | tf_op jit(solution)/shard_map/add | solution.py:106
  (96 shorter events, 2.6 us)
Async XLA Ops:
  0.0 12.5 %copy-start.6 = (f32[16,16,256]{2,1,0:T(8,128)S(1)}, f32[16,16,256]{2,1,0:T(8,128)}, u32[]{:S(2)}) copy-start(f32[16,16,256]{2,1,0:T(8,128)} %param.11) | copy-start | bytes 786436
  0.0 12.5 %copy-start.1 = (f32[16,16,256]{2,1,0:T(8,128)S(1)}, f32[16,16,256]{2,1,0:T(8,128)}, u32[]{:S(2)}) copy-start(f32[16,16,256]{2,1,0:T(8,128)} %param.12) | copy-start | bytes 786436
  0.0 12.5 %copy-start.5 = (f32[16,16,256]{2,1,0:T(8,128)S(1)}, f32[16,16,256]{2,1,0:T(8,128)}, u32[]{:S(2)}) copy-start(f32[16,16,256]{2,1,0:T(8,128)} %param.13) | copy-start | bytes 786436
  1.1 7.6 %collective-permute-start = (f32[3,4,16,256]{3,2,1,0:T(8,128)S(1)}, f32[3,4,16,256]{3,2,1,0:T(8,128)S(1)}, u32[]{:S(2)}, u32[]{:S(2)}) collective-permute-start(f32[3,4,16,256]{3,2,1,0:T(8,128)S(1)} %get-tuple-element.21), channel_id=1, source_target_pairs={{0,4},{4,8},{8,12},{1,5},{5,9},{9,13},{2,6},{6,10},{10,14},{3,7},{... | collective-permute-start | bytes 589832 | tf_op jit(solution)/shard_map/ppermute | solution.py:21
  5.2 7.3 %collective-permute-start.1 = (f32[3,4,16,256]{3,2,1,0:T(8,128)S(1)}, f32[3,4,16,256]{3,2,1,0:T(8,128)S(1)}, u32[]{:S(2)}, u32[]{:S(2)}) collective-permute-start(f32[3,4,16,256]{3,2,1,0:T(8,128)S(1)} %get-tuple-element.22), channel_id=1, source_target_pairs={{4,0},{8,4},{12,8},{5,1},{9,5},{13,9},{6,2},{10,6},{14,10},{7,3},{... | collective-permute-start | bytes 589832 | tf_op jit(solution)/shard_map/ppermute | solution.py:22
  12.6 6.9 %copy-start.12 = (s32[64]{0:T(128)S(1)}, s32[64]{0:T(128)}, u32[]{:S(2)}) copy-start(s32[64]{0:T(128)} %param.14) | copy-start | bytes 772
  12.7 10.5 %collective-permute-start.2 = (f32[3,24,4,256]{3,2,1,0:T(4,128)S(1)}, f32[3,24,4,256]{3,2,1,0:T(4,128)S(1)}, u32[]{:S(2)}, u32[]{:S(2)}) collective-permute-start(f32[3,24,4,256]{3,2,1,0:T(4,128)S(1)} %get-tuple-element.19), channel_id=1, source_target_pairs={{0,1},{1,2},{2,3},{4,5},{5,6},{6,7},{8,9},{9,10},{10,11},{12,13},{... | collective-permute-start | bytes 884744 | tf_op jit(solution)/shard_map/ppermute | solution.py:21
  17.6 8.0 %collective-permute-start.3 = (f32[3,24,4,256]{3,2,1,0:T(4,128)S(1)}, f32[3,24,4,256]{3,2,1,0:T(4,128)S(1)}, u32[]{:S(2)}, u32[]{:S(2)}) collective-permute-start(f32[3,24,4,256]{3,2,1,0:T(4,128)S(1)} %get-tuple-element.20), channel_id=1, source_target_pairs={{1,0},{2,1},{3,2},{5,4},{6,5},{7,6},{9,8},{10,9},{11,10},{13,12},{... | collective-permute-start | bytes 884744 | tf_op jit(solution)/shard_map/ppermute | solution.py:22
  29.3 1.0 %copy-start.2 = (f32[16,16,256]{2,1,0:T(8,128)S(1)}, f32[16,16,256]{2,1,0:T(8,128)}, u32[]{:S(2)}) copy-start(f32[16,16,256]{2,1,0:T(8,128)} %param.12) | copy-start | bytes 786436
  30.2 0.9 %copy-start = (f32[256,128]{1,0:T(8,128)S(1)}, f32[256,128]{1,0:T(8,128)}, u32[]{:S(2)}) copy-start(f32[256,128]{1,0:T(8,128)} %constant.47.clone) | copy-start | bytes 393220
  31.4 1.0 %copy-start.7 = (f32[256,128]{1,0:T(8,128)S(1)}, f32[256,128]{1,0:T(8,128)}, u32[]{:S(2)}) copy-start(f32[256,128]{1,0:T(8,128)} %constant.48.clone) | copy-start | bytes 393220
  31.8 1.0 %copy-start.11 = (f32[136]{0:T(256)S(1)}, f32[136]{0:T(256)}, u32[]{:S(2)}) copy-start(f32[136]{0:T(256)} %constant.49.clone) | copy-start | bytes 1636
  31.8 1.0 %copy-start.13 = (pred[136,256]{1,0:T(8,128)(4,1)S(1)}, pred[136,256]{1,0:T(8,128)(4,1)}, u32[]{:S(2)}) copy-start(pred[136,256]{1,0:T(8,128)(4,1)} %constant.51.clone) | copy-start | bytes 104452
  32.4 0.8 %copy-start.9 = (pred[136,256]{1,0:T(8,128)(4,1)S(1)}, pred[136,256]{1,0:T(8,128)(4,1)}, u32[]{:S(2)}) copy-start(pred[136,256]{1,0:T(8,128)(4,1)} %constant.52.clone) | copy-start | bytes 104452
  33.5 0.8 %copy-start.3 = (f32[5,17,8,128]{3,1,2,0:T(8,128)}, f32[5,17,8,128]{3,1,2,0:T(8,128)S(1)}, u32[]{:S(2)}) copy-start(f32[5,17,8,128]{3,1,2,0:T(8,128)S(1)} %copy_dynamic-update-slice_fusion) | copy-start | bytes 1044484
  35.6 12.4 %all-to-all-start = ((f32[4,5,5,8,128]{4,3,2,1,0:T(8,128)}), f32[4,5,5,8,128]{4,3,2,1,0:T(8,128)}, u32[]{:S(2)}, u32[]{:S(2)}) async-start(f32[4,5,5,8,128]{4,3,2,1,0:T(8,128)} %multiply_add_fusion), calls=%async_computation | async-start | bytes 819200 | tf_op jit(solution)/shard_map/all_to_all | solution.py:210
  47.9 1.2 %copy-start.4 = (f32[5,17,8,128]{3,1,2,0:T(8,128)S(1)}, f32[5,17,8,128]{3,1,2,0:T(8,128)}, u32[]{:S(2)}) copy-start(f32[5,17,8,128]{3,1,2,0:T(8,128)} %copy-done.3) | copy-start | bytes 1044484
  50.0 8.1 %collective-permute-start.4 = (f32[5,24,5,128]{3,1,2,0:T(8,128)S(1)}, f32[5,24,5,128]{3,1,2,0:T(8,128)S(1)}, u32[]{:S(2)}, u32[]{:S(2)}) collective-permute-start(f32[5,24,5,128]{3,1,2,0:T(8,128)S(1)} %get-tuple-element.35), channel_id=1, source_target_pairs={{0,1},{1,2},{2,3},{4,5},{5,6},{6,7},{8,9},{9,10},{10,11},{12,13},{... | collective-permute-start | bytes 921608 | tf_op jit(solution)/shard_map/ppermute | solution.py:21
  54.3 8.2 %collective-permute-start.5 = (f32[5,24,5,128]{3,1,2,0:T(8,128)S(1)}, f32[5,24,5,128]{3,1,2,0:T(8,128)S(1)}, u32[]{:S(2)}, u32[]{:S(2)}) collective-permute-start(f32[5,24,5,128]{3,1,2,0:T(8,128)S(1)} %get-tuple-element.36), channel_id=1, source_target_pairs={{1,0},{2,1},{3,2},{5,4},{6,5},{7,6},{9,8},{10,9},{11,10},{13,12},{... | collective-permute-start | bytes 921608 | tf_op jit(solution)/shard_map/ppermute | solution.py:22
  63.8 1.4 %copy-start.8 = (pred[256,136]{1,0:T(32,128)(4,1)S(1)}, pred[256,136]{1,0:T(32,128)(4,1)}, u32[]{:S(2)}) copy-start(pred[256,136]{1,0:T(32,128)(4,1)} %constant.50.clone) | copy-start | bytes 104452
  64.5 2.6 %copy-start.10 = (f32[20,10]{1,0:T(8,128)S(1)}, f32[20,10]{1,0:T(8,128)}, u32[]{:S(2)}) copy-start(f32[20,10]{1,0:T(8,128)} %constant.53.clone) | copy-start | bytes 2404
  65.8 5.5 %collective-permute-start.7 = (f32[2,20,256]{2,1,0:T(8,128)S(1)}, f32[2,20,256]{2,1,0:T(8,128)S(1)}, u32[]{:S(2)}, u32[]{:S(2)}) collective-permute-start(f32[2,20,256]{2,1,0:T(8,128)S(1)} %get-tuple-element.42), channel_id=1, source_target_pairs={{4,0},{8,4},{12,8},{5,1},{9,5},{13,9},{6,2},{10,6},{14,10},{7,3},{... | collective-permute-start | bytes 122888 | tf_op jit(solution)/shard_map/ppermute | solution.py:30
  67.3 5.4 %collective-permute-start.6 = (f32[3,20,256]{2,1,0:T(8,128)S(1)}, f32[3,20,256]{2,1,0:T(8,128)S(1)}, u32[]{:S(2)}, u32[]{:S(2)}) collective-permute-start(f32[3,20,256]{2,1,0:T(8,128)S(1)} %pad_maximum_fusion.11), channel_id=1, source_target_pairs={{0,4},{4,8},{8,12},{1,5},{5,9},{9,13},{2,6},{6,10},{10,14},{3,7},{... | collective-permute-start | bytes 184328 | tf_op jit(solution)/shard_map/ppermute | solution.py:30

commit v19 on v16

--- a/solution.py
+++ b/solution.py
@@ -275,16 +275,16 @@
     owner_rows = (slot_ids[:, None] + 1 == jnp.arange(width_x + 1)[None, :]).astype(jnp.float32)
 
     def rim_rows(coarse_row):
-        row_z = jnp.dot(corr_wide[:, coarse_row], pair_z.T, precision=lax.Precision.HIGHEST)
-        row_fine = jnp.dot(owner_rows, row_z, precision=lax.Precision.HIGHEST)
+        row_z = jnp.dot(corr_wide[:, coarse_row], pair_z.T, precision=lax.Precision.HIGH)
+        row_fine = jnp.dot(owner_rows, row_z, precision=lax.Precision.HIGH)
         return jnp.broadcast_to(row_fine[:, None], (width_x, NU, depth_cells))
 
     correction = jnp.concatenate([rim_rows(0), correction, rim_rows(half_y + 1)], axis=1)
     base = smooth_rows + correction
-    last_z = jnp.dot(last_corr, pair_z.T, precision=lax.Precision.HIGHEST)
+    last_z = jnp.dot(last_corr, pair_z.T, precision=lax.Precision.HIGH)
     fine_y = np.arange(width_y + 2 * NU) - NU
     rows_ext = jnp.asarray((fine_y[:, None] // 2 + 1 == np.arange(half_y + 2)[None, :]).astype(np.float32))
-    last_fine = jnp.dot(rows_ext, last_z, precision=lax.Precision.HIGHEST)
+    last_fine = jnp.dot(rows_ext, last_z, precision=lax.Precision.HIGH)
     up_block = jnp.concatenate([base[width_x - NU :], last_fine[None]], axis=0)
     below_prev = passed_along(up_block, "slab", 1)
     above_next = passed_along(base[:NU], "slab", -1)

time: 67.6 us -> 67.4 us (level)
  no operation moved by 1% of the time
where the time goes in v19:
time: 67.4 us; the launch traced here: 66.9 us
  starting transfers between devices  27 us (40%)
  waiting for transfers between devices  19 us (28%)
  other arithmetic  9.81 us (15%)
  matrix products  4.27 us (6%)
  local copies, waits for them, and re-layouts  3.64 us (5%)
  between operations  3.21 us (5%)
    ppermute x3, starting transfers between devices, padded(): before = lax.ppermute(last, axis, up)  12.1 us
    ppermute x3, waiting for transfers between devices, padded(): after = lax.ppermute(leading, axis, down)  10.6 us
    ppermute x4, starting transfers between devices, passed_along(): return lax.ppermute(array, axis, pairs)  9.82 us
    ppermute x4, waiting for transfers between devices, passed_along(): return lax.ppermute(array, axis, pairs)  5.98 us
    ppermute x3, starting transfers between devices, padded(): after = lax.ppermute(leading, axis, down)  5.13 us
    add x4, other arithmetic, sweeps(): field_ext = center + OMEGA * (source_now - product) / faces_now[7]  3.86 us
    ppermute x3, waiting for transfers between devices, padded(): before = lax.ppermute(last, axis, up)  2.35 us
    dot_general x5, matrix products, z_sum(): return jnp.dot(flat, pick_z, precision=lax.Precision.HIGH)  1.48 us
  transfers between devices with their start and end apart: 10, of which 8 were waited for; matrix products, arithmetic and copies ran while one was open for 5% of the time, Pallas kernels for 0%

profile of v19, /device:TPU:1, one launch (start us, length us, event | category | flops | bytes accessed | tf_op | source)
XLA Modules:
  0.0 66.9 jit_solution(12933485091453209358)
XLA Ops:
  0.0 1.1 %pad_maximum_fusion.8 = (f32[3,4,16,256]{3,2,1,0:T(8,128)S(1)}, f32[3,4,16,256]{3,2,1,0:T(8,128)S(1)}) fusion(f32[1,16,16,256]{3,2,1,0:T(8,128)} %bitcast.231, f32[1,16,16,256]{3,2,1,0:T(8,128)} %bitcast.224, f32[1,16,16,256]{3,2,1,0:T(8,128)} %bitcast.233), kind=kLoop, calls=%fused_computation.123 | loop fusion | flops 196608 | bytes 1179648 | tf_op jit(solution)/shard_map/slice | solution.py:19
  1.1 4.0 %collective-permute-start = (f32[3,4,16,256]{3,2,1,0:T(8,128)S(1)}, f32[3,4,16,256]{3,2,1,0:T(8,128)S(1)}, u32[]{:S(2)}, u32[]{:S(2)}) collective-permute-start(f32[3,4,16,256]{3,2,1,0:T(8,128)S(1)} %get-tuple-element.23), channel_id=1, source_target_pairs={{0,4},{4,8},{8,12},{1,5},{5,9},{9,13},{2,6},{6,10},{10,14},{3,7},{... | collective-permute-start | bytes 589832 | tf_op jit(solution)/shard_map/ppermute | solution.py:21
  5.2 1.3 %collective-permute-start.1 = (f32[3,4,16,256]{3,2,1,0:T(8,128)S(1)}, f32[3,4,16,256]{3,2,1,0:T(8,128)S(1)}, u32[]{:S(2)}, u32[]{:S(2)}) collective-permute-start(f32[3,4,16,256]{3,2,1,0:T(8,128)S(1)} %get-tuple-element.24), channel_id=1, source_target_pairs={{4,0},{8,4},{12,8},{5,1},{9,5},{13,9},{6,2},{10,6},{14,10},{7,3},{... | collective-permute-start | bytes 589832 | tf_op jit(solution)/shard_map/ppermute | solution.py:22
  7.4 1.3 %collective-permute-done = f32[3,4,16,256]{3,2,1,0:T(8,128)S(1)} collective-permute-done((f32[3,4,16,256]{3,2,1,0:T(8,128)S(1)}, f32[3,4,16,256]{3,2,1,0:T(8,128)S(1)}, u32[]{:S(2)}, u32[]{:S(2)}) %collective-permute-start) | collective-permute-done | bytes 196640 | tf_op jit(solution)/shard_map/ppermute | solution.py:21
  8.7 3.8 %collective-permute-done.1 = f32[3,4,16,256]{3,2,1,0:T(8,128)S(1)} collective-permute-done((f32[3,4,16,256]{3,2,1,0:T(8,128)S(1)}, f32[3,4,16,256]{3,2,1,0:T(8,128)S(1)}, u32[]{:S(2)}, u32[]{:S(2)}) %collective-permute-start.1) | collective-permute-done | bytes 196640 | tf_op jit(solution)/shard_map/ppermute | solution.py:22
  12.6 0.1 fusion.145
  12.7 4.9 %collective-permute-start.2 = (f32[3,24,4,256]{3,2,1,0:T(4,128)S(1)}, f32[3,24,4,256]{3,2,1,0:T(4,128)S(1)}, u32[]{:S(2)}, u32[]{:S(2)}) collective-permute-start(f32[3,24,4,256]{3,2,1,0:T(4,128)S(1)} %get-tuple-element.21), channel_id=1, source_target_pairs={{0,1},{1,2},{2,3},{4,5},{5,6},{6,7},{8,9},{9,10},{10,11},{12,13},{... | collective-permute-start | bytes 884744 | tf_op jit(solution)/shard_map/ppermute | solution.py:21
  17.6 1.9 %collective-permute-start.3 = (f32[3,24,4,256]{3,2,1,0:T(4,128)S(1)}, f32[3,24,4,256]{3,2,1,0:T(4,128)S(1)}, u32[]{:S(2)}, u32[]{:S(2)}) collective-permute-start(f32[3,24,4,256]{3,2,1,0:T(4,128)S(1)} %get-tuple-element.22), channel_id=1, source_target_pairs={{1,0},{2,1},{3,2},{5,4},{6,5},{7,6},{9,8},{10,9},{11,10},{13,12},{... | collective-permute-start | bytes 884744 | tf_op jit(solution)/shard_map/ppermute | solution.py:22
  19.6 0.2 select_reduce_fusion
  19.7 0.7 fusion.158
  23.2 2.4 %collective-permute-done.3 = f32[3,24,4,256]{3,2,1,0:T(4,128)S(1)} collective-permute-done((f32[3,24,4,256]{3,2,1,0:T(4,128)S(1)}, f32[3,24,4,256]{3,2,1,0:T(4,128)S(1)}, u32[]{:S(2)}, u32[]{:S(2)}) %collective-permute-start.3) | collective-permute-done | bytes 294944 | tf_op jit(solution)/shard_map/ppermute | solution.py:22
  25.7 0.3 pad_maximum_fusion
  25.9 0.1 slice_bitcast_fusion
  26.1 0.2 fusion.147
  26.3 0.2 divide_select_fusion
  26.5 0.2 divide_select_fusion.1
  26.7 0.2 fusion.148
  26.9 0.2 divide_select_fusion.2
  27.2 1.1 %fusion.7 = (f32[22,22,256]{2,1,0:T(8,128)S(1)}, f32[22,22,256]{2,1,0:T(8,128)S(1)}, f32[22,22,256]{2,1,0:T(8,128)S(1)}) fusion(f32[24,24,256]{2,1,0:T(8,128)S(1)} %get-tuple-element.20, f32[24,24,256]{2,1,0:T(8,128)S(1)} %get-tuple-element.19, f32[22,22,255]{2,1,0:T(8,128)S(1)} %get-tuple-element.30, f32[22,22,255]{2,1,0:T(8,128)S(1)} %get-tuple-element.29, ...), kind=kLoop, calls=%fused_computation.22 | loop fusion | flops 3345408 | bytes 8423108 | tf_op jit(solution)/shard_map/add | solution.py:106
  28.3 0.2 fusion.149
  28.5 0.8 %fusion.26 = f32[20,20,256]{2,1,0:T(8,128)S(1)} fusion(f32[22,22,256]{2,1,0:T(8,128)S(1)} %get-tuple-element.15, f32[24,23,256]{2,1,0:T(8,128)S(1)} %divide_select_fusion, f32[23,24,256]{2,1,0:T(8,128)S(1)} %divide_select_fusion.1, f32[24,24,256]{2,1,0:T(8,128)S(1)} %get-tuple-element.19, f32[20,20,255]{2,1,0:T(8,128)S(1)} %get-tuple-element.34, ...), kind=kLoop, calls=%fused_computation.49 | loop fusion | flops 1740800 | bytes 6224880 | tf_op jit(solution)/shard_map/add | solution.py:106
  29.3 0.1 fusion.152
  29.4 0.5 fusion.146
  29.9 0.4 copy-done
  30.3 0.3 fusion.163
  30.6 0.3 fusion.159
  31.0 0.3 fusion.160
  31.3 0.3 fusion.162
  31.7 0.3 fusion.161
  32.0 0.3 fusion.11
  32.4 0.2 convolution_bitcast_fusion.2
  32.8 0.3 convolution_bitcast_fusion.1
  33.1 3.2 %collective-permute-start.4 = (f32[5,4,8,128]{3,1,2,0:T(4,128)S(1)}, f32[5,4,8,128]{3,1,2,0:T(4,128)S(1)}, u32[]{:S(2)}, u32[]{:S(2)}) collective-permute-start(f32[5,4,8,128]{3,1,2,0:T(4,128)S(1)} %convolution_bitcast_fusion.1), channel_id=1, source_target_pairs={{0,4},{4,8},{8,12},{1,5},{5,9},{9,13},{2,6},{6,10},{10,14},{3,7},{... | collective-permute-start | bytes 245768 | tf_op jit(solution)/shard_map/ppermute | solution.py:30
  36.3 1.3 %collective-permute-start.5 = (f32[5,5,8,128]{3,1,2,0:T(8,128)S(1)}, f32[5,5,8,128]{3,1,2,0:T(8,128)S(1)}, u32[]{:S(2)}, u32[]{:S(2)}) collective-permute-start(f32[5,5,8,128]{3,1,2,0:T(8,128)S(1)} %pad_maximum_fusion.9), channel_id=1, source_target_pairs={{4,0},{8,4},{12,8},{5,1},{9,5},{13,9},{6,2},{10,6},{14,10},{7,3},{... | collective-permute-start | bytes 307208 | tf_op jit(solution)/shard_map/ppermute | solution.py:30
  37.6 0.1 collective-permute-done.4
  37.9 4.5 %collective-permute-done.5 = f32[5,5,8,128]{3,1,2,0:T(8,128)S(1)} collective-permute-done((f32[5,5,8,128]{3,1,2,0:T(8,128)S(1)}, f32[5,5,8,128]{3,1,2,0:T(8,128)S(1)}, u32[]{:S(2)}, u32[]{:S(2)}) %collective-permute-start.5) | collective-permute-done | bytes 102432 | tf_op jit(solution)/shard_map/ppermute | solution.py:30
  42.4 0.1 multiply_add_fusion.1
  42.5 0.5 maximum_add_fusion
  43.1 3.2 %collective-permute-start.6 = (f32[5,24,5,128]{3,1,2,0:T(8,128)S(1)}, f32[5,24,5,128]{3,1,2,0:T(8,128)S(1)}, u32[]{:S(2)}, u32[]{:S(2)}) collective-permute-start(f32[5,24,5,128]{3,1,2,0:T(8,128)S(1)} %get-tuple-element.37), channel_id=1, source_target_pairs={{0,1},{1,2},{2,3},{4,5},{5,6},{6,7},{8,9},{9,10},{10,11},{12,13},{... | collective-permute-start | bytes 921608 | tf_op jit(solution)/shard_map/ppermute | solution.py:21
  46.3 1.9 %collective-permute-start.7 = (f32[5,24,5,128]{3,1,2,0:T(8,128)S(1)}, f32[5,24,5,128]{3,1,2,0:T(8,128)S(1)}, u32[]{:S(2)}, u32[]{:S(2)}) collective-permute-start(f32[5,24,5,128]{3,1,2,0:T(8,128)S(1)} %get-tuple-element.38), channel_id=1, source_target_pairs={{1,0},{2,1},{3,2},{5,4},{6,5},{7,6},{9,8},{10,9},{11,10},{13,12},{... | collective-permute-start | bytes 921608 | tf_op jit(solution)/shard_map/ppermute | solution.py:22
  48.2 0.8 %and_convert_fusion = f32[2]{0:T(128)S(1)} fusion(s32[19]{0:T(128)S(1)} %iota_add_fusion, f32[19]{0:T(128)S(1)} %select_reduce_fusion, f32[]{:T(128)} %bitcast.21), kind=kLoop, calls=%fused_computation.247 | loop fusion | flops 8 | bytes 28 | tf_op jit(solution)/shard_map/convert_element_type | solution.py:295
  49.0 1.1 %collective-permute-done.6 = f32[5,24,5,128]{3,1,2,0:T(8,128)S(1)} collective-permute-done((f32[5,24,5,128]{3,1,2,0:T(8,128)S(1)}, f32[5,24,5,128]{3,1,2,0:T(8,128)S(1)}, u32[]{:S(2)}, u32[]{:S(2)}) %collective-permute-start.6) | collective-permute-done | bytes 307232 | tf_op jit(solution)/shard_map/ppermute | solution.py:21
  50.0 4.4 %collective-permute-done.7 = f32[5,24,5,128]{3,1,2,0:T(8,128)S(1)} collective-permute-done((f32[5,24,5,128]{3,1,2,0:T(8,128)S(1)}, f32[5,24,5,128]{3,1,2,0:T(8,128)S(1)}, u32[]{:S(2)}, u32[]{:S(2)}) %collective-permute-start.7) | collective-permute-done | bytes 307232 | tf_op jit(solution)/shard_map/ppermute | solution.py:22
  54.6 0.2 fusion.62
  54.8 0.1 fusion.155
  55.0 0.3 fusion.70
  55.3 0.1 fusion.156
  55.4 0.3 fusion.81
  55.8 0.2 multiply_reduce_fusion
  56.0 0.2 fusion.119
  56.2 0.2 fusion.117
  56.4 0.2 fusion.108
  56.7 0.2 fusion.123
  56.8 0.2 fusion.121
  57.0 0.3 fusion.59
  57.5 0.1 fusion.164
  57.6 1.3 %collective-permute-start.9 = (f32[2,20,256]{2,1,0:T(8,128)S(1)}, f32[2,20,256]{2,1,0:T(8,128)S(1)}, u32[]{:S(2)}, u32[]{:S(2)}) collective-permute-start(f32[2,20,256]{2,1,0:T(8,128)S(1)} %get-tuple-element.44), channel_id=1, source_target_pairs={{4,0},{8,4},{12,8},{5,1},{9,5},{13,9},{6,2},{10,6},{14,10},{7,3},{... | collective-permute-start | bytes 122888 | tf_op jit(solution)/shard_map/ppermute | solution.py:30
  58.9 0.1 fusion.165
  59.1 4.0 %collective-permute-start.8 = (f32[3,20,256]{2,1,0:T(8,128)S(1)}, f32[3,20,256]{2,1,0:T(8,128)S(1)}, u32[]{:S(2)}, u32[]{:S(2)}) collective-permute-start(f32[3,20,256]{2,1,0:T(8,128)S(1)} %pad_maximum_fusion.11), channel_id=1, source_target_pairs={{0,4},{4,8},{8,12},{1,5},{5,9},{9,13},{2,6},{6,10},{10,14},{3,7},{... | collective-permute-start | bytes 184328 | tf_op jit(solution)/shard_map/ppermute | solution.py:30
  63.2 1.3 %collective-permute-done.8 = f32[3,20,256]{2,1,0:T(8,128)S(1)} collective-permute-done((f32[3,20,256]{2,1,0:T(8,128)S(1)}, f32[3,20,256]{2,1,0:T(8,128)S(1)}, u32[]{:S(2)}, u32[]{:S(2)}) %collective-permute-start.8) | collective-permute-done | bytes 61472 | tf_op jit(solution)/shard_map/ppermute | solution.py:30
  64.6 0.2 fusion.150
  64.8 0.8 %fusion.36 = f32[18,18,256]{2,1,0:T(8,128)S(1)} fusion(f32[20,20,256]{2,1,0:T(8,128)S(1)} %pad_maximum_fusion.3, f32[24,23,256]{2,1,0:T(8,128)S(1)} %divide_select_fusion, f32[2,20,256]{2,1,0:T(8,128)S(1)} %multiply_add_fusion.3, f32[16,20,256]{2,1,0:T(8,128)S(1)} %multiply_add_fusion, f32[23,24,256]{2,1,0:T(8,128)S(1)} %divide_select_fusion.1, ...), kind=kLoop, calls=%fused_computation.65 | loop fusion | flops 1575936 | bytes 4882000 | tf_op jit(solution)/shard_map/add | solution.py:106
  65.7 0.1 fusion.153
  65.8 1.1 %fusion.49 = f32[16,16,256]{2,1,0:T(8,128)} fusion(f32[18,18,256]{2,1,0:T(8,128)S(1)} %fusion.36, f32[24,24,256]{2,1,0:T(8,128)S(1)} %get-tuple-element.19, f32[16,16,255]{2,1,0:T(8,128)S(1)} %get-tuple-element.42, f32[16,16,255]{2,1,0:T(8,128)S(1)} %get-tuple-element.41, f32[24,23,256]{2,1,0:T(8,128)S(1)} %divide_select_fusion, ...), kind=kLoop, calls=%fused_computation.88 | loop fusion | flops 1114112 | bytes 4161648 | tf_op jit(solution)/shard_map/add | solution.py:106
  (84 shorter events, 2.4 us)
Async XLA Ops:
  0.0 12.5 %copy-start.3 = (f32[16,16,256]{2,1,0:T(8,128)S(1)}, f32[16,16,256]{2,1,0:T(8,128)}, u32[]{:S(2)}) copy-start(f32[16,16,256]{2,1,0:T(8,128)} %param.11) | copy-start | bytes 786436
  0.0 12.5 %copy-start.1 = (f32[16,16,256]{2,1,0:T(8,128)S(1)}, f32[16,16,256]{2,1,0:T(8,128)}, u32[]{:S(2)}) copy-start(f32[16,16,256]{2,1,0:T(8,128)} %param.12) | copy-start | bytes 786436
  0.0 12.5 %copy-start.2 = (f32[16,16,256]{2,1,0:T(8,128)S(1)}, f32[16,16,256]{2,1,0:T(8,128)}, u32[]{:S(2)}) copy-start(f32[16,16,256]{2,1,0:T(8,128)} %param.13) | copy-start | bytes 786436
  1.1 7.6 %collective-permute-start = (f32[3,4,16,256]{3,2,1,0:T(8,128)S(1)}, f32[3,4,16,256]{3,2,1,0:T(8,128)S(1)}, u32[]{:S(2)}, u32[]{:S(2)}) collective-permute-start(f32[3,4,16,256]{3,2,1,0:T(8,128)S(1)} %get-tuple-element.23), channel_id=1, source_target_pairs={{0,4},{4,8},{8,12},{1,5},{5,9},{9,13},{2,6},{6,10},{10,14},{3,7},{... | collective-permute-start | bytes 589832 | tf_op jit(solution)/shard_map/ppermute | solution.py:21
  5.2 7.3 %collective-permute-start.1 = (f32[3,4,16,256]{3,2,1,0:T(8,128)S(1)}, f32[3,4,16,256]{3,2,1,0:T(8,128)S(1)}, u32[]{:S(2)}, u32[]{:S(2)}) collective-permute-start(f32[3,4,16,256]{3,2,1,0:T(8,128)S(1)} %get-tuple-element.24), channel_id=1, source_target_pairs={{4,0},{8,4},{12,8},{5,1},{9,5},{13,9},{6,2},{10,6},{14,10},{7,3},{... | collective-permute-start | bytes 589832 | tf_op jit(solution)/shard_map/ppermute | solution.py:22
  12.6 6.9 %copy-start.9 = (s32[64]{0:T(128)S(1)}, s32[64]{0:T(128)}, u32[]{:S(2)}) copy-start(s32[64]{0:T(128)} %param.14) | copy-start | bytes 772
  12.7 10.5 %collective-permute-start.2 = (f32[3,24,4,256]{3,2,1,0:T(4,128)S(1)}, f32[3,24,4,256]{3,2,1,0:T(4,128)S(1)}, u32[]{:S(2)}, u32[]{:S(2)}) collective-permute-start(f32[3,24,4,256]{3,2,1,0:T(4,128)S(1)} %get-tuple-element.21), channel_id=1, source_target_pairs={{0,1},{1,2},{2,3},{4,5},{5,6},{6,7},{8,9},{9,10},{10,11},{12,13},{... | collective-permute-start | bytes 884744 | tf_op jit(solution)/shard_map/ppermute | solution.py:21
  17.6 8.0 %collective-permute-start.3 = (f32[3,24,4,256]{3,2,1,0:T(4,128)S(1)}, f32[3,24,4,256]{3,2,1,0:T(4,128)S(1)}, u32[]{:S(2)}, u32[]{:S(2)}) collective-permute-start(f32[3,24,4,256]{3,2,1,0:T(4,128)S(1)} %get-tuple-element.22), channel_id=1, source_target_pairs={{1,0},{2,1},{3,2},{5,4},{6,5},{7,6},{9,8},{10,9},{11,10},{13,12},{... | collective-permute-start | bytes 884744 | tf_op jit(solution)/shard_map/ppermute | solution.py:22
  29.4 0.9 %copy-start = (f32[256,128]{1,0:T(8,128)S(1)}, f32[256,128]{1,0:T(8,128)}, u32[]{:S(2)}) copy-start(f32[256,128]{1,0:T(8,128)} %constant.45.clone) | copy-start | bytes 393220
  30.6 1.0 %copy-start.4 = (f32[256,128]{1,0:T(8,128)S(1)}, f32[256,128]{1,0:T(8,128)}, u32[]{:S(2)}) copy-start(f32[256,128]{1,0:T(8,128)} %constant.46.clone) | copy-start | bytes 393220
  31.0 1.0 %copy-start.8 = (f32[136]{0:T(256)S(1)}, f32[136]{0:T(256)}, u32[]{:S(2)}) copy-start(f32[136]{0:T(256)} %constant.47.clone) | copy-start | bytes 1636
  31.0 1.0 %copy-start.10 = (pred[136,256]{1,0:T(8,128)(4,1)S(1)}, pred[136,256]{1,0:T(8,128)(4,1)}, u32[]{:S(2)}) copy-start(pred[136,256]{1,0:T(8,128)(4,1)} %constant.49.clone) | copy-start | bytes 104452
  31.6 0.8 %copy-start.6 = (pred[136,256]{1,0:T(8,128)(4,1)S(1)}, pred[136,256]{1,0:T(8,128)(4,1)}, u32[]{:S(2)}) copy-start(pred[136,256]{1,0:T(8,128)(4,1)} %constant.50.clone) | copy-start | bytes 104452
  33.1 4.7 %collective-permute-start.4 = (f32[5,4,8,128]{3,1,2,0:T(4,128)S(1)}, f32[5,4,8,128]{3,1,2,0:T(4,128)S(1)}, u32[]{:S(2)}, u32[]{:S(2)}) collective-permute-start(f32[5,4,8,128]{3,1,2,0:T(4,128)S(1)} %convolution_bitcast_fusion.1), channel_id=1, source_target_pairs={{0,4},{4,8},{8,12},{1,5},{5,9},{9,13},{2,6},{6,10},{10,14},{3,7},{... | collective-permute-start | bytes 245768 | tf_op jit(solution)/shard_map/ppermute | solution.py:30
  36.3 6.1 %collective-permute-start.5 = (f32[5,5,8,128]{3,1,2,0:T(8,128)S(1)}, f32[5,5,8,128]{3,1,2,0:T(8,128)S(1)}, u32[]{:S(2)}, u32[]{:S(2)}) collective-permute-start(f32[5,5,8,128]{3,1,2,0:T(8,128)S(1)} %pad_maximum_fusion.9), channel_id=1, source_target_pairs={{4,0},{8,4},{12,8},{5,1},{9,5},{13,9},{6,2},{10,6},{14,10},{7,3},{... | collective-permute-start | bytes 307208 | tf_op jit(solution)/shard_map/ppermute | solution.py:30
  43.1 7.0 %collective-permute-start.6 = (f32[5,24,5,128]{3,1,2,0:T(8,128)S(1)}, f32[5,24,5,128]{3,1,2,0:T(8,128)S(1)}, u32[]{:S(2)}, u32[]{:S(2)}) collective-permute-start(f32[5,24,5,128]{3,1,2,0:T(8,128)S(1)} %get-tuple-element.37), channel_id=1, source_target_pairs={{0,1},{1,2},{2,3},{4,5},{5,6},{6,7},{8,9},{9,10},{10,11},{12,13},{... | collective-permute-start | bytes 921608 | tf_op jit(solution)/shard_map/ppermute | solution.py:21
  46.3 8.2 %collective-permute-start.7 = (f32[5,24,5,128]{3,1,2,0:T(8,128)S(1)}, f32[5,24,5,128]{3,1,2,0:T(8,128)S(1)}, u32[]{:S(2)}, u32[]{:S(2)}) collective-permute-start(f32[5,24,5,128]{3,1,2,0:T(8,128)S(1)} %get-tuple-element.38), channel_id=1, source_target_pairs={{1,0},{2,1},{3,2},{5,4},{6,5},{7,6},{9,8},{10,9},{11,10},{13,12},{... | collective-permute-start | bytes 921608 | tf_op jit(solution)/shard_map/ppermute | solution.py:22
  55.8 1.3 %copy-start.5 = (pred[256,136]{1,0:T(32,128)(4,1)S(1)}, pred[256,136]{1,0:T(32,128)(4,1)}, u32[]{:S(2)}) copy-start(pred[256,136]{1,0:T(32,128)(4,1)} %constant.48.clone) | copy-start | bytes 104452
  56.4 2.6 %copy-start.7 = (f32[20,10]{1,0:T(8,128)S(1)}, f32[20,10]{1,0:T(8,128)}, u32[]{:S(2)}) copy-start(f32[20,10]{1,0:T(8,128)} %constant.51.clone) | copy-start | bytes 2404
  57.6 5.5 %collective-permute-start.9 = (f32[2,20,256]{2,1,0:T(8,128)S(1)}, f32[2,20,256]{2,1,0:T(8,128)S(1)}, u32[]{:S(2)}, u32[]{:S(2)}) collective-permute-start(f32[2,20,256]{2,1,0:T(8,128)S(1)} %get-tuple-element.44), channel_id=1, source_target_pairs={{4,0},{8,4},{12,8},{5,1},{9,5},{13,9},{6,2},{10,6},{14,10},{7,3},{... | collective-permute-start | bytes 122888 | tf_op jit(solution)/shard_map/ppermute | solution.py:30
  59.1 5.4 %collective-permute-start.8 = (f32[3,20,256]{2,1,0:T(8,128)S(1)}, f32[3,20,256]{2,1,0:T(8,128)S(1)}, u32[]{:S(2)}, u32[]{:S(2)}) collective-permute-start(f32[3,20,256]{2,1,0:T(8,128)S(1)} %pad_maximum_fusion.11), channel_id=1, source_target_pairs={{0,4},{4,8},{8,12},{1,5},{5,9},{9,13},{2,6},{6,10},{10,14},{3,7},{... | collective-permute-start | bytes 184328 | tf_op jit(solution)/shard_map/ppermute | solution.py:30

commit v20 on v19

--- a/solution.py
+++ b/solution.py
@@ -200,7 +200,7 @@
     slot_range = jnp.arange(width_x)
     last_slot = (slot_range == count_live - 1).astype(jnp.float32)
     tail_pick = (slot_range[None, :] == count_live - NCS + jnp.arange(NCS)[:, None]).astype(jnp.float32)
-    tail_planes = jnp.einsum("ks,qsjl->qkjl", tail_pick, coarse, precision=lax.Precision.HIGHEST)
+    tail_planes = jnp.einsum("ks,qsjl->qkjl", tail_pick, coarse, precision=lax.Precision.HIGH)
     head_planes = jnp.concatenate([coarse[:, :NCS], edge_sums[:, None]], axis=1)
     tail_planes, head_planes = lax.optimization_barrier((tail_planes, head_planes))
     from_prev = passed_along(tail_planes, "slab", 1)
@@ -211,7 +211,7 @@
     x_ext = jnp.concatenate([from_prev, coarse, jnp.zeros_like(tail_planes)], axis=1)
     wide_range = jnp.arange(width_x + 2 * NCS)[:, None]
     place = (wide_range == NCS + count_live + jnp.arange(NCS)[None, :]).astype(jnp.float32)
-    x_ext = x_ext + jnp.einsum("tk,qkjl->qtjl", place, from_next[:, :NCS], precision=lax.Precision.HIGHEST)
+    x_ext = x_ext + jnp.einsum("tk,qkjl->qtjl", place, from_next[:, :NCS], precision=lax.Precision.HIGH)
     coarse_rim = NCS
     rim_y = NCS + 1
     coef_ext = padded(x_ext, ((("pencil", "sub"), 2),), rim_y)

time: 67.4 us -> 67.3 us (level)
  no operation moved by 1% of the time
where the time goes in v20:
time: 67.3 us; the launch traced here: 66.9 us
  starting transfers between devices  27.1 us (40%)
  waiting for transfers between devices  19 us (28%)
  other arithmetic  9.81 us (15%)
  matrix products  4.18 us (6%)
  local copies, waits for them, and re-layouts  3.64 us (5%)
  between operations  3.21 us (5%)
    ppermute x3, starting transfers between devices, padded(): before = lax.ppermute(last, axis, up)  12.1 us
    ppermute x3, waiting for transfers between devices, padded(): after = lax.ppermute(leading, axis, down)  10.6 us
    ppermute x4, starting transfers between devices, passed_along(): return lax.ppermute(array, axis, pairs)  9.83 us
    ppermute x4, waiting for transfers between devices, passed_along(): return lax.ppermute(array, axis, pairs)  5.98 us
    ppermute x3, starting transfers between devices, padded(): after = lax.ppermute(leading, axis, down)  5.13 us
    add x4, other arithmetic, sweeps(): field_ext = center + OMEGA * (source_now - product) / faces_now[7]  3.86 us
    ppermute x3, waiting for transfers between devices, padded(): before = lax.ppermute(last, axis, up)  2.35 us
    dot_general x5, matrix products, z_sum(): return jnp.dot(flat, pick_z, precision=lax.Precision.HIGH)  1.48 us
  transfers between devices with their start and end apart: 10, of which 8 were waited for; matrix products, arithmetic and copies ran while one was open for 5% of the time, Pallas kernels for 0%

profile of v20, /device:TPU:1, one launch (start us, length us, event | category | flops | bytes accessed | tf_op | source)
XLA Modules:
  0.0 66.9 jit_solution(1517294754859910027)
XLA Ops:
  0.0 1.1 %pad_maximum_fusion.8 = (f32[3,4,16,256]{3,2,1,0:T(8,128)S(1)}, f32[3,4,16,256]{3,2,1,0:T(8,128)S(1)}) fusion(f32[1,16,16,256]{3,2,1,0:T(8,128)} %bitcast.231, f32[1,16,16,256]{3,2,1,0:T(8,128)} %bitcast.224, f32[1,16,16,256]{3,2,1,0:T(8,128)} %bitcast.233), kind=kLoop, calls=%fused_computation.123 | loop fusion | flops 196608 | bytes 1179648 | tf_op jit(solution)/shard_map/slice | solution.py:19
  1.1 4.0 %collective-permute-start = (f32[3,4,16,256]{3,2,1,0:T(8,128)S(1)}, f32[3,4,16,256]{3,2,1,0:T(8,128)S(1)}, u32[]{:S(2)}, u32[]{:S(2)}) collective-permute-start(f32[3,4,16,256]{3,2,1,0:T(8,128)S(1)} %get-tuple-element.23), channel_id=1, source_target_pairs={{0,4},{4,8},{8,12},{1,5},{5,9},{9,13},{2,6},{6,10},{10,14},{3,7},{... | collective-permute-start | bytes 589832 | tf_op jit(solution)/shard_map/ppermute | solution.py:21
  5.2 1.3 %collective-permute-start.1 = (f32[3,4,16,256]{3,2,1,0:T(8,128)S(1)}, f32[3,4,16,256]{3,2,1,0:T(8,128)S(1)}, u32[]{:S(2)}, u32[]{:S(2)}) collective-permute-start(f32[3,4,16,256]{3,2,1,0:T(8,128)S(1)} %get-tuple-element.24), channel_id=1, source_target_pairs={{4,0},{8,4},{12,8},{5,1},{9,5},{13,9},{6,2},{10,6},{14,10},{7,3},{... | collective-permute-start | bytes 589832 | tf_op jit(solution)/shard_map/ppermute | solution.py:22
  7.4 1.3 %collective-permute-done = f32[3,4,16,256]{3,2,1,0:T(8,128)S(1)} collective-permute-done((f32[3,4,16,256]{3,2,1,0:T(8,128)S(1)}, f32[3,4,16,256]{3,2,1,0:T(8,128)S(1)}, u32[]{:S(2)}, u32[]{:S(2)}) %collective-permute-start) | collective-permute-done | bytes 196640 | tf_op jit(solution)/shard_map/ppermute | solution.py:21
  8.7 3.8 %collective-permute-done.1 = f32[3,4,16,256]{3,2,1,0:T(8,128)S(1)} collective-permute-done((f32[3,4,16,256]{3,2,1,0:T(8,128)S(1)}, f32[3,4,16,256]{3,2,1,0:T(8,128)S(1)}, u32[]{:S(2)}, u32[]{:S(2)}) %collective-permute-start.1) | collective-permute-done | bytes 196640 | tf_op jit(solution)/shard_map/ppermute | solution.py:22
  12.6 0.1 fusion.145
  12.7 4.9 %collective-permute-start.2 = (f32[3,24,4,256]{3,2,1,0:T(4,128)S(1)}, f32[3,24,4,256]{3,2,1,0:T(4,128)S(1)}, u32[]{:S(2)}, u32[]{:S(2)}) collective-permute-start(f32[3,24,4,256]{3,2,1,0:T(4,128)S(1)} %get-tuple-element.21), channel_id=1, source_target_pairs={{0,1},{1,2},{2,3},{4,5},{5,6},{6,7},{8,9},{9,10},{10,11},{12,13},{... | collective-permute-start | bytes 884744 | tf_op jit(solution)/shard_map/ppermute | solution.py:21
  17.6 1.9 %collective-permute-start.3 = (f32[3,24,4,256]{3,2,1,0:T(4,128)S(1)}, f32[3,24,4,256]{3,2,1,0:T(4,128)S(1)}, u32[]{:S(2)}, u32[]{:S(2)}) collective-permute-start(f32[3,24,4,256]{3,2,1,0:T(4,128)S(1)} %get-tuple-element.22), channel_id=1, source_target_pairs={{1,0},{2,1},{3,2},{5,4},{6,5},{7,6},{9,8},{10,9},{11,10},{13,12},{... | collective-permute-start | bytes 884744 | tf_op jit(solution)/shard_map/ppermute | solution.py:22
  19.6 0.2 select_reduce_fusion
  19.7 0.7 fusion.158
  23.2 2.4 %collective-permute-done.3 = f32[3,24,4,256]{3,2,1,0:T(4,128)S(1)} collective-permute-done((f32[3,24,4,256]{3,2,1,0:T(4,128)S(1)}, f32[3,24,4,256]{3,2,1,0:T(4,128)S(1)}, u32[]{:S(2)}, u32[]{:S(2)}) %collective-permute-start.3) | collective-permute-done | bytes 294944 | tf_op jit(solution)/shard_map/ppermute | solution.py:22
  25.7 0.3 pad_maximum_fusion
  25.9 0.1 slice_bitcast_fusion
  26.1 0.2 fusion.147
  26.3 0.2 divide_select_fusion
  26.5 0.2 divide_select_fusion.1
  26.7 0.2 fusion.148
  26.9 0.2 divide_select_fusion.2
  27.2 1.1 %fusion.7 = (f32[22,22,256]{2,1,0:T(8,128)S(1)}, f32[22,22,256]{2,1,0:T(8,128)S(1)}, f32[22,22,256]{2,1,0:T(8,128)S(1)}) fusion(f32[24,24,256]{2,1,0:T(8,128)S(1)} %get-tuple-element.20, f32[24,24,256]{2,1,0:T(8,128)S(1)} %get-tuple-element.19, f32[22,22,255]{2,1,0:T(8,128)S(1)} %get-tuple-element.30, f32[22,22,255]{2,1,0:T(8,128)S(1)} %get-tuple-element.29, ...), kind=kLoop, calls=%fused_computation.22 | loop fusion | flops 3345408 | bytes 8423108 | tf_op jit(solution)/shard_map/add | solution.py:106
  28.3 0.2 fusion.149
  28.5 0.8 %fusion.26 = f32[20,20,256]{2,1,0:T(8,128)S(1)} fusion(f32[22,22,256]{2,1,0:T(8,128)S(1)} %get-tuple-element.15, f32[24,23,256]{2,1,0:T(8,128)S(1)} %divide_select_fusion, f32[23,24,256]{2,1,0:T(8,128)S(1)} %divide_select_fusion.1, f32[24,24,256]{2,1,0:T(8,128)S(1)} %get-tuple-element.19, f32[20,20,255]{2,1,0:T(8,128)S(1)} %get-tuple-element.34, ...), kind=kLoop, calls=%fused_computation.49 | loop fusion | flops 1740800 | bytes 6224880 | tf_op jit(solution)/shard_map/add | solution.py:106
  29.3 0.1 fusion.152
  29.4 0.5 fusion.146
  29.9 0.4 copy-done
  30.3 0.3 fusion.163
  30.6 0.3 fusion.159
  31.0 0.3 fusion.160
  31.3 0.3 fusion.162
  31.7 0.3 fusion.161
  32.0 0.3 fusion.11
  32.4 0.2 convolution_bitcast_fusion.2
  32.8 0.2 convolution_bitcast_fusion.1
  33.1 3.2 %collective-permute-start.4 = (f32[5,4,8,128]{3,1,2,0:T(4,128)S(1)}, f32[5,4,8,128]{3,1,2,0:T(4,128)S(1)}, u32[]{:S(2)}, u32[]{:S(2)}) collective-permute-start(f32[5,4,8,128]{3,1,2,0:T(4,128)S(1)} %convolution_bitcast_fusion.1), channel_id=1, source_target_pairs={{0,4},{4,8},{8,12},{1,5},{5,9},{9,13},{2,6},{6,10},{10,14},{3,7},{... | collective-permute-start | bytes 245768 | tf_op jit(solution)/shard_map/ppermute | solution.py:30
  36.3 1.3 %collective-permute-start.5 = (f32[5,5,8,128]{3,1,2,0:T(8,128)S(1)}, f32[5,5,8,128]{3,1,2,0:T(8,128)S(1)}, u32[]{:S(2)}, u32[]{:S(2)}) collective-permute-start(f32[5,5,8,128]{3,1,2,0:T(8,128)S(1)} %pad_maximum_fusion.9), channel_id=1, source_target_pairs={{4,0},{8,4},{12,8},{5,1},{9,5},{13,9},{6,2},{10,6},{14,10},{7,3},{... | collective-permute-start | bytes 307208 | tf_op jit(solution)/shard_map/ppermute | solution.py:30
  37.6 0.1 collective-permute-done.4
  37.8 4.5 %collective-permute-done.5 = f32[5,5,8,128]{3,1,2,0:T(8,128)S(1)} collective-permute-done((f32[5,5,8,128]{3,1,2,0:T(8,128)S(1)}, f32[5,5,8,128]{3,1,2,0:T(8,128)S(1)}, u32[]{:S(2)}, u32[]{:S(2)}) %collective-permute-start.5) | collective-permute-done | bytes 102432 | tf_op jit(solution)/shard_map/ppermute | solution.py:30
  42.4 0.1 multiply_add_fusion.1
  42.5 0.4 maximum_add_fusion
  43.0 3.2 %collective-permute-start.6 = (f32[5,24,5,128]{3,1,2,0:T(8,128)S(1)}, f32[5,24,5,128]{3,1,2,0:T(8,128)S(1)}, u32[]{:S(2)}, u32[]{:S(2)}) collective-permute-start(f32[5,24,5,128]{3,1,2,0:T(8,128)S(1)} %get-tuple-element.37), channel_id=1, source_target_pairs={{0,1},{1,2},{2,3},{4,5},{5,6},{6,7},{8,9},{9,10},{10,11},{12,13},{... | collective-permute-start | bytes 921608 | tf_op jit(solution)/shard_map/ppermute | solution.py:21
  46.2 1.9 %collective-permute-start.7 = (f32[5,24,5,128]{3,1,2,0:T(8,128)S(1)}, f32[5,24,5,128]{3,1,2,0:T(8,128)S(1)}, u32[]{:S(2)}, u32[]{:S(2)}) collective-permute-start(f32[5,24,5,128]{3,1,2,0:T(8,128)S(1)} %get-tuple-element.38), channel_id=1, source_target_pairs={{1,0},{2,1},{3,2},{5,4},{6,5},{7,6},{9,8},{10,9},{11,10},{13,12},{... | collective-permute-start | bytes 921608 | tf_op jit(solution)/shard_map/ppermute | solution.py:22
  48.1 0.8 %and_convert_fusion = f32[2]{0:T(128)S(1)} fusion(s32[19]{0:T(128)S(1)} %iota_add_fusion, f32[19]{0:T(128)S(1)} %select_reduce_fusion, f32[]{:T(128)} %bitcast.21), kind=kLoop, calls=%fused_computation.247 | loop fusion | flops 8 | bytes 28 | tf_op jit(solution)/shard_map/convert_element_type | solution.py:295
  48.9 1.1 %collective-permute-done.6 = f32[5,24,5,128]{3,1,2,0:T(8,128)S(1)} collective-permute-done((f32[5,24,5,128]{3,1,2,0:T(8,128)S(1)}, f32[5,24,5,128]{3,1,2,0:T(8,128)S(1)}, u32[]{:S(2)}, u32[]{:S(2)}) %collective-permute-start.6) | collective-permute-done | bytes 307232 | tf_op jit(solution)/shard_map/ppermute | solution.py:21
  50.0 4.4 %collective-permute-done.7 = f32[5,24,5,128]{3,1,2,0:T(8,128)S(1)} collective-permute-done((f32[5,24,5,128]{3,1,2,0:T(8,128)S(1)}, f32[5,24,5,128]{3,1,2,0:T(8,128)S(1)}, u32[]{:S(2)}, u32[]{:S(2)}) %collective-permute-start.7) | collective-permute-done | bytes 307232 | tf_op jit(solution)/shard_map/ppermute | solution.py:22
  54.5 0.2 fusion.62
  54.7 0.1 fusion.155
  54.9 0.3 fusion.70
  55.2 0.1 fusion.156
  55.3 0.3 fusion.81
  55.7 0.2 multiply_reduce_fusion
  55.9 0.2 fusion.119
  56.1 0.2 fusion.117
  56.3 0.2 fusion.108
  56.6 0.2 fusion.123
  56.8 0.2 fusion.121
  57.0 0.3 fusion.59
  57.4 0.1 fusion.164
  57.5 1.3 %collective-permute-start.9 = (f32[2,20,256]{2,1,0:T(8,128)S(1)}, f32[2,20,256]{2,1,0:T(8,128)S(1)}, u32[]{:S(2)}, u32[]{:S(2)}) collective-permute-start(f32[2,20,256]{2,1,0:T(8,128)S(1)} %get-tuple-element.44), channel_id=1, source_target_pairs={{4,0},{8,4},{12,8},{5,1},{9,5},{13,9},{6,2},{10,6},{14,10},{7,3},{... | collective-permute-start | bytes 122888 | tf_op jit(solution)/shard_map/ppermute | solution.py:30
  58.9 0.1 fusion.165
  59.0 4.0 %collective-permute-start.8 = (f32[3,20,256]{2,1,0:T(8,128)S(1)}, f32[3,20,256]{2,1,0:T(8,128)S(1)}, u32[]{:S(2)}, u32[]{:S(2)}) collective-permute-start(f32[3,20,256]{2,1,0:T(8,128)S(1)} %pad_maximum_fusion.11), channel_id=1, source_target_pairs={{0,4},{4,8},{8,12},{1,5},{5,9},{9,13},{2,6},{6,10},{10,14},{3,7},{... | collective-permute-start | bytes 184328 | tf_op jit(solution)/shard_map/ppermute | solution.py:30
  63.1 1.3 %collective-permute-done.8 = f32[3,20,256]{2,1,0:T(8,128)S(1)} collective-permute-done((f32[3,20,256]{2,1,0:T(8,128)S(1)}, f32[3,20,256]{2,1,0:T(8,128)S(1)}, u32[]{:S(2)}, u32[]{:S(2)}) %collective-permute-start.8) | collective-permute-done | bytes 61472 | tf_op jit(solution)/shard_map/ppermute | solution.py:30
  64.6 0.2 fusion.150
  64.8 0.8 %fusion.36 = f32[18,18,256]{2,1,0:T(8,128)S(1)} fusion(f32[20,20,256]{2,1,0:T(8,128)S(1)} %pad_maximum_fusion.3, f32[24,23,256]{2,1,0:T(8,128)S(1)} %divide_select_fusion, f32[2,20,256]{2,1,0:T(8,128)S(1)} %multiply_add_fusion.3, f32[16,20,256]{2,1,0:T(8,128)S(1)} %multiply_add_fusion, f32[23,24,256]{2,1,0:T(8,128)S(1)} %divide_select_fusion.1, ...), kind=kLoop, calls=%fused_computation.65 | loop fusion | flops 1575936 | bytes 4882000 | tf_op jit(solution)/shard_map/add | solution.py:106
  65.6 0.1 fusion.153
  65.7 1.1 %fusion.49 = f32[16,16,256]{2,1,0:T(8,128)} fusion(f32[18,18,256]{2,1,0:T(8,128)S(1)} %fusion.36, f32[24,24,256]{2,1,0:T(8,128)S(1)} %get-tuple-element.19, f32[16,16,255]{2,1,0:T(8,128)S(1)} %get-tuple-element.42, f32[16,16,255]{2,1,0:T(8,128)S(1)} %get-tuple-element.41, f32[24,23,256]{2,1,0:T(8,128)S(1)} %divide_select_fusion, ...), kind=kLoop, calls=%fused_computation.88 | loop fusion | flops 1114112 | bytes 4161648 | tf_op jit(solution)/shard_map/add | solution.py:106
  (84 shorter events, 2.4 us)
Async XLA Ops:
  0.0 12.5 %copy-start.3 = (f32[16,16,256]{2,1,0:T(8,128)S(1)}, f32[16,16,256]{2,1,0:T(8,128)}, u32[]{:S(2)}) copy-start(f32[16,16,256]{2,1,0:T(8,128)} %param.11) | copy-start | bytes 786436
  0.0 12.5 %copy-start.1 = (f32[16,16,256]{2,1,0:T(8,128)S(1)}, f32[16,16,256]{2,1,0:T(8,128)}, u32[]{:S(2)}) copy-start(f32[16,16,256]{2,1,0:T(8,128)} %param.12) | copy-start | bytes 786436
  0.0 12.5 %copy-start.2 = (f32[16,16,256]{2,1,0:T(8,128)S(1)}, f32[16,16,256]{2,1,0:T(8,128)}, u32[]{:S(2)}) copy-start(f32[16,16,256]{2,1,0:T(8,128)} %param.13) | copy-start | bytes 786436
  1.1 7.6 %collective-permute-start = (f32[3,4,16,256]{3,2,1,0:T(8,128)S(1)}, f32[3,4,16,256]{3,2,1,0:T(8,128)S(1)}, u32[]{:S(2)}, u32[]{:S(2)}) collective-permute-start(f32[3,4,16,256]{3,2,1,0:T(8,128)S(1)} %get-tuple-element.23), channel_id=1, source_target_pairs={{0,4},{4,8},{8,12},{1,5},{5,9},{9,13},{2,6},{6,10},{10,14},{3,7},{... | collective-permute-start | bytes 589832 | tf_op jit(solution)/shard_map/ppermute | solution.py:21
  5.2 7.3 %collective-permute-start.1 = (f32[3,4,16,256]{3,2,1,0:T(8,128)S(1)}, f32[3,4,16,256]{3,2,1,0:T(8,128)S(1)}, u32[]{:S(2)}, u32[]{:S(2)}) collective-permute-start(f32[3,4,16,256]{3,2,1,0:T(8,128)S(1)} %get-tuple-element.24), channel_id=1, source_target_pairs={{4,0},{8,4},{12,8},{5,1},{9,5},{13,9},{6,2},{10,6},{14,10},{7,3},{... | collective-permute-start | bytes 589832 | tf_op jit(solution)/shard_map/ppermute | solution.py:22
  12.6 6.9 %copy-start.9 = (s32[64]{0:T(128)S(1)}, s32[64]{0:T(128)}, u32[]{:S(2)}) copy-start(s32[64]{0:T(128)} %param.14) | copy-start | bytes 772
  12.7 10.5 %collective-permute-start.2 = (f32[3,24,4,256]{3,2,1,0:T(4,128)S(1)}, f32[3,24,4,256]{3,2,1,0:T(4,128)S(1)}, u32[]{:S(2)}, u32[]{:S(2)}) collective-permute-start(f32[3,24,4,256]{3,2,1,0:T(4,128)S(1)} %get-tuple-element.21), channel_id=1, source_target_pairs={{0,1},{1,2},{2,3},{4,5},{5,6},{6,7},{8,9},{9,10},{10,11},{12,13},{... | collective-permute-start | bytes 884744 | tf_op jit(solution)/shard_map/ppermute | solution.py:21
  17.6 8.0 %collective-permute-start.3 = (f32[3,24,4,256]{3,2,1,0:T(4,128)S(1)}, f32[3,24,4,256]{3,2,1,0:T(4,128)S(1)}, u32[]{:S(2)}, u32[]{:S(2)}) collective-permute-start(f32[3,24,4,256]{3,2,1,0:T(4,128)S(1)} %get-tuple-element.22), channel_id=1, source_target_pairs={{1,0},{2,1},{3,2},{5,4},{6,5},{7,6},{9,8},{10,9},{11,10},{13,12},{... | collective-permute-start | bytes 884744 | tf_op jit(solution)/shard_map/ppermute | solution.py:22
  29.4 0.9 %copy-start = (f32[256,128]{1,0:T(8,128)S(1)}, f32[256,128]{1,0:T(8,128)}, u32[]{:S(2)}) copy-start(f32[256,128]{1,0:T(8,128)} %constant.45.clone) | copy-start | bytes 393220
  30.6 1.0 %copy-start.4 = (f32[256,128]{1,0:T(8,128)S(1)}, f32[256,128]{1,0:T(8,128)}, u32[]{:S(2)}) copy-start(f32[256,128]{1,0:T(8,128)} %constant.46.clone) | copy-start | bytes 393220
  31.0 1.0 %copy-start.8 = (f32[136]{0:T(256)S(1)}, f32[136]{0:T(256)}, u32[]{:S(2)}) copy-start(f32[136]{0:T(256)} %constant.47.clone) | copy-start | bytes 1636
  31.0 1.0 %copy-start.10 = (pred[136,256]{1,0:T(8,128)(4,1)S(1)}, pred[136,256]{1,0:T(8,128)(4,1)}, u32[]{:S(2)}) copy-start(pred[136,256]{1,0:T(8,128)(4,1)} %constant.49.clone) | copy-start | bytes 104452
  31.6 0.8 %copy-start.6 = (pred[136,256]{1,0:T(8,128)(4,1)S(1)}, pred[136,256]{1,0:T(8,128)(4,1)}, u32[]{:S(2)}) copy-start(pred[136,256]{1,0:T(8,128)(4,1)} %constant.50.clone) | copy-start | bytes 104452
  33.1 4.7 %collective-permute-start.4 = (f32[5,4,8,128]{3,1,2,0:T(4,128)S(1)}, f32[5,4,8,128]{3,1,2,0:T(4,128)S(1)}, u32[]{:S(2)}, u32[]{:S(2)}) collective-permute-start(f32[5,4,8,128]{3,1,2,0:T(4,128)S(1)} %convolution_bitcast_fusion.1), channel_id=1, source_target_pairs={{0,4},{4,8},{8,12},{1,5},{5,9},{9,13},{2,6},{6,10},{10,14},{3,7},{... | collective-permute-start | bytes 245768 | tf_op jit(solution)/shard_map/ppermute | solution.py:30
  36.3 6.1 %collective-permute-start.5 = (f32[5,5,8,128]{3,1,2,0:T(8,128)S(1)}, f32[5,5,8,128]{3,1,2,0:T(8,128)S(1)}, u32[]{:S(2)}, u32[]{:S(2)}) collective-permute-start(f32[5,5,8,128]{3,1,2,0:T(8,128)S(1)} %pad_maximum_fusion.9), channel_id=1, source_target_pairs={{4,0},{8,4},{12,8},{5,1},{9,5},{13,9},{6,2},{10,6},{14,10},{7,3},{... | collective-permute-start | bytes 307208 | tf_op jit(solution)/shard_map/ppermute | solution.py:30
  43.0 7.0 %collective-permute-start.6 = (f32[5,24,5,128]{3,1,2,0:T(8,128)S(1)}, f32[5,24,5,128]{3,1,2,0:T(8,128)S(1)}, u32[]{:S(2)}, u32[]{:S(2)}) collective-permute-start(f32[5,24,5,128]{3,1,2,0:T(8,128)S(1)} %get-tuple-element.37), channel_id=1, source_target_pairs={{0,1},{1,2},{2,3},{4,5},{5,6},{6,7},{8,9},{9,10},{10,11},{12,13},{... | collective-permute-start | bytes 921608 | tf_op jit(solution)/shard_map/ppermute | solution.py:21
  46.2 8.2 %collective-permute-start.7 = (f32[5,24,5,128]{3,1,2,0:T(8,128)S(1)}, f32[5,24,5,128]{3,1,2,0:T(8,128)S(1)}, u32[]{:S(2)}, u32[]{:S(2)}) collective-permute-start(f32[5,24,5,128]{3,1,2,0:T(8,128)S(1)} %get-tuple-element.38), channel_id=1, source_target_pairs={{1,0},{2,1},{3,2},{5,4},{6,5},{7,6},{9,8},{10,9},{11,10},{13,12},{... | collective-permute-start | bytes 921608 | tf_op jit(solution)/shard_map/ppermute | solution.py:22
  55.7 1.3 %copy-start.5 = (pred[256,136]{1,0:T(32,128)(4,1)S(1)}, pred[256,136]{1,0:T(32,128)(4,1)}, u32[]{:S(2)}) copy-start(pred[256,136]{1,0:T(32,128)(4,1)} %constant.48.clone) | copy-start | bytes 104452
  56.3 2.6 %copy-start.7 = (f32[20,10]{1,0:T(8,128)S(1)}, f32[20,10]{1,0:T(8,128)}, u32[]{:S(2)}) copy-start(f32[20,10]{1,0:T(8,128)} %constant.51.clone) | copy-start | bytes 2404
  57.5 5.5 %collective-permute-start.9 = (f32[2,20,256]{2,1,0:T(8,128)S(1)}, f32[2,20,256]{2,1,0:T(8,128)S(1)}, u32[]{:S(2)}, u32[]{:S(2)}) collective-permute-start(f32[2,20,256]{2,1,0:T(8,128)S(1)} %get-tuple-element.44), channel_id=1, source_target_pairs={{4,0},{8,4},{12,8},{5,1},{9,5},{13,9},{6,2},{10,6},{14,10},{7,3},{... | collective-permute-start | bytes 122888 | tf_op jit(solution)/shard_map/ppermute | solution.py:30
  59.0 5.4 %collective-permute-start.8 = (f32[3,20,256]{2,1,0:T(8,128)S(1)}, f32[3,20,256]{2,1,0:T(8,128)S(1)}, u32[]{:S(2)}, u32[]{:S(2)}) collective-permute-start(f32[3,20,256]{2,1,0:T(8,128)S(1)} %pad_maximum_fusion.11), channel_id=1, source_target_pairs={{0,4},{4,8},{8,12},{1,5},{5,9},{9,13},{2,6},{6,10},{10,14},{3,7},{... | collective-permute-start | bytes 184328 | tf_op jit(solution)/shard_map/ppermute | solution.py:30

commit v21 on v20

--- a/solution.py
+++ b/solution.py
@@ -88,21 +88,24 @@
     return (center, safe_diag * center - beside_all)
 
 
-def crop(array, rim):
-    if rim == 0:
-        return array
-    return array[rim : array.shape[0] - rim, rim : array.shape[1] - rim]
+def crop(array, rim, rim_y=None):
+    rim_y = rim if rim_y is None else rim_y
+    return array[rim : array.shape[0] - rim, rim_y : array.shape[1] - rim_y]
 
 
 def sweeps(field_ext, source_ext, faces_ext, count, width):
-    def rim_of(array):
-        return (array.shape[0] - width) // 2
+    def rims(array):
+        return (array.shape[0] - width) // 2, (array.shape[1] - width) // 2
+
+    def cut(array, out_x, out_y):
+        rim_x, rim_y = rims(array)
+        return crop(array, rim_x - out_x, rim_y - out_y)
 
     for sweep_index in range(count):
-        out_rim = rim_of(field_ext) - 1
-        faces_now = tuple(crop(member, rim_of(member) - out_rim) for member in faces_ext)
+        out_x, out_y = (rim - 1 for rim in rims(field_ext))
+        faces_now = tuple(cut(member, out_x, out_y) for member in faces_ext)
         center, product = apply_fine(field_ext, faces_now)
-        source_now = crop(source_ext, rim_of(source_ext) - out_rim)
+        source_now = cut(source_ext, out_x, out_y)
         field_ext = center + OMEGA * (source_now - product) / faces_now[7]
     return field_ext
 
@@ -118,20 +121,21 @@
     sides = (("slab", 0), (("pencil", "sub"), 1))
     stacked_sides = (("slab", 1), (("pencil", "sub"), 2))
     fine_rim = 2 * NU
-    ext_x = padded(jnp.stack([permeability, source, pressure]), (("slab", 1),), fine_rim)
+    rim_x = NU + 1
+    ext_x = padded(jnp.stack([permeability, source, pressure]), (("slab", 1),), rim_x)
     ext_x, aggregate = lax.optimization_barrier((ext_x, aggregate))
     ext_all = padded(ext_x, ((("pencil", "sub"), 2),), fine_rim)
     perm_ext = ext_all[0]
     source_ext = crop(ext_all[1], 1)
-    glob_x = slab_index * width_x - fine_rim + jnp.arange(width_x + 2 * fine_rim)
+    glob_x = slab_index * width_x - rim_x + jnp.arange(width_x + 2 * rim_x)
     glob_y = row_index * width_y - fine_rim + jnp.arange(width_y + 2 * fine_rim)
     inside_x = (glob_x >= 0) & (glob_x < total_x)
     inside_y = (glob_y >= 0) & (glob_y < total_y)
     faces_ext = geometry(perm_ext, glob_x, glob_y, inside_x, inside_y, total_x, total_y)
     smooth_ext = sweeps(ext_all[2], source_ext, faces_ext, NU, width_x)
-    faces_zero = tuple(crop(member, fine_rim - 1) for member in faces_ext)
-    smooth_rows = smooth_ext[NU : NU + width_x]
-    center, product = apply_fine(crop(smooth_ext, NU - 1), faces_zero)
+    faces_zero = tuple(crop(member, rim_x - 1, fine_rim - 1) for member in faces_ext)
+    smooth_rows = smooth_ext[1 : 1 + width_x]
+    center, product = apply_fine(crop(smooth_ext, 0, NU - 1), faces_zero)
     residual = source - product
     half_y = width_y // 2
     half_z = depth_cells // 2

time: 67.3 us -> 65.6 us (0.975)
  waiting for transfers between devices: 19 us -> 17.6 us
    ppermute x3, waiting for transfers between devices: 2.35 us -> 1.33 us  [padded(): before = lax.ppermute(last, axis, up)]
where the time goes in v21:
time: 65.6 us; the launch traced here: 65.1 us
  starting transfers between devices  27 us (41%)
  waiting for transfers between devices  17.6 us (27%)
  other arithmetic  9.56 us (15%)
  matrix products  4.2 us (6%)
  local copies, waits for them, and re-layouts  3.38 us (5%)
  between operations  3.29 us (5%)
    ppermute x3, starting transfers between devices, padded(): before = lax.ppermute(last, axis, up)  12.1 us
    ppermute x3, waiting for transfers between devices, padded(): after = lax.ppermute(leading, axis, down)  10.3 us
    ppermute x4, starting transfers between devices, passed_along(): return lax.ppermute(array, axis, pairs)  9.83 us
    ppermute x4, waiting for transfers between devices, passed_along(): return lax.ppermute(array, axis, pairs)  5.98 us
    ppermute x3, starting transfers between devices, padded(): after = lax.ppermute(leading, axis, down)  5.13 us
    add x4, other arithmetic, sweeps(): field_ext = center + OMEGA * (source_now - product) / faces_now[7]  3.68 us
    dot_general x5, matrix products, z_sum(): return jnp.dot(flat, pick_z, precision=lax.Precision.HIGH)  1.48 us
    ppermute x3, waiting for transfers between devices, padded(): before = lax.ppermute(last, axis, up)  1.33 us
  transfers between devices with their start and end apart: 10, of which 8 were waited for; matrix products, arithmetic and copies ran while one was open for 5% of the time, Pallas kernels for 0%

profile of v21, /device:TPU:1, one launch (start us, length us, event | category | flops | bytes accessed | tf_op | source)
XLA Modules:
  0.0 65.1 jit_solution(2746218023354402655)
XLA Ops:
  0.0 1.0 %pad_maximum_fusion.9 = (f32[3,3,16,256]{3,2,1,0:T(8,128)S(1)}, f32[3,3,16,256]{3,2,1,0:T(8,128)S(1)}) fusion(f32[1,16,16,256]{3,2,1,0:T(8,128)} %bitcast.231, f32[1,16,16,256]{3,2,1,0:T(8,128)} %bitcast.224, f32[1,16,16,256]{3,2,1,0:T(8,128)} %bitcast.233), kind=kLoop, calls=%fused_computation.178 | loop fusion | flops 147456 | bytes 1081344 | tf_op jit(solution)/shard_map/slice | solution.py:19
  1.0 4.0 %collective-permute-start = (f32[3,3,16,256]{3,2,1,0:T(8,128)S(1)}, f32[3,3,16,256]{3,2,1,0:T(8,128)S(1)}, u32[]{:S(2)}, u32[]{:S(2)}) collective-permute-start(f32[3,3,16,256]{3,2,1,0:T(8,128)S(1)} %get-tuple-element.23), channel_id=1, source_target_pairs={{0,4},{4,8},{8,12},{1,5},{5,9},{9,13},{2,6},{6,10},{10,14},{3,7},{... | collective-permute-start | bytes 442376 | tf_op jit(solution)/shard_map/ppermute | solution.py:21
  5.1 1.3 %collective-permute-start.1 = (f32[3,3,16,256]{3,2,1,0:T(8,128)S(1)}, f32[3,3,16,256]{3,2,1,0:T(8,128)S(1)}, u32[]{:S(2)}, u32[]{:S(2)}) collective-permute-start(f32[3,3,16,256]{3,2,1,0:T(8,128)S(1)} %get-tuple-element.24), channel_id=1, source_target_pairs={{4,0},{8,4},{12,8},{5,1},{9,5},{13,9},{6,2},{10,6},{14,10},{7,3},{... | collective-permute-start | bytes 442376 | tf_op jit(solution)/shard_map/ppermute | solution.py:22
  7.4 0.1 collective-permute-done
  7.6 3.8 %collective-permute-done.1 = f32[3,3,16,256]{3,2,1,0:T(8,128)S(1)} collective-permute-done((f32[3,3,16,256]{3,2,1,0:T(8,128)S(1)}, f32[3,3,16,256]{3,2,1,0:T(8,128)S(1)}, u32[]{:S(2)}, u32[]{:S(2)}) %collective-permute-start.1) | collective-permute-done | bytes 147488 | tf_op jit(solution)/shard_map/ppermute | solution.py:22
  11.5 0.1 fusion.145
  11.6 4.9 %collective-permute-start.2 = (f32[3,22,4,256]{3,2,1,0:T(4,128)S(1)}, f32[3,22,4,256]{3,2,1,0:T(4,128)S(1)}, u32[]{:S(2)}, u32[]{:S(2)}) collective-permute-start(f32[3,22,4,256]{3,2,1,0:T(4,128)S(1)} %get-tuple-element.21), channel_id=1, source_target_pairs={{0,1},{1,2},{2,3},{4,5},{5,6},{6,7},{8,9},{9,10},{10,11},{12,13},{... | collective-permute-start | bytes 811016 | tf_op jit(solution)/shard_map/ppermute | solution.py:21
  16.4 1.9 %collective-permute-start.3 = (f32[3,22,4,256]{3,2,1,0:T(4,128)S(1)}, f32[3,22,4,256]{3,2,1,0:T(4,128)S(1)}, u32[]{:S(2)}, u32[]{:S(2)}) collective-permute-start(f32[3,22,4,256]{3,2,1,0:T(4,128)S(1)} %get-tuple-element.22), channel_id=1, source_target_pairs={{1,0},{2,1},{3,2},{5,4},{6,5},{7,6},{9,8},{10,9},{11,10},{13,12},{... | collective-permute-start | bytes 811016 | tf_op jit(solution)/shard_map/ppermute | solution.py:22
  18.4 0.2 select_reduce_fusion
  18.6 0.7 %fusion.158 = (f32[1]{0:T(128)}, f32[1]{0:T(128)}, f32[1]{0:T(128)}) fusion(f32[19]{0:T(128)S(1)} %select_reduce_fusion), kind=kLoop, calls=%fused_computation.296 | loop fusion | bytes 24 | tf_op jit(solution)/shard_map/slice | solution.py:148
  22.1 2.1 %collective-permute-done.3 = f32[3,22,4,256]{3,2,1,0:T(4,128)S(1)} collective-permute-done((f32[3,22,4,256]{3,2,1,0:T(4,128)S(1)}, f32[3,22,4,256]{3,2,1,0:T(4,128)S(1)}, u32[]{:S(2)}, u32[]{:S(2)}) %collective-permute-start.3) | collective-permute-done | bytes 270368 | tf_op jit(solution)/shard_map/ppermute | solution.py:22
  24.2 0.3 pad_maximum_fusion
  24.5 0.1 slice_bitcast_fusion
  24.6 0.2 fusion.147
  24.8 0.2 divide_select_fusion
  25.0 0.2 divide_select_fusion.1
  25.2 0.3 fusion.148
  25.5 1.0 %fusion.15 = (f32[20,22,256]{2,1,0:T(8,128)S(1)}, f32[20,22,256]{2,1,0:T(8,128)S(1)}, f32[20,22,256]{2,1,0:T(8,128)S(1)}) fusion(f32[22,24,256]{2,1,0:T(8,128)S(1)} %get-tuple-element.20, f32[22,24,256]{2,1,0:T(8,128)S(1)} %get-tuple-element.19, f32[20,22,255]{2,1,0:T(8,128)S(1)} %get-tuple-element.30, f32[20,22,255]{2,1,0:T(8,128)S(1)} %get-tuple-element.29, ...), kind=kLoop, calls=%fused_computation.31 | loop fusion | flops 3041280 | bytes 7657464 | tf_op jit(solution)/shard_map/add | solution.py:109
  26.5 0.2 fusion.151
  26.7 0.7 %fusion.38 = f32[18,20,256]{2,1,0:T(8,128)S(1)} fusion(f32[20,22,256]{2,1,0:T(8,128)S(1)} %get-tuple-element.15, f32[22,23,256]{2,1,0:T(8,128)S(1)} %divide_select_fusion, f32[21,24,256]{2,1,0:T(8,128)S(1)} %divide_select_fusion.1, f32[22,24,256]{2,1,0:T(8,128)S(1)} %get-tuple-element.19, f32[18,20,255]{2,1,0:T(8,128)S(1)} %get-tuple-element.38, ...), kind=kLoop, calls=%fused_computation.67 | loop fusion | flops 1566720 | bytes 5606880 | tf_op jit(solution)/shard_map/add | solution.py:109
  27.5 0.1 fusion.153
  27.6 0.5 fusion.146
  28.1 0.4 copy-done
  28.5 0.3 fusion.163
  28.8 0.3 fusion.159
  29.2 0.3 fusion.160
  29.5 0.3 fusion.162
  29.8 0.3 fusion.161
  30.2 0.3 fusion
  30.6 0.2 convolution_bitcast_fusion.2
  31.0 0.2 convolution_bitcast_fusion.1
  31.3 3.2 %collective-permute-start.4 = (f32[5,4,8,128]{3,1,2,0:T(4,128)S(1)}, f32[5,4,8,128]{3,1,2,0:T(4,128)S(1)}, u32[]{:S(2)}, u32[]{:S(2)}) collective-permute-start(f32[5,4,8,128]{3,1,2,0:T(4,128)S(1)} %convolution_bitcast_fusion.1), channel_id=1, source_target_pairs={{0,4},{4,8},{8,12},{1,5},{5,9},{9,13},{2,6},{6,10},{10,14},{3,7},{... | collective-permute-start | bytes 245768 | tf_op jit(solution)/shard_map/ppermute | solution.py:30
  34.5 1.3 %collective-permute-start.5 = (f32[5,5,8,128]{3,1,2,0:T(8,128)S(1)}, f32[5,5,8,128]{3,1,2,0:T(8,128)S(1)}, u32[]{:S(2)}, u32[]{:S(2)}) collective-permute-start(f32[5,5,8,128]{3,1,2,0:T(8,128)S(1)} %pad_maximum_fusion.6), channel_id=1, source_target_pairs={{4,0},{8,4},{12,8},{5,1},{9,5},{13,9},{6,2},{10,6},{14,10},{7,3},{... | collective-permute-start | bytes 307208 | tf_op jit(solution)/shard_map/ppermute | solution.py:30
  35.8 0.1 collective-permute-done.4
  36.0 4.5 %collective-permute-done.5 = f32[5,5,8,128]{3,1,2,0:T(8,128)S(1)} collective-permute-done((f32[5,5,8,128]{3,1,2,0:T(8,128)S(1)}, f32[5,5,8,128]{3,1,2,0:T(8,128)S(1)}, u32[]{:S(2)}, u32[]{:S(2)}) %collective-permute-start.5) | collective-permute-done | bytes 102432 | tf_op jit(solution)/shard_map/ppermute | solution.py:30
  40.6 0.1 multiply_add_fusion.1
  40.7 0.4 maximum_add_fusion
  41.2 3.2 %collective-permute-start.6 = (f32[5,24,5,128]{3,1,2,0:T(8,128)S(1)}, f32[5,24,5,128]{3,1,2,0:T(8,128)S(1)}, u32[]{:S(2)}, u32[]{:S(2)}) collective-permute-start(f32[5,24,5,128]{3,1,2,0:T(8,128)S(1)} %get-tuple-element.35), channel_id=1, source_target_pairs={{0,1},{1,2},{2,3},{4,5},{5,6},{6,7},{8,9},{9,10},{10,11},{12,13},{... | collective-permute-start | bytes 921608 | tf_op jit(solution)/shard_map/ppermute | solution.py:21
  44.4 1.9 %collective-permute-start.7 = (f32[5,24,5,128]{3,1,2,0:T(8,128)S(1)}, f32[5,24,5,128]{3,1,2,0:T(8,128)S(1)}, u32[]{:S(2)}, u32[]{:S(2)}) collective-permute-start(f32[5,24,5,128]{3,1,2,0:T(8,128)S(1)} %get-tuple-element.36), channel_id=1, source_target_pairs={{1,0},{2,1},{3,2},{5,4},{6,5},{7,6},{9,8},{10,9},{11,10},{13,12},{... | collective-permute-start | bytes 921608 | tf_op jit(solution)/shard_map/ppermute | solution.py:22
  46.3 0.6 and_convert_fusion
  46.9 1.2 %collective-permute-done.6 = f32[5,24,5,128]{3,1,2,0:T(8,128)S(1)} collective-permute-done((f32[5,24,5,128]{3,1,2,0:T(8,128)S(1)}, f32[5,24,5,128]{3,1,2,0:T(8,128)S(1)}, u32[]{:S(2)}, u32[]{:S(2)}) %collective-permute-start.6) | collective-permute-done | bytes 307232 | tf_op jit(solution)/shard_map/ppermute | solution.py:21
  48.1 4.4 %collective-permute-done.7 = f32[5,24,5,128]{3,1,2,0:T(8,128)S(1)} collective-permute-done((f32[5,24,5,128]{3,1,2,0:T(8,128)S(1)}, f32[5,24,5,128]{3,1,2,0:T(8,128)S(1)}, u32[]{:S(2)}, u32[]{:S(2)}) %collective-permute-start.7) | collective-permute-done | bytes 307232 | tf_op jit(solution)/shard_map/ppermute | solution.py:22
  52.7 0.2 fusion.62
  52.9 0.1 fusion.155
  53.1 0.3 fusion.70
  53.4 0.1 fusion.156
  53.5 0.3 fusion.81
  53.9 0.2 multiply_reduce_fusion
  54.1 0.2 fusion.119
  54.3 0.2 fusion.117
  54.5 0.3 fusion.108
  54.8 0.2 fusion.123
  55.0 0.2 fusion.121
  55.2 0.3 fusion.59
  55.6 0.1 fusion.164
  55.7 1.3 %collective-permute-start.9 = (f32[2,20,256]{2,1,0:T(8,128)S(1)}, f32[2,20,256]{2,1,0:T(8,128)S(1)}, u32[]{:S(2)}, u32[]{:S(2)}) collective-permute-start(f32[2,20,256]{2,1,0:T(8,128)S(1)} %get-tuple-element.44), channel_id=1, source_target_pairs={{4,0},{8,4},{12,8},{5,1},{9,5},{13,9},{6,2},{10,6},{14,10},{7,3},{... | collective-permute-start | bytes 122888 | tf_op jit(solution)/shard_map/ppermute | solution.py:30
  57.1 0.1 fusion.165
  57.2 4.0 %collective-permute-start.8 = (f32[3,20,256]{2,1,0:T(8,128)S(1)}, f32[3,20,256]{2,1,0:T(8,128)S(1)}, u32[]{:S(2)}, u32[]{:S(2)}) collective-permute-start(f32[3,20,256]{2,1,0:T(8,128)S(1)} %pad_maximum_fusion.11), channel_id=1, source_target_pairs={{0,4},{4,8},{8,12},{1,5},{5,9},{9,13},{2,6},{6,10},{10,14},{3,7},{... | collective-permute-start | bytes 184328 | tf_op jit(solution)/shard_map/ppermute | solution.py:30
  61.3 1.3 %collective-permute-done.8 = f32[3,20,256]{2,1,0:T(8,128)S(1)} collective-permute-done((f32[3,20,256]{2,1,0:T(8,128)S(1)}, f32[3,20,256]{2,1,0:T(8,128)S(1)}, u32[]{:S(2)}, u32[]{:S(2)}) %collective-permute-start.8) | collective-permute-done | bytes 61472 | tf_op jit(solution)/shard_map/ppermute | solution.py:30
  62.6 0.1 multiply_add_fusion
  62.8 0.2 fusion.149
  63.0 0.8 %fusion.26 = f32[18,18,256]{2,1,0:T(8,128)S(1)} fusion(f32[20,20,256]{2,1,0:T(8,128)S(1)} %pad_maximum_fusion.3, f32[22,23,256]{2,1,0:T(8,128)S(1)} %divide_select_fusion, f32[2,20,256]{2,1,0:T(8,128)S(1)} %multiply_add_fusion.3, f32[16,20,256]{2,1,0:T(8,128)S(1)} %multiply_add_fusion, f32[21,24,256]{2,1,0:T(8,128)S(1)} %divide_select_fusion.1, ...), kind=kLoop, calls=%fused_computation.51 | loop fusion | flops 1575936 | bytes 4837120 | tf_op jit(solution)/shard_map/add | solution.py:109
  63.8 0.1 fusion.152
  63.9 1.1 %fusion.49 = f32[16,16,256]{2,1,0:T(8,128)} fusion(f32[18,18,256]{2,1,0:T(8,128)S(1)} %fusion.26, f32[22,24,256]{2,1,0:T(8,128)S(1)} %get-tuple-element.19, f32[16,16,255]{2,1,0:T(8,128)S(1)} %get-tuple-element.40, f32[16,16,255]{2,1,0:T(8,128)S(1)} %get-tuple-element.39, f32[22,23,256]{2,1,0:T(8,128)S(1)} %divide_select_fusion, ...), kind=kLoop, calls=%fused_computation.88 | loop fusion | flops 1114112 | bytes 4116768 | tf_op jit(solution)/shard_map/add | solution.py:109
  (85 shorter events, 2.4 us)
Async XLA Ops:
  0.0 11.4 %copy-start.3 = (f32[16,16,256]{2,1,0:T(8,128)S(1)}, f32[16,16,256]{2,1,0:T(8,128)}, u32[]{:S(2)}) copy-start(f32[16,16,256]{2,1,0:T(8,128)} %param.11) | copy-start | bytes 786436
  0.0 11.4 %copy-start.1 = (f32[16,16,256]{2,1,0:T(8,128)S(1)}, f32[16,16,256]{2,1,0:T(8,128)}, u32[]{:S(2)}) copy-start(f32[16,16,256]{2,1,0:T(8,128)} %param.12) | copy-start | bytes 786436
  0.0 11.4 %copy-start.2 = (f32[16,16,256]{2,1,0:T(8,128)S(1)}, f32[16,16,256]{2,1,0:T(8,128)}, u32[]{:S(2)}) copy-start(f32[16,16,256]{2,1,0:T(8,128)} %param.13) | copy-start | bytes 786436
  1.0 6.5 %collective-permute-start = (f32[3,3,16,256]{3,2,1,0:T(8,128)S(1)}, f32[3,3,16,256]{3,2,1,0:T(8,128)S(1)}, u32[]{:S(2)}, u32[]{:S(2)}) collective-permute-start(f32[3,3,16,256]{3,2,1,0:T(8,128)S(1)} %get-tuple-element.23), channel_id=1, source_target_pairs={{0,4},{4,8},{8,12},{1,5},{5,9},{9,13},{2,6},{6,10},{10,14},{3,7},{... | collective-permute-start | bytes 442376 | tf_op jit(solution)/shard_map/ppermute | solution.py:21
  5.1 6.3 %collective-permute-start.1 = (f32[3,3,16,256]{3,2,1,0:T(8,128)S(1)}, f32[3,3,16,256]{3,2,1,0:T(8,128)S(1)}, u32[]{:S(2)}, u32[]{:S(2)}) collective-permute-start(f32[3,3,16,256]{3,2,1,0:T(8,128)S(1)} %get-tuple-element.24), channel_id=1, source_target_pairs={{4,0},{8,4},{12,8},{5,1},{9,5},{13,9},{6,2},{10,6},{14,10},{7,3},{... | collective-permute-start | bytes 442376 | tf_op jit(solution)/shard_map/ppermute | solution.py:22
  7.4 10.9 %copy-start.9 = (s32[64]{0:T(128)S(1)}, s32[64]{0:T(128)}, u32[]{:S(2)}) copy-start(s32[64]{0:T(128)} %param.14) | copy-start | bytes 772
  11.6 10.6 %collective-permute-start.2 = (f32[3,22,4,256]{3,2,1,0:T(4,128)S(1)}, f32[3,22,4,256]{3,2,1,0:T(4,128)S(1)}, u32[]{:S(2)}, u32[]{:S(2)}) collective-permute-start(f32[3,22,4,256]{3,2,1,0:T(4,128)S(1)} %get-tuple-element.21), channel_id=1, source_target_pairs={{0,1},{1,2},{2,3},{4,5},{5,6},{6,7},{8,9},{9,10},{10,11},{12,13},{... | collective-permute-start | bytes 811016 | tf_op jit(solution)/shard_map/ppermute | solution.py:21
  16.4 7.8 %collective-permute-start.3 = (f32[3,22,4,256]{3,2,1,0:T(4,128)S(1)}, f32[3,22,4,256]{3,2,1,0:T(4,128)S(1)}, u32[]{:S(2)}, u32[]{:S(2)}) collective-permute-start(f32[3,22,4,256]{3,2,1,0:T(4,128)S(1)} %get-tuple-element.22), channel_id=1, source_target_pairs={{1,0},{2,1},{3,2},{5,4},{6,5},{7,6},{9,8},{10,9},{11,10},{13,12},{... | collective-permute-start | bytes 811016 | tf_op jit(solution)/shard_map/ppermute | solution.py:22
  27.6 0.9 %copy-start = (f32[256,128]{1,0:T(8,128)S(1)}, f32[256,128]{1,0:T(8,128)}, u32[]{:S(2)}) copy-start(f32[256,128]{1,0:T(8,128)} %constant.47.clone) | copy-start | bytes 393220
  28.8 1.0 %copy-start.4 = (f32[256,128]{1,0:T(8,128)S(1)}, f32[256,128]{1,0:T(8,128)}, u32[]{:S(2)}) copy-start(f32[256,128]{1,0:T(8,128)} %constant.48.clone) | copy-start | bytes 393220
  29.1 1.0 %copy-start.8 = (f32[136]{0:T(256)S(1)}, f32[136]{0:T(256)}, u32[]{:S(2)}) copy-start(f32[136]{0:T(256)} %constant.49.clone) | copy-start | bytes 1636
  29.1 1.0 %copy-start.10 = (pred[136,256]{1,0:T(8,128)(4,1)S(1)}, pred[136,256]{1,0:T(8,128)(4,1)}, u32[]{:S(2)}) copy-start(pred[136,256]{1,0:T(8,128)(4,1)} %constant.51.clone) | copy-start | bytes 104452
  29.8 0.8 %copy-start.6 = (pred[136,256]{1,0:T(8,128)(4,1)S(1)}, pred[136,256]{1,0:T(8,128)(4,1)}, u32[]{:S(2)}) copy-start(pred[136,256]{1,0:T(8,128)(4,1)} %constant.52.clone) | copy-start | bytes 104452
  31.3 4.7 %collective-permute-start.4 = (f32[5,4,8,128]{3,1,2,0:T(4,128)S(1)}, f32[5,4,8,128]{3,1,2,0:T(4,128)S(1)}, u32[]{:S(2)}, u32[]{:S(2)}) collective-permute-start(f32[5,4,8,128]{3,1,2,0:T(4,128)S(1)} %convolution_bitcast_fusion.1), channel_id=1, source_target_pairs={{0,4},{4,8},{8,12},{1,5},{5,9},{9,13},{2,6},{6,10},{10,14},{3,7},{... | collective-permute-start | bytes 245768 | tf_op jit(solution)/shard_map/ppermute | solution.py:30
  34.5 6.1 %collective-permute-start.5 = (f32[5,5,8,128]{3,1,2,0:T(8,128)S(1)}, f32[5,5,8,128]{3,1,2,0:T(8,128)S(1)}, u32[]{:S(2)}, u32[]{:S(2)}) collective-permute-start(f32[5,5,8,128]{3,1,2,0:T(8,128)S(1)} %pad_maximum_fusion.6), channel_id=1, source_target_pairs={{4,0},{8,4},{12,8},{5,1},{9,5},{13,9},{6,2},{10,6},{14,10},{7,3},{... | collective-permute-start | bytes 307208 | tf_op jit(solution)/shard_map/ppermute | solution.py:30
  41.2 7.0 %collective-permute-start.6 = (f32[5,24,5,128]{3,1,2,0:T(8,128)S(1)}, f32[5,24,5,128]{3,1,2,0:T(8,128)S(1)}, u32[]{:S(2)}, u32[]{:S(2)}) collective-permute-start(f32[5,24,5,128]{3,1,2,0:T(8,128)S(1)} %get-tuple-element.35), channel_id=1, source_target_pairs={{0,1},{1,2},{2,3},{4,5},{5,6},{6,7},{8,9},{9,10},{10,11},{12,13},{... | collective-permute-start | bytes 921608 | tf_op jit(solution)/shard_map/ppermute | solution.py:21
  44.4 8.2 %collective-permute-start.7 = (f32[5,24,5,128]{3,1,2,0:T(8,128)S(1)}, f32[5,24,5,128]{3,1,2,0:T(8,128)S(1)}, u32[]{:S(2)}, u32[]{:S(2)}) collective-permute-start(f32[5,24,5,128]{3,1,2,0:T(8,128)S(1)} %get-tuple-element.36), channel_id=1, source_target_pairs={{1,0},{2,1},{3,2},{5,4},{6,5},{7,6},{9,8},{10,9},{11,10},{13,12},{... | collective-permute-start | bytes 921608 | tf_op jit(solution)/shard_map/ppermute | solution.py:22
  53.9 1.3 %copy-start.5 = (pred[256,136]{1,0:T(32,128)(4,1)S(1)}, pred[256,136]{1,0:T(32,128)(4,1)}, u32[]{:S(2)}) copy-start(pred[256,136]{1,0:T(32,128)(4,1)} %constant.50.clone) | copy-start | bytes 104452
  54.8 2.3 %copy-start.7 = (f32[20,10]{1,0:T(8,128)S(1)}, f32[20,10]{1,0:T(8,128)}, u32[]{:S(2)}) copy-start(f32[20,10]{1,0:T(8,128)} %constant.53.clone) | copy-start | bytes 2404
  55.7 5.5 %collective-permute-start.9 = (f32[2,20,256]{2,1,0:T(8,128)S(1)}, f32[2,20,256]{2,1,0:T(8,128)S(1)}, u32[]{:S(2)}, u32[]{:S(2)}) collective-permute-start(f32[2,20,256]{2,1,0:T(8,128)S(1)} %get-tuple-element.44), channel_id=1, source_target_pairs={{4,0},{8,4},{12,8},{5,1},{9,5},{13,9},{6,2},{10,6},{14,10},{7,3},{... | collective-permute-start | bytes 122888 | tf_op jit(solution)/shard_map/ppermute | solution.py:30
  57.2 5.4 %collective-permute-start.8 = (f32[3,20,256]{2,1,0:T(8,128)S(1)}, f32[3,20,256]{2,1,0:T(8,128)S(1)}, u32[]{:S(2)}, u32[]{:S(2)}) collective-permute-start(f32[3,20,256]{2,1,0:T(8,128)S(1)} %pad_maximum_fusion.11), channel_id=1, source_target_pairs={{0,4},{4,8},{8,12},{1,5},{5,9},{9,13},{2,6},{6,10},{10,14},{3,7},{... | collective-permute-start | bytes 184328 | tf_op jit(solution)/shard_map/ppermute | solution.py:30

commit v22 on v21

--- a/solution.py
+++ b/solution.py
@@ -218,7 +218,10 @@
     x_ext = x_ext + jnp.einsum("tk,qkjl->qtjl", place, from_next[:, :NCS], precision=lax.Precision.HIGH)
     coarse_rim = NCS
     rim_y = NCS + 1
-    coef_ext = padded(x_ext, ((("pencil", "sub"), 2),), rim_y)
+    rows_axis = ("pencil", "sub")
+    from_below = passed_along(x_ext[:, :, half_y - rim_y :], rows_axis, 1)
+    from_above = passed_along(x_ext[:, :, : rim_y - 1], rows_axis, -1)
+    coef_ext = jnp.concatenate([from_below, x_ext, from_above], axis=2)
     coarse_corr = jnp.zeros((width_x + 2 * NCS, half_y + 2 * rim_y, half_z), jnp.float32)
     for sweep_index in range(NCS):
         out_rim = NCS - 1 - sweep_index

time: 65.6 us -> 64.6 us (0.985)
  the two profiles are of different devices: /device:TPU:1 before, /device:TPU:10 now
where the time goes in v22:
time: 64.6 us; the launch traced here: 64.1 us
  starting transfers between devices  26.2 us (41%)
  waiting for transfers between devices  17 us (26%)
  other arithmetic  9.61 us (15%)
  matrix products  4.22 us (7%)
  local copies, waits for them, and re-layouts  3.98 us (6%)
  between operations  3.12 us (5%)
    ppermute x6, starting transfers between devices, passed_along(): return lax.ppermute(array, axis, pairs)  16 us
    ppermute x6, waiting for transfers between devices, passed_along(): return lax.ppermute(array, axis, pairs)  12.5 us
    ppermute x2, starting transfers between devices, padded(): before = lax.ppermute(last, axis, up)  5.9 us
    ppermute x2, starting transfers between devices, padded(): after = lax.ppermute(leading, axis, down)  4.28 us
    ppermute x2, waiting for transfers between devices, padded(): before = lax.ppermute(last, axis, up)  3.9 us
    add x4, other arithmetic, sweeps(): field_ext = center + OMEGA * (source_now - product) / faces_now[7]  3.68 us
    dot_general x5, matrix products, z_sum(): return jnp.dot(flat, pick_z, precision=lax.Precision.HIGH)  1.47 us
  transfers between devices with their start and end apart: 10, of which 8 were waited for; matrix products, arithmetic and copies ran while one was open for 5% of the time, Pallas kernels for 0%

profile of v22, /device:TPU:10, one launch (start us, length us, event | category | flops | bytes accessed | tf_op | source)
XLA Modules:
  0.0 64.1 jit_solution(10790294850994583734)
XLA Ops:
  0.0 1.0 %pad_maximum_fusion.9 = (f32[3,3,16,256]{3,2,1,0:T(8,128)S(1)}, f32[3,3,16,256]{3,2,1,0:T(8,128)S(1)}) fusion(f32[1,16,16,256]{3,2,1,0:T(8,128)} %bitcast.231, f32[1,16,16,256]{3,2,1,0:T(8,128)} %bitcast.224, f32[1,16,16,256]{3,2,1,0:T(8,128)} %bitcast.233), kind=kLoop, calls=%fused_computation.178 | loop fusion | flops 147456 | bytes 1081344 | tf_op jit(solution)/shard_map/slice | solution.py:19
  1.0 2.4 %collective-permute-start.1 = (f32[3,3,16,256]{3,2,1,0:T(8,128)S(1)}, f32[3,3,16,256]{3,2,1,0:T(8,128)S(1)}, u32[]{:S(2)}, u32[]{:S(2)}) collective-permute-start(f32[3,3,16,256]{3,2,1,0:T(8,128)S(1)} %get-tuple-element.24), channel_id=1, source_target_pairs={{4,0},{8,4},{12,8},{5,1},{9,5},{13,9},{6,2},{10,6},{14,10},{7,3},{... | collective-permute-start | bytes 442376 | tf_op jit(solution)/shard_map/ppermute | solution.py:22
  3.4 3.5 %collective-permute-start = (f32[3,3,16,256]{3,2,1,0:T(8,128)S(1)}, f32[3,3,16,256]{3,2,1,0:T(8,128)S(1)}, u32[]{:S(2)}, u32[]{:S(2)}) collective-permute-start(f32[3,3,16,256]{3,2,1,0:T(8,128)S(1)} %get-tuple-element.23), channel_id=1, source_target_pairs={{0,4},{4,8},{8,12},{1,5},{5,9},{9,13},{2,6},{6,10},{10,14},{3,7},{... | collective-permute-start | bytes 442376 | tf_op jit(solution)/shard_map/ppermute | solution.py:21
  7.9 0.6 collective-permute-done.1
  8.5 2.1 %collective-permute-done = f32[3,3,16,256]{3,2,1,0:T(8,128)S(1)} collective-permute-done((f32[3,3,16,256]{3,2,1,0:T(8,128)S(1)}, f32[3,3,16,256]{3,2,1,0:T(8,128)S(1)}, u32[]{:S(2)}, u32[]{:S(2)}) %collective-permute-start) | collective-permute-done | bytes 147488 | tf_op jit(solution)/shard_map/ppermute | solution.py:21
  10.8 1.9 %collective-permute-start.3 = (f32[3,22,4,256]{3,2,1,0:T(4,128)S(1)}, f32[3,22,4,256]{3,2,1,0:T(4,128)S(1)}, u32[]{:S(2)}, u32[]{:S(2)}) collective-permute-start(f32[3,22,4,256]{3,2,1,0:T(4,128)S(1)} %get-tuple-element.22), channel_id=1, source_target_pairs={{1,0},{2,1},{3,2},{5,4},{6,5},{7,6},{9,8},{10,9},{11,10},{13,12},{... | collective-permute-start | bytes 811016 | tf_op jit(solution)/shard_map/ppermute | solution.py:22
  12.7 2.4 %collective-permute-start.2 = (f32[3,22,4,256]{3,2,1,0:T(4,128)S(1)}, f32[3,22,4,256]{3,2,1,0:T(4,128)S(1)}, u32[]{:S(2)}, u32[]{:S(2)}) collective-permute-start(f32[3,22,4,256]{3,2,1,0:T(4,128)S(1)} %get-tuple-element.21), channel_id=1, source_target_pairs={{0,1},{1,2},{2,3},{4,5},{5,6},{6,7},{8,9},{9,10},{10,11},{12,13},{... | collective-permute-start | bytes 811016 | tf_op jit(solution)/shard_map/ppermute | solution.py:21
  15.2 0.2 select_reduce_fusion
  15.4 0.6 fusion.157
  18.7 1.8 %collective-permute-done.2 = f32[3,22,4,256]{3,2,1,0:T(4,128)S(1)} collective-permute-done((f32[3,22,4,256]{3,2,1,0:T(4,128)S(1)}, f32[3,22,4,256]{3,2,1,0:T(4,128)S(1)}, u32[]{:S(2)}, u32[]{:S(2)}) %collective-permute-start.2) | collective-permute-done | bytes 270368 | tf_op jit(solution)/shard_map/ppermute | solution.py:21
  20.5 0.3 pad_maximum_fusion
  20.8 0.1 slice_bitcast_fusion
  20.9 0.2 fusion.147
  21.1 0.2 divide_select_fusion
  21.3 0.2 divide_select_fusion.1
  21.5 0.3 fusion.148
  21.8 1.0 %fusion.15 = (f32[20,22,256]{2,1,0:T(8,128)S(1)}, f32[20,22,256]{2,1,0:T(8,128)S(1)}, f32[20,22,256]{2,1,0:T(8,128)S(1)}) fusion(f32[22,24,256]{2,1,0:T(8,128)S(1)} %get-tuple-element.20, f32[22,24,256]{2,1,0:T(8,128)S(1)} %get-tuple-element.19, f32[20,22,255]{2,1,0:T(8,128)S(1)} %get-tuple-element.30, f32[20,22,255]{2,1,0:T(8,128)S(1)} %get-tuple-element.29, ...), kind=kLoop, calls=%fused_computation.31 | loop fusion | flops 3041280 | bytes 7657464 | tf_op jit(solution)/shard_map/add | solution.py:109
  22.8 0.2 fusion.150
  23.1 0.7 %fusion.38 = f32[18,20,256]{2,1,0:T(8,128)S(1)} fusion(f32[20,22,256]{2,1,0:T(8,128)S(1)} %get-tuple-element.15, f32[22,23,256]{2,1,0:T(8,128)S(1)} %divide_select_fusion, f32[21,24,256]{2,1,0:T(8,128)S(1)} %divide_select_fusion.1, f32[22,24,256]{2,1,0:T(8,128)S(1)} %get-tuple-element.19, f32[18,20,255]{2,1,0:T(8,128)S(1)} %get-tuple-element.36, ...), kind=kLoop, calls=%fused_computation.67 | loop fusion | flops 1566720 | bytes 5606880 | tf_op jit(solution)/shard_map/add | solution.py:109
  23.8 0.1 fusion.152
  24.0 0.7 %copy-done = f32[256,128]{1,0:T(8,128)S(1)} copy-done((f32[256,128]{1,0:T(8,128)S(1)}, f32[256,128]{1,0:T(8,128)}, u32[]{:S(2)}) %copy-start) | copy-done | bytes 131096
  24.7 0.3 fusion.161
  25.0 0.5 fusion.146
  25.5 0.3 fusion.159
  25.9 0.3 fusion.158
  26.2 0.3 copy-done.4
  26.4 0.3 fusion.160
  26.8 0.3 fusion
  27.1 0.3 fusion.162
  27.5 0.2 convolution_bitcast_fusion.2
  27.9 0.2 convolution_bitcast_fusion.1
  28.2 3.5 %collective-permute-start.4 = (f32[5,4,8,128]{3,1,2,0:T(4,128)S(1)}, f32[5,4,8,128]{3,1,2,0:T(4,128)S(1)}, u32[]{:S(2)}, u32[]{:S(2)}) collective-permute-start(f32[5,4,8,128]{3,1,2,0:T(4,128)S(1)} %convolution_bitcast_fusion.1), channel_id=1, source_target_pairs={{0,4},{4,8},{8,12},{1,5},{5,9},{9,13},{2,6},{6,10},{10,14},{3,7},{... | collective-permute-start | bytes 245768 | tf_op jit(solution)/shard_map/ppermute | solution.py:30
  31.7 2.4 %collective-permute-start.5 = (f32[5,5,8,128]{3,1,2,0:T(8,128)S(1)}, f32[5,5,8,128]{3,1,2,0:T(8,128)S(1)}, u32[]{:S(2)}, u32[]{:S(2)}) collective-permute-start(f32[5,5,8,128]{3,1,2,0:T(8,128)S(1)} %pad_maximum_fusion.6), channel_id=1, source_target_pairs={{4,0},{8,4},{12,8},{5,1},{9,5},{13,9},{6,2},{10,6},{14,10},{7,3},{... | collective-permute-start | bytes 307208 | tf_op jit(solution)/shard_map/ppermute | solution.py:30
  34.0 0.5 collective-permute-done.4
  34.6 4.3 %collective-permute-done.5 = f32[5,5,8,128]{3,1,2,0:T(8,128)S(1)} collective-permute-done((f32[5,5,8,128]{3,1,2,0:T(8,128)S(1)}, f32[5,5,8,128]{3,1,2,0:T(8,128)S(1)}, u32[]{:S(2)}, u32[]{:S(2)}) %collective-permute-start.5) | collective-permute-done | bytes 102432 | tf_op jit(solution)/shard_map/ppermute | solution.py:30
  38.9 0.1 multiply_add_fusion.1
  39.0 0.4 maximum_add_fusion
  39.5 1.9 %collective-permute-start.7 = (f32[5,24,4,128]{3,1,2,0:T(8,128)S(1)}, f32[5,24,4,128]{3,1,2,0:T(8,128)S(1)}, u32[]{:S(2)}, u32[]{:S(2)}) collective-permute-start(f32[5,24,4,128]{3,1,2,0:T(8,128)S(1)} %slice.835), channel_id=1, source_target_pairs={{1,0},{2,1},{3,2},{5,4},{6,5},{7,6},{9,8},{10,9},{11,10},{13,12},{... | collective-permute-start | bytes 737288 | tf_op jit(solution)/shard_map/ppermute | solution.py:30
  41.4 2.4 %collective-permute-start.6 = (f32[5,24,5,128]{3,1,2,0:T(8,128)S(1)}, f32[5,24,5,128]{3,1,2,0:T(8,128)S(1)}, u32[]{:S(2)}, u32[]{:S(2)}) collective-permute-start(f32[5,24,5,128]{3,1,2,0:T(8,128)S(1)} %slice.834), channel_id=1, source_target_pairs={{0,1},{1,2},{2,3},{4,5},{5,6},{6,7},{8,9},{9,10},{10,11},{12,13},{... | collective-permute-start | bytes 921608 | tf_op jit(solution)/shard_map/ppermute | solution.py:30
  43.9 0.7 %and_convert_fusion = f32[2]{0:T(128)S(1)} fusion(s32[19]{0:T(128)S(1)} %iota_add_fusion, f32[19]{0:T(128)S(1)} %select_reduce_fusion, f32[]{:T(128)} %bitcast.21), kind=kLoop, calls=%fused_computation.247 | loop fusion | flops 8 | bytes 28 | tf_op jit(solution)/shard_map/convert_element_type | solution.py:302
  44.6 0.6 collective-permute-done.7
  45.1 4.5 %collective-permute-done.6 = f32[5,24,5,128]{3,1,2,0:T(8,128)S(1)} collective-permute-done((f32[5,24,5,128]{3,1,2,0:T(8,128)S(1)}, f32[5,24,5,128]{3,1,2,0:T(8,128)S(1)}, u32[]{:S(2)}, u32[]{:S(2)}) %collective-permute-start.6) | collective-permute-done | bytes 307232 | tf_op jit(solution)/shard_map/ppermute | solution.py:30
  49.8 0.2 fusion.62
  50.0 0.1 fusion.154
  50.1 0.3 fusion.70
  50.5 0.1 fusion.155
  50.6 0.3 fusion.81
  51.0 0.2 multiply_reduce_fusion
  51.2 0.2 fusion.117
  51.4 0.2 fusion.119
  51.6 0.3 fusion.108
  51.8 0.2 fusion.121
  52.0 0.2 fusion.123
  52.2 0.3 fusion.59
  52.7 2.4 %collective-permute-start.9 = (f32[2,20,256]{2,1,0:T(8,128)S(1)}, f32[2,20,256]{2,1,0:T(8,128)S(1)}, u32[]{:S(2)}, u32[]{:S(2)}) collective-permute-start(f32[2,20,256]{2,1,0:T(8,128)S(1)} %get-tuple-element.42), channel_id=1, source_target_pairs={{4,0},{8,4},{12,8},{5,1},{9,5},{13,9},{6,2},{10,6},{14,10},{7,3},{... | collective-permute-start | bytes 122888 | tf_op jit(solution)/shard_map/ppermute | solution.py:30
  55.1 0.1 fusion.163
  55.2 0.2 fusion.164
  55.4 3.4 %collective-permute-start.8 = (f32[3,20,256]{2,1,0:T(8,128)S(1)}, f32[3,20,256]{2,1,0:T(8,128)S(1)}, u32[]{:S(2)}, u32[]{:S(2)}) collective-permute-start(f32[3,20,256]{2,1,0:T(8,128)S(1)} %pad_maximum_fusion.11), channel_id=1, source_target_pairs={{0,4},{4,8},{8,12},{1,5},{5,9},{9,13},{2,6},{6,10},{10,14},{3,7},{... | collective-permute-start | bytes 184328 | tf_op jit(solution)/shard_map/ppermute | solution.py:30
  58.9 2.7 %collective-permute-done.8 = f32[3,20,256]{2,1,0:T(8,128)S(1)} collective-permute-done((f32[3,20,256]{2,1,0:T(8,128)S(1)}, f32[3,20,256]{2,1,0:T(8,128)S(1)}, u32[]{:S(2)}, u32[]{:S(2)}) %collective-permute-start.8) | collective-permute-done | bytes 61472 | tf_op jit(solution)/shard_map/ppermute | solution.py:30
  61.7 0.1 multiply_add_fusion
  61.8 0.2 fusion.149
  62.0 0.8 %fusion.26 = f32[18,18,256]{2,1,0:T(8,128)S(1)} fusion(f32[20,20,256]{2,1,0:T(8,128)S(1)} %pad_maximum_fusion.3, f32[22,23,256]{2,1,0:T(8,128)S(1)} %divide_select_fusion, f32[2,20,256]{2,1,0:T(8,128)S(1)} %multiply_add_fusion.3, f32[16,20,256]{2,1,0:T(8,128)S(1)} %multiply_add_fusion, f32[21,24,256]{2,1,0:T(8,128)S(1)} %divide_select_fusion.1, ...), kind=kLoop, calls=%fused_computation.51 | loop fusion | flops 1575936 | bytes 4837120 | tf_op jit(solution)/shard_map/add | solution.py:109
  62.8 0.1 fusion.151
  63.0 1.1 %fusion.49 = f32[16,16,256]{2,1,0:T(8,128)} fusion(f32[18,18,256]{2,1,0:T(8,128)S(1)} %fusion.26, f32[22,24,256]{2,1,0:T(8,128)S(1)} %get-tuple-element.19, f32[16,16,255]{2,1,0:T(8,128)S(1)} %get-tuple-element.38, f32[16,16,255]{2,1,0:T(8,128)S(1)} %get-tuple-element.37, f32[22,23,256]{2,1,0:T(8,128)S(1)} %divide_select_fusion, ...), kind=kLoop, calls=%fused_computation.88 | loop fusion | flops 1114112 | bytes 4116768 | tf_op jit(solution)/shard_map/add | solution.py:109
  (86 shorter events, 2.5 us)
Async XLA Ops:
  0.0 10.6 %copy-start.2 = (f32[16,16,256]{2,1,0:T(8,128)S(1)}, f32[16,16,256]{2,1,0:T(8,128)}, u32[]{:S(2)}) copy-start(f32[16,16,256]{2,1,0:T(8,128)} %param.13) | copy-start | bytes 786436
  0.0 10.6 %copy-start.1 = (f32[16,16,256]{2,1,0:T(8,128)S(1)}, f32[16,16,256]{2,1,0:T(8,128)}, u32[]{:S(2)}) copy-start(f32[16,16,256]{2,1,0:T(8,128)} %param.12) | copy-start | bytes 786436
  0.0 10.6 %copy-start.3 = (f32[16,16,256]{2,1,0:T(8,128)S(1)}, f32[16,16,256]{2,1,0:T(8,128)}, u32[]{:S(2)}) copy-start(f32[16,16,256]{2,1,0:T(8,128)} %param.11) | copy-start | bytes 786436
  1.0 7.5 %collective-permute-start.1 = (f32[3,3,16,256]{3,2,1,0:T(8,128)S(1)}, f32[3,3,16,256]{3,2,1,0:T(8,128)S(1)}, u32[]{:S(2)}, u32[]{:S(2)}) collective-permute-start(f32[3,3,16,256]{3,2,1,0:T(8,128)S(1)} %get-tuple-element.24), channel_id=1, source_target_pairs={{4,0},{8,4},{12,8},{5,1},{9,5},{13,9},{6,2},{10,6},{14,10},{7,3},{... | collective-permute-start | bytes 442376 | tf_op jit(solution)/shard_map/ppermute | solution.py:22
  3.4 7.2 %collective-permute-start = (f32[3,3,16,256]{3,2,1,0:T(8,128)S(1)}, f32[3,3,16,256]{3,2,1,0:T(8,128)S(1)}, u32[]{:S(2)}, u32[]{:S(2)}) collective-permute-start(f32[3,3,16,256]{3,2,1,0:T(8,128)S(1)} %get-tuple-element.23), channel_id=1, source_target_pairs={{0,4},{4,8},{8,12},{1,5},{5,9},{9,13},{2,6},{6,10},{10,14},{3,7},{... | collective-permute-start | bytes 442376 | tf_op jit(solution)/shard_map/ppermute | solution.py:21
  10.7 4.5 %copy-start.9 = (s32[64]{0:T(128)S(1)}, s32[64]{0:T(128)}, u32[]{:S(2)}) copy-start(s32[64]{0:T(128)} %param.14) | copy-start | bytes 772
  10.8 7.9 %collective-permute-start.3 = (f32[3,22,4,256]{3,2,1,0:T(4,128)S(1)}, f32[3,22,4,256]{3,2,1,0:T(4,128)S(1)}, u32[]{:S(2)}, u32[]{:S(2)}) collective-permute-start(f32[3,22,4,256]{3,2,1,0:T(4,128)S(1)} %get-tuple-element.22), channel_id=1, source_target_pairs={{1,0},{2,1},{3,2},{5,4},{6,5},{7,6},{9,8},{10,9},{11,10},{13,12},{... | collective-permute-start | bytes 811016 | tf_op jit(solution)/shard_map/ppermute | solution.py:22
  12.7 7.8 %collective-permute-start.2 = (f32[3,22,4,256]{3,2,1,0:T(4,128)S(1)}, f32[3,22,4,256]{3,2,1,0:T(4,128)S(1)}, u32[]{:S(2)}, u32[]{:S(2)}) collective-permute-start(f32[3,22,4,256]{3,2,1,0:T(4,128)S(1)} %get-tuple-element.21), channel_id=1, source_target_pairs={{0,1},{1,2},{2,3},{4,5},{5,6},{6,7},{8,9},{9,10},{10,11},{12,13},{... | collective-permute-start | bytes 811016 | tf_op jit(solution)/shard_map/ppermute | solution.py:21
  23.8 0.9 %copy-start = (f32[256,128]{1,0:T(8,128)S(1)}, f32[256,128]{1,0:T(8,128)}, u32[]{:S(2)}) copy-start(f32[256,128]{1,0:T(8,128)} %constant.47.clone) | copy-start | bytes 393220
  25.5 0.9 %copy-start.4 = (f32[256,128]{1,0:T(8,128)S(1)}, f32[256,128]{1,0:T(8,128)}, u32[]{:S(2)}) copy-start(f32[256,128]{1,0:T(8,128)} %constant.48.clone) | copy-start | bytes 393220
  25.5 1.2 %copy-start.8 = (f32[136]{0:T(256)S(1)}, f32[136]{0:T(256)}, u32[]{:S(2)}) copy-start(f32[136]{0:T(256)} %constant.49.clone) | copy-start | bytes 1636
  25.5 1.2 %copy-start.10 = (pred[136,256]{1,0:T(8,128)(4,1)S(1)}, pred[136,256]{1,0:T(8,128)(4,1)}, u32[]{:S(2)}) copy-start(pred[136,256]{1,0:T(8,128)(4,1)} %constant.51.clone) | copy-start | bytes 104452
  26.7 0.8 %copy-start.6 = (pred[136,256]{1,0:T(8,128)(4,1)S(1)}, pred[136,256]{1,0:T(8,128)(4,1)}, u32[]{:S(2)}) copy-start(pred[136,256]{1,0:T(8,128)(4,1)} %constant.52.clone) | copy-start | bytes 104452
  28.2 6.3 %collective-permute-start.4 = (f32[5,4,8,128]{3,1,2,0:T(4,128)S(1)}, f32[5,4,8,128]{3,1,2,0:T(4,128)S(1)}, u32[]{:S(2)}, u32[]{:S(2)}) collective-permute-start(f32[5,4,8,128]{3,1,2,0:T(4,128)S(1)} %convolution_bitcast_fusion.1), channel_id=1, source_target_pairs={{0,4},{4,8},{8,12},{1,5},{5,9},{9,13},{2,6},{6,10},{10,14},{3,7},{... | collective-permute-start | bytes 245768 | tf_op jit(solution)/shard_map/ppermute | solution.py:30
  31.7 7.2 %collective-permute-start.5 = (f32[5,5,8,128]{3,1,2,0:T(8,128)S(1)}, f32[5,5,8,128]{3,1,2,0:T(8,128)S(1)}, u32[]{:S(2)}, u32[]{:S(2)}) collective-permute-start(f32[5,5,8,128]{3,1,2,0:T(8,128)S(1)} %pad_maximum_fusion.6), channel_id=1, source_target_pairs={{4,0},{8,4},{12,8},{5,1},{9,5},{13,9},{6,2},{10,6},{14,10},{7,3},{... | collective-permute-start | bytes 307208 | tf_op jit(solution)/shard_map/ppermute | solution.py:30
  39.5 5.6 %collective-permute-start.7 = (f32[5,24,4,128]{3,1,2,0:T(8,128)S(1)}, f32[5,24,4,128]{3,1,2,0:T(8,128)S(1)}, u32[]{:S(2)}, u32[]{:S(2)}) collective-permute-start(f32[5,24,4,128]{3,1,2,0:T(8,128)S(1)} %slice.835), channel_id=1, source_target_pairs={{1,0},{2,1},{3,2},{5,4},{6,5},{7,6},{9,8},{10,9},{11,10},{13,12},{... | collective-permute-start | bytes 737288 | tf_op jit(solution)/shard_map/ppermute | solution.py:30
  41.4 8.2 %collective-permute-start.6 = (f32[5,24,5,128]{3,1,2,0:T(8,128)S(1)}, f32[5,24,5,128]{3,1,2,0:T(8,128)S(1)}, u32[]{:S(2)}, u32[]{:S(2)}) collective-permute-start(f32[5,24,5,128]{3,1,2,0:T(8,128)S(1)} %slice.834), channel_id=1, source_target_pairs={{0,1},{1,2},{2,3},{4,5},{5,6},{6,7},{8,9},{9,10},{10,11},{12,13},{... | collective-permute-start | bytes 921608 | tf_op jit(solution)/shard_map/ppermute | solution.py:30
  51.0 1.3 %copy-start.5 = (pred[256,136]{1,0:T(32,128)(4,1)S(1)}, pred[256,136]{1,0:T(32,128)(4,1)}, u32[]{:S(2)}) copy-start(pred[256,136]{1,0:T(32,128)(4,1)} %constant.50.clone) | copy-start | bytes 104452
  51.8 3.4 %copy-start.7 = (f32[20,10]{1,0:T(8,128)S(1)}, f32[20,10]{1,0:T(8,128)}, u32[]{:S(2)}) copy-start(f32[20,10]{1,0:T(8,128)} %constant.53.clone) | copy-start | bytes 2404
  52.7 6.2 %collective-permute-start.9 = (f32[2,20,256]{2,1,0:T(8,128)S(1)}, f32[2,20,256]{2,1,0:T(8,128)S(1)}, u32[]{:S(2)}, u32[]{:S(2)}) collective-permute-start(f32[2,20,256]{2,1,0:T(8,128)S(1)} %get-tuple-element.42), channel_id=1, source_target_pairs={{4,0},{8,4},{12,8},{5,1},{9,5},{13,9},{6,2},{10,6},{14,10},{7,3},{... | collective-permute-start | bytes 122888 | tf_op jit(solution)/shard_map/ppermute | solution.py:30
  55.4 6.2 %collective-permute-start.8 = (f32[3,20,256]{2,1,0:T(8,128)S(1)}, f32[3,20,256]{2,1,0:T(8,128)S(1)}, u32[]{:S(2)}, u32[]{:S(2)}) collective-permute-start(f32[3,20,256]{2,1,0:T(8,128)S(1)} %pad_maximum_fusion.11), channel_id=1, source_target_pairs={{0,4},{4,8},{8,12},{1,5},{5,9},{9,13},{2,6},{6,10},{10,14},{3,7},{... | collective-permute-start | bytes 184328 | tf_op jit(solution)/shard_map/ppermute | solution.py:30

commit v23 on v22

--- a/solution.py
+++ b/solution.py
@@ -205,17 +205,18 @@
     last_slot = (slot_range == count_live - 1).astype(jnp.float32)
     tail_pick = (slot_range[None, :] == count_live - NCS + jnp.arange(NCS)[:, None]).astype(jnp.float32)
     tail_planes = jnp.einsum("ks,qsjl->qkjl", tail_pick, coarse, precision=lax.Precision.HIGH)
-    head_planes = jnp.concatenate([coarse[:, :NCS], edge_sums[:, None]], axis=1)
+    ahead = NCS - 1
+    head_planes = jnp.concatenate([coarse[:, :ahead], edge_sums[:, None]], axis=1)
     tail_planes, head_planes = lax.optimization_barrier((tail_planes, head_planes))
     from_prev = passed_along(tail_planes, "slab", 1)
     from_next = passed_along(head_planes, "slab", -1)
-    coarse = coarse + from_next[:, NCS][:, None] * last_slot[None, :, None, None]
+    coarse = coarse + from_next[:, ahead][:, None] * last_slot[None, :, None, None]
     prev_last = (jnp.arange(NCS) == NCS - 1).astype(jnp.float32)
     from_prev = from_prev + edge_sums[:, None] * prev_last[None, :, None, None]
     x_ext = jnp.concatenate([from_prev, coarse, jnp.zeros_like(tail_planes)], axis=1)
     wide_range = jnp.arange(width_x + 2 * NCS)[:, None]
-    place = (wide_range == NCS + count_live + jnp.arange(NCS)[None, :]).astype(jnp.float32)
-    x_ext = x_ext + jnp.einsum("tk,qkjl->qtjl", place, from_next[:, :NCS], precision=lax.Precision.HIGH)
+    place = (wide_range == NCS + count_live + jnp.arange(ahead)[None, :]).astype(jnp.float32)
+    x_ext = x_ext + jnp.einsum("tk,qkjl->qtjl", place, from_next[:, :ahead], precision=lax.Precision.HIGH)
     coarse_rim = NCS
     rim_y = NCS + 1
     rows_axis = ("pencil", "sub")

time: 64.6 us -> 62.5 us (0.967)
  the two profiles are of different devices: /device:TPU:10 before, /device:TPU:26 now
where the time goes in v23:
time: 62.5 us; the launch traced here: 62 us
  waiting for transfers between devices  21.5 us (34%)
  starting transfers between devices  19.6 us (31%)
  other arithmetic  9.61 us (15%)
  matrix products  4.22 us (7%)
  local copies, waits for them, and re-layouts  3.99 us (6%)
  between operations  3.11 us (5%)
    ppermute x6, waiting for transfers between devices, passed_along(): return lax.ppermute(array, axis, pairs)  14.8 us
    ppermute x6, starting transfers between devices, passed_along(): return lax.ppermute(array, axis, pairs)  11.6 us
    ppermute x2, waiting for transfers between devices, padded(): before = lax.ppermute(last, axis, up)  5.93 us
    ppermute x2, starting transfers between devices, padded(): after = lax.ppermute(leading, axis, down)  4.28 us
    ppermute x2, starting transfers between devices, padded(): before = lax.ppermute(last, axis, up)  3.71 us
    add x4, other arithmetic, sweeps(): field_ext = center + OMEGA * (source_now - product) / faces_now[7]  3.68 us
    dot_general x5, matrix products, z_sum(): return jnp.dot(flat, pick_z, precision=lax.Precision.HIGH)  1.47 us
  transfers between devices with their start and end apart: 10, of which 9 were waited for; matrix products, arithmetic and copies ran while one was open for 5% of the time, Pallas kernels for 0%

profile of v23, /device:TPU:26, one launch (start us, length us, event | category | flops | bytes accessed | tf_op | source)
XLA Modules:
  0.0 62.0 jit_solution(5307403772627143158)
XLA Ops:
  0.0 1.0 %pad_maximum_fusion.8 = (f32[3,3,16,256]{3,2,1,0:T(8,128)S(1)}, f32[3,3,16,256]{3,2,1,0:T(8,128)S(1)}) fusion(f32[1,16,16,256]{3,2,1,0:T(8,128)} %bitcast.231, f32[1,16,16,256]{3,2,1,0:T(8,128)} %bitcast.224, f32[1,16,16,256]{3,2,1,0:T(8,128)} %bitcast.233), kind=kLoop, calls=%fused_computation.177 | loop fusion | flops 147456 | bytes 1081344 | tf_op jit(solution)/shard_map/slice | solution.py:19
  1.0 2.4 %collective-permute-start.1 = (f32[3,3,16,256]{3,2,1,0:T(8,128)S(1)}, f32[3,3,16,256]{3,2,1,0:T(8,128)S(1)}, u32[]{:S(2)}, u32[]{:S(2)}) collective-permute-start(f32[3,3,16,256]{3,2,1,0:T(8,128)S(1)} %get-tuple-element.24), channel_id=1, source_target_pairs={{4,0},{8,4},{12,8},{5,1},{9,5},{13,9},{6,2},{10,6},{14,10},{7,3},{... | collective-permute-start | bytes 442376 | tf_op jit(solution)/shard_map/ppermute | solution.py:22
  3.4 1.3 %collective-permute-start = (f32[3,3,16,256]{3,2,1,0:T(8,128)S(1)}, f32[3,3,16,256]{3,2,1,0:T(8,128)S(1)}, u32[]{:S(2)}, u32[]{:S(2)}) collective-permute-start(f32[3,3,16,256]{3,2,1,0:T(8,128)S(1)} %get-tuple-element.23), channel_id=1, source_target_pairs={{0,4},{4,8},{8,12},{1,5},{5,9},{9,13},{2,6},{6,10},{10,14},{3,7},{... | collective-permute-start | bytes 442376 | tf_op jit(solution)/shard_map/ppermute | solution.py:21
  5.8 0.7 %collective-permute-done.1 = f32[3,3,16,256]{3,2,1,0:T(8,128)S(1)} collective-permute-done((f32[3,3,16,256]{3,2,1,0:T(8,128)S(1)}, f32[3,3,16,256]{3,2,1,0:T(8,128)S(1)}, u32[]{:S(2)}, u32[]{:S(2)}) %collective-permute-start.1) | collective-permute-done | bytes 147488 | tf_op jit(solution)/shard_map/ppermute | solution.py:22
  6.5 4.1 %collective-permute-done = f32[3,3,16,256]{3,2,1,0:T(8,128)S(1)} collective-permute-done((f32[3,3,16,256]{3,2,1,0:T(8,128)S(1)}, f32[3,3,16,256]{3,2,1,0:T(8,128)S(1)}, u32[]{:S(2)}, u32[]{:S(2)}) %collective-permute-start) | collective-permute-done | bytes 147488 | tf_op jit(solution)/shard_map/ppermute | solution.py:21
  10.8 1.9 %collective-permute-start.3 = (f32[3,22,4,256]{3,2,1,0:T(4,128)S(1)}, f32[3,22,4,256]{3,2,1,0:T(4,128)S(1)}, u32[]{:S(2)}, u32[]{:S(2)}) collective-permute-start(f32[3,22,4,256]{3,2,1,0:T(4,128)S(1)} %get-tuple-element.22), channel_id=1, source_target_pairs={{1,0},{2,1},{3,2},{5,4},{6,5},{7,6},{9,8},{10,9},{11,10},{13,12},{... | collective-permute-start | bytes 811016 | tf_op jit(solution)/shard_map/ppermute | solution.py:22
  12.7 2.4 %collective-permute-start.2 = (f32[3,22,4,256]{3,2,1,0:T(4,128)S(1)}, f32[3,22,4,256]{3,2,1,0:T(4,128)S(1)}, u32[]{:S(2)}, u32[]{:S(2)}) collective-permute-start(f32[3,22,4,256]{3,2,1,0:T(4,128)S(1)} %get-tuple-element.21), channel_id=1, source_target_pairs={{0,1},{1,2},{2,3},{4,5},{5,6},{6,7},{8,9},{9,10},{10,11},{12,13},{... | collective-permute-start | bytes 811016 | tf_op jit(solution)/shard_map/ppermute | solution.py:21
  15.2 0.2 select_reduce_fusion
  15.4 0.6 %fusion.157 = (f32[1]{0:T(128)}, f32[1]{0:T(128)}, f32[1]{0:T(128)}) fusion(f32[19]{0:T(128)S(1)} %select_reduce_fusion), kind=kLoop, calls=%fused_computation.295 | loop fusion | bytes 24 | tf_op jit(solution)/shard_map/slice | solution.py:148
  18.7 1.8 %collective-permute-done.2 = f32[3,22,4,256]{3,2,1,0:T(4,128)S(1)} collective-permute-done((f32[3,22,4,256]{3,2,1,0:T(4,128)S(1)}, f32[3,22,4,256]{3,2,1,0:T(4,128)S(1)}, u32[]{:S(2)}, u32[]{:S(2)}) %collective-permute-start.2) | collective-permute-done | bytes 270368 | tf_op jit(solution)/shard_map/ppermute | solution.py:21
  20.5 0.3 pad_maximum_fusion
  20.8 0.1 slice_bitcast_fusion
  20.9 0.2 fusion.147
  21.1 0.2 divide_select_fusion
  21.3 0.2 divide_select_fusion.1
  21.5 0.3 fusion.148
  21.8 1.0 %fusion.15 = (f32[20,22,256]{2,1,0:T(8,128)S(1)}, f32[20,22,256]{2,1,0:T(8,128)S(1)}, f32[20,22,256]{2,1,0:T(8,128)S(1)}) fusion(f32[22,24,256]{2,1,0:T(8,128)S(1)} %get-tuple-element.20, f32[22,24,256]{2,1,0:T(8,128)S(1)} %get-tuple-element.19, f32[20,22,255]{2,1,0:T(8,128)S(1)} %get-tuple-element.30, f32[20,22,255]{2,1,0:T(8,128)S(1)} %get-tuple-element.29, ...), kind=kLoop, calls=%fused_computation.31 | loop fusion | flops 3041280 | bytes 7657464 | tf_op jit(solution)/shard_map/add | solution.py:109
  22.8 0.2 fusion.150
  23.1 0.7 %fusion.38 = f32[18,20,256]{2,1,0:T(8,128)S(1)} fusion(f32[20,22,256]{2,1,0:T(8,128)S(1)} %get-tuple-element.15, f32[22,23,256]{2,1,0:T(8,128)S(1)} %divide_select_fusion, f32[21,24,256]{2,1,0:T(8,128)S(1)} %divide_select_fusion.1, f32[22,24,256]{2,1,0:T(8,128)S(1)} %get-tuple-element.19, f32[18,20,255]{2,1,0:T(8,128)S(1)} %get-tuple-element.36, ...), kind=kLoop, calls=%fused_computation.67 | loop fusion | flops 1566720 | bytes 5606880 | tf_op jit(solution)/shard_map/add | solution.py:109
  23.8 0.1 fusion.152
  24.0 0.7 %copy-done = f32[256,128]{1,0:T(8,128)S(1)} copy-done((f32[256,128]{1,0:T(8,128)S(1)}, f32[256,128]{1,0:T(8,128)}, u32[]{:S(2)}) %copy-start) | copy-done | bytes 131096
  24.7 0.3 fusion.161
  25.0 0.5 fusion.146
  25.6 0.3 fusion.159
  25.9 0.3 fusion.158
  26.2 0.3 copy-done.4
  26.4 0.3 fusion.160
  26.8 0.3 fusion
  27.2 0.3 fusion.162
  27.5 0.2 convolution_bitcast_fusion.2
  27.9 0.2 convolution_bitcast_fusion.1
  28.2 2.4 %collective-permute-start.5 = (f32[5,4,8,128]{3,1,2,0:T(4,128)S(1)}, f32[5,4,8,128]{3,1,2,0:T(4,128)S(1)}, u32[]{:S(2)}, u32[]{:S(2)}) collective-permute-start(f32[5,4,8,128]{3,1,2,0:T(4,128)S(1)} %pad_maximum_fusion.10), channel_id=1, source_target_pairs={{4,0},{8,4},{12,8},{5,1},{9,5},{13,9},{6,2},{10,6},{14,10},{7,3},{... | collective-permute-start | bytes 245768 | tf_op jit(solution)/shard_map/ppermute | solution.py:30
  30.5 1.3 %collective-permute-start.4 = (f32[5,4,8,128]{3,1,2,0:T(4,128)S(1)}, f32[5,4,8,128]{3,1,2,0:T(4,128)S(1)}, u32[]{:S(2)}, u32[]{:S(2)}) collective-permute-start(f32[5,4,8,128]{3,1,2,0:T(4,128)S(1)} %convolution_bitcast_fusion.1), channel_id=1, source_target_pairs={{0,4},{4,8},{8,12},{1,5},{5,9},{9,13},{2,6},{6,10},{10,14},{3,7},{... | collective-permute-start | bytes 245768 | tf_op jit(solution)/shard_map/ppermute | solution.py:30
  31.8 0.7 %collective-permute-done.5 = f32[5,4,8,128]{3,1,2,0:T(4,128)S(1)} collective-permute-done((f32[5,4,8,128]{3,1,2,0:T(4,128)S(1)}, f32[5,4,8,128]{3,1,2,0:T(4,128)S(1)}, u32[]{:S(2)}, u32[]{:S(2)}) %collective-permute-start.5) | collective-permute-done | bytes 81952 | tf_op jit(solution)/shard_map/ppermute | solution.py:30
  32.6 0.1 multiply_add_fusion.1
  32.7 4.2 %collective-permute-done.4 = f32[5,4,8,128]{3,1,2,0:T(4,128)S(1)} collective-permute-done((f32[5,4,8,128]{3,1,2,0:T(4,128)S(1)}, f32[5,4,8,128]{3,1,2,0:T(4,128)S(1)}, u32[]{:S(2)}, u32[]{:S(2)}) %collective-permute-start.4) | collective-permute-done | bytes 81952 | tf_op jit(solution)/shard_map/ppermute | solution.py:30
  37.0 0.4 maximum_add_fusion
  37.5 1.9 %collective-permute-start.7 = (f32[5,24,4,128]{3,1,2,0:T(8,128)S(1)}, f32[5,24,4,128]{3,1,2,0:T(8,128)S(1)}, u32[]{:S(2)}, u32[]{:S(2)}) collective-permute-start(f32[5,24,4,128]{3,1,2,0:T(8,128)S(1)} %slice.835), channel_id=1, source_target_pairs={{1,0},{2,1},{3,2},{5,4},{6,5},{7,6},{9,8},{10,9},{11,10},{13,12},{... | collective-permute-start | bytes 737288 | tf_op jit(solution)/shard_map/ppermute | solution.py:30
  39.4 2.4 %collective-permute-start.6 = (f32[5,24,5,128]{3,1,2,0:T(8,128)S(1)}, f32[5,24,5,128]{3,1,2,0:T(8,128)S(1)}, u32[]{:S(2)}, u32[]{:S(2)}) collective-permute-start(f32[5,24,5,128]{3,1,2,0:T(8,128)S(1)} %slice.834), channel_id=1, source_target_pairs={{0,1},{1,2},{2,3},{4,5},{5,6},{6,7},{8,9},{9,10},{10,11},{12,13},{... | collective-permute-start | bytes 921608 | tf_op jit(solution)/shard_map/ppermute | solution.py:30
  41.8 0.7 %and_convert_fusion = f32[2]{0:T(128)S(1)} fusion(s32[19]{0:T(128)S(1)} %iota_add_fusion, f32[19]{0:T(128)S(1)} %select_reduce_fusion, f32[]{:T(128)} %bitcast.21), kind=kLoop, calls=%fused_computation.247 | loop fusion | flops 8 | bytes 28 | tf_op jit(solution)/shard_map/convert_element_type | solution.py:303
  42.5 0.6 collective-permute-done.7
  43.1 4.5 %collective-permute-done.6 = f32[5,24,5,128]{3,1,2,0:T(8,128)S(1)} collective-permute-done((f32[5,24,5,128]{3,1,2,0:T(8,128)S(1)}, f32[5,24,5,128]{3,1,2,0:T(8,128)S(1)}, u32[]{:S(2)}, u32[]{:S(2)}) %collective-permute-start.6) | collective-permute-done | bytes 307232 | tf_op jit(solution)/shard_map/ppermute | solution.py:30
  47.7 0.2 fusion.62
  48.0 0.1 fusion.154
  48.1 0.3 fusion.70
  48.4 0.1 fusion.155
  48.5 0.3 fusion.81
  48.9 0.2 multiply_reduce_fusion
  49.2 0.2 fusion.117
  49.4 0.2 fusion.119
  49.5 0.3 fusion.108
  49.8 0.2 fusion.121
  50.0 0.2 fusion.123
  50.2 0.3 fusion.59
  50.6 2.4 %collective-permute-start.9 = (f32[2,20,256]{2,1,0:T(8,128)S(1)}, f32[2,20,256]{2,1,0:T(8,128)S(1)}, u32[]{:S(2)}, u32[]{:S(2)}) collective-permute-start(f32[2,20,256]{2,1,0:T(8,128)S(1)} %get-tuple-element.42), channel_id=1, source_target_pairs={{4,0},{8,4},{12,8},{5,1},{9,5},{13,9},{6,2},{10,6},{14,10},{7,3},{... | collective-permute-start | bytes 122888 | tf_op jit(solution)/shard_map/ppermute | solution.py:30
  53.0 0.1 fusion.163
  53.1 0.2 fusion.164
  53.3 1.3 %collective-permute-start.8 = (f32[3,20,256]{2,1,0:T(8,128)S(1)}, f32[3,20,256]{2,1,0:T(8,128)S(1)}, u32[]{:S(2)}, u32[]{:S(2)}) collective-permute-start(f32[3,20,256]{2,1,0:T(8,128)S(1)} %pad_maximum_fusion.11), channel_id=1, source_target_pairs={{0,4},{4,8},{8,12},{1,5},{5,9},{9,13},{2,6},{6,10},{10,14},{3,7},{... | collective-permute-start | bytes 184328 | tf_op jit(solution)/shard_map/ppermute | solution.py:30
  54.8 4.8 %collective-permute-done.8 = f32[3,20,256]{2,1,0:T(8,128)S(1)} collective-permute-done((f32[3,20,256]{2,1,0:T(8,128)S(1)}, f32[3,20,256]{2,1,0:T(8,128)S(1)}, u32[]{:S(2)}, u32[]{:S(2)}) %collective-permute-start.8) | collective-permute-done | bytes 61472 | tf_op jit(solution)/shard_map/ppermute | solution.py:30
  59.6 0.1 multiply_add_fusion
  59.7 0.2 fusion.149
  59.9 0.8 %fusion.26 = f32[18,18,256]{2,1,0:T(8,128)S(1)} fusion(f32[20,20,256]{2,1,0:T(8,128)S(1)} %pad_maximum_fusion.3, f32[22,23,256]{2,1,0:T(8,128)S(1)} %divide_select_fusion, f32[2,20,256]{2,1,0:T(8,128)S(1)} %multiply_add_fusion.3, f32[16,20,256]{2,1,0:T(8,128)S(1)} %multiply_add_fusion, f32[21,24,256]{2,1,0:T(8,128)S(1)} %divide_select_fusion.1, ...), kind=kLoop, calls=%fused_computation.51 | loop fusion | flops 1575936 | bytes 4837120 | tf_op jit(solution)/shard_map/add | solution.py:109
  60.7 0.1 fusion.151
  60.9 1.1 %fusion.49 = f32[16,16,256]{2,1,0:T(8,128)} fusion(f32[18,18,256]{2,1,0:T(8,128)S(1)} %fusion.26, f32[22,24,256]{2,1,0:T(8,128)S(1)} %get-tuple-element.19, f32[16,16,255]{2,1,0:T(8,128)S(1)} %get-tuple-element.38, f32[16,16,255]{2,1,0:T(8,128)S(1)} %get-tuple-element.37, f32[22,23,256]{2,1,0:T(8,128)S(1)} %divide_select_fusion, ...), kind=kLoop, calls=%fused_computation.88 | loop fusion | flops 1114112 | bytes 4116768 | tf_op jit(solution)/shard_map/add | solution.py:109
  (86 shorter events, 2.6 us)
Async XLA Ops:
  0.0 10.6 %copy-start.2 = (f32[16,16,256]{2,1,0:T(8,128)S(1)}, f32[16,16,256]{2,1,0:T(8,128)}, u32[]{:S(2)}) copy-start(f32[16,16,256]{2,1,0:T(8,128)} %param.13) | copy-start | bytes 786436
  0.0 10.6 %copy-start.1 = (f32[16,16,256]{2,1,0:T(8,128)S(1)}, f32[16,16,256]{2,1,0:T(8,128)}, u32[]{:S(2)}) copy-start(f32[16,16,256]{2,1,0:T(8,128)} %param.12) | copy-start | bytes 786436
  0.0 10.6 %copy-start.3 = (f32[16,16,256]{2,1,0:T(8,128)S(1)}, f32[16,16,256]{2,1,0:T(8,128)}, u32[]{:S(2)}) copy-start(f32[16,16,256]{2,1,0:T(8,128)} %param.11) | copy-start | bytes 786436
  1.0 5.5 %collective-permute-start.1 = (f32[3,3,16,256]{3,2,1,0:T(8,128)S(1)}, f32[3,3,16,256]{3,2,1,0:T(8,128)S(1)}, u32[]{:S(2)}, u32[]{:S(2)}) collective-permute-start(f32[3,3,16,256]{3,2,1,0:T(8,128)S(1)} %get-tuple-element.24), channel_id=1, source_target_pairs={{4,0},{8,4},{12,8},{5,1},{9,5},{13,9},{6,2},{10,6},{14,10},{7,3},{... | collective-permute-start | bytes 442376 | tf_op jit(solution)/shard_map/ppermute | solution.py:22
  3.4 7.2 %collective-permute-start = (f32[3,3,16,256]{3,2,1,0:T(8,128)S(1)}, f32[3,3,16,256]{3,2,1,0:T(8,128)S(1)}, u32[]{:S(2)}, u32[]{:S(2)}) collective-permute-start(f32[3,3,16,256]{3,2,1,0:T(8,128)S(1)} %get-tuple-element.23), channel_id=1, source_target_pairs={{0,4},{4,8},{8,12},{1,5},{5,9},{9,13},{2,6},{6,10},{10,14},{3,7},{... | collective-permute-start | bytes 442376 | tf_op jit(solution)/shard_map/ppermute | solution.py:21
  10.7 4.5 %copy-start.9 = (s32[64]{0:T(128)S(1)}, s32[64]{0:T(128)}, u32[]{:S(2)}) copy-start(s32[64]{0:T(128)} %param.14) | copy-start | bytes 772
  10.8 7.9 %collective-permute-start.3 = (f32[3,22,4,256]{3,2,1,0:T(4,128)S(1)}, f32[3,22,4,256]{3,2,1,0:T(4,128)S(1)}, u32[]{:S(2)}, u32[]{:S(2)}) collective-permute-start(f32[3,22,4,256]{3,2,1,0:T(4,128)S(1)} %get-tuple-element.22), channel_id=1, source_target_pairs={{1,0},{2,1},{3,2},{5,4},{6,5},{7,6},{9,8},{10,9},{11,10},{13,12},{... | collective-permute-start | bytes 811016 | tf_op jit(solution)/shard_map/ppermute | solution.py:22
  12.7 7.8 %collective-permute-start.2 = (f32[3,22,4,256]{3,2,1,0:T(4,128)S(1)}, f32[3,22,4,256]{3,2,1,0:T(4,128)S(1)}, u32[]{:S(2)}, u32[]{:S(2)}) collective-permute-start(f32[3,22,4,256]{3,2,1,0:T(4,128)S(1)} %get-tuple-element.21), channel_id=1, source_target_pairs={{0,1},{1,2},{2,3},{4,5},{5,6},{6,7},{8,9},{9,10},{10,11},{12,13},{... | collective-permute-start | bytes 811016 | tf_op jit(solution)/shard_map/ppermute | solution.py:21
  23.8 0.9 %copy-start = (f32[256,128]{1,0:T(8,128)S(1)}, f32[256,128]{1,0:T(8,128)}, u32[]{:S(2)}) copy-start(f32[256,128]{1,0:T(8,128)} %constant.47.clone) | copy-start | bytes 393220
  25.5 0.9 %copy-start.4 = (f32[256,128]{1,0:T(8,128)S(1)}, f32[256,128]{1,0:T(8,128)}, u32[]{:S(2)}) copy-start(f32[256,128]{1,0:T(8,128)} %constant.48.clone) | copy-start | bytes 393220
  25.5 1.2 %copy-start.8 = (f32[136]{0:T(256)S(1)}, f32[136]{0:T(256)}, u32[]{:S(2)}) copy-start(f32[136]{0:T(256)} %constant.49.clone) | copy-start | bytes 1636
  25.5 1.2 %copy-start.10 = (pred[136,256]{1,0:T(8,128)(4,1)S(1)}, pred[136,256]{1,0:T(8,128)(4,1)}, u32[]{:S(2)}) copy-start(pred[136,256]{1,0:T(8,128)(4,1)} %constant.51.clone) | copy-start | bytes 104452
  26.7 0.8 %copy-start.6 = (pred[136,256]{1,0:T(8,128)(4,1)S(1)}, pred[136,256]{1,0:T(8,128)(4,1)}, u32[]{:S(2)}) copy-start(pred[136,256]{1,0:T(8,128)(4,1)} %constant.52.clone) | copy-start | bytes 104452
  28.2 4.4 %collective-permute-start.5 = (f32[5,4,8,128]{3,1,2,0:T(4,128)S(1)}, f32[5,4,8,128]{3,1,2,0:T(4,128)S(1)}, u32[]{:S(2)}, u32[]{:S(2)}) collective-permute-start(f32[5,4,8,128]{3,1,2,0:T(4,128)S(1)} %pad_maximum_fusion.10), channel_id=1, source_target_pairs={{4,0},{8,4},{12,8},{5,1},{9,5},{13,9},{6,2},{10,6},{14,10},{7,3},{... | collective-permute-start | bytes 245768 | tf_op jit(solution)/shard_map/ppermute | solution.py:30
  30.5 6.3 %collective-permute-start.4 = (f32[5,4,8,128]{3,1,2,0:T(4,128)S(1)}, f32[5,4,8,128]{3,1,2,0:T(4,128)S(1)}, u32[]{:S(2)}, u32[]{:S(2)}) collective-permute-start(f32[5,4,8,128]{3,1,2,0:T(4,128)S(1)} %convolution_bitcast_fusion.1), channel_id=1, source_target_pairs={{0,4},{4,8},{8,12},{1,5},{5,9},{9,13},{2,6},{6,10},{10,14},{3,7},{... | collective-permute-start | bytes 245768 | tf_op jit(solution)/shard_map/ppermute | solution.py:30
  37.5 5.6 %collective-permute-start.7 = (f32[5,24,4,128]{3,1,2,0:T(8,128)S(1)}, f32[5,24,4,128]{3,1,2,0:T(8,128)S(1)}, u32[]{:S(2)}, u32[]{:S(2)}) collective-permute-start(f32[5,24,4,128]{3,1,2,0:T(8,128)S(1)} %slice.835), channel_id=1, source_target_pairs={{1,0},{2,1},{3,2},{5,4},{6,5},{7,6},{9,8},{10,9},{11,10},{13,12},{... | collective-permute-start | bytes 737288 | tf_op jit(solution)/shard_map/ppermute | solution.py:30
  39.4 8.2 %collective-permute-start.6 = (f32[5,24,5,128]{3,1,2,0:T(8,128)S(1)}, f32[5,24,5,128]{3,1,2,0:T(8,128)S(1)}, u32[]{:S(2)}, u32[]{:S(2)}) collective-permute-start(f32[5,24,5,128]{3,1,2,0:T(8,128)S(1)} %slice.834), channel_id=1, source_target_pairs={{0,1},{1,2},{2,3},{4,5},{5,6},{6,7},{8,9},{9,10},{10,11},{12,13},{... | collective-permute-start | bytes 921608 | tf_op jit(solution)/shard_map/ppermute | solution.py:30
  48.9 1.3 %copy-start.5 = (pred[256,136]{1,0:T(32,128)(4,1)S(1)}, pred[256,136]{1,0:T(32,128)(4,1)}, u32[]{:S(2)}) copy-start(pred[256,136]{1,0:T(32,128)(4,1)} %constant.50.clone) | copy-start | bytes 104452
  49.8 3.3 %copy-start.7 = (f32[20,10]{1,0:T(8,128)S(1)}, f32[20,10]{1,0:T(8,128)}, u32[]{:S(2)}) copy-start(f32[20,10]{1,0:T(8,128)} %constant.53.clone) | copy-start | bytes 2404
  50.6 4.1 %collective-permute-start.9 = (f32[2,20,256]{2,1,0:T(8,128)S(1)}, f32[2,20,256]{2,1,0:T(8,128)S(1)}, u32[]{:S(2)}, u32[]{:S(2)}) collective-permute-start(f32[2,20,256]{2,1,0:T(8,128)S(1)} %get-tuple-element.42), channel_id=1, source_target_pairs={{4,0},{8,4},{12,8},{5,1},{9,5},{13,9},{6,2},{10,6},{14,10},{7,3},{... | collective-permute-start | bytes 122888 | tf_op jit(solution)/shard_map/ppermute | solution.py:30
  53.3 6.2 %collective-permute-start.8 = (f32[3,20,256]{2,1,0:T(8,128)S(1)}, f32[3,20,256]{2,1,0:T(8,128)S(1)}, u32[]{:S(2)}, u32[]{:S(2)}) collective-permute-start(f32[3,20,256]{2,1,0:T(8,128)S(1)} %pad_maximum_fusion.11), channel_id=1, source_target_pairs={{0,4},{4,8},{8,12},{1,5},{5,9},{9,13},{2,6},{6,10},{10,14},{3,7},{... | collective-permute-start | bytes 184328 | tf_op jit(solution)/shard_map/ppermute | solution.py:30

commit v24 on v23

--- a/solution.py
+++ b/solution.py
@@ -295,7 +295,7 @@
     last_fine = jnp.dot(rows_ext, last_z, precision=lax.Precision.HIGH)
     up_block = jnp.concatenate([base[width_x - NU :], last_fine[None]], axis=0)
     below_prev = passed_along(up_block, "slab", 1)
-    above_next = passed_along(base[:NU], "slab", -1)
+    above_next = passed_along(jnp.concatenate([base[:NU], last_fine[None]], axis=0), "slab", -1)[:NU]
     from_owner = (slot_ids == -1).astype(jnp.float32)
     own = base + from_owner[:, None, None] * below_prev[NU][None]
     next_ids = ext_ids[width_x + 1 :]

time: 62.5 us -> 65.1 us (1.042)
  the two profiles are of different devices: /device:TPU:26 before, /device:TPU:1 now
where the time goes in v24:
time: 65.1 us; the launch traced here: 64.6 us
  starting transfers between devices  27.5 us (42%)
  waiting for transfers between devices  16.6 us (25%)
  other arithmetic  9.55 us (15%)
  matrix products  4.22 us (6%)
  local copies, waits for them, and re-layouts  3.41 us (5%)
  between operations  3.32 us (5%)
    ppermute x6, starting transfers between devices, passed_along(): return lax.ppermute(array, axis, pairs)  15.4 us
    ppermute x6, waiting for transfers between devices, passed_along(): return lax.ppermute(array, axis, pairs)  10.6 us
    ppermute x2, starting transfers between devices, padded(): before = lax.ppermute(last, axis, up)  8.91 us
    ppermute x2, waiting for transfers between devices, padded(): after = lax.ppermute(leading, axis, down)  5.89 us
    add x4, other arithmetic, sweeps(): field_ext = center + OMEGA * (source_now - product) / faces_now[7]  3.68 us
    ppermute x2, starting transfers between devices, padded(): after = lax.ppermute(leading, axis, down)  3.21 us
    dot_general x5, matrix products, z_sum(): return jnp.dot(flat, pick_z, precision=lax.Precision.HIGH)  1.47 us
  transfers between devices with their start and end apart: 10, of which 6 were waited for; matrix products, arithmetic and copies ran while one was open for 5% of the time, Pallas kernels for 0%

profile of v24, /device:TPU:1, one launch (start us, length us, event | category | flops | bytes accessed | tf_op | source)
XLA Modules:
  0.0 64.6 jit_solution(17892374636966031260)
XLA Ops:
  0.0 1.0 %pad_maximum_fusion.8 = (f32[3,3,16,256]{3,2,1,0:T(8,128)S(1)}, f32[3,3,16,256]{3,2,1,0:T(8,128)S(1)}) fusion(f32[1,16,16,256]{3,2,1,0:T(8,128)} %bitcast.231, f32[1,16,16,256]{3,2,1,0:T(8,128)} %bitcast.224, f32[1,16,16,256]{3,2,1,0:T(8,128)} %bitcast.233), kind=kLoop, calls=%fused_computation.177 | loop fusion | flops 147456 | bytes 1081344 | tf_op jit(solution)/shard_map/slice | solution.py:19
  1.0 4.0 %collective-permute-start = (f32[3,3,16,256]{3,2,1,0:T(8,128)S(1)}, f32[3,3,16,256]{3,2,1,0:T(8,128)S(1)}, u32[]{:S(2)}, u32[]{:S(2)}) collective-permute-start(f32[3,3,16,256]{3,2,1,0:T(8,128)S(1)} %get-tuple-element.23), channel_id=1, source_target_pairs={{0,4},{4,8},{8,12},{1,5},{5,9},{9,13},{2,6},{6,10},{10,14},{3,7},{... | collective-permute-start | bytes 442376 | tf_op jit(solution)/shard_map/ppermute | solution.py:21
  5.1 1.3 %collective-permute-start.1 = (f32[3,3,16,256]{3,2,1,0:T(8,128)S(1)}, f32[3,3,16,256]{3,2,1,0:T(8,128)S(1)}, u32[]{:S(2)}, u32[]{:S(2)}) collective-permute-start(f32[3,3,16,256]{3,2,1,0:T(8,128)S(1)} %get-tuple-element.24), channel_id=1, source_target_pairs={{4,0},{8,4},{12,8},{5,1},{9,5},{13,9},{6,2},{10,6},{14,10},{7,3},{... | collective-permute-start | bytes 442376 | tf_op jit(solution)/shard_map/ppermute | solution.py:22
  7.4 0.1 collective-permute-done
  7.6 3.8 %collective-permute-done.1 = f32[3,3,16,256]{3,2,1,0:T(8,128)S(1)} collective-permute-done((f32[3,3,16,256]{3,2,1,0:T(8,128)S(1)}, f32[3,3,16,256]{3,2,1,0:T(8,128)S(1)}, u32[]{:S(2)}, u32[]{:S(2)}) %collective-permute-start.1) | collective-permute-done | bytes 147488 | tf_op jit(solution)/shard_map/ppermute | solution.py:22
  11.5 0.1 fusion.145
  11.6 4.9 %collective-permute-start.2 = (f32[3,22,4,256]{3,2,1,0:T(4,128)S(1)}, f32[3,22,4,256]{3,2,1,0:T(4,128)S(1)}, u32[]{:S(2)}, u32[]{:S(2)}) collective-permute-start(f32[3,22,4,256]{3,2,1,0:T(4,128)S(1)} %get-tuple-element.21), channel_id=1, source_target_pairs={{0,1},{1,2},{2,3},{4,5},{5,6},{6,7},{8,9},{9,10},{10,11},{12,13},{... | collective-permute-start | bytes 811016 | tf_op jit(solution)/shard_map/ppermute | solution.py:21
  16.4 1.9 %collective-permute-start.3 = (f32[3,22,4,256]{3,2,1,0:T(4,128)S(1)}, f32[3,22,4,256]{3,2,1,0:T(4,128)S(1)}, u32[]{:S(2)}, u32[]{:S(2)}) collective-permute-start(f32[3,22,4,256]{3,2,1,0:T(4,128)S(1)} %get-tuple-element.22), channel_id=1, source_target_pairs={{1,0},{2,1},{3,2},{5,4},{6,5},{7,6},{9,8},{10,9},{11,10},{13,12},{... | collective-permute-start | bytes 811016 | tf_op jit(solution)/shard_map/ppermute | solution.py:22
  18.4 0.2 select_reduce_fusion
  18.6 0.7 %fusion.157 = (f32[1]{0:T(128)}, f32[1]{0:T(128)}, f32[1]{0:T(128)}) fusion(f32[19]{0:T(128)S(1)} %select_reduce_fusion), kind=kLoop, calls=%fused_computation.296 | loop fusion | bytes 24 | tf_op jit(solution)/shard_map/slice | solution.py:148
  22.1 2.1 %collective-permute-done.3 = f32[3,22,4,256]{3,2,1,0:T(4,128)S(1)} collective-permute-done((f32[3,22,4,256]{3,2,1,0:T(4,128)S(1)}, f32[3,22,4,256]{3,2,1,0:T(4,128)S(1)}, u32[]{:S(2)}, u32[]{:S(2)}) %collective-permute-start.3) | collective-permute-done | bytes 270368 | tf_op jit(solution)/shard_map/ppermute | solution.py:22
  24.2 0.3 pad_maximum_fusion
  24.5 0.1 slice_bitcast_fusion
  24.6 0.2 fusion.147
  24.8 0.2 divide_select_fusion
  25.0 0.2 divide_select_fusion.1
  25.2 0.3 fusion.148
  25.5 1.0 %fusion.15 = (f32[20,22,256]{2,1,0:T(8,128)S(1)}, f32[20,22,256]{2,1,0:T(8,128)S(1)}, f32[20,22,256]{2,1,0:T(8,128)S(1)}) fusion(f32[22,24,256]{2,1,0:T(8,128)S(1)} %get-tuple-element.20, f32[22,24,256]{2,1,0:T(8,128)S(1)} %get-tuple-element.19, f32[20,22,255]{2,1,0:T(8,128)S(1)} %get-tuple-element.30, f32[20,22,255]{2,1,0:T(8,128)S(1)} %get-tuple-element.29, ...), kind=kLoop, calls=%fused_computation.31 | loop fusion | flops 3041280 | bytes 7657464 | tf_op jit(solution)/shard_map/add | solution.py:109
  26.5 0.2 fusion.150
  26.7 0.7 %fusion.38 = f32[18,20,256]{2,1,0:T(8,128)S(1)} fusion(f32[20,22,256]{2,1,0:T(8,128)S(1)} %get-tuple-element.15, f32[22,23,256]{2,1,0:T(8,128)S(1)} %divide_select_fusion, f32[21,24,256]{2,1,0:T(8,128)S(1)} %divide_select_fusion.1, f32[22,24,256]{2,1,0:T(8,128)S(1)} %get-tuple-element.19, f32[18,20,255]{2,1,0:T(8,128)S(1)} %get-tuple-element.36, ...), kind=kLoop, calls=%fused_computation.67 | loop fusion | flops 1566720 | bytes 5606880 | tf_op jit(solution)/shard_map/add | solution.py:109
  27.5 0.1 fusion.152
  27.6 0.5 fusion.146
  28.1 0.4 copy-done
  28.5 0.3 fusion.162
  28.8 0.3 fusion.158
  29.2 0.3 fusion.159
  29.5 0.3 fusion.161
  29.8 0.3 fusion.160
  30.2 0.3 fusion
  30.6 0.2 convolution_bitcast_fusion.2
  31.0 0.2 convolution_bitcast_fusion.1
  31.3 1.3 %collective-permute-start.5 = (f32[5,4,8,128]{3,1,2,0:T(4,128)S(1)}, f32[5,4,8,128]{3,1,2,0:T(4,128)S(1)}, u32[]{:S(2)}, u32[]{:S(2)}) collective-permute-start(f32[5,4,8,128]{3,1,2,0:T(4,128)S(1)} %pad_maximum_fusion.12), channel_id=1, source_target_pairs={{4,0},{8,4},{12,8},{5,1},{9,5},{13,9},{6,2},{10,6},{14,10},{7,3},{... | collective-permute-start | bytes 245768 | tf_op jit(solution)/shard_map/ppermute | solution.py:30
  32.6 4.0 %collective-permute-start.4 = (f32[5,4,8,128]{3,1,2,0:T(4,128)S(1)}, f32[5,4,8,128]{3,1,2,0:T(4,128)S(1)}, u32[]{:S(2)}, u32[]{:S(2)}) collective-permute-start(f32[5,4,8,128]{3,1,2,0:T(4,128)S(1)} %convolution_bitcast_fusion.1), channel_id=1, source_target_pairs={{0,4},{4,8},{8,12},{1,5},{5,9},{9,13},{2,6},{6,10},{10,14},{3,7},{... | collective-permute-start | bytes 245768 | tf_op jit(solution)/shard_map/ppermute | solution.py:30
  36.6 0.1 multiply_add_fusion.1
  36.7 1.3 %collective-permute-done.4 = f32[5,4,8,128]{3,1,2,0:T(4,128)S(1)} collective-permute-done((f32[5,4,8,128]{3,1,2,0:T(4,128)S(1)}, f32[5,4,8,128]{3,1,2,0:T(4,128)S(1)}, u32[]{:S(2)}, u32[]{:S(2)}) %collective-permute-start.4) | collective-permute-done | bytes 81952 | tf_op jit(solution)/shard_map/ppermute | solution.py:30
  38.0 0.1 multiply_add_fusion.2
  38.1 0.4 maximum_add_fusion
  38.6 2.9 %collective-permute-start.6 = (f32[5,24,5,128]{3,1,2,0:T(8,128)S(1)}, f32[5,24,5,128]{3,1,2,0:T(8,128)S(1)}, u32[]{:S(2)}, u32[]{:S(2)}) collective-permute-start(f32[5,24,5,128]{3,1,2,0:T(8,128)S(1)} %slice.838), channel_id=1, source_target_pairs={{0,1},{1,2},{2,3},{4,5},{5,6},{6,7},{8,9},{9,10},{10,11},{12,13},{... | collective-permute-start | bytes 921608 | tf_op jit(solution)/shard_map/ppermute | solution.py:30
  41.5 1.9 %collective-permute-start.7 = (f32[5,24,4,128]{3,1,2,0:T(8,128)S(1)}, f32[5,24,4,128]{3,1,2,0:T(8,128)S(1)}, u32[]{:S(2)}, u32[]{:S(2)}) collective-permute-start(f32[5,24,4,128]{3,1,2,0:T(8,128)S(1)} %slice.839), channel_id=1, source_target_pairs={{1,0},{2,1},{3,2},{5,4},{6,5},{7,6},{9,8},{10,9},{11,10},{13,12},{... | collective-permute-start | bytes 737288 | tf_op jit(solution)/shard_map/ppermute | solution.py:30
  43.5 5.6 %collective-permute-done.7 = f32[5,24,4,128]{3,1,2,0:T(8,128)S(1)} collective-permute-done((f32[5,24,4,128]{3,1,2,0:T(8,128)S(1)}, f32[5,24,4,128]{3,1,2,0:T(8,128)S(1)}, u32[]{:S(2)}, u32[]{:S(2)}) %collective-permute-start.7) | collective-permute-done | bytes 245792 | tf_op jit(solution)/shard_map/ppermute | solution.py:30
  49.2 0.2 fusion.62
  49.4 0.1 fusion.154
  49.6 0.3 fusion.70
  49.9 0.1 fusion.155
  50.0 0.3 fusion.81
  50.3 0.1 fusion.156
  50.4 0.2 multiply_reduce_fusion
  50.6 0.2 fusion.119
  50.8 0.2 fusion.117
  51.0 0.3 fusion.108
  51.3 0.2 fusion.123
  51.5 0.2 fusion.121
  51.7 0.3 fusion.59
  52.1 0.1 fusion.163
  52.2 0.2 fusion.164
  52.4 4.0 %collective-permute-start.8 = (f32[3,20,256]{2,1,0:T(8,128)S(1)}, f32[3,20,256]{2,1,0:T(8,128)S(1)}, u32[]{:S(2)}, u32[]{:S(2)}) collective-permute-start(f32[3,20,256]{2,1,0:T(8,128)S(1)} %get-tuple-element.53), channel_id=1, source_target_pairs={{0,4},{4,8},{8,12},{1,5},{5,9},{9,13},{2,6},{6,10},{10,14},{3,7},{... | collective-permute-start | bytes 184328 | tf_op jit(solution)/shard_map/ppermute | solution.py:30
  56.4 0.6 and_convert_fusion
  57.1 1.3 %collective-permute-start.9 = (f32[3,20,256]{2,1,0:T(8,128)S(1)}, f32[3,20,256]{2,1,0:T(8,128)S(1)}, u32[]{:S(2)}, u32[]{:S(2)}) collective-permute-start(f32[3,20,256]{2,1,0:T(8,128)S(1)} %get-tuple-element.54), channel_id=1, source_target_pairs={{4,0},{8,4},{12,8},{5,1},{9,5},{13,9},{6,2},{10,6},{14,10},{7,3},{... | collective-permute-start | bytes 184328 | tf_op jit(solution)/shard_map/ppermute | solution.py:30
  58.4 0.1 multiply_add_fusion
  58.5 3.7 %collective-permute-done.9 = f32[3,20,256]{2,1,0:T(8,128)S(1)} collective-permute-done((f32[3,20,256]{2,1,0:T(8,128)S(1)}, f32[3,20,256]{2,1,0:T(8,128)S(1)}, u32[]{:S(2)}, u32[]{:S(2)}) %collective-permute-start.9) | collective-permute-done | bytes 61472 | tf_op jit(solution)/shard_map/ppermute | solution.py:30
  62.3 0.2 fusion.149
  62.5 0.8 %fusion.26 = f32[18,18,256]{2,1,0:T(8,128)S(1)} fusion(f32[20,20,256]{2,1,0:T(8,128)S(1)} %pad_maximum_fusion.3, f32[22,23,256]{2,1,0:T(8,128)S(1)} %divide_select_fusion, f32[2,20,256]{2,1,0:T(8,128)S(1)} %slice_add_fusion.4, f32[16,20,256]{2,1,0:T(8,128)S(1)} %multiply_add_fusion, f32[21,24,256]{2,1,0:T(8,128)S(1)} %divide_select_fusion.1, ...), kind=kLoop, calls=%fused_computation.51 | loop fusion | flops 1575936 | bytes 4837120 | tf_op jit(solution)/shard_map/add | solution.py:109
  63.3 0.1 fusion.151
  63.4 1.1 %fusion.49 = f32[16,16,256]{2,1,0:T(8,128)} fusion(f32[18,18,256]{2,1,0:T(8,128)S(1)} %fusion.26, f32[22,24,256]{2,1,0:T(8,128)S(1)} %get-tuple-element.19, f32[16,16,255]{2,1,0:T(8,128)S(1)} %get-tuple-element.38, f32[16,16,255]{2,1,0:T(8,128)S(1)} %get-tuple-element.37, f32[22,23,256]{2,1,0:T(8,128)S(1)} %divide_select_fusion, ...), kind=kLoop, calls=%fused_computation.88 | loop fusion | flops 1114112 | bytes 4116768 | tf_op jit(solution)/shard_map/add | solution.py:109
  (86 shorter events, 2.2 us)
Async XLA Ops:
  0.0 11.4 %copy-start.3 = (f32[16,16,256]{2,1,0:T(8,128)S(1)}, f32[16,16,256]{2,1,0:T(8,128)}, u32[]{:S(2)}) copy-start(f32[16,16,256]{2,1,0:T(8,128)} %param.11) | copy-start | bytes 786436
  0.0 11.4 %copy-start.1 = (f32[16,16,256]{2,1,0:T(8,128)S(1)}, f32[16,16,256]{2,1,0:T(8,128)}, u32[]{:S(2)}) copy-start(f32[16,16,256]{2,1,0:T(8,128)} %param.12) | copy-start | bytes 786436
  0.0 11.4 %copy-start.2 = (f32[16,16,256]{2,1,0:T(8,128)S(1)}, f32[16,16,256]{2,1,0:T(8,128)}, u32[]{:S(2)}) copy-start(f32[16,16,256]{2,1,0:T(8,128)} %param.13) | copy-start | bytes 786436
  1.0 6.5 %collective-permute-start = (f32[3,3,16,256]{3,2,1,0:T(8,128)S(1)}, f32[3,3,16,256]{3,2,1,0:T(8,128)S(1)}, u32[]{:S(2)}, u32[]{:S(2)}) collective-permute-start(f32[3,3,16,256]{3,2,1,0:T(8,128)S(1)} %get-tuple-element.23), channel_id=1, source_target_pairs={{0,4},{4,8},{8,12},{1,5},{5,9},{9,13},{2,6},{6,10},{10,14},{3,7},{... | collective-permute-start | bytes 442376 | tf_op jit(solution)/shard_map/ppermute | solution.py:21
  5.1 6.3 %collective-permute-start.1 = (f32[3,3,16,256]{3,2,1,0:T(8,128)S(1)}, f32[3,3,16,256]{3,2,1,0:T(8,128)S(1)}, u32[]{:S(2)}, u32[]{:S(2)}) collective-permute-start(f32[3,3,16,256]{3,2,1,0:T(8,128)S(1)} %get-tuple-element.24), channel_id=1, source_target_pairs={{4,0},{8,4},{12,8},{5,1},{9,5},{13,9},{6,2},{10,6},{14,10},{7,3},{... | collective-permute-start | bytes 442376 | tf_op jit(solution)/shard_map/ppermute | solution.py:22
  11.5 6.9 %copy-start.9 = (s32[64]{0:T(128)S(1)}, s32[64]{0:T(128)}, u32[]{:S(2)}) copy-start(s32[64]{0:T(128)} %param.14) | copy-start | bytes 772
  11.6 10.6 %collective-permute-start.2 = (f32[3,22,4,256]{3,2,1,0:T(4,128)S(1)}, f32[3,22,4,256]{3,2,1,0:T(4,128)S(1)}, u32[]{:S(2)}, u32[]{:S(2)}) collective-permute-start(f32[3,22,4,256]{3,2,1,0:T(4,128)S(1)} %get-tuple-element.21), channel_id=1, source_target_pairs={{0,1},{1,2},{2,3},{4,5},{5,6},{6,7},{8,9},{9,10},{10,11},{12,13},{... | collective-permute-start | bytes 811016 | tf_op jit(solution)/shard_map/ppermute | solution.py:21
  16.4 7.8 %collective-permute-start.3 = (f32[3,22,4,256]{3,2,1,0:T(4,128)S(1)}, f32[3,22,4,256]{3,2,1,0:T(4,128)S(1)}, u32[]{:S(2)}, u32[]{:S(2)}) collective-permute-start(f32[3,22,4,256]{3,2,1,0:T(4,128)S(1)} %get-tuple-element.22), channel_id=1, source_target_pairs={{1,0},{2,1},{3,2},{5,4},{6,5},{7,6},{9,8},{10,9},{11,10},{13,12},{... | collective-permute-start | bytes 811016 | tf_op jit(solution)/shard_map/ppermute | solution.py:22
  27.6 0.9 %copy-start = (f32[256,128]{1,0:T(8,128)S(1)}, f32[256,128]{1,0:T(8,128)}, u32[]{:S(2)}) copy-start(f32[256,128]{1,0:T(8,128)} %constant.47.clone) | copy-start | bytes 393220
  28.8 1.0 %copy-start.4 = (f32[256,128]{1,0:T(8,128)S(1)}, f32[256,128]{1,0:T(8,128)}, u32[]{:S(2)}) copy-start(f32[256,128]{1,0:T(8,128)} %constant.48.clone) | copy-start | bytes 393220
  29.1 1.0 %copy-start.8 = (f32[136]{0:T(256)S(1)}, f32[136]{0:T(256)}, u32[]{:S(2)}) copy-start(f32[136]{0:T(256)} %constant.49.clone) | copy-start | bytes 1636
  29.1 1.0 %copy-start.10 = (pred[136,256]{1,0:T(8,128)(4,1)S(1)}, pred[136,256]{1,0:T(8,128)(4,1)}, u32[]{:S(2)}) copy-start(pred[136,256]{1,0:T(8,128)(4,1)} %constant.51.clone) | copy-start | bytes 104452
  29.8 0.8 %copy-start.6 = (pred[136,256]{1,0:T(8,128)(4,1)S(1)}, pred[136,256]{1,0:T(8,128)(4,1)}, u32[]{:S(2)}) copy-start(pred[136,256]{1,0:T(8,128)(4,1)} %constant.52.clone) | copy-start | bytes 104452
  31.3 5.3 %collective-permute-start.5 = (f32[5,4,8,128]{3,1,2,0:T(4,128)S(1)}, f32[5,4,8,128]{3,1,2,0:T(4,128)S(1)}, u32[]{:S(2)}, u32[]{:S(2)}) collective-permute-start(f32[5,4,8,128]{3,1,2,0:T(4,128)S(1)} %pad_maximum_fusion.12), channel_id=1, source_target_pairs={{4,0},{8,4},{12,8},{5,1},{9,5},{13,9},{6,2},{10,6},{14,10},{7,3},{... | collective-permute-start | bytes 245768 | tf_op jit(solution)/shard_map/ppermute | solution.py:30
  32.6 5.5 %collective-permute-start.4 = (f32[5,4,8,128]{3,1,2,0:T(4,128)S(1)}, f32[5,4,8,128]{3,1,2,0:T(4,128)S(1)}, u32[]{:S(2)}, u32[]{:S(2)}) collective-permute-start(f32[5,4,8,128]{3,1,2,0:T(4,128)S(1)} %convolution_bitcast_fusion.1), channel_id=1, source_target_pairs={{0,4},{4,8},{8,12},{1,5},{5,9},{9,13},{2,6},{6,10},{10,14},{3,7},{... | collective-permute-start | bytes 245768 | tf_op jit(solution)/shard_map/ppermute | solution.py:30
  38.6 10.4 %collective-permute-start.6 = (f32[5,24,5,128]{3,1,2,0:T(8,128)S(1)}, f32[5,24,5,128]{3,1,2,0:T(8,128)S(1)}, u32[]{:S(2)}, u32[]{:S(2)}) collective-permute-start(f32[5,24,5,128]{3,1,2,0:T(8,128)S(1)} %slice.838), channel_id=1, source_target_pairs={{0,1},{1,2},{2,3},{4,5},{5,6},{6,7},{8,9},{9,10},{10,11},{12,13},{... | collective-permute-start | bytes 921608 | tf_op jit(solution)/shard_map/ppermute | solution.py:30
  41.5 7.5 %collective-permute-start.7 = (f32[5,24,4,128]{3,1,2,0:T(8,128)S(1)}, f32[5,24,4,128]{3,1,2,0:T(8,128)S(1)}, u32[]{:S(2)}, u32[]{:S(2)}) collective-permute-start(f32[5,24,4,128]{3,1,2,0:T(8,128)S(1)} %slice.839), channel_id=1, source_target_pairs={{1,0},{2,1},{3,2},{5,4},{6,5},{7,6},{9,8},{10,9},{11,10},{13,12},{... | collective-permute-start | bytes 737288 | tf_op jit(solution)/shard_map/ppermute | solution.py:30
  50.4 1.3 %copy-start.5 = (pred[256,136]{1,0:T(32,128)(4,1)S(1)}, pred[256,136]{1,0:T(32,128)(4,1)}, u32[]{:S(2)}) copy-start(pred[256,136]{1,0:T(32,128)(4,1)} %constant.50.clone) | copy-start | bytes 104452
  51.3 1.0 %copy-start.7 = (f32[20,10]{1,0:T(8,128)S(1)}, f32[20,10]{1,0:T(8,128)}, u32[]{:S(2)}) copy-start(f32[20,10]{1,0:T(8,128)} %constant.53.clone) | copy-start | bytes 2404
  52.4 5.9 %collective-permute-start.8 = (f32[3,20,256]{2,1,0:T(8,128)S(1)}, f32[3,20,256]{2,1,0:T(8,128)S(1)}, u32[]{:S(2)}, u32[]{:S(2)}) collective-permute-start(f32[3,20,256]{2,1,0:T(8,128)S(1)} %get-tuple-element.53), channel_id=1, source_target_pairs={{0,4},{4,8},{8,12},{1,5},{5,9},{9,13},{2,6},{6,10},{10,14},{3,7},{... | collective-permute-start | bytes 184328 | tf_op jit(solution)/shard_map/ppermute | solution.py:30
  57.1 5.1 %collective-permute-start.9 = (f32[3,20,256]{2,1,0:T(8,128)S(1)}, f32[3,20,256]{2,1,0:T(8,128)S(1)}, u32[]{:S(2)}, u32[]{:S(2)}) collective-permute-start(f32[3,20,256]{2,1,0:T(8,128)S(1)} %get-tuple-element.54), channel_id=1, source_target_pairs={{4,0},{8,4},{12,8},{5,1},{9,5},{13,9},{6,2},{10,6},{14,10},{7,3},{... | collective-permute-start | bytes 184328 | tf_op jit(solution)/shard_map/ppermute | solution.py:30

commit v25 on v23

--- a/solution.py
+++ b/solution.py
@@ -123,7 +123,6 @@
     fine_rim = 2 * NU
     rim_x = NU + 1
     ext_x = padded(jnp.stack([permeability, source, pressure]), (("slab", 1),), rim_x)
-    ext_x, aggregate = lax.optimization_barrier((ext_x, aggregate))
     ext_all = padded(ext_x, ((("pencil", "sub"), 2),), fine_rim)
     perm_ext = ext_all[0]
     source_ext = crop(ext_all[1], 1)

time: 62.5 us -> 63.8 us (1.021)
  the two profiles are of different devices: /device:TPU:26 before, /device:TPU:18 now
where the time goes in v25:
time: 63.8 us; the launch traced here: 63.4 us
  starting transfers between devices  26.2 us (41%)
  waiting for transfers between devices  15.4 us (24%)
  other arithmetic  11.5 us (18%)
  matrix products  4.21 us (7%)
  between operations  3.23 us (5%)
  local copies, waits for them, and re-layouts  2.84 us (4%)
    ppermute x6, starting transfers between devices, passed_along(): return lax.ppermute(array, axis, pairs)  16 us
    ppermute x6, waiting for transfers between devices, passed_along(): return lax.ppermute(array, axis, pairs)  10.4 us
    ppermute x2, starting transfers between devices, padded(): before = lax.ppermute(last, axis, up)  5.91 us
    ppermute x2, starting transfers between devices, padded(): after = lax.ppermute(leading, axis, down)  4.28 us
    ppermute x2, waiting for transfers between devices, padded(): before = lax.ppermute(last, axis, up)  3.82 us
    add x4, other arithmetic, sweeps(): field_ext = center + OMEGA * (source_now - product) / faces_now[7]  3.67 us
    slice x2, other arithmetic, padded(): last = lax.slice_in_dim(array, length - width, length, axis=dim)  2.31 us
    dot_general x5, matrix products, z_sum(): return jnp.dot(flat, pick_z, precision=lax.Precision.HIGH)  1.46 us
  transfers between devices with their start and end apart: 10, of which 7 were waited for; matrix products, arithmetic and copies ran while one was open for 6% of the time, Pallas kernels for 0%

profile of v25, /device:TPU:18, one launch (start us, length us, event | category | flops | bytes accessed | tf_op | source)
XLA Modules:
  0.0 63.4 jit_solution(1527962066039400284)
XLA Ops:
  0.0 1.0 %pad_maximum_fusion.12 = (f32[3,3,16,256]{3,2,1,0:T(8,128)S(1)}, f32[3,3,16,256]{3,2,1,0:T(8,128)S(1)}) fusion(f32[1,16,16,256]{3,2,1,0:T(8,128)} %bitcast.227, f32[1,16,16,256]{3,2,1,0:T(8,128)} %bitcast.224, f32[1,16,16,256]{3,2,1,0:T(8,128)} %bitcast.230), kind=kLoop, calls=%fused_computation.181 | loop fusion | flops 147456 | bytes 1081344 | tf_op jit(solution)/shard_map/slice | solution.py:19
  1.0 2.4 %collective-permute-start.1 = (f32[3,3,16,256]{3,2,1,0:T(8,128)S(1)}, f32[3,3,16,256]{3,2,1,0:T(8,128)S(1)}, u32[]{:S(2)}, u32[]{:S(2)}) collective-permute-start(f32[3,3,16,256]{3,2,1,0:T(8,128)S(1)} %get-tuple-element.20), channel_id=1, source_target_pairs={{4,0},{8,4},{12,8},{5,1},{9,5},{13,9},{6,2},{10,6},{14,10},{7,3},{... | collective-permute-start | bytes 442376 | tf_op jit(solution)/shard_map/ppermute | solution.py:22
  3.4 3.5 %collective-permute-start = (f32[3,3,16,256]{3,2,1,0:T(8,128)S(1)}, f32[3,3,16,256]{3,2,1,0:T(8,128)S(1)}, u32[]{:S(2)}, u32[]{:S(2)}) collective-permute-start(f32[3,3,16,256]{3,2,1,0:T(8,128)S(1)} %get-tuple-element.19), channel_id=1, source_target_pairs={{0,4},{4,8},{8,12},{1,5},{5,9},{9,13},{2,6},{6,10},{10,14},{3,7},{... | collective-permute-start | bytes 442376 | tf_op jit(solution)/shard_map/ppermute | solution.py:21
  7.3 0.7 %convert_element_type.122 = f32[64]{0:T(128)S(1)} convert(s32[64]{0:T(128)} %param.14) | non-fusion elementwise | flops 64 | bytes 512 | tf_op jit(solution)/shard_map/convert_element_type | solution.py:145
  8.0 0.2 select_reduce_fusion
  8.2 0.7 %fusion.156 = (f32[1]{0:T(128)}, f32[1]{0:T(128)}, f32[1]{0:T(128)}) fusion(f32[19]{0:T(128)S(1)} %select_reduce_fusion), kind=kLoop, calls=%fused_computation.298 | loop fusion | bytes 24 | tf_op jit(solution)/shard_map/slice | solution.py:147
  11.9 1.3 %pad_maximum_fusion.9 = (f32[3,22,4,256]{3,2,1,0:T(4,128)S(1)}, f32[3,22,4,256]{3,2,1,0:T(4,128)S(1)}) fusion(f32[3,3,16,256]{3,2,1,0:T(8,128)S(1)} %collective-permute-done.1, f32[3,3,16,256]{3,2,1,0:T(8,128)S(1)} %collective-permute-done, f32[1,16,16,256]{3,2,1,0:T(8,128)} %bitcast.228, f32[1,16,16,256]{3,2,1,0:T(8,128)} %bitcast.225, ...), kind=kLoop, calls=%fused_computation.83 | loop fusion | flops 540672 | bytes 1622016 | tf_op jit(solution)/shard_map/slice | solution.py:19
  13.2 1.9 %collective-permute-start.3 = (f32[3,22,4,256]{3,2,1,0:T(4,128)S(1)}, f32[3,22,4,256]{3,2,1,0:T(4,128)S(1)}, u32[]{:S(2)}, u32[]{:S(2)}) collective-permute-start(f32[3,22,4,256]{3,2,1,0:T(4,128)S(1)} %get-tuple-element.18), channel_id=1, source_target_pairs={{1,0},{2,1},{3,2},{5,4},{6,5},{7,6},{9,8},{10,9},{11,10},{13,12},{... | collective-permute-start | bytes 811016 | tf_op jit(solution)/shard_map/ppermute | solution.py:22
  15.1 2.4 %collective-permute-start.2 = (f32[3,22,4,256]{3,2,1,0:T(4,128)S(1)}, f32[3,22,4,256]{3,2,1,0:T(4,128)S(1)}, u32[]{:S(2)}, u32[]{:S(2)}) collective-permute-start(f32[3,22,4,256]{3,2,1,0:T(4,128)S(1)} %get-tuple-element.17), channel_id=1, source_target_pairs={{0,1},{1,2},{2,3},{4,5},{5,6},{6,7},{8,9},{9,10},{10,11},{12,13},{... | collective-permute-start | bytes 811016 | tf_op jit(solution)/shard_map/ppermute | solution.py:21
  18.0 1.1 %collective-permute-done.3 = f32[3,22,4,256]{3,2,1,0:T(4,128)S(1)} collective-permute-done((f32[3,22,4,256]{3,2,1,0:T(4,128)S(1)}, f32[3,22,4,256]{3,2,1,0:T(4,128)S(1)}, u32[]{:S(2)}, u32[]{:S(2)}) %collective-permute-start.3) | collective-permute-done | bytes 270368 | tf_op jit(solution)/shard_map/ppermute | solution.py:22
  19.1 3.8 %collective-permute-done.2 = f32[3,22,4,256]{3,2,1,0:T(4,128)S(1)} collective-permute-done((f32[3,22,4,256]{3,2,1,0:T(4,128)S(1)}, f32[3,22,4,256]{3,2,1,0:T(4,128)S(1)}, u32[]{:S(2)}, u32[]{:S(2)}) %collective-permute-start.2) | collective-permute-done | bytes 270368 | tf_op jit(solution)/shard_map/ppermute | solution.py:21
  22.9 0.3 pad_maximum_fusion
  23.2 0.1 slice_bitcast_fusion
  23.3 0.2 fusion.146
  23.5 0.2 divide_select_fusion
  23.7 0.2 divide_select_fusion.1
  23.9 0.3 fusion.147
  24.2 1.0 %fusion.15 = (f32[20,22,256]{2,1,0:T(8,128)S(1)}, f32[20,22,256]{2,1,0:T(8,128)S(1)}, f32[20,22,256]{2,1,0:T(8,128)S(1)}) fusion(f32[22,24,256]{2,1,0:T(8,128)S(1)} %get-tuple-element.16, f32[22,24,256]{2,1,0:T(8,128)S(1)} %get-tuple-element.15, f32[20,22,255]{2,1,0:T(8,128)S(1)} %get-tuple-element.26, f32[20,22,255]{2,1,0:T(8,128)S(1)} %get-tuple-element.25, ...), kind=kLoop, calls=%fused_computation.30 | loop fusion | flops 3041280 | bytes 7657464 | tf_op jit(solution)/shard_map/add | solution.py:109
  25.2 0.2 fusion.149
  25.4 0.7 %fusion.38 = f32[18,20,256]{2,1,0:T(8,128)S(1)} fusion(f32[20,22,256]{2,1,0:T(8,128)S(1)} %get-tuple-element.11, f32[22,23,256]{2,1,0:T(8,128)S(1)} %divide_select_fusion, f32[21,24,256]{2,1,0:T(8,128)S(1)} %divide_select_fusion.1, f32[22,24,256]{2,1,0:T(8,128)S(1)} %get-tuple-element.15, f32[18,20,255]{2,1,0:T(8,128)S(1)} %get-tuple-element.32, ...), kind=kLoop, calls=%fused_computation.66 | loop fusion | flops 1566720 | bytes 5606880 | tf_op jit(solution)/shard_map/add | solution.py:109
  26.2 0.1 fusion.151
  26.4 0.3 fusion.160
  26.7 0.5 fusion.145
  27.2 0.3 fusion.158
  27.5 0.3 fusion.157
  27.8 0.3 fusion.159
  28.1 0.3 fusion
  28.5 0.3 fusion.161
  28.8 0.2 convolution_bitcast_fusion.2
  29.2 0.2 convolution_bitcast_fusion.1
  29.5 2.4 %collective-permute-start.5 = (f32[5,4,8,128]{3,1,2,0:T(4,128)S(1)}, f32[5,4,8,128]{3,1,2,0:T(4,128)S(1)}, u32[]{:S(2)}, u32[]{:S(2)}) collective-permute-start(f32[5,4,8,128]{3,1,2,0:T(4,128)S(1)} %pad_maximum_fusion.14), channel_id=1, source_target_pairs={{4,0},{8,4},{12,8},{5,1},{9,5},{13,9},{6,2},{10,6},{14,10},{7,3},{... | collective-permute-start | bytes 245768 | tf_op jit(solution)/shard_map/ppermute | solution.py:30
  31.9 3.5 %collective-permute-start.4 = (f32[5,4,8,128]{3,1,2,0:T(4,128)S(1)}, f32[5,4,8,128]{3,1,2,0:T(4,128)S(1)}, u32[]{:S(2)}, u32[]{:S(2)}) collective-permute-start(f32[5,4,8,128]{3,1,2,0:T(4,128)S(1)} %convolution_bitcast_fusion.1), channel_id=1, source_target_pairs={{0,4},{4,8},{8,12},{1,5},{5,9},{9,13},{2,6},{6,10},{10,14},{3,7},{... | collective-permute-start | bytes 245768 | tf_op jit(solution)/shard_map/ppermute | solution.py:30
  35.4 0.5 collective-permute-done.5
  35.9 0.1 multiply_add_fusion.1
  36.0 2.2 %collective-permute-done.4 = f32[5,4,8,128]{3,1,2,0:T(4,128)S(1)} collective-permute-done((f32[5,4,8,128]{3,1,2,0:T(4,128)S(1)}, f32[5,4,8,128]{3,1,2,0:T(4,128)S(1)}, u32[]{:S(2)}, u32[]{:S(2)}) %collective-permute-start.4) | collective-permute-done | bytes 81952 | tf_op jit(solution)/shard_map/ppermute | solution.py:30
  38.3 0.4 maximum_add_fusion
  38.8 1.9 %collective-permute-start.7 = (f32[5,24,4,128]{3,1,2,0:T(8,128)S(1)}, f32[5,24,4,128]{3,1,2,0:T(8,128)S(1)}, u32[]{:S(2)}, u32[]{:S(2)}) collective-permute-start(f32[5,24,4,128]{3,1,2,0:T(8,128)S(1)} %slice.835), channel_id=1, source_target_pairs={{1,0},{2,1},{3,2},{5,4},{6,5},{7,6},{9,8},{10,9},{11,10},{13,12},{... | collective-permute-start | bytes 737288 | tf_op jit(solution)/shard_map/ppermute | solution.py:30
  40.7 2.4 %collective-permute-start.6 = (f32[5,24,5,128]{3,1,2,0:T(8,128)S(1)}, f32[5,24,5,128]{3,1,2,0:T(8,128)S(1)}, u32[]{:S(2)}, u32[]{:S(2)}) collective-permute-start(f32[5,24,5,128]{3,1,2,0:T(8,128)S(1)} %slice.834), channel_id=1, source_target_pairs={{0,1},{1,2},{2,3},{4,5},{5,6},{6,7},{8,9},{9,10},{10,11},{12,13},{... | collective-permute-start | bytes 921608 | tf_op jit(solution)/shard_map/ppermute | solution.py:30
  43.2 0.7 %and_convert_fusion = f32[2]{0:T(128)S(1)} fusion(s32[19]{0:T(128)S(1)} %iota_add_fusion, f32[19]{0:T(128)S(1)} %select_reduce_fusion, f32[]{:T(128)} %bitcast.21), kind=kLoop, calls=%fused_computation.251 | loop fusion | flops 8 | bytes 28 | tf_op jit(solution)/shard_map/convert_element_type | solution.py:302
  43.9 0.5 collective-permute-done.7
  44.4 4.5 %collective-permute-done.6 = f32[5,24,5,128]{3,1,2,0:T(8,128)S(1)} collective-permute-done((f32[5,24,5,128]{3,1,2,0:T(8,128)S(1)}, f32[5,24,5,128]{3,1,2,0:T(8,128)S(1)}, u32[]{:S(2)}, u32[]{:S(2)}) %collective-permute-start.6) | collective-permute-done | bytes 307232 | tf_op jit(solution)/shard_map/ppermute | solution.py:30
  49.1 0.2 fusion.62
  49.3 0.1 fusion.153
  49.4 0.3 fusion.70
  49.7 0.1 fusion.154
  49.9 0.3 fusion.81
  50.2 0.1 fusion.155
  50.3 0.2 multiply_reduce_fusion
  50.5 0.2 fusion.117
  50.7 0.2 fusion.119
  50.9 0.3 fusion.108
  51.1 0.2 fusion.121
  51.3 0.2 fusion.123
  51.5 0.3 fusion.59
  51.9 2.4 %collective-permute-start.9 = (f32[2,20,256]{2,1,0:T(8,128)S(1)}, f32[2,20,256]{2,1,0:T(8,128)S(1)}, u32[]{:S(2)}, u32[]{:S(2)}) collective-permute-start(f32[2,20,256]{2,1,0:T(8,128)S(1)} %get-tuple-element.38), channel_id=1, source_target_pairs={{4,0},{8,4},{12,8},{5,1},{9,5},{13,9},{6,2},{10,6},{14,10},{7,3},{... | collective-permute-start | bytes 122888 | tf_op jit(solution)/shard_map/ppermute | solution.py:30
  54.3 0.1 fusion.162
  54.5 0.2 fusion.163
  54.6 3.5 %collective-permute-start.8 = (f32[3,20,256]{2,1,0:T(8,128)S(1)}, f32[3,20,256]{2,1,0:T(8,128)S(1)}, u32[]{:S(2)}, u32[]{:S(2)}) collective-permute-start(f32[3,20,256]{2,1,0:T(8,128)S(1)} %pad_maximum_fusion.15), channel_id=1, source_target_pairs={{0,4},{4,8},{8,12},{1,5},{5,9},{9,13},{2,6},{6,10},{10,14},{3,7},{... | collective-permute-start | bytes 184328 | tf_op jit(solution)/shard_map/ppermute | solution.py:30
  58.2 2.7 %collective-permute-done.8 = f32[3,20,256]{2,1,0:T(8,128)S(1)} collective-permute-done((f32[3,20,256]{2,1,0:T(8,128)S(1)}, f32[3,20,256]{2,1,0:T(8,128)S(1)}, u32[]{:S(2)}, u32[]{:S(2)}) %collective-permute-start.8) | collective-permute-done | bytes 61472 | tf_op jit(solution)/shard_map/ppermute | solution.py:30
  60.9 0.1 multiply_add_fusion
  61.1 0.2 fusion.148
  61.3 0.8 %fusion.26 = f32[18,18,256]{2,1,0:T(8,128)S(1)} fusion(f32[20,20,256]{2,1,0:T(8,128)S(1)} %pad_maximum_fusion.2, f32[22,23,256]{2,1,0:T(8,128)S(1)} %divide_select_fusion, f32[2,20,256]{2,1,0:T(8,128)S(1)} %multiply_add_fusion.3, f32[16,20,256]{2,1,0:T(8,128)S(1)} %multiply_add_fusion, f32[21,24,256]{2,1,0:T(8,128)S(1)} %divide_select_fusion.1, ...), kind=kLoop, calls=%fused_computation.50 | loop fusion | flops 1575936 | bytes 4837120 | tf_op jit(solution)/shard_map/add | solution.py:109
  62.1 0.1 fusion.150
  62.2 1.1 %fusion.49 = f32[16,16,256]{2,1,0:T(8,128)} fusion(f32[18,18,256]{2,1,0:T(8,128)S(1)} %fusion.26, f32[22,24,256]{2,1,0:T(8,128)S(1)} %get-tuple-element.15, f32[16,16,255]{2,1,0:T(8,128)S(1)} %get-tuple-element.34, f32[16,16,255]{2,1,0:T(8,128)S(1)} %get-tuple-element.33, f32[22,23,256]{2,1,0:T(8,128)S(1)} %divide_select_fusion, ...), kind=kLoop, calls=%fused_computation.92 | loop fusion | flops 1114112 | bytes 4116768 | tf_op jit(solution)/shard_map/add | solution.py:109
  (83 shorter events, 2.2 us)
Async XLA Ops:
  0.0 22.9 %copy-start.2 = (f32[16,16,256]{2,1,0:T(8,128)S(1)}, f32[16,16,256]{2,1,0:T(8,128)}, u32[]{:S(2)}) copy-start(f32[16,16,256]{2,1,0:T(8,128)} %param.13) | copy-start | bytes 786436
  0.0 22.9 %copy-start.1 = (f32[16,16,256]{2,1,0:T(8,128)S(1)}, f32[16,16,256]{2,1,0:T(8,128)}, u32[]{:S(2)}) copy-start(f32[16,16,256]{2,1,0:T(8,128)} %param.12) | copy-start | bytes 786436
  0.0 22.9 %copy-start.3 = (f32[16,16,256]{2,1,0:T(8,128)S(1)}, f32[16,16,256]{2,1,0:T(8,128)}, u32[]{:S(2)}) copy-start(f32[16,16,256]{2,1,0:T(8,128)} %param.11) | copy-start | bytes 786436
  1.0 10.9 %collective-permute-start.1 = (f32[3,3,16,256]{3,2,1,0:T(8,128)S(1)}, f32[3,3,16,256]{3,2,1,0:T(8,128)S(1)}, u32[]{:S(2)}, u32[]{:S(2)}) collective-permute-start(f32[3,3,16,256]{3,2,1,0:T(8,128)S(1)} %get-tuple-element.20), channel_id=1, source_target_pairs={{4,0},{8,4},{12,8},{5,1},{9,5},{13,9},{6,2},{10,6},{14,10},{7,3},{... | collective-permute-start | bytes 442376 | tf_op jit(solution)/shard_map/ppermute | solution.py:22
  3.4 8.5 %collective-permute-start = (f32[3,3,16,256]{3,2,1,0:T(8,128)S(1)}, f32[3,3,16,256]{3,2,1,0:T(8,128)S(1)}, u32[]{:S(2)}, u32[]{:S(2)}) collective-permute-start(f32[3,3,16,256]{3,2,1,0:T(8,128)S(1)} %get-tuple-element.19), channel_id=1, source_target_pairs={{0,4},{4,8},{8,12},{1,5},{5,9},{9,13},{2,6},{6,10},{10,14},{3,7},{... | collective-permute-start | bytes 442376 | tf_op jit(solution)/shard_map/ppermute | solution.py:21
  13.2 5.9 %collective-permute-start.3 = (f32[3,22,4,256]{3,2,1,0:T(4,128)S(1)}, f32[3,22,4,256]{3,2,1,0:T(4,128)S(1)}, u32[]{:S(2)}, u32[]{:S(2)}) collective-permute-start(f32[3,22,4,256]{3,2,1,0:T(4,128)S(1)} %get-tuple-element.18), channel_id=1, source_target_pairs={{1,0},{2,1},{3,2},{5,4},{6,5},{7,6},{9,8},{10,9},{11,10},{13,12},{... | collective-permute-start | bytes 811016 | tf_op jit(solution)/shard_map/ppermute | solution.py:22
  15.1 7.8 %collective-permute-start.2 = (f32[3,22,4,256]{3,2,1,0:T(4,128)S(1)}, f32[3,22,4,256]{3,2,1,0:T(4,128)S(1)}, u32[]{:S(2)}, u32[]{:S(2)}) collective-permute-start(f32[3,22,4,256]{3,2,1,0:T(4,128)S(1)} %get-tuple-element.17), channel_id=1, source_target_pairs={{0,1},{1,2},{2,3},{4,5},{5,6},{6,7},{8,9},{9,10},{10,11},{12,13},{... | collective-permute-start | bytes 811016 | tf_op jit(solution)/shard_map/ppermute | solution.py:21
  25.4 0.9 %copy-start = (f32[256,128]{1,0:T(8,128)S(1)}, f32[256,128]{1,0:T(8,128)}, u32[]{:S(2)}) copy-start(f32[256,128]{1,0:T(8,128)} %constant.47.clone) | copy-start | bytes 393220
  26.7 1.1 %copy-start.4 = (f32[256,128]{1,0:T(8,128)S(1)}, f32[256,128]{1,0:T(8,128)}, u32[]{:S(2)}) copy-start(f32[256,128]{1,0:T(8,128)} %constant.48.clone) | copy-start | bytes 393220
  26.7 1.4 %copy-start.8 = (f32[136]{0:T(256)S(1)}, f32[136]{0:T(256)}, u32[]{:S(2)}) copy-start(f32[136]{0:T(256)} %constant.49.clone) | copy-start | bytes 1636
  26.7 1.4 %copy-start.9 = (pred[136,256]{1,0:T(8,128)(4,1)S(1)}, pred[136,256]{1,0:T(8,128)(4,1)}, u32[]{:S(2)}) copy-start(pred[136,256]{1,0:T(8,128)(4,1)} %constant.51.clone) | copy-start | bytes 104452
  27.8 1.0 %copy-start.6 = (pred[136,256]{1,0:T(8,128)(4,1)S(1)}, pred[136,256]{1,0:T(8,128)(4,1)}, u32[]{:S(2)}) copy-start(pred[136,256]{1,0:T(8,128)(4,1)} %constant.52.clone) | copy-start | bytes 104452
  29.5 6.3 %collective-permute-start.5 = (f32[5,4,8,128]{3,1,2,0:T(4,128)S(1)}, f32[5,4,8,128]{3,1,2,0:T(4,128)S(1)}, u32[]{:S(2)}, u32[]{:S(2)}) collective-permute-start(f32[5,4,8,128]{3,1,2,0:T(4,128)S(1)} %pad_maximum_fusion.14), channel_id=1, source_target_pairs={{4,0},{8,4},{12,8},{5,1},{9,5},{13,9},{6,2},{10,6},{14,10},{7,3},{... | collective-permute-start | bytes 245768 | tf_op jit(solution)/shard_map/ppermute | solution.py:30
  31.9 6.3 %collective-permute-start.4 = (f32[5,4,8,128]{3,1,2,0:T(4,128)S(1)}, f32[5,4,8,128]{3,1,2,0:T(4,128)S(1)}, u32[]{:S(2)}, u32[]{:S(2)}) collective-permute-start(f32[5,4,8,128]{3,1,2,0:T(4,128)S(1)} %convolution_bitcast_fusion.1), channel_id=1, source_target_pairs={{0,4},{4,8},{8,12},{1,5},{5,9},{9,13},{2,6},{6,10},{10,14},{3,7},{... | collective-permute-start | bytes 245768 | tf_op jit(solution)/shard_map/ppermute | solution.py:30
  38.8 5.6 %collective-permute-start.7 = (f32[5,24,4,128]{3,1,2,0:T(8,128)S(1)}, f32[5,24,4,128]{3,1,2,0:T(8,128)S(1)}, u32[]{:S(2)}, u32[]{:S(2)}) collective-permute-start(f32[5,24,4,128]{3,1,2,0:T(8,128)S(1)} %slice.835), channel_id=1, source_target_pairs={{1,0},{2,1},{3,2},{5,4},{6,5},{7,6},{9,8},{10,9},{11,10},{13,12},{... | collective-permute-start | bytes 737288 | tf_op jit(solution)/shard_map/ppermute | solution.py:30
  40.7 8.2 %collective-permute-start.6 = (f32[5,24,5,128]{3,1,2,0:T(8,128)S(1)}, f32[5,24,5,128]{3,1,2,0:T(8,128)S(1)}, u32[]{:S(2)}, u32[]{:S(2)}) collective-permute-start(f32[5,24,5,128]{3,1,2,0:T(8,128)S(1)} %slice.834), channel_id=1, source_target_pairs={{0,1},{1,2},{2,3},{4,5},{5,6},{6,7},{8,9},{9,10},{10,11},{12,13},{... | collective-permute-start | bytes 921608 | tf_op jit(solution)/shard_map/ppermute | solution.py:30
  50.2 1.3 %copy-start.5 = (pred[256,136]{1,0:T(32,128)(4,1)S(1)}, pred[256,136]{1,0:T(32,128)(4,1)}, u32[]{:S(2)}) copy-start(pred[256,136]{1,0:T(32,128)(4,1)} %constant.50.clone) | copy-start | bytes 104452
  50.5 4.0 %copy-start.7 = (f32[20,10]{1,0:T(8,128)S(1)}, f32[20,10]{1,0:T(8,128)}, u32[]{:S(2)}) copy-start(f32[20,10]{1,0:T(8,128)} %constant.53.clone) | copy-start | bytes 2404
  51.9 6.2 %collective-permute-start.9 = (f32[2,20,256]{2,1,0:T(8,128)S(1)}, f32[2,20,256]{2,1,0:T(8,128)S(1)}, u32[]{:S(2)}, u32[]{:S(2)}) collective-permute-start(f32[2,20,256]{2,1,0:T(8,128)S(1)} %get-tuple-element.38), channel_id=1, source_target_pairs={{4,0},{8,4},{12,8},{5,1},{9,5},{13,9},{6,2},{10,6},{14,10},{7,3},{... | collective-permute-start | bytes 122888 | tf_op jit(solution)/shard_map/ppermute | solution.py:30
  54.6 6.2 %collective-permute-start.8 = (f32[3,20,256]{2,1,0:T(8,128)S(1)}, f32[3,20,256]{2,1,0:T(8,128)S(1)}, u32[]{:S(2)}, u32[]{:S(2)}) collective-permute-start(f32[3,20,256]{2,1,0:T(8,128)S(1)} %pad_maximum_fusion.15), channel_id=1, source_target_pairs={{0,4},{4,8},{8,12},{1,5},{5,9},{9,13},{2,6},{6,10},{10,14},{3,7},{... | collective-permute-start | bytes 184328 | tf_op jit(solution)/shard_map/ppermute | solution.py:30

commit v26 on v23

--- a/solution.py
+++ b/solution.py
@@ -213,8 +213,8 @@
     coarse = coarse + from_next[:, ahead][:, None] * last_slot[None, :, None, None]
     prev_last = (jnp.arange(NCS) == NCS - 1).astype(jnp.float32)
     from_prev = from_prev + edge_sums[:, None] * prev_last[None, :, None, None]
-    x_ext = jnp.concatenate([from_prev, coarse, jnp.zeros_like(tail_planes)], axis=1)
-    wide_range = jnp.arange(width_x + 2 * NCS)[:, None]
+    x_ext = jnp.concatenate([from_prev, coarse, jnp.zeros_like(tail_planes[:, :ahead])], axis=1)
+    wide_range = jnp.arange(width_x + NCS + ahead)[:, None]
     place = (wide_range == NCS + count_live + jnp.arange(ahead)[None, :]).astype(jnp.float32)
     x_ext = x_ext + jnp.einsum("tk,qkjl->qtjl", place, from_next[:, :ahead], precision=lax.Precision.HIGH)
     coarse_rim = NCS

time: 62.5 us -> 62.5 us (level)
  the two profiles are of different devices: /device:TPU:26 before, /device:TPU:30 now
where the time goes in v26:
time: 62.5 us; the launch traced here: 62 us
  waiting for transfers between devices  21.5 us (34%)
  starting transfers between devices  19.6 us (31%)
  other arithmetic  9.62 us (15%)
  matrix products  4.22 us (7%)
  local copies, waits for them, and re-layouts  3.98 us (6%)
  between operations  3.11 us (5%)
    ppermute x6, waiting for transfers between devices, passed_along(): return lax.ppermute(array, axis, pairs)  14.8 us
    ppermute x6, starting transfers between devices, passed_along(): return lax.ppermute(array, axis, pairs)  11.6 us
    ppermute x2, waiting for transfers between devices, padded(): before = lax.ppermute(last, axis, up)  5.93 us
    ppermute x2, starting transfers between devices, padded(): after = lax.ppermute(leading, axis, down)  4.28 us
    ppermute x2, starting transfers between devices, padded(): before = lax.ppermute(last, axis, up)  3.71 us
    add x4, other arithmetic, sweeps(): field_ext = center + OMEGA * (source_now - product) / faces_now[7]  3.68 us
    dot_general x5, matrix products, z_sum(): return jnp.dot(flat, pick_z, precision=lax.Precision.HIGH)  1.48 us
  transfers between devices with their start and end apart: 10, of which 9 were waited for; matrix products, arithmetic and copies ran while one was open for 5% of the time, Pallas kernels for 0%

profile of v26, /device:TPU:30, one launch (start us, length us, event | category | flops | bytes accessed | tf_op | source)
XLA Modules:
  0.0 62.0 jit_solution(2085774620081825672)
XLA Ops:
  0.0 1.0 %pad_maximum_fusion.8 = (f32[3,3,16,256]{3,2,1,0:T(8,128)S(1)}, f32[3,3,16,256]{3,2,1,0:T(8,128)S(1)}) fusion(f32[1,16,16,256]{3,2,1,0:T(8,128)} %bitcast.231, f32[1,16,16,256]{3,2,1,0:T(8,128)} %bitcast.224, f32[1,16,16,256]{3,2,1,0:T(8,128)} %bitcast.233), kind=kLoop, calls=%fused_computation.177 | loop fusion | flops 147456 | bytes 1081344 | tf_op jit(solution)/shard_map/slice | solution.py:19
  1.0 2.4 %collective-permute-start.1 = (f32[3,3,16,256]{3,2,1,0:T(8,128)S(1)}, f32[3,3,16,256]{3,2,1,0:T(8,128)S(1)}, u32[]{:S(2)}, u32[]{:S(2)}) collective-permute-start(f32[3,3,16,256]{3,2,1,0:T(8,128)S(1)} %get-tuple-element.24), channel_id=1, source_target_pairs={{4,0},{8,4},{12,8},{5,1},{9,5},{13,9},{6,2},{10,6},{14,10},{7,3},{... | collective-permute-start | bytes 442376 | tf_op jit(solution)/shard_map/ppermute | solution.py:22
  3.4 1.3 %collective-permute-start = (f32[3,3,16,256]{3,2,1,0:T(8,128)S(1)}, f32[3,3,16,256]{3,2,1,0:T(8,128)S(1)}, u32[]{:S(2)}, u32[]{:S(2)}) collective-permute-start(f32[3,3,16,256]{3,2,1,0:T(8,128)S(1)} %get-tuple-element.23), channel_id=1, source_target_pairs={{0,4},{4,8},{8,12},{1,5},{5,9},{9,13},{2,6},{6,10},{10,14},{3,7},{... | collective-permute-start | bytes 442376 | tf_op jit(solution)/shard_map/ppermute | solution.py:21
  5.8 0.7 %collective-permute-done.1 = f32[3,3,16,256]{3,2,1,0:T(8,128)S(1)} collective-permute-done((f32[3,3,16,256]{3,2,1,0:T(8,128)S(1)}, f32[3,3,16,256]{3,2,1,0:T(8,128)S(1)}, u32[]{:S(2)}, u32[]{:S(2)}) %collective-permute-start.1) | collective-permute-done | bytes 147488 | tf_op jit(solution)/shard_map/ppermute | solution.py:22
  6.5 4.1 %collective-permute-done = f32[3,3,16,256]{3,2,1,0:T(8,128)S(1)} collective-permute-done((f32[3,3,16,256]{3,2,1,0:T(8,128)S(1)}, f32[3,3,16,256]{3,2,1,0:T(8,128)S(1)}, u32[]{:S(2)}, u32[]{:S(2)}) %collective-permute-start) | collective-permute-done | bytes 147488 | tf_op jit(solution)/shard_map/ppermute | solution.py:21
  10.8 1.9 %collective-permute-start.3 = (f32[3,22,4,256]{3,2,1,0:T(4,128)S(1)}, f32[3,22,4,256]{3,2,1,0:T(4,128)S(1)}, u32[]{:S(2)}, u32[]{:S(2)}) collective-permute-start(f32[3,22,4,256]{3,2,1,0:T(4,128)S(1)} %get-tuple-element.22), channel_id=1, source_target_pairs={{1,0},{2,1},{3,2},{5,4},{6,5},{7,6},{9,8},{10,9},{11,10},{13,12},{... | collective-permute-start | bytes 811016 | tf_op jit(solution)/shard_map/ppermute | solution.py:22
  12.7 2.4 %collective-permute-start.2 = (f32[3,22,4,256]{3,2,1,0:T(4,128)S(1)}, f32[3,22,4,256]{3,2,1,0:T(4,128)S(1)}, u32[]{:S(2)}, u32[]{:S(2)}) collective-permute-start(f32[3,22,4,256]{3,2,1,0:T(4,128)S(1)} %get-tuple-element.21), channel_id=1, source_target_pairs={{0,1},{1,2},{2,3},{4,5},{5,6},{6,7},{8,9},{9,10},{10,11},{12,13},{... | collective-permute-start | bytes 811016 | tf_op jit(solution)/shard_map/ppermute | solution.py:21
  15.2 0.2 select_reduce_fusion
  15.4 0.6 %fusion.157 = (f32[1]{0:T(128)}, f32[1]{0:T(128)}, f32[1]{0:T(128)}) fusion(f32[19]{0:T(128)S(1)} %select_reduce_fusion), kind=kLoop, calls=%fused_computation.295 | loop fusion | bytes 24 | tf_op jit(solution)/shard_map/slice | solution.py:148
  18.7 1.8 %collective-permute-done.2 = f32[3,22,4,256]{3,2,1,0:T(4,128)S(1)} collective-permute-done((f32[3,22,4,256]{3,2,1,0:T(4,128)S(1)}, f32[3,22,4,256]{3,2,1,0:T(4,128)S(1)}, u32[]{:S(2)}, u32[]{:S(2)}) %collective-permute-start.2) | collective-permute-done | bytes 270368 | tf_op jit(solution)/shard_map/ppermute | solution.py:21
  20.5 0.3 pad_maximum_fusion
  20.8 0.1 slice_bitcast_fusion
  20.9 0.2 fusion.147
  21.1 0.2 divide_select_fusion
  21.3 0.2 divide_select_fusion.1
  21.5 0.3 fusion.148
  21.8 1.0 %fusion.15 = (f32[20,22,256]{2,1,0:T(8,128)S(1)}, f32[20,22,256]{2,1,0:T(8,128)S(1)}, f32[20,22,256]{2,1,0:T(8,128)S(1)}) fusion(f32[22,24,256]{2,1,0:T(8,128)S(1)} %get-tuple-element.20, f32[22,24,256]{2,1,0:T(8,128)S(1)} %get-tuple-element.19, f32[20,22,255]{2,1,0:T(8,128)S(1)} %get-tuple-element.30, f32[20,22,255]{2,1,0:T(8,128)S(1)} %get-tuple-element.29, ...), kind=kLoop, calls=%fused_computation.31 | loop fusion | flops 3041280 | bytes 7657464 | tf_op jit(solution)/shard_map/add | solution.py:109
  22.8 0.2 fusion.150
  23.1 0.7 %fusion.38 = f32[18,20,256]{2,1,0:T(8,128)S(1)} fusion(f32[20,22,256]{2,1,0:T(8,128)S(1)} %get-tuple-element.15, f32[22,23,256]{2,1,0:T(8,128)S(1)} %divide_select_fusion, f32[21,24,256]{2,1,0:T(8,128)S(1)} %divide_select_fusion.1, f32[22,24,256]{2,1,0:T(8,128)S(1)} %get-tuple-element.19, f32[18,20,255]{2,1,0:T(8,128)S(1)} %get-tuple-element.36, ...), kind=kLoop, calls=%fused_computation.67 | loop fusion | flops 1566720 | bytes 5606880 | tf_op jit(solution)/shard_map/add | solution.py:109
  23.8 0.1 fusion.152
  24.0 0.7 %copy-done = f32[256,128]{1,0:T(8,128)S(1)} copy-done((f32[256,128]{1,0:T(8,128)S(1)}, f32[256,128]{1,0:T(8,128)}, u32[]{:S(2)}) %copy-start) | copy-done | bytes 131096
  24.7 0.3 fusion.161
  25.0 0.5 fusion.146
  25.6 0.3 fusion.159
  25.9 0.3 fusion.158
  26.2 0.3 copy-done.4
  26.4 0.3 fusion.160
  26.8 0.3 fusion
  27.2 0.3 fusion.162
  27.5 0.2 convolution_bitcast_fusion.2
  27.9 0.2 convolution_bitcast_fusion.1
  28.2 2.4 %collective-permute-start.5 = (f32[5,4,8,128]{3,1,2,0:T(4,128)S(1)}, f32[5,4,8,128]{3,1,2,0:T(4,128)S(1)}, u32[]{:S(2)}, u32[]{:S(2)}) collective-permute-start(f32[5,4,8,128]{3,1,2,0:T(4,128)S(1)} %pad_maximum_fusion.10), channel_id=1, source_target_pairs={{4,0},{8,4},{12,8},{5,1},{9,5},{13,9},{6,2},{10,6},{14,10},{7,3},{... | collective-permute-start | bytes 245768 | tf_op jit(solution)/shard_map/ppermute | solution.py:30
  30.5 1.3 %collective-permute-start.4 = (f32[5,4,8,128]{3,1,2,0:T(4,128)S(1)}, f32[5,4,8,128]{3,1,2,0:T(4,128)S(1)}, u32[]{:S(2)}, u32[]{:S(2)}) collective-permute-start(f32[5,4,8,128]{3,1,2,0:T(4,128)S(1)} %convolution_bitcast_fusion.1), channel_id=1, source_target_pairs={{0,4},{4,8},{8,12},{1,5},{5,9},{9,13},{2,6},{6,10},{10,14},{3,7},{... | collective-permute-start | bytes 245768 | tf_op jit(solution)/shard_map/ppermute | solution.py:30
  31.8 0.7 %collective-permute-done.5 = f32[5,4,8,128]{3,1,2,0:T(4,128)S(1)} collective-permute-done((f32[5,4,8,128]{3,1,2,0:T(4,128)S(1)}, f32[5,4,8,128]{3,1,2,0:T(4,128)S(1)}, u32[]{:S(2)}, u32[]{:S(2)}) %collective-permute-start.5) | collective-permute-done | bytes 81952 | tf_op jit(solution)/shard_map/ppermute | solution.py:30
  32.6 0.1 multiply_add_fusion.1
  32.7 4.2 %collective-permute-done.4 = f32[5,4,8,128]{3,1,2,0:T(4,128)S(1)} collective-permute-done((f32[5,4,8,128]{3,1,2,0:T(4,128)S(1)}, f32[5,4,8,128]{3,1,2,0:T(4,128)S(1)}, u32[]{:S(2)}, u32[]{:S(2)}) %collective-permute-start.4) | collective-permute-done | bytes 81952 | tf_op jit(solution)/shard_map/ppermute | solution.py:30
  37.0 0.4 maximum_add_fusion
  37.5 1.9 %collective-permute-start.7 = (f32[5,23,4,128]{3,1,2,0:T(8,128)S(1)}, f32[5,23,4,128]{3,1,2,0:T(8,128)S(1)}, u32[]{:S(2)}, u32[]{:S(2)}) collective-permute-start(f32[5,23,4,128]{3,1,2,0:T(8,128)S(1)} %slice.835), channel_id=1, source_target_pairs={{1,0},{2,1},{3,2},{5,4},{6,5},{7,6},{9,8},{10,9},{11,10},{13,12},{... | collective-permute-start | bytes 706568 | tf_op jit(solution)/shard_map/ppermute | solution.py:30
  39.4 2.4 %collective-permute-start.6 = (f32[5,23,5,128]{3,1,2,0:T(8,128)S(1)}, f32[5,23,5,128]{3,1,2,0:T(8,128)S(1)}, u32[]{:S(2)}, u32[]{:S(2)}) collective-permute-start(f32[5,23,5,128]{3,1,2,0:T(8,128)S(1)} %slice.834), channel_id=1, source_target_pairs={{0,1},{1,2},{2,3},{4,5},{5,6},{6,7},{8,9},{9,10},{10,11},{12,13},{... | collective-permute-start | bytes 883208 | tf_op jit(solution)/shard_map/ppermute | solution.py:30
  41.8 0.7 %and_convert_fusion = f32[2]{0:T(128)S(1)} fusion(s32[19]{0:T(128)S(1)} %iota_add_fusion, f32[19]{0:T(128)S(1)} %select_reduce_fusion, f32[]{:T(128)} %bitcast.21), kind=kLoop, calls=%fused_computation.247 | loop fusion | flops 8 | bytes 28 | tf_op jit(solution)/shard_map/convert_element_type | solution.py:303
  42.5 0.6 collective-permute-done.7
  43.1 4.5 %collective-permute-done.6 = f32[5,23,5,128]{3,1,2,0:T(8,128)S(1)} collective-permute-done((f32[5,23,5,128]{3,1,2,0:T(8,128)S(1)}, f32[5,23,5,128]{3,1,2,0:T(8,128)S(1)}, u32[]{:S(2)}, u32[]{:S(2)}) %collective-permute-start.6) | collective-permute-done | bytes 294432 | tf_op jit(solution)/shard_map/ppermute | solution.py:30
  47.7 0.2 fusion.62
  48.0 0.1 fusion.154
  48.1 0.3 fusion.70
  48.4 0.1 fusion.155
  48.5 0.3 fusion.81
  48.9 0.2 multiply_reduce_fusion
  49.2 0.2 fusion.117
  49.4 0.2 fusion.119
  49.5 0.3 fusion.108
  49.8 0.2 fusion.121
  50.0 0.2 fusion.123
  50.2 0.3 fusion.59
  50.6 2.4 %collective-permute-start.9 = (f32[2,20,256]{2,1,0:T(8,128)S(1)}, f32[2,20,256]{2,1,0:T(8,128)S(1)}, u32[]{:S(2)}, u32[]{:S(2)}) collective-permute-start(f32[2,20,256]{2,1,0:T(8,128)S(1)} %get-tuple-element.42), channel_id=1, source_target_pairs={{4,0},{8,4},{12,8},{5,1},{9,5},{13,9},{6,2},{10,6},{14,10},{7,3},{... | collective-permute-start | bytes 122888 | tf_op jit(solution)/shard_map/ppermute | solution.py:30
  53.0 0.1 fusion.163
  53.1 0.2 fusion.164
  53.3 1.3 %collective-permute-start.8 = (f32[3,20,256]{2,1,0:T(8,128)S(1)}, f32[3,20,256]{2,1,0:T(8,128)S(1)}, u32[]{:S(2)}, u32[]{:S(2)}) collective-permute-start(f32[3,20,256]{2,1,0:T(8,128)S(1)} %pad_maximum_fusion.11), channel_id=1, source_target_pairs={{0,4},{4,8},{8,12},{1,5},{5,9},{9,13},{2,6},{6,10},{10,14},{3,7},{... | collective-permute-start | bytes 184328 | tf_op jit(solution)/shard_map/ppermute | solution.py:30
  54.8 4.8 %collective-permute-done.8 = f32[3,20,256]{2,1,0:T(8,128)S(1)} collective-permute-done((f32[3,20,256]{2,1,0:T(8,128)S(1)}, f32[3,20,256]{2,1,0:T(8,128)S(1)}, u32[]{:S(2)}, u32[]{:S(2)}) %collective-permute-start.8) | collective-permute-done | bytes 61472 | tf_op jit(solution)/shard_map/ppermute | solution.py:30
  59.6 0.1 multiply_add_fusion
  59.7 0.2 fusion.149
  59.9 0.8 %fusion.26 = f32[18,18,256]{2,1,0:T(8,128)S(1)} fusion(f32[20,20,256]{2,1,0:T(8,128)S(1)} %pad_maximum_fusion.3, f32[22,23,256]{2,1,0:T(8,128)S(1)} %divide_select_fusion, f32[2,20,256]{2,1,0:T(8,128)S(1)} %multiply_add_fusion.3, f32[16,20,256]{2,1,0:T(8,128)S(1)} %multiply_add_fusion, f32[21,24,256]{2,1,0:T(8,128)S(1)} %divide_select_fusion.1, ...), kind=kLoop, calls=%fused_computation.51 | loop fusion | flops 1575936 | bytes 4837120 | tf_op jit(solution)/shard_map/add | solution.py:109
  60.8 0.1 fusion.151
  60.9 1.1 %fusion.49 = f32[16,16,256]{2,1,0:T(8,128)} fusion(f32[18,18,256]{2,1,0:T(8,128)S(1)} %fusion.26, f32[22,24,256]{2,1,0:T(8,128)S(1)} %get-tuple-element.19, f32[16,16,255]{2,1,0:T(8,128)S(1)} %get-tuple-element.38, f32[16,16,255]{2,1,0:T(8,128)S(1)} %get-tuple-element.37, f32[22,23,256]{2,1,0:T(8,128)S(1)} %divide_select_fusion, ...), kind=kLoop, calls=%fused_computation.88 | loop fusion | flops 1114112 | bytes 4116768 | tf_op jit(solution)/shard_map/add | solution.py:109
  (86 shorter events, 2.6 us)
Async XLA Ops:
  0.0 10.6 %copy-start.2 = (f32[16,16,256]{2,1,0:T(8,128)S(1)}, f32[16,16,256]{2,1,0:T(8,128)}, u32[]{:S(2)}) copy-start(f32[16,16,256]{2,1,0:T(8,128)} %param.13) | copy-start | bytes 786436
  0.0 10.6 %copy-start.1 = (f32[16,16,256]{2,1,0:T(8,128)S(1)}, f32[16,16,256]{2,1,0:T(8,128)}, u32[]{:S(2)}) copy-start(f32[16,16,256]{2,1,0:T(8,128)} %param.12) | copy-start | bytes 786436
  0.0 10.6 %copy-start.3 = (f32[16,16,256]{2,1,0:T(8,128)S(1)}, f32[16,16,256]{2,1,0:T(8,128)}, u32[]{:S(2)}) copy-start(f32[16,16,256]{2,1,0:T(8,128)} %param.11) | copy-start | bytes 786436
  1.0 5.5 %collective-permute-start.1 = (f32[3,3,16,256]{3,2,1,0:T(8,128)S(1)}, f32[3,3,16,256]{3,2,1,0:T(8,128)S(1)}, u32[]{:S(2)}, u32[]{:S(2)}) collective-permute-start(f32[3,3,16,256]{3,2,1,0:T(8,128)S(1)} %get-tuple-element.24), channel_id=1, source_target_pairs={{4,0},{8,4},{12,8},{5,1},{9,5},{13,9},{6,2},{10,6},{14,10},{7,3},{... | collective-permute-start | bytes 442376 | tf_op jit(solution)/shard_map/ppermute | solution.py:22
  3.4 7.2 %collective-permute-start = (f32[3,3,16,256]{3,2,1,0:T(8,128)S(1)}, f32[3,3,16,256]{3,2,1,0:T(8,128)S(1)}, u32[]{:S(2)}, u32[]{:S(2)}) collective-permute-start(f32[3,3,16,256]{3,2,1,0:T(8,128)S(1)} %get-tuple-element.23), channel_id=1, source_target_pairs={{0,4},{4,8},{8,12},{1,5},{5,9},{9,13},{2,6},{6,10},{10,14},{3,7},{... | collective-permute-start | bytes 442376 | tf_op jit(solution)/shard_map/ppermute | solution.py:21
  10.7 4.5 %copy-start.9 = (s32[64]{0:T(128)S(1)}, s32[64]{0:T(128)}, u32[]{:S(2)}) copy-start(s32[64]{0:T(128)} %param.14) | copy-start | bytes 772
  10.8 7.9 %collective-permute-start.3 = (f32[3,22,4,256]{3,2,1,0:T(4,128)S(1)}, f32[3,22,4,256]{3,2,1,0:T(4,128)S(1)}, u32[]{:S(2)}, u32[]{:S(2)}) collective-permute-start(f32[3,22,4,256]{3,2,1,0:T(4,128)S(1)} %get-tuple-element.22), channel_id=1, source_target_pairs={{1,0},{2,1},{3,2},{5,4},{6,5},{7,6},{9,8},{10,9},{11,10},{13,12},{... | collective-permute-start | bytes 811016 | tf_op jit(solution)/shard_map/ppermute | solution.py:22
  12.7 7.8 %collective-permute-start.2 = (f32[3,22,4,256]{3,2,1,0:T(4,128)S(1)}, f32[3,22,4,256]{3,2,1,0:T(4,128)S(1)}, u32[]{:S(2)}, u32[]{:S(2)}) collective-permute-start(f32[3,22,4,256]{3,2,1,0:T(4,128)S(1)} %get-tuple-element.21), channel_id=1, source_target_pairs={{0,1},{1,2},{2,3},{4,5},{5,6},{6,7},{8,9},{9,10},{10,11},{12,13},{... | collective-permute-start | bytes 811016 | tf_op jit(solution)/shard_map/ppermute | solution.py:21
  23.8 0.9 %copy-start = (f32[256,128]{1,0:T(8,128)S(1)}, f32[256,128]{1,0:T(8,128)}, u32[]{:S(2)}) copy-start(f32[256,128]{1,0:T(8,128)} %constant.47.clone) | copy-start | bytes 393220
  25.5 0.9 %copy-start.4 = (f32[256,128]{1,0:T(8,128)S(1)}, f32[256,128]{1,0:T(8,128)}, u32[]{:S(2)}) copy-start(f32[256,128]{1,0:T(8,128)} %constant.48.clone) | copy-start | bytes 393220
  25.5 1.2 %copy-start.8 = (f32[136]{0:T(256)S(1)}, f32[136]{0:T(256)}, u32[]{:S(2)}) copy-start(f32[136]{0:T(256)} %constant.49.clone) | copy-start | bytes 1636
  25.5 1.2 %copy-start.10 = (pred[136,256]{1,0:T(8,128)(4,1)S(1)}, pred[136,256]{1,0:T(8,128)(4,1)}, u32[]{:S(2)}) copy-start(pred[136,256]{1,0:T(8,128)(4,1)} %constant.51.clone) | copy-start | bytes 104452
  26.7 0.8 %copy-start.6 = (pred[136,256]{1,0:T(8,128)(4,1)S(1)}, pred[136,256]{1,0:T(8,128)(4,1)}, u32[]{:S(2)}) copy-start(pred[136,256]{1,0:T(8,128)(4,1)} %constant.52.clone) | copy-start | bytes 104452
  28.2 4.4 %collective-permute-start.5 = (f32[5,4,8,128]{3,1,2,0:T(4,128)S(1)}, f32[5,4,8,128]{3,1,2,0:T(4,128)S(1)}, u32[]{:S(2)}, u32[]{:S(2)}) collective-permute-start(f32[5,4,8,128]{3,1,2,0:T(4,128)S(1)} %pad_maximum_fusion.10), channel_id=1, source_target_pairs={{4,0},{8,4},{12,8},{5,1},{9,5},{13,9},{6,2},{10,6},{14,10},{7,3},{... | collective-permute-start | bytes 245768 | tf_op jit(solution)/shard_map/ppermute | solution.py:30
  30.5 6.3 %collective-permute-start.4 = (f32[5,4,8,128]{3,1,2,0:T(4,128)S(1)}, f32[5,4,8,128]{3,1,2,0:T(4,128)S(1)}, u32[]{:S(2)}, u32[]{:S(2)}) collective-permute-start(f32[5,4,8,128]{3,1,2,0:T(4,128)S(1)} %convolution_bitcast_fusion.1), channel_id=1, source_target_pairs={{0,4},{4,8},{8,12},{1,5},{5,9},{9,13},{2,6},{6,10},{10,14},{3,7},{... | collective-permute-start | bytes 245768 | tf_op jit(solution)/shard_map/ppermute | solution.py:30
  37.5 5.6 %collective-permute-start.7 = (f32[5,23,4,128]{3,1,2,0:T(8,128)S(1)}, f32[5,23,4,128]{3,1,2,0:T(8,128)S(1)}, u32[]{:S(2)}, u32[]{:S(2)}) collective-permute-start(f32[5,23,4,128]{3,1,2,0:T(8,128)S(1)} %slice.835), channel_id=1, source_target_pairs={{1,0},{2,1},{3,2},{5,4},{6,5},{7,6},{9,8},{10,9},{11,10},{13,12},{... | collective-permute-start | bytes 706568 | tf_op jit(solution)/shard_map/ppermute | solution.py:30
  39.4 8.2 %collective-permute-start.6 = (f32[5,23,5,128]{3,1,2,0:T(8,128)S(1)}, f32[5,23,5,128]{3,1,2,0:T(8,128)S(1)}, u32[]{:S(2)}, u32[]{:S(2)}) collective-permute-start(f32[5,23,5,128]{3,1,2,0:T(8,128)S(1)} %slice.834), channel_id=1, source_target_pairs={{0,1},{1,2},{2,3},{4,5},{5,6},{6,7},{8,9},{9,10},{10,11},{12,13},{... | collective-permute-start | bytes 883208 | tf_op jit(solution)/shard_map/ppermute | solution.py:30
  48.9 1.3 %copy-start.5 = (pred[256,136]{1,0:T(32,128)(4,1)S(1)}, pred[256,136]{1,0:T(32,128)(4,1)}, u32[]{:S(2)}) copy-start(pred[256,136]{1,0:T(32,128)(4,1)} %constant.50.clone) | copy-start | bytes 104452
  49.8 3.3 %copy-start.7 = (f32[20,10]{1,0:T(8,128)S(1)}, f32[20,10]{1,0:T(8,128)}, u32[]{:S(2)}) copy-start(f32[20,10]{1,0:T(8,128)} %constant.53.clone) | copy-start | bytes 2404
  50.6 4.1 %collective-permute-start.9 = (f32[2,20,256]{2,1,0:T(8,128)S(1)}, f32[2,20,256]{2,1,0:T(8,128)S(1)}, u32[]{:S(2)}, u32[]{:S(2)}) collective-permute-start(f32[2,20,256]{2,1,0:T(8,128)S(1)} %get-tuple-element.42), channel_id=1, source_target_pairs={{4,0},{8,4},{12,8},{5,1},{9,5},{13,9},{6,2},{10,6},{14,10},{7,3},{... | collective-permute-start | bytes 122888 | tf_op jit(solution)/shard_map/ppermute | solution.py:30
  53.3 6.2 %collective-permute-start.8 = (f32[3,20,256]{2,1,0:T(8,128)S(1)}, f32[3,20,256]{2,1,0:T(8,128)S(1)}, u32[]{:S(2)}, u32[]{:S(2)}) collective-permute-start(f32[3,20,256]{2,1,0:T(8,128)S(1)} %pad_maximum_fusion.11), channel_id=1, source_target_pairs={{0,4},{4,8},{8,12},{1,5},{5,9},{9,13},{2,6},{6,10},{10,14},{3,7},{... | collective-permute-start | bytes 184328 | tf_op jit(solution)/shard_map/ppermute | solution.py:30
